TPU v7x, 32 devices: a whole 2x2x4 slice. The times are simulated.
32 devices in a mesh: date: 8 (over z, y), az: 4 (over x, core).
Axes of the slice: x: 2, y: 2, z: 4, core: 2. Of those that a mesh axis runs over, the one named last changes fastest.
Arguments:
- slc: bfloat16 [8, 2, 640, 4096], P('date', None, 'az'), may hold values from -18 to 18
- az_offset: int32 [8], P('date'), may hold values from -12 to 12
- az_kernel: int32 [8], P('date'), may hold values from 0 to 63
- rg_offset: int32 [8, 640], P('date', 'az'), may hold values from -12 to 12
- rg_kernel: int32 [8, 640], P('date', 'az'), may hold values from 0 to 63
- partners: int32 [8, 4], P('date'), may hold values from 0 to 7, as said below
Outputs:
- interferograms: float32 [8, 4, 2, 32, 1024], P('date', None, None, 'az')
Inputs may be any that keep to these rules, and one draw needn't show every extreme that they name: `partners`: each row holds 4 distinct dates other than its own date, each within 4 dates of it; some date has a partner 4 dates later and some date one 4 dates earlier.
All inputs are finite; a program needn't handle non-finite values.
Results may differ from a plain program's by a relative error of at most 0.004.
Values may be sent and summed in bfloat16 or wider, within the bound.
No kernel may reach another device: no remote copies, remote signals or barrier semaphores. Data moves between devices by JAX's collectives and lax.ppermute only.
A program may use at most 128 MiB of HBM per device.

v0:
```python
import jax
import jax.numpy as jnp
from jax import lax
from jax.sharding import PartitionSpec as P
from jax.experimental import pallas as pl
from jax.experimental.pallas import tpu as pltpu

PARTNERS = 4
GAP = 4
OFFAZ = 12
OFFRG = 12
NFRAC = 64
LOOK_AZ = 20
LOOK_RG = 4


def padded_2(cells, sides, width):
    for axis, dim in sides:
        count = lax.axis_size(axis)
        ends = count - 1
        head = lax.slice_in_dim(cells, 0, width, axis=dim)
        tail = lax.slice_in_dim(cells, cells.shape[dim] - width, cells.shape[dim], axis=dim)
        cells = jnp.concatenate(
            [
                lax.ppermute(tail, axis, [(i, (i + 1) % count) for i in range(ends)]),
                cells,
                lax.ppermute(head, axis, [((i + 1) % count, i) for i in range(ends)]),
            ],
            axis=dim,
        )
    return cells


def shifted(block, axis, distance):
    count = lax.axis_size(axis)
    route = [(i + distance, i) for i in range(count) if 0 <= i + distance < count]
    return lax.ppermute(block, axis, route)


def swapped(block, axis):
    count = lax.axis_size(axis)
    return lax.ppermute(block, axis, [(i, i ^ 1) for i in range(count)])


def kernel_table():
    frac = jnp.arange(NFRAC, dtype=jnp.float32)[:, None] / NFRAC
    taps = jnp.arange(8, dtype=jnp.float32)[None, :]
    place = taps - 3.0 - frac
    return jnp.sinc(place) * (0.5 + 0.5 * jnp.cos(jnp.pi * place / 4.5))


def resample_block(padded, shift_lines, kern_lines, shift_range, kern_range):
    table = kernel_table()
    nlines = shift_range.shape[0]
    nrange = padded.shape[2]
    border = OFFAZ + 4
    start = border + shift_lines - 3
    window = lax.dynamic_slice_in_dim(padded, start, nlines + 7, 1)
    weights = table[kern_lines]
    along = jnp.zeros((2, nlines, nrange), jnp.float32)
    for tap in range(8):
        along = along + weights[tap] * window[:, tap : tap + nlines, :].astype(jnp.float32)
    margin = OFFRG + 4
    widened = jnp.pad(along, ((0, 0), (0, 0), (margin, margin)))
    selector = (kern_range[:, None] == jnp.arange(NFRAC, dtype=jnp.int32)[None, :]).astype(
        jnp.float32
    )
    range_weights = jnp.dot(selector, table, precision=lax.Precision.HIGHEST)
    targets = shift_range[:, None] + jnp.arange(8, dtype=jnp.int32)[None, :] - 3
    result = jnp.zeros((2, nlines, nrange), jnp.float32)
    for offset in range(-OFFRG - 3, OFFRG + 5):
        coeff = jnp.sum(jnp.where(targets == offset, range_weights, 0.0), axis=1)
        result = (
            result
            + coeff[None, :, None] * widened[:, :, margin + offset : margin + offset + nrange]
        )
    return result.astype(jnp.bfloat16)


CHUNK = 512


def looks_kernel(first_ref, second_ref, out_ref):
    first_re = first_ref[0].astype(jnp.float32)
    first_im = first_ref[1].astype(jnp.float32)
    second_re = second_ref[0].astype(jnp.float32)
    second_im = second_ref[1].astype(jnp.float32)
    real_part = first_re * second_re + first_im * second_im
    imag_part = first_im * second_re - first_re * second_im
    rows = real_part.shape[0]
    groups = rows // LOOK_AZ
    real_lines = real_part.reshape(LOOK_AZ, groups, CHUNK).sum(axis=0)
    imag_lines = imag_part.reshape(LOOK_AZ, groups, CHUNK).sum(axis=0)
    pooling = (
        lax.broadcasted_iota(jnp.int32, (CHUNK, CHUNK // LOOK_RG), 0) // LOOK_RG
        == lax.broadcasted_iota(jnp.int32, (CHUNK, CHUNK // LOOK_RG), 1)
    ).astype(jnp.float32)
    real_looks = jnp.dot(real_lines, pooling, precision=lax.Precision.HIGHEST, preferred_element_type=jnp.float32)
    imag_looks = jnp.dot(imag_lines, pooling, precision=lax.Precision.HIGHEST, preferred_element_type=jnp.float32)
    out_ref[0] = real_looks / (LOOK_AZ * LOOK_RG)
    out_ref[1] = imag_looks / (LOOK_AZ * LOOK_RG)


def looks(first, second):
    nlines = first.shape[1]
    width = first.shape[2]
    groups = nlines // LOOK_AZ
    spec = pl.BlockSpec((2, nlines, CHUNK), lambda j: (0, 0, j))
    return pl.pallas_call(
        looks_kernel,
        grid=(width // CHUNK,),
        in_specs=[spec, spec],
        out_specs=pl.BlockSpec((2, groups, CHUNK // LOOK_RG), lambda j: (0, 0, j)),
        out_shape=jax.ShapeDtypeStruct((2, groups, width // LOOK_RG), jnp.float32),
    )(first, second)


def look_order(image):
    nlines = image.shape[1]
    groups = nlines // LOOK_AZ
    return image.reshape(2, groups, LOOK_AZ, image.shape[2]).transpose(0, 2, 1, 3).reshape(image.shape)


def conj(block):
    return jnp.stack([block[0], -block[1]])


def shards(slc, az_offset, az_kernel, rg_offset, rg_kernel, partners):
    padded = padded_2(slc, (("az", 2),), OFFAZ + 4)
    resampled = resample_block(padded[0], az_offset[0], az_kernel[0], rg_offset[0], rg_kernel[0])
    resampled = look_order(resampled)
    half = resampled.shape[2] // 2
    own_left = resampled[:, :, :half]
    own_right = resampled[:, :, half:]
    date = lax.axis_index("date")
    even = date % 2 == 0

    left_2 = shifted(own_left, "date", 2)
    left_4 = shifted(left_2, "date", 2)
    left_a = swapped(left_2, "date")
    left_x = swapped(jnp.where(even, left_4, own_left), "date")
    right_2 = shifted(own_right, "date", -2)
    right_4 = shifted(right_2, "date", -2)
    right_a = swapped(right_2, "date")
    right_x = swapped(jnp.where(even, own_right, right_4), "date")

    ahead_2 = looks(own_left, left_2)
    ahead_4 = looks(own_left, left_4)
    ahead_a = looks(own_left, left_a)
    ahead_x = looks(own_left, left_x)
    behind_2 = looks(own_right, right_2)
    behind_4 = looks(own_right, right_4)
    behind_a = looks(own_right, right_a)
    behind_x = looks(own_right, right_x)
    ahead = {
        1: jnp.where(even, ahead_x, ahead_a),
        2: ahead_2,
        3: jnp.where(even, ahead_a, ahead_x),
        4: ahead_4,
    }
    behind = {
        1: jnp.where(even, behind_a, behind_x),
        2: behind_2,
        3: jnp.where(even, behind_x, behind_a),
        4: behind_4,
    }
    full = {}
    for s in range(1, GAP + 1):
        right_of_ahead = conj(shifted(behind[s], "date", s))
        left_of_behind = conj(shifted(ahead[s], "date", -s))
        full[s] = jnp.concatenate([ahead[s], right_of_ahead], axis=2)
        full[-s] = jnp.concatenate([left_of_behind, behind[s]], axis=2)

    listed = partners[0]
    outputs = []
    for slot in range(PARTNERS):
        value = jnp.zeros_like(full[1])
        for step, block in full.items():
            value = jnp.where(listed[slot] == date + step, block, value)
        outputs.append(value)
    return jnp.stack(outputs)[None]


def solution(mesh):
    in_specs = (
        P("date", None, "az", None),
        P("date"),
        P("date"),
        P("date", "az"),
        P("date", "az"),
        P("date", None),
    )
    out_specs = P("date", None, None, "az", None)
    return jax.shard_map(shards, mesh=mesh, in_specs=in_specs, out_specs=out_specs, check_vma=False)
```

profile of v0, /device:TPU:0, one launch (start us, length us, event | category | flops | bytes accessed | tf_op | source)
XLA Modules:
  0.0 301.4 jit_solution(18055549392705850179)
XLA Ops:
  0.0 1.1 fusion.98
  1.1 1.3 collective-permute-start.1
  2.4 3.0 %collective-permute-start = (bf16[1,2,16,4096]{3,2,1,0:T(8,128)(2,1)S(1)}, bf16[1,2,16,4096]{3,2,1,0:T(8,128)(2,1)S(1)}, u32[]{:S(2)}, u32[]{:S(2)}) collective-permute-start(bf16[1,2,16,4096]{3,2,1,0:T(8,128)(2,1)S(1)} %get-tuple-element.40), channel_id=1, source_target_pairs={{0,1},{1,2},{2,3},{4,5},{5,6},{6,7},{8,9},{9,10},{10,11},{12,13},{... | collective-permute-start | bytes 786440 | tf_op jit(solution)/shard_map/ppermute | solution.py:25
  6.1 0.1 fusion.63
  6.2 0.1 constant_dynamic-slice_fusion
  6.9 0.6 fusion.107
  7.6 1.1 select_reduce_fusion.31
  8.7 0.0 collective-permute-done.1
  8.7 0.0 collective-permute-done
  8.7 3.5 %fusion.23 = bf16[2,167,4096]{2,1,0:T(8,128)(2,1)S(1)} fusion(s32[]{:T(128)S(6)} %select_n.600, bf16[1,2,16,4096]{3,2,1,0:T(8,128)(2,1)S(1)} %collective-permute-done, bf16[1,2,160,4096]{3,2,1,0:T(8,128)(2,1)} %param.6, bf16[1,2,16,4096]{3,2,1,0:T(8,128)(2,1)S(1)} %collective-permute-done.1), kind=kLoop, calls=%fused_computation.39 | loop fusion | flops 8208384 | bytes 5881860 | tf_op jit(solution)/shard_map/dynamic_slice | solution.py:58
  12.2 10.3 %multiply_add_fusion = f32[2,160,4096]{2,1,0:T(8,128)S(1)} fusion(bf16[2,167,4096]{2,1,0:T(8,128)(2,1)S(1)} %fusion.23, f32[]{:T(128)} %bitcast.14, f32[]{:T(128)} %bitcast.13, f32[]{:T(128)} %bitcast.12, f32[]{:T(128)} %bitcast.11, f32[]{:T(128)} %bitcast.10, f32[]{:T(128)} %bitcast.9, f32[]{:T(128)} %bitcast.8, f32[]{:T(128)} %bitcast.4), kind=kLoop, calls=%fused_computation.33 | loop fusion | flops 30146560 | bytes 26214432 | tf_op jit(solution)/shard_map/add | solution.py:62
  22.5 43.5 %add_convert_fusion = bf16[2,160,4096]{2,1,0:T(8,128)(2,1)S(1)} fusion(f32[2,160,4096]{2,1,0:T(8,128)S(1)} %multiply_add_fusion, f32[160]{0:T(256)S(1)} %get-tuple-element.6, f32[160]{0:T(256)S(1)} %get-tuple-element.7, f32[160]{0:T(256)S(1)} %get-tuple-element.8, f32[160]{0:T(256)S(1)} %get-tuple-element.9, f32[160]{0:T(256)S(1)} %get-tuple-element.10, ...), kind=kLoop, calls=%fused_computation | loop fusion | flops 83886080 | bytes 7884800 | tf_op jit(solution)/shard_map/convert_element_type | solution.py:77
  66.0 2.7 copy.10
  68.7 1.7 copy.13
  70.4 0.0 copy-start.2
  70.5 0.1 slice.333.first_ref
  70.6 0.0 copy-start.9
  70.6 1.4 collective-permute-start.2
  72.0 32.8 %collective-permute-done.2.second_ref = bf16[2,160,2048]{2,1,0:T(8,128)(2,1)} collective-permute-done((bf16[2,160,2048]{2,1,0:T(8,128)(2,1)S(1)}, bf16[2,160,2048]{2,1,0:T(8,128)(2,1)}, u32[]{:S(2)}, u32[]{:S(2)}) %collective-permute-start.2) | collective-permute-done | bytes 1310752 | tf_op jit(solution)/shard_map/ppermute | solution.py:37
  104.9 1.3 collective-permute-start.3
  106.2 32.3 %collective-permute-done.3.second_ref = bf16[2,160,2048]{2,1,0:T(8,128)(2,1)} collective-permute-done((bf16[2,160,2048]{2,1,0:T(8,128)(2,1)}, bf16[2,160,2048]{2,1,0:T(8,128)(2,1)}, u32[]{:S(2)}, u32[]{:S(2)}) %collective-permute-start.3) | collective-permute-done | bytes 1310752 | tf_op jit(solution)/shard_map/ppermute | solution.py:37
  138.5 3.4 %broadcast_select_fusion.1 = (bf16[2,160,2048]{2,1,0:T(8,128)(2,1)}, bf16[2,160,2048]{2,1,0:T(8,128)(2,1)S(1)}) fusion(bf16[2,160,2048]{2,1,0:T(8,128)(2,1)} %collective-permute-done.3.second_ref, pred[]{:T(512)S(6)} %eq.398, bf16[2,160,4096]{2,1,0:T(8,128)(2,1)} %bitcast.55), kind=kLoop, calls=%fused_computation.42 | loop fusion | flops 655360 | bytes 6553601 | tf_op jit(solution)/shard_map/jit(_where)/select_n | solution.py:141
  141.9 4.7 %collective-permute-start.5 = (bf16[2,160,2048]{2,1,0:T(8,128)(2,1)S(1)}, bf16[2,160,2048]{2,1,0:T(8,128)(2,1)}, u32[]{:S(2)}, u32[]{:S(2)}) collective-permute-start(bf16[2,160,2048]{2,1,0:T(8,128)(2,1)S(1)} %get-tuple-element.38.first_ref), channel_id=1, source_target_pairs={{0,8},{4,12},{8,16},{12,20},{16,24},{20,28},{1,9},{5,13},{9,17},{1... | collective-permute-start | bytes 3932168 | tf_op jit(solution)/shard_map/ppermute | solution.py:37
  146.6 1.1 collective-permute-start.8
  147.7 0.9 collective-permute-start.9
  148.6 24.4 %collective-permute-done.5.second_ref = bf16[2,160,2048]{2,1,0:T(8,128)(2,1)} collective-permute-done((bf16[2,160,2048]{2,1,0:T(8,128)(2,1)S(1)}, bf16[2,160,2048]{2,1,0:T(8,128)(2,1)}, u32[]{:S(2)}, u32[]{:S(2)}) %collective-permute-start.5) | collective-permute-done | bytes 1310752 | tf_op jit(solution)/shard_map/ppermute | solution.py:37
  173.0 5.5 %collective-permute-start.6 = (bf16[2,160,2048]{2,1,0:T(8,128)(2,1)}, bf16[2,160,2048]{2,1,0:T(8,128)(2,1)}, u32[]{:S(2)}, u32[]{:S(2)}) collective-permute-start(bf16[2,160,2048]{2,1,0:T(8,128)(2,1)} %collective-permute-done.5.second_ref), channel_id=1, source_target_pairs={{0,8},{4,12},{8,16},{12,20},{16,24},{20,28},{1,9},{5,13},{9,17},{1... | collective-permute-start | bytes 3932168 | tf_op jit(solution)/shard_map/ppermute | solution.py:37
  178.5 4.4 %shard_map.70 = f32[2,8,512]{2,1,0:T(8,128)} custom-call(bf16[2,160,2048]{2,1,0:T(8,128)(2,1)} %copy-done, bf16[2,160,2048]{2,1,0:T(8,128)(2,1)} %collective-permute-done.2.second_ref), custom_call_target="tpu_custom_call" | custom-call | tf_op jit(solution)/shard_map/pallas_call | solution.py:109
  182.9 2.7 collective-permute-start.14
  185.6 0.7 fusion.108
  206.5 0.0 collective-permute-done.14
  206.5 4.4 %shard_map.64 = f32[2,8,512]{2,1,0:T(8,128)} custom-call(bf16[2,160,2048]{2,1,0:T(8,128)(2,1)} %copy-done, bf16[2,160,2048]{2,1,0:T(8,128)(2,1)} %collective-permute-done.3.second_ref), custom_call_target="tpu_custom_call" | custom-call | tf_op jit(solution)/shard_map/pallas_call | solution.py:109
  210.9 3.8 %collective-permute-start.4 = (f32[2,8,512]{2,1,0:T(8,128)}, f32[2,8,512]{2,1,0:T(8,128)S(1)}, u32[]{:S(2)}, u32[]{:S(2)}) collective-permute-start(f32[2,8,512]{2,1,0:T(8,128)} %shard_map.64), channel_id=1, source_target_pairs={{0,16},{4,20},{8,24},{12,28},{1,17},{5,21},{9,25},{13,29},{2,18},{... | collective-permute-start | bytes 98312 | tf_op jit(solution)/shard_map/ppermute | solution.py:37
  214.7 0.0 collective-permute-done.8.second_ref
  214.7 4.4 %shard_map.66 = f32[2,8,512]{2,1,0:T(8,128)} custom-call(bf16[2,160,2048]{2,1,0:T(8,128)(2,1)} %copy-done, bf16[2,160,2048]{2,1,0:T(8,128)(2,1)} %collective-permute-done.8.second_ref), custom_call_target="tpu_custom_call" | custom-call | tf_op jit(solution)/shard_map/pallas_call | solution.py:109
  219.1 1.1 collective-permute-start.12
  220.2 0.0 collective-permute-done.9.second_ref
  220.2 4.4 %shard_map.67 = f32[2,8,512]{2,1,0:T(8,128)} custom-call(bf16[2,160,2048]{2,1,0:T(8,128)(2,1)} %copy-done, bf16[2,160,2048]{2,1,0:T(8,128)(2,1)} %collective-permute-done.9.second_ref), custom_call_target="tpu_custom_call" | custom-call | tf_op jit(solution)/shard_map/pallas_call | solution.py:109
  224.6 0.0 collective-permute-done.6.second_ref
  224.6 1.5 broadcast_select_fusion
  226.1 1.4 collective-permute-start.11
  227.4 0.8 broadcast_select_fusion.5
  228.2 2.6 collective-permute-start.16
  230.8 0.0 collective-permute-done.4
  230.9 2.2 collective-permute-start.10
  233.0 4.4 %shard_map.71 = f32[2,8,512]{2,1,0:T(8,128)} custom-call(bf16[2,160,2048]{2,1,0:T(8,128)(2,1)} %copy-done.1, bf16[2,160,2048]{2,1,0:T(8,128)(2,1)} %collective-permute-done.5.second_ref), custom_call_target="tpu_custom_call" | custom-call | tf_op jit(solution)/shard_map/pallas_call | solution.py:109
  237.4 1.4 collective-permute-start.15
  238.8 35.9 %collective-permute-done.16 = f32[2,8,512]{2,1,0:T(8,128)S(1)} collective-permute-done((f32[2,8,512]{2,1,0:T(8,128)S(1)}, f32[2,8,512]{2,1,0:T(8,128)S(1)}, u32[]{:S(2)}, u32[]{:S(2)}) %collective-permute-start.16) | collective-permute-done | bytes 32800 | tf_op jit(solution)/shard_map/ppermute | solution.py:37
  274.7 0.0 collective-permute-done.15
  274.7 0.0 collective-permute-done.10
  274.8 4.4 %shard_map.65 = f32[2,8,512]{2,1,0:T(8,128)} custom-call(bf16[2,160,2048]{2,1,0:T(8,128)(2,1)} %copy-done.1, bf16[2,160,2048]{2,1,0:T(8,128)(2,1)} %collective-permute-done.6.second_ref), custom_call_target="tpu_custom_call" | custom-call | tf_op jit(solution)/shard_map/pallas_call | solution.py:109
  279.1 1.4 collective-permute-start.7
  280.6 0.0 collective-permute-done.12.second_ref
  280.6 1.1 copy-done.3
  281.7 4.4 %shard_map.69 = f32[2,8,512]{2,1,0:T(8,128)} custom-call(bf16[2,160,2048]{2,1,0:T(8,128)(2,1)} %copy-done.1, bf16[2,160,2048]{2,1,0:T(8,128)(2,1)} %copy-done.3), custom_call_target="tpu_custom_call" | custom-call | tf_op jit(solution)/shard_map/pallas_call | solution.py:109
  286.0 0.0 collective-permute-done.11.second_ref
  286.0 4.4 %shard_map.68 = f32[2,8,512]{2,1,0:T(8,128)} custom-call(bf16[2,160,2048]{2,1,0:T(8,128)(2,1)} %copy-done.1, bf16[2,160,2048]{2,1,0:T(8,128)(2,1)} %collective-permute-done.11.second_ref), custom_call_target="tpu_custom_call" | custom-call | tf_op jit(solution)/shard_map/pallas_call | solution.py:109
  290.4 0.8 broadcast_select_fusion.4
  291.2 1.3 collective-permute-start.17
  292.5 0.0 collective-permute-done.7
  292.5 1.3 collective-permute-start.13
  293.8 3.7 %collective-permute-done.17 = f32[2,8,512]{2,1,0:T(8,128)S(1)} collective-permute-done((f32[2,8,512]{2,1,0:T(8,128)S(1)}, f32[2,8,512]{2,1,0:T(8,128)S(1)}, u32[]{:S(2)}, u32[]{:S(2)}) %collective-permute-start.17) | collective-permute-done | bytes 32800 | tf_op jit(solution)/shard_map/ppermute | solution.py:37
  297.5 3.0 collective-permute-done.13
  300.6 0.7 maximum_bitcast_fusion
  (37 shorter events, 0.3 us)
Async XLA Ops:
  1.1 7.6 %collective-permute-start.1 = (bf16[1,2,16,4096]{3,2,1,0:T(8,128)(2,1)S(1)}, bf16[1,2,16,4096]{3,2,1,0:T(8,128)(2,1)S(1)}, u32[]{:S(2)}, u32[]{:S(2)}) collective-permute-start(bf16[1,2,16,4096]{3,2,1,0:T(8,128)(2,1)S(1)} %get-tuple-element.39), channel_id=1, source_target_pairs={{1,0},{2,1},{3,2},{5,4},{6,5},{7,6},{9,8},{10,9},{11,10},{13,12},{... | collective-permute-start | bytes 786440 | tf_op jit(solution)/shard_map/ppermute | solution.py:27
  2.4 6.3 %collective-permute-start = (bf16[1,2,16,4096]{3,2,1,0:T(8,128)(2,1)S(1)}, bf16[1,2,16,4096]{3,2,1,0:T(8,128)(2,1)S(1)}, u32[]{:S(2)}, u32[]{:S(2)}) collective-permute-start(bf16[1,2,16,4096]{3,2,1,0:T(8,128)(2,1)S(1)} %get-tuple-element.40), channel_id=1, source_target_pairs={{0,1},{1,2},{2,3},{4,5},{5,6},{6,7},{8,9},{9,10},{10,11},{12,13},{... | collective-permute-start | bytes 786440 | tf_op jit(solution)/shard_map/ppermute | solution.py:25
  70.4 34.4 %copy-start.2 = (bf16[2,20,8,4096]{3,2,1,0:T(8,128)(2,1)}, bf16[2,20,8,4096]{3,2,1,0:T(8,128)(2,1)S(1)}, u32[]{:S(2)}) copy-start(bf16[2,20,8,4096]{3,2,1,0:T(8,128)(2,1)S(1)} %copy.13) | copy-start | bytes 7864324
  70.6 108.0 %copy-start = (bf16[2,160,2048]{2,1,0:T(8,128)(2,1)}, bf16[2,160,2048]{2,1,0:T(8,128)(2,1)S(1)}, u32[]{:S(2)}) copy-start(bf16[2,160,2048]{2,1,0:T(8,128)(2,1)S(1)} %slice.333.first_ref) | copy-start | bytes 3932164
  70.6 115.0 %copy-start.9 = (s32[1,4]{1,0:T(1,128)S(1)}, s32[1,4]{1,0:T(1,128)}, u32[]{:S(2)}) copy-start(s32[1,4]{1,0:T(1,128)} %param.11) | copy-start | bytes 52
  70.6 34.3 %collective-permute-start.2 = (bf16[2,160,2048]{2,1,0:T(8,128)(2,1)S(1)}, bf16[2,160,2048]{2,1,0:T(8,128)(2,1)}, u32[]{:S(2)}, u32[]{:S(2)}) collective-permute-start(bf16[2,160,2048]{2,1,0:T(8,128)(2,1)S(1)} %slice.333.first_ref), channel_id=1, source_target_pairs={{8,0},{12,4},{16,8},{20,12},{24,16},{28,20},{9,1},{13,5},{17,9},{2... | collective-permute-start | bytes 3932168 | tf_op jit(solution)/shard_map/ppermute | solution.py:37
  104.9 33.6 %collective-permute-start.3 = (bf16[2,160,2048]{2,1,0:T(8,128)(2,1)}, bf16[2,160,2048]{2,1,0:T(8,128)(2,1)}, u32[]{:S(2)}, u32[]{:S(2)}) collective-permute-start(bf16[2,160,2048]{2,1,0:T(8,128)(2,1)} %collective-permute-done.2.second_ref), channel_id=1, source_target_pairs={{8,0},{12,4},{16,8},{20,12},{24,16},{28,20},{9,1},{13,5},{17,9},{2... | collective-permute-start | bytes 3932168 | tf_op jit(solution)/shard_map/ppermute | solution.py:37
  141.9 82.7 %copy-start.1 = (bf16[2,160,2048]{2,1,0:T(8,128)(2,1)}, bf16[2,160,2048]{2,1,0:T(8,128)(2,1)S(1)}, u32[]{:S(2)}) copy-start(bf16[2,160,2048]{2,1,0:T(8,128)(2,1)S(1)} %get-tuple-element.38.first_ref) | copy-start | bytes 3932164
  141.9 31.1 %collective-permute-start.5 = (bf16[2,160,2048]{2,1,0:T(8,128)(2,1)S(1)}, bf16[2,160,2048]{2,1,0:T(8,128)(2,1)}, u32[]{:S(2)}, u32[]{:S(2)}) collective-permute-start(bf16[2,160,2048]{2,1,0:T(8,128)(2,1)S(1)} %get-tuple-element.38.first_ref), channel_id=1, source_target_pairs={{0,8},{4,12},{8,16},{12,20},{16,24},{20,28},{1,9},{5,13},{9,17},{1... | collective-permute-start | bytes 3932168 | tf_op jit(solution)/shard_map/ppermute | solution.py:37
  146.6 68.1 %collective-permute-start.8 = (bf16[2,160,2048]{2,1,0:T(8,128)(2,1)}, bf16[2,160,2048]{2,1,0:T(8,128)(2,1)}, u32[]{:S(2)}, u32[]{:S(2)}) collective-permute-start(bf16[2,160,2048]{2,1,0:T(8,128)(2,1)} %collective-permute-done.2.second_ref), channel_id=1, source_target_pairs={{0,4},{4,0},{8,12},{12,8},{16,20},{20,16},{24,28},{28,24},{1,5},{5... | collective-permute-start | bytes 3932168 | tf_op jit(solution)/shard_map/ppermute | solution.py:42
  147.7 72.5 %collective-permute-start.9 = (bf16[2,160,2048]{2,1,0:T(8,128)(2,1)}, bf16[2,160,2048]{2,1,0:T(8,128)(2,1)}, u32[]{:S(2)}, u32[]{:S(2)}) collective-permute-start(bf16[2,160,2048]{2,1,0:T(8,128)(2,1)} %get-tuple-element.37), channel_id=1, source_target_pairs={{0,4},{4,0},{8,12},{12,8},{16,20},{20,16},{24,28},{28,24},{1,5},{5... | collective-permute-start | bytes 3932168 | tf_op jit(solution)/shard_map/ppermute | solution.py:42
  173.0 51.6 %collective-permute-start.6 = (bf16[2,160,2048]{2,1,0:T(8,128)(2,1)}, bf16[2,160,2048]{2,1,0:T(8,128)(2,1)}, u32[]{:S(2)}, u32[]{:S(2)}) collective-permute-start(bf16[2,160,2048]{2,1,0:T(8,128)(2,1)} %collective-permute-done.5.second_ref), channel_id=1, source_target_pairs={{0,8},{4,12},{8,16},{12,20},{16,24},{20,28},{1,9},{5,13},{9,17},{1... | collective-permute-start | bytes 3932168 | tf_op jit(solution)/shard_map/ppermute | solution.py:37
  182.9 23.6 %collective-permute-start.14 = (f32[2,8,512]{2,1,0:T(8,128)}, f32[2,8,512]{2,1,0:T(8,128)S(1)}, u32[]{:S(2)}, u32[]{:S(2)}) collective-permute-start(f32[2,8,512]{2,1,0:T(8,128)} %shard_map.70), channel_id=1, source_target_pairs={{0,8},{4,12},{8,16},{12,20},{16,24},{20,28},{1,9},{5,13},{9,17},{1... | collective-permute-start | bytes 98312 | tf_op jit(solution)/shard_map/ppermute | solution.py:37
  210.9 19.9 %collective-permute-start.4 = (f32[2,8,512]{2,1,0:T(8,128)}, f32[2,8,512]{2,1,0:T(8,128)S(1)}, u32[]{:S(2)}, u32[]{:S(2)}) collective-permute-start(f32[2,8,512]{2,1,0:T(8,128)} %shard_map.64), channel_id=1, source_target_pairs={{0,16},{4,20},{8,24},{12,28},{1,17},{5,21},{9,25},{13,29},{2,18},{... | collective-permute-start | bytes 98312 | tf_op jit(solution)/shard_map/ppermute | solution.py:37
  219.1 8.3 %copy-start.8 = (f32[2,8,512]{2,1,0:T(8,128)S(1)}, f32[2,8,512]{2,1,0:T(8,128)}, u32[]{:S(2)}) copy-start(f32[2,8,512]{2,1,0:T(8,128)} %shard_map.66) | copy-start | bytes 98308
  219.1 61.5 %collective-permute-start.12 = (bf16[2,160,2048]{2,1,0:T(8,128)(2,1)}, bf16[2,160,2048]{2,1,0:T(8,128)(2,1)S(1)}, u32[]{:S(2)}, u32[]{:S(2)}) collective-permute-start(bf16[2,160,2048]{2,1,0:T(8,128)(2,1)} %collective-permute-done.5.second_ref), channel_id=1, source_target_pairs={{0,4},{4,0},{8,12},{12,8},{16,20},{20,16},{24,28},{28,24},{1,5},{5... | collective-permute-start | bytes 3932168 | tf_op jit(solution)/shard_map/ppermute | solution.py:42
  226.1 59.9 %collective-permute-start.11 = (bf16[2,160,2048]{2,1,0:T(8,128)(2,1)S(1)}, bf16[2,160,2048]{2,1,0:T(8,128)(2,1)}, u32[]{:S(2)}, u32[]{:S(2)}) collective-permute-start(bf16[2,160,2048]{2,1,0:T(8,128)(2,1)S(1)} %broadcast_select_fusion), channel_id=1, source_target_pairs={{0,4},{4,0},{8,12},{12,8},{16,20},{20,16},{24,28},{28,24},{1,5},{5... | collective-permute-start | bytes 3932168 | tf_op jit(solution)/shard_map/ppermute | solution.py:42
  228.2 46.5 %collective-permute-start.16 = (f32[2,8,512]{2,1,0:T(8,128)S(1)}, f32[2,8,512]{2,1,0:T(8,128)S(1)}, u32[]{:S(2)}, u32[]{:S(2)}) collective-permute-start(f32[2,8,512]{2,1,0:T(8,128)S(1)} %get-tuple-element.42), channel_id=1, source_target_pairs={{0,4},{4,8},{8,12},{12,16},{16,20},{20,24},{24,28},{1,5},{5,9},{9,... | collective-permute-start | bytes 98312 | tf_op jit(solution)/shard_map/ppermute | solution.py:37
  230.9 69.6 %copy-start.4 = (f32[2,8,512]{2,1,0:T(8,128)S(1)}, f32[2,8,512]{2,1,0:T(8,128)}, u32[]{:S(2)}) copy-start(f32[2,8,512]{2,1,0:T(8,128)} %shard_map.70) | copy-start | bytes 98308
  230.9 69.6 %copy-start.5 = (f32[2,8,512]{2,1,0:T(8,128)S(1)}, f32[2,8,512]{2,1,0:T(8,128)}, u32[]{:S(2)}) copy-start(f32[2,8,512]{2,1,0:T(8,128)} %shard_map.64) | copy-start | bytes 98308
  230.9 43.9 %collective-permute-start.10 = (f32[2,8,512]{2,1,0:T(8,128)S(1)}, f32[2,8,512]{2,1,0:T(8,128)S(1)}, u32[]{:S(2)}, u32[]{:S(2)}) collective-permute-start(f32[2,8,512]{2,1,0:T(8,128)S(1)} %get-tuple-element.41), channel_id=1, source_target_pairs={{0,12},{4,16},{8,20},{12,24},{16,28},{1,13},{5,17},{9,21},{13,25},... | collective-permute-start | bytes 98312 | tf_op jit(solution)/shard_map/ppermute | solution.py:37
  237.4 63.0 %copy-start.6 = (f32[2,8,512]{2,1,0:T(8,128)S(1)}, f32[2,8,512]{2,1,0:T(8,128)}, u32[]{:S(2)}) copy-start(f32[2,8,512]{2,1,0:T(8,128)} %shard_map.71) | copy-start | bytes 98308
  237.4 37.3 %collective-permute-start.15 = (f32[2,8,512]{2,1,0:T(8,128)}, f32[2,8,512]{2,1,0:T(8,128)S(1)}, u32[]{:S(2)}, u32[]{:S(2)}) collective-permute-start(f32[2,8,512]{2,1,0:T(8,128)} %shard_map.71), channel_id=1, source_target_pairs={{8,0},{12,4},{16,8},{20,12},{24,16},{28,20},{9,1},{13,5},{17,9},{2... | collective-permute-start | bytes 98312 | tf_op jit(solution)/shard_map/ppermute | solution.py:37
  279.1 21.3 %copy-start.7 = (f32[2,8,512]{2,1,0:T(8,128)S(1)}, f32[2,8,512]{2,1,0:T(8,128)}, u32[]{:S(2)}) copy-start(f32[2,8,512]{2,1,0:T(8,128)} %shard_map.65) | copy-start | bytes 98308
  279.1 13.3 %collective-permute-start.7 = (f32[2,8,512]{2,1,0:T(8,128)}, f32[2,8,512]{2,1,0:T(8,128)S(1)}, u32[]{:S(2)}, u32[]{:S(2)}) collective-permute-start(f32[2,8,512]{2,1,0:T(8,128)} %shard_map.65), channel_id=1, source_target_pairs={{16,0},{20,4},{24,8},{28,12},{17,1},{21,5},{25,9},{29,13},{18,2},{... | collective-permute-start | bytes 98312 | tf_op jit(solution)/shard_map/ppermute | solution.py:37
  280.6 1.1 copy-start.3
  291.2 6.3 %collective-permute-start.17 = (f32[2,8,512]{2,1,0:T(8,128)S(1)}, f32[2,8,512]{2,1,0:T(8,128)S(1)}, u32[]{:S(2)}, u32[]{:S(2)}) collective-permute-start(f32[2,8,512]{2,1,0:T(8,128)S(1)} %get-tuple-element.44), channel_id=1, source_target_pairs={{4,0},{8,4},{12,8},{16,12},{20,16},{24,20},{28,24},{5,1},{9,5},{13... | collective-permute-start | bytes 98312 | tf_op jit(solution)/shard_map/ppermute | solution.py:37
  292.5 7.9 %collective-permute-start.13 = (f32[2,8,512]{2,1,0:T(8,128)S(1)}, f32[2,8,512]{2,1,0:T(8,128)S(1)}, u32[]{:S(2)}, u32[]{:S(2)}) collective-permute-start(f32[2,8,512]{2,1,0:T(8,128)S(1)} %get-tuple-element.43), channel_id=1, source_target_pairs={{12,0},{16,4},{20,8},{24,12},{28,16},{13,1},{17,5},{21,9},{25,13},... | collective-permute-start | bytes 98312 | tf_op jit(solution)/shard_map/ppermute | solution.py:37
where the time goes:
time: 303 us; the launch traced here: 301 us
  waiting for transfers between devices  132 us (44%)
  other arithmetic  64.8 us (21%)
  starting transfers between devices  38.4 us (13%)
  Pallas kernels  34.9 us (12%)
  between operations  22 us (7%)
  local copies, waits for them, and re-layouts  8.04 us (3%)
    ppermute x12, waiting for transfers between devices, shifted(): return lax.ppermute(block, axis, route)  132 us
    convert_element_type x1, other arithmetic, resample_block(): return result.astype(jnp.bfloat16)  43.5 us
    pallas_call x8, Pallas kernels, looks(): pl.pallas_call(looks_kernel, grid=(width // CHUNK,), in_specs=[spec, spec...  34.9 us
    ppermute x12, starting transfers between devices, shifted(): return lax.ppermute(block, axis, route)  29.6 us
    add x1, other arithmetic, resample_block(): along + weights[tap] * window[:, tap:tap + nlines, :].astype(jnp.float32)  10.3 us
  transfers between devices with their start and end apart: 18, of which 6 were waited for; matrix products, arithmetic and copies ran while one was open for 2% of the time, Pallas kernels for 12%

commit v1 on v0

--- a/solution.py
+++ b/solution.py
@@ -67,14 +67,16 @@
     )
     range_weights = jnp.dot(selector, table, precision=lax.Precision.HIGHEST)
     targets = shift_range[:, None] + jnp.arange(8, dtype=jnp.int32)[None, :] - 3
-    result = jnp.zeros((2, nlines, nrange), jnp.float32)
-    for offset in range(-OFFRG - 3, OFFRG + 5):
-        coeff = jnp.sum(jnp.where(targets == offset, range_weights, 0.0), axis=1)
-        result = (
-            result
-            + coeff[None, :, None] * widened[:, :, margin + offset : margin + offset + nrange]
-        )
-    return result.astype(jnp.bfloat16)
+    half = nrange // 2
+    halves = []
+    for first in (0, half):
+        result = jnp.zeros((2, nlines, half), jnp.float32)
+        for offset in range(-OFFRG - 3, OFFRG + 5):
+            coeff = jnp.sum(jnp.where(targets == offset, range_weights, 0.0), axis=1)
+            low = margin + first + offset
+            result = result + coeff[None, :, None] * widened[:, :, low : low + half]
+        halves.append(look_order(result.astype(jnp.bfloat16)))
+    return halves
 
 
 CHUNK = 512
@@ -127,42 +129,30 @@
 
 def shards(slc, az_offset, az_kernel, rg_offset, rg_kernel, partners):
     padded = padded_2(slc, (("az", 2),), OFFAZ + 4)
-    resampled = resample_block(padded[0], az_offset[0], az_kernel[0], rg_offset[0], rg_kernel[0])
-    resampled = look_order(resampled)
-    half = resampled.shape[2] // 2
-    own_left = resampled[:, :, :half]
-    own_right = resampled[:, :, half:]
+    own_left, own_right = resample_block(padded[0], az_offset[0], az_kernel[0], rg_offset[0], rg_kernel[0])
     date = lax.axis_index("date")
     even = date % 2 == 0
 
     left_2 = shifted(own_left, "date", 2)
+    left_1 = swapped(jnp.where(even, left_2, own_left), "date")
     left_4 = shifted(left_2, "date", 2)
-    left_a = swapped(left_2, "date")
-    left_x = swapped(jnp.where(even, left_4, own_left), "date")
+    left_3 = shifted(left_1, "date", 2)
     right_2 = shifted(own_right, "date", -2)
+    right_1 = swapped(jnp.where(even, own_right, right_2), "date")
     right_4 = shifted(right_2, "date", -2)
-    right_a = swapped(right_2, "date")
-    right_x = swapped(jnp.where(even, own_right, right_4), "date")
+    right_3 = shifted(right_1, "date", -2)
 
-    ahead_2 = looks(own_left, left_2)
-    ahead_4 = looks(own_left, left_4)
-    ahead_a = looks(own_left, left_a)
-    ahead_x = looks(own_left, left_x)
-    behind_2 = looks(own_right, right_2)
-    behind_4 = looks(own_right, right_4)
-    behind_a = looks(own_right, right_a)
-    behind_x = looks(own_right, right_x)
     ahead = {
-        1: jnp.where(even, ahead_x, ahead_a),
-        2: ahead_2,
-        3: jnp.where(even, ahead_a, ahead_x),
-        4: ahead_4,
+        1: looks(own_left, left_1),
+        2: looks(own_left, left_2),
+        3: looks(own_left, left_3),
+        4: looks(own_left, left_4),
     }
     behind = {
-        1: jnp.where(even, behind_a, behind_x),
-        2: behind_2,
-        3: jnp.where(even, behind_x, behind_a),
-        4: behind_4,
+        1: looks(own_right, right_1),
+        2: looks(own_right, right_2),
+        3: looks(own_right, right_3),
+        4: looks(own_right, right_4),
     }
     full = {}
     for s in range(1, GAP + 1):

time: 303 us -> 235 us (0.78)
  waiting for transfers between devices: 132 us -> 47.9 us
  starting transfers between devices: 38.4 us -> 49.6 us
  other arithmetic: 64.8 us -> 68.5 us
    ppermute x12 -> x14, waiting for transfers between devices: 132 us -> 47.9 us  [shifted(): return lax.ppermute(block, axis, route)]
    ppermute x12 -> x14, starting transfers between devices: 29.6 us -> 43.1 us  [shifted(): return lax.ppermute(block, axis, route)]
    convert_element_type x1 -> x2, other arithmetic: 43.5 us -> 44.1 us  [resample_block(): halves.append(look_order(result.astype(jnp.bfloat16)))]
    select_n x4 -> x2, other arithmetic: 6.4 us -> 6.66 us  [the longest x1 3.84 us: shards(): right_1 = swapped(jnp.where(even, own_right, right_2), 'date')]
  transfers between devices with their start and end apart: 18 -> 18, of which waited for: 6 -> 7; matrix products, arithmetic and copies ran while one was open for 2% -> 14% of each run, Pallas kernels for 12% -> 15%
where the time goes in v1:
time: 235 us; the launch traced here: 234 us
  other arithmetic  68.5 us (29%)
  starting transfers between devices  49.6 us (21%)
  waiting for transfers between devices  47.9 us (20%)
  Pallas kernels  35 us (15%)
  between operations  22.4 us (10%)
  local copies, waits for them, and re-layouts  9.1 us (4%)
    ppermute x14, waiting for transfers between devices, shifted(): return lax.ppermute(block, axis, route)  47.9 us
    convert_element_type x2, other arithmetic, resample_block(): halves.append(look_order(result.astype(jnp.bfloat16)))  44.1 us
    ppermute x14, starting transfers between devices, shifted(): return lax.ppermute(block, axis, route)  43.1 us
    pallas_call x8, Pallas kernels, looks(): pl.pallas_call(looks_kernel, grid=(width // CHUNK,), in_specs=[spec, spec...  35 us
    add x1, other arithmetic, resample_block(): along + weights[tap] * window[:, tap:tap + nlines, :].astype(jnp.float32)  10.1 us
  transfers between devices with their start and end apart: 18, of which 7 were waited for; matrix products, arithmetic and copies ran while one was open for 14% of the time, Pallas kernels for 15%

profile of v1, /device:TPU:0, one launch (start us, length us, event | category | flops | bytes accessed | tf_op | source)
XLA Modules:
  0.0 233.5 jit_solution(3187973299729815051)
XLA Ops:
  0.0 1.1 fusion.146
  1.1 1.3 collective-permute-start.1
  2.4 3.0 %collective-permute-start = (bf16[1,2,16,4096]{3,2,1,0:T(8,128)(2,1)S(1)}, bf16[1,2,16,4096]{3,2,1,0:T(8,128)(2,1)S(1)}, u32[]{:S(2)}, u32[]{:S(2)}) collective-permute-start(bf16[1,2,16,4096]{3,2,1,0:T(8,128)(2,1)S(1)} %get-tuple-element.38), channel_id=1, source_target_pairs={{0,1},{1,2},{2,3},{4,5},{5,6},{6,7},{8,9},{9,10},{10,11},{12,13},{... | collective-permute-start | bytes 786440 | tf_op jit(solution)/shard_map/ppermute | solution.py:25
  6.1 0.1 fusion.111
  6.2 0.1 constant_dynamic-slice_fusion
  6.9 0.6 fusion.155
  7.6 1.1 select_reduce_fusion.31
  8.7 0.0 collective-permute-done.1
  8.7 3.5 %fusion.2 = bf16[2,167,4096]{2,1,0:T(8,128)(2,1)S(1)} fusion(s32[]{:T(128)S(6)} %select_n.612, bf16[1,2,16,4096]{3,2,1,0:T(8,128)(2,1)S(1)} %collective-permute-done, bf16[1,2,160,4096]{3,2,1,0:T(8,128)(2,1)} %param.6, bf16[1,2,16,4096]{3,2,1,0:T(8,128)(2,1)S(1)} %collective-permute-done.1), kind=kLoop, calls=%fused_computation.6 | loop fusion | flops 8208384 | bytes 5881860 | tf_op jit(solution)/shard_map/dynamic_slice | solution.py:58
  12.2 10.1 %multiply_add_fusion = f32[2,160,4096]{2,1,0:T(8,128)S(1)} fusion(bf16[2,167,4096]{2,1,0:T(8,128)(2,1)S(1)} %fusion.2, f32[]{:T(128)} %bitcast.14, f32[]{:T(128)} %bitcast.13, f32[]{:T(128)} %bitcast.12, f32[]{:T(128)} %bitcast.11, f32[]{:T(128)} %bitcast.10, f32[]{:T(128)} %bitcast.9, f32[]{:T(128)} %bitcast.8, f32[]{:T(128)} %bitcast.4), kind=kLoop, calls=%fused_computation | loop fusion | flops 30146560 | bytes 26214432 | tf_op jit(solution)/shard_map/add | solution.py:62
  22.3 22.1 %fusion.71 = bf16[2,160,2048]{2,1,0:T(8,128)(2,1)S(1)} fusion(f32[2,160,4096]{2,1,0:T(8,128)S(1)} %multiply_add_fusion, f32[160]{0:T(256)S(1)} %get-tuple-element.6, f32[160]{0:T(256)S(1)} %get-tuple-element.7, f32[160]{0:T(256)S(1)} %get-tuple-element.8, f32[160]{0:T(256)S(1)} %get-tuple-element.9, f32[160]{0:T(256)S(1)} %get-tuple-element.10, ...), kind=kLoop, calls=%fused_computation.118 | loop fusion | flops 41943040 | bytes 48529408 | tf_op jit(solution)/shard_map/convert_element_type | solution.py:78
  44.4 1.3 copy.15
  45.8 0.7 copy.23
  46.5 6.0 %collective-permute-start.5 = (bf16[2,160,2048]{2,1,0:T(8,128)(2,1)S(1)}, bf16[2,160,2048]{2,1,0:T(8,128)(2,1)}, u32[]{:S(2)}, u32[]{:S(2)}) collective-permute-start(bf16[2,160,2048]{2,1,0:T(8,128)(2,1)S(1)} %bitcast.64), channel_id=1, source_target_pairs={{0,8},{4,12},{8,16},{12,20},{16,24},{20,28},{1,9},{5,13},{9,17},{1... | collective-permute-start | bytes 3932168 | tf_op jit(solution)/shard_map/ppermute | solution.py:37
  52.5 22.0 %fusion.35 = bf16[2,160,2048]{2,1,0:T(8,128)(2,1)S(1)} fusion(f32[2,160,4096]{2,1,0:T(8,128)S(1)} %multiply_add_fusion, f32[160]{0:T(256)S(1)} %get-tuple-element.6, f32[160]{0:T(256)S(1)} %get-tuple-element.7, f32[160]{0:T(256)S(1)} %get-tuple-element.8, f32[160]{0:T(256)S(1)} %get-tuple-element.9, f32[160]{0:T(256)S(1)} %get-tuple-element.10, ...), kind=kLoop, calls=%fused_computation.56 | loop fusion | flops 41943040 | bytes 51150848 | tf_op jit(solution)/shard_map/convert_element_type | solution.py:78
  74.6 1.3 copy.13
  75.9 0.7 copy.24
  76.7 0.3 copy-done.3
  77.0 1.3 collective-permute-start.2
  78.3 2.1 collective-permute-done.5.second_ref
  80.5 3.8 %broadcast_select_fusion = bf16[2,160,2048]{2,1,0:T(8,128)(2,1)} fusion(bf16[2,160,2048]{2,1,0:T(8,128)(2,1)} %collective-permute-done.5.second_ref, pred[]{:T(512)S(6)} %eq.309, bf16[2,20,8,2048]{3,0,1,2:T(2,128)(2,1)} %bitcast.75), kind=kLoop, calls=%fused_computation.121 | loop fusion | flops 655360 | bytes 3932161 | tf_op jit(solution)/shard_map/jit(_where)/select_n | solution.py:141
  84.3 1.9 collective-permute-start.11
  86.2 5.7 %collective-permute-start.6 = (bf16[2,160,2048]{2,1,0:T(8,128)(2,1)}, bf16[2,160,2048]{2,1,0:T(8,128)(2,1)}, u32[]{:S(2)}, u32[]{:S(2)}) collective-permute-start(bf16[2,160,2048]{2,1,0:T(8,128)(2,1)} %collective-permute-done.5.second_ref), channel_id=1, source_target_pairs={{0,8},{4,12},{8,16},{12,20},{16,24},{20,28},{1,9},{5,13},{9,17},{1... | collective-permute-start | bytes 3932168 | tf_op jit(solution)/shard_map/ppermute | solution.py:37
  91.9 18.6 %collective-permute-done.2.second_ref = bf16[2,160,2048]{2,1,0:T(8,128)(2,1)} collective-permute-done((bf16[2,160,2048]{2,1,0:T(8,128)(2,1)S(1)}, bf16[2,160,2048]{2,1,0:T(8,128)(2,1)}, u32[]{:S(2)}, u32[]{:S(2)}) %collective-permute-start.2) | collective-permute-done | bytes 1310752 | tf_op jit(solution)/shard_map/ppermute | solution.py:37
  110.5 2.8 %broadcast_select_fusion.1 = bf16[2,160,2048]{2,1,0:T(8,128)(2,1)S(1)} fusion(bf16[2,160,2048]{2,1,0:T(8,128)(2,1)} %collective-permute-done.2.second_ref, pred[]{:T(512)S(6)} %eq.309, bf16[2,20,8,2048]{3,0,1,2:T(2,128)(2,1)S(1)} %bitcast.77), kind=kLoop, calls=%fused_computation.122 | loop fusion | flops 655360 | bytes 3932161 | tf_op jit(solution)/shard_map/jit(_where)/select_n | solution.py:137
  113.3 0.3 collective-permute-start.8
  113.6 1.3 collective-permute-start.3
  114.9 4.4 %shard_map.69 = f32[2,8,512]{2,1,0:T(8,128)} custom-call(bf16[2,160,2048]{2,1,0:T(8,128)(2,1)} %bitcast.65, bf16[2,160,2048]{2,1,0:T(8,128)(2,1)} %collective-permute-done.5.second_ref), custom_call_target="tpu_custom_call" | custom-call | tf_op jit(solution)/shard_map/pallas_call | solution.py:111
  119.3 1.3 collective-permute-start.15
  120.6 0.6 fusion.156
  141.7 4.4 %shard_map.68 = f32[2,8,512]{2,1,0:T(8,128)} custom-call(bf16[2,160,2048]{2,1,0:T(8,128)(2,1)} %bitcast.70, bf16[2,160,2048]{2,1,0:T(8,128)(2,1)} %collective-permute-done.2.second_ref), custom_call_target="tpu_custom_call" | custom-call | tf_op jit(solution)/shard_map/pallas_call | solution.py:111
  146.1 0.8 collective-permute-done.15
  146.9 4.6 %collective-permute-start.14 = (f32[2,8,512]{2,1,0:T(8,128)}, f32[2,8,512]{2,1,0:T(8,128)S(1)}, u32[]{:S(2)}, u32[]{:S(2)}) collective-permute-start(f32[2,8,512]{2,1,0:T(8,128)} %shard_map.68), channel_id=1, source_target_pairs={{0,8},{4,12},{8,16},{12,20},{16,24},{20,28},{1,9},{5,13},{9,17},{1... | collective-permute-start | bytes 98312 | tf_op jit(solution)/shard_map/ppermute | solution.py:37
  151.5 1.6 collective-permute-done.14
  153.1 0.0 collective-permute-done.11.second_ref
  153.1 4.4 %shard_map.71 = f32[2,8,512]{2,1,0:T(8,128)} custom-call(bf16[2,160,2048]{2,1,0:T(8,128)(2,1)} %bitcast.66, bf16[2,160,2048]{2,1,0:T(8,128)(2,1)} %collective-permute-done.11.second_ref), custom_call_target="tpu_custom_call" | custom-call | tf_op jit(solution)/shard_map/pallas_call | solution.py:111
  157.5 1.3 collective-permute-start.17
  158.8 6.9 %collective-permute-start.12 = (bf16[2,160,2048]{2,1,0:T(8,128)(2,1)}, bf16[2,160,2048]{2,1,0:T(8,128)(2,1)}, u32[]{:S(2)}, u32[]{:S(2)}) collective-permute-start(bf16[2,160,2048]{2,1,0:T(8,128)(2,1)} %collective-permute-done.11.second_ref), channel_id=1, source_target_pairs={{0,8},{4,12},{8,16},{12,20},{16,24},{20,28},{1,9},{5,13},{9,17},{1... | collective-permute-start | bytes 3932168 | tf_op jit(solution)/shard_map/ppermute | solution.py:37
  165.7 0.0 collective-permute-done.6.second_ref
  165.7 4.4 %shard_map.65 = f32[2,8,512]{2,1,0:T(8,128)} custom-call(bf16[2,160,2048]{2,1,0:T(8,128)(2,1)} %bitcast.67, bf16[2,160,2048]{2,1,0:T(8,128)(2,1)} %collective-permute-done.6.second_ref), custom_call_target="tpu_custom_call" | custom-call | tf_op jit(solution)/shard_map/pallas_call | solution.py:111
  170.1 1.3 collective-permute-start.7
  171.4 4.4 %shard_map.70 = f32[2,8,512]{2,1,0:T(8,128)} custom-call(bf16[2,160,2048]{2,1,0:T(8,128)(2,1)} %bitcast.71, bf16[2,160,2048]{2,1,0:T(8,128)(2,1)} %collective-permute-done.8.second_ref), custom_call_target="tpu_custom_call" | custom-call | tf_op jit(solution)/shard_map/pallas_call | solution.py:111
  175.7 2.9 %collective-permute-start.16 = (f32[2,8,512]{2,1,0:T(8,128)}, f32[2,8,512]{2,1,0:T(8,128)S(1)}, u32[]{:S(2)}, u32[]{:S(2)}) collective-permute-start(f32[2,8,512]{2,1,0:T(8,128)} %shard_map.70), channel_id=1, source_target_pairs={{0,4},{4,8},{8,12},{12,16},{16,20},{20,24},{24,28},{1,5},{5,9},{9,... | collective-permute-start | bytes 98312 | tf_op jit(solution)/shard_map/ppermute | solution.py:37
  178.6 0.0 collective-permute-done.3.second_ref
  178.6 1.1 copy-done.5
  179.7 4.4 %shard_map.64 = f32[2,8,512]{2,1,0:T(8,128)} custom-call(bf16[2,160,2048]{2,1,0:T(8,128)(2,1)} %bitcast.72, bf16[2,160,2048]{2,1,0:T(8,128)(2,1)} %copy-done.5), custom_call_target="tpu_custom_call" | custom-call | tf_op jit(solution)/shard_map/pallas_call | solution.py:111
  184.1 5.4 %collective-permute-start.4 = (f32[2,8,512]{2,1,0:T(8,128)}, f32[2,8,512]{2,1,0:T(8,128)S(1)}, u32[]{:S(2)}, u32[]{:S(2)}) collective-permute-start(f32[2,8,512]{2,1,0:T(8,128)} %shard_map.64), channel_id=1, source_target_pairs={{0,16},{4,20},{8,24},{12,28},{1,17},{5,21},{9,25},{13,29},{2,18},{... | collective-permute-start | bytes 98312 | tf_op jit(solution)/shard_map/ppermute | solution.py:37
  189.5 0.0 collective-permute-done.17
  189.5 1.3 collective-permute-start.9
  190.8 0.0 collective-permute-done.7
  190.9 1.2 collective-permute-done.4
  192.1 0.0 copy-start.9
  192.2 4.4 %shard_map.67 = f32[2,8,512]{2,1,0:T(8,128)} custom-call(bf16[2,160,2048]{2,1,0:T(8,128)(2,1)} %bitcast.68, bf16[2,160,2048]{2,1,0:T(8,128)(2,1)} %collective-permute-done.12.second_ref), custom_call_target="tpu_custom_call" | custom-call | tf_op jit(solution)/shard_map/pallas_call | solution.py:111
  196.6 1.4 collective-permute-start.13
  198.0 21.6 %collective-permute-done.9.second_ref = bf16[2,160,2048]{2,1,0:T(8,128)(2,1)S(1)} collective-permute-done((bf16[2,160,2048]{2,1,0:T(8,128)(2,1)}, bf16[2,160,2048]{2,1,0:T(8,128)(2,1)S(1)}, u32[]{:S(2)}, u32[]{:S(2)}) %collective-permute-start.9) | collective-permute-done | bytes 1310752 | tf_op jit(solution)/shard_map/ppermute | solution.py:37
  219.6 1.1 copy-done.6
  220.7 4.4 %shard_map.66 = f32[2,8,512]{2,1,0:T(8,128)} custom-call(bf16[2,160,2048]{2,1,0:T(8,128)(2,1)} %bitcast.73, bf16[2,160,2048]{2,1,0:T(8,128)(2,1)} %copy-done.6), custom_call_target="tpu_custom_call" | custom-call | tf_op jit(solution)/shard_map/pallas_call | solution.py:111
  225.1 2.6 %collective-permute-start.10 = (f32[2,8,512]{2,1,0:T(8,128)}, f32[2,8,512]{2,1,0:T(8,128)S(1)}, u32[]{:S(2)}, u32[]{:S(2)}) collective-permute-start(f32[2,8,512]{2,1,0:T(8,128)} %shard_map.66), channel_id=1, source_target_pairs={{0,12},{4,16},{8,20},{12,24},{16,28},{1,13},{5,17},{9,21},{13,25},... | collective-permute-start | bytes 98312 | tf_op jit(solution)/shard_map/ppermute | solution.py:37
  227.7 1.9 collective-permute-done.10
  229.6 0.8 select_select_fusion.2
  230.4 0.8 select_select_fusion.1
  231.2 0.8 select_select_fusion
  232.0 0.8 select_select_fusion.3
  232.8 0.7 maximum_bitcast_fusion
  (49 shorter events, 0.2 us)
Async XLA Ops:
  1.1 7.6 %collective-permute-start.1 = (bf16[1,2,16,4096]{3,2,1,0:T(8,128)(2,1)S(1)}, bf16[1,2,16,4096]{3,2,1,0:T(8,128)(2,1)S(1)}, u32[]{:S(2)}, u32[]{:S(2)}) collective-permute-start(bf16[1,2,16,4096]{3,2,1,0:T(8,128)(2,1)S(1)} %get-tuple-element.37), channel_id=1, source_target_pairs={{1,0},{2,1},{3,2},{5,4},{6,5},{7,6},{9,8},{10,9},{11,10},{13,12},{... | collective-permute-start | bytes 786440 | tf_op jit(solution)/shard_map/ppermute | solution.py:27
  2.4 6.3 %collective-permute-start = (bf16[1,2,16,4096]{3,2,1,0:T(8,128)(2,1)S(1)}, bf16[1,2,16,4096]{3,2,1,0:T(8,128)(2,1)S(1)}, u32[]{:S(2)}, u32[]{:S(2)}) collective-permute-start(bf16[1,2,16,4096]{3,2,1,0:T(8,128)(2,1)S(1)} %get-tuple-element.38), channel_id=1, source_target_pairs={{0,1},{1,2},{2,3},{4,5},{5,6},{6,7},{8,9},{9,10},{10,11},{12,13},{... | collective-permute-start | bytes 786440 | tf_op jit(solution)/shard_map/ppermute | solution.py:25
  45.8 28.8 %copy-start.2 = (bf16[2,160,2048]{2,0,1:T(2,128)(2,1)}, bf16[2,160,2048]{2,0,1:T(2,128)(2,1)S(1)}, u32[]{:S(2)}) copy-start(bf16[2,160,2048]{2,0,1:T(2,128)(2,1)S(1)} %copy.15) | copy-start | bytes 3932164
  46.5 28.0 %copy-start = (bf16[2,20,8,2048]{3,2,1,0:T(8,128)(2,1)}, bf16[2,20,8,2048]{3,2,1,0:T(8,128)(2,1)S(1)}, u32[]{:S(2)}) copy-start(bf16[2,20,8,2048]{3,2,1,0:T(8,128)(2,1)S(1)} %copy.23) | copy-start | bytes 3932164
  46.5 33.9 %collective-permute-start.5 = (bf16[2,160,2048]{2,1,0:T(8,128)(2,1)S(1)}, bf16[2,160,2048]{2,1,0:T(8,128)(2,1)}, u32[]{:S(2)}, u32[]{:S(2)}) collective-permute-start(bf16[2,160,2048]{2,1,0:T(8,128)(2,1)S(1)} %bitcast.64), channel_id=1, source_target_pairs={{0,8},{4,12},{8,16},{12,20},{16,24},{20,28},{1,9},{5,13},{9,17},{1... | collective-permute-start | bytes 3932168 | tf_op jit(solution)/shard_map/ppermute | solution.py:37
  75.9 1.1 copy-start.3
  77.0 36.3 %copy-start.1 = (bf16[2,20,8,2048]{3,2,1,0:T(8,128)(2,1)}, bf16[2,20,8,2048]{3,2,1,0:T(8,128)(2,1)S(1)}, u32[]{:S(2)}) copy-start(bf16[2,20,8,2048]{3,2,1,0:T(8,128)(2,1)S(1)} %copy.24) | copy-start | bytes 3932164
  77.0 33.5 %collective-permute-start.2 = (bf16[2,160,2048]{2,1,0:T(8,128)(2,1)S(1)}, bf16[2,160,2048]{2,1,0:T(8,128)(2,1)}, u32[]{:S(2)}, u32[]{:S(2)}) collective-permute-start(bf16[2,160,2048]{2,1,0:T(8,128)(2,1)S(1)} %bitcast.69), channel_id=1, source_target_pairs={{8,0},{12,4},{16,8},{20,12},{24,16},{28,20},{9,1},{13,5},{17,9},{2... | collective-permute-start | bytes 3932168 | tf_op jit(solution)/shard_map/ppermute | solution.py:37
  78.3 32.2 %copy-start.4 = (bf16[2,160,2048]{2,0,1:T(2,128)(2,1)S(1)}, bf16[2,160,2048]{2,0,1:T(2,128)(2,1)}, u32[]{:S(2)}) copy-start(bf16[2,160,2048]{2,0,1:T(2,128)(2,1)} %copy-done.3) | copy-start | bytes 3932164
  84.3 36.2 %copy-start.14 = (s32[1,4]{1,0:T(1,128)S(1)}, s32[1,4]{1,0:T(1,128)}, u32[]{:S(2)}) copy-start(s32[1,4]{1,0:T(1,128)} %param.11) | copy-start | bytes 52
  84.3 68.8 %collective-permute-start.11 = (bf16[2,160,2048]{2,1,0:T(8,128)(2,1)}, bf16[2,160,2048]{2,1,0:T(8,128)(2,1)}, u32[]{:S(2)}, u32[]{:S(2)}) collective-permute-start(bf16[2,160,2048]{2,1,0:T(8,128)(2,1)} %broadcast_select_fusion), channel_id=1, source_target_pairs={{0,4},{4,0},{8,12},{12,8},{16,20},{20,16},{24,28},{28,24},{1,5},{5... | collective-permute-start | bytes 3932168 | tf_op jit(solution)/shard_map/ppermute | solution.py:42
  86.2 79.5 %collective-permute-start.6 = (bf16[2,160,2048]{2,1,0:T(8,128)(2,1)}, bf16[2,160,2048]{2,1,0:T(8,128)(2,1)}, u32[]{:S(2)}, u32[]{:S(2)}) collective-permute-start(bf16[2,160,2048]{2,1,0:T(8,128)(2,1)} %collective-permute-done.5.second_ref), channel_id=1, source_target_pairs={{0,8},{4,12},{8,16},{12,20},{16,24},{20,28},{1,9},{5,13},{9,17},{1... | collective-permute-start | bytes 3932168 | tf_op jit(solution)/shard_map/ppermute | solution.py:37
  113.3 58.0 %collective-permute-start.8 = (bf16[2,160,2048]{2,1,0:T(8,128)(2,1)S(1)}, bf16[2,160,2048]{2,1,0:T(8,128)(2,1)}, u32[]{:S(2)}, u32[]{:S(2)}) collective-permute-start(bf16[2,160,2048]{2,1,0:T(8,128)(2,1)S(1)} %broadcast_select_fusion.1), channel_id=1, source_target_pairs={{0,4},{4,0},{8,12},{12,8},{16,20},{20,16},{24,28},{28,24},{1,5},{5... | collective-permute-start | bytes 3932168 | tf_op jit(solution)/shard_map/ppermute | solution.py:42
  113.6 65.0 %collective-permute-start.3 = (bf16[2,160,2048]{2,1,0:T(8,128)(2,1)}, bf16[2,160,2048]{2,1,0:T(8,128)(2,1)S(1)}, u32[]{:S(2)}, u32[]{:S(2)}) collective-permute-start(bf16[2,160,2048]{2,1,0:T(8,128)(2,1)} %collective-permute-done.2.second_ref), channel_id=1, source_target_pairs={{8,0},{12,4},{16,8},{20,12},{24,16},{28,20},{9,1},{13,5},{17,9},{2... | collective-permute-start | bytes 3932168 | tf_op jit(solution)/shard_map/ppermute | solution.py:37
  119.3 27.6 %collective-permute-start.15 = (f32[2,8,512]{2,1,0:T(8,128)}, f32[2,8,512]{2,1,0:T(8,128)S(1)}, u32[]{:S(2)}, u32[]{:S(2)}) collective-permute-start(f32[2,8,512]{2,1,0:T(8,128)} %shard_map.69), channel_id=1, source_target_pairs={{8,0},{12,4},{16,8},{20,12},{24,16},{28,20},{9,1},{13,5},{17,9},{2... | collective-permute-start | bytes 98312 | tf_op jit(solution)/shard_map/ppermute | solution.py:37
  146.9 6.3 %collective-permute-start.14 = (f32[2,8,512]{2,1,0:T(8,128)}, f32[2,8,512]{2,1,0:T(8,128)S(1)}, u32[]{:S(2)}, u32[]{:S(2)}) collective-permute-start(f32[2,8,512]{2,1,0:T(8,128)} %shard_map.68), channel_id=1, source_target_pairs={{0,8},{4,12},{8,16},{12,20},{16,24},{20,28},{1,9},{5,13},{9,17},{1... | collective-permute-start | bytes 98312 | tf_op jit(solution)/shard_map/ppermute | solution.py:37
  157.5 32.0 %collective-permute-start.17 = (f32[2,8,512]{2,1,0:T(8,128)}, f32[2,8,512]{2,1,0:T(8,128)S(1)}, u32[]{:S(2)}, u32[]{:S(2)}) collective-permute-start(f32[2,8,512]{2,1,0:T(8,128)} %shard_map.71), channel_id=1, source_target_pairs={{4,0},{8,4},{12,8},{16,12},{20,16},{24,20},{28,24},{5,1},{9,5},{13... | collective-permute-start | bytes 98312 | tf_op jit(solution)/shard_map/ppermute | solution.py:37
  158.8 33.3 %collective-permute-start.12 = (bf16[2,160,2048]{2,1,0:T(8,128)(2,1)}, bf16[2,160,2048]{2,1,0:T(8,128)(2,1)}, u32[]{:S(2)}, u32[]{:S(2)}) collective-permute-start(bf16[2,160,2048]{2,1,0:T(8,128)(2,1)} %collective-permute-done.11.second_ref), channel_id=1, source_target_pairs={{0,8},{4,12},{8,16},{12,20},{16,24},{20,28},{1,9},{5,13},{9,17},{1... | collective-permute-start | bytes 3932168 | tf_op jit(solution)/shard_map/ppermute | solution.py:37
  170.1 20.8 %collective-permute-start.7 = (f32[2,8,512]{2,1,0:T(8,128)}, f32[2,8,512]{2,1,0:T(8,128)S(1)}, u32[]{:S(2)}, u32[]{:S(2)}) collective-permute-start(f32[2,8,512]{2,1,0:T(8,128)} %shard_map.65), channel_id=1, source_target_pairs={{16,0},{20,4},{24,8},{28,12},{17,1},{21,5},{25,9},{29,13},{18,2},{... | collective-permute-start | bytes 98312 | tf_op jit(solution)/shard_map/ppermute | solution.py:37
  175.7 15.1 %collective-permute-start.16 = (f32[2,8,512]{2,1,0:T(8,128)}, f32[2,8,512]{2,1,0:T(8,128)S(1)}, u32[]{:S(2)}, u32[]{:S(2)}) collective-permute-start(f32[2,8,512]{2,1,0:T(8,128)} %shard_map.70), channel_id=1, source_target_pairs={{0,4},{4,8},{8,12},{12,16},{16,20},{20,24},{24,28},{1,5},{5,9},{9,... | collective-permute-start | bytes 98312 | tf_op jit(solution)/shard_map/ppermute | solution.py:37
  178.6 1.1 copy-start.5
  184.1 8.0 %collective-permute-start.4 = (f32[2,8,512]{2,1,0:T(8,128)}, f32[2,8,512]{2,1,0:T(8,128)S(1)}, u32[]{:S(2)}, u32[]{:S(2)}) collective-permute-start(f32[2,8,512]{2,1,0:T(8,128)} %shard_map.64), channel_id=1, source_target_pairs={{0,16},{4,20},{8,24},{12,28},{1,17},{5,21},{9,25},{13,29},{2,18},{... | collective-permute-start | bytes 98312 | tf_op jit(solution)/shard_map/ppermute | solution.py:37
  189.5 30.1 %collective-permute-start.9 = (bf16[2,160,2048]{2,1,0:T(8,128)(2,1)}, bf16[2,160,2048]{2,1,0:T(8,128)(2,1)S(1)}, u32[]{:S(2)}, u32[]{:S(2)}) collective-permute-start(bf16[2,160,2048]{2,1,0:T(8,128)(2,1)} %collective-permute-done.8.second_ref), channel_id=1, source_target_pairs={{8,0},{12,4},{16,8},{20,12},{24,16},{28,20},{9,1},{13,5},{17,9},{2... | collective-permute-start | bytes 3932168 | tf_op jit(solution)/shard_map/ppermute | solution.py:37
  192.1 37.4 %copy-start.7 = (f32[2,8,512]{2,1,0:T(8,128)S(1)}, f32[2,8,512]{2,1,0:T(8,128)}, u32[]{:S(2)}) copy-start(f32[2,8,512]{2,1,0:T(8,128)} %shard_map.69) | copy-start | bytes 98308
  192.1 37.4 %copy-start.8 = (f32[2,8,512]{2,1,0:T(8,128)S(1)}, f32[2,8,512]{2,1,0:T(8,128)}, u32[]{:S(2)}) copy-start(f32[2,8,512]{2,1,0:T(8,128)} %shard_map.68) | copy-start | bytes 98308
  192.1 37.4 %copy-start.9 = (f32[2,8,512]{2,1,0:T(8,128)S(1)}, f32[2,8,512]{2,1,0:T(8,128)}, u32[]{:S(2)}) copy-start(f32[2,8,512]{2,1,0:T(8,128)} %shard_map.71) | copy-start | bytes 98308
  192.1 37.4 %copy-start.10 = (f32[2,8,512]{2,1,0:T(8,128)S(1)}, f32[2,8,512]{2,1,0:T(8,128)}, u32[]{:S(2)}) copy-start(f32[2,8,512]{2,1,0:T(8,128)} %shard_map.65) | copy-start | bytes 98308
  192.1 37.4 %copy-start.11 = (f32[2,8,512]{2,1,0:T(8,128)S(1)}, f32[2,8,512]{2,1,0:T(8,128)}, u32[]{:S(2)}) copy-start(f32[2,8,512]{2,1,0:T(8,128)} %shard_map.70) | copy-start | bytes 98308
  192.1 37.4 %copy-start.12 = (f32[2,8,512]{2,1,0:T(8,128)S(1)}, f32[2,8,512]{2,1,0:T(8,128)}, u32[]{:S(2)}) copy-start(f32[2,8,512]{2,1,0:T(8,128)} %shard_map.64) | copy-start | bytes 98308
  196.6 33.0 %copy-start.13 = (f32[2,8,512]{2,1,0:T(8,128)S(1)}, f32[2,8,512]{2,1,0:T(8,128)}, u32[]{:S(2)}) copy-start(f32[2,8,512]{2,1,0:T(8,128)} %shard_map.67) | copy-start | bytes 98308
  196.6 31.1 %collective-permute-start.13 = (f32[2,8,512]{2,1,0:T(8,128)}, f32[2,8,512]{2,1,0:T(8,128)S(1)}, u32[]{:S(2)}, u32[]{:S(2)}) collective-permute-start(f32[2,8,512]{2,1,0:T(8,128)} %shard_map.67), channel_id=1, source_target_pairs={{12,0},{16,4},{20,8},{24,12},{28,16},{13,1},{17,5},{21,9},{25,13},... | collective-permute-start | bytes 98312 | tf_op jit(solution)/shard_map/ppermute | solution.py:37
  219.6 1.1 copy-start.6
  225.1 4.5 %collective-permute-start.10 = (f32[2,8,512]{2,1,0:T(8,128)}, f32[2,8,512]{2,1,0:T(8,128)S(1)}, u32[]{:S(2)}, u32[]{:S(2)}) collective-permute-start(f32[2,8,512]{2,1,0:T(8,128)} %shard_map.66), channel_id=1, source_target_pairs={{0,12},{4,16},{8,20},{12,24},{16,28},{1,13},{5,17},{9,21},{13,25},... | collective-permute-start | bytes 98312 | tf_op jit(solution)/shard_map/ppermute | solution.py:37

commit v2 on v1

--- a/solution.py
+++ b/solution.py
@@ -49,34 +49,59 @@
     return jnp.sinc(place) * (0.5 + 0.5 * jnp.cos(jnp.pi * place / 4.5))
 
 
+ROWS = 16
+EDGE = 128
+
+
+def resample_kernel(weights_ref, window_ref, coeff_ref, shift_ref, out_ref):
+    step = pl.program_id(1)
+    first = pl.multiple_of(step * ROWS, ROWS)
+    window = window_ref[0, pl.ds(first, ROWS + 8), :]
+    along = weights_ref[0] * window[0:ROWS, :]
+    for tap in range(1, 8):
+        along = along + weights_ref[tap] * window[tap : tap + ROWS, :]
+    nrange = along.shape[1]
+    zeros = jnp.zeros((ROWS, EDGE), jnp.float32)
+    row = jnp.concatenate([zeros, along, zeros], axis=1)
+    width = row.shape[1]
+    shift = shift_ref[...]
+    for bit in range(5):
+        moved = pltpu.roll(row, width - (1 << bit), 1)
+        row = jnp.where(((shift >> bit) & 1) == 1, moved, row)
+    coeff = coeff_ref[...]
+    result = None
+    for tap in range(8):
+        moved = pltpu.roll(row, width - (EDGE - 15 + tap), 1)[:, :nrange]
+        term = coeff[:, tap : tap + 1] * moved
+        result = term if result is None else result + term
+    out_ref[0] = result.astype(out_ref.dtype)
+
+
 def resample_block(padded, shift_lines, kern_lines, shift_range, kern_range):
     table = kernel_table()
     nlines = shift_range.shape[0]
     nrange = padded.shape[2]
     border = OFFAZ + 4
     start = border + shift_lines - 3
-    window = lax.dynamic_slice_in_dim(padded, start, nlines + 7, 1)
+    window = lax.dynamic_slice_in_dim(padded, start, nlines + 7, 1).astype(jnp.float32)
+    window = jnp.pad(window, ((0, 0), (0, 1), (0, 0)))
     weights = table[kern_lines]
-    along = jnp.zeros((2, nlines, nrange), jnp.float32)
-    for tap in range(8):
-        along = along + weights[tap] * window[:, tap : tap + nlines, :].astype(jnp.float32)
-    margin = OFFRG + 4
-    widened = jnp.pad(along, ((0, 0), (0, 0), (margin, margin)))
-    selector = (kern_range[:, None] == jnp.arange(NFRAC, dtype=jnp.int32)[None, :]).astype(
-        jnp.float32
-    )
-    range_weights = jnp.dot(selector, table, precision=lax.Precision.HIGHEST)
-    targets = shift_range[:, None] + jnp.arange(8, dtype=jnp.int32)[None, :] - 3
+    coeff = jnp.take(table, kern_range, axis=0)
+    shift = (shift_range + OFFRG)[:, None]
+    out = pl.pallas_call(
+        resample_kernel,
+        grid=(2, nlines // ROWS),
+        in_specs=[
+            pl.BlockSpec(memory_space=pltpu.SMEM),
+            pl.BlockSpec((1, nlines + 8, nrange), lambda c, t: (c, 0, 0)),
+            pl.BlockSpec((ROWS, 8), lambda c, t: (t, 0)),
+            pl.BlockSpec((ROWS, 1), lambda c, t: (t, 0)),
+        ],
+        out_specs=pl.BlockSpec((1, ROWS, nrange), lambda c, t: (c, t, 0)),
+        out_shape=jax.ShapeDtypeStruct((2, nlines, nrange), jnp.bfloat16),
+    )(weights, window, coeff, shift)
     half = nrange // 2
-    halves = []
-    for first in (0, half):
-        result = jnp.zeros((2, nlines, half), jnp.float32)
-        for offset in range(-OFFRG - 3, OFFRG + 5):
-            coeff = jnp.sum(jnp.where(targets == offset, range_weights, 0.0), axis=1)
-            low = margin + first + offset
-            result = result + coeff[None, :, None] * widened[:, :, low : low + half]
-        halves.append(look_order(result.astype(jnp.bfloat16)))
-    return halves
+    return look_order(out[:, :, :half]), look_order(out[:, :, half:])
 
 
 CHUNK = 512

time: 235 us -> 229 us (0.974)
  other arithmetic: 68.5 us -> 18.6 us
  Pallas kernels: 35 us -> 72.6 us
  waiting for transfers between devices: 47.9 us -> 52.2 us
  local copies, waits for them, and re-layouts: 9.1 us -> 13 us
    convert_element_type x2 -> x1, other arithmetic: 44.1 us -> 3.5 us  [resample_block(): lax.dynamic_slice_in_dim(padded, start, nlines + 7, 1).astype(jnp.float32)]
    pallas_call x0 -> x1, Pallas kernels: none -> 37.7 us  [resample_block(): pl.pallas_call(resample_kernel, grid=(2, nlines // ROWS), in_specs=[pl.Bl...]
    add x1, other arithmetic: 10.1 us -> 0.68 us  [resample_block(): shift = (shift_range + OFFRG)[:, None]]
    ppermute x14, waiting for transfers between devices: 47.9 us -> 52.2 us  [shifted(): return lax.ppermute(block, axis, route)]
    slice x1 -> x3, local copies, waits for them, and re-layouts: 0.6 us -> 4.72 us  [resample_block(): return (look_order(out[:, :, :half]), look_order(out[:, :, half:]))]
    dynamic_slice x1 -> x0, other arithmetic: 3.51 us -> none  [resample_block(): window = lax.dynamic_slice_in_dim(padded, start, nlines + 7, 1)]
    pad x0 -> x1, other arithmetic: none -> 3.08 us  [resample_block(): window = jnp.pad(window, ((0, 0), (0, 1), (0, 0)))]
    convert_element_type x2 -> x0, local copies, waits for them, and re-layouts: 2.7 us -> none  [resample_block(): halves.append(look_order(result.astype(jnp.bfloat16)))]
  transfers between devices with their start and end apart: 18 -> 18, of which waited for: 7 -> 6; matrix products, arithmetic and copies ran while one was open for 14% -> 6% of each run, Pallas kernels for 15% -> 15%
where the time goes in v2:
time: 229 us; the launch traced here: 227 us
  Pallas kernels  72.6 us (32%)
  waiting for transfers between devices  52.2 us (23%)
  starting transfers between devices  48.7 us (21%)
  between operations  21.7 us (9%)
  other arithmetic  18.6 us (8%)
  local copies, waits for them, and re-layouts  13 us (6%)
    ppermute x14, waiting for transfers between devices, shifted(): return lax.ppermute(block, axis, route)  52.2 us
    ppermute x14, starting transfers between devices, shifted(): return lax.ppermute(block, axis, route)  42.4 us
    pallas_call x1, Pallas kernels, resample_block(): pl.pallas_call(resample_kernel, grid=(2, nlines // ROWS), in_specs=[pl.Bl...  37.7 us
    pallas_call x8, Pallas kernels, looks(): pl.pallas_call(looks_kernel, grid=(width // CHUNK,), in_specs=[spec, spec...  34.9 us
    slice x3, local copies, waits for them, and re-layouts, resample_block(): return (look_order(out[:, :, :half]), look_order(out[:, :, half:]))  4.72 us
  transfers between devices with their start and end apart: 18, of which 6 were waited for; matrix products, arithmetic and copies ran while one was open for 6% of the time, Pallas kernels for 15%

profile of v2, /device:TPU:0, one launch (start us, length us, event | category | flops | bytes accessed | tf_op | source)
XLA Modules:
  0.0 226.7 jit_solution(9991955749794239112)
XLA Ops:
  0.0 1.1 fusion.31
  1.1 1.3 collective-permute-start.1
  2.4 3.0 %collective-permute-start = (bf16[1,2,16,4096]{3,2,1,0:T(8,128)(2,1)S(1)}, bf16[1,2,16,4096]{3,2,1,0:T(8,128)(2,1)S(1)}, u32[]{:S(2)}, u32[]{:S(2)}) collective-permute-start(bf16[1,2,16,4096]{3,2,1,0:T(8,128)(2,1)S(1)} %get-tuple-element.8), channel_id=1, source_target_pairs={{0,1},{1,2},{2,3},{4,5},{5,6},{6,7},{8,9},{9,10},{10,11},{12,13},{... | collective-permute-start | bytes 786440 | tf_op jit(solution)/shard_map/ppermute | solution.py:25
  5.4 0.7 compare_select_fusion
  6.1 0.7 compare_and_fusion
  6.8 0.7 add_bitcast_fusion
  7.5 0.1 fusion.8
  8.9 0.1 copy.20
  9.0 0.7 dynamic-slice_reduce_fusion.weights_ref
  9.7 0.7 copy.21.shift_ref
  10.4 0.7 gather_fusion
  11.1 0.7 broadcast_select_fusion.2.coeff_ref
  11.8 0.0 collective-permute-done.1
  11.8 3.5 %fusion.2 = bf16[2,167,4096]{2,1,0:T(8,128)(2,1)S(1)} fusion(s32[]{:T(128)S(6)} %select_n.502, bf16[1,2,16,4096]{3,2,1,0:T(8,128)(2,1)S(1)} %collective-permute-done, bf16[1,2,160,4096]{3,2,1,0:T(8,128)(2,1)} %param.6, bf16[1,2,16,4096]{3,2,1,0:T(8,128)(2,1)S(1)} %collective-permute-done.1), kind=kLoop, calls=%fused_computation.6 | loop fusion | flops 8208384 | bytes 5881860 | tf_op jit(solution)/shard_map/convert_element_type | solution.py:86
  15.3 3.1 %pad_convert_fusion.window_ref = f32[2,168,4096]{2,1,0:T(8,128)} fusion(bf16[2,167,4096]{2,1,0:T(8,128)(2,1)S(1)} %fusion.2), kind=kLoop, calls=%fused_computation.7 | loop fusion | flops 1376256 | bytes 8241152 | tf_op jit(solution)/shard_map/jit(_pad)/pad | solution.py:87
  18.4 37.7 %shard_map.64 = bf16[2,160,4096]{2,1,0:T(8,128)(2,1)} custom-call(f32[8]{0:T(128)} %dynamic-slice_reduce_fusion.weights_ref, f32[2,168,4096]{2,1,0:T(8,128)} %pad_convert_fusion.window_ref, f32[160,8]{1,0:T(8,128)} %broadcast_select_fusion.2.coeff_ref, s32[160,1]{1,0:T(8,128)} %copy.21.shift_ref), custom_call_target="tpu_custom_call" | custom-call | tf_op jit(solution)/shard_map/pallas_call | solution.py:91
  56.1 2.0 fusion.30
  58.1 1.3 copy.24
  59.5 0.7 copy.32
  60.2 0.3 copy-done.4
  60.5 6.0 %collective-permute-start.5 = (bf16[2,160,2048]{2,1,0:T(8,128)(2,1)S(1)}, bf16[2,160,2048]{2,1,0:T(8,128)(2,1)}, u32[]{:S(2)}, u32[]{:S(2)}) collective-permute-start(bf16[2,160,2048]{2,1,0:T(8,128)(2,1)S(1)} %bitcast.65), channel_id=1, source_target_pairs={{0,8},{4,12},{8,16},{12,20},{16,24},{20,28},{1,9},{5,13},{9,17},{1... | collective-permute-start | bytes 3932168 | tf_op jit(solution)/shard_map/ppermute | solution.py:37
  66.6 1.3 copy.22
  68.0 0.7 copy.33
  68.7 0.4 copy-done.2
  69.1 1.3 collective-permute-start.2
  70.4 24.1 %collective-permute-done.5.second_ref = bf16[2,160,2048]{2,1,0:T(8,128)(2,1)} collective-permute-done((bf16[2,160,2048]{2,1,0:T(8,128)(2,1)S(1)}, bf16[2,160,2048]{2,1,0:T(8,128)(2,1)}, u32[]{:S(2)}, u32[]{:S(2)}) %collective-permute-start.5) | collective-permute-done | bytes 1310752 | tf_op jit(solution)/shard_map/ppermute | solution.py:37
  94.5 3.8 %broadcast_select_fusion = bf16[2,160,2048]{2,1,0:T(8,128)(2,1)} fusion(bf16[2,160,2048]{2,1,0:T(8,128)(2,1)} %collective-permute-done.5.second_ref, pred[]{:T(512)S(6)} %eq.130, bf16[2,20,8,2048]{3,0,1,2:T(2,128)(2,1)} %bitcast.73), kind=kLoop, calls=%fused_computation.10 | loop fusion | flops 655360 | bytes 3932161 | tf_op jit(solution)/shard_map/jit(_where)/select_n | solution.py:166
  98.3 1.9 collective-permute-start.11
  100.2 5.6 %collective-permute-start.6 = (bf16[2,160,2048]{2,1,0:T(8,128)(2,1)}, bf16[2,160,2048]{2,1,0:T(8,128)(2,1)}, u32[]{:S(2)}, u32[]{:S(2)}) collective-permute-start(bf16[2,160,2048]{2,1,0:T(8,128)(2,1)} %collective-permute-done.5.second_ref), channel_id=1, source_target_pairs={{0,8},{4,12},{8,16},{12,20},{16,24},{20,28},{1,9},{5,13},{9,17},{1... | collective-permute-start | bytes 3932168 | tf_op jit(solution)/shard_map/ppermute | solution.py:37
  105.9 2.8 %broadcast_select_fusion.1 = bf16[2,160,2048]{2,1,0:T(8,128)(2,1)S(1)} fusion(bf16[2,160,2048]{2,1,0:T(8,128)(2,1)} %collective-permute-done.2.second_ref, pred[]{:T(512)S(6)} %eq.130, bf16[2,20,8,2048]{3,0,1,2:T(2,128)(2,1)S(1)} %bitcast.71), kind=kLoop, calls=%fused_computation.11 | loop fusion | flops 655360 | bytes 3932161 | tf_op jit(solution)/shard_map/jit(_where)/select_n | solution.py:162
  108.7 0.0 copy-start.16
  108.7 0.1 collective-permute-start.8
  108.8 1.3 collective-permute-start.3
  110.1 4.4 %shard_map.70 = f32[2,8,512]{2,1,0:T(8,128)} custom-call(bf16[2,160,2048]{2,1,0:T(8,128)(2,1)} %bitcast.66, bf16[2,160,2048]{2,1,0:T(8,128)(2,1)} %collective-permute-done.5.second_ref), custom_call_target="tpu_custom_call" | custom-call | tf_op jit(solution)/shard_map/pallas_call | solution.py:136
  114.4 1.3 collective-permute-start.15
  115.7 0.6 fusion.40
  136.2 4.4 %shard_map.69 = f32[2,8,512]{2,1,0:T(8,128)} custom-call(bf16[2,160,2048]{2,1,0:T(8,128)(2,1)} %bitcast.61, bf16[2,160,2048]{2,1,0:T(8,128)(2,1)} %collective-permute-done.2.second_ref), custom_call_target="tpu_custom_call" | custom-call | tf_op jit(solution)/shard_map/pallas_call | solution.py:136
  140.6 1.3 collective-permute-done.15
  142.0 3.8 %collective-permute-start.14 = (f32[2,8,512]{2,1,0:T(8,128)}, f32[2,8,512]{2,1,0:T(8,128)S(1)}, u32[]{:S(2)}, u32[]{:S(2)}) collective-permute-start(f32[2,8,512]{2,1,0:T(8,128)} %shard_map.69), channel_id=1, source_target_pairs={{0,8},{4,12},{8,16},{12,20},{16,24},{20,28},{1,9},{5,13},{9,17},{1... | collective-permute-start | bytes 98312 | tf_op jit(solution)/shard_map/ppermute | solution.py:37
  145.8 1.9 collective-permute-done.14
  147.7 4.4 %shard_map.72 = f32[2,8,512]{2,1,0:T(8,128)} custom-call(bf16[2,160,2048]{2,1,0:T(8,128)(2,1)} %bitcast.67, bf16[2,160,2048]{2,1,0:T(8,128)(2,1)} %collective-permute-done.11.second_ref), custom_call_target="tpu_custom_call" | custom-call | tf_op jit(solution)/shard_map/pallas_call | solution.py:136
  152.1 1.3 collective-permute-start.17
  153.3 7.0 %collective-permute-start.12 = (bf16[2,160,2048]{2,1,0:T(8,128)(2,1)}, bf16[2,160,2048]{2,1,0:T(8,128)(2,1)}, u32[]{:S(2)}, u32[]{:S(2)}) collective-permute-start(bf16[2,160,2048]{2,1,0:T(8,128)(2,1)} %collective-permute-done.11.second_ref), channel_id=1, source_target_pairs={{0,8},{4,12},{8,16},{12,20},{16,24},{20,28},{1,9},{5,13},{9,17},{1... | collective-permute-start | bytes 3932168 | tf_op jit(solution)/shard_map/ppermute | solution.py:37
  160.4 4.4 %shard_map.66 = f32[2,8,512]{2,1,0:T(8,128)} custom-call(bf16[2,160,2048]{2,1,0:T(8,128)(2,1)} %bitcast.68, bf16[2,160,2048]{2,1,0:T(8,128)(2,1)} %collective-permute-done.6.second_ref), custom_call_target="tpu_custom_call" | custom-call | tf_op jit(solution)/shard_map/pallas_call | solution.py:136
  164.8 1.3 collective-permute-start.7
  166.0 0.0 collective-permute-done.8.second_ref
  166.1 1.1 copy-done.5
  167.2 4.4 %shard_map.71 = f32[2,8,512]{2,1,0:T(8,128)} custom-call(bf16[2,160,2048]{2,1,0:T(8,128)(2,1)} %bitcast.62, bf16[2,160,2048]{2,1,0:T(8,128)(2,1)} %copy-done.5), custom_call_target="tpu_custom_call" | custom-call | tf_op jit(solution)/shard_map/pallas_call | solution.py:136
  171.6 2.8 %collective-permute-start.16 = (f32[2,8,512]{2,1,0:T(8,128)}, f32[2,8,512]{2,1,0:T(8,128)S(1)}, u32[]{:S(2)}, u32[]{:S(2)}) collective-permute-start(f32[2,8,512]{2,1,0:T(8,128)} %shard_map.71), channel_id=1, source_target_pairs={{0,4},{4,8},{8,12},{12,16},{16,20},{20,24},{24,28},{1,5},{5,9},{9,... | collective-permute-start | bytes 98312 | tf_op jit(solution)/shard_map/ppermute | solution.py:37
  174.4 4.4 %shard_map.65 = f32[2,8,512]{2,1,0:T(8,128)} custom-call(bf16[2,160,2048]{2,1,0:T(8,128)(2,1)} %bitcast.63, bf16[2,160,2048]{2,1,0:T(8,128)(2,1)} %collective-permute-done.3.second_ref), custom_call_target="tpu_custom_call" | custom-call | tf_op jit(solution)/shard_map/pallas_call | solution.py:136
  178.7 5.4 %collective-permute-start.4 = (f32[2,8,512]{2,1,0:T(8,128)}, f32[2,8,512]{2,1,0:T(8,128)S(1)}, u32[]{:S(2)}, u32[]{:S(2)}) collective-permute-start(f32[2,8,512]{2,1,0:T(8,128)} %shard_map.65), channel_id=1, source_target_pairs={{0,16},{4,20},{8,24},{12,28},{1,17},{5,21},{9,25},{13,29},{2,18},{... | collective-permute-start | bytes 98312 | tf_op jit(solution)/shard_map/ppermute | solution.py:37
  184.2 1.3 collective-permute-start.9
  185.6 0.9 collective-permute-done.4
  186.5 4.4 %shard_map.68 = f32[2,8,512]{2,1,0:T(8,128)} custom-call(bf16[2,160,2048]{2,1,0:T(8,128)(2,1)} %bitcast.69, bf16[2,160,2048]{2,1,0:T(8,128)(2,1)} %collective-permute-done.12.second_ref), custom_call_target="tpu_custom_call" | custom-call | tf_op jit(solution)/shard_map/pallas_call | solution.py:136
  190.9 1.3 collective-permute-start.13
  192.2 0.0 copy-start.10
  192.3 22.0 %collective-permute-done.9.second_ref = bf16[2,160,2048]{2,1,0:T(8,128)(2,1)S(1)} collective-permute-done((bf16[2,160,2048]{2,1,0:T(8,128)(2,1)S(1)}, bf16[2,160,2048]{2,1,0:T(8,128)(2,1)S(1)}, u32[]{:S(2)}, u32[]{:S(2)}) %collective-permute-start.9) | collective-permute-done | bytes 1310752 | tf_op jit(solution)/shard_map/ppermute | solution.py:37
  214.3 1.1 copy-done.7
  215.3 4.4 %shard_map.67 = f32[2,8,512]{2,1,0:T(8,128)} custom-call(bf16[2,160,2048]{2,1,0:T(8,128)(2,1)} %bitcast.64, bf16[2,160,2048]{2,1,0:T(8,128)(2,1)} %copy-done.7), custom_call_target="tpu_custom_call" | custom-call | tf_op jit(solution)/shard_map/pallas_call | solution.py:136
  219.7 2.6 %collective-permute-start.10 = (f32[2,8,512]{2,1,0:T(8,128)}, f32[2,8,512]{2,1,0:T(8,128)S(1)}, u32[]{:S(2)}, u32[]{:S(2)}) collective-permute-start(f32[2,8,512]{2,1,0:T(8,128)} %shard_map.67), channel_id=1, source_target_pairs={{0,12},{4,16},{8,20},{12,24},{16,28},{1,13},{5,17},{9,21},{13,25},... | collective-permute-start | bytes 98312 | tf_op jit(solution)/shard_map/ppermute | solution.py:37
  222.4 1.9 collective-permute-done.10
  224.3 0.8 select_select_fusion.2
  225.1 0.8 select_select_fusion.1
  226.0 0.7 maximum_bitcast_fusion
  (59 shorter events, 0.3 us)
Async XLA Ops:
  1.1 10.8 %collective-permute-start.1 = (bf16[1,2,16,4096]{3,2,1,0:T(8,128)(2,1)S(1)}, bf16[1,2,16,4096]{3,2,1,0:T(8,128)(2,1)S(1)}, u32[]{:S(2)}, u32[]{:S(2)}) collective-permute-start(bf16[1,2,16,4096]{3,2,1,0:T(8,128)(2,1)S(1)} %get-tuple-element.7), channel_id=1, source_target_pairs={{1,0},{2,1},{3,2},{5,4},{6,5},{7,6},{9,8},{10,9},{11,10},{13,12},{... | collective-permute-start | bytes 786440 | tf_op jit(solution)/shard_map/ppermute | solution.py:27
  2.4 9.5 %collective-permute-start = (bf16[1,2,16,4096]{3,2,1,0:T(8,128)(2,1)S(1)}, bf16[1,2,16,4096]{3,2,1,0:T(8,128)(2,1)S(1)}, u32[]{:S(2)}, u32[]{:S(2)}) collective-permute-start(bf16[1,2,16,4096]{3,2,1,0:T(8,128)(2,1)S(1)} %get-tuple-element.8), channel_id=1, source_target_pairs={{0,1},{1,2},{2,3},{4,5},{5,6},{6,7},{8,9},{9,10},{10,11},{12,13},{... | collective-permute-start | bytes 786440 | tf_op jit(solution)/shard_map/ppermute | solution.py:25
  59.5 1.1 copy-start.4
  60.5 7.4 %copy-start.1 = (bf16[2,20,8,2048]{3,2,1,0:T(8,128)(2,1)}, bf16[2,20,8,2048]{3,2,1,0:T(8,128)(2,1)S(1)}, u32[]{:S(2)}) copy-start(bf16[2,20,8,2048]{3,2,1,0:T(8,128)(2,1)S(1)} %copy.32) | copy-start | bytes 3932164
  60.5 33.9 %collective-permute-start.5 = (bf16[2,160,2048]{2,1,0:T(8,128)(2,1)S(1)}, bf16[2,160,2048]{2,1,0:T(8,128)(2,1)}, u32[]{:S(2)}, u32[]{:S(2)}) collective-permute-start(bf16[2,160,2048]{2,1,0:T(8,128)(2,1)S(1)} %bitcast.65), channel_id=1, source_target_pairs={{0,8},{4,12},{8,16},{12,20},{16,24},{20,28},{1,9},{5,13},{9,17},{1... | collective-permute-start | bytes 3932168 | tf_op jit(solution)/shard_map/ppermute | solution.py:37
  67.9 1.1 copy-start.2
  69.1 29.3 %copy-start = (bf16[2,20,8,2048]{3,2,1,0:T(8,128)(2,1)}, bf16[2,20,8,2048]{3,2,1,0:T(8,128)(2,1)S(1)}, u32[]{:S(2)}) copy-start(bf16[2,20,8,2048]{3,2,1,0:T(8,128)(2,1)S(1)} %copy.33) | copy-start | bytes 3932164
  69.1 36.8 %collective-permute-start.2 = (bf16[2,160,2048]{2,1,0:T(8,128)(2,1)S(1)}, bf16[2,160,2048]{2,1,0:T(8,128)(2,1)}, u32[]{:S(2)}, u32[]{:S(2)}) collective-permute-start(bf16[2,160,2048]{2,1,0:T(8,128)(2,1)S(1)} %bitcast.60), channel_id=1, source_target_pairs={{8,0},{12,4},{16,8},{20,12},{24,16},{28,20},{9,1},{13,5},{17,9},{2... | collective-permute-start | bytes 3932168 | tf_op jit(solution)/shard_map/ppermute | solution.py:37
  70.4 35.5 %copy-start.3 = (bf16[2,160,2048]{2,0,1:T(2,128)(2,1)S(1)}, bf16[2,160,2048]{2,0,1:T(2,128)(2,1)}, u32[]{:S(2)}) copy-start(bf16[2,160,2048]{2,0,1:T(2,128)(2,1)} %copy-done.2) | copy-start | bytes 3932164
  98.3 49.4 %collective-permute-start.11 = (bf16[2,160,2048]{2,1,0:T(8,128)(2,1)}, bf16[2,160,2048]{2,1,0:T(8,128)(2,1)}, u32[]{:S(2)}, u32[]{:S(2)}) collective-permute-start(bf16[2,160,2048]{2,1,0:T(8,128)(2,1)} %broadcast_select_fusion), channel_id=1, source_target_pairs={{0,4},{4,0},{8,12},{12,8},{16,20},{20,16},{24,28},{28,24},{1,5},{5... | collective-permute-start | bytes 3932168 | tf_op jit(solution)/shard_map/ppermute | solution.py:42
  100.2 60.2 %collective-permute-start.6 = (bf16[2,160,2048]{2,1,0:T(8,128)(2,1)}, bf16[2,160,2048]{2,1,0:T(8,128)(2,1)}, u32[]{:S(2)}, u32[]{:S(2)}) collective-permute-start(bf16[2,160,2048]{2,1,0:T(8,128)(2,1)} %collective-permute-done.5.second_ref), channel_id=1, source_target_pairs={{0,8},{4,12},{8,16},{12,20},{16,24},{20,28},{1,9},{5,13},{9,17},{1... | collective-permute-start | bytes 3932168 | tf_op jit(solution)/shard_map/ppermute | solution.py:37
  108.7 7.1 %copy-start.16 = (s32[1,4]{1,0:T(1,128)S(1)}, s32[1,4]{1,0:T(1,128)}, u32[]{:S(2)}) copy-start(s32[1,4]{1,0:T(1,128)} %param.11) | copy-start | bytes 52
  108.7 57.3 %collective-permute-start.8 = (bf16[2,160,2048]{2,1,0:T(8,128)(2,1)S(1)}, bf16[2,160,2048]{2,1,0:T(8,128)(2,1)S(1)}, u32[]{:S(2)}, u32[]{:S(2)}) collective-permute-start(bf16[2,160,2048]{2,1,0:T(8,128)(2,1)S(1)} %broadcast_select_fusion.1), channel_id=1, source_target_pairs={{0,4},{4,0},{8,12},{12,8},{16,20},{20,16},{24,28},{28,24},{1,5},{5... | collective-permute-start | bytes 3932168 | tf_op jit(solution)/shard_map/ppermute | solution.py:42
  108.8 65.6 %collective-permute-start.3 = (bf16[2,160,2048]{2,1,0:T(8,128)(2,1)}, bf16[2,160,2048]{2,1,0:T(8,128)(2,1)}, u32[]{:S(2)}, u32[]{:S(2)}) collective-permute-start(bf16[2,160,2048]{2,1,0:T(8,128)(2,1)} %collective-permute-done.2.second_ref), channel_id=1, source_target_pairs={{8,0},{12,4},{16,8},{20,12},{24,16},{28,20},{9,1},{13,5},{17,9},{2... | collective-permute-start | bytes 3932168 | tf_op jit(solution)/shard_map/ppermute | solution.py:37
  114.4 27.5 %collective-permute-start.15 = (f32[2,8,512]{2,1,0:T(8,128)}, f32[2,8,512]{2,1,0:T(8,128)S(1)}, u32[]{:S(2)}, u32[]{:S(2)}) collective-permute-start(f32[2,8,512]{2,1,0:T(8,128)} %shard_map.70), channel_id=1, source_target_pairs={{8,0},{12,4},{16,8},{20,12},{24,16},{28,20},{9,1},{13,5},{17,9},{2... | collective-permute-start | bytes 98312 | tf_op jit(solution)/shard_map/ppermute | solution.py:37
  142.0 5.7 %collective-permute-start.14 = (f32[2,8,512]{2,1,0:T(8,128)}, f32[2,8,512]{2,1,0:T(8,128)S(1)}, u32[]{:S(2)}, u32[]{:S(2)}) collective-permute-start(f32[2,8,512]{2,1,0:T(8,128)} %shard_map.69), channel_id=1, source_target_pairs={{0,8},{4,12},{8,16},{12,20},{16,24},{20,28},{1,9},{5,13},{9,17},{1... | collective-permute-start | bytes 98312 | tf_op jit(solution)/shard_map/ppermute | solution.py:37
  152.1 32.1 %collective-permute-start.17 = (f32[2,8,512]{2,1,0:T(8,128)}, f32[2,8,512]{2,1,0:T(8,128)S(1)}, u32[]{:S(2)}, u32[]{:S(2)}) collective-permute-start(f32[2,8,512]{2,1,0:T(8,128)} %shard_map.72), channel_id=1, source_target_pairs={{4,0},{8,4},{12,8},{16,12},{20,16},{24,20},{28,24},{5,1},{9,5},{13... | collective-permute-start | bytes 98312 | tf_op jit(solution)/shard_map/ppermute | solution.py:37
  153.3 33.2 %collective-permute-start.12 = (bf16[2,160,2048]{2,1,0:T(8,128)(2,1)}, bf16[2,160,2048]{2,1,0:T(8,128)(2,1)}, u32[]{:S(2)}, u32[]{:S(2)}) collective-permute-start(bf16[2,160,2048]{2,1,0:T(8,128)(2,1)} %collective-permute-done.11.second_ref), channel_id=1, source_target_pairs={{0,8},{4,12},{8,16},{12,20},{16,24},{20,28},{1,9},{5,13},{9,17},{1... | collective-permute-start | bytes 3932168 | tf_op jit(solution)/shard_map/ppermute | solution.py:37
  164.8 20.8 %collective-permute-start.7 = (f32[2,8,512]{2,1,0:T(8,128)}, f32[2,8,512]{2,1,0:T(8,128)S(1)}, u32[]{:S(2)}, u32[]{:S(2)}) collective-permute-start(f32[2,8,512]{2,1,0:T(8,128)} %shard_map.66), channel_id=1, source_target_pairs={{16,0},{20,4},{24,8},{28,12},{17,1},{21,5},{25,9},{29,13},{18,2},{... | collective-permute-start | bytes 98312 | tf_op jit(solution)/shard_map/ppermute | solution.py:37
  166.1 1.1 copy-start.5
  171.5 12.6 %copy-start.6 = (bf16[2,160,2048]{2,1,0:T(8,128)(2,1)S(1)}, bf16[2,160,2048]{2,1,0:T(8,128)(2,1)}, u32[]{:S(2)}) copy-start(bf16[2,160,2048]{2,1,0:T(8,128)(2,1)} %copy-done.5) | copy-start | bytes 3932164
  171.6 14.0 %collective-permute-start.16 = (f32[2,8,512]{2,1,0:T(8,128)}, f32[2,8,512]{2,1,0:T(8,128)S(1)}, u32[]{:S(2)}, u32[]{:S(2)}) collective-permute-start(f32[2,8,512]{2,1,0:T(8,128)} %shard_map.71), channel_id=1, source_target_pairs={{0,4},{4,8},{8,12},{12,16},{16,20},{20,24},{24,28},{1,5},{5,9},{9,... | collective-permute-start | bytes 98312 | tf_op jit(solution)/shard_map/ppermute | solution.py:37
  178.7 7.8 %collective-permute-start.4 = (f32[2,8,512]{2,1,0:T(8,128)}, f32[2,8,512]{2,1,0:T(8,128)S(1)}, u32[]{:S(2)}, u32[]{:S(2)}) collective-permute-start(f32[2,8,512]{2,1,0:T(8,128)} %shard_map.65), channel_id=1, source_target_pairs={{0,16},{4,20},{8,24},{12,28},{1,17},{5,21},{9,25},{13,29},{2,18},{... | collective-permute-start | bytes 98312 | tf_op jit(solution)/shard_map/ppermute | solution.py:37
  184.2 30.1 %collective-permute-start.9 = (bf16[2,160,2048]{2,1,0:T(8,128)(2,1)S(1)}, bf16[2,160,2048]{2,1,0:T(8,128)(2,1)S(1)}, u32[]{:S(2)}, u32[]{:S(2)}) collective-permute-start(bf16[2,160,2048]{2,1,0:T(8,128)(2,1)S(1)} %copy-done.6), channel_id=1, source_target_pairs={{8,0},{12,4},{16,8},{20,12},{24,16},{28,20},{9,1},{13,5},{17,9},{2... | collective-permute-start | bytes 3932168 | tf_op jit(solution)/shard_map/ppermute | solution.py:37
  190.9 31.4 %collective-permute-start.13 = (f32[2,8,512]{2,1,0:T(8,128)}, f32[2,8,512]{2,1,0:T(8,128)S(1)}, u32[]{:S(2)}, u32[]{:S(2)}) collective-permute-start(f32[2,8,512]{2,1,0:T(8,128)} %shard_map.68), channel_id=1, source_target_pairs={{12,0},{16,4},{20,8},{24,12},{28,16},{13,1},{17,5},{21,9},{25,13},... | collective-permute-start | bytes 98312 | tf_op jit(solution)/shard_map/ppermute | solution.py:37
  192.2 32.0 %copy-start.8 = (f32[2,8,512]{2,1,0:T(8,128)S(1)}, f32[2,8,512]{2,1,0:T(8,128)}, u32[]{:S(2)}) copy-start(f32[2,8,512]{2,1,0:T(8,128)} %shard_map.70) | copy-start | bytes 98308
  192.2 32.0 %copy-start.9 = (f32[2,8,512]{2,1,0:T(8,128)S(1)}, f32[2,8,512]{2,1,0:T(8,128)}, u32[]{:S(2)}) copy-start(f32[2,8,512]{2,1,0:T(8,128)} %shard_map.69) | copy-start | bytes 98308
  192.2 32.0 %copy-start.10 = (f32[2,8,512]{2,1,0:T(8,128)S(1)}, f32[2,8,512]{2,1,0:T(8,128)}, u32[]{:S(2)}) copy-start(f32[2,8,512]{2,1,0:T(8,128)} %shard_map.72) | copy-start | bytes 98308
  192.2 32.0 %copy-start.11 = (f32[2,8,512]{2,1,0:T(8,128)S(1)}, f32[2,8,512]{2,1,0:T(8,128)}, u32[]{:S(2)}) copy-start(f32[2,8,512]{2,1,0:T(8,128)} %shard_map.66) | copy-start | bytes 98308
  192.2 32.0 %copy-start.12 = (f32[2,8,512]{2,1,0:T(8,128)S(1)}, f32[2,8,512]{2,1,0:T(8,128)}, u32[]{:S(2)}) copy-start(f32[2,8,512]{2,1,0:T(8,128)} %shard_map.71) | copy-start | bytes 98308
  192.3 32.0 %copy-start.13 = (f32[2,8,512]{2,1,0:T(8,128)S(1)}, f32[2,8,512]{2,1,0:T(8,128)}, u32[]{:S(2)}) copy-start(f32[2,8,512]{2,1,0:T(8,128)} %shard_map.65) | copy-start | bytes 98308
  192.3 32.0 %copy-start.14 = (f32[2,8,512]{2,1,0:T(8,128)S(1)}, f32[2,8,512]{2,1,0:T(8,128)}, u32[]{:S(2)}) copy-start(f32[2,8,512]{2,1,0:T(8,128)} %shard_map.68) | copy-start | bytes 98308
  214.3 1.1 copy-start.7
  219.7 6.2 %copy-start.15 = (f32[2,8,512]{2,1,0:T(8,128)S(1)}, f32[2,8,512]{2,1,0:T(8,128)}, u32[]{:S(2)}) copy-start(f32[2,8,512]{2,1,0:T(8,128)} %shard_map.67) | copy-start | bytes 98308
  219.7 4.5 %collective-permute-start.10 = (f32[2,8,512]{2,1,0:T(8,128)}, f32[2,8,512]{2,1,0:T(8,128)S(1)}, u32[]{:S(2)}, u32[]{:S(2)}) collective-permute-start(f32[2,8,512]{2,1,0:T(8,128)} %shard_map.67), channel_id=1, source_target_pairs={{0,12},{4,16},{8,20},{12,24},{16,28},{1,13},{5,17},{9,21},{13,25},... | collective-permute-start | bytes 98312 | tf_op jit(solution)/shard_map/ppermute | solution.py:37

commit v3 on v1

--- a/solution.py
+++ b/solution.py
@@ -1,3 +1,5 @@
+import functools
+
 import jax
 import jax.numpy as jnp
 from jax import lax
@@ -49,34 +51,79 @@
     return jnp.sinc(place) * (0.5 + 0.5 * jnp.cos(jnp.pi * place / 4.5))
 
 
+ROWS = 16
+EDGE = 128
+PIECE = 512
+SPAN = 768
+
+
+def resample_kernel(side, weights_ref, window_ref, coeff_ref, shift_ref, out_ref, row_ref):
+    step = pl.program_id(0)
+    first = pl.multiple_of(step * ROWS, ROWS)
+    half = out_ref.shape[2]
+    width = row_ref.shape[2]
+    if side == 0:
+        row_ref[:, :, 0:EDGE] = jnp.zeros((2, ROWS, EDGE), jnp.float32)
+        lo, hi, src = EDGE, width, 0
+    else:
+        row_ref[:, :, width - EDGE : width] = jnp.zeros((2, ROWS, EDGE), jnp.float32)
+        lo, hi, src = 0, width - EDGE, half - EDGE
+    for comp in range(2):
+        for j in range(lo, hi, 256):
+            take = min(256, hi - j)
+            window = window_ref[comp, pl.ds(first, ROWS + 8), src + j - lo : src + j - lo + take]
+            along = weights_ref[0] * window[0:ROWS, :]
+            for tap in range(1, 8):
+                along = along + weights_ref[tap] * window[tap : tap + ROWS, :]
+            row_ref[comp, :, j : j + take] = along
+    shift = shift_ref[...]
+    bits = [((shift >> bit) & 1) == 1 for bit in range(5)]
+    coeff = coeff_ref[...]
+    for comp in range(2):
+        for piece in range(0, half, PIECE):
+            row = row_ref[comp, :, piece : piece + SPAN]
+            for bit in range(5):
+                moved = pltpu.roll(row, SPAN - (1 << bit), 1)
+                row = jnp.where(bits[bit], moved, row)
+            result = None
+            for tap in range(8):
+                moved = pltpu.roll(row, SPAN - (EDGE - 15 + tap), 1)[:, :PIECE]
+                term = coeff[:, tap : tap + 1] * moved
+                result = term if result is None else result + term
+            out_ref[comp, :, piece : piece + PIECE] = result.astype(out_ref.dtype)
+
+
+def resample_half(side, weights, window, coeff, shift):
+    nlines = coeff.shape[0]
+    half = window.shape[2] // 2
+    return pl.pallas_call(
+        functools.partial(resample_kernel, side),
+        grid=(nlines // ROWS,),
+        in_specs=[
+            pl.BlockSpec(memory_space=pltpu.SMEM),
+            pl.BlockSpec(window.shape, lambda t: (0, 0, 0)),
+            pl.BlockSpec((ROWS, 8), lambda t: (t, 0)),
+            pl.BlockSpec((ROWS, 1), lambda t: (t, 0)),
+        ],
+        out_specs=pl.BlockSpec((2, ROWS, half), lambda t: (0, t, 0)),
+        out_shape=jax.ShapeDtypeStruct((2, nlines, half), jnp.bfloat16),
+        scratch_shapes=[pltpu.VMEM((2, ROWS, half + 2 * EDGE), jnp.float32)],
+    )(weights, window, coeff, shift)
+
+
 def resample_block(padded, shift_lines, kern_lines, shift_range, kern_range):
     table = kernel_table()
     nlines = shift_range.shape[0]
-    nrange = padded.shape[2]
     border = OFFAZ + 4
     start = border + shift_lines - 3
-    window = lax.dynamic_slice_in_dim(padded, start, nlines + 7, 1)
+    window = lax.dynamic_slice_in_dim(padded, start, nlines + 7, 1).astype(jnp.float32)
+    window = jnp.pad(window, ((0, 0), (0, 1), (0, 0)))
     weights = table[kern_lines]
-    along = jnp.zeros((2, nlines, nrange), jnp.float32)
-    for tap in range(8):
-        along = along + weights[tap] * window[:, tap : tap + nlines, :].astype(jnp.float32)
-    margin = OFFRG + 4
-    widened = jnp.pad(along, ((0, 0), (0, 0), (margin, margin)))
-    selector = (kern_range[:, None] == jnp.arange(NFRAC, dtype=jnp.int32)[None, :]).astype(
-        jnp.float32
-    )
-    range_weights = jnp.dot(selector, table, precision=lax.Precision.HIGHEST)
-    targets = shift_range[:, None] + jnp.arange(8, dtype=jnp.int32)[None, :] - 3
-    half = nrange // 2
-    halves = []
-    for first in (0, half):
-        result = jnp.zeros((2, nlines, half), jnp.float32)
-        for offset in range(-OFFRG - 3, OFFRG + 5):
-            coeff = jnp.sum(jnp.where(targets == offset, range_weights, 0.0), axis=1)
-            low = margin + first + offset
-            result = result + coeff[None, :, None] * widened[:, :, low : low + half]
-        halves.append(look_order(result.astype(jnp.bfloat16)))
-    return halves
+    coeff = jnp.take(table, kern_range, axis=0)
+    shift = (shift_range + OFFRG)[:, None]
+    left = resample_half(0, weights, window, coeff, shift)
+    right = resample_half(1, weights, window, coeff, shift)
+    return look_order(left), look_order(right)
 
 
 CHUNK = 512

time: 235 us -> 259 us (1.10)
  Pallas kernels: 35 us -> 105 us
  other arithmetic: 68.5 us -> 17.8 us
  local copies, waits for them, and re-layouts: 9.1 us -> 13.7 us
    pallas_call x0 -> x2, Pallas kernels: none -> 69.7 us  [resample_half(): pl.pallas_call(functools.partial(resample_kernel, side), grid=(nlines //...]
    convert_element_type x2 -> x1, other arithmetic: 44.1 us -> 3.5 us  [resample_block(): lax.dynamic_slice_in_dim(padded, start, nlines + 7, 1).astype(jnp.float32)]
    add x1, other arithmetic: 10.1 us -> 0.68 us  [resample_block(): shift = (shift_range + OFFRG)[:, None]]
    pallas_call x0 -> x2, local copies, waits for them, and re-layouts: none -> 5.33 us  [resample_half(): pl.pallas_call(functools.partial(resample_kernel, side), grid=(nlines //...]
    dynamic_slice x1 -> x0, other arithmetic: 3.51 us -> none  [resample_block(): window = lax.dynamic_slice_in_dim(padded, start, nlines + 7, 1)]
    pad x0 -> x1, other arithmetic: none -> 3.08 us  [resample_block(): window = jnp.pad(window, ((0, 0), (0, 1), (0, 0)))]
    ppermute x2, starting transfers between devices: 2.18 us -> 5.03 us  [swapped(): return lax.ppermute(block, axis, [(i, i ^ 1) for i in range(count)])]
    convert_element_type x2 -> x0, local copies, waits for them, and re-layouts: 2.7 us -> none  [resample_block(): halves.append(look_order(result.astype(jnp.bfloat16)))]
  transfers between devices with their start and end apart: 18 -> 18, of which waited for: 7 -> 5; matrix products, arithmetic and copies ran while one was open for 14% -> 6% of each run, Pallas kernels for 15% -> 27%
where the time goes in v3:
time: 259 us; the launch traced here: 257 us
  Pallas kernels  105 us (41%)
  starting transfers between devices  49.8 us (19%)
  waiting for transfers between devices  49.6 us (19%)
  between operations  21.4 us (8%)
  other arithmetic  17.8 us (7%)
  local copies, waits for them, and re-layouts  13.7 us (5%)
    pallas_call x2, Pallas kernels, resample_half(): pl.pallas_call(functools.partial(resample_kernel, side), grid=(nlines //...  69.7 us
    ppermute x14, waiting for transfers between devices, shifted(): return lax.ppermute(block, axis, route)  49.6 us
    ppermute x14, starting transfers between devices, shifted(): return lax.ppermute(block, axis, route)  40.4 us
    pallas_call x8, Pallas kernels, looks(): pl.pallas_call(looks_kernel, grid=(width // CHUNK,), in_specs=[spec, spec...  35 us
    pallas_call x2, local copies, waits for them, and re-layouts, resample_half(): pl.pallas_call(functools.partial(resample_kernel, side), grid=(nlines //...  5.33 us
  transfers between devices with their start and end apart: 18, of which 5 were waited for; matrix products, arithmetic and copies ran while one was open for 6% of the time, Pallas kernels for 27%

profile of v3, /device:TPU:0, one launch (start us, length us, event | category | flops | bytes accessed | tf_op | source)
XLA Modules:
  0.0 257.1 jit_solution(8830006504037774652)
XLA Ops:
  0.0 1.1 fusion.30
  1.1 1.3 collective-permute-start.1
  2.4 3.0 %collective-permute-start = (bf16[1,2,16,4096]{3,2,1,0:T(8,128)(2,1)S(1)}, bf16[1,2,16,4096]{3,2,1,0:T(8,128)(2,1)S(1)}, u32[]{:S(2)}, u32[]{:S(2)}) collective-permute-start(bf16[1,2,16,4096]{3,2,1,0:T(8,128)(2,1)S(1)} %get-tuple-element.6), channel_id=1, source_target_pairs={{0,1},{1,2},{2,3},{4,5},{5,6},{6,7},{8,9},{9,10},{10,11},{12,13},{... | collective-permute-start | bytes 786440 | tf_op jit(solution)/shard_map/ppermute | solution.py:27
  5.4 0.7 compare_select_fusion
  6.1 0.7 compare_and_fusion
  6.8 0.7 add_bitcast_fusion
  7.5 0.1 fusion.8
  8.9 0.1 copy.22
  9.0 0.7 dynamic-slice_reduce_fusion.weights_ref
  9.7 0.7 copy.23.shift_ref
  10.5 0.7 gather_fusion
  11.1 0.7 broadcast_select_fusion.2.coeff_ref
  11.9 0.0 collective-permute-done.1
  11.9 3.5 %fusion.2 = bf16[2,167,4096]{2,1,0:T(8,128)(2,1)S(1)} fusion(s32[]{:T(128)S(6)} %select_n.502, bf16[1,2,16,4096]{3,2,1,0:T(8,128)(2,1)S(1)} %collective-permute-done, bf16[1,2,160,4096]{3,2,1,0:T(8,128)(2,1)} %param.6, bf16[1,2,16,4096]{3,2,1,0:T(8,128)(2,1)S(1)} %collective-permute-done.1), kind=kLoop, calls=%fused_computation.6 | loop fusion | flops 8208384 | bytes 5881860 | tf_op jit(solution)/shard_map/convert_element_type | solution.py:119
  15.4 3.1 %pad_convert_fusion.window_ref = f32[2,168,4096]{2,1,0:T(8,128)} fusion(bf16[2,167,4096]{2,1,0:T(8,128)(2,1)S(1)} %fusion.2), kind=kLoop, calls=%fused_computation.7 | loop fusion | flops 1376256 | bytes 8241152 | tf_op jit(solution)/shard_map/jit(_pad)/pad | solution.py:120
  18.5 34.8 %shard_map.64 = bf16[2,160,2048]{2,1,0:T(8,128)(2,1)} custom-call(f32[8]{0:T(128)} %dynamic-slice_reduce_fusion.weights_ref, f32[2,168,4096]{2,1,0:T(8,128)} %pad_convert_fusion.window_ref, f32[160,8]{1,0:T(8,128)} %broadcast_select_fusion.2.coeff_ref, s32[160,1]{1,0:T(8,128)} %copy.23.shift_ref), custom_call_target="tpu_custom_call" | custom-call | tf_op jit(solution)/shard_map/pallas_call | solution.py:99
  53.3 2.7 %copy.24 = bf16[2,160,2048]{2,0,1:T(2,128)(2,1)S(1)} copy(bf16[2,160,2048]{2,1,0:T(8,128)(2,1)} %shard_map.64) | data formatting | bytes 2621440 | tf_op jit(solution)/shard_map/pallas_call | solution.py:99
  55.9 0.7 copy.36
  56.7 0.4 copy-done.4
  57.0 1.3 collective-permute-start.2
  58.3 34.9 %shard_map.66 = bf16[2,160,2048]{2,1,0:T(8,128)(2,1)} custom-call(f32[8]{0:T(128)} %dynamic-slice_reduce_fusion.weights_ref, f32[2,168,4096]{2,1,0:T(8,128)} %pad_convert_fusion.window_ref, f32[160,8]{1,0:T(8,128)} %broadcast_select_fusion.2.coeff_ref, s32[160,1]{1,0:T(8,128)} %copy.23.shift_ref), custom_call_target="tpu_custom_call" | custom-call | tf_op jit(solution)/shard_map/pallas_call | solution.py:99
  93.2 2.7 %copy.27 = bf16[2,160,2048]{2,0,1:T(2,128)(2,1)S(1)} copy(bf16[2,160,2048]{2,1,0:T(8,128)(2,1)} %shard_map.66) | data formatting | bytes 2621440 | tf_op jit(solution)/shard_map/pallas_call | solution.py:99
  95.9 0.7 copy.35
  96.6 0.4 copy-done.2
  97.0 6.6 %collective-permute-start.5 = (bf16[2,160,2048]{2,1,0:T(8,128)(2,1)S(1)}, bf16[2,160,2048]{2,1,0:T(8,128)(2,1)}, u32[]{:S(2)}, u32[]{:S(2)}) collective-permute-start(bf16[2,160,2048]{2,1,0:T(8,128)(2,1)S(1)} %bitcast.60), channel_id=1, source_target_pairs={{0,8},{4,12},{8,16},{12,20},{16,24},{20,28},{1,9},{5,13},{9,17},{1... | collective-permute-start | bytes 3932168 | tf_op jit(solution)/shard_map/ppermute | solution.py:39
  103.6 0.0 collective-permute-done.2.second_ref
  103.6 4.3 %broadcast_select_fusion.1 = bf16[2,160,2048]{2,1,0:T(8,128)(2,1)} fusion(bf16[2,160,2048]{2,1,0:T(8,128)(2,1)} %collective-permute-done.2.second_ref, pred[]{:T(512)S(6)} %eq.130, bf16[2,20,8,2048]{3,0,1,2:T(2,128)(2,1)} %bitcast.73), kind=kLoop, calls=%fused_computation.11 | loop fusion | flops 655360 | bytes 3932161 | tf_op jit(solution)/shard_map/jit(_where)/select_n | solution.py:184
  108.0 1.6 collective-permute-start.8
  109.5 1.3 collective-permute-start.3
  110.8 20.6 %collective-permute-done.5.second_ref = bf16[2,160,2048]{2,1,0:T(8,128)(2,1)} collective-permute-done((bf16[2,160,2048]{2,1,0:T(8,128)(2,1)S(1)}, bf16[2,160,2048]{2,1,0:T(8,128)(2,1)}, u32[]{:S(2)}, u32[]{:S(2)}) %collective-permute-start.5) | collective-permute-done | bytes 1310752 | tf_op jit(solution)/shard_map/ppermute | solution.py:39
  131.4 1.5 broadcast_select_fusion
  132.9 0.0 copy-start.16
  133.0 3.5 %collective-permute-start.11 = (bf16[2,160,2048]{2,1,0:T(8,128)(2,1)S(1)}, bf16[2,160,2048]{2,1,0:T(8,128)(2,1)S(1)}, u32[]{:S(2)}, u32[]{:S(2)}) collective-permute-start(bf16[2,160,2048]{2,1,0:T(8,128)(2,1)S(1)} %broadcast_select_fusion), channel_id=1, source_target_pairs={{0,4},{4,0},{8,12},{12,8},{16,20},{20,16},{24,28},{28,24},{1,5},{5... | collective-permute-start | bytes 3932168 | tf_op jit(solution)/shard_map/ppermute | solution.py:44
  136.4 5.6 %collective-permute-start.6 = (bf16[2,160,2048]{2,1,0:T(8,128)(2,1)}, bf16[2,160,2048]{2,1,0:T(8,128)(2,1)}, u32[]{:S(2)}, u32[]{:S(2)}) collective-permute-start(bf16[2,160,2048]{2,1,0:T(8,128)(2,1)} %collective-permute-done.5.second_ref), channel_id=1, source_target_pairs={{0,8},{4,12},{8,16},{12,20},{16,24},{20,28},{1,9},{5,13},{9,17},{1... | collective-permute-start | bytes 3932168 | tf_op jit(solution)/shard_map/ppermute | solution.py:39
  142.0 4.4 %shard_map.70 = f32[2,8,512]{2,1,0:T(8,128)} custom-call(bf16[2,160,2048]{2,1,0:T(8,128)(2,1)} %bitcast.66, bf16[2,160,2048]{2,1,0:T(8,128)(2,1)} %collective-permute-done.2.second_ref), custom_call_target="tpu_custom_call" | custom-call | tf_op jit(solution)/shard_map/pallas_call | solution.py:158
  146.4 2.5 collective-permute-start.14
  148.9 0.6 fusion.39
  169.2 4.4 %shard_map.71 = f32[2,8,512]{2,1,0:T(8,128)} custom-call(bf16[2,160,2048]{2,1,0:T(8,128)(2,1)} %bitcast.61, bf16[2,160,2048]{2,1,0:T(8,128)(2,1)} %collective-permute-done.5.second_ref), custom_call_target="tpu_custom_call" | custom-call | tf_op jit(solution)/shard_map/pallas_call | solution.py:158
  173.5 0.0 collective-permute-done.14
  173.5 1.3 collective-permute-start.15
  174.9 5.3 %collective-permute-done.15 = f32[2,8,512]{2,1,0:T(8,128)S(1)} collective-permute-done((f32[2,8,512]{2,1,0:T(8,128)}, f32[2,8,512]{2,1,0:T(8,128)S(1)}, u32[]{:S(2)}, u32[]{:S(2)}) %collective-permute-start.15) | collective-permute-done | bytes 32800 | tf_op jit(solution)/shard_map/ppermute | solution.py:39
  180.1 4.4 %shard_map.72 = f32[2,8,512]{2,1,0:T(8,128)} custom-call(bf16[2,160,2048]{2,1,0:T(8,128)(2,1)} %bitcast.67, bf16[2,160,2048]{2,1,0:T(8,128)(2,1)} %collective-permute-done.8.second_ref), custom_call_target="tpu_custom_call" | custom-call | tf_op jit(solution)/shard_map/pallas_call | solution.py:158
  184.5 1.9 collective-permute-start.16
  186.4 1.3 collective-permute-start.9
  187.8 4.4 %shard_map.65 = f32[2,8,512]{2,1,0:T(8,128)} custom-call(bf16[2,160,2048]{2,1,0:T(8,128)(2,1)} %bitcast.68, bf16[2,160,2048]{2,1,0:T(8,128)(2,1)} %collective-permute-done.3.second_ref), custom_call_target="tpu_custom_call" | custom-call | tf_op jit(solution)/shard_map/pallas_call | solution.py:158
  192.1 6.0 %collective-permute-start.4 = (f32[2,8,512]{2,1,0:T(8,128)}, f32[2,8,512]{2,1,0:T(8,128)S(1)}, u32[]{:S(2)}, u32[]{:S(2)}) collective-permute-start(f32[2,8,512]{2,1,0:T(8,128)} %shard_map.65), channel_id=1, source_target_pairs={{0,16},{4,20},{8,24},{12,28},{1,17},{5,21},{9,25},{13,29},{2,18},{... | collective-permute-start | bytes 98312 | tf_op jit(solution)/shard_map/ppermute | solution.py:39
  198.2 1.2 copy-done.5
  199.3 4.4 %shard_map.73 = f32[2,8,512]{2,1,0:T(8,128)} custom-call(bf16[2,160,2048]{2,1,0:T(8,128)(2,1)} %bitcast.62, bf16[2,160,2048]{2,1,0:T(8,128)(2,1)} %copy-done.5), custom_call_target="tpu_custom_call" | custom-call | tf_op jit(solution)/shard_map/pallas_call | solution.py:158
  203.7 1.4 collective-permute-start.17
  205.1 4.4 %shard_map.67 = f32[2,8,512]{2,1,0:T(8,128)} custom-call(bf16[2,160,2048]{2,1,0:T(8,128)(2,1)} %bitcast.63, bf16[2,160,2048]{2,1,0:T(8,128)(2,1)} %collective-permute-done.6.second_ref), custom_call_target="tpu_custom_call" | custom-call | tf_op jit(solution)/shard_map/pallas_call | solution.py:158
  209.5 1.3 collective-permute-start.7
  210.8 5.5 %collective-permute-start.12 = (bf16[2,160,2048]{2,1,0:T(8,128)(2,1)S(1)}, bf16[2,160,2048]{2,1,0:T(8,128)(2,1)S(1)}, u32[]{:S(2)}, u32[]{:S(2)}) collective-permute-start(bf16[2,160,2048]{2,1,0:T(8,128)(2,1)S(1)} %copy-done.6), channel_id=1, source_target_pairs={{0,8},{4,12},{8,16},{12,20},{16,24},{20,28},{1,9},{5,13},{9,17},{1... | collective-permute-start | bytes 3932168 | tf_op jit(solution)/shard_map/ppermute | solution.py:39
  216.4 4.3 %collective-permute-done.7 = f32[2,8,512]{2,1,0:T(8,128)S(1)} collective-permute-done((f32[2,8,512]{2,1,0:T(8,128)}, f32[2,8,512]{2,1,0:T(8,128)S(1)}, u32[]{:S(2)}, u32[]{:S(2)}) %collective-permute-start.7) | collective-permute-done | bytes 32800 | tf_op jit(solution)/shard_map/ppermute | solution.py:39
  220.8 4.4 %shard_map.68 = f32[2,8,512]{2,1,0:T(8,128)} custom-call(bf16[2,160,2048]{2,1,0:T(8,128)(2,1)} %bitcast.69, bf16[2,160,2048]{2,1,0:T(8,128)(2,1)} %collective-permute-done.9.second_ref), custom_call_target="tpu_custom_call" | custom-call | tf_op jit(solution)/shard_map/pallas_call | solution.py:158
  225.1 3.0 %collective-permute-start.10 = (f32[2,8,512]{2,1,0:T(8,128)}, f32[2,8,512]{2,1,0:T(8,128)S(1)}, u32[]{:S(2)}, u32[]{:S(2)}) collective-permute-start(f32[2,8,512]{2,1,0:T(8,128)} %shard_map.68), channel_id=1, source_target_pairs={{0,12},{4,16},{8,20},{12,24},{16,28},{1,13},{5,17},{9,21},{13,25},... | collective-permute-start | bytes 98312 | tf_op jit(solution)/shard_map/ppermute | solution.py:39
  228.2 0.0 copy-start.12
  228.3 13.6 %collective-permute-done.12.second_ref = bf16[2,160,2048]{2,1,0:T(8,128)(2,1)S(1)} collective-permute-done((bf16[2,160,2048]{2,1,0:T(8,128)(2,1)S(1)}, bf16[2,160,2048]{2,1,0:T(8,128)(2,1)S(1)}, u32[]{:S(2)}, u32[]{:S(2)}) %collective-permute-start.12) | collective-permute-done | bytes 1310752 | tf_op jit(solution)/shard_map/ppermute | solution.py:39
  241.9 1.1 copy-done.7
  243.0 4.4 %shard_map.69 = f32[2,8,512]{2,1,0:T(8,128)} custom-call(bf16[2,160,2048]{2,1,0:T(8,128)(2,1)} %bitcast.64, bf16[2,160,2048]{2,1,0:T(8,128)(2,1)} %copy-done.7), custom_call_target="tpu_custom_call" | custom-call | tf_op jit(solution)/shard_map/pallas_call | solution.py:158
  247.3 1.4 collective-permute-start.13
  248.8 5.7 %collective-permute-done.13 = f32[2,8,512]{2,1,0:T(8,128)S(1)} collective-permute-done((f32[2,8,512]{2,1,0:T(8,128)}, f32[2,8,512]{2,1,0:T(8,128)S(1)}, u32[]{:S(2)}, u32[]{:S(2)}) %collective-permute-start.13) | collective-permute-done | bytes 32800 | tf_op jit(solution)/shard_map/ppermute | solution.py:39
  254.6 0.8 select_select_fusion.2
  255.4 0.8 select_select_fusion.1
  256.3 0.7 maximum_bitcast_fusion
  (59 shorter events, 0.3 us)
Async XLA Ops:
  1.1 10.8 %collective-permute-start.1 = (bf16[1,2,16,4096]{3,2,1,0:T(8,128)(2,1)S(1)}, bf16[1,2,16,4096]{3,2,1,0:T(8,128)(2,1)S(1)}, u32[]{:S(2)}, u32[]{:S(2)}) collective-permute-start(bf16[1,2,16,4096]{3,2,1,0:T(8,128)(2,1)S(1)} %get-tuple-element.5), channel_id=1, source_target_pairs={{1,0},{2,1},{3,2},{5,4},{6,5},{7,6},{9,8},{10,9},{11,10},{13,12},{... | collective-permute-start | bytes 786440 | tf_op jit(solution)/shard_map/ppermute | solution.py:29
  2.4 9.5 %collective-permute-start = (bf16[1,2,16,4096]{3,2,1,0:T(8,128)(2,1)S(1)}, bf16[1,2,16,4096]{3,2,1,0:T(8,128)(2,1)S(1)}, u32[]{:S(2)}, u32[]{:S(2)}) collective-permute-start(bf16[1,2,16,4096]{3,2,1,0:T(8,128)(2,1)S(1)} %get-tuple-element.6), channel_id=1, source_target_pairs={{0,1},{1,2},{2,3},{4,5},{5,6},{6,7},{8,9},{9,10},{10,11},{12,13},{... | collective-permute-start | bytes 786440 | tf_op jit(solution)/shard_map/ppermute | solution.py:27
  55.9 1.1 copy-start.4
  57.0 36.2 %copy-start.1 = (bf16[2,20,8,2048]{3,2,1,0:T(8,128)(2,1)}, bf16[2,20,8,2048]{3,2,1,0:T(8,128)(2,1)S(1)}, u32[]{:S(2)}) copy-start(bf16[2,20,8,2048]{3,2,1,0:T(8,128)(2,1)S(1)} %copy.36) | copy-start | bytes 3932164
  57.0 46.6 %collective-permute-start.2 = (bf16[2,160,2048]{2,1,0:T(8,128)(2,1)S(1)}, bf16[2,160,2048]{2,1,0:T(8,128)(2,1)}, u32[]{:S(2)}, u32[]{:S(2)}) collective-permute-start(bf16[2,160,2048]{2,1,0:T(8,128)(2,1)S(1)} %bitcast.65), channel_id=1, source_target_pairs={{8,0},{12,4},{16,8},{20,12},{24,16},{28,20},{9,1},{13,5},{17,9},{2... | collective-permute-start | bytes 3932168 | tf_op jit(solution)/shard_map/ppermute | solution.py:39
  95.9 1.1 copy-start.2
  97.0 11.0 %copy-start = (bf16[2,20,8,2048]{3,2,1,0:T(8,128)(2,1)}, bf16[2,20,8,2048]{3,2,1,0:T(8,128)(2,1)S(1)}, u32[]{:S(2)}) copy-start(bf16[2,20,8,2048]{3,2,1,0:T(8,128)(2,1)S(1)} %copy.35) | copy-start | bytes 3932164
  97.0 34.4 %collective-permute-start.5 = (bf16[2,160,2048]{2,1,0:T(8,128)(2,1)S(1)}, bf16[2,160,2048]{2,1,0:T(8,128)(2,1)}, u32[]{:S(2)}, u32[]{:S(2)}) collective-permute-start(bf16[2,160,2048]{2,1,0:T(8,128)(2,1)S(1)} %bitcast.60), channel_id=1, source_target_pairs={{0,8},{4,12},{8,16},{12,20},{16,24},{20,28},{1,9},{5,13},{9,17},{1... | collective-permute-start | bytes 3932168 | tf_op jit(solution)/shard_map/ppermute | solution.py:39
  103.6 27.8 %copy-start.3 = (bf16[2,160,2048]{2,0,1:T(2,128)(2,1)S(1)}, bf16[2,160,2048]{2,0,1:T(2,128)(2,1)}, u32[]{:S(2)}) copy-start(bf16[2,160,2048]{2,0,1:T(2,128)(2,1)} %copy-done.2) | copy-start | bytes 3932164
  108.0 72.1 %collective-permute-start.8 = (bf16[2,160,2048]{2,1,0:T(8,128)(2,1)}, bf16[2,160,2048]{2,1,0:T(8,128)(2,1)}, u32[]{:S(2)}, u32[]{:S(2)}) collective-permute-start(bf16[2,160,2048]{2,1,0:T(8,128)(2,1)} %broadcast_select_fusion.1), channel_id=1, source_target_pairs={{0,4},{4,0},{8,12},{12,8},{16,20},{20,16},{24,28},{28,24},{1,5},{5... | collective-permute-start | bytes 3932168 | tf_op jit(solution)/shard_map/ppermute | solution.py:44
  109.5 78.2 %collective-permute-start.3 = (bf16[2,160,2048]{2,1,0:T(8,128)(2,1)}, bf16[2,160,2048]{2,1,0:T(8,128)(2,1)}, u32[]{:S(2)}, u32[]{:S(2)}) collective-permute-start(bf16[2,160,2048]{2,1,0:T(8,128)(2,1)} %collective-permute-done.2.second_ref), channel_id=1, source_target_pairs={{8,0},{12,4},{16,8},{20,12},{24,16},{28,20},{9,1},{13,5},{17,9},{2... | collective-permute-start | bytes 3932168 | tf_op jit(solution)/shard_map/ppermute | solution.py:39
  132.9 16.0 %copy-start.16 = (s32[1,4]{1,0:T(1,128)S(1)}, s32[1,4]{1,0:T(1,128)}, u32[]{:S(2)}) copy-start(s32[1,4]{1,0:T(1,128)} %param.11) | copy-start | bytes 52
  133.0 65.2 %collective-permute-start.11 = (bf16[2,160,2048]{2,1,0:T(8,128)(2,1)S(1)}, bf16[2,160,2048]{2,1,0:T(8,128)(2,1)S(1)}, u32[]{:S(2)}, u32[]{:S(2)}) collective-permute-start(bf16[2,160,2048]{2,1,0:T(8,128)(2,1)S(1)} %broadcast_select_fusion), channel_id=1, source_target_pairs={{0,4},{4,0},{8,12},{12,8},{16,20},{20,16},{24,28},{28,24},{1,5},{5... | collective-permute-start | bytes 3932168 | tf_op jit(solution)/shard_map/ppermute | solution.py:44
  136.4 68.7 %collective-permute-start.6 = (bf16[2,160,2048]{2,1,0:T(8,128)(2,1)}, bf16[2,160,2048]{2,1,0:T(8,128)(2,1)}, u32[]{:S(2)}, u32[]{:S(2)}) collective-permute-start(bf16[2,160,2048]{2,1,0:T(8,128)(2,1)} %collective-permute-done.5.second_ref), channel_id=1, source_target_pairs={{0,8},{4,12},{8,16},{12,20},{16,24},{20,28},{1,9},{5,13},{9,17},{1... | collective-permute-start | bytes 3932168 | tf_op jit(solution)/shard_map/ppermute | solution.py:39
  146.4 27.2 %collective-permute-start.14 = (f32[2,8,512]{2,1,0:T(8,128)}, f32[2,8,512]{2,1,0:T(8,128)S(1)}, u32[]{:S(2)}, u32[]{:S(2)}) collective-permute-start(f32[2,8,512]{2,1,0:T(8,128)} %shard_map.70), channel_id=1, source_target_pairs={{0,8},{4,12},{8,16},{12,20},{16,24},{20,28},{1,9},{5,13},{9,17},{1... | collective-permute-start | bytes 98312 | tf_op jit(solution)/shard_map/ppermute | solution.py:39
  173.5 6.6 %collective-permute-start.15 = (f32[2,8,512]{2,1,0:T(8,128)}, f32[2,8,512]{2,1,0:T(8,128)S(1)}, u32[]{:S(2)}, u32[]{:S(2)}) collective-permute-start(f32[2,8,512]{2,1,0:T(8,128)} %shard_map.71), channel_id=1, source_target_pairs={{8,0},{12,4},{16,8},{20,12},{24,16},{28,20},{9,1},{13,5},{17,9},{2... | collective-permute-start | bytes 98312 | tf_op jit(solution)/shard_map/ppermute | solution.py:39
  184.5 26.3 %collective-permute-start.16 = (f32[2,8,512]{2,1,0:T(8,128)}, f32[2,8,512]{2,1,0:T(8,128)S(1)}, u32[]{:S(2)}, u32[]{:S(2)}) collective-permute-start(f32[2,8,512]{2,1,0:T(8,128)} %shard_map.72), channel_id=1, source_target_pairs={{0,4},{4,8},{8,12},{12,16},{16,20},{20,24},{24,28},{1,5},{5,9},{9,... | collective-permute-start | bytes 98312 | tf_op jit(solution)/shard_map/ppermute | solution.py:39
  186.4 34.3 %collective-permute-start.9 = (bf16[2,160,2048]{2,1,0:T(8,128)(2,1)}, bf16[2,160,2048]{2,1,0:T(8,128)(2,1)}, u32[]{:S(2)}, u32[]{:S(2)}) collective-permute-start(bf16[2,160,2048]{2,1,0:T(8,128)(2,1)} %collective-permute-done.8.second_ref), channel_id=1, source_target_pairs={{8,0},{12,4},{16,8},{20,12},{24,16},{28,20},{9,1},{13,5},{17,9},{2... | collective-permute-start | bytes 3932168 | tf_op jit(solution)/shard_map/ppermute | solution.py:39
  192.1 24.2 %collective-permute-start.4 = (f32[2,8,512]{2,1,0:T(8,128)}, f32[2,8,512]{2,1,0:T(8,128)S(1)}, u32[]{:S(2)}, u32[]{:S(2)}) collective-permute-start(f32[2,8,512]{2,1,0:T(8,128)} %shard_map.65), channel_id=1, source_target_pairs={{0,16},{4,20},{8,24},{12,28},{1,17},{5,21},{9,25},{13,29},{2,18},{... | collective-permute-start | bytes 98312 | tf_op jit(solution)/shard_map/ppermute | solution.py:39
  198.1 1.2 copy-start.5
  203.7 7.1 %copy-start.6 = (bf16[2,160,2048]{2,1,0:T(8,128)(2,1)S(1)}, bf16[2,160,2048]{2,1,0:T(8,128)(2,1)}, u32[]{:S(2)}) copy-start(bf16[2,160,2048]{2,1,0:T(8,128)(2,1)} %copy-done.5) | copy-start | bytes 3932164
  203.7 12.7 %collective-permute-start.17 = (f32[2,8,512]{2,1,0:T(8,128)}, f32[2,8,512]{2,1,0:T(8,128)S(1)}, u32[]{:S(2)}, u32[]{:S(2)}) collective-permute-start(f32[2,8,512]{2,1,0:T(8,128)} %shard_map.73), channel_id=1, source_target_pairs={{4,0},{8,4},{12,8},{16,12},{20,16},{24,20},{28,24},{5,1},{9,5},{13... | collective-permute-start | bytes 98312 | tf_op jit(solution)/shard_map/ppermute | solution.py:39
  209.5 11.3 %collective-permute-start.7 = (f32[2,8,512]{2,1,0:T(8,128)}, f32[2,8,512]{2,1,0:T(8,128)S(1)}, u32[]{:S(2)}, u32[]{:S(2)}) collective-permute-start(f32[2,8,512]{2,1,0:T(8,128)} %shard_map.67), channel_id=1, source_target_pairs={{16,0},{20,4},{24,8},{28,12},{17,1},{21,5},{25,9},{29,13},{18,2},{... | collective-permute-start | bytes 98312 | tf_op jit(solution)/shard_map/ppermute | solution.py:39
  210.8 31.1 %collective-permute-start.12 = (bf16[2,160,2048]{2,1,0:T(8,128)(2,1)S(1)}, bf16[2,160,2048]{2,1,0:T(8,128)(2,1)S(1)}, u32[]{:S(2)}, u32[]{:S(2)}) collective-permute-start(bf16[2,160,2048]{2,1,0:T(8,128)(2,1)S(1)} %copy-done.6), channel_id=1, source_target_pairs={{0,8},{4,12},{8,16},{12,20},{16,24},{20,28},{1,9},{5,13},{9,17},{1... | collective-permute-start | bytes 3932168 | tf_op jit(solution)/shard_map/ppermute | solution.py:39
  225.1 23.6 %collective-permute-start.10 = (f32[2,8,512]{2,1,0:T(8,128)}, f32[2,8,512]{2,1,0:T(8,128)S(1)}, u32[]{:S(2)}, u32[]{:S(2)}) collective-permute-start(f32[2,8,512]{2,1,0:T(8,128)} %shard_map.68), channel_id=1, source_target_pairs={{0,12},{4,16},{8,20},{12,24},{16,28},{1,13},{5,17},{9,21},{13,25},... | collective-permute-start | bytes 98312 | tf_op jit(solution)/shard_map/ppermute | solution.py:39
  228.2 26.4 %copy-start.8 = (f32[2,8,512]{2,1,0:T(8,128)S(1)}, f32[2,8,512]{2,1,0:T(8,128)}, u32[]{:S(2)}) copy-start(f32[2,8,512]{2,1,0:T(8,128)} %shard_map.70) | copy-start | bytes 98308
  228.2 26.4 %copy-start.9 = (f32[2,8,512]{2,1,0:T(8,128)S(1)}, f32[2,8,512]{2,1,0:T(8,128)}, u32[]{:S(2)}) copy-start(f32[2,8,512]{2,1,0:T(8,128)} %shard_map.71) | copy-start | bytes 98308
  228.2 26.4 %copy-start.10 = (f32[2,8,512]{2,1,0:T(8,128)S(1)}, f32[2,8,512]{2,1,0:T(8,128)}, u32[]{:S(2)}) copy-start(f32[2,8,512]{2,1,0:T(8,128)} %shard_map.72) | copy-start | bytes 98308
  228.2 26.4 %copy-start.11 = (f32[2,8,512]{2,1,0:T(8,128)S(1)}, f32[2,8,512]{2,1,0:T(8,128)}, u32[]{:S(2)}) copy-start(f32[2,8,512]{2,1,0:T(8,128)} %shard_map.65) | copy-start | bytes 98308
  228.2 26.4 %copy-start.12 = (f32[2,8,512]{2,1,0:T(8,128)S(1)}, f32[2,8,512]{2,1,0:T(8,128)}, u32[]{:S(2)}) copy-start(f32[2,8,512]{2,1,0:T(8,128)} %shard_map.73) | copy-start | bytes 98308
  228.3 26.3 %copy-start.13 = (f32[2,8,512]{2,1,0:T(8,128)S(1)}, f32[2,8,512]{2,1,0:T(8,128)}, u32[]{:S(2)}) copy-start(f32[2,8,512]{2,1,0:T(8,128)} %shard_map.67) | copy-start | bytes 98308
  228.3 26.3 %copy-start.14 = (f32[2,8,512]{2,1,0:T(8,128)S(1)}, f32[2,8,512]{2,1,0:T(8,128)}, u32[]{:S(2)}) copy-start(f32[2,8,512]{2,1,0:T(8,128)} %shard_map.68) | copy-start | bytes 98308
  241.9 1.1 copy-start.7
  247.3 8.9 %copy-start.15 = (f32[2,8,512]{2,1,0:T(8,128)S(1)}, f32[2,8,512]{2,1,0:T(8,128)}, u32[]{:S(2)}) copy-start(f32[2,8,512]{2,1,0:T(8,128)} %shard_map.69) | copy-start | bytes 98308
  247.3 7.2 %collective-permute-start.13 = (f32[2,8,512]{2,1,0:T(8,128)}, f32[2,8,512]{2,1,0:T(8,128)S(1)}, u32[]{:S(2)}, u32[]{:S(2)}) collective-permute-start(f32[2,8,512]{2,1,0:T(8,128)} %shard_map.69), channel_id=1, source_target_pairs={{12,0},{16,4},{20,8},{24,12},{28,16},{13,1},{17,5},{21,9},{25,13},... | collective-permute-start | bytes 98312 | tf_op jit(solution)/shard_map/ppermute | solution.py:39

commit v4 on v2

--- a/solution.py
+++ b/solution.py
@@ -1,3 +1,5 @@
+import functools
+
 import jax
 import jax.numpy as jnp
 from jax import lax
@@ -51,18 +53,21 @@
 
 ROWS = 16
 EDGE = 128
-
-
-def resample_kernel(weights_ref, window_ref, coeff_ref, shift_ref, out_ref):
+PIECES = 2
+
+
+def resample_kernel(side, weights_ref, window_ref, coeff_ref, shift_ref, out_ref):
     step = pl.program_id(1)
     first = pl.multiple_of(step * ROWS, ROWS)
-    window = window_ref[0, pl.ds(first, ROWS + 8), :]
+    half = out_ref.shape[2]
+    low = max(side * half - EDGE, 0)
+    high = min(side * half + half + EDGE, window_ref.shape[2])
+    window = window_ref[0, pl.ds(first, ROWS + 8), low:high]
     along = weights_ref[0] * window[0:ROWS, :]
     for tap in range(1, 8):
         along = along + weights_ref[tap] * window[tap : tap + ROWS, :]
-    nrange = along.shape[1]
     zeros = jnp.zeros((ROWS, EDGE), jnp.float32)
-    row = jnp.concatenate([zeros, along, zeros], axis=1)
+    row = jnp.concatenate([zeros, along] if side == 0 else [along, zeros], axis=1)
     width = row.shape[1]
     shift = shift_ref[...]
     for bit in range(5):
@@ -71,16 +76,32 @@
     coeff = coeff_ref[...]
     result = None
     for tap in range(8):
-        moved = pltpu.roll(row, width - (EDGE - 15 + tap), 1)[:, :nrange]
+        moved = pltpu.roll(row, width - (EDGE - 15 + tap), 1)[:, :half]
         term = coeff[:, tap : tap + 1] * moved
         result = term if result is None else result + term
     out_ref[0] = result.astype(out_ref.dtype)
 
 
+def resample_half(side, weights, window, coeff, shift):
+    nlines = coeff.shape[0]
+    half = window.shape[2] // 2
+    return pl.pallas_call(
+        functools.partial(resample_kernel, side),
+        grid=(2, nlines // ROWS),
+        in_specs=[
+            pl.BlockSpec(memory_space=pltpu.SMEM),
+            pl.BlockSpec((1,) + window.shape[1:], lambda c, t: (c, 0, 0)),
+            pl.BlockSpec((ROWS, 8), lambda c, t: (t, 0)),
+            pl.BlockSpec((ROWS, 1), lambda c, t: (t, 0)),
+        ],
+        out_specs=pl.BlockSpec((1, ROWS, half), lambda c, t: (c, t, 0)),
+        out_shape=jax.ShapeDtypeStruct((2, nlines, half), jnp.bfloat16),
+    )(weights, window, coeff, shift)
+
+
 def resample_block(padded, shift_lines, kern_lines, shift_range, kern_range):
     table = kernel_table()
     nlines = shift_range.shape[0]
-    nrange = padded.shape[2]
     border = OFFAZ + 4
     start = border + shift_lines - 3
     window = lax.dynamic_slice_in_dim(padded, start, nlines + 7, 1).astype(jnp.float32)
@@ -88,20 +109,12 @@
     weights = table[kern_lines]
     coeff = jnp.take(table, kern_range, axis=0)
     shift = (shift_range + OFFRG)[:, None]
-    out = pl.pallas_call(
-        resample_kernel,
-        grid=(2, nlines // ROWS),
-        in_specs=[
-            pl.BlockSpec(memory_space=pltpu.SMEM),
-            pl.BlockSpec((1, nlines + 8, nrange), lambda c, t: (c, 0, 0)),
-            pl.BlockSpec((ROWS, 8), lambda c, t: (t, 0)),
-            pl.BlockSpec((ROWS, 1), lambda c, t: (t, 0)),
-        ],
-        out_specs=pl.BlockSpec((1, ROWS, nrange), lambda c, t: (c, t, 0)),
-        out_shape=jax.ShapeDtypeStruct((2, nlines, nrange), jnp.bfloat16),
-    )(weights, window, coeff, shift)
-    half = nrange // 2
-    return look_order(out[:, :, :half]), look_order(out[:, :, half:])
+    halves = []
+    for side in range(2):
+        ordered = look_order(resample_half(side, weights, window, coeff, shift))
+        width = ordered.shape[2] // PIECES
+        halves.append([ordered[:, :, p * width : (p + 1) * width] for p in range(PIECES)])
+    return halves
 
 
 CHUNK = 512
@@ -157,28 +170,25 @@
     own_left, own_right = resample_block(padded[0], az_offset[0], az_kernel[0], rg_offset[0], rg_kernel[0])
     date = lax.axis_index("date")
     even = date % 2 == 0
-
-    left_2 = shifted(own_left, "date", 2)
-    left_1 = swapped(jnp.where(even, left_2, own_left), "date")
-    left_4 = shifted(left_2, "date", 2)
-    left_3 = shifted(left_1, "date", 2)
-    right_2 = shifted(own_right, "date", -2)
-    right_1 = swapped(jnp.where(even, own_right, right_2), "date")
-    right_4 = shifted(right_2, "date", -2)
-    right_3 = shifted(right_1, "date", -2)
-
-    ahead = {
-        1: looks(own_left, left_1),
-        2: looks(own_left, left_2),
-        3: looks(own_left, left_3),
-        4: looks(own_left, left_4),
-    }
-    behind = {
-        1: looks(own_right, right_1),
-        2: looks(own_right, right_2),
-        3: looks(own_right, right_3),
-        4: looks(own_right, right_4),
-    }
+    ahead_parts = {s: [] for s in range(1, GAP + 1)}
+    behind_parts = {s: [] for s in range(1, GAP + 1)}
+    for piece in range(PIECES):
+        own = own_left[piece]
+        left_2 = shifted(own, "date", 2)
+        left_1 = swapped(jnp.where(even, left_2, own), "date")
+        left_4 = shifted(left_2, "date", 2)
+        left_3 = shifted(left_1, "date", 2)
+        for s, other in ((2, left_2), (1, left_1), (4, left_4), (3, left_3)):
+            ahead_parts[s].append(looks(own, other))
+        own = own_right[piece]
+        right_2 = shifted(own, "date", -2)
+        right_1 = swapped(jnp.where(even, own, right_2), "date")
+        right_4 = shifted(right_2, "date", -2)
+        right_3 = shifted(right_1, "date", -2)
+        for s, other in ((2, right_2), (1, right_1), (4, right_4), (3, right_3)):
+            behind_parts[s].append(looks(own, other))
+    ahead = {s: jnp.concatenate(parts, axis=2) for s, parts in ahead_parts.items()}
+    behind = {s: jnp.concatenate(parts, axis=2) for s, parts in behind_parts.items()}
     full = {}
     for s in range(1, GAP + 1):
         right_of_ahead = conj(shifted(behind[s], "date", s))

time: 229 us -> 257 us (1.12)
  starting transfers between devices: 48.7 us -> 72 us
  waiting for transfers between devices: 52.2 us -> 34.9 us
  Pallas kernels: 72.6 us -> 87.5 us
  other arithmetic: 18.6 us -> 25.3 us
    ppermute x14 -> x20, starting transfers between devices: 42.4 us -> 61.8 us  [shifted(): return lax.ppermute(block, axis, route)]
    ppermute x14 -> x20, waiting for transfers between devices: 52.2 us -> 34.9 us  [shifted(): return lax.ppermute(block, axis, route)]
    pallas_call x8 -> x16, Pallas kernels: 34.9 us -> 42.4 us  [looks(): pl.pallas_call(looks_kernel, grid=(width // CHUNK,), in_specs=[spec, spec...]
    pallas_call x1 -> x2, Pallas kernels: 37.7 us -> 45.1 us  [resample_half(): pl.pallas_call(functools.partial(resample_kernel, side), grid=(2, nlines...]
    concatenate x0 -> x8, other arithmetic: none -> 5.81 us  [shards(): jnp.concatenate(parts, axis=2)]
    pallas_call x0 -> x2, local copies, waits for them, and re-layouts: none -> 5.33 us  [resample_half(): pl.pallas_call(functools.partial(resample_kernel, side), grid=(2, nlines...]
    slice x3 -> x2, local copies, waits for them, and re-layouts: 4.72 us -> 0.1 us  [resample_block(): ordered[:, :, p * width:(p + 1) * width]]
    ppermute x2 -> x4, starting transfers between devices: 1.98 us -> 5.83 us  [swapped(): return lax.ppermute(block, axis, [(i, i ^ 1) for i in range(count)])]
  transfers between devices with their start and end apart: 18 -> 26, of which waited for: 6 -> 5; matrix products, arithmetic and copies ran while one was open for 6% -> 8% of each run, Pallas kernels for 15% -> 26%
where the time goes in v4:
time: 257 us; the launch traced here: 254 us
  Pallas kernels  87.5 us (34%)
  starting transfers between devices  72 us (28%)
  waiting for transfers between devices  34.9 us (14%)
  other arithmetic  25.3 us (10%)
  between operations  21.6 us (8%)
  local copies, waits for them, and re-layouts  12.8 us (5%)
    ppermute x20, starting transfers between devices, shifted(): return lax.ppermute(block, axis, route)  61.8 us
    pallas_call x2, Pallas kernels, resample_half(): pl.pallas_call(functools.partial(resample_kernel, side), grid=(2, nlines...  45.1 us
    pallas_call x16, Pallas kernels, looks(): pl.pallas_call(looks_kernel, grid=(width // CHUNK,), in_specs=[spec, spec...  42.4 us
    ppermute x20, waiting for transfers between devices, shifted(): return lax.ppermute(block, axis, route)  34.9 us
    ppermute x4, starting transfers between devices, swapped(): return lax.ppermute(block, axis, [(i, i ^ 1) for i in range(count)])  5.83 us
    concatenate x8, other arithmetic, shards(): jnp.concatenate(parts, axis=2)  5.81 us
    pallas_call x2, local copies, waits for them, and re-layouts, resample_half(): pl.pallas_call(functools.partial(resample_kernel, side), grid=(2, nlines...  5.33 us
  transfers between devices with their start and end apart: 26, of which 5 were waited for; matrix products, arithmetic and copies ran while one was open for 8% of the time, Pallas kernels for 26%

profile of v4, /device:TPU:0, one launch (start us, length us, event | category | flops | bytes accessed | tf_op | source)
XLA Modules:
  0.0 254.2 jit_solution(3157629856648193297)
XLA Ops:
  0.0 1.1 fusion.30
  1.1 1.3 collective-permute-start.1
  2.4 3.0 %collective-permute-start = (bf16[1,2,16,4096]{3,2,1,0:T(8,128)(2,1)S(1)}, bf16[1,2,16,4096]{3,2,1,0:T(8,128)(2,1)S(1)}, u32[]{:S(2)}, u32[]{:S(2)}) collective-permute-start(bf16[1,2,16,4096]{3,2,1,0:T(8,128)(2,1)S(1)} %get-tuple-element.6), channel_id=1, source_target_pairs={{0,1},{1,2},{2,3},{4,5},{5,6},{6,7},{8,9},{9,10},{10,11},{12,13},{... | collective-permute-start | bytes 786440 | tf_op jit(solution)/shard_map/ppermute | solution.py:27
  11.9 3.5 %fusion.2 = bf16[2,167,4096]{2,1,0:T(8,128)(2,1)S(1)} fusion(s32[]{:T(128)S(6)} %select_n.510, bf16[1,2,16,4096]{3,2,1,0:T(8,128)(2,1)S(1)} %collective-permute-done, bf16[1,2,160,4096]{3,2,1,0:T(8,128)(2,1)} %param.6, bf16[1,2,16,4096]{3,2,1,0:T(8,128)(2,1)S(1)} %collective-permute-done.1), kind=kLoop, calls=%fused_computation.6 | loop fusion | flops 8208384 | bytes 5881860 | tf_op jit(solution)/shard_map/convert_element_type | solution.py:107
  15.3 3.1 %pad_convert_fusion.window_ref = f32[2,168,4096]{2,1,0:T(8,128)} fusion(bf16[2,167,4096]{2,1,0:T(8,128)(2,1)S(1)} %fusion.2), kind=kLoop, calls=%fused_computation.7 | loop fusion | flops 1376256 | bytes 8241152 | tf_op jit(solution)/shard_map/jit(_pad)/pad | solution.py:108
  18.4 22.5 %shard_map.64 = bf16[2,160,2048]{2,1,0:T(8,128)(2,1)} custom-call(f32[8]{0:T(128)} %dynamic-slice_reduce_fusion.weights_ref, f32[2,168,4096]{2,1,0:T(8,128)} %pad_convert_fusion.window_ref, f32[160,8]{1,0:T(8,128)} %broadcast_select_fusion.4.coeff_ref, s32[160,1]{1,0:T(8,128)} %copy.23.shift_ref), custom_call_target="tpu_custom_call" | custom-call | tf_op jit(solution)/shard_map/pallas_call | solution.py:88
  40.9 2.7 %copy.24 = bf16[2,160,2048]{2,0,1:T(2,128)(2,1)S(1)} copy(bf16[2,160,2048]{2,1,0:T(8,128)(2,1)} %shard_map.64) | data formatting | bytes 2621440 | tf_op jit(solution)/shard_map/pallas_call | solution.py:88
  44.4 1.3 collective-permute-start.2
  45.7 22.6 %shard_map.67 = bf16[2,160,2048]{2,1,0:T(8,128)(2,1)} custom-call(f32[8]{0:T(128)} %dynamic-slice_reduce_fusion.weights_ref, f32[2,168,4096]{2,1,0:T(8,128)} %pad_convert_fusion.window_ref, f32[160,8]{1,0:T(8,128)} %broadcast_select_fusion.4.coeff_ref, s32[160,1]{1,0:T(8,128)} %copy.23.shift_ref), custom_call_target="tpu_custom_call" | custom-call | tf_op jit(solution)/shard_map/pallas_call | solution.py:88
  68.3 2.7 %copy.27 = bf16[2,160,2048]{2,0,1:T(2,128)(2,1)S(1)} copy(bf16[2,160,2048]{2,1,0:T(8,128)(2,1)} %shard_map.67) | data formatting | bytes 2621440 | tf_op jit(solution)/shard_map/pallas_call | solution.py:88
  71.7 1.1 copy-done.4
  72.8 6.4 %collective-permute-start.7 = (bf16[2,160,1024]{2,1,0:T(8,128)(2,1)S(1)}, bf16[2,160,1024]{2,1,0:T(8,128)(2,1)}, u32[]{:S(2)}, u32[]{:S(2)}) collective-permute-start(bf16[2,160,1024]{2,1,0:T(8,128)(2,1)S(1)} %slice.142.first_ref), channel_id=1, source_target_pairs={{0,8},{4,12},{8,16},{12,20},{16,24},{20,28},{1,9},{5,13},{9,17},{1... | collective-permute-start | bytes 1966088 | tf_op jit(solution)/shard_map/ppermute | solution.py:39
  79.3 2.1 broadcast_select_fusion.3
  81.4 1.3 collective-permute-start.4
  82.7 10.6 %collective-permute-done.7.second_ref = bf16[2,160,1024]{2,1,0:T(8,128)(2,1)} collective-permute-done((bf16[2,160,1024]{2,1,0:T(8,128)(2,1)S(1)}, bf16[2,160,1024]{2,1,0:T(8,128)(2,1)}, u32[]{:S(2)}, u32[]{:S(2)}) %collective-permute-start.7) | collective-permute-done | bytes 655392 | tf_op jit(solution)/shard_map/ppermute | solution.py:39
  93.3 1.0 broadcast_select_fusion.1
  94.3 5.4 %collective-permute-start.9 = (bf16[2,160,1024]{2,1,0:T(8,128)(2,1)S(1)}, bf16[2,160,1024]{2,1,0:T(8,128)(2,1)}, u32[]{:S(2)}, u32[]{:S(2)}) collective-permute-start(bf16[2,160,1024]{2,1,0:T(8,128)(2,1)S(1)} %get-tuple-element.10.first_ref), channel_id=1, source_target_pairs={{0,8},{4,12},{8,16},{12,20},{16,24},{20,28},{1,9},{5,13},{9,17},{1... | collective-permute-start | bytes 1966088 | tf_op jit(solution)/shard_map/ppermute | solution.py:39
  120.0 3.2 %collective-permute-start.12 = (bf16[2,160,1024]{2,1,0:T(8,128)(2,1)}, bf16[2,160,1024]{2,1,0:T(8,128)(2,1)}, u32[]{:S(2)}, u32[]{:S(2)}) collective-permute-start(bf16[2,160,1024]{2,1,0:T(8,128)(2,1)} %get-tuple-element.7), channel_id=1, source_target_pairs={{0,4},{4,0},{8,12},{12,8},{16,20},{20,16},{24,28},{28,24},{1,5},{5... | collective-permute-start | bytes 1966088 | tf_op jit(solution)/shard_map/ppermute | solution.py:44
  123.3 2.6 %shard_map.74 = f32[2,8,256]{2,1,0:T(8,128)} custom-call(bf16[2,160,1024]{2,1,0:T(8,128)(2,1)} %copy-done, bf16[2,160,1024]{2,1,0:T(8,128)(2,1)} %collective-permute-done.2.second_ref), custom_call_target="tpu_custom_call" | custom-call | tf_op jit(solution)/shard_map/pallas_call | solution.py:149
  125.9 1.3 collective-permute-start.3
  127.2 2.7 %shard_map.76 = f32[2,8,256]{2,1,0:T(8,128)} custom-call(bf16[2,160,1024]{2,1,0:T(8,128)(2,1)} %copy-done.1, bf16[2,160,1024]{2,1,0:T(8,128)(2,1)} %collective-permute-done.7.second_ref), custom_call_target="tpu_custom_call" | custom-call | tf_op jit(solution)/shard_map/pallas_call | solution.py:149
  129.9 5.5 %collective-permute-start.8 = (bf16[2,160,1024]{2,1,0:T(8,128)(2,1)}, bf16[2,160,1024]{2,1,0:T(8,128)(2,1)}, u32[]{:S(2)}, u32[]{:S(2)}) collective-permute-start(bf16[2,160,1024]{2,1,0:T(8,128)(2,1)} %collective-permute-done.7.second_ref), channel_id=1, source_target_pairs={{0,8},{4,12},{8,16},{12,20},{16,24},{20,28},{1,9},{5,13},{9,17},{1... | collective-permute-start | bytes 1966088 | tf_op jit(solution)/shard_map/ppermute | solution.py:39
  135.4 2.6 %shard_map.75 = f32[2,8,256]{2,1,0:T(8,128)} custom-call(bf16[2,160,1024]{2,1,0:T(8,128)(2,1)} %copy-done.3, bf16[2,160,1024]{2,1,0:T(8,128)(2,1)} %collective-permute-done.4.second_ref), custom_call_target="tpu_custom_call" | custom-call | tf_op jit(solution)/shard_map/pallas_call | solution.py:149
  138.1 2.0 broadcast_select_fusion.2
  140.1 0.8 collective-permute-start.14
  141.0 2.6 %shard_map.77 = f32[2,8,256]{2,1,0:T(8,128)} custom-call(bf16[2,160,1024]{2,1,0:T(8,128)(2,1)} %copy-done.2, bf16[2,160,1024]{2,1,0:T(8,128)(2,1)} %collective-permute-done.9.second_ref), custom_call_target="tpu_custom_call" | custom-call | tf_op jit(solution)/shard_map/pallas_call | solution.py:149
  144.2 3.3 %collective-permute-start.22 = (f32[2,8,512]{2,1,0:T(8,128)S(1)}, f32[2,8,512]{2,1,0:T(8,128)S(1)}, u32[]{:S(2)}, u32[]{:S(2)}) collective-permute-start(f32[2,8,512]{2,1,0:T(8,128)S(1)} %pad_maximum_fusion.12), channel_id=1, source_target_pairs={{0,8},{4,12},{8,16},{12,20},{16,24},{20,28},{1,9},{5,13},{9,17},{1... | collective-permute-start | bytes 98312 | tf_op jit(solution)/shard_map/ppermute | solution.py:39
  148.3 2.6 %shard_map.65 = f32[2,8,256]{2,1,0:T(8,128)} custom-call(bf16[2,160,1024]{2,1,0:T(8,128)(2,1)} %copy-done, bf16[2,160,1024]{2,1,0:T(8,128)(2,1)} %collective-permute-done.3.second_ref), custom_call_target="tpu_custom_call" | custom-call | tf_op jit(solution)/shard_map/pallas_call | solution.py:149
  150.9 1.3 collective-permute-start.23
  152.2 2.7 %shard_map.68 = f32[2,8,256]{2,1,0:T(8,128)} custom-call(bf16[2,160,1024]{2,1,0:T(8,128)(2,1)} %copy-done.1, bf16[2,160,1024]{2,1,0:T(8,128)(2,1)} %collective-permute-done.8.second_ref), custom_call_target="tpu_custom_call" | custom-call | tf_op jit(solution)/shard_map/pallas_call | solution.py:149
  154.9 1.7 collective-permute-start.19
  156.6 2.6 %shard_map.78 = f32[2,8,256]{2,1,0:T(8,128)} custom-call(bf16[2,160,1024]{2,1,0:T(8,128)(2,1)} %copy-done, bf16[2,160,1024]{2,1,0:T(8,128)(2,1)} %collective-permute-done.12.second_ref), custom_call_target="tpu_custom_call" | custom-call | tf_op jit(solution)/shard_map/pallas_call | solution.py:149
  159.2 1.4 collective-permute-start.13
  160.7 2.7 %shard_map.80 = f32[2,8,256]{2,1,0:T(8,128)} custom-call(bf16[2,160,1024]{2,1,0:T(8,128)(2,1)} %copy-done.1, bf16[2,160,1024]{2,1,0:T(8,128)(2,1)} %collective-permute-done.17.second_ref), custom_call_target="tpu_custom_call" | custom-call | tf_op jit(solution)/shard_map/pallas_call | solution.py:149
  163.3 1.3 collective-permute-start.5
  164.6 6.7 %collective-permute-start.10 = (bf16[2,160,1024]{2,1,0:T(8,128)(2,1)}, bf16[2,160,1024]{2,1,0:T(8,128)(2,1)}, u32[]{:S(2)}, u32[]{:S(2)}) collective-permute-start(bf16[2,160,1024]{2,1,0:T(8,128)(2,1)} %collective-permute-done.9.second_ref), channel_id=1, source_target_pairs={{0,8},{4,12},{8,16},{12,20},{16,24},{20,28},{1,9},{5,13},{9,17},{1... | collective-permute-start | bytes 1966088 | tf_op jit(solution)/shard_map/ppermute | solution.py:39
  171.4 3.2 %collective-permute-start.18 = (bf16[2,160,1024]{2,1,0:T(8,128)(2,1)}, bf16[2,160,1024]{2,1,0:T(8,128)(2,1)S(1)}, u32[]{:S(2)}, u32[]{:S(2)}) collective-permute-start(bf16[2,160,1024]{2,1,0:T(8,128)(2,1)} %collective-permute-done.17.second_ref), channel_id=1, source_target_pairs={{0,8},{4,12},{8,16},{12,20},{16,24},{20,28},{1,9},{5,13},{9,17},{1... | collective-permute-start | bytes 1966088 | tf_op jit(solution)/shard_map/ppermute | solution.py:39
  174.6 2.7 %shard_map.79 = f32[2,8,256]{2,1,0:T(8,128)} custom-call(bf16[2,160,1024]{2,1,0:T(8,128)(2,1)} %copy-done.3, bf16[2,160,1024]{2,1,0:T(8,128)(2,1)} %copy-done.7), custom_call_target="tpu_custom_call" | custom-call | tf_op jit(solution)/shard_map/pallas_call | solution.py:149
  177.3 1.3 pad_maximum_fusion.14
  178.6 12.7 %collective-permute-done.5.second_ref = bf16[2,160,1024]{2,1,0:T(8,128)(2,1)} collective-permute-done((bf16[2,160,1024]{2,1,0:T(8,128)(2,1)}, bf16[2,160,1024]{2,1,0:T(8,128)(2,1)}, u32[]{:S(2)}, u32[]{:S(2)}) %collective-permute-start.5) | collective-permute-done | bytes 655392 | tf_op jit(solution)/shard_map/ppermute | solution.py:39
  191.3 2.2 collective-permute-start.24
  193.5 2.7 %shard_map.66 = f32[2,8,256]{2,1,0:T(8,128)} custom-call(bf16[2,160,1024]{2,1,0:T(8,128)(2,1)} %copy-done.3, bf16[2,160,1024]{2,1,0:T(8,128)(2,1)} %collective-permute-done.5.second_ref), custom_call_target="tpu_custom_call" | custom-call | tf_op jit(solution)/shard_map/pallas_call | solution.py:149
  196.9 5.4 %collective-permute-start.6 = (f32[2,8,512]{2,1,0:T(8,128)S(1)}, f32[2,8,512]{2,1,0:T(8,128)}, u32[]{:S(2)}, u32[]{:S(2)}) collective-permute-start(f32[2,8,512]{2,1,0:T(8,128)S(1)} %pad_maximum_fusion.8), channel_id=1, source_target_pairs={{0,16},{4,20},{8,24},{12,28},{1,17},{5,21},{9,25},{13,29},{2,18},{... | collective-permute-start | bytes 98312 | tf_op jit(solution)/shard_map/ppermute | solution.py:39
  202.3 2.6 %shard_map.81 = f32[2,8,256]{2,1,0:T(8,128)} custom-call(bf16[2,160,1024]{2,1,0:T(8,128)(2,1)} %copy-done.2, bf16[2,160,1024]{2,1,0:T(8,128)(2,1)} %copy-done.9), custom_call_target="tpu_custom_call" | custom-call | tf_op jit(solution)/shard_map/pallas_call | solution.py:149
  204.9 0.8 pad_maximum_fusion.15
  205.7 1.3 collective-permute-start.25
  207.0 2.7 %shard_map.69 = f32[2,8,256]{2,1,0:T(8,128)} custom-call(bf16[2,160,1024]{2,1,0:T(8,128)(2,1)} %copy-done.2, bf16[2,160,1024]{2,1,0:T(8,128)(2,1)} %collective-permute-done.10.second_ref), custom_call_target="tpu_custom_call" | custom-call | tf_op jit(solution)/shard_map/pallas_call | solution.py:149
  210.4 1.3 collective-permute-start.11
  211.7 2.7 %shard_map.70 = f32[2,8,256]{2,1,0:T(8,128)} custom-call(bf16[2,160,1024]{2,1,0:T(8,128)(2,1)} %copy-done, bf16[2,160,1024]{2,1,0:T(8,128)(2,1)} %copy-done.11), custom_call_target="tpu_custom_call" | custom-call | tf_op jit(solution)/shard_map/pallas_call | solution.py:149
  214.4 1.4 collective-permute-start.15
  215.9 2.7 %shard_map.72 = f32[2,8,256]{2,1,0:T(8,128)} custom-call(bf16[2,160,1024]{2,1,0:T(8,128)(2,1)} %copy-done.1, bf16[2,160,1024]{2,1,0:T(8,128)(2,1)} %copy-done.12), custom_call_target="tpu_custom_call" | custom-call | tf_op jit(solution)/shard_map/pallas_call | solution.py:149
  218.5 5.4 %collective-permute-start.20 = (bf16[2,160,1024]{2,1,0:T(8,128)(2,1)S(1)}, bf16[2,160,1024]{2,1,0:T(8,128)(2,1)S(1)}, u32[]{:S(2)}, u32[]{:S(2)}) collective-permute-start(bf16[2,160,1024]{2,1,0:T(8,128)(2,1)S(1)} %copy-done.10), channel_id=1, source_target_pairs={{0,8},{4,12},{8,16},{12,20},{16,24},{20,28},{1,9},{5,13},{9,17},{1... | collective-permute-start | bytes 1966088 | tf_op jit(solution)/shard_map/ppermute | solution.py:39
  224.8 5.8 %collective-permute-done.15.second_ref = bf16[2,160,1024]{2,1,0:T(8,128)(2,1)} collective-permute-done((bf16[2,160,1024]{2,1,0:T(8,128)(2,1)S(1)}, bf16[2,160,1024]{2,1,0:T(8,128)(2,1)}, u32[]{:S(2)}, u32[]{:S(2)}) %collective-permute-start.15) | collective-permute-done | bytes 655392 | tf_op jit(solution)/shard_map/ppermute | solution.py:39
  230.6 2.6 %shard_map.71 = f32[2,8,256]{2,1,0:T(8,128)} custom-call(bf16[2,160,1024]{2,1,0:T(8,128)(2,1)} %copy-done.3, bf16[2,160,1024]{2,1,0:T(8,128)(2,1)} %collective-permute-done.15.second_ref), custom_call_target="tpu_custom_call" | custom-call | tf_op jit(solution)/shard_map/pallas_call | solution.py:149
  233.2 0.8 pad_maximum_fusion.10
  234.0 5.2 %collective-permute-start.16 = (f32[2,8,512]{2,1,0:T(8,128)S(1)}, f32[2,8,512]{2,1,0:T(8,128)S(1)}, u32[]{:S(2)}, u32[]{:S(2)}) collective-permute-start(f32[2,8,512]{2,1,0:T(8,128)S(1)} %pad_maximum_fusion.10), channel_id=1, source_target_pairs={{0,12},{4,16},{8,20},{12,24},{16,28},{1,13},{5,17},{9,21},{13,25},... | collective-permute-start | bytes 98312 | tf_op jit(solution)/shard_map/ppermute | solution.py:39
  239.2 0.9 copy-done.13
  240.1 2.7 %shard_map.73 = f32[2,8,256]{2,1,0:T(8,128)} custom-call(bf16[2,160,1024]{2,1,0:T(8,128)(2,1)} %copy-done.2, bf16[2,160,1024]{2,1,0:T(8,128)(2,1)} %copy-done.13), custom_call_target="tpu_custom_call" | custom-call | tf_op jit(solution)/shard_map/pallas_call | solution.py:149
  243.5 1.3 collective-permute-start.21
  244.8 5.4 %collective-permute-done.21 = f32[2,8,512]{2,1,0:T(8,128)S(1)} collective-permute-done((f32[2,8,512]{2,1,0:T(8,128)S(1)}, f32[2,8,512]{2,1,0:T(8,128)S(1)}, u32[]{:S(2)}, u32[]{:S(2)}) %collective-permute-start.21) | collective-permute-done | bytes 32800 | tf_op jit(solution)/shard_map/ppermute | solution.py:39
  250.3 0.8 select_select_fusion.2
  251.1 0.8 select_select_fusion.1
  251.9 0.8 select_select_fusion
  252.7 0.8 select_select_fusion.3
  (125 shorter events, 12.5 us)
Async XLA Ops:
  1.1 10.8 %collective-permute-start.1 = (bf16[1,2,16,4096]{3,2,1,0:T(8,128)(2,1)S(1)}, bf16[1,2,16,4096]{3,2,1,0:T(8,128)(2,1)S(1)}, u32[]{:S(2)}, u32[]{:S(2)}) collective-permute-start(bf16[1,2,16,4096]{3,2,1,0:T(8,128)(2,1)S(1)} %get-tuple-element.5), channel_id=1, source_target_pairs={{1,0},{2,1},{3,2},{5,4},{6,5},{7,6},{9,8},{10,9},{11,10},{13,12},{... | collective-permute-start | bytes 786440 | tf_op jit(solution)/shard_map/ppermute | solution.py:29
  2.4 9.5 %collective-permute-start = (bf16[1,2,16,4096]{3,2,1,0:T(8,128)(2,1)S(1)}, bf16[1,2,16,4096]{3,2,1,0:T(8,128)(2,1)S(1)}, u32[]{:S(2)}, u32[]{:S(2)}) collective-permute-start(bf16[1,2,16,4096]{3,2,1,0:T(8,128)(2,1)S(1)} %get-tuple-element.6), channel_id=1, source_target_pairs={{0,1},{1,2},{2,3},{4,5},{5,6},{6,7},{8,9},{9,10},{10,11},{12,13},{... | collective-permute-start | bytes 786440 | tf_op jit(solution)/shard_map/ppermute | solution.py:27
  44.4 23.9 %copy-start = (bf16[2,160,1024]{2,1,0:T(8,128)(2,1)}, bf16[2,160,1024]{2,1,0:T(8,128)(2,1)S(1)}, u32[]{:S(2)}) copy-start(bf16[2,160,1024]{2,1,0:T(8,128)(2,1)S(1)} %slice.138.first_ref) | copy-start | bytes 1966084
  44.4 34.9 %collective-permute-start.2 = (bf16[2,160,1024]{2,1,0:T(8,128)(2,1)S(1)}, bf16[2,160,1024]{2,1,0:T(8,128)(2,1)}, u32[]{:S(2)}, u32[]{:S(2)}) collective-permute-start(bf16[2,160,1024]{2,1,0:T(8,128)(2,1)S(1)} %slice.138.first_ref), channel_id=1, source_target_pairs={{8,0},{12,4},{16,8},{20,12},{24,16},{28,20},{9,1},{13,5},{17,9},{2... | collective-permute-start | bytes 1966088 | tf_op jit(solution)/shard_map/ppermute | solution.py:39
  71.7 1.1 copy-start.4
  72.8 21.5 %copy-start.1 = (bf16[2,160,1024]{2,1,0:T(8,128)(2,1)}, bf16[2,160,1024]{2,1,0:T(8,128)(2,1)S(1)}, u32[]{:S(2)}) copy-start(bf16[2,160,1024]{2,1,0:T(8,128)(2,1)S(1)} %slice.142.first_ref) | copy-start | bytes 1966084
  72.8 20.5 %collective-permute-start.7 = (bf16[2,160,1024]{2,1,0:T(8,128)(2,1)S(1)}, bf16[2,160,1024]{2,1,0:T(8,128)(2,1)}, u32[]{:S(2)}, u32[]{:S(2)}) collective-permute-start(bf16[2,160,1024]{2,1,0:T(8,128)(2,1)S(1)} %slice.142.first_ref), channel_id=1, source_target_pairs={{0,8},{4,12},{8,16},{12,20},{16,24},{20,28},{1,9},{5,13},{9,17},{1... | collective-permute-start | bytes 1966088 | tf_op jit(solution)/shard_map/ppermute | solution.py:39
  79.3 14.0 %copy-start.5 = (bf16[2,20,8,2048]{3,2,1,0:T(8,128)(2,1)S(1)}, bf16[2,20,8,2048]{3,2,1,0:T(8,128)(2,1)}, u32[]{:S(2)}) copy-start(bf16[2,20,8,2048]{3,2,1,0:T(8,128)(2,1)} %copy-done.4) | copy-start | bytes 3932164
  79.3 20.4 %copy-start.31 = (s32[1,4]{1,0:T(1,128)S(1)}, s32[1,4]{1,0:T(1,128)}, u32[]{:S(2)}) copy-start(s32[1,4]{1,0:T(1,128)} %param.11) | copy-start | bytes 52
  81.4 48.5 %copy-start.3 = (bf16[2,160,1024]{2,1,0:T(8,128)(2,1)}, bf16[2,160,1024]{2,1,0:T(8,128)(2,1)S(1)}, u32[]{:S(2)}) copy-start(bf16[2,160,1024]{2,1,0:T(8,128)(2,1)S(1)} %get-tuple-element.8.first_ref) | copy-start | bytes 1966084
  81.4 48.5 %collective-permute-start.4 = (bf16[2,160,1024]{2,1,0:T(8,128)(2,1)S(1)}, bf16[2,160,1024]{2,1,0:T(8,128)(2,1)}, u32[]{:S(2)}, u32[]{:S(2)}) collective-permute-start(bf16[2,160,1024]{2,1,0:T(8,128)(2,1)S(1)} %get-tuple-element.8.first_ref), channel_id=1, source_target_pairs={{8,0},{12,4},{16,8},{20,12},{24,16},{28,20},{9,1},{13,5},{17,9},{2... | collective-permute-start | bytes 1966088 | tf_op jit(solution)/shard_map/ppermute | solution.py:39
  94.3 45.8 %copy-start.2 = (bf16[2,160,1024]{2,1,0:T(8,128)(2,1)}, bf16[2,160,1024]{2,1,0:T(8,128)(2,1)S(1)}, u32[]{:S(2)}) copy-start(bf16[2,160,1024]{2,1,0:T(8,128)(2,1)S(1)} %get-tuple-element.10.first_ref) | copy-start | bytes 1966084
  94.3 45.8 %collective-permute-start.9 = (bf16[2,160,1024]{2,1,0:T(8,128)(2,1)S(1)}, bf16[2,160,1024]{2,1,0:T(8,128)(2,1)}, u32[]{:S(2)}, u32[]{:S(2)}) collective-permute-start(bf16[2,160,1024]{2,1,0:T(8,128)(2,1)S(1)} %get-tuple-element.10.first_ref), channel_id=1, source_target_pairs={{0,8},{4,12},{8,16},{12,20},{16,24},{20,28},{1,9},{5,13},{9,17},{1... | collective-permute-start | bytes 1966088 | tf_op jit(solution)/shard_map/ppermute | solution.py:39
  120.0 34.8 %collective-permute-start.12 = (bf16[2,160,1024]{2,1,0:T(8,128)(2,1)}, bf16[2,160,1024]{2,1,0:T(8,128)(2,1)}, u32[]{:S(2)}, u32[]{:S(2)}) collective-permute-start(bf16[2,160,1024]{2,1,0:T(8,128)(2,1)} %get-tuple-element.7), channel_id=1, source_target_pairs={{0,4},{4,0},{8,12},{12,8},{16,20},{20,16},{24,28},{28,24},{1,5},{5... | collective-permute-start | bytes 1966088 | tf_op jit(solution)/shard_map/ppermute | solution.py:44
  123.2 36.0 %collective-permute-start.17 = (bf16[2,160,1024]{2,1,0:T(8,128)(2,1)}, bf16[2,160,1024]{2,1,0:T(8,128)(2,1)}, u32[]{:S(2)}, u32[]{:S(2)}) collective-permute-start(bf16[2,160,1024]{2,1,0:T(8,128)(2,1)} %get-tuple-element.9), channel_id=1, source_target_pairs={{0,4},{4,0},{8,12},{12,8},{16,20},{20,16},{24,28},{28,24},{1,5},{5... | collective-permute-start | bytes 1966088 | tf_op jit(solution)/shard_map/ppermute | solution.py:44
  125.9 18.2 %collective-permute-start.3 = (bf16[2,160,1024]{2,1,0:T(8,128)(2,1)}, bf16[2,160,1024]{2,1,0:T(8,128)(2,1)}, u32[]{:S(2)}, u32[]{:S(2)}) collective-permute-start(bf16[2,160,1024]{2,1,0:T(8,128)(2,1)} %collective-permute-done.2.second_ref), channel_id=1, source_target_pairs={{8,0},{12,4},{16,8},{20,12},{24,16},{28,20},{9,1},{13,5},{17,9},{2... | collective-permute-start | bytes 1966088 | tf_op jit(solution)/shard_map/ppermute | solution.py:39
  129.9 13.7 %copy-start.6 = (bf16[2,20,8,2048]{3,2,1,0:T(8,128)(2,1)S(1)}, bf16[2,20,8,2048]{3,2,1,0:T(8,128)(2,1)}, u32[]{:S(2)}) copy-start(bf16[2,20,8,2048]{3,2,1,0:T(8,128)(2,1)} %copy-done.4) | copy-start | bytes 3932164
  129.9 21.0 %collective-permute-start.8 = (bf16[2,160,1024]{2,1,0:T(8,128)(2,1)}, bf16[2,160,1024]{2,1,0:T(8,128)(2,1)}, u32[]{:S(2)}, u32[]{:S(2)}) collective-permute-start(bf16[2,160,1024]{2,1,0:T(8,128)(2,1)} %collective-permute-done.7.second_ref), channel_id=1, source_target_pairs={{0,8},{4,12},{8,16},{12,20},{16,24},{20,28},{1,9},{5,13},{9,17},{1... | collective-permute-start | bytes 1966088 | tf_op jit(solution)/shard_map/ppermute | solution.py:39
  138.1 5.6 %copy-start.14 = (f32[2,8,256]{2,1,0:T(8,128)S(1)}, f32[2,8,256]{2,1,0:T(8,128)}, u32[]{:S(2)}) copy-start(f32[2,8,256]{2,1,0:T(8,128)} %shard_map.74) | copy-start | bytes 49156
  138.1 5.6 %copy-start.16 = (f32[2,8,256]{2,1,0:T(8,128)S(1)}, f32[2,8,256]{2,1,0:T(8,128)}, u32[]{:S(2)}) copy-start(f32[2,8,256]{2,1,0:T(8,128)} %shard_map.75) | copy-start | bytes 49156
  138.1 9.4 %copy-start.15 = (f32[2,8,256]{2,1,0:T(8,128)S(1)}, f32[2,8,256]{2,1,0:T(8,128)}, u32[]{:S(2)}) copy-start(f32[2,8,256]{2,1,0:T(8,128)} %shard_map.76) | copy-start | bytes 49156
  140.1 31.3 %collective-permute-start.14 = (bf16[2,160,1024]{2,1,0:T(8,128)(2,1)}, bf16[2,160,1024]{2,1,0:T(8,128)(2,1)S(1)}, u32[]{:S(2)}, u32[]{:S(2)}) collective-permute-start(bf16[2,160,1024]{2,1,0:T(8,128)(2,1)} %broadcast_select_fusion.2), channel_id=1, source_target_pairs={{0,4},{4,0},{8,12},{12,8},{16,20},{20,16},{24,28},{28,24},{1,5},{5... | collective-permute-start | bytes 1966088 | tf_op jit(solution)/shard_map/ppermute | solution.py:44
  144.2 19.1 %collective-permute-start.22 = (f32[2,8,512]{2,1,0:T(8,128)S(1)}, f32[2,8,512]{2,1,0:T(8,128)S(1)}, u32[]{:S(2)}, u32[]{:S(2)}) collective-permute-start(f32[2,8,512]{2,1,0:T(8,128)S(1)} %pad_maximum_fusion.12), channel_id=1, source_target_pairs={{0,8},{4,12},{8,16},{12,20},{16,24},{20,28},{1,9},{5,13},{9,17},{1... | collective-permute-start | bytes 98312 | tf_op jit(solution)/shard_map/ppermute | solution.py:39
  150.9 13.7 %collective-permute-start.23 = (f32[2,8,512]{2,1,0:T(8,128)S(1)}, f32[2,8,512]{2,1,0:T(8,128)S(1)}, u32[]{:S(2)}, u32[]{:S(2)}) collective-permute-start(f32[2,8,512]{2,1,0:T(8,128)S(1)} %pad_maximum_fusion.13), channel_id=1, source_target_pairs={{8,0},{12,4},{16,8},{20,12},{24,16},{28,20},{9,1},{13,5},{17,9},{2... | collective-permute-start | bytes 98312 | tf_op jit(solution)/shard_map/ppermute | solution.py:39
  154.9 41.3 %copy-start.18 = (f32[2,8,256]{2,1,0:T(8,128)S(1)}, f32[2,8,256]{2,1,0:T(8,128)}, u32[]{:S(2)}) copy-start(f32[2,8,256]{2,1,0:T(8,128)} %shard_map.65) | copy-start | bytes 49156
  154.9 42.0 %collective-permute-start.19 = (bf16[2,160,1024]{2,1,0:T(8,128)(2,1)S(1)}, bf16[2,160,1024]{2,1,0:T(8,128)(2,1)S(1)}, u32[]{:S(2)}, u32[]{:S(2)}) collective-permute-start(bf16[2,160,1024]{2,1,0:T(8,128)(2,1)S(1)} %broadcast_select_fusion), channel_id=1, source_target_pairs={{0,4},{4,0},{8,12},{12,8},{16,20},{20,16},{24,28},{28,24},{1,5},{5... | collective-permute-start | bytes 1966088 | tf_op jit(solution)/shard_map/ppermute | solution.py:44
  159.2 18.0 %copy-start.20 = (f32[2,8,256]{2,1,0:T(8,128)S(1)}, f32[2,8,256]{2,1,0:T(8,128)}, u32[]{:S(2)}) copy-start(f32[2,8,256]{2,1,0:T(8,128)} %shard_map.78) | copy-start | bytes 49156
  159.2 51.1 %collective-permute-start.13 = (bf16[2,160,1024]{2,1,0:T(8,128)(2,1)}, bf16[2,160,1024]{2,1,0:T(8,128)(2,1)S(1)}, u32[]{:S(2)}, u32[]{:S(2)}) collective-permute-start(bf16[2,160,1024]{2,1,0:T(8,128)(2,1)} %collective-permute-done.12.second_ref), channel_id=1, source_target_pairs={{8,0},{12,4},{16,8},{20,12},{24,16},{28,20},{9,1},{13,5},{17,9},{2... | collective-permute-start | bytes 1966088 | tf_op jit(solution)/shard_map/ppermute | solution.py:39
  163.3 27.9 %collective-permute-start.5 = (bf16[2,160,1024]{2,1,0:T(8,128)(2,1)}, bf16[2,160,1024]{2,1,0:T(8,128)(2,1)}, u32[]{:S(2)}, u32[]{:S(2)}) collective-permute-start(bf16[2,160,1024]{2,1,0:T(8,128)(2,1)} %collective-permute-done.4.second_ref), channel_id=1, source_target_pairs={{8,0},{12,4},{16,8},{20,12},{24,16},{28,20},{9,1},{13,5},{17,9},{2... | collective-permute-start | bytes 1966088 | tf_op jit(solution)/shard_map/ppermute | solution.py:39
  164.6 41.1 %collective-permute-start.10 = (bf16[2,160,1024]{2,1,0:T(8,128)(2,1)}, bf16[2,160,1024]{2,1,0:T(8,128)(2,1)}, u32[]{:S(2)}, u32[]{:S(2)}) collective-permute-start(bf16[2,160,1024]{2,1,0:T(8,128)(2,1)} %collective-permute-done.9.second_ref), channel_id=1, source_target_pairs={{0,8},{4,12},{8,16},{12,20},{16,24},{20,28},{1,9},{5,13},{9,17},{1... | collective-permute-start | bytes 1966088 | tf_op jit(solution)/shard_map/ppermute | solution.py:39
  171.4 3.2 %copy-start.7 = (bf16[2,160,1024]{2,1,0:T(8,128)(2,1)}, bf16[2,160,1024]{2,1,0:T(8,128)(2,1)S(1)}, u32[]{:S(2)}) copy-start(bf16[2,160,1024]{2,1,0:T(8,128)(2,1)S(1)} %collective-permute-done.14.second_ref) | copy-start | bytes 1966084
  171.4 43.0 %collective-permute-start.18 = (bf16[2,160,1024]{2,1,0:T(8,128)(2,1)}, bf16[2,160,1024]{2,1,0:T(8,128)(2,1)S(1)}, u32[]{:S(2)}, u32[]{:S(2)}) collective-permute-start(bf16[2,160,1024]{2,1,0:T(8,128)(2,1)} %collective-permute-done.17.second_ref), channel_id=1, source_target_pairs={{0,8},{4,12},{8,16},{12,20},{16,24},{20,28},{1,9},{5,13},{9,17},{1... | collective-permute-start | bytes 1966088 | tf_op jit(solution)/shard_map/ppermute | solution.py:39
  174.6 35.1 %copy-start.19 = (f32[2,8,256]{2,1,0:T(8,128)S(1)}, f32[2,8,256]{2,1,0:T(8,128)}, u32[]{:S(2)}) copy-start(f32[2,8,256]{2,1,0:T(8,128)} %shard_map.68) | copy-start | bytes 49156
  177.3 27.7 %copy-start.22 = (f32[2,8,256]{2,1,0:T(8,128)S(1)}, f32[2,8,256]{2,1,0:T(8,128)}, u32[]{:S(2)}) copy-start(f32[2,8,256]{2,1,0:T(8,128)} %shard_map.80) | copy-start | bytes 49156
  178.6 35.8 %copy-start.8 = (bf16[2,160,1024]{2,1,0:T(8,128)(2,1)S(1)}, bf16[2,160,1024]{2,1,0:T(8,128)(2,1)}, u32[]{:S(2)}) copy-start(bf16[2,160,1024]{2,1,0:T(8,128)(2,1)} %copy-done.7) | copy-start | bytes 1966084
  191.3 27.3 %collective-permute-start.24 = (f32[2,8,512]{2,1,0:T(8,128)}, f32[2,8,512]{2,1,0:T(8,128)S(1)}, u32[]{:S(2)}, u32[]{:S(2)}) collective-permute-start(f32[2,8,512]{2,1,0:T(8,128)} %pad_maximum_fusion.14), channel_id=1, source_target_pairs={{0,4},{4,8},{8,12},{12,16},{16,20},{20,24},{24,28},{1,5},{5,9},{9,... | collective-permute-start | bytes 98312 | tf_op jit(solution)/shard_map/ppermute | solution.py:39
  196.9 5.4 %copy-start.9 = (bf16[2,160,1024]{2,1,0:T(8,128)(2,1)}, bf16[2,160,1024]{2,1,0:T(8,128)(2,1)S(1)}, u32[]{:S(2)}) copy-start(bf16[2,160,1024]{2,1,0:T(8,128)(2,1)S(1)} %collective-permute-done.19.second_ref) | copy-start | bytes 1966084
  196.9 27.1 %collective-permute-start.6 = (f32[2,8,512]{2,1,0:T(8,128)S(1)}, f32[2,8,512]{2,1,0:T(8,128)}, u32[]{:S(2)}, u32[]{:S(2)}) collective-permute-start(f32[2,8,512]{2,1,0:T(8,128)S(1)} %pad_maximum_fusion.8), channel_id=1, source_target_pairs={{0,16},{4,20},{8,24},{12,28},{1,17},{5,21},{9,25},{13,29},{2,18},{... | collective-permute-start | bytes 98312 | tf_op jit(solution)/shard_map/ppermute | solution.py:39
  204.9 13.6 %copy-start.10 = (bf16[2,160,1024]{2,1,0:T(8,128)(2,1)S(1)}, bf16[2,160,1024]{2,1,0:T(8,128)(2,1)}, u32[]{:S(2)}) copy-start(bf16[2,160,1024]{2,1,0:T(8,128)(2,1)} %copy-done.9) | copy-start | bytes 1966084
  205.7 19.0 %collective-permute-start.25 = (f32[2,8,512]{2,1,0:T(8,128)S(1)}, f32[2,8,512]{2,1,0:T(8,128)S(1)}, u32[]{:S(2)}, u32[]{:S(2)}) collective-permute-start(f32[2,8,512]{2,1,0:T(8,128)S(1)} %pad_maximum_fusion.15), channel_id=1, source_target_pairs={{4,0},{8,4},{12,8},{16,12},{20,16},{24,20},{28,24},{5,1},{9,5},{13... | collective-permute-start | bytes 98312 | tf_op jit(solution)/shard_map/ppermute | solution.py:39
  210.4 1.3 copy-start.11
  210.4 14.3 %collective-permute-start.11 = (f32[2,8,512]{2,1,0:T(8,128)S(1)}, f32[2,8,512]{2,1,0:T(8,128)S(1)}, u32[]{:S(2)}, u32[]{:S(2)}) collective-permute-start(f32[2,8,512]{2,1,0:T(8,128)S(1)} %pad_maximum_fusion.9), channel_id=1, source_target_pairs={{16,0},{20,4},{24,8},{28,12},{17,1},{21,5},{25,9},{29,13},{18,2},{... | collective-permute-start | bytes 98312 | tf_op jit(solution)/shard_map/ppermute | solution.py:39
  214.3 18.9 %copy-start.28 = (f32[2,8,256]{2,1,0:T(8,128)S(1)}, f32[2,8,256]{2,1,0:T(8,128)}, u32[]{:S(2)}) copy-start(f32[2,8,256]{2,1,0:T(8,128)} %shard_map.70) | copy-start | bytes 49156
  214.3 35.8 %copy-start.17 = (f32[2,8,256]{2,1,0:T(8,128)S(1)}, f32[2,8,256]{2,1,0:T(8,128)}, u32[]{:S(2)}) copy-start(f32[2,8,256]{2,1,0:T(8,128)} %shard_map.77) | copy-start | bytes 49156
  214.3 35.9 %copy-start.21 = (f32[2,8,256]{2,1,0:T(8,128)S(1)}, f32[2,8,256]{2,1,0:T(8,128)}, u32[]{:S(2)}) copy-start(f32[2,8,256]{2,1,0:T(8,128)} %shard_map.78) | copy-start | bytes 49156
  214.4 35.9 %copy-start.23 = (f32[2,8,256]{2,1,0:T(8,128)S(1)}, f32[2,8,256]{2,1,0:T(8,128)}, u32[]{:S(2)}) copy-start(f32[2,8,256]{2,1,0:T(8,128)} %shard_map.80) | copy-start | bytes 49156
  214.4 35.9 %copy-start.24 = (f32[2,8,256]{2,1,0:T(8,128)S(1)}, f32[2,8,256]{2,1,0:T(8,128)}, u32[]{:S(2)}) copy-start(f32[2,8,256]{2,1,0:T(8,128)} %shard_map.79) | copy-start | bytes 49156
  214.4 35.9 %copy-start.25 = (f32[2,8,256]{2,1,0:T(8,128)S(1)}, f32[2,8,256]{2,1,0:T(8,128)}, u32[]{:S(2)}) copy-start(f32[2,8,256]{2,1,0:T(8,128)} %shard_map.66) | copy-start | bytes 49156
  214.4 35.9 %copy-start.26 = (f32[2,8,256]{2,1,0:T(8,128)S(1)}, f32[2,8,256]{2,1,0:T(8,128)}, u32[]{:S(2)}) copy-start(f32[2,8,256]{2,1,0:T(8,128)} %shard_map.81) | copy-start | bytes 49156
  214.4 35.9 %copy-start.27 = (f32[2,8,256]{2,1,0:T(8,128)S(1)}, f32[2,8,256]{2,1,0:T(8,128)}, u32[]{:S(2)}) copy-start(f32[2,8,256]{2,1,0:T(8,128)} %shard_map.69) | copy-start | bytes 49156
  214.4 1.4 copy-start.12
  214.4 16.1 %collective-permute-start.15 = (bf16[2,160,1024]{2,1,0:T(8,128)(2,1)S(1)}, bf16[2,160,1024]{2,1,0:T(8,128)(2,1)}, u32[]{:S(2)}, u32[]{:S(2)}) collective-permute-start(bf16[2,160,1024]{2,1,0:T(8,128)(2,1)S(1)} %copy-done.8), channel_id=1, source_target_pairs={{8,0},{12,4},{16,8},{20,12},{24,16},{28,20},{9,1},{13,5},{17,9},{2... | collective-permute-start | bytes 1966088 | tf_op jit(solution)/shard_map/ppermute | solution.py:39
  218.5 24.2 %copy-start.29 = (f32[2,8,256]{2,1,0:T(8,128)S(1)}, f32[2,8,256]{2,1,0:T(8,128)}, u32[]{:S(2)}) copy-start(f32[2,8,256]{2,1,0:T(8,128)} %shard_map.72) | copy-start | bytes 49156
  218.5 20.7 %collective-permute-start.20 = (bf16[2,160,1024]{2,1,0:T(8,128)(2,1)S(1)}, bf16[2,160,1024]{2,1,0:T(8,128)(2,1)S(1)}, u32[]{:S(2)}, u32[]{:S(2)}) collective-permute-start(bf16[2,160,1024]{2,1,0:T(8,128)(2,1)S(1)} %copy-done.10), channel_id=1, source_target_pairs={{0,8},{4,12},{8,16},{12,20},{16,24},{20,28},{1,9},{5,13},{9,17},{1... | collective-permute-start | bytes 1966088 | tf_op jit(solution)/shard_map/ppermute | solution.py:39
  233.2 18.7 %copy-start.30 = (f32[2,8,256]{2,1,0:T(8,128)S(1)}, f32[2,8,256]{2,1,0:T(8,128)}, u32[]{:S(2)}) copy-start(f32[2,8,256]{2,1,0:T(8,128)} %shard_map.71) | copy-start | bytes 49156
  234.0 10.8 %collective-permute-start.16 = (f32[2,8,512]{2,1,0:T(8,128)S(1)}, f32[2,8,512]{2,1,0:T(8,128)S(1)}, u32[]{:S(2)}, u32[]{:S(2)}) collective-permute-start(f32[2,8,512]{2,1,0:T(8,128)S(1)} %pad_maximum_fusion.10), channel_id=1, source_target_pairs={{0,12},{4,16},{8,20},{12,24},{16,28},{1,13},{5,17},{9,21},{13,25},... | collective-permute-start | bytes 98312 | tf_op jit(solution)/shard_map/ppermute | solution.py:39
  239.2 0.9 copy-start.13
  243.5 6.7 %collective-permute-start.21 = (f32[2,8,512]{2,1,0:T(8,128)S(1)}, f32[2,8,512]{2,1,0:T(8,128)S(1)}, u32[]{:S(2)}, u32[]{:S(2)}) collective-permute-start(f32[2,8,512]{2,1,0:T(8,128)S(1)} %pad_maximum_fusion.11), channel_id=1, source_target_pairs={{12,0},{16,4},{20,8},{24,12},{28,16},{13,1},{17,5},{21,9},{25,13},... | collective-permute-start | bytes 98312 | tf_op jit(solution)/shard_map/ppermute | solution.py:39

commit v5 on v2

--- a/solution.py
+++ b/solution.py
@@ -31,15 +31,14 @@
     return cells
 
 
+def routed(block, axis, distance, keep):
+    count = lax.axis_size(axis)
+    route = [(i + distance, i) for i in range(count) if 0 <= i + distance < count and keep(i, count)]
+    return lax.ppermute(block, axis, route)
+
+
 def shifted(block, axis, distance):
-    count = lax.axis_size(axis)
-    route = [(i + distance, i) for i in range(count) if 0 <= i + distance < count]
-    return lax.ppermute(block, axis, route)
-
-
-def swapped(block, axis):
-    count = lax.axis_size(axis)
-    return lax.ppermute(block, axis, [(i, i ^ 1) for i in range(count)])
+    return routed(block, axis, distance, lambda i, count: True)
 
 
 def kernel_table():
@@ -158,14 +157,22 @@
     date = lax.axis_index("date")
     even = date % 2 == 0
 
-    left_2 = shifted(own_left, "date", 2)
-    left_1 = swapped(jnp.where(even, left_2, own_left), "date")
-    left_4 = shifted(left_2, "date", 2)
-    left_3 = shifted(left_1, "date", 2)
-    right_2 = shifted(own_right, "date", -2)
-    right_1 = swapped(jnp.where(even, own_right, right_2), "date")
-    right_4 = shifted(right_2, "date", -2)
-    right_3 = shifted(right_1, "date", -2)
+    left_2 = routed(own_left, "date", 2, lambda i, n: True)
+    left_4 = routed(left_2, "date", 2, lambda i, n: i + 4 < n)
+    left_1_even = routed(own_left, "date", 1, lambda i, n: i % 2 == 0)
+    left_1_odd = routed(left_2, "date", -1, lambda i, n: i % 2 == 1 and i + 1 < n)
+    left_3_even = routed(left_1_even, "date", 2, lambda i, n: i % 2 == 0 and i + 3 < n)
+    left_3_odd = routed(left_1_odd, "date", 2, lambda i, n: i % 2 == 1 and i + 3 < n)
+    left_1 = jnp.where(even, left_1_even, left_1_odd)
+    left_3 = jnp.where(even, left_3_even, left_3_odd)
+    right_2 = routed(own_right, "date", -2, lambda i, n: True)
+    right_4 = routed(right_2, "date", -2, lambda i, n: i >= 4)
+    right_1_odd = routed(own_right, "date", -1, lambda i, n: i % 2 == 1)
+    right_1_even = routed(right_2, "date", 1, lambda i, n: i % 2 == 0 and i >= 1)
+    right_3_odd = routed(right_1_odd, "date", -2, lambda i, n: i % 2 == 1 and i >= 3)
+    right_3_even = routed(right_1_even, "date", -2, lambda i, n: i % 2 == 0 and i >= 3)
+    right_1 = jnp.where(even, right_1_even, right_1_odd)
+    right_3 = jnp.where(even, right_3_even, right_3_odd)
 
     ahead = {
         1: looks(own_left, left_1),

time: 229 us -> 260 us (1.14)
  the two profiles are of different devices: /device:TPU:0 before, /device:TPU:28 now
where the time goes in v5:
time: 260 us; the launch traced here: 258 us
  starting transfers between devices  76.6 us (29%)
  Pallas kernels  72.7 us (28%)
  waiting for transfers between devices  55.9 us (22%)
  between operations  21.5 us (8%)
  other arithmetic  20.8 us (8%)
  local copies, waits for them, and re-layouts  10.2 us (4%)
    ppermute x20, starting transfers between devices, routed(): return lax.ppermute(block, axis, route)  72.3 us
    ppermute x20, waiting for transfers between devices, routed(): return lax.ppermute(block, axis, route)  55.9 us
    pallas_call x1, Pallas kernels, resample_block(): pl.pallas_call(resample_kernel, grid=(2, nlines // ROWS), in_specs=[pl.Bl...  37.7 us
    pallas_call x8, Pallas kernels, looks(): pl.pallas_call(looks_kernel, grid=(width // CHUNK,), in_specs=[spec, spec...  35 us
  transfers between devices with their start and end apart: 22, of which 4 were waited for; matrix products, arithmetic and copies ran while one was open for 7% of the time, Pallas kernels for 14%

profile of v5, /device:TPU:28, one launch (start us, length us, event | category | flops | bytes accessed | tf_op | source)
XLA Modules:
  0.0 257.7 jit_solution(13695442786811407209)
XLA Ops:
  0.0 1.1 fusion.31
  1.1 1.3 collective-permute-start.1
  2.4 3.0 %collective-permute-start = (bf16[1,2,16,4096]{3,2,1,0:T(8,128)(2,1)S(1)}, bf16[1,2,16,4096]{3,2,1,0:T(8,128)(2,1)S(1)}, u32[]{:S(2)}, u32[]{:S(2)}) collective-permute-start(bf16[1,2,16,4096]{3,2,1,0:T(8,128)(2,1)S(1)} %get-tuple-element.8), channel_id=1, source_target_pairs={{0,1},{1,2},{2,3},{4,5},{5,6},{6,7},{8,9},{9,10},{10,11},{12,13},{... | collective-permute-start | bytes 786440 | tf_op jit(solution)/shard_map/ppermute | solution.py:25
  5.4 0.7 compare_select_fusion
  6.1 0.7 compare_and_fusion
  6.8 0.7 add_bitcast_fusion
  7.5 0.1 fusion.8
  8.9 0.1 copy.20
  9.0 0.7 dynamic-slice_reduce_fusion.weights_ref
  9.8 0.8 copy.21.shift_ref
  10.5 0.7 gather_fusion
  11.2 0.7 broadcast_select_fusion.4.coeff_ref
  11.9 0.0 collective-permute-done.1
  11.9 0.0 collective-permute-done
  11.9 3.5 %fusion.2 = bf16[2,167,4096]{2,1,0:T(8,128)(2,1)S(1)} fusion(s32[]{:T(128)S(6)} %select_n.510, bf16[1,2,16,4096]{3,2,1,0:T(8,128)(2,1)S(1)} %collective-permute-done, bf16[1,2,160,4096]{3,2,1,0:T(8,128)(2,1)} %param.6, bf16[1,2,16,4096]{3,2,1,0:T(8,128)(2,1)S(1)} %collective-permute-done.1), kind=kLoop, calls=%fused_computation.6 | loop fusion | flops 8208384 | bytes 5881860 | tf_op jit(solution)/shard_map/convert_element_type | solution.py:85
  15.4 3.1 %pad_convert_fusion.window_ref = f32[2,168,4096]{2,1,0:T(8,128)} fusion(bf16[2,167,4096]{2,1,0:T(8,128)(2,1)S(1)} %fusion.2), kind=kLoop, calls=%fused_computation.7 | loop fusion | flops 1376256 | bytes 8241152 | tf_op jit(solution)/shard_map/jit(_pad)/pad | solution.py:86
  18.5 37.7 %shard_map.64 = bf16[2,160,4096]{2,1,0:T(8,128)(2,1)} custom-call(f32[8]{0:T(128)} %dynamic-slice_reduce_fusion.weights_ref, f32[2,168,4096]{2,1,0:T(8,128)} %pad_convert_fusion.window_ref, f32[160,8]{1,0:T(8,128)} %broadcast_select_fusion.4.coeff_ref, s32[160,1]{1,0:T(8,128)} %copy.21.shift_ref), custom_call_target="tpu_custom_call" | custom-call | tf_op jit(solution)/shard_map/pallas_call | solution.py:90
  56.2 2.0 fusion.30
  58.2 1.3 copy.24
  59.6 0.7 copy.28
  60.3 1.3 collective-permute-start.5
  61.6 1.3 copy.22
  63.0 0.7 copy.29
  63.7 0.0 copy-start.10
  63.7 5.8 %collective-permute-start.2 = (bf16[2,160,2048]{2,1,0:T(8,128)(2,1)S(1)}, bf16[2,160,2048]{2,1,0:T(8,128)(2,1)}, u32[]{:S(2)}, u32[]{:S(2)}) collective-permute-start(bf16[2,160,2048]{2,1,0:T(8,128)(2,1)S(1)} %bitcast.56), channel_id=1, source_target_pairs={{8,0},{12,4},{16,8},{20,12},{24,16},{28,20},{9,1},{13,5},{17,9},{2... | collective-permute-start | bytes 3932168 | tf_op jit(solution)/shard_map/ppermute | solution.py:37
  69.6 1.3 collective-permute-start.15
  70.8 6.7 %collective-permute-start.8 = (bf16[2,160,2048]{2,1,0:T(8,128)(2,1)S(1)}, bf16[2,160,2048]{2,1,0:T(8,128)(2,1)}, u32[]{:S(2)}, u32[]{:S(2)}) collective-permute-start(bf16[2,160,2048]{2,1,0:T(8,128)(2,1)S(1)} %bitcast.57), channel_id=1, source_target_pairs={{4,0},{12,8},{20,16},{28,24},{5,1},{13,9},{21,17},{29,25},{6,2},{1... | collective-permute-start | bytes 3932168 | tf_op jit(solution)/shard_map/ppermute | solution.py:37
  77.5 16.3 %collective-permute-done.5.second_ref = bf16[2,160,2048]{2,1,0:T(8,128)(2,1)} collective-permute-done((bf16[2,160,2048]{2,1,0:T(8,128)(2,1)S(1)}, bf16[2,160,2048]{2,1,0:T(8,128)(2,1)}, u32[]{:S(2)}, u32[]{:S(2)}) %collective-permute-start.5) | collective-permute-done | bytes 1310752 | tf_op jit(solution)/shard_map/ppermute | solution.py:37
  93.8 3.5 %collective-permute-start.13 = (bf16[2,160,2048]{2,1,0:T(8,128)(2,1)}, bf16[2,160,2048]{2,1,0:T(8,128)(2,1)}, u32[]{:S(2)}, u32[]{:S(2)}) collective-permute-start(bf16[2,160,2048]{2,1,0:T(8,128)(2,1)} %collective-permute-done.5.second_ref), channel_id=1, source_target_pairs={{12,8},{20,16},{28,24},{13,9},{21,17},{29,25},{14,10},{22,18},{30,... | collective-permute-start | bytes 3932168 | tf_op jit(solution)/shard_map/ppermute | solution.py:37
  97.3 1.3 collective-permute-start.6
  98.6 0.0 collective-permute-done.2.second_ref
  98.6 1.8 collective-permute-start.10
  100.4 4.4 %shard_map.70 = f32[2,8,512]{2,1,0:T(8,128)} custom-call(bf16[2,160,2048]{2,1,0:T(8,128)(2,1)} %bitcast.64, bf16[2,160,2048]{2,1,0:T(8,128)(2,1)} %collective-permute-done.5.second_ref), custom_call_target="tpu_custom_call" | custom-call | tf_op jit(solution)/shard_map/pallas_call | solution.py:135
  104.8 4.1 %collective-permute-start.19 = (f32[2,8,512]{2,1,0:T(8,128)}, f32[2,8,512]{2,1,0:T(8,128)S(1)}, u32[]{:S(2)}, u32[]{:S(2)}) collective-permute-start(f32[2,8,512]{2,1,0:T(8,128)} %shard_map.70), channel_id=1, source_target_pairs={{8,0},{12,4},{16,8},{20,12},{24,16},{28,20},{9,1},{13,5},{17,9},{2... | collective-permute-start | bytes 98312 | tf_op jit(solution)/shard_map/ppermute | solution.py:37
  108.9 0.7 fusion.40
  129.2 4.4 %shard_map.69 = f32[2,8,512]{2,1,0:T(8,128)} custom-call(bf16[2,160,2048]{2,1,0:T(8,128)(2,1)} %bitcast.58, bf16[2,160,2048]{2,1,0:T(8,128)(2,1)} %collective-permute-done.2.second_ref), custom_call_target="tpu_custom_call" | custom-call | tf_op jit(solution)/shard_map/pallas_call | solution.py:135
  133.6 1.3 collective-permute-start.18
  134.9 4.7 %collective-permute-done.18 = f32[2,8,512]{2,1,0:T(8,128)S(1)} collective-permute-done((f32[2,8,512]{2,1,0:T(8,128)}, f32[2,8,512]{2,1,0:T(8,128)S(1)}, u32[]{:S(2)}, u32[]{:S(2)}) %collective-permute-start.18) | collective-permute-done | bytes 32800 | tf_op jit(solution)/shard_map/ppermute | solution.py:37
  139.6 1.8 collective-permute-start.3
  141.4 1.3 collective-permute-start.16
  142.7 0.9 collective-permute-start.9
  143.6 2.5 broadcast_select_fusion.second_ref
  146.2 4.4 %shard_map.72 = f32[2,8,512]{2,1,0:T(8,128)} custom-call(bf16[2,160,2048]{2,1,0:T(8,128)(2,1)} %bitcast.65, bf16[2,160,2048]{2,1,0:T(8,128)(2,1)} %broadcast_select_fusion.second_ref), custom_call_target="tpu_custom_call" | custom-call | tf_op jit(solution)/shard_map/pallas_call | solution.py:135
  150.5 9.0 %collective-permute-start.21 = (f32[2,8,512]{2,1,0:T(8,128)}, f32[2,8,512]{2,1,0:T(8,128)S(1)}, u32[]{:S(2)}, u32[]{:S(2)}) collective-permute-start(f32[2,8,512]{2,1,0:T(8,128)} %shard_map.72), channel_id=1, source_target_pairs={{4,0},{8,4},{12,8},{16,12},{20,16},{24,20},{28,24},{5,1},{9,5},{13... | collective-permute-start | bytes 98312 | tf_op jit(solution)/shard_map/ppermute | solution.py:37
  159.6 4.4 %shard_map.66 = f32[2,8,512]{2,1,0:T(8,128)} custom-call(bf16[2,160,2048]{2,1,0:T(8,128)(2,1)} %bitcast.66, bf16[2,160,2048]{2,1,0:T(8,128)(2,1)} %collective-permute-done.6.second_ref), custom_call_target="tpu_custom_call" | custom-call | tf_op jit(solution)/shard_map/pallas_call | solution.py:135
  164.0 1.3 collective-permute-start.7
  165.2 2.5 broadcast_select_fusion.1.second_ref
  167.8 4.4 %shard_map.71 = f32[2,8,512]{2,1,0:T(8,128)} custom-call(bf16[2,160,2048]{2,1,0:T(8,128)(2,1)} %bitcast.59, bf16[2,160,2048]{2,1,0:T(8,128)(2,1)} %broadcast_select_fusion.1.second_ref), custom_call_target="tpu_custom_call" | custom-call | tf_op jit(solution)/shard_map/pallas_call | solution.py:135
  172.1 1.3 collective-permute-start.20
  173.4 4.4 %shard_map.65 = f32[2,8,512]{2,1,0:T(8,128)} custom-call(bf16[2,160,2048]{2,1,0:T(8,128)(2,1)} %bitcast.60, bf16[2,160,2048]{2,1,0:T(8,128)(2,1)} %collective-permute-done.3.second_ref), custom_call_target="tpu_custom_call" | custom-call | tf_op jit(solution)/shard_map/pallas_call | solution.py:135
  177.8 0.7 collective-permute-start.14
  178.6 1.8 collective-permute-start.11
  180.4 1.3 collective-permute-start.4
  181.8 29.3 %collective-permute-done.4 = f32[2,8,512]{2,1,0:T(8,128)S(1)} collective-permute-done((f32[2,8,512]{2,1,0:T(8,128)}, f32[2,8,512]{2,1,0:T(8,128)S(1)}, u32[]{:S(2)}, u32[]{:S(2)}) %collective-permute-start.4) | collective-permute-done | bytes 32800 | tf_op jit(solution)/shard_map/ppermute | solution.py:37
  211.1 1.3 broadcast_select_fusion.2.second_ref
  212.3 4.4 %shard_map.68 = f32[2,8,512]{2,1,0:T(8,128)} custom-call(bf16[2,160,2048]{2,1,0:T(8,128)(2,1)} %bitcast.67, bf16[2,160,2048]{2,1,0:T(8,128)(2,1)} %broadcast_select_fusion.2.second_ref), custom_call_target="tpu_custom_call" | custom-call | tf_op jit(solution)/shard_map/pallas_call | solution.py:135
  216.7 24.4 %collective-permute-start.17 = (f32[2,8,512]{2,1,0:T(8,128)}, f32[2,8,512]{2,1,0:T(8,128)S(1)}, u32[]{:S(2)}, u32[]{:S(2)}) collective-permute-start(f32[2,8,512]{2,1,0:T(8,128)} %shard_map.68), channel_id=1, source_target_pairs={{12,0},{16,4},{20,8},{24,12},{28,16},{13,1},{17,5},{21,9},{25,13},... | collective-permute-start | bytes 98312 | tf_op jit(solution)/shard_map/ppermute | solution.py:37
  241.1 2.5 broadcast_select_fusion.3.second_ref
  243.7 4.4 %shard_map.67 = f32[2,8,512]{2,1,0:T(8,128)} custom-call(bf16[2,160,2048]{2,1,0:T(8,128)(2,1)} %bitcast.61, bf16[2,160,2048]{2,1,0:T(8,128)(2,1)} %broadcast_select_fusion.3.second_ref), custom_call_target="tpu_custom_call" | custom-call | tf_op jit(solution)/shard_map/pallas_call | solution.py:135
  248.1 1.4 collective-permute-start.12
  249.6 5.6 %collective-permute-done.12 = f32[2,8,512]{2,1,0:T(8,128)S(1)} collective-permute-done((f32[2,8,512]{2,1,0:T(8,128)}, f32[2,8,512]{2,1,0:T(8,128)S(1)}, u32[]{:S(2)}, u32[]{:S(2)}) %collective-permute-start.12) | collective-permute-done | bytes 32800 | tf_op jit(solution)/shard_map/ppermute | solution.py:37
  255.2 0.8 select_select_fusion.2
  256.0 0.8 select_select_fusion.1
  256.9 0.7 maximum_bitcast_fusion
  (55 shorter events, 0.2 us)
Async XLA Ops:
  1.1 10.8 %collective-permute-start.1 = (bf16[1,2,16,4096]{3,2,1,0:T(8,128)(2,1)S(1)}, bf16[1,2,16,4096]{3,2,1,0:T(8,128)(2,1)S(1)}, u32[]{:S(2)}, u32[]{:S(2)}) collective-permute-start(bf16[1,2,16,4096]{3,2,1,0:T(8,128)(2,1)S(1)} %get-tuple-element.7), channel_id=1, source_target_pairs={{1,0},{2,1},{3,2},{5,4},{6,5},{7,6},{9,8},{10,9},{11,10},{13,12},{... | collective-permute-start | bytes 786440 | tf_op jit(solution)/shard_map/ppermute | solution.py:27
  2.4 9.5 %collective-permute-start = (bf16[1,2,16,4096]{3,2,1,0:T(8,128)(2,1)S(1)}, bf16[1,2,16,4096]{3,2,1,0:T(8,128)(2,1)S(1)}, u32[]{:S(2)}, u32[]{:S(2)}) collective-permute-start(bf16[1,2,16,4096]{3,2,1,0:T(8,128)(2,1)S(1)} %get-tuple-element.8), channel_id=1, source_target_pairs={{0,1},{1,2},{2,3},{4,5},{5,6},{6,7},{8,9},{9,10},{10,11},{12,13},{... | collective-permute-start | bytes 786440 | tf_op jit(solution)/shard_map/ppermute | solution.py:25
  60.3 9.3 %copy-start.1 = (bf16[2,20,8,2048]{3,2,1,0:T(8,128)(2,1)}, bf16[2,20,8,2048]{3,2,1,0:T(8,128)(2,1)S(1)}, u32[]{:S(2)}) copy-start(bf16[2,20,8,2048]{3,2,1,0:T(8,128)(2,1)S(1)} %copy.28) | copy-start | bytes 3932164
  60.3 33.5 %collective-permute-start.5 = (bf16[2,160,2048]{2,1,0:T(8,128)(2,1)S(1)}, bf16[2,160,2048]{2,1,0:T(8,128)(2,1)}, u32[]{:S(2)}, u32[]{:S(2)}) collective-permute-start(bf16[2,160,2048]{2,1,0:T(8,128)(2,1)S(1)} %bitcast.62), channel_id=1, source_target_pairs={{0,8},{4,12},{8,16},{12,20},{16,24},{20,28},{1,9},{5,13},{9,17},{1... | collective-permute-start | bytes 3932168 | tf_op jit(solution)/shard_map/ppermute | solution.py:37
  63.7 41.1 %copy-start = (bf16[2,20,8,2048]{3,2,1,0:T(8,128)(2,1)}, bf16[2,20,8,2048]{3,2,1,0:T(8,128)(2,1)S(1)}, u32[]{:S(2)}) copy-start(bf16[2,20,8,2048]{3,2,1,0:T(8,128)(2,1)S(1)} %copy.29) | copy-start | bytes 3932164
  63.7 45.2 %copy-start.10 = (s32[1,4]{1,0:T(1,128)S(1)}, s32[1,4]{1,0:T(1,128)}, u32[]{:S(2)}) copy-start(s32[1,4]{1,0:T(1,128)} %param.11) | copy-start | bytes 52
  63.7 34.9 %collective-permute-start.2 = (bf16[2,160,2048]{2,1,0:T(8,128)(2,1)S(1)}, bf16[2,160,2048]{2,1,0:T(8,128)(2,1)}, u32[]{:S(2)}, u32[]{:S(2)}) collective-permute-start(bf16[2,160,2048]{2,1,0:T(8,128)(2,1)S(1)} %bitcast.56), channel_id=1, source_target_pairs={{8,0},{12,4},{16,8},{20,12},{24,16},{28,20},{9,1},{13,5},{17,9},{2... | collective-permute-start | bytes 3932168 | tf_op jit(solution)/shard_map/ppermute | solution.py:37
  69.6 35.2 %collective-permute-start.15 = (bf16[2,160,2048]{2,1,0:T(8,128)(2,1)S(1)}, bf16[2,160,2048]{2,1,0:T(8,128)(2,1)}, u32[]{:S(2)}, u32[]{:S(2)}) collective-permute-start(bf16[2,160,2048]{2,1,0:T(8,128)(2,1)S(1)} %bitcast.63), channel_id=1, source_target_pairs={{0,4},{8,12},{16,20},{24,28},{1,5},{9,13},{17,21},{25,29},{2,6},{1... | collective-permute-start | bytes 3932168 | tf_op jit(solution)/shard_map/ppermute | solution.py:37
  70.8 70.6 %collective-permute-start.8 = (bf16[2,160,2048]{2,1,0:T(8,128)(2,1)S(1)}, bf16[2,160,2048]{2,1,0:T(8,128)(2,1)}, u32[]{:S(2)}, u32[]{:S(2)}) collective-permute-start(bf16[2,160,2048]{2,1,0:T(8,128)(2,1)S(1)} %bitcast.57), channel_id=1, source_target_pairs={{4,0},{12,8},{20,16},{28,24},{5,1},{13,9},{21,17},{29,25},{6,2},{1... | collective-permute-start | bytes 3932168 | tf_op jit(solution)/shard_map/ppermute | solution.py:37
  93.8 48.9 %collective-permute-start.13 = (bf16[2,160,2048]{2,1,0:T(8,128)(2,1)}, bf16[2,160,2048]{2,1,0:T(8,128)(2,1)}, u32[]{:S(2)}, u32[]{:S(2)}) collective-permute-start(bf16[2,160,2048]{2,1,0:T(8,128)(2,1)} %collective-permute-done.5.second_ref), channel_id=1, source_target_pairs={{12,8},{20,16},{28,24},{13,9},{21,17},{29,25},{14,10},{22,18},{30,... | collective-permute-start | bytes 3932168 | tf_op jit(solution)/shard_map/ppermute | solution.py:37
  97.3 53.2 %collective-permute-start.6 = (bf16[2,160,2048]{2,1,0:T(8,128)(2,1)}, bf16[2,160,2048]{2,1,0:T(8,128)(2,1)}, u32[]{:S(2)}, u32[]{:S(2)}) collective-permute-start(bf16[2,160,2048]{2,1,0:T(8,128)(2,1)} %collective-permute-done.5.second_ref), channel_id=1, source_target_pairs={{8,16},{12,20},{16,24},{20,28},{9,17},{13,21},{17,25},{21,29},{10,... | collective-permute-start | bytes 3932168 | tf_op jit(solution)/shard_map/ppermute | solution.py:37
  98.6 65.3 %collective-permute-start.10 = (bf16[2,160,2048]{2,1,0:T(8,128)(2,1)}, bf16[2,160,2048]{2,1,0:T(8,128)(2,1)}, u32[]{:S(2)}, u32[]{:S(2)}) collective-permute-start(bf16[2,160,2048]{2,1,0:T(8,128)(2,1)} %collective-permute-done.2.second_ref), channel_id=1, source_target_pairs={{0,4},{8,12},{16,20},{1,5},{9,13},{17,21},{2,6},{10,14},{18,22},{3... | collective-permute-start | bytes 3932168 | tf_op jit(solution)/shard_map/ppermute | solution.py:37
  104.8 28.8 %collective-permute-start.19 = (f32[2,8,512]{2,1,0:T(8,128)}, f32[2,8,512]{2,1,0:T(8,128)S(1)}, u32[]{:S(2)}, u32[]{:S(2)}) collective-permute-start(f32[2,8,512]{2,1,0:T(8,128)} %shard_map.70), channel_id=1, source_target_pairs={{8,0},{12,4},{16,8},{20,12},{24,16},{28,20},{9,1},{13,5},{17,9},{2... | collective-permute-start | bytes 98312 | tf_op jit(solution)/shard_map/ppermute | solution.py:37
  133.6 6.0 %collective-permute-start.18 = (f32[2,8,512]{2,1,0:T(8,128)}, f32[2,8,512]{2,1,0:T(8,128)S(1)}, u32[]{:S(2)}, u32[]{:S(2)}) collective-permute-start(f32[2,8,512]{2,1,0:T(8,128)} %shard_map.69), channel_id=1, source_target_pairs={{0,8},{4,12},{8,16},{12,20},{16,24},{20,28},{1,9},{5,13},{9,17},{1... | collective-permute-start | bytes 98312 | tf_op jit(solution)/shard_map/ppermute | solution.py:37
  139.6 32.5 %collective-permute-start.3 = (bf16[2,160,2048]{2,1,0:T(8,128)(2,1)}, bf16[2,160,2048]{2,1,0:T(8,128)(2,1)}, u32[]{:S(2)}, u32[]{:S(2)}) collective-permute-start(bf16[2,160,2048]{2,1,0:T(8,128)(2,1)} %collective-permute-done.2.second_ref), channel_id=1, source_target_pairs={{8,0},{12,4},{16,8},{20,12},{9,1},{13,5},{17,9},{21,13},{10,2},{14... | collective-permute-start | bytes 3932168 | tf_op jit(solution)/shard_map/ppermute | solution.py:37
  141.4 69.6 %collective-permute-start.16 = (bf16[2,160,2048]{2,1,0:T(8,128)(2,1)}, bf16[2,160,2048]{2,1,0:T(8,128)(2,1)S(1)}, u32[]{:S(2)}, u32[]{:S(2)}) collective-permute-start(bf16[2,160,2048]{2,1,0:T(8,128)(2,1)} %collective-permute-done.15), channel_id=1, source_target_pairs={{4,12},{12,20},{20,28},{5,13},{13,21},{21,29},{6,14},{14,22},{22,3... | collective-permute-start | bytes 3932168 | tf_op jit(solution)/shard_map/ppermute | solution.py:37
  142.7 98.4 %collective-permute-start.9 = (bf16[2,160,2048]{2,1,0:T(8,128)(2,1)}, bf16[2,160,2048]{2,1,0:T(8,128)(2,1)S(1)}, u32[]{:S(2)}, u32[]{:S(2)}) collective-permute-start(bf16[2,160,2048]{2,1,0:T(8,128)(2,1)} %collective-permute-done.8), channel_id=1, source_target_pairs={{8,0},{16,8},{24,16},{9,1},{17,9},{25,17},{10,2},{18,10},{26,18},{... | collective-permute-start | bytes 3932168 | tf_op jit(solution)/shard_map/ppermute | solution.py:37
  150.5 27.3 %collective-permute-start.21 = (f32[2,8,512]{2,1,0:T(8,128)}, f32[2,8,512]{2,1,0:T(8,128)S(1)}, u32[]{:S(2)}, u32[]{:S(2)}) collective-permute-start(f32[2,8,512]{2,1,0:T(8,128)} %shard_map.72), channel_id=1, source_target_pairs={{4,0},{8,4},{12,8},{16,12},{20,16},{24,20},{28,24},{5,1},{9,5},{13... | collective-permute-start | bytes 98312 | tf_op jit(solution)/shard_map/ppermute | solution.py:37
  164.0 14.6 %collective-permute-start.7 = (f32[2,8,512]{2,1,0:T(8,128)}, f32[2,8,512]{2,1,0:T(8,128)S(1)}, u32[]{:S(2)}, u32[]{:S(2)}) collective-permute-start(f32[2,8,512]{2,1,0:T(8,128)} %shard_map.66), channel_id=1, source_target_pairs={{16,0},{20,4},{24,8},{28,12},{17,1},{21,5},{25,9},{29,13},{18,2},{... | collective-permute-start | bytes 98312 | tf_op jit(solution)/shard_map/ppermute | solution.py:37
  172.1 8.3 %collective-permute-start.20 = (f32[2,8,512]{2,1,0:T(8,128)}, f32[2,8,512]{2,1,0:T(8,128)S(1)}, u32[]{:S(2)}, u32[]{:S(2)}) collective-permute-start(f32[2,8,512]{2,1,0:T(8,128)} %shard_map.71), channel_id=1, source_target_pairs={{0,4},{4,8},{8,12},{12,16},{16,20},{20,24},{24,28},{1,5},{5,9},{9,... | collective-permute-start | bytes 98312 | tf_op jit(solution)/shard_map/ppermute | solution.py:37
  177.8 33.3 %collective-permute-start.14 = (bf16[2,160,2048]{2,1,0:T(8,128)(2,1)}, bf16[2,160,2048]{2,1,0:T(8,128)(2,1)S(1)}, u32[]{:S(2)}, u32[]{:S(2)}) collective-permute-start(bf16[2,160,2048]{2,1,0:T(8,128)(2,1)} %collective-permute-done.13), channel_id=1, source_target_pairs={{8,16},{16,24},{9,17},{17,25},{10,18},{18,26},{11,19},{19,27}} | collective-permute-start | bytes 3932168 | tf_op jit(solution)/shard_map/ppermute | solution.py:37
  178.6 62.5 %collective-permute-start.11 = (bf16[2,160,2048]{2,1,0:T(8,128)(2,1)}, bf16[2,160,2048]{2,1,0:T(8,128)(2,1)}, u32[]{:S(2)}, u32[]{:S(2)}) collective-permute-start(bf16[2,160,2048]{2,1,0:T(8,128)(2,1)} %collective-permute-done.10), channel_id=1, source_target_pairs={{12,4},{20,12},{13,5},{21,13},{14,6},{22,14},{15,7},{23,15}} | collective-permute-start | bytes 3932168 | tf_op jit(solution)/shard_map/ppermute | solution.py:37
  180.4 30.6 %collective-permute-start.4 = (f32[2,8,512]{2,1,0:T(8,128)}, f32[2,8,512]{2,1,0:T(8,128)S(1)}, u32[]{:S(2)}, u32[]{:S(2)}) collective-permute-start(f32[2,8,512]{2,1,0:T(8,128)} %shard_map.65), channel_id=1, source_target_pairs={{0,16},{4,20},{8,24},{12,28},{1,17},{5,21},{9,25},{13,29},{2,18},{... | collective-permute-start | bytes 98312 | tf_op jit(solution)/shard_map/ppermute | solution.py:37
  216.7 32.8 %collective-permute-start.17 = (f32[2,8,512]{2,1,0:T(8,128)}, f32[2,8,512]{2,1,0:T(8,128)S(1)}, u32[]{:S(2)}, u32[]{:S(2)}) collective-permute-start(f32[2,8,512]{2,1,0:T(8,128)} %shard_map.68), channel_id=1, source_target_pairs={{12,0},{16,4},{20,8},{24,12},{28,16},{13,1},{17,5},{21,9},{25,13},... | collective-permute-start | bytes 98312 | tf_op jit(solution)/shard_map/ppermute | solution.py:37
  243.7 11.5 %copy-start.2 = (f32[2,8,512]{2,1,0:T(8,128)S(1)}, f32[2,8,512]{2,1,0:T(8,128)}, u32[]{:S(2)}) copy-start(f32[2,8,512]{2,1,0:T(8,128)} %shard_map.70) | copy-start | bytes 98308
  243.7 11.5 %copy-start.3 = (f32[2,8,512]{2,1,0:T(8,128)S(1)}, f32[2,8,512]{2,1,0:T(8,128)}, u32[]{:S(2)}) copy-start(f32[2,8,512]{2,1,0:T(8,128)} %shard_map.69) | copy-start | bytes 98308
  243.7 11.5 %copy-start.4 = (f32[2,8,512]{2,1,0:T(8,128)S(1)}, f32[2,8,512]{2,1,0:T(8,128)}, u32[]{:S(2)}) copy-start(f32[2,8,512]{2,1,0:T(8,128)} %shard_map.72) | copy-start | bytes 98308
  243.7 11.5 %copy-start.5 = (f32[2,8,512]{2,1,0:T(8,128)S(1)}, f32[2,8,512]{2,1,0:T(8,128)}, u32[]{:S(2)}) copy-start(f32[2,8,512]{2,1,0:T(8,128)} %shard_map.66) | copy-start | bytes 98308
  243.7 11.6 %copy-start.6 = (f32[2,8,512]{2,1,0:T(8,128)S(1)}, f32[2,8,512]{2,1,0:T(8,128)}, u32[]{:S(2)}) copy-start(f32[2,8,512]{2,1,0:T(8,128)} %shard_map.71) | copy-start | bytes 98308
  243.7 11.6 %copy-start.7 = (f32[2,8,512]{2,1,0:T(8,128)S(1)}, f32[2,8,512]{2,1,0:T(8,128)}, u32[]{:S(2)}) copy-start(f32[2,8,512]{2,1,0:T(8,128)} %shard_map.65) | copy-start | bytes 98308
  243.7 11.6 %copy-start.8 = (f32[2,8,512]{2,1,0:T(8,128)S(1)}, f32[2,8,512]{2,1,0:T(8,128)}, u32[]{:S(2)}) copy-start(f32[2,8,512]{2,1,0:T(8,128)} %shard_map.68) | copy-start | bytes 98308
  248.1 8.7 %copy-start.9 = (f32[2,8,512]{2,1,0:T(8,128)S(1)}, f32[2,8,512]{2,1,0:T(8,128)}, u32[]{:S(2)}) copy-start(f32[2,8,512]{2,1,0:T(8,128)} %shard_map.67) | copy-start | bytes 98308
  248.1 7.0 %collective-permute-start.12 = (f32[2,8,512]{2,1,0:T(8,128)}, f32[2,8,512]{2,1,0:T(8,128)S(1)}, u32[]{:S(2)}, u32[]{:S(2)}) collective-permute-start(f32[2,8,512]{2,1,0:T(8,128)} %shard_map.67), channel_id=1, source_target_pairs={{0,12},{4,16},{8,20},{12,24},{16,28},{1,13},{5,17},{9,21},{13,25},... | collective-permute-start | bytes 98312 | tf_op jit(solution)/shard_map/ppermute | solution.py:37

commit v6 on v2

--- a/solution.py
+++ b/solution.py
@@ -179,6 +179,7 @@
         3: looks(own_right, right_3),
         4: looks(own_right, right_4),
     }
+    ahead, behind = lax.optimization_barrier((ahead, behind))
     full = {}
     for s in range(1, GAP + 1):
         right_of_ahead = conj(shifted(behind[s], "date", s))

time: 229 us -> 245 us (1.070)
  waiting for transfers between devices: 52.2 us -> 73.4 us
    ppermute x2, waiting for transfers between devices: 0.01 us -> 40 us  [swapped(): return lax.ppermute(block, axis, [(i, i ^ 1) for i in range(count)])]
    ppermute x14, waiting for transfers between devices: 52.2 us -> 33.4 us  [shifted(): return lax.ppermute(block, axis, route)]
  transfers between devices with their start and end apart: 18 -> 18, of which waited for: 6 -> 7; matrix products, arithmetic and copies ran while one was open for 6% -> 6% of each run, Pallas kernels for 15% -> 13%
where the time goes in v6:
time: 245 us; the launch traced here: 243 us
  waiting for transfers between devices  73.4 us (30%)
  Pallas kernels  72.6 us (30%)
  starting transfers between devices  48.3 us (20%)
  between operations  20.7 us (8%)
  other arithmetic  16.8 us (7%)
  local copies, waits for them, and re-layouts  10.9 us (4%)
    ppermute x14, starting transfers between devices, shifted(): return lax.ppermute(block, axis, route)  42.4 us
    ppermute x2, waiting for transfers between devices, swapped(): return lax.ppermute(block, axis, [(i, i ^ 1) for i in range(count)])  40 us
    pallas_call x1, Pallas kernels, resample_block(): pl.pallas_call(resample_kernel, grid=(2, nlines // ROWS), in_specs=[pl.Bl...  37.7 us
    pallas_call x8, Pallas kernels, looks(): pl.pallas_call(looks_kernel, grid=(width // CHUNK,), in_specs=[spec, spec...  34.9 us
    ppermute x14, waiting for transfers between devices, shifted(): return lax.ppermute(block, axis, route)  33.4 us
  transfers between devices with their start and end apart: 18, of which 7 were waited for; matrix products, arithmetic and copies ran while one was open for 6% of the time, Pallas kernels for 13%

profile of v6, /device:TPU:0, one launch (start us, length us, event | category | flops | bytes accessed | tf_op | source)
XLA Modules:
  0.0 242.8 jit_solution(14542223621290535442)
XLA Ops:
  0.0 1.1 fusion.31
  1.1 2.4 collective-permute-start
  3.4 1.3 collective-permute-start.1
  4.8 0.7 compare_select_fusion
  5.5 0.7 compare_and_fusion
  6.1 0.7 add_bitcast_fusion
  6.8 0.1 fusion.8
  8.3 0.1 copy.20
  8.3 0.7 dynamic-slice_reduce_fusion.weights_ref
  9.1 0.7 copy.21.shift_ref
  9.8 0.7 gather_fusion
  10.5 0.7 broadcast_select_fusion.2.coeff_ref
  11.2 0.0 collective-permute-done
  11.2 3.5 %fusion.2 = bf16[2,167,4096]{2,1,0:T(8,128)(2,1)S(1)} fusion(s32[]{:T(128)S(6)} %select_n.502, bf16[1,2,16,4096]{3,2,1,0:T(8,128)(2,1)S(1)} %collective-permute-done, bf16[1,2,160,4096]{3,2,1,0:T(8,128)(2,1)} %param.6, bf16[1,2,16,4096]{3,2,1,0:T(8,128)(2,1)S(1)} %collective-permute-done.1), kind=kLoop, calls=%fused_computation.6 | loop fusion | flops 8208384 | bytes 5881860 | tf_op jit(solution)/shard_map/convert_element_type | solution.py:86
  14.7 3.1 %pad_convert_fusion.window_ref = f32[2,168,4096]{2,1,0:T(8,128)} fusion(bf16[2,167,4096]{2,1,0:T(8,128)(2,1)S(1)} %fusion.2), kind=kLoop, calls=%fused_computation.7 | loop fusion | flops 1376256 | bytes 8241152 | tf_op jit(solution)/shard_map/jit(_pad)/pad | solution.py:87
  17.8 37.7 %shard_map.64 = bf16[2,160,4096]{2,1,0:T(8,128)(2,1)} custom-call(f32[8]{0:T(128)} %dynamic-slice_reduce_fusion.weights_ref, f32[2,168,4096]{2,1,0:T(8,128)} %pad_convert_fusion.window_ref, f32[160,8]{1,0:T(8,128)} %broadcast_select_fusion.2.coeff_ref, s32[160,1]{1,0:T(8,128)} %copy.21.shift_ref), custom_call_target="tpu_custom_call" | custom-call | tf_op jit(solution)/shard_map/pallas_call | solution.py:91
  55.5 2.0 fusion.30
  57.5 1.3 copy.24
  58.9 0.7 copy.32
  59.6 0.4 copy-done.4
  60.0 5.4 %collective-permute-start.6 = (bf16[2,160,2048]{2,1,0:T(8,128)(2,1)S(1)}, bf16[2,160,2048]{2,1,0:T(8,128)(2,1)}, u32[]{:S(2)}, u32[]{:S(2)}) collective-permute-start(bf16[2,160,2048]{2,1,0:T(8,128)(2,1)S(1)} %bitcast.60), channel_id=1, source_target_pairs={{0,8},{4,12},{8,16},{12,20},{16,24},{20,28},{1,9},{5,13},{9,17},{1... | collective-permute-start | bytes 3932168 | tf_op jit(solution)/shard_map/ppermute | solution.py:37
  65.4 1.3 copy.22
  66.8 0.7 copy.33
  67.5 0.4 copy-done.2
  67.9 1.5 collective-permute-start.2
  69.4 22.6 %collective-permute-done.6.second_ref = bf16[2,160,2048]{2,1,0:T(8,128)(2,1)} collective-permute-done((bf16[2,160,2048]{2,1,0:T(8,128)(2,1)S(1)}, bf16[2,160,2048]{2,1,0:T(8,128)(2,1)}, u32[]{:S(2)}, u32[]{:S(2)}) %collective-permute-start.6) | collective-permute-done | bytes 1310752 | tf_op jit(solution)/shard_map/ppermute | solution.py:37
  92.0 2.8 %broadcast_select_fusion = bf16[2,160,2048]{2,1,0:T(8,128)(2,1)S(1)} fusion(bf16[2,160,2048]{2,1,0:T(8,128)(2,1)} %collective-permute-done.6.second_ref, pred[]{:T(512)S(6)} %eq.128, bf16[2,20,8,2048]{3,0,1,2:T(2,128)(2,1)} %bitcast.73), kind=kLoop, calls=%fused_computation.10 | loop fusion | flops 655360 | bytes 3932161 | tf_op jit(solution)/shard_map/jit(_where)/select_n | solution.py:166
  94.7 2.0 collective-permute-start.7
  96.7 3.6 %collective-permute-done.2.second_ref = bf16[2,160,2048]{2,1,0:T(8,128)(2,1)} collective-permute-done((bf16[2,160,2048]{2,1,0:T(8,128)(2,1)S(1)}, bf16[2,160,2048]{2,1,0:T(8,128)(2,1)}, u32[]{:S(2)}, u32[]{:S(2)}) %collective-permute-start.2) | collective-permute-done | bytes 1310752 | tf_op jit(solution)/shard_map/ppermute | solution.py:37
  100.3 2.8 %broadcast_select_fusion.1 = bf16[2,160,2048]{2,1,0:T(8,128)(2,1)S(1)} fusion(bf16[2,160,2048]{2,1,0:T(8,128)(2,1)} %collective-permute-done.2.second_ref, pred[]{:T(512)S(6)} %eq.128, bf16[2,20,8,2048]{3,0,1,2:T(2,128)(2,1)S(1)} %bitcast.71), kind=kLoop, calls=%fused_computation.11 | loop fusion | flops 655360 | bytes 3932161 | tf_op jit(solution)/shard_map/jit(_where)/select_n | solution.py:162
  103.2 0.3 collective-permute-start.3
  103.4 3.4 %collective-permute-start.9 = (bf16[2,160,2048]{2,1,0:T(8,128)(2,1)}, bf16[2,160,2048]{2,1,0:T(8,128)(2,1)}, u32[]{:S(2)}, u32[]{:S(2)}) collective-permute-start(bf16[2,160,2048]{2,1,0:T(8,128)(2,1)} %collective-permute-done.6.second_ref), channel_id=1, source_target_pairs={{0,8},{4,12},{8,16},{12,20},{16,24},{20,28},{1,9},{5,13},{9,17},{1... | collective-permute-start | bytes 3932168 | tf_op jit(solution)/shard_map/ppermute | solution.py:37
  106.9 1.3 collective-permute-start.5
  108.2 17.5 %collective-permute-done.7.second_ref = bf16[2,160,2048]{2,1,0:T(8,128)(2,1)S(1)} collective-permute-done((bf16[2,160,2048]{2,1,0:T(8,128)(2,1)S(1)}, bf16[2,160,2048]{2,1,0:T(8,128)(2,1)S(1)}, u32[]{:S(2)}, u32[]{:S(2)}) %collective-permute-start.7) | collective-permute-done | bytes 1310752 | tf_op jit(solution)/shard_map/ppermute | solution.py:42
  125.7 5.6 %collective-permute-start.8 = (bf16[2,160,2048]{2,1,0:T(8,128)(2,1)S(1)}, bf16[2,160,2048]{2,1,0:T(8,128)(2,1)}, u32[]{:S(2)}, u32[]{:S(2)}) collective-permute-start(bf16[2,160,2048]{2,1,0:T(8,128)(2,1)S(1)} %collective-permute-done.7.second_ref), channel_id=1, source_target_pairs={{0,8},{4,12},{8,16},{12,20},{16,24},{20,28},{1,9},{5,13},{9,17},{1... | collective-permute-start | bytes 3932168 | tf_op jit(solution)/shard_map/ppermute | solution.py:37
  131.3 22.5 %collective-permute-done.3.second_ref = bf16[2,160,2048]{2,1,0:T(8,128)(2,1)S(1)} collective-permute-done((bf16[2,160,2048]{2,1,0:T(8,128)(2,1)S(1)}, bf16[2,160,2048]{2,1,0:T(8,128)(2,1)S(1)}, u32[]{:S(2)}, u32[]{:S(2)}) %collective-permute-start.3) | collective-permute-done | bytes 1310752 | tf_op jit(solution)/shard_map/ppermute | solution.py:42
  153.8 1.3 collective-permute-start.4
  155.1 4.4 %shard_map.70 = f32[2,8,512]{2,1,0:T(8,128)} custom-call(bf16[2,160,2048]{2,1,0:T(8,128)(2,1)} %bitcast.61, bf16[2,160,2048]{2,1,0:T(8,128)(2,1)} %collective-permute-done.6.second_ref), custom_call_target="tpu_custom_call" | custom-call | tf_op jit(solution)/shard_map/pallas_call | solution.py:136
  159.4 4.4 %shard_map.66 = f32[2,8,512]{2,1,0:T(8,128)} custom-call(bf16[2,160,2048]{2,1,0:T(8,128)(2,1)} %bitcast.66, bf16[2,160,2048]{2,1,0:T(8,128)(2,1)} %collective-permute-done.2.second_ref), custom_call_target="tpu_custom_call" | custom-call | tf_op jit(solution)/shard_map/pallas_call | solution.py:136
  163.8 4.4 %shard_map.69 = f32[2,8,512]{2,1,0:T(8,128)} custom-call(bf16[2,160,2048]{2,1,0:T(8,128)(2,1)} %bitcast.62, bf16[2,160,2048]{2,1,0:T(8,128)(2,1)} %copy-done.5), custom_call_target="tpu_custom_call" | custom-call | tf_op jit(solution)/shard_map/pallas_call | solution.py:136
  168.2 4.4 %shard_map.65 = f32[2,8,512]{2,1,0:T(8,128)} custom-call(bf16[2,160,2048]{2,1,0:T(8,128)(2,1)} %bitcast.67, bf16[2,160,2048]{2,1,0:T(8,128)(2,1)} %copy-done.6), custom_call_target="tpu_custom_call" | custom-call | tf_op jit(solution)/shard_map/pallas_call | solution.py:136
  172.6 4.4 %shard_map.72 = f32[2,8,512]{2,1,0:T(8,128)} custom-call(bf16[2,160,2048]{2,1,0:T(8,128)(2,1)} %bitcast.63, bf16[2,160,2048]{2,1,0:T(8,128)(2,1)} %collective-permute-done.9.second_ref), custom_call_target="tpu_custom_call" | custom-call | tf_op jit(solution)/shard_map/pallas_call | solution.py:136
  176.9 0.0 collective-permute-done.5.second_ref
  176.9 4.4 %shard_map.68 = f32[2,8,512]{2,1,0:T(8,128)} custom-call(bf16[2,160,2048]{2,1,0:T(8,128)(2,1)} %bitcast.68, bf16[2,160,2048]{2,1,0:T(8,128)(2,1)} %collective-permute-done.5.second_ref), custom_call_target="tpu_custom_call" | custom-call | tf_op jit(solution)/shard_map/pallas_call | solution.py:136
  181.3 0.0 collective-permute-done.8.second_ref
  181.3 4.4 %shard_map.71 = f32[2,8,512]{2,1,0:T(8,128)} custom-call(bf16[2,160,2048]{2,1,0:T(8,128)(2,1)} %bitcast.64, bf16[2,160,2048]{2,1,0:T(8,128)(2,1)} %collective-permute-done.8.second_ref), custom_call_target="tpu_custom_call" | custom-call | tf_op jit(solution)/shard_map/pallas_call | solution.py:136
  185.7 0.0 copy-start.10
  185.7 2.0 collective-permute-done.4.second_ref
  187.7 4.4 %shard_map.67 = f32[2,8,512]{2,1,0:T(8,128)} custom-call(bf16[2,160,2048]{2,1,0:T(8,128)(2,1)} %bitcast.69, bf16[2,160,2048]{2,1,0:T(8,128)(2,1)} %collective-permute-done.4.second_ref), custom_call_target="tpu_custom_call" | custom-call | tf_op jit(solution)/shard_map/pallas_call | solution.py:136
  192.1 5.2 %collective-permute-start.10 = (f32[2,8,512]{2,1,0:T(8,128)S(1)}, f32[2,8,512]{2,1,0:T(8,128)S(1)}, u32[]{:S(2)}, u32[]{:S(2)}) collective-permute-start(f32[2,8,512]{2,1,0:T(8,128)S(1)} %copy-done.12), channel_id=1, source_target_pairs={{0,16},{4,20},{8,24},{12,28},{1,17},{5,21},{9,25},{13,29},{2,18},{... | collective-permute-start | bytes 98312 | tf_op jit(solution)/shard_map/ppermute | solution.py:37
  197.3 0.6 fusion.40
  216.9 1.3 collective-permute-start.11
  218.2 5.7 %collective-permute-start.12 = (f32[2,8,512]{2,1,0:T(8,128)}, f32[2,8,512]{2,1,0:T(8,128)S(1)}, u32[]{:S(2)}, u32[]{:S(2)}) collective-permute-start(f32[2,8,512]{2,1,0:T(8,128)} %shard_map.67), channel_id=1, source_target_pairs={{0,12},{4,16},{8,20},{12,24},{16,28},{1,13},{5,17},{9,21},{13,25},... | collective-permute-start | bytes 98312 | tf_op jit(solution)/shard_map/ppermute | solution.py:37
  223.9 1.3 collective-permute-start.13
  225.2 3.8 %collective-permute-start.14 = (f32[2,8,512]{2,1,0:T(8,128)S(1)}, f32[2,8,512]{2,1,0:T(8,128)S(1)}, u32[]{:S(2)}, u32[]{:S(2)}) collective-permute-start(f32[2,8,512]{2,1,0:T(8,128)S(1)} %copy-done.8), channel_id=1, source_target_pairs={{0,8},{4,12},{8,16},{12,20},{16,24},{20,28},{1,9},{5,13},{9,17},{1... | collective-permute-start | bytes 98312 | tf_op jit(solution)/shard_map/ppermute | solution.py:37
  228.9 0.0 collective-permute-done.10
  229.0 1.3 collective-permute-start.15
  230.3 4.2 %collective-permute-start.16 = (f32[2,8,512]{2,1,0:T(8,128)S(1)}, f32[2,8,512]{2,1,0:T(8,128)S(1)}, u32[]{:S(2)}, u32[]{:S(2)}) collective-permute-start(f32[2,8,512]{2,1,0:T(8,128)S(1)} %copy-done.10), channel_id=1, source_target_pairs={{0,4},{4,8},{8,12},{12,16},{16,20},{20,24},{24,28},{1,5},{5,9},{9,... | collective-permute-start | bytes 98312 | tf_op jit(solution)/shard_map/ppermute | solution.py:37
  234.5 0.0 collective-permute-done.12
  234.5 1.3 collective-permute-start.17
  235.9 0.1 collective-permute-done.16
  236.1 5.0 %collective-permute-done.17 = f32[2,8,512]{2,1,0:T(8,128)S(1)} collective-permute-done((f32[2,8,512]{2,1,0:T(8,128)S(1)}, f32[2,8,512]{2,1,0:T(8,128)S(1)}, u32[]{:S(2)}, u32[]{:S(2)}) %collective-permute-start.17) | collective-permute-done | bytes 32800 | tf_op jit(solution)/shard_map/ppermute | solution.py:37
  241.1 0.8 select_select_fusion.3
  242.0 0.7 maximum_bitcast_fusion
  (53 shorter events, 0.3 us)
Async XLA Ops:
  1.1 10.1 %collective-permute-start = (bf16[1,2,16,4096]{3,2,1,0:T(8,128)(2,1)S(1)}, bf16[1,2,16,4096]{3,2,1,0:T(8,128)(2,1)S(1)}, u32[]{:S(2)}, u32[]{:S(2)}) collective-permute-start(bf16[1,2,16,4096]{3,2,1,0:T(8,128)(2,1)S(1)} %get-tuple-element.24), channel_id=1, source_target_pairs={{0,1},{1,2},{2,3},{4,5},{5,6},{6,7},{8,9},{9,10},{10,11},{12,13},{... | collective-permute-start | bytes 786440 | tf_op jit(solution)/shard_map/ppermute | solution.py:25
  3.4 7.8 %collective-permute-start.1 = (bf16[1,2,16,4096]{3,2,1,0:T(8,128)(2,1)S(1)}, bf16[1,2,16,4096]{3,2,1,0:T(8,128)(2,1)S(1)}, u32[]{:S(2)}, u32[]{:S(2)}) collective-permute-start(bf16[1,2,16,4096]{3,2,1,0:T(8,128)(2,1)S(1)} %get-tuple-element.23), channel_id=1, source_target_pairs={{1,0},{2,1},{3,2},{5,4},{6,5},{7,6},{9,8},{10,9},{11,10},{13,12},{... | collective-permute-start | bytes 786440 | tf_op jit(solution)/shard_map/ppermute | solution.py:27
  58.9 1.1 copy-start.4
  60.0 6.8 %copy-start = (bf16[2,20,8,2048]{3,2,1,0:T(8,128)(2,1)}, bf16[2,20,8,2048]{3,2,1,0:T(8,128)(2,1)S(1)}, u32[]{:S(2)}) copy-start(bf16[2,20,8,2048]{3,2,1,0:T(8,128)(2,1)S(1)} %copy.32) | copy-start | bytes 3932164
  60.0 32.0 %collective-permute-start.6 = (bf16[2,160,2048]{2,1,0:T(8,128)(2,1)S(1)}, bf16[2,160,2048]{2,1,0:T(8,128)(2,1)}, u32[]{:S(2)}, u32[]{:S(2)}) collective-permute-start(bf16[2,160,2048]{2,1,0:T(8,128)(2,1)S(1)} %bitcast.60), channel_id=1, source_target_pairs={{0,8},{4,12},{8,16},{12,20},{16,24},{20,28},{1,9},{5,13},{9,17},{1... | collective-permute-start | bytes 3932168 | tf_op jit(solution)/shard_map/ppermute | solution.py:37
  66.7 1.1 copy-start.2
  67.9 26.9 %copy-start.1 = (bf16[2,20,8,2048]{3,2,1,0:T(8,128)(2,1)}, bf16[2,20,8,2048]{3,2,1,0:T(8,128)(2,1)S(1)}, u32[]{:S(2)}) copy-start(bf16[2,20,8,2048]{3,2,1,0:T(8,128)(2,1)S(1)} %copy.33) | copy-start | bytes 3932164
  67.9 32.5 %collective-permute-start.2 = (bf16[2,160,2048]{2,1,0:T(8,128)(2,1)S(1)}, bf16[2,160,2048]{2,1,0:T(8,128)(2,1)}, u32[]{:S(2)}, u32[]{:S(2)}) collective-permute-start(bf16[2,160,2048]{2,1,0:T(8,128)(2,1)S(1)} %bitcast.65), channel_id=1, source_target_pairs={{8,0},{12,4},{16,8},{20,12},{24,16},{28,20},{9,1},{13,5},{17,9},{2... | collective-permute-start | bytes 3932168 | tf_op jit(solution)/shard_map/ppermute | solution.py:37
  69.3 31.0 %copy-start.3 = (bf16[2,160,2048]{2,0,1:T(2,128)(2,1)S(1)}, bf16[2,160,2048]{2,0,1:T(2,128)(2,1)}, u32[]{:S(2)}) copy-start(bf16[2,160,2048]{2,0,1:T(2,128)(2,1)} %copy-done.2) | copy-start | bytes 3932164
  94.7 31.0 %collective-permute-start.7 = (bf16[2,160,2048]{2,1,0:T(8,128)(2,1)S(1)}, bf16[2,160,2048]{2,1,0:T(8,128)(2,1)S(1)}, u32[]{:S(2)}, u32[]{:S(2)}) collective-permute-start(bf16[2,160,2048]{2,1,0:T(8,128)(2,1)S(1)} %broadcast_select_fusion), channel_id=1, source_target_pairs={{0,4},{4,0},{8,12},{12,8},{16,20},{20,16},{24,28},{28,24},{1,5},{5... | collective-permute-start | bytes 3932168 | tf_op jit(solution)/shard_map/ppermute | solution.py:42
  103.2 50.6 %collective-permute-start.3 = (bf16[2,160,2048]{2,1,0:T(8,128)(2,1)S(1)}, bf16[2,160,2048]{2,1,0:T(8,128)(2,1)S(1)}, u32[]{:S(2)}, u32[]{:S(2)}) collective-permute-start(bf16[2,160,2048]{2,1,0:T(8,128)(2,1)S(1)} %broadcast_select_fusion.1), channel_id=1, source_target_pairs={{0,4},{4,0},{8,12},{12,8},{16,20},{20,16},{24,28},{28,24},{1,5},{5... | collective-permute-start | bytes 3932168 | tf_op jit(solution)/shard_map/ppermute | solution.py:42
  103.4 69.1 %collective-permute-start.9 = (bf16[2,160,2048]{2,1,0:T(8,128)(2,1)}, bf16[2,160,2048]{2,1,0:T(8,128)(2,1)}, u32[]{:S(2)}, u32[]{:S(2)}) collective-permute-start(bf16[2,160,2048]{2,1,0:T(8,128)(2,1)} %collective-permute-done.6.second_ref), channel_id=1, source_target_pairs={{0,8},{4,12},{8,16},{12,20},{16,24},{20,28},{1,9},{5,13},{9,17},{1... | collective-permute-start | bytes 3932168 | tf_op jit(solution)/shard_map/ppermute | solution.py:37
  106.9 70.1 %collective-permute-start.5 = (bf16[2,160,2048]{2,1,0:T(8,128)(2,1)}, bf16[2,160,2048]{2,1,0:T(8,128)(2,1)}, u32[]{:S(2)}, u32[]{:S(2)}) collective-permute-start(bf16[2,160,2048]{2,1,0:T(8,128)(2,1)} %collective-permute-done.2.second_ref), channel_id=1, source_target_pairs={{8,0},{12,4},{16,8},{20,12},{24,16},{28,20},{9,1},{13,5},{17,9},{2... | collective-permute-start | bytes 3932168 | tf_op jit(solution)/shard_map/ppermute | solution.py:37
  125.7 33.7 %copy-start.5 = (bf16[2,160,2048]{2,1,0:T(8,128)(2,1)}, bf16[2,160,2048]{2,1,0:T(8,128)(2,1)S(1)}, u32[]{:S(2)}) copy-start(bf16[2,160,2048]{2,1,0:T(8,128)(2,1)S(1)} %collective-permute-done.7.second_ref) | copy-start | bytes 3932164
  125.7 55.6 %collective-permute-start.8 = (bf16[2,160,2048]{2,1,0:T(8,128)(2,1)S(1)}, bf16[2,160,2048]{2,1,0:T(8,128)(2,1)}, u32[]{:S(2)}, u32[]{:S(2)}) collective-permute-start(bf16[2,160,2048]{2,1,0:T(8,128)(2,1)S(1)} %collective-permute-done.7.second_ref), channel_id=1, source_target_pairs={{0,8},{4,12},{8,16},{12,20},{16,24},{20,28},{1,9},{5,13},{9,17},{1... | collective-permute-start | bytes 3932168 | tf_op jit(solution)/shard_map/ppermute | solution.py:37
  153.8 5.7 %copy-start.6 = (bf16[2,160,2048]{2,1,0:T(8,128)(2,1)}, bf16[2,160,2048]{2,1,0:T(8,128)(2,1)S(1)}, u32[]{:S(2)}) copy-start(bf16[2,160,2048]{2,1,0:T(8,128)(2,1)S(1)} %collective-permute-done.3.second_ref) | copy-start | bytes 3932164
  153.8 33.9 %collective-permute-start.4 = (bf16[2,160,2048]{2,1,0:T(8,128)(2,1)S(1)}, bf16[2,160,2048]{2,1,0:T(8,128)(2,1)}, u32[]{:S(2)}, u32[]{:S(2)}) collective-permute-start(bf16[2,160,2048]{2,1,0:T(8,128)(2,1)S(1)} %collective-permute-done.3.second_ref), channel_id=1, source_target_pairs={{8,0},{12,4},{16,8},{20,12},{24,16},{28,20},{9,1},{13,5},{17,9},{2... | collective-permute-start | bytes 3932168 | tf_op jit(solution)/shard_map/ppermute | solution.py:37
  185.7 6.4 %copy-start.12 = (f32[2,8,512]{2,1,0:T(8,128)S(1)}, f32[2,8,512]{2,1,0:T(8,128)}, u32[]{:S(2)}) copy-start(f32[2,8,512]{2,1,0:T(8,128)} %shard_map.68) | copy-start | bytes 98308
  185.7 11.6 %copy-start.15 = (s32[1,4]{1,0:T(1,128)S(1)}, s32[1,4]{1,0:T(1,128)}, u32[]{:S(2)}) copy-start(s32[1,4]{1,0:T(1,128)} %param.11) | copy-start | bytes 52
  185.7 31.2 %copy-start.11 = (f32[2,8,512]{2,1,0:T(8,128)S(1)}, f32[2,8,512]{2,1,0:T(8,128)}, u32[]{:S(2)}) copy-start(f32[2,8,512]{2,1,0:T(8,128)} %shard_map.72) | copy-start | bytes 98308
  185.7 38.2 %copy-start.13 = (f32[2,8,512]{2,1,0:T(8,128)S(1)}, f32[2,8,512]{2,1,0:T(8,128)}, u32[]{:S(2)}) copy-start(f32[2,8,512]{2,1,0:T(8,128)} %shard_map.71) | copy-start | bytes 98308
  185.7 39.5 %copy-start.8 = (f32[2,8,512]{2,1,0:T(8,128)S(1)}, f32[2,8,512]{2,1,0:T(8,128)}, u32[]{:S(2)}) copy-start(f32[2,8,512]{2,1,0:T(8,128)} %shard_map.66) | copy-start | bytes 98308
  185.7 43.3 %copy-start.7 = (f32[2,8,512]{2,1,0:T(8,128)S(1)}, f32[2,8,512]{2,1,0:T(8,128)}, u32[]{:S(2)}) copy-start(f32[2,8,512]{2,1,0:T(8,128)} %shard_map.70) | copy-start | bytes 98308
  185.7 44.6 %copy-start.10 = (f32[2,8,512]{2,1,0:T(8,128)S(1)}, f32[2,8,512]{2,1,0:T(8,128)}, u32[]{:S(2)}) copy-start(f32[2,8,512]{2,1,0:T(8,128)} %shard_map.65) | copy-start | bytes 98308
  185.7 48.8 %copy-start.9 = (f32[2,8,512]{2,1,0:T(8,128)S(1)}, f32[2,8,512]{2,1,0:T(8,128)}, u32[]{:S(2)}) copy-start(f32[2,8,512]{2,1,0:T(8,128)} %shard_map.69) | copy-start | bytes 98308
  192.1 49.8 %copy-start.14 = (f32[2,8,512]{2,1,0:T(8,128)S(1)}, f32[2,8,512]{2,1,0:T(8,128)}, u32[]{:S(2)}) copy-start(f32[2,8,512]{2,1,0:T(8,128)} %shard_map.67) | copy-start | bytes 98308
  192.1 36.9 %collective-permute-start.10 = (f32[2,8,512]{2,1,0:T(8,128)S(1)}, f32[2,8,512]{2,1,0:T(8,128)S(1)}, u32[]{:S(2)}, u32[]{:S(2)}) collective-permute-start(f32[2,8,512]{2,1,0:T(8,128)S(1)} %copy-done.12), channel_id=1, source_target_pairs={{0,16},{4,20},{8,24},{12,28},{1,17},{5,21},{9,25},{13,29},{2,18},{... | collective-permute-start | bytes 98312 | tf_op jit(solution)/shard_map/ppermute | solution.py:37
  216.9 13.4 %collective-permute-start.11 = (f32[2,8,512]{2,1,0:T(8,128)S(1)}, f32[2,8,512]{2,1,0:T(8,128)S(1)}, u32[]{:S(2)}, u32[]{:S(2)}) collective-permute-start(f32[2,8,512]{2,1,0:T(8,128)S(1)} %copy-done.11), channel_id=1, source_target_pairs={{16,0},{20,4},{24,8},{28,12},{17,1},{21,5},{25,9},{29,13},{18,2},{... | collective-permute-start | bytes 98312 | tf_op jit(solution)/shard_map/ppermute | solution.py:37
  218.2 16.3 %collective-permute-start.12 = (f32[2,8,512]{2,1,0:T(8,128)}, f32[2,8,512]{2,1,0:T(8,128)S(1)}, u32[]{:S(2)}, u32[]{:S(2)}) collective-permute-start(f32[2,8,512]{2,1,0:T(8,128)} %shard_map.67), channel_id=1, source_target_pairs={{0,12},{4,16},{8,20},{12,24},{16,28},{1,13},{5,17},{9,21},{13,25},... | collective-permute-start | bytes 98312 | tf_op jit(solution)/shard_map/ppermute | solution.py:37
  223.9 11.9 %collective-permute-start.13 = (f32[2,8,512]{2,1,0:T(8,128)S(1)}, f32[2,8,512]{2,1,0:T(8,128)S(1)}, u32[]{:S(2)}, u32[]{:S(2)}) collective-permute-start(f32[2,8,512]{2,1,0:T(8,128)S(1)} %copy-done.13), channel_id=1, source_target_pairs={{12,0},{16,4},{20,8},{24,12},{28,16},{13,1},{17,5},{21,9},{25,13},... | collective-permute-start | bytes 98312 | tf_op jit(solution)/shard_map/ppermute | solution.py:37
  225.2 10.7 %collective-permute-start.14 = (f32[2,8,512]{2,1,0:T(8,128)S(1)}, f32[2,8,512]{2,1,0:T(8,128)S(1)}, u32[]{:S(2)}, u32[]{:S(2)}) collective-permute-start(f32[2,8,512]{2,1,0:T(8,128)S(1)} %copy-done.8), channel_id=1, source_target_pairs={{0,8},{4,12},{8,16},{12,20},{16,24},{20,28},{1,9},{5,13},{9,17},{1... | collective-permute-start | bytes 98312 | tf_op jit(solution)/shard_map/ppermute | solution.py:37
  229.0 6.9 %collective-permute-start.15 = (f32[2,8,512]{2,1,0:T(8,128)S(1)}, f32[2,8,512]{2,1,0:T(8,128)S(1)}, u32[]{:S(2)}, u32[]{:S(2)}) collective-permute-start(f32[2,8,512]{2,1,0:T(8,128)S(1)} %copy-done.7), channel_id=1, source_target_pairs={{8,0},{12,4},{16,8},{20,12},{24,16},{28,20},{9,1},{13,5},{17,9},{2... | collective-permute-start | bytes 98312 | tf_op jit(solution)/shard_map/ppermute | solution.py:37
  230.3 5.8 %collective-permute-start.16 = (f32[2,8,512]{2,1,0:T(8,128)S(1)}, f32[2,8,512]{2,1,0:T(8,128)S(1)}, u32[]{:S(2)}, u32[]{:S(2)}) collective-permute-start(f32[2,8,512]{2,1,0:T(8,128)S(1)} %copy-done.10), channel_id=1, source_target_pairs={{0,4},{4,8},{8,12},{12,16},{16,20},{20,24},{24,28},{1,5},{5,9},{9,... | collective-permute-start | bytes 98312 | tf_op jit(solution)/shard_map/ppermute | solution.py:37
  234.5 6.6 %collective-permute-start.17 = (f32[2,8,512]{2,1,0:T(8,128)S(1)}, f32[2,8,512]{2,1,0:T(8,128)S(1)}, u32[]{:S(2)}, u32[]{:S(2)}) collective-permute-start(f32[2,8,512]{2,1,0:T(8,128)S(1)} %copy-done.9), channel_id=1, source_target_pairs={{4,0},{8,4},{12,8},{16,12},{20,16},{24,20},{28,24},{5,1},{9,5},{13... | collective-permute-start | bytes 98312 | tf_op jit(solution)/shard_map/ppermute | solution.py:37

commit v7 on v2

--- a/solution.py
+++ b/solution.py
@@ -49,7 +49,7 @@
     return jnp.sinc(place) * (0.5 + 0.5 * jnp.cos(jnp.pi * place / 4.5))
 
 
-ROWS = 16
+ROWS = 32
 EDGE = 128
 
 
@@ -99,6 +99,9 @@
         ],
         out_specs=pl.BlockSpec((1, ROWS, nrange), lambda c, t: (c, t, 0)),
         out_shape=jax.ShapeDtypeStruct((2, nlines, nrange), jnp.bfloat16),
+        cost_estimate=pl.CostEstimate(
+            flops=2 * nlines * nrange * 60, transcendentals=0, bytes_accessed=2 * nlines * nrange * 6
+        ),
     )(weights, window, coeff, shift)
     half = nrange // 2
     return look_order(out[:, :, :half]), look_order(out[:, :, half:])
@@ -139,6 +142,9 @@
         in_specs=[spec, spec],
         out_specs=pl.BlockSpec((2, groups, CHUNK // LOOK_RG), lambda j: (0, 0, j)),
         out_shape=jax.ShapeDtypeStruct((2, groups, width // LOOK_RG), jnp.float32),
+        cost_estimate=pl.CostEstimate(
+            flops=nlines * width * 40, transcendentals=0, bytes_accessed=2 * 2 * nlines * width * 2
+        ),
     )(first, second)
 
 

time: 229 us -> 224 us (0.978)
  Pallas kernels: 72.6 us -> 68.1 us
    pallas_call x1, Pallas kernels: 37.7 us -> 33.1 us  [resample_block(): pl.pallas_call(resample_kernel, grid=(2, nlines // ROWS), in_specs=[pl.Bl...]
  transfers between devices with their start and end apart: 18 -> 18, of which waited for: 6 -> 6; matrix products, arithmetic and copies ran while one was open for 6% -> 7% of each run, Pallas kernels for 15% -> 16%
where the time goes in v7:
time: 224 us; the launch traced here: 222 us
  Pallas kernels  68.1 us (30%)
  waiting for transfers between devices  52 us (23%)
  starting transfers between devices  48.9 us (22%)
  between operations  21.7 us (10%)
  other arithmetic  18.6 us (8%)
  local copies, waits for them, and re-layouts  12.9 us (6%)
    ppermute x14, waiting for transfers between devices, shifted(): return lax.ppermute(block, axis, route)  52 us
    ppermute x14, starting transfers between devices, shifted(): return lax.ppermute(block, axis, route)  42.6 us
    pallas_call x8, Pallas kernels, looks(): pl.pallas_call(looks_kernel, grid=(width // CHUNK,), in_specs=[spec, spec...  34.9 us
    pallas_call x1, Pallas kernels, resample_block(): pl.pallas_call(resample_kernel, grid=(2, nlines // ROWS), in_specs=[pl.Bl...  33.1 us
    slice x3, local copies, waits for them, and re-layouts, resample_block(): return (look_order(out[:, :, :half]), look_order(out[:, :, half:]))  4.72 us
  transfers between devices with their start and end apart: 18, of which 6 were waited for; matrix products, arithmetic and copies ran while one was open for 7% of the time, Pallas kernels for 16%

profile of v7, /device:TPU:0, one launch (start us, length us, event | category | flops | bytes accessed | tf_op | source)
XLA Modules:
  0.0 222.2 jit_solution(17035462294482237702)
XLA Ops:
  0.0 1.1 fusion.31
  1.1 1.3 collective-permute-start.1
  2.4 3.0 %collective-permute-start = (bf16[1,2,16,4096]{3,2,1,0:T(8,128)(2,1)S(1)}, bf16[1,2,16,4096]{3,2,1,0:T(8,128)(2,1)S(1)}, u32[]{:S(2)}, u32[]{:S(2)}) collective-permute-start(bf16[1,2,16,4096]{3,2,1,0:T(8,128)(2,1)S(1)} %get-tuple-element.8), channel_id=1, source_target_pairs={{0,1},{1,2},{2,3},{4,5},{5,6},{6,7},{8,9},{9,10},{10,11},{12,13},{... | collective-permute-start | bytes 786440 | tf_op jit(solution)/shard_map/ppermute | solution.py:25
  5.4 0.7 compare_select_fusion
  6.1 0.7 compare_and_fusion
  6.8 0.7 add_bitcast_fusion
  7.5 0.1 fusion.8
  8.9 0.1 copy.20
  9.0 0.7 dynamic-slice_reduce_fusion.weights_ref
  9.7 0.7 copy.21.shift_ref
  10.4 0.7 gather_fusion
  11.1 0.7 broadcast_select_fusion.2.coeff_ref
  11.8 0.0 collective-permute-done.1
  11.8 0.0 collective-permute-done
  11.8 3.5 %fusion.2 = bf16[2,167,4096]{2,1,0:T(8,128)(2,1)S(1)} fusion(s32[]{:T(128)S(6)} %select_n.502, bf16[1,2,16,4096]{3,2,1,0:T(8,128)(2,1)S(1)} %collective-permute-done, bf16[1,2,160,4096]{3,2,1,0:T(8,128)(2,1)} %param.6, bf16[1,2,16,4096]{3,2,1,0:T(8,128)(2,1)S(1)} %collective-permute-done.1), kind=kLoop, calls=%fused_computation.6 | loop fusion | flops 8208384 | bytes 5881860 | tf_op jit(solution)/shard_map/convert_element_type | solution.py:86
  15.3 3.1 %pad_convert_fusion.window_ref = f32[2,168,4096]{2,1,0:T(8,128)} fusion(bf16[2,167,4096]{2,1,0:T(8,128)(2,1)S(1)} %fusion.2), kind=kLoop, calls=%fused_computation.7 | loop fusion | flops 1376256 | bytes 8241152 | tf_op jit(solution)/shard_map/jit(_pad)/pad | solution.py:87
  18.4 33.1 %shard_map.64 = bf16[2,160,4096]{2,1,0:T(8,128)(2,1)} custom-call(f32[8]{0:T(128)} %dynamic-slice_reduce_fusion.weights_ref, f32[2,168,4096]{2,1,0:T(8,128)} %pad_convert_fusion.window_ref, f32[160,8]{1,0:T(8,128)} %broadcast_select_fusion.2.coeff_ref, s32[160,1]{1,0:T(8,128)} %copy.21.shift_ref), custom_call_target="tpu_custom_call" | custom-call | flops 78643200 | bytes 7864320 | tf_op jit(solution)/shard_map/pallas_call | solution.py:91
  51.5 2.0 fusion.30
  53.5 1.3 copy.24
  54.9 0.7 copy.32
  55.6 0.3 copy-done.4
  55.9 6.1 %collective-permute-start.5 = (bf16[2,160,2048]{2,1,0:T(8,128)(2,1)S(1)}, bf16[2,160,2048]{2,1,0:T(8,128)(2,1)}, u32[]{:S(2)}, u32[]{:S(2)}) collective-permute-start(bf16[2,160,2048]{2,1,0:T(8,128)(2,1)S(1)} %bitcast.65), channel_id=1, source_target_pairs={{0,8},{4,12},{8,16},{12,20},{16,24},{20,28},{1,9},{5,13},{9,17},{1... | collective-permute-start | bytes 3932168 | tf_op jit(solution)/shard_map/ppermute | solution.py:37
  62.0 1.3 copy.22
  63.4 0.7 copy.33
  64.1 0.4 copy-done.2
  64.5 1.5 collective-permute-start.2
  66.0 23.9 %collective-permute-done.5.second_ref = bf16[2,160,2048]{2,1,0:T(8,128)(2,1)} collective-permute-done((bf16[2,160,2048]{2,1,0:T(8,128)(2,1)S(1)}, bf16[2,160,2048]{2,1,0:T(8,128)(2,1)}, u32[]{:S(2)}, u32[]{:S(2)}) %collective-permute-start.5) | collective-permute-done | bytes 1310752 | tf_op jit(solution)/shard_map/ppermute | solution.py:37
  89.9 3.8 %broadcast_select_fusion = bf16[2,160,2048]{2,1,0:T(8,128)(2,1)} fusion(bf16[2,160,2048]{2,1,0:T(8,128)(2,1)} %collective-permute-done.5.second_ref, pred[]{:T(512)S(6)} %eq.130, bf16[2,20,8,2048]{3,0,1,2:T(2,128)(2,1)} %bitcast.73), kind=kLoop, calls=%fused_computation.10 | loop fusion | flops 655360 | bytes 3932161 | tf_op jit(solution)/shard_map/jit(_where)/select_n | solution.py:172
  93.8 1.9 collective-permute-start.11
  95.7 5.6 %collective-permute-start.6 = (bf16[2,160,2048]{2,1,0:T(8,128)(2,1)}, bf16[2,160,2048]{2,1,0:T(8,128)(2,1)}, u32[]{:S(2)}, u32[]{:S(2)}) collective-permute-start(bf16[2,160,2048]{2,1,0:T(8,128)(2,1)} %collective-permute-done.5.second_ref), channel_id=1, source_target_pairs={{0,8},{4,12},{8,16},{12,20},{16,24},{20,28},{1,9},{5,13},{9,17},{1... | collective-permute-start | bytes 3932168 | tf_op jit(solution)/shard_map/ppermute | solution.py:37
  101.3 2.8 %broadcast_select_fusion.1 = bf16[2,160,2048]{2,1,0:T(8,128)(2,1)S(1)} fusion(bf16[2,160,2048]{2,1,0:T(8,128)(2,1)} %collective-permute-done.2.second_ref, pred[]{:T(512)S(6)} %eq.130, bf16[2,20,8,2048]{3,0,1,2:T(2,128)(2,1)S(1)} %bitcast.71), kind=kLoop, calls=%fused_computation.11 | loop fusion | flops 655360 | bytes 3932161 | tf_op jit(solution)/shard_map/jit(_where)/select_n | solution.py:168
  104.1 0.0 copy-start.16
  104.1 0.1 collective-permute-start.8
  104.2 1.3 collective-permute-start.3
  105.5 4.4 %shard_map.70 = f32[2,8,512]{2,1,0:T(8,128)} custom-call(bf16[2,160,2048]{2,1,0:T(8,128)(2,1)} %bitcast.66, bf16[2,160,2048]{2,1,0:T(8,128)(2,1)} %collective-permute-done.5.second_ref), custom_call_target="tpu_custom_call" | custom-call | flops 13107200 | bytes 2621440 | tf_op jit(solution)/shard_map/pallas_call | solution.py:139
  109.9 1.3 collective-permute-start.15
  111.2 0.6 fusion.40
  131.7 4.4 %shard_map.69 = f32[2,8,512]{2,1,0:T(8,128)} custom-call(bf16[2,160,2048]{2,1,0:T(8,128)(2,1)} %bitcast.61, bf16[2,160,2048]{2,1,0:T(8,128)(2,1)} %collective-permute-done.2.second_ref), custom_call_target="tpu_custom_call" | custom-call | flops 13107200 | bytes 2621440 | tf_op jit(solution)/shard_map/pallas_call | solution.py:139
  136.0 1.3 collective-permute-done.15
  137.4 3.8 %collective-permute-start.14 = (f32[2,8,512]{2,1,0:T(8,128)}, f32[2,8,512]{2,1,0:T(8,128)S(1)}, u32[]{:S(2)}, u32[]{:S(2)}) collective-permute-start(f32[2,8,512]{2,1,0:T(8,128)} %shard_map.69), channel_id=1, source_target_pairs={{0,8},{4,12},{8,16},{12,20},{16,24},{20,28},{1,9},{5,13},{9,17},{1... | collective-permute-start | bytes 98312 | tf_op jit(solution)/shard_map/ppermute | solution.py:37
  141.2 1.9 collective-permute-done.14
  143.1 4.4 %shard_map.72 = f32[2,8,512]{2,1,0:T(8,128)} custom-call(bf16[2,160,2048]{2,1,0:T(8,128)(2,1)} %bitcast.67, bf16[2,160,2048]{2,1,0:T(8,128)(2,1)} %collective-permute-done.11.second_ref), custom_call_target="tpu_custom_call" | custom-call | flops 13107200 | bytes 2621440 | tf_op jit(solution)/shard_map/pallas_call | solution.py:139
  147.5 1.3 collective-permute-start.17
  148.8 7.0 %collective-permute-start.12 = (bf16[2,160,2048]{2,1,0:T(8,128)(2,1)}, bf16[2,160,2048]{2,1,0:T(8,128)(2,1)}, u32[]{:S(2)}, u32[]{:S(2)}) collective-permute-start(bf16[2,160,2048]{2,1,0:T(8,128)(2,1)} %collective-permute-done.11.second_ref), channel_id=1, source_target_pairs={{0,8},{4,12},{8,16},{12,20},{16,24},{20,28},{1,9},{5,13},{9,17},{1... | collective-permute-start | bytes 3932168 | tf_op jit(solution)/shard_map/ppermute | solution.py:37
  155.8 4.4 %shard_map.66 = f32[2,8,512]{2,1,0:T(8,128)} custom-call(bf16[2,160,2048]{2,1,0:T(8,128)(2,1)} %bitcast.68, bf16[2,160,2048]{2,1,0:T(8,128)(2,1)} %collective-permute-done.6.second_ref), custom_call_target="tpu_custom_call" | custom-call | flops 13107200 | bytes 2621440 | tf_op jit(solution)/shard_map/pallas_call | solution.py:139
  160.2 1.3 collective-permute-start.7
  161.5 1.1 copy-done.5
  162.6 4.4 %shard_map.71 = f32[2,8,512]{2,1,0:T(8,128)} custom-call(bf16[2,160,2048]{2,1,0:T(8,128)(2,1)} %bitcast.62, bf16[2,160,2048]{2,1,0:T(8,128)(2,1)} %copy-done.5), custom_call_target="tpu_custom_call" | custom-call | flops 13107200 | bytes 2621440 | tf_op jit(solution)/shard_map/pallas_call | solution.py:139
  167.0 2.8 %collective-permute-start.16 = (f32[2,8,512]{2,1,0:T(8,128)}, f32[2,8,512]{2,1,0:T(8,128)S(1)}, u32[]{:S(2)}, u32[]{:S(2)}) collective-permute-start(f32[2,8,512]{2,1,0:T(8,128)} %shard_map.71), channel_id=1, source_target_pairs={{0,4},{4,8},{8,12},{12,16},{16,20},{20,24},{24,28},{1,5},{5,9},{9,... | collective-permute-start | bytes 98312 | tf_op jit(solution)/shard_map/ppermute | solution.py:37
  169.8 4.4 %shard_map.65 = f32[2,8,512]{2,1,0:T(8,128)} custom-call(bf16[2,160,2048]{2,1,0:T(8,128)(2,1)} %bitcast.63, bf16[2,160,2048]{2,1,0:T(8,128)(2,1)} %collective-permute-done.3.second_ref), custom_call_target="tpu_custom_call" | custom-call | flops 13107200 | bytes 2621440 | tf_op jit(solution)/shard_map/pallas_call | solution.py:139
  174.2 5.4 %collective-permute-start.4 = (f32[2,8,512]{2,1,0:T(8,128)}, f32[2,8,512]{2,1,0:T(8,128)S(1)}, u32[]{:S(2)}, u32[]{:S(2)}) collective-permute-start(f32[2,8,512]{2,1,0:T(8,128)} %shard_map.65), channel_id=1, source_target_pairs={{0,16},{4,20},{8,24},{12,28},{1,17},{5,21},{9,25},{13,29},{2,18},{... | collective-permute-start | bytes 98312 | tf_op jit(solution)/shard_map/ppermute | solution.py:37
  179.6 1.3 collective-permute-start.9
  181.0 0.9 collective-permute-done.4
  182.0 4.4 %shard_map.68 = f32[2,8,512]{2,1,0:T(8,128)} custom-call(bf16[2,160,2048]{2,1,0:T(8,128)(2,1)} %bitcast.69, bf16[2,160,2048]{2,1,0:T(8,128)(2,1)} %collective-permute-done.12.second_ref), custom_call_target="tpu_custom_call" | custom-call | flops 13107200 | bytes 2621440 | tf_op jit(solution)/shard_map/pallas_call | solution.py:139
  186.3 1.3 collective-permute-start.13
  187.7 0.0 copy-start.10
  187.7 22.0 %collective-permute-done.9.second_ref = bf16[2,160,2048]{2,1,0:T(8,128)(2,1)S(1)} collective-permute-done((bf16[2,160,2048]{2,1,0:T(8,128)(2,1)S(1)}, bf16[2,160,2048]{2,1,0:T(8,128)(2,1)S(1)}, u32[]{:S(2)}, u32[]{:S(2)}) %collective-permute-start.9) | collective-permute-done | bytes 1310752 | tf_op jit(solution)/shard_map/ppermute | solution.py:37
  209.7 1.1 copy-done.7
  210.8 4.4 %shard_map.67 = f32[2,8,512]{2,1,0:T(8,128)} custom-call(bf16[2,160,2048]{2,1,0:T(8,128)(2,1)} %bitcast.64, bf16[2,160,2048]{2,1,0:T(8,128)(2,1)} %copy-done.7), custom_call_target="tpu_custom_call" | custom-call | flops 13107200 | bytes 2621440 | tf_op jit(solution)/shard_map/pallas_call | solution.py:139
  215.1 2.6 %collective-permute-start.10 = (f32[2,8,512]{2,1,0:T(8,128)}, f32[2,8,512]{2,1,0:T(8,128)S(1)}, u32[]{:S(2)}, u32[]{:S(2)}) collective-permute-start(f32[2,8,512]{2,1,0:T(8,128)} %shard_map.67), channel_id=1, source_target_pairs={{0,12},{4,16},{8,20},{12,24},{16,28},{1,13},{5,17},{9,21},{13,25},... | collective-permute-start | bytes 98312 | tf_op jit(solution)/shard_map/ppermute | solution.py:37
  217.8 1.9 collective-permute-done.10
  219.7 0.8 select_select_fusion.2
  220.5 0.8 select_select_fusion.1
  221.4 0.7 maximum_bitcast_fusion
  (59 shorter events, 0.3 us)
Async XLA Ops:
  1.1 10.8 %collective-permute-start.1 = (bf16[1,2,16,4096]{3,2,1,0:T(8,128)(2,1)S(1)}, bf16[1,2,16,4096]{3,2,1,0:T(8,128)(2,1)S(1)}, u32[]{:S(2)}, u32[]{:S(2)}) collective-permute-start(bf16[1,2,16,4096]{3,2,1,0:T(8,128)(2,1)S(1)} %get-tuple-element.7), channel_id=1, source_target_pairs={{1,0},{2,1},{3,2},{5,4},{6,5},{7,6},{9,8},{10,9},{11,10},{13,12},{... | collective-permute-start | bytes 786440 | tf_op jit(solution)/shard_map/ppermute | solution.py:27
  2.4 9.5 %collective-permute-start = (bf16[1,2,16,4096]{3,2,1,0:T(8,128)(2,1)S(1)}, bf16[1,2,16,4096]{3,2,1,0:T(8,128)(2,1)S(1)}, u32[]{:S(2)}, u32[]{:S(2)}) collective-permute-start(bf16[1,2,16,4096]{3,2,1,0:T(8,128)(2,1)S(1)} %get-tuple-element.8), channel_id=1, source_target_pairs={{0,1},{1,2},{2,3},{4,5},{5,6},{6,7},{8,9},{9,10},{10,11},{12,13},{... | collective-permute-start | bytes 786440 | tf_op jit(solution)/shard_map/ppermute | solution.py:25
  54.9 1.1 copy-start.4
  55.9 7.4 %copy-start.1 = (bf16[2,20,8,2048]{3,2,1,0:T(8,128)(2,1)}, bf16[2,20,8,2048]{3,2,1,0:T(8,128)(2,1)S(1)}, u32[]{:S(2)}) copy-start(bf16[2,20,8,2048]{3,2,1,0:T(8,128)(2,1)S(1)} %copy.32) | copy-start | bytes 3932164
  55.9 34.0 %collective-permute-start.5 = (bf16[2,160,2048]{2,1,0:T(8,128)(2,1)S(1)}, bf16[2,160,2048]{2,1,0:T(8,128)(2,1)}, u32[]{:S(2)}, u32[]{:S(2)}) collective-permute-start(bf16[2,160,2048]{2,1,0:T(8,128)(2,1)S(1)} %bitcast.65), channel_id=1, source_target_pairs={{0,8},{4,12},{8,16},{12,20},{16,24},{20,28},{1,9},{5,13},{9,17},{1... | collective-permute-start | bytes 3932168 | tf_op jit(solution)/shard_map/ppermute | solution.py:37
  63.4 1.1 copy-start.2
  64.5 29.3 %copy-start = (bf16[2,20,8,2048]{3,2,1,0:T(8,128)(2,1)}, bf16[2,20,8,2048]{3,2,1,0:T(8,128)(2,1)S(1)}, u32[]{:S(2)}) copy-start(bf16[2,20,8,2048]{3,2,1,0:T(8,128)(2,1)S(1)} %copy.33) | copy-start | bytes 3932164
  64.5 36.8 %collective-permute-start.2 = (bf16[2,160,2048]{2,1,0:T(8,128)(2,1)S(1)}, bf16[2,160,2048]{2,1,0:T(8,128)(2,1)}, u32[]{:S(2)}, u32[]{:S(2)}) collective-permute-start(bf16[2,160,2048]{2,1,0:T(8,128)(2,1)S(1)} %bitcast.60), channel_id=1, source_target_pairs={{8,0},{12,4},{16,8},{20,12},{24,16},{28,20},{9,1},{13,5},{17,9},{2... | collective-permute-start | bytes 3932168 | tf_op jit(solution)/shard_map/ppermute | solution.py:37
  66.0 35.3 %copy-start.3 = (bf16[2,160,2048]{2,0,1:T(2,128)(2,1)S(1)}, bf16[2,160,2048]{2,0,1:T(2,128)(2,1)}, u32[]{:S(2)}) copy-start(bf16[2,160,2048]{2,0,1:T(2,128)(2,1)} %copy-done.2) | copy-start | bytes 3932164
  93.8 49.4 %collective-permute-start.11 = (bf16[2,160,2048]{2,1,0:T(8,128)(2,1)}, bf16[2,160,2048]{2,1,0:T(8,128)(2,1)}, u32[]{:S(2)}, u32[]{:S(2)}) collective-permute-start(bf16[2,160,2048]{2,1,0:T(8,128)(2,1)} %broadcast_select_fusion), channel_id=1, source_target_pairs={{0,4},{4,0},{8,12},{12,8},{16,20},{20,16},{24,28},{28,24},{1,5},{5... | collective-permute-start | bytes 3932168 | tf_op jit(solution)/shard_map/ppermute | solution.py:42
  95.7 60.2 %collective-permute-start.6 = (bf16[2,160,2048]{2,1,0:T(8,128)(2,1)}, bf16[2,160,2048]{2,1,0:T(8,128)(2,1)}, u32[]{:S(2)}, u32[]{:S(2)}) collective-permute-start(bf16[2,160,2048]{2,1,0:T(8,128)(2,1)} %collective-permute-done.5.second_ref), channel_id=1, source_target_pairs={{0,8},{4,12},{8,16},{12,20},{16,24},{20,28},{1,9},{5,13},{9,17},{1... | collective-permute-start | bytes 3932168 | tf_op jit(solution)/shard_map/ppermute | solution.py:37
  104.1 7.1 %copy-start.16 = (s32[1,4]{1,0:T(1,128)S(1)}, s32[1,4]{1,0:T(1,128)}, u32[]{:S(2)}) copy-start(s32[1,4]{1,0:T(1,128)} %param.11) | copy-start | bytes 52
  104.1 57.3 %collective-permute-start.8 = (bf16[2,160,2048]{2,1,0:T(8,128)(2,1)S(1)}, bf16[2,160,2048]{2,1,0:T(8,128)(2,1)S(1)}, u32[]{:S(2)}, u32[]{:S(2)}) collective-permute-start(bf16[2,160,2048]{2,1,0:T(8,128)(2,1)S(1)} %broadcast_select_fusion.1), channel_id=1, source_target_pairs={{0,4},{4,0},{8,12},{12,8},{16,20},{20,16},{24,28},{28,24},{1,5},{5... | collective-permute-start | bytes 3932168 | tf_op jit(solution)/shard_map/ppermute | solution.py:42
  104.2 65.6 %collective-permute-start.3 = (bf16[2,160,2048]{2,1,0:T(8,128)(2,1)}, bf16[2,160,2048]{2,1,0:T(8,128)(2,1)}, u32[]{:S(2)}, u32[]{:S(2)}) collective-permute-start(bf16[2,160,2048]{2,1,0:T(8,128)(2,1)} %collective-permute-done.2.second_ref), channel_id=1, source_target_pairs={{8,0},{12,4},{16,8},{20,12},{24,16},{28,20},{9,1},{13,5},{17,9},{2... | collective-permute-start | bytes 3932168 | tf_op jit(solution)/shard_map/ppermute | solution.py:37
  109.9 27.5 %collective-permute-start.15 = (f32[2,8,512]{2,1,0:T(8,128)}, f32[2,8,512]{2,1,0:T(8,128)S(1)}, u32[]{:S(2)}, u32[]{:S(2)}) collective-permute-start(f32[2,8,512]{2,1,0:T(8,128)} %shard_map.70), channel_id=1, source_target_pairs={{8,0},{12,4},{16,8},{20,12},{24,16},{28,20},{9,1},{13,5},{17,9},{2... | collective-permute-start | bytes 98312 | tf_op jit(solution)/shard_map/ppermute | solution.py:37
  137.4 5.7 %collective-permute-start.14 = (f32[2,8,512]{2,1,0:T(8,128)}, f32[2,8,512]{2,1,0:T(8,128)S(1)}, u32[]{:S(2)}, u32[]{:S(2)}) collective-permute-start(f32[2,8,512]{2,1,0:T(8,128)} %shard_map.69), channel_id=1, source_target_pairs={{0,8},{4,12},{8,16},{12,20},{16,24},{20,28},{1,9},{5,13},{9,17},{1... | collective-permute-start | bytes 98312 | tf_op jit(solution)/shard_map/ppermute | solution.py:37
  147.5 32.1 %collective-permute-start.17 = (f32[2,8,512]{2,1,0:T(8,128)}, f32[2,8,512]{2,1,0:T(8,128)S(1)}, u32[]{:S(2)}, u32[]{:S(2)}) collective-permute-start(f32[2,8,512]{2,1,0:T(8,128)} %shard_map.72), channel_id=1, source_target_pairs={{4,0},{8,4},{12,8},{16,12},{20,16},{24,20},{28,24},{5,1},{9,5},{13... | collective-permute-start | bytes 98312 | tf_op jit(solution)/shard_map/ppermute | solution.py:37
  148.8 33.2 %collective-permute-start.12 = (bf16[2,160,2048]{2,1,0:T(8,128)(2,1)}, bf16[2,160,2048]{2,1,0:T(8,128)(2,1)}, u32[]{:S(2)}, u32[]{:S(2)}) collective-permute-start(bf16[2,160,2048]{2,1,0:T(8,128)(2,1)} %collective-permute-done.11.second_ref), channel_id=1, source_target_pairs={{0,8},{4,12},{8,16},{12,20},{16,24},{20,28},{1,9},{5,13},{9,17},{1... | collective-permute-start | bytes 3932168 | tf_op jit(solution)/shard_map/ppermute | solution.py:37
  160.2 20.8 %collective-permute-start.7 = (f32[2,8,512]{2,1,0:T(8,128)}, f32[2,8,512]{2,1,0:T(8,128)S(1)}, u32[]{:S(2)}, u32[]{:S(2)}) collective-permute-start(f32[2,8,512]{2,1,0:T(8,128)} %shard_map.66), channel_id=1, source_target_pairs={{16,0},{20,4},{24,8},{28,12},{17,1},{21,5},{25,9},{29,13},{18,2},{... | collective-permute-start | bytes 98312 | tf_op jit(solution)/shard_map/ppermute | solution.py:37
  161.5 1.1 copy-start.5
  167.0 12.6 %copy-start.6 = (bf16[2,160,2048]{2,1,0:T(8,128)(2,1)S(1)}, bf16[2,160,2048]{2,1,0:T(8,128)(2,1)}, u32[]{:S(2)}) copy-start(bf16[2,160,2048]{2,1,0:T(8,128)(2,1)} %copy-done.5) | copy-start | bytes 3932164
  167.0 14.0 %collective-permute-start.16 = (f32[2,8,512]{2,1,0:T(8,128)}, f32[2,8,512]{2,1,0:T(8,128)S(1)}, u32[]{:S(2)}, u32[]{:S(2)}) collective-permute-start(f32[2,8,512]{2,1,0:T(8,128)} %shard_map.71), channel_id=1, source_target_pairs={{0,4},{4,8},{8,12},{12,16},{16,20},{20,24},{24,28},{1,5},{5,9},{9,... | collective-permute-start | bytes 98312 | tf_op jit(solution)/shard_map/ppermute | solution.py:37
  174.2 7.8 %collective-permute-start.4 = (f32[2,8,512]{2,1,0:T(8,128)}, f32[2,8,512]{2,1,0:T(8,128)S(1)}, u32[]{:S(2)}, u32[]{:S(2)}) collective-permute-start(f32[2,8,512]{2,1,0:T(8,128)} %shard_map.65), channel_id=1, source_target_pairs={{0,16},{4,20},{8,24},{12,28},{1,17},{5,21},{9,25},{13,29},{2,18},{... | collective-permute-start | bytes 98312 | tf_op jit(solution)/shard_map/ppermute | solution.py:37
  179.6 30.1 %collective-permute-start.9 = (bf16[2,160,2048]{2,1,0:T(8,128)(2,1)S(1)}, bf16[2,160,2048]{2,1,0:T(8,128)(2,1)S(1)}, u32[]{:S(2)}, u32[]{:S(2)}) collective-permute-start(bf16[2,160,2048]{2,1,0:T(8,128)(2,1)S(1)} %copy-done.6), channel_id=1, source_target_pairs={{8,0},{12,4},{16,8},{20,12},{24,16},{28,20},{9,1},{13,5},{17,9},{2... | collective-permute-start | bytes 3932168 | tf_op jit(solution)/shard_map/ppermute | solution.py:37
  186.3 31.4 %collective-permute-start.13 = (f32[2,8,512]{2,1,0:T(8,128)}, f32[2,8,512]{2,1,0:T(8,128)S(1)}, u32[]{:S(2)}, u32[]{:S(2)}) collective-permute-start(f32[2,8,512]{2,1,0:T(8,128)} %shard_map.68), channel_id=1, source_target_pairs={{12,0},{16,4},{20,8},{24,12},{28,16},{13,1},{17,5},{21,9},{25,13},... | collective-permute-start | bytes 98312 | tf_op jit(solution)/shard_map/ppermute | solution.py:37
  187.6 32.0 %copy-start.8 = (f32[2,8,512]{2,1,0:T(8,128)S(1)}, f32[2,8,512]{2,1,0:T(8,128)}, u32[]{:S(2)}) copy-start(f32[2,8,512]{2,1,0:T(8,128)} %shard_map.70) | copy-start | bytes 98308
  187.6 32.0 %copy-start.9 = (f32[2,8,512]{2,1,0:T(8,128)S(1)}, f32[2,8,512]{2,1,0:T(8,128)}, u32[]{:S(2)}) copy-start(f32[2,8,512]{2,1,0:T(8,128)} %shard_map.69) | copy-start | bytes 98308
  187.7 32.0 %copy-start.10 = (f32[2,8,512]{2,1,0:T(8,128)S(1)}, f32[2,8,512]{2,1,0:T(8,128)}, u32[]{:S(2)}) copy-start(f32[2,8,512]{2,1,0:T(8,128)} %shard_map.72) | copy-start | bytes 98308
  187.7 32.0 %copy-start.11 = (f32[2,8,512]{2,1,0:T(8,128)S(1)}, f32[2,8,512]{2,1,0:T(8,128)}, u32[]{:S(2)}) copy-start(f32[2,8,512]{2,1,0:T(8,128)} %shard_map.66) | copy-start | bytes 98308
  187.7 32.0 %copy-start.12 = (f32[2,8,512]{2,1,0:T(8,128)S(1)}, f32[2,8,512]{2,1,0:T(8,128)}, u32[]{:S(2)}) copy-start(f32[2,8,512]{2,1,0:T(8,128)} %shard_map.71) | copy-start | bytes 98308
  187.7 32.0 %copy-start.13 = (f32[2,8,512]{2,1,0:T(8,128)S(1)}, f32[2,8,512]{2,1,0:T(8,128)}, u32[]{:S(2)}) copy-start(f32[2,8,512]{2,1,0:T(8,128)} %shard_map.65) | copy-start | bytes 98308
  187.7 32.0 %copy-start.14 = (f32[2,8,512]{2,1,0:T(8,128)S(1)}, f32[2,8,512]{2,1,0:T(8,128)}, u32[]{:S(2)}) copy-start(f32[2,8,512]{2,1,0:T(8,128)} %shard_map.68) | copy-start | bytes 98308
  209.7 1.1 copy-start.7
  215.1 6.2 %copy-start.15 = (f32[2,8,512]{2,1,0:T(8,128)S(1)}, f32[2,8,512]{2,1,0:T(8,128)}, u32[]{:S(2)}) copy-start(f32[2,8,512]{2,1,0:T(8,128)} %shard_map.67) | copy-start | bytes 98308
  215.1 4.5 %collective-permute-start.10 = (f32[2,8,512]{2,1,0:T(8,128)}, f32[2,8,512]{2,1,0:T(8,128)S(1)}, u32[]{:S(2)}, u32[]{:S(2)}) collective-permute-start(f32[2,8,512]{2,1,0:T(8,128)} %shard_map.67), channel_id=1, source_target_pairs={{0,12},{4,16},{8,20},{12,24},{16,28},{1,13},{5,17},{9,21},{13,25},... | collective-permute-start | bytes 98312 | tf_op jit(solution)/shard_map/ppermute | solution.py:37

commit v8 on v7

--- a/solution.py
+++ b/solution.py
@@ -173,18 +173,11 @@
     right_4 = shifted(right_2, "date", -2)
     right_3 = shifted(right_1, "date", -2)
 
-    ahead = {
-        1: looks(own_left, left_1),
-        2: looks(own_left, left_2),
-        3: looks(own_left, left_3),
-        4: looks(own_left, left_4),
-    }
-    behind = {
-        1: looks(own_right, right_1),
-        2: looks(own_right, right_2),
-        3: looks(own_right, right_3),
-        4: looks(own_right, right_4),
-    }
+    ahead = {s: looks(own_left, other) for s, other in ((2, left_2), (1, left_1), (4, left_4))}
+    behind = {s: looks(own_right, other) for s, other in ((2, right_2), (1, right_1), (4, right_4))}
+    ahead, behind, left_3, right_3 = lax.optimization_barrier((ahead, behind, left_3, right_3))
+    ahead[3] = looks(own_left, left_3)
+    behind[3] = looks(own_right, right_3)
     full = {}
     for s in range(1, GAP + 1):
         right_of_ahead = conj(shifted(behind[s], "date", s))

time: 224 us -> 248 us (1.11)
  waiting for transfers between devices: 52 us -> 74.6 us
  starting transfers between devices: 48.9 us -> 56.2 us
  other arithmetic: 18.6 us -> 15.9 us
    ppermute x2, waiting for transfers between devices: 0.01 us -> 44.1 us  [swapped(): return lax.ppermute(block, axis, [(i, i ^ 1) for i in range(count)])]
    ppermute x14, waiting for transfers between devices: 52 us -> 30.4 us  [shifted(): return lax.ppermute(block, axis, route)]
    ppermute x14, starting transfers between devices: 42.6 us -> 47.8 us  [shifted(): return lax.ppermute(block, axis, route)]
    ppermute x2, starting transfers between devices: 1.98 us -> 4.71 us  [swapped(): return lax.ppermute(block, axis, [(i, i ^ 1) for i in range(count)])]
  transfers between devices with their start and end apart: 18 -> 18, of which waited for: 6 -> 6; matrix products, arithmetic and copies ran while one was open for 7% -> 5% of each run, Pallas kernels for 16% -> 14%
where the time goes in v8:
time: 248 us; the launch traced here: 246 us
  waiting for transfers between devices  74.6 us (30%)
  Pallas kernels  68.1 us (27%)
  starting transfers between devices  56.2 us (23%)
  between operations  20.9 us (8%)
  other arithmetic  15.9 us (6%)
  local copies, waits for them, and re-layouts  10.9 us (4%)
    ppermute x14, starting transfers between devices, shifted(): return lax.ppermute(block, axis, route)  47.8 us
    ppermute x2, waiting for transfers between devices, swapped(): return lax.ppermute(block, axis, [(i, i ^ 1) for i in range(count)])  44.1 us
    pallas_call x8, Pallas kernels, looks(): pl.pallas_call(looks_kernel, grid=(width // CHUNK,), in_specs=[spec, spec...  35 us
    pallas_call x1, Pallas kernels, resample_block(): pl.pallas_call(resample_kernel, grid=(2, nlines // ROWS), in_specs=[pl.Bl...  33.2 us
    ppermute x14, waiting for transfers between devices, shifted(): return lax.ppermute(block, axis, route)  30.4 us
  transfers between devices with their start and end apart: 18, of which 6 were waited for; matrix products, arithmetic and copies ran while one was open for 5% of the time, Pallas kernels for 14%

profile of v8, /device:TPU:0, one launch (start us, length us, event | category | flops | bytes accessed | tf_op | source)
XLA Modules:
  0.0 246.4 jit_solution(1905594109896708450)
XLA Ops:
  0.0 1.1 fusion.31
  1.1 2.4 collective-permute-start
  3.4 1.3 collective-permute-start.1
  4.8 0.7 compare_select_fusion
  5.5 0.7 compare_and_fusion
  6.1 0.7 add_bitcast_fusion
  6.8 0.1 fusion.8
  7.6 0.1 copy.20
  7.7 0.7 dynamic-slice_reduce_fusion.weights_ref
  9.1 0.7 copy.21.shift_ref
  9.8 0.7 gather_fusion
  10.5 0.7 broadcast_select_fusion.2.coeff_ref
  11.2 0.0 collective-permute-done
  11.2 3.5 %fusion.2 = bf16[2,167,4096]{2,1,0:T(8,128)(2,1)S(1)} fusion(s32[]{:T(128)S(6)} %select_n.502, bf16[1,2,16,4096]{3,2,1,0:T(8,128)(2,1)S(1)} %collective-permute-done, bf16[1,2,160,4096]{3,2,1,0:T(8,128)(2,1)} %param.6, bf16[1,2,16,4096]{3,2,1,0:T(8,128)(2,1)S(1)} %collective-permute-done.1), kind=kLoop, calls=%fused_computation.6 | loop fusion | flops 8208384 | bytes 5881860 | tf_op jit(solution)/shard_map/convert_element_type | solution.py:86
  14.7 3.1 %pad_convert_fusion.window_ref = f32[2,168,4096]{2,1,0:T(8,128)} fusion(bf16[2,167,4096]{2,1,0:T(8,128)(2,1)S(1)} %fusion.2), kind=kLoop, calls=%fused_computation.7 | loop fusion | flops 1376256 | bytes 8241152 | tf_op jit(solution)/shard_map/jit(_pad)/pad | solution.py:87
  17.7 33.2 %shard_map.64 = bf16[2,160,4096]{2,1,0:T(8,128)(2,1)} custom-call(f32[8]{0:T(128)} %dynamic-slice_reduce_fusion.weights_ref, f32[2,168,4096]{2,1,0:T(8,128)} %pad_convert_fusion.window_ref, f32[160,8]{1,0:T(8,128)} %broadcast_select_fusion.2.coeff_ref, s32[160,1]{1,0:T(8,128)} %copy.21.shift_ref), custom_call_target="tpu_custom_call" | custom-call | flops 78643200 | bytes 7864320 | tf_op jit(solution)/shard_map/pallas_call | solution.py:91
  50.9 2.0 fusion.30
  52.9 1.3 copy.22
  54.3 0.7 copy.33
  55.0 0.3 copy-done.4
  55.4 1.3 collective-permute-start.2
  56.6 1.3 copy.24
  58.0 0.7 copy.32
  58.8 0.4 copy-done.2
  59.1 6.1 %collective-permute-start.5 = (bf16[2,160,2048]{2,1,0:T(8,128)(2,1)S(1)}, bf16[2,160,2048]{2,1,0:T(8,128)(2,1)}, u32[]{:S(2)}, u32[]{:S(2)}) collective-permute-start(bf16[2,160,2048]{2,1,0:T(8,128)(2,1)S(1)} %bitcast.65), channel_id=1, source_target_pairs={{0,8},{4,12},{8,16},{12,20},{16,24},{20,28},{1,9},{5,13},{9,17},{1... | collective-permute-start | bytes 3932168 | tf_op jit(solution)/shard_map/ppermute | solution.py:37
  65.2 22.3 %collective-permute-done.2.second_ref = bf16[2,160,2048]{2,1,0:T(8,128)(2,1)} collective-permute-done((bf16[2,160,2048]{2,1,0:T(8,128)(2,1)S(1)}, bf16[2,160,2048]{2,1,0:T(8,128)(2,1)}, u32[]{:S(2)}, u32[]{:S(2)}) %collective-permute-start.2) | collective-permute-done | bytes 1310752 | tf_op jit(solution)/shard_map/ppermute | solution.py:37
  87.5 3.2 %broadcast_select_fusion.1 = bf16[2,160,2048]{2,1,0:T(8,128)(2,1)S(1)} fusion(bf16[2,160,2048]{2,1,0:T(8,128)(2,1)} %collective-permute-done.2.second_ref, pred[]{:T(512)S(6)} %eq.128, bf16[2,20,8,2048]{3,0,1,2:T(2,128)(2,1)} %bitcast.73), kind=kLoop, calls=%fused_computation.11 | loop fusion | flops 655360 | bytes 3932161 | tf_op jit(solution)/shard_map/jit(_where)/select_n | solution.py:168
  90.7 2.0 collective-permute-start.3
  92.8 0.0 collective-permute-done.5.second_ref
  92.8 1.5 broadcast_select_fusion
  94.3 2.7 %collective-permute-start.6 = (bf16[2,160,2048]{2,1,0:T(8,128)(2,1)S(1)}, bf16[2,160,2048]{2,1,0:T(8,128)(2,1)}, u32[]{:S(2)}, u32[]{:S(2)}) collective-permute-start(bf16[2,160,2048]{2,1,0:T(8,128)(2,1)S(1)} %broadcast_select_fusion), channel_id=1, source_target_pairs={{0,4},{4,0},{8,12},{12,8},{16,20},{20,16},{24,28},{28,24},{1,5},{5... | collective-permute-start | bytes 3932168 | tf_op jit(solution)/shard_map/ppermute | solution.py:42
  97.0 1.3 collective-permute-start.4
  98.2 6.3 %collective-permute-start.7 = (bf16[2,160,2048]{2,1,0:T(8,128)(2,1)}, bf16[2,160,2048]{2,1,0:T(8,128)(2,1)}, u32[]{:S(2)}, u32[]{:S(2)}) collective-permute-start(bf16[2,160,2048]{2,1,0:T(8,128)(2,1)} %collective-permute-done.5.second_ref), channel_id=1, source_target_pairs={{0,8},{4,12},{8,16},{12,20},{16,24},{20,28},{1,9},{5,13},{9,17},{1... | collective-permute-start | bytes 3932168 | tf_op jit(solution)/shard_map/ppermute | solution.py:37
  104.5 17.3 %collective-permute-done.3.second_ref = bf16[2,160,2048]{2,1,0:T(8,128)(2,1)} collective-permute-done((bf16[2,160,2048]{2,1,0:T(8,128)(2,1)S(1)}, bf16[2,160,2048]{2,1,0:T(8,128)(2,1)}, u32[]{:S(2)}, u32[]{:S(2)}) %collective-permute-start.3) | collective-permute-done | bytes 1310752 | tf_op jit(solution)/shard_map/ppermute | solution.py:42
  121.8 1.3 collective-permute-start.8
  123.1 26.8 %collective-permute-done.6.second_ref = bf16[2,160,2048]{2,1,0:T(8,128)(2,1)} collective-permute-done((bf16[2,160,2048]{2,1,0:T(8,128)(2,1)S(1)}, bf16[2,160,2048]{2,1,0:T(8,128)(2,1)}, u32[]{:S(2)}, u32[]{:S(2)}) %collective-permute-start.6) | collective-permute-done | bytes 1310752 | tf_op jit(solution)/shard_map/ppermute | solution.py:42
  149.9 4.5 %collective-permute-start.9 = (bf16[2,160,2048]{2,1,0:T(8,128)(2,1)}, bf16[2,160,2048]{2,1,0:T(8,128)(2,1)S(1)}, u32[]{:S(2)}, u32[]{:S(2)}) collective-permute-start(bf16[2,160,2048]{2,1,0:T(8,128)(2,1)} %collective-permute-done.6.second_ref), channel_id=1, source_target_pairs={{0,8},{4,12},{8,16},{12,20},{16,24},{20,28},{1,9},{5,13},{9,17},{1... | collective-permute-start | bytes 3932168 | tf_op jit(solution)/shard_map/ppermute | solution.py:37
  154.5 4.4 %shard_map.66 = f32[2,8,512]{2,1,0:T(8,128)} custom-call(bf16[2,160,2048]{2,1,0:T(8,128)(2,1)} %bitcast.61, bf16[2,160,2048]{2,1,0:T(8,128)(2,1)} %collective-permute-done.2.second_ref), custom_call_target="tpu_custom_call" | custom-call | flops 13107200 | bytes 2621440 | tf_op jit(solution)/shard_map/pallas_call | solution.py:139
  158.9 4.4 %shard_map.69 = f32[2,8,512]{2,1,0:T(8,128)} custom-call(bf16[2,160,2048]{2,1,0:T(8,128)(2,1)} %bitcast.66, bf16[2,160,2048]{2,1,0:T(8,128)(2,1)} %collective-permute-done.5.second_ref), custom_call_target="tpu_custom_call" | custom-call | flops 13107200 | bytes 2621440 | tf_op jit(solution)/shard_map/pallas_call | solution.py:139
  163.2 4.4 %shard_map.65 = f32[2,8,512]{2,1,0:T(8,128)} custom-call(bf16[2,160,2048]{2,1,0:T(8,128)(2,1)} %bitcast.62, bf16[2,160,2048]{2,1,0:T(8,128)(2,1)} %collective-permute-done.3.second_ref), custom_call_target="tpu_custom_call" | custom-call | flops 13107200 | bytes 2621440 | tf_op jit(solution)/shard_map/pallas_call | solution.py:139
  167.6 4.4 %shard_map.68 = f32[2,8,512]{2,1,0:T(8,128)} custom-call(bf16[2,160,2048]{2,1,0:T(8,128)(2,1)} %bitcast.67, bf16[2,160,2048]{2,1,0:T(8,128)(2,1)} %collective-permute-done.6.second_ref), custom_call_target="tpu_custom_call" | custom-call | flops 13107200 | bytes 2621440 | tf_op jit(solution)/shard_map/pallas_call | solution.py:139
  171.9 0.0 collective-permute-done.4.second_ref
  171.9 4.4 %shard_map.67 = f32[2,8,512]{2,1,0:T(8,128)} custom-call(bf16[2,160,2048]{2,1,0:T(8,128)(2,1)} %bitcast.63, bf16[2,160,2048]{2,1,0:T(8,128)(2,1)} %collective-permute-done.4.second_ref), custom_call_target="tpu_custom_call" | custom-call | flops 13107200 | bytes 2621440 | tf_op jit(solution)/shard_map/pallas_call | solution.py:139
  176.3 0.0 collective-permute-done.7.second_ref
  176.3 4.4 %shard_map.70 = f32[2,8,512]{2,1,0:T(8,128)} custom-call(bf16[2,160,2048]{2,1,0:T(8,128)(2,1)} %bitcast.68, bf16[2,160,2048]{2,1,0:T(8,128)(2,1)} %collective-permute-done.7.second_ref), custom_call_target="tpu_custom_call" | custom-call | flops 13107200 | bytes 2621440 | tf_op jit(solution)/shard_map/pallas_call | solution.py:139
  180.8 2.7 %collective-permute-done.9.second_ref = bf16[2,160,2048]{2,1,0:T(8,128)(2,1)S(1)} collective-permute-done((bf16[2,160,2048]{2,1,0:T(8,128)(2,1)}, bf16[2,160,2048]{2,1,0:T(8,128)(2,1)S(1)}, u32[]{:S(2)}, u32[]{:S(2)}) %collective-permute-start.9) | collective-permute-done | bytes 1310752 | tf_op jit(solution)/shard_map/ppermute | solution.py:37
  183.5 3.0 %collective-permute-start.16 = (f32[2,8,512]{2,1,0:T(8,128)S(1)}, f32[2,8,512]{2,1,0:T(8,128)S(1)}, u32[]{:S(2)}, u32[]{:S(2)}) collective-permute-start(f32[2,8,512]{2,1,0:T(8,128)S(1)} %copy-done.9), channel_id=1, source_target_pairs={{0,4},{4,8},{8,12},{12,16},{16,20},{20,24},{24,28},{1,5},{5,9},{9,... | collective-permute-start | bytes 98312 | tf_op jit(solution)/shard_map/ppermute | solution.py:37
  186.5 0.7 fusion.40
  206.3 1.3 collective-permute-start.17
  207.6 6.7 %collective-permute-start.14 = (f32[2,8,512]{2,1,0:T(8,128)S(1)}, f32[2,8,512]{2,1,0:T(8,128)S(1)}, u32[]{:S(2)}, u32[]{:S(2)}) collective-permute-start(f32[2,8,512]{2,1,0:T(8,128)S(1)} %copy-done.7), channel_id=1, source_target_pairs={{0,8},{4,12},{8,16},{12,20},{16,24},{20,28},{1,9},{5,13},{9,17},{1... | collective-permute-start | bytes 98312 | tf_op jit(solution)/shard_map/ppermute | solution.py:37
  214.3 1.3 collective-permute-start.15
  215.6 4.4 %shard_map.71 = f32[2,8,512]{2,1,0:T(8,128)} custom-call(bf16[2,160,2048]{2,1,0:T(8,128)(2,1)} %bitcast.64, bf16[2,160,2048]{2,1,0:T(8,128)(2,1)} %copy-done.5), custom_call_target="tpu_custom_call" | custom-call | flops 13107200 | bytes 2621440 | tf_op jit(solution)/shard_map/pallas_call | solution.py:139
  220.0 0.0 copy-start.13
  220.0 4.3 %collective-permute-start.12 = (f32[2,8,512]{2,1,0:T(8,128)}, f32[2,8,512]{2,1,0:T(8,128)S(1)}, u32[]{:S(2)}, u32[]{:S(2)}) collective-permute-start(f32[2,8,512]{2,1,0:T(8,128)} %shard_map.71), channel_id=1, source_target_pairs={{0,12},{4,16},{8,20},{12,24},{16,28},{1,13},{5,17},{9,21},{13,25},... | collective-permute-start | bytes 98312 | tf_op jit(solution)/shard_map/ppermute | solution.py:37
  224.4 4.4 %shard_map.72 = f32[2,8,512]{2,1,0:T(8,128)} custom-call(bf16[2,160,2048]{2,1,0:T(8,128)(2,1)} %bitcast.69, bf16[2,160,2048]{2,1,0:T(8,128)(2,1)} %copy-done.6), custom_call_target="tpu_custom_call" | custom-call | flops 13107200 | bytes 2621440 | tf_op jit(solution)/shard_map/pallas_call | solution.py:139
  228.7 0.0 collective-permute-done.16
  228.7 1.4 collective-permute-start.13
  230.2 0.0 collective-permute-done.17
  230.2 7.7 %collective-permute-start.10 = (f32[2,8,512]{2,1,0:T(8,128)S(1)}, f32[2,8,512]{2,1,0:T(8,128)S(1)}, u32[]{:S(2)}, u32[]{:S(2)}) collective-permute-start(f32[2,8,512]{2,1,0:T(8,128)S(1)} %copy-done.11), channel_id=1, source_target_pairs={{0,16},{4,20},{8,24},{12,28},{1,17},{5,21},{9,25},{13,29},{2,18},{... | collective-permute-start | bytes 98312 | tf_op jit(solution)/shard_map/ppermute | solution.py:37
  237.9 1.3 collective-permute-start.11
  239.4 0.1 collective-permute-done.10
  239.5 5.2 %collective-permute-done.11 = f32[2,8,512]{2,1,0:T(8,128)S(1)} collective-permute-done((f32[2,8,512]{2,1,0:T(8,128)S(1)}, f32[2,8,512]{2,1,0:T(8,128)S(1)}, u32[]{:S(2)}, u32[]{:S(2)}) %collective-permute-start.11) | collective-permute-done | bytes 32800 | tf_op jit(solution)/shard_map/ppermute | solution.py:37
  244.7 0.8 select_select_fusion
  245.7 0.7 maximum_bitcast_fusion
  (53 shorter events, 0.3 us)
Async XLA Ops:
  1.1 10.1 %collective-permute-start = (bf16[1,2,16,4096]{3,2,1,0:T(8,128)(2,1)S(1)}, bf16[1,2,16,4096]{3,2,1,0:T(8,128)(2,1)S(1)}, u32[]{:S(2)}, u32[]{:S(2)}) collective-permute-start(bf16[1,2,16,4096]{3,2,1,0:T(8,128)(2,1)S(1)} %get-tuple-element.24), channel_id=1, source_target_pairs={{0,1},{1,2},{2,3},{4,5},{5,6},{6,7},{8,9},{9,10},{10,11},{12,13},{... | collective-permute-start | bytes 786440 | tf_op jit(solution)/shard_map/ppermute | solution.py:25
  3.4 7.8 %collective-permute-start.1 = (bf16[1,2,16,4096]{3,2,1,0:T(8,128)(2,1)S(1)}, bf16[1,2,16,4096]{3,2,1,0:T(8,128)(2,1)S(1)}, u32[]{:S(2)}, u32[]{:S(2)}) collective-permute-start(bf16[1,2,16,4096]{3,2,1,0:T(8,128)(2,1)S(1)} %get-tuple-element.23), channel_id=1, source_target_pairs={{1,0},{2,1},{3,2},{5,4},{6,5},{7,6},{9,8},{10,9},{11,10},{13,12},{... | collective-permute-start | bytes 786440 | tf_op jit(solution)/shard_map/ppermute | solution.py:27
  54.3 1.1 copy-start.4
  55.4 2.6 %copy-start = (bf16[2,20,8,2048]{3,2,1,0:T(8,128)(2,1)}, bf16[2,20,8,2048]{3,2,1,0:T(8,128)(2,1)S(1)}, u32[]{:S(2)}) copy-start(bf16[2,20,8,2048]{3,2,1,0:T(8,128)(2,1)S(1)} %copy.33) | copy-start | bytes 3932164
  55.4 32.2 %collective-permute-start.2 = (bf16[2,160,2048]{2,1,0:T(8,128)(2,1)S(1)}, bf16[2,160,2048]{2,1,0:T(8,128)(2,1)}, u32[]{:S(2)}, u32[]{:S(2)}) collective-permute-start(bf16[2,160,2048]{2,1,0:T(8,128)(2,1)S(1)} %bitcast.60), channel_id=1, source_target_pairs={{8,0},{12,4},{16,8},{20,12},{24,16},{28,20},{9,1},{13,5},{17,9},{2... | collective-permute-start | bytes 3932168 | tf_op jit(solution)/shard_map/ppermute | solution.py:37
  58.0 1.1 copy-start.2
  59.1 31.6 %copy-start.1 = (bf16[2,20,8,2048]{3,2,1,0:T(8,128)(2,1)}, bf16[2,20,8,2048]{3,2,1,0:T(8,128)(2,1)S(1)}, u32[]{:S(2)}) copy-start(bf16[2,20,8,2048]{3,2,1,0:T(8,128)(2,1)S(1)} %copy.32) | copy-start | bytes 3932164
  59.1 33.6 %collective-permute-start.5 = (bf16[2,160,2048]{2,1,0:T(8,128)(2,1)S(1)}, bf16[2,160,2048]{2,1,0:T(8,128)(2,1)}, u32[]{:S(2)}, u32[]{:S(2)}) collective-permute-start(bf16[2,160,2048]{2,1,0:T(8,128)(2,1)S(1)} %bitcast.65), channel_id=1, source_target_pairs={{0,8},{4,12},{8,16},{12,20},{16,24},{20,28},{1,9},{5,13},{9,17},{1... | collective-permute-start | bytes 3932168 | tf_op jit(solution)/shard_map/ppermute | solution.py:37
  65.2 27.6 %copy-start.3 = (bf16[2,160,2048]{2,0,1:T(2,128)(2,1)S(1)}, bf16[2,160,2048]{2,0,1:T(2,128)(2,1)}, u32[]{:S(2)}) copy-start(bf16[2,160,2048]{2,0,1:T(2,128)(2,1)} %copy-done.2) | copy-start | bytes 3932164
  90.7 31.1 %collective-permute-start.3 = (bf16[2,160,2048]{2,1,0:T(8,128)(2,1)S(1)}, bf16[2,160,2048]{2,1,0:T(8,128)(2,1)}, u32[]{:S(2)}, u32[]{:S(2)}) collective-permute-start(bf16[2,160,2048]{2,1,0:T(8,128)(2,1)S(1)} %broadcast_select_fusion.1), channel_id=1, source_target_pairs={{0,4},{4,0},{8,12},{12,8},{16,20},{20,16},{24,28},{28,24},{1,5},{5... | collective-permute-start | bytes 3932168 | tf_op jit(solution)/shard_map/ppermute | solution.py:42
  94.3 55.6 %collective-permute-start.6 = (bf16[2,160,2048]{2,1,0:T(8,128)(2,1)S(1)}, bf16[2,160,2048]{2,1,0:T(8,128)(2,1)}, u32[]{:S(2)}, u32[]{:S(2)}) collective-permute-start(bf16[2,160,2048]{2,1,0:T(8,128)(2,1)S(1)} %broadcast_select_fusion), channel_id=1, source_target_pairs={{0,4},{4,0},{8,12},{12,8},{16,20},{20,16},{24,28},{28,24},{1,5},{5... | collective-permute-start | bytes 3932168 | tf_op jit(solution)/shard_map/ppermute | solution.py:42
  97.0 75.0 %collective-permute-start.4 = (bf16[2,160,2048]{2,1,0:T(8,128)(2,1)}, bf16[2,160,2048]{2,1,0:T(8,128)(2,1)}, u32[]{:S(2)}, u32[]{:S(2)}) collective-permute-start(bf16[2,160,2048]{2,1,0:T(8,128)(2,1)} %collective-permute-done.2.second_ref), channel_id=1, source_target_pairs={{8,0},{12,4},{16,8},{20,12},{24,16},{28,20},{9,1},{13,5},{17,9},{2... | collective-permute-start | bytes 3932168 | tf_op jit(solution)/shard_map/ppermute | solution.py:37
  98.2 78.1 %collective-permute-start.7 = (bf16[2,160,2048]{2,1,0:T(8,128)(2,1)}, bf16[2,160,2048]{2,1,0:T(8,128)(2,1)}, u32[]{:S(2)}, u32[]{:S(2)}) collective-permute-start(bf16[2,160,2048]{2,1,0:T(8,128)(2,1)} %collective-permute-done.5.second_ref), channel_id=1, source_target_pairs={{0,8},{4,12},{8,16},{12,20},{16,24},{20,28},{1,9},{5,13},{9,17},{1... | collective-permute-start | bytes 3932168 | tf_op jit(solution)/shard_map/ppermute | solution.py:37
  121.8 58.9 %collective-permute-start.8 = (bf16[2,160,2048]{2,1,0:T(8,128)(2,1)}, bf16[2,160,2048]{2,1,0:T(8,128)(2,1)S(1)}, u32[]{:S(2)}, u32[]{:S(2)}) collective-permute-start(bf16[2,160,2048]{2,1,0:T(8,128)(2,1)} %collective-permute-done.3.second_ref), channel_id=1, source_target_pairs={{8,0},{12,4},{16,8},{20,12},{24,16},{28,20},{9,1},{13,5},{17,9},{2... | collective-permute-start | bytes 3932168 | tf_op jit(solution)/shard_map/ppermute | solution.py:37
  149.9 33.5 %collective-permute-start.9 = (bf16[2,160,2048]{2,1,0:T(8,128)(2,1)}, bf16[2,160,2048]{2,1,0:T(8,128)(2,1)S(1)}, u32[]{:S(2)}, u32[]{:S(2)}) collective-permute-start(bf16[2,160,2048]{2,1,0:T(8,128)(2,1)} %collective-permute-done.6.second_ref), channel_id=1, source_target_pairs={{0,8},{4,12},{8,16},{12,20},{16,24},{20,28},{1,9},{5,13},{9,17},{1... | collective-permute-start | bytes 3932168 | tf_op jit(solution)/shard_map/ppermute | solution.py:37
  176.3 7.2 %copy-start.9 = (f32[2,8,512]{2,1,0:T(8,128)S(1)}, f32[2,8,512]{2,1,0:T(8,128)}, u32[]{:S(2)}) copy-start(f32[2,8,512]{2,1,0:T(8,128)} %shard_map.65) | copy-start | bytes 98308
  176.3 10.2 %copy-start.15 = (s32[1,4]{1,0:T(1,128)S(1)}, s32[1,4]{1,0:T(1,128)}, u32[]{:S(2)}) copy-start(s32[1,4]{1,0:T(1,128)} %param.11) | copy-start | bytes 52
  176.3 30.0 %copy-start.10 = (f32[2,8,512]{2,1,0:T(8,128)S(1)}, f32[2,8,512]{2,1,0:T(8,128)}, u32[]{:S(2)}) copy-start(f32[2,8,512]{2,1,0:T(8,128)} %shard_map.68) | copy-start | bytes 98308
  176.3 31.3 %copy-start.7 = (f32[2,8,512]{2,1,0:T(8,128)S(1)}, f32[2,8,512]{2,1,0:T(8,128)}, u32[]{:S(2)}) copy-start(f32[2,8,512]{2,1,0:T(8,128)} %shard_map.66) | copy-start | bytes 98308
  176.3 38.0 %copy-start.8 = (f32[2,8,512]{2,1,0:T(8,128)S(1)}, f32[2,8,512]{2,1,0:T(8,128)}, u32[]{:S(2)}) copy-start(f32[2,8,512]{2,1,0:T(8,128)} %shard_map.69) | copy-start | bytes 98308
  180.8 34.9 %copy-start.5 = (bf16[2,160,2048]{2,1,0:T(8,128)(2,1)}, bf16[2,160,2048]{2,1,0:T(8,128)(2,1)S(1)}, u32[]{:S(2)}) copy-start(bf16[2,160,2048]{2,1,0:T(8,128)(2,1)S(1)} %collective-permute-done.8.second_ref) | copy-start | bytes 3932164
  183.5 36.5 %copy-start.6 = (bf16[2,160,2048]{2,1,0:T(8,128)(2,1)}, bf16[2,160,2048]{2,1,0:T(8,128)(2,1)S(1)}, u32[]{:S(2)}) copy-start(bf16[2,160,2048]{2,1,0:T(8,128)(2,1)S(1)} %collective-permute-done.9.second_ref) | copy-start | bytes 3932164
  183.5 45.3 %collective-permute-start.16 = (f32[2,8,512]{2,1,0:T(8,128)S(1)}, f32[2,8,512]{2,1,0:T(8,128)S(1)}, u32[]{:S(2)}, u32[]{:S(2)}) collective-permute-start(f32[2,8,512]{2,1,0:T(8,128)S(1)} %copy-done.9), channel_id=1, source_target_pairs={{0,4},{4,8},{8,12},{12,16},{16,20},{20,24},{24,28},{1,5},{5,9},{9,... | collective-permute-start | bytes 98312 | tf_op jit(solution)/shard_map/ppermute | solution.py:37
  206.3 23.9 %collective-permute-start.17 = (f32[2,8,512]{2,1,0:T(8,128)S(1)}, f32[2,8,512]{2,1,0:T(8,128)S(1)}, u32[]{:S(2)}, u32[]{:S(2)}) collective-permute-start(f32[2,8,512]{2,1,0:T(8,128)S(1)} %copy-done.10), channel_id=1, source_target_pairs={{4,0},{8,4},{12,8},{16,12},{20,16},{24,20},{28,24},{5,1},{9,5},{13... | collective-permute-start | bytes 98312 | tf_op jit(solution)/shard_map/ppermute | solution.py:37
  207.6 30.3 %collective-permute-start.14 = (f32[2,8,512]{2,1,0:T(8,128)S(1)}, f32[2,8,512]{2,1,0:T(8,128)S(1)}, u32[]{:S(2)}, u32[]{:S(2)}) collective-permute-start(f32[2,8,512]{2,1,0:T(8,128)S(1)} %copy-done.7), channel_id=1, source_target_pairs={{0,8},{4,12},{8,16},{12,20},{16,24},{20,28},{1,9},{5,13},{9,17},{1... | collective-permute-start | bytes 98312 | tf_op jit(solution)/shard_map/ppermute | solution.py:37
  214.3 24.9 %collective-permute-start.15 = (f32[2,8,512]{2,1,0:T(8,128)S(1)}, f32[2,8,512]{2,1,0:T(8,128)S(1)}, u32[]{:S(2)}, u32[]{:S(2)}) collective-permute-start(f32[2,8,512]{2,1,0:T(8,128)S(1)} %copy-done.8), channel_id=1, source_target_pairs={{8,0},{12,4},{16,8},{20,12},{24,16},{28,20},{9,1},{13,5},{17,9},{2... | collective-permute-start | bytes 98312 | tf_op jit(solution)/shard_map/ppermute | solution.py:37
  220.0 10.2 %copy-start.11 = (f32[2,8,512]{2,1,0:T(8,128)S(1)}, f32[2,8,512]{2,1,0:T(8,128)}, u32[]{:S(2)}) copy-start(f32[2,8,512]{2,1,0:T(8,128)} %shard_map.67) | copy-start | bytes 98308
  220.0 17.9 %copy-start.12 = (f32[2,8,512]{2,1,0:T(8,128)S(1)}, f32[2,8,512]{2,1,0:T(8,128)}, u32[]{:S(2)}) copy-start(f32[2,8,512]{2,1,0:T(8,128)} %shard_map.70) | copy-start | bytes 98308
  220.0 24.7 %copy-start.13 = (f32[2,8,512]{2,1,0:T(8,128)S(1)}, f32[2,8,512]{2,1,0:T(8,128)}, u32[]{:S(2)}) copy-start(f32[2,8,512]{2,1,0:T(8,128)} %shard_map.71) | copy-start | bytes 98308
  220.0 19.3 %collective-permute-start.12 = (f32[2,8,512]{2,1,0:T(8,128)}, f32[2,8,512]{2,1,0:T(8,128)S(1)}, u32[]{:S(2)}, u32[]{:S(2)}) collective-permute-start(f32[2,8,512]{2,1,0:T(8,128)} %shard_map.71), channel_id=1, source_target_pairs={{0,12},{4,16},{8,20},{12,24},{16,28},{1,13},{5,17},{9,21},{13,25},... | collective-permute-start | bytes 98312 | tf_op jit(solution)/shard_map/ppermute | solution.py:37
  228.7 16.8 %copy-start.14 = (f32[2,8,512]{2,1,0:T(8,128)S(1)}, f32[2,8,512]{2,1,0:T(8,128)}, u32[]{:S(2)}) copy-start(f32[2,8,512]{2,1,0:T(8,128)} %shard_map.72) | copy-start | bytes 98308
  228.7 10.6 %collective-permute-start.13 = (f32[2,8,512]{2,1,0:T(8,128)}, f32[2,8,512]{2,1,0:T(8,128)S(1)}, u32[]{:S(2)}, u32[]{:S(2)}) collective-permute-start(f32[2,8,512]{2,1,0:T(8,128)} %shard_map.72), channel_id=1, source_target_pairs={{12,0},{16,4},{20,8},{24,12},{28,16},{13,1},{17,5},{21,9},{25,13},... | collective-permute-start | bytes 98312 | tf_op jit(solution)/shard_map/ppermute | solution.py:37
  230.2 9.3 %collective-permute-start.10 = (f32[2,8,512]{2,1,0:T(8,128)S(1)}, f32[2,8,512]{2,1,0:T(8,128)S(1)}, u32[]{:S(2)}, u32[]{:S(2)}) collective-permute-start(f32[2,8,512]{2,1,0:T(8,128)S(1)} %copy-done.11), channel_id=1, source_target_pairs={{0,16},{4,20},{8,24},{12,28},{1,17},{5,21},{9,25},{13,29},{2,18},{... | collective-permute-start | bytes 98312 | tf_op jit(solution)/shard_map/ppermute | solution.py:37
  237.9 6.8 %collective-permute-start.11 = (f32[2,8,512]{2,1,0:T(8,128)S(1)}, f32[2,8,512]{2,1,0:T(8,128)S(1)}, u32[]{:S(2)}, u32[]{:S(2)}) collective-permute-start(f32[2,8,512]{2,1,0:T(8,128)S(1)} %copy-done.12), channel_id=1, source_target_pairs={{16,0},{20,4},{24,8},{28,12},{17,1},{21,5},{25,9},{29,13},{18,2},{... | collective-permute-start | bytes 98312 | tf_op jit(solution)/shard_map/ppermute | solution.py:37

commit v9 on v7

--- a/solution.py
+++ b/solution.py
@@ -185,10 +185,17 @@
         3: looks(own_right, right_3),
         4: looks(own_right, right_4),
     }
+    count = lax.axis_size("date")
+    target = lax.broadcasted_iota(jnp.int32, (count, 1, 1, 1), 0) - date
+    sent = jnp.zeros((count,) + ahead[1].shape, jnp.float32)
+    for s in range(1, GAP + 1):
+        sent = jnp.where(target == s, ahead[s][None], sent)
+        sent = jnp.where(target == -s, behind[s][None], sent)
+    got = lax.all_to_all(sent, "date", 0, 0, tiled=True)
     full = {}
     for s in range(1, GAP + 1):
-        right_of_ahead = conj(shifted(behind[s], "date", s))
-        left_of_behind = conj(shifted(ahead[s], "date", -s))
+        right_of_ahead = conj(lax.dynamic_index_in_dim(got, jnp.minimum(date + s, count - 1), 0, keepdims=False))
+        left_of_behind = conj(lax.dynamic_index_in_dim(got, jnp.maximum(date - s, 0), 0, keepdims=False))
         full[s] = jnp.concatenate([ahead[s], right_of_ahead], axis=2)
         full[-s] = jnp.concatenate([left_of_behind, behind[s]], axis=2)
 

time: 224 us -> 221 us (0.987)
  waiting for transfers between devices: 52 us -> 68.3 us
  starting transfers between devices: 48.9 us -> 34.1 us
    ppermute x2, waiting for transfers between devices: 0.01 us -> 44.5 us  [swapped(): return lax.ppermute(block, axis, [(i, i ^ 1) for i in range(count)])]
    ppermute x14 -> x6, waiting for transfers between devices: 52 us -> 23.8 us  [shifted(): return lax.ppermute(block, axis, route)]
    ppermute x14 -> x6, starting transfers between devices: 42.6 us -> 22.1 us  [shifted(): return lax.ppermute(block, axis, route)]
    all_to_all x0 -> x1, starting transfers between devices: none -> 3.41 us  [shards(): got = lax.all_to_all(sent, 'date', 0, 0, tiled=True)]
    select_n x1, other arithmetic: 3.82 us -> 1.51 us  [shards(): right_1 = swapped(jnp.where(even, own_right, right_2), 'date')]
    ppermute x2, starting transfers between devices: 1.98 us -> 4.24 us  [swapped(): return lax.ppermute(block, axis, [(i, i ^ 1) for i in range(count)])]
  transfers between devices with their start and end apart: 18 -> 11, of which waited for: 6 -> 3; matrix products, arithmetic and copies ran while one was open for 7% -> 6% of each run, Pallas kernels for 16% -> 14%
where the time goes in v9:
time: 221 us; the launch traced here: 220 us
  waiting for transfers between devices  68.3 us (31%)
  Pallas kernels  68.1 us (31%)
  starting transfers between devices  34.1 us (15%)
  between operations  21.5 us (10%)
  other arithmetic  16.8 us (8%)
  local copies, waits for them, and re-layouts  10.8 us (5%)
    ppermute x2, waiting for transfers between devices, swapped(): return lax.ppermute(block, axis, [(i, i ^ 1) for i in range(count)])  44.5 us
    pallas_call x8, Pallas kernels, looks(): pl.pallas_call(looks_kernel, grid=(width // CHUNK,), in_specs=[spec, spec...  35 us
    pallas_call x1, Pallas kernels, resample_block(): pl.pallas_call(resample_kernel, grid=(2, nlines // ROWS), in_specs=[pl.Bl...  33.2 us
    ppermute x6, waiting for transfers between devices, shifted(): return lax.ppermute(block, axis, route)  23.8 us
    ppermute x6, starting transfers between devices, shifted(): return lax.ppermute(block, axis, route)  22.1 us
    slice x3, local copies, waits for them, and re-layouts, resample_block(): return (look_order(out[:, :, :half]), look_order(out[:, :, half:]))  4.72 us
  transfers between devices with their start and end apart: 11, of which 3 were waited for; matrix products, arithmetic and copies ran while one was open for 6% of the time, Pallas kernels for 14%

profile of v9, /device:TPU:0, one launch (start us, length us, event | category | flops | bytes accessed | tf_op | source)
XLA Modules:
  0.0 219.6 jit_solution(14108837953866125984)
XLA Ops:
  0.0 1.1 fusion.48
  1.1 1.3 collective-permute-start.1
  2.4 3.0 %collective-permute-start = (bf16[1,2,16,4096]{3,2,1,0:T(8,128)(2,1)S(1)}, bf16[1,2,16,4096]{3,2,1,0:T(8,128)(2,1)S(1)}, u32[]{:S(2)}, u32[]{:S(2)}) collective-permute-start(bf16[1,2,16,4096]{3,2,1,0:T(8,128)(2,1)S(1)} %get-tuple-element.8), channel_id=1, source_target_pairs={{0,1},{1,2},{2,3},{4,5},{5,6},{6,7},{8,9},{9,10},{10,11},{12,13},{... | collective-permute-start | bytes 786440 | tf_op jit(solution)/shard_map/ppermute | solution.py:25
  5.4 0.7 compare_select_fusion
  6.1 0.7 compare_and_fusion
  6.8 0.7 add_bitcast_fusion
  7.5 0.1 fusion.17
  8.9 0.1 copy.20
  9.0 0.7 fusion.14.weights_ref
  9.7 0.7 copy.21.shift_ref
  10.4 0.7 gather_fusion
  11.1 0.7 broadcast_select_fusion.2.coeff_ref
  11.8 0.0 collective-permute-done.1
  11.8 0.0 collective-permute-done
  11.8 3.5 %fusion.2 = bf16[2,167,4096]{2,1,0:T(8,128)(2,1)S(1)} fusion(s32[]{:T(128)S(6)} %select_n.544, bf16[1,2,16,4096]{3,2,1,0:T(8,128)(2,1)S(1)} %collective-permute-done, bf16[1,2,160,4096]{3,2,1,0:T(8,128)(2,1)} %param.6, bf16[1,2,16,4096]{3,2,1,0:T(8,128)(2,1)S(1)} %collective-permute-done.1), kind=kLoop, calls=%fused_computation.6 | loop fusion | flops 8208384 | bytes 5881860 | tf_op jit(solution)/shard_map/convert_element_type | solution.py:86
  15.3 3.1 %pad_convert_fusion.window_ref = f32[2,168,4096]{2,1,0:T(8,128)} fusion(bf16[2,167,4096]{2,1,0:T(8,128)(2,1)S(1)} %fusion.2), kind=kLoop, calls=%fused_computation.7 | loop fusion | flops 1376256 | bytes 8241152 | tf_op jit(solution)/shard_map/jit(_pad)/pad | solution.py:87
  18.4 33.2 %shard_map.64 = bf16[2,160,4096]{2,1,0:T(8,128)(2,1)} custom-call(f32[8]{0:T(128)} %fusion.14.weights_ref, f32[2,168,4096]{2,1,0:T(8,128)} %pad_convert_fusion.window_ref, f32[160,8]{1,0:T(8,128)} %broadcast_select_fusion.2.coeff_ref, s32[160,1]{1,0:T(8,128)} %copy.21.shift_ref), custom_call_target="tpu_custom_call" | custom-call | flops 78643200 | bytes 7864320 | tf_op jit(solution)/shard_map/pallas_call | solution.py:91
  51.5 2.0 fusion.47
  53.6 1.3 copy.24
  54.9 0.0 copy-start.4
  54.9 0.7 copy.32
  55.7 0.3 copy-done.4
  56.0 1.3 collective-permute-start.4
  57.3 1.3 copy.22
  58.6 0.0 copy-done
  58.7 0.0 copy-start.2
  58.7 0.7 copy.33
  59.4 0.3 copy-done.2
  59.7 6.7 %collective-permute-start.2 = (bf16[2,160,2048]{2,1,0:T(8,128)(2,1)S(1)}, bf16[2,160,2048]{2,1,0:T(8,128)(2,1)}, u32[]{:S(2)}, u32[]{:S(2)}) collective-permute-start(bf16[2,160,2048]{2,1,0:T(8,128)(2,1)S(1)} %bitcast.97), channel_id=1, source_target_pairs={{0,8},{4,12},{8,16},{12,20},{16,24},{20,28},{1,9},{5,13},{9,17},{1... | collective-permute-start | bytes 3932168 | tf_op jit(solution)/shard_map/ppermute | solution.py:37
  66.4 23.8 %collective-permute-done.4.second_ref = bf16[2,160,2048]{2,1,0:T(8,128)(2,1)} collective-permute-done((bf16[2,160,2048]{2,1,0:T(8,128)(2,1)S(1)}, bf16[2,160,2048]{2,1,0:T(8,128)(2,1)}, u32[]{:S(2)}, u32[]{:S(2)}) %collective-permute-start.4) | collective-permute-done | bytes 1310752 | tf_op jit(solution)/shard_map/ppermute | solution.py:37
  90.2 3.2 %broadcast_select_fusion = bf16[2,160,2048]{2,1,0:T(8,128)(2,1)S(1)} fusion(bf16[2,160,2048]{2,1,0:T(8,128)(2,1)} %collective-permute-done.4.second_ref, pred[]{:T(512)S(6)} %eq.195, bf16[2,20,8,2048]{3,0,1,2:T(2,128)(2,1)} %bitcast.105), kind=kLoop, calls=%fused_computation.10 | loop fusion | flops 655360 | bytes 3932161 | tf_op jit(solution)/shard_map/jit(_where)/select_n | solution.py:168
  93.4 0.0 copy-done.1
  93.4 2.0 collective-permute-start.8
  95.4 0.0 collective-permute-done.2.second_ref
  95.4 0.0 copy-done.3
  95.4 1.5 broadcast_select_fusion.1
  96.9 2.3 %collective-permute-start.6 = (bf16[2,160,2048]{2,1,0:T(8,128)(2,1)S(1)}, bf16[2,160,2048]{2,1,0:T(8,128)(2,1)S(1)}, u32[]{:S(2)}, u32[]{:S(2)}) collective-permute-start(bf16[2,160,2048]{2,1,0:T(8,128)(2,1)S(1)} %broadcast_select_fusion.1), channel_id=1, source_target_pairs={{0,4},{4,0},{8,12},{12,8},{16,20},{20,16},{24,28},{28,24},{1,5},{5... | collective-permute-start | bytes 3932168 | tf_op jit(solution)/shard_map/ppermute | solution.py:42
  99.2 1.3 collective-permute-start.5
  100.4 6.3 %collective-permute-start.3 = (bf16[2,160,2048]{2,1,0:T(8,128)(2,1)}, bf16[2,160,2048]{2,1,0:T(8,128)(2,1)}, u32[]{:S(2)}, u32[]{:S(2)}) collective-permute-start(bf16[2,160,2048]{2,1,0:T(8,128)(2,1)} %collective-permute-done.2.second_ref), channel_id=1, source_target_pairs={{0,8},{4,12},{8,16},{12,20},{16,24},{20,28},{1,9},{5,13},{9,17},{1... | collective-permute-start | bytes 3932168 | tf_op jit(solution)/shard_map/ppermute | solution.py:37
  106.7 18.4 %collective-permute-done.8.second_ref = bf16[2,160,2048]{2,1,0:T(8,128)(2,1)S(1)} collective-permute-done((bf16[2,160,2048]{2,1,0:T(8,128)(2,1)S(1)}, bf16[2,160,2048]{2,1,0:T(8,128)(2,1)S(1)}, u32[]{:S(2)}, u32[]{:S(2)}) %collective-permute-start.8) | collective-permute-done | bytes 1310752 | tf_op jit(solution)/shard_map/ppermute | solution.py:42
  125.1 1.3 collective-permute-start.9
  126.4 26.2 %collective-permute-done.6.second_ref = bf16[2,160,2048]{2,1,0:T(8,128)(2,1)S(1)} collective-permute-done((bf16[2,160,2048]{2,1,0:T(8,128)(2,1)S(1)}, bf16[2,160,2048]{2,1,0:T(8,128)(2,1)S(1)}, u32[]{:S(2)}, u32[]{:S(2)}) %collective-permute-start.6) | collective-permute-done | bytes 1310752 | tf_op jit(solution)/shard_map/ppermute | solution.py:42
  152.5 5.3 %collective-permute-start.7 = (bf16[2,160,2048]{2,1,0:T(8,128)(2,1)S(1)}, bf16[2,160,2048]{2,1,0:T(8,128)(2,1)}, u32[]{:S(2)}, u32[]{:S(2)}) collective-permute-start(bf16[2,160,2048]{2,1,0:T(8,128)(2,1)S(1)} %collective-permute-done.6.second_ref), channel_id=1, source_target_pairs={{0,8},{4,12},{8,16},{12,20},{16,24},{20,28},{1,9},{5,13},{9,17},{1... | collective-permute-start | bytes 3932168 | tf_op jit(solution)/shard_map/ppermute | solution.py:37
  157.8 4.4 %shard_map.70 = f32[2,8,512]{2,1,0:T(8,128)} custom-call(bf16[2,160,2048]{2,1,0:T(8,128)(2,1)} %bitcast.93, bf16[2,160,2048]{2,1,0:T(8,128)(2,1)} %collective-permute-done.4.second_ref), custom_call_target="tpu_custom_call" | custom-call | flops 13107200 | bytes 2621440 | tf_op jit(solution)/shard_map/pallas_call | solution.py:139
  162.2 0.0 copy-done.6
  162.2 4.4 %shard_map.69 = f32[2,8,512]{2,1,0:T(8,128)} custom-call(bf16[2,160,2048]{2,1,0:T(8,128)(2,1)} %bitcast.98, bf16[2,160,2048]{2,1,0:T(8,128)(2,1)} %collective-permute-done.2.second_ref), custom_call_target="tpu_custom_call" | custom-call | flops 13107200 | bytes 2621440 | tf_op jit(solution)/shard_map/pallas_call | solution.py:139
  166.6 4.4 %shard_map.72 = f32[2,8,512]{2,1,0:T(8,128)} custom-call(bf16[2,160,2048]{2,1,0:T(8,128)(2,1)} %bitcast.94, bf16[2,160,2048]{2,1,0:T(8,128)(2,1)} %copy-done.5), custom_call_target="tpu_custom_call" | custom-call | flops 13107200 | bytes 2621440 | tf_op jit(solution)/shard_map/pallas_call | solution.py:139
  170.9 4.4 %shard_map.71 = f32[2,8,512]{2,1,0:T(8,128)} custom-call(bf16[2,160,2048]{2,1,0:T(8,128)(2,1)} %bitcast.99, bf16[2,160,2048]{2,1,0:T(8,128)(2,1)} %copy-done.6), custom_call_target="tpu_custom_call" | custom-call | flops 13107200 | bytes 2621440 | tf_op jit(solution)/shard_map/pallas_call | solution.py:139
  175.3 0.0 collective-permute-done.5.second_ref
  175.3 4.4 %shard_map.66 = f32[2,8,512]{2,1,0:T(8,128)} custom-call(bf16[2,160,2048]{2,1,0:T(8,128)(2,1)} %bitcast.95, bf16[2,160,2048]{2,1,0:T(8,128)(2,1)} %collective-permute-done.5.second_ref), custom_call_target="tpu_custom_call" | custom-call | flops 13107200 | bytes 2621440 | tf_op jit(solution)/shard_map/pallas_call | solution.py:139
  179.7 0.0 collective-permute-done.3.second_ref
  179.7 4.4 %shard_map.65 = f32[2,8,512]{2,1,0:T(8,128)} custom-call(bf16[2,160,2048]{2,1,0:T(8,128)(2,1)} %bitcast.100, bf16[2,160,2048]{2,1,0:T(8,128)(2,1)} %collective-permute-done.3.second_ref), custom_call_target="tpu_custom_call" | custom-call | flops 13107200 | bytes 2621440 | tf_op jit(solution)/shard_map/pallas_call | solution.py:139
  184.0 0.0 collective-permute-done.9.second_ref
  184.0 4.4 %shard_map.68 = f32[2,8,512]{2,1,0:T(8,128)} custom-call(bf16[2,160,2048]{2,1,0:T(8,128)(2,1)} %bitcast.96, bf16[2,160,2048]{2,1,0:T(8,128)(2,1)} %collective-permute-done.9.second_ref), custom_call_target="tpu_custom_call" | custom-call | flops 13107200 | bytes 2621440 | tf_op jit(solution)/shard_map/pallas_call | solution.py:139
  188.5 0.0 copy-start.15
  188.5 0.0 collective-permute-done.7.second_ref
  188.5 4.4 %shard_map.67 = f32[2,8,512]{2,1,0:T(8,128)} custom-call(bf16[2,160,2048]{2,1,0:T(8,128)(2,1)} %bitcast.101, bf16[2,160,2048]{2,1,0:T(8,128)(2,1)} %collective-permute-done.7.second_ref), custom_call_target="tpu_custom_call" | custom-call | flops 13107200 | bytes 2621440 | tf_op jit(solution)/shard_map/pallas_call | solution.py:139
  193.0 1.6 select_select_fusion
  194.6 3.4 %all-to-all-start = ((f32[8,2,8,512]{3,2,1,0:T(8,128)}), f32[8,2,8,512]{3,2,1,0:T(8,128)S(1)}, u32[]{:S(2)}, u32[]{:S(2)}) async-start(f32[8,2,8,512]{3,2,1,0:T(8,128)} %select_select_fusion), calls=%async_computation | async-start | bytes 524288 | tf_op jit(solution)/shard_map/all_to_all | solution.py:194
  198.0 0.0 copy-done.15
  198.0 0.7 fusion.49
  218.5 0.0 all-to-all-done
  218.7 0.0 copy-done.14
  218.9 0.7 maximum_bitcast_fusion
  (41 shorter events, 0.3 us)
Async XLA Ops:
  1.1 10.8 %collective-permute-start.1 = (bf16[1,2,16,4096]{3,2,1,0:T(8,128)(2,1)S(1)}, bf16[1,2,16,4096]{3,2,1,0:T(8,128)(2,1)S(1)}, u32[]{:S(2)}, u32[]{:S(2)}) collective-permute-start(bf16[1,2,16,4096]{3,2,1,0:T(8,128)(2,1)S(1)} %get-tuple-element.7), channel_id=1, source_target_pairs={{1,0},{2,1},{3,2},{5,4},{6,5},{7,6},{9,8},{10,9},{11,10},{13,12},{... | collective-permute-start | bytes 786440 | tf_op jit(solution)/shard_map/ppermute | solution.py:27
  2.4 9.5 %collective-permute-start = (bf16[1,2,16,4096]{3,2,1,0:T(8,128)(2,1)S(1)}, bf16[1,2,16,4096]{3,2,1,0:T(8,128)(2,1)S(1)}, u32[]{:S(2)}, u32[]{:S(2)}) collective-permute-start(bf16[1,2,16,4096]{3,2,1,0:T(8,128)(2,1)S(1)} %get-tuple-element.8), channel_id=1, source_target_pairs={{0,1},{1,2},{2,3},{4,5},{5,6},{6,7},{8,9},{9,10},{10,11},{12,13},{... | collective-permute-start | bytes 786440 | tf_op jit(solution)/shard_map/ppermute | solution.py:25
  54.9 1.1 copy-start.4
  56.0 2.6 %copy-start = (bf16[2,20,8,2048]{3,2,1,0:T(8,128)(2,1)}, bf16[2,20,8,2048]{3,2,1,0:T(8,128)(2,1)S(1)}, u32[]{:S(2)}) copy-start(bf16[2,20,8,2048]{3,2,1,0:T(8,128)(2,1)S(1)} %copy.32) | copy-start | bytes 3932164
  56.0 34.2 %collective-permute-start.4 = (bf16[2,160,2048]{2,1,0:T(8,128)(2,1)S(1)}, bf16[2,160,2048]{2,1,0:T(8,128)(2,1)}, u32[]{:S(2)}, u32[]{:S(2)}) collective-permute-start(bf16[2,160,2048]{2,1,0:T(8,128)(2,1)S(1)} %bitcast.92), channel_id=1, source_target_pairs={{8,0},{12,4},{16,8},{20,12},{24,16},{28,20},{9,1},{13,5},{17,9},{2... | collective-permute-start | bytes 3932168 | tf_op jit(solution)/shard_map/ppermute | solution.py:37
  58.7 1.1 copy-start.2
  59.7 33.7 %copy-start.1 = (bf16[2,20,8,2048]{3,2,1,0:T(8,128)(2,1)}, bf16[2,20,8,2048]{3,2,1,0:T(8,128)(2,1)S(1)}, u32[]{:S(2)}) copy-start(bf16[2,20,8,2048]{3,2,1,0:T(8,128)(2,1)S(1)} %copy.33) | copy-start | bytes 3932164
  59.7 35.7 %collective-permute-start.2 = (bf16[2,160,2048]{2,1,0:T(8,128)(2,1)S(1)}, bf16[2,160,2048]{2,1,0:T(8,128)(2,1)}, u32[]{:S(2)}, u32[]{:S(2)}) collective-permute-start(bf16[2,160,2048]{2,1,0:T(8,128)(2,1)S(1)} %bitcast.97), channel_id=1, source_target_pairs={{0,8},{4,12},{8,16},{12,20},{16,24},{20,28},{1,9},{5,13},{9,17},{1... | collective-permute-start | bytes 3932168 | tf_op jit(solution)/shard_map/ppermute | solution.py:37
  66.4 29.0 %copy-start.3 = (bf16[2,160,2048]{2,0,1:T(2,128)(2,1)S(1)}, bf16[2,160,2048]{2,0,1:T(2,128)(2,1)}, u32[]{:S(2)}) copy-start(bf16[2,160,2048]{2,0,1:T(2,128)(2,1)} %copy-done.2) | copy-start | bytes 3932164
  93.4 31.7 %collective-permute-start.8 = (bf16[2,160,2048]{2,1,0:T(8,128)(2,1)S(1)}, bf16[2,160,2048]{2,1,0:T(8,128)(2,1)S(1)}, u32[]{:S(2)}, u32[]{:S(2)}) collective-permute-start(bf16[2,160,2048]{2,1,0:T(8,128)(2,1)S(1)} %broadcast_select_fusion), channel_id=1, source_target_pairs={{0,4},{4,0},{8,12},{12,8},{16,20},{20,16},{24,28},{28,24},{1,5},{5... | collective-permute-start | bytes 3932168 | tf_op jit(solution)/shard_map/ppermute | solution.py:42
  96.9 55.6 %collective-permute-start.6 = (bf16[2,160,2048]{2,1,0:T(8,128)(2,1)S(1)}, bf16[2,160,2048]{2,1,0:T(8,128)(2,1)S(1)}, u32[]{:S(2)}, u32[]{:S(2)}) collective-permute-start(bf16[2,160,2048]{2,1,0:T(8,128)(2,1)S(1)} %broadcast_select_fusion.1), channel_id=1, source_target_pairs={{0,4},{4,0},{8,12},{12,8},{16,20},{20,16},{24,28},{28,24},{1,5},{5... | collective-permute-start | bytes 3932168 | tf_op jit(solution)/shard_map/ppermute | solution.py:42
  99.2 76.2 %collective-permute-start.5 = (bf16[2,160,2048]{2,1,0:T(8,128)(2,1)}, bf16[2,160,2048]{2,1,0:T(8,128)(2,1)}, u32[]{:S(2)}, u32[]{:S(2)}) collective-permute-start(bf16[2,160,2048]{2,1,0:T(8,128)(2,1)} %collective-permute-done.4.second_ref), channel_id=1, source_target_pairs={{8,0},{12,4},{16,8},{20,12},{24,16},{28,20},{9,1},{13,5},{17,9},{2... | collective-permute-start | bytes 3932168 | tf_op jit(solution)/shard_map/ppermute | solution.py:37
  100.4 79.2 %collective-permute-start.3 = (bf16[2,160,2048]{2,1,0:T(8,128)(2,1)}, bf16[2,160,2048]{2,1,0:T(8,128)(2,1)}, u32[]{:S(2)}, u32[]{:S(2)}) collective-permute-start(bf16[2,160,2048]{2,1,0:T(8,128)(2,1)} %collective-permute-done.2.second_ref), channel_id=1, source_target_pairs={{0,8},{4,12},{8,16},{12,20},{16,24},{20,28},{1,9},{5,13},{9,17},{1... | collective-permute-start | bytes 3932168 | tf_op jit(solution)/shard_map/ppermute | solution.py:37
  125.1 37.1 %copy-start.5 = (bf16[2,160,2048]{2,1,0:T(8,128)(2,1)}, bf16[2,160,2048]{2,1,0:T(8,128)(2,1)S(1)}, u32[]{:S(2)}) copy-start(bf16[2,160,2048]{2,1,0:T(8,128)(2,1)S(1)} %collective-permute-done.8.second_ref) | copy-start | bytes 3932164
  125.1 59.0 %collective-permute-start.9 = (bf16[2,160,2048]{2,1,0:T(8,128)(2,1)S(1)}, bf16[2,160,2048]{2,1,0:T(8,128)(2,1)}, u32[]{:S(2)}, u32[]{:S(2)}) collective-permute-start(bf16[2,160,2048]{2,1,0:T(8,128)(2,1)S(1)} %collective-permute-done.8.second_ref), channel_id=1, source_target_pairs={{8,0},{12,4},{16,8},{20,12},{24,16},{28,20},{9,1},{13,5},{17,9},{2... | collective-permute-start | bytes 3932168 | tf_op jit(solution)/shard_map/ppermute | solution.py:37
  152.5 9.7 %copy-start.6 = (bf16[2,160,2048]{2,1,0:T(8,128)(2,1)}, bf16[2,160,2048]{2,1,0:T(8,128)(2,1)S(1)}, u32[]{:S(2)}) copy-start(bf16[2,160,2048]{2,1,0:T(8,128)(2,1)S(1)} %collective-permute-done.6.second_ref) | copy-start | bytes 3932164
  152.5 35.9 %collective-permute-start.7 = (bf16[2,160,2048]{2,1,0:T(8,128)(2,1)S(1)}, bf16[2,160,2048]{2,1,0:T(8,128)(2,1)}, u32[]{:S(2)}, u32[]{:S(2)}) collective-permute-start(bf16[2,160,2048]{2,1,0:T(8,128)(2,1)S(1)} %collective-permute-done.6.second_ref), channel_id=1, source_target_pairs={{0,8},{4,12},{8,16},{12,20},{16,24},{20,28},{1,9},{5,13},{9,17},{1... | collective-permute-start | bytes 3932168 | tf_op jit(solution)/shard_map/ppermute | solution.py:37
  188.4 4.5 %copy-start.7 = (f32[2,8,512]{2,1,0:T(8,128)S(1)}, f32[2,8,512]{2,1,0:T(8,128)}, u32[]{:S(2)}) copy-start(f32[2,8,512]{2,1,0:T(8,128)} %shard_map.70) | copy-start | bytes 98308
  188.4 4.5 %copy-start.8 = (f32[2,8,512]{2,1,0:T(8,128)S(1)}, f32[2,8,512]{2,1,0:T(8,128)}, u32[]{:S(2)}) copy-start(f32[2,8,512]{2,1,0:T(8,128)} %shard_map.69) | copy-start | bytes 98308
  188.4 4.5 %copy-start.9 = (f32[2,8,512]{2,1,0:T(8,128)S(1)}, f32[2,8,512]{2,1,0:T(8,128)}, u32[]{:S(2)}) copy-start(f32[2,8,512]{2,1,0:T(8,128)} %shard_map.72) | copy-start | bytes 98308
  188.4 4.5 %copy-start.10 = (f32[2,8,512]{2,1,0:T(8,128)S(1)}, f32[2,8,512]{2,1,0:T(8,128)}, u32[]{:S(2)}) copy-start(f32[2,8,512]{2,1,0:T(8,128)} %shard_map.71) | copy-start | bytes 98308
  188.4 4.5 %copy-start.11 = (f32[2,8,512]{2,1,0:T(8,128)S(1)}, f32[2,8,512]{2,1,0:T(8,128)}, u32[]{:S(2)}) copy-start(f32[2,8,512]{2,1,0:T(8,128)} %shard_map.66) | copy-start | bytes 98308
  188.4 4.5 %copy-start.12 = (f32[2,8,512]{2,1,0:T(8,128)S(1)}, f32[2,8,512]{2,1,0:T(8,128)}, u32[]{:S(2)}) copy-start(f32[2,8,512]{2,1,0:T(8,128)} %shard_map.65) | copy-start | bytes 98308
  188.4 4.5 %copy-start.13 = (f32[2,8,512]{2,1,0:T(8,128)S(1)}, f32[2,8,512]{2,1,0:T(8,128)}, u32[]{:S(2)}) copy-start(f32[2,8,512]{2,1,0:T(8,128)} %shard_map.68) | copy-start | bytes 98308
  188.5 9.6 %copy-start.15 = (s32[1,4]{1,0:T(1,128)S(1)}, s32[1,4]{1,0:T(1,128)}, u32[]{:S(2)}) copy-start(s32[1,4]{1,0:T(1,128)} %param.11) | copy-start | bytes 52
  192.9 25.8 %copy-start.14 = (f32[2,8,512]{2,1,0:T(8,128)S(1)}, f32[2,8,512]{2,1,0:T(8,128)}, u32[]{:S(2)}) copy-start(f32[2,8,512]{2,1,0:T(8,128)} %shard_map.67) | copy-start | bytes 98308
  194.6 24.0 %all-to-all-start = ((f32[8,2,8,512]{3,2,1,0:T(8,128)}), f32[8,2,8,512]{3,2,1,0:T(8,128)S(1)}, u32[]{:S(2)}, u32[]{:S(2)}) async-start(f32[8,2,8,512]{3,2,1,0:T(8,128)} %select_select_fusion), calls=%async_computation | async-start | bytes 524288 | tf_op jit(solution)/shard_map/all_to_all | solution.py:194

commit v10 on v9

--- a/solution.py
+++ b/solution.py
@@ -110,42 +110,47 @@
 CHUNK = 512
 
 
-def looks_kernel(first_ref, second_ref, out_ref):
+def looks_kernel(first_ref, *refs):
+    count = len(refs) // 2
     first_re = first_ref[0].astype(jnp.float32)
     first_im = first_ref[1].astype(jnp.float32)
-    second_re = second_ref[0].astype(jnp.float32)
-    second_im = second_ref[1].astype(jnp.float32)
-    real_part = first_re * second_re + first_im * second_im
-    imag_part = first_im * second_re - first_re * second_im
-    rows = real_part.shape[0]
+    rows = first_re.shape[0]
     groups = rows // LOOK_AZ
-    real_lines = real_part.reshape(LOOK_AZ, groups, CHUNK).sum(axis=0)
-    imag_lines = imag_part.reshape(LOOK_AZ, groups, CHUNK).sum(axis=0)
     pooling = (
         lax.broadcasted_iota(jnp.int32, (CHUNK, CHUNK // LOOK_RG), 0) // LOOK_RG
         == lax.broadcasted_iota(jnp.int32, (CHUNK, CHUNK // LOOK_RG), 1)
     ).astype(jnp.float32)
-    real_looks = jnp.dot(real_lines, pooling, precision=lax.Precision.HIGHEST, preferred_element_type=jnp.float32)
-    imag_looks = jnp.dot(imag_lines, pooling, precision=lax.Precision.HIGHEST, preferred_element_type=jnp.float32)
-    out_ref[0] = real_looks / (LOOK_AZ * LOOK_RG)
-    out_ref[1] = imag_looks / (LOOK_AZ * LOOK_RG)
-
-
-def looks(first, second):
+    for second_ref, out_ref in zip(refs[:count], refs[count:]):
+        second_re = second_ref[0].astype(jnp.float32)
+        second_im = second_ref[1].astype(jnp.float32)
+        real_part = first_re * second_re + first_im * second_im
+        imag_part = first_im * second_re - first_re * second_im
+        real_lines = real_part.reshape(LOOK_AZ, groups, CHUNK).sum(axis=0)
+        imag_lines = imag_part.reshape(LOOK_AZ, groups, CHUNK).sum(axis=0)
+        real_looks = jnp.dot(real_lines, pooling, precision=lax.Precision.HIGHEST, preferred_element_type=jnp.float32)
+        imag_looks = jnp.dot(imag_lines, pooling, precision=lax.Precision.HIGHEST, preferred_element_type=jnp.float32)
+        out_ref[0] = real_looks / (LOOK_AZ * LOOK_RG)
+        out_ref[1] = imag_looks / (LOOK_AZ * LOOK_RG)
+
+
+def looks(first, others):
     nlines = first.shape[1]
     width = first.shape[2]
     groups = nlines // LOOK_AZ
     spec = pl.BlockSpec((2, nlines, CHUNK), lambda j: (0, 0, j))
+    out_spec = pl.BlockSpec((2, groups, CHUNK // LOOK_RG), lambda j: (0, 0, j))
+    shape = jax.ShapeDtypeStruct((2, groups, width // LOOK_RG), jnp.float32)
+    count = len(others)
     return pl.pallas_call(
         looks_kernel,
         grid=(width // CHUNK,),
-        in_specs=[spec, spec],
-        out_specs=pl.BlockSpec((2, groups, CHUNK // LOOK_RG), lambda j: (0, 0, j)),
-        out_shape=jax.ShapeDtypeStruct((2, groups, width // LOOK_RG), jnp.float32),
+        in_specs=[spec] * (count + 1),
+        out_specs=[out_spec] * count,
+        out_shape=[shape] * count,
         cost_estimate=pl.CostEstimate(
-            flops=nlines * width * 40, transcendentals=0, bytes_accessed=2 * 2 * nlines * width * 2
+            flops=count * nlines * width * 40, transcendentals=0, bytes_accessed=(count + 1) * 2 * nlines * width * 2
         ),
-    )(first, second)
+    )(first, *others)
 
 
 def look_order(image):
@@ -173,18 +178,8 @@
     right_4 = shifted(right_2, "date", -2)
     right_3 = shifted(right_1, "date", -2)
 
-    ahead = {
-        1: looks(own_left, left_1),
-        2: looks(own_left, left_2),
-        3: looks(own_left, left_3),
-        4: looks(own_left, left_4),
-    }
-    behind = {
-        1: looks(own_right, right_1),
-        2: looks(own_right, right_2),
-        3: looks(own_right, right_3),
-        4: looks(own_right, right_4),
-    }
+    ahead = dict(zip((1, 2, 3, 4), looks(own_left, [left_1, left_2, left_3, left_4])))
+    behind = dict(zip((1, 2, 3, 4), looks(own_right, [right_1, right_2, right_3, right_4])))
     count = lax.axis_size("date")
     target = lax.broadcasted_iota(jnp.int32, (count, 1, 1, 1), 0) - date
     sent = jnp.zeros((count,) + ahead[1].shape, jnp.float32)

time: 221 us -> 225 us (1.018)
  waiting for transfers between devices: 68.3 us -> 96.3 us
  Pallas kernels: 68.1 us -> 46.7 us
  starting transfers between devices: 34.1 us -> 30.4 us
    ppermute x6, waiting for transfers between devices: 23.8 us -> 57.3 us  [shifted(): return lax.ppermute(block, axis, route)]
    pallas_call x8 -> x2, Pallas kernels: 35 us -> 13.5 us  [looks(): pl.pallas_call(looks_kernel, grid=(width // CHUNK,), in_specs=[spec] * (c...]
    ppermute x2, waiting for transfers between devices: 44.5 us -> 39 us  [swapped(): return lax.ppermute(block, axis, [(i, i ^ 1) for i in range(count)])]
    ppermute x6, starting transfers between devices: 22.1 us -> 18.4 us  [shifted(): return lax.ppermute(block, axis, route)]
  transfers between devices with their start and end apart: 11 -> 11, of which waited for: 3 -> 6; matrix products, arithmetic and copies ran while one was open for 6% -> 6% of each run, Pallas kernels for 14% -> 3%
where the time goes in v10:
time: 225 us; the launch traced here: 224 us
  waiting for transfers between devices  96.3 us (43%)
  Pallas kernels  46.7 us (21%)
  starting transfers between devices  30.4 us (14%)
  between operations  21.8 us (10%)
  other arithmetic  16.3 us (7%)
  local copies, waits for them, and re-layouts  12.4 us (6%)
    ppermute x6, waiting for transfers between devices, shifted(): return lax.ppermute(block, axis, route)  57.3 us
    ppermute x2, waiting for transfers between devices, swapped(): return lax.ppermute(block, axis, [(i, i ^ 1) for i in range(count)])  39 us
    pallas_call x1, Pallas kernels, resample_block(): pl.pallas_call(resample_kernel, grid=(2, nlines // ROWS), in_specs=[pl.Bl...  33.1 us
    ppermute x6, starting transfers between devices, shifted(): return lax.ppermute(block, axis, route)  18.4 us
    pallas_call x2, Pallas kernels, looks(): pl.pallas_call(looks_kernel, grid=(width // CHUNK,), in_specs=[spec] * (c...  13.5 us
    all_to_all x1, starting transfers between devices, shards(): got = lax.all_to_all(sent, 'date', 0, 0, tiled=True)  5.13 us
    slice x3, local copies, waits for them, and re-layouts, resample_block(): return (look_order(out[:, :, :half]), look_order(out[:, :, half:]))  4.72 us
  transfers between devices with their start and end apart: 11, of which 6 were waited for; matrix products, arithmetic and copies ran while one was open for 6% of the time, Pallas kernels for 3%

profile of v10, /device:TPU:0, one launch (start us, length us, event | category | flops | bytes accessed | tf_op | source)
XLA Modules:
  0.0 223.7 jit_solution(12673531534228857178)
XLA Ops:
  0.0 1.1 fusion.48
  1.1 2.4 %collective-permute-start = (bf16[1,2,16,4096]{3,2,1,0:T(8,128)(2,1)S(1)}, bf16[1,2,16,4096]{3,2,1,0:T(8,128)(2,1)S(1)}, u32[]{:S(2)}, u32[]{:S(2)}) collective-permute-start(bf16[1,2,16,4096]{3,2,1,0:T(8,128)(2,1)S(1)} %get-tuple-element.24), channel_id=1, source_target_pairs={{0,1},{1,2},{2,3},{4,5},{5,6},{6,7},{8,9},{9,10},{10,11},{12,13},{... | collective-permute-start | bytes 786440 | tf_op jit(solution)/shard_map/ppermute | solution.py:25
  3.4 1.3 collective-permute-start.1
  4.8 0.7 compare_select_fusion
  5.5 0.7 compare_and_fusion
  6.1 0.7 add_bitcast_fusion
  6.8 0.1 fusion.17
  8.3 0.1 copy.20
  8.3 0.8 fusion.14.weights_ref
  9.1 0.7 copy.21.shift_ref
  9.8 0.7 gather_fusion
  10.5 0.7 broadcast_select_fusion.2.coeff_ref
  11.2 0.0 collective-permute-done
  11.2 0.0 collective-permute-done.1
  11.3 3.5 %fusion.2 = bf16[2,167,4096]{2,1,0:T(8,128)(2,1)S(1)} fusion(s32[]{:T(128)S(6)} %select_n.544, bf16[1,2,16,4096]{3,2,1,0:T(8,128)(2,1)S(1)} %collective-permute-done, bf16[1,2,160,4096]{3,2,1,0:T(8,128)(2,1)} %param.6, bf16[1,2,16,4096]{3,2,1,0:T(8,128)(2,1)S(1)} %collective-permute-done.1), kind=kLoop, calls=%fused_computation.6 | loop fusion | flops 8208384 | bytes 5881860 | tf_op jit(solution)/shard_map/convert_element_type | solution.py:86
  14.7 3.1 %pad_convert_fusion.window_ref = f32[2,168,4096]{2,1,0:T(8,128)} fusion(bf16[2,167,4096]{2,1,0:T(8,128)(2,1)S(1)} %fusion.2), kind=kLoop, calls=%fused_computation.7 | loop fusion | flops 1376256 | bytes 8241152 | tf_op jit(solution)/shard_map/jit(_pad)/pad | solution.py:87
  17.8 33.1 %shard_map.64 = bf16[2,160,4096]{2,1,0:T(8,128)(2,1)} custom-call(f32[8]{0:T(128)} %fusion.14.weights_ref, f32[2,168,4096]{2,1,0:T(8,128)} %pad_convert_fusion.window_ref, f32[160,8]{1,0:T(8,128)} %broadcast_select_fusion.2.coeff_ref, s32[160,1]{1,0:T(8,128)} %copy.21.shift_ref), custom_call_target="tpu_custom_call" | custom-call | flops 78643200 | bytes 7864320 | tf_op jit(solution)/shard_map/pallas_call | solution.py:91
  50.9 2.0 fusion.47
  53.0 1.3 copy.22
  54.3 1.8 copy.33
  56.1 5.4 %collective-permute-start.2 = (bf16[2,160,2048]{2,1,0:T(8,128)(2,1)}, bf16[2,160,2048]{2,1,0:T(8,128)(2,1)}, u32[]{:S(2)}, u32[]{:S(2)}) collective-permute-start(bf16[2,160,2048]{2,1,0:T(8,128)(2,1)} %bitcast.88.first_ref), channel_id=1, source_target_pairs={{0,8},{4,12},{8,16},{12,20},{16,24},{20,28},{1,9},{5,13},{9,17},{1... | collective-permute-start | bytes 3932168 | tf_op jit(solution)/shard_map/ppermute | solution.py:37
  61.5 1.3 copy.24
  62.9 1.8 copy.32
  64.7 1.5 collective-permute-start.6
  66.2 22.3 %collective-permute-done.2.refs_1_ = bf16[2,160,2048]{2,1,0:T(8,128)(2,1)} collective-permute-done((bf16[2,160,2048]{2,1,0:T(8,128)(2,1)}, bf16[2,160,2048]{2,1,0:T(8,128)(2,1)}, u32[]{:S(2)}, u32[]{:S(2)}) %collective-permute-start.2) | collective-permute-done | bytes 1310752 | tf_op jit(solution)/shard_map/ppermute | solution.py:37
  88.4 1.5 broadcast_select_fusion.1
  89.9 2.9 %collective-permute-start.3 = (bf16[2,160,2048]{2,1,0:T(8,128)(2,1)S(1)}, bf16[2,160,2048]{2,1,0:T(8,128)(2,1)S(1)}, u32[]{:S(2)}, u32[]{:S(2)}) collective-permute-start(bf16[2,160,2048]{2,1,0:T(8,128)(2,1)S(1)} %broadcast_select_fusion.1), channel_id=1, source_target_pairs={{0,4},{4,0},{8,12},{12,8},{16,20},{20,16},{24,28},{28,24},{1,5},{5... | collective-permute-start | bytes 3932168 | tf_op jit(solution)/shard_map/ppermute | solution.py:42
  92.8 4.6 %collective-permute-done.6.refs_1_ = bf16[2,160,2048]{2,1,0:T(8,128)(2,1)} collective-permute-done((bf16[2,160,2048]{2,1,0:T(8,128)(2,1)}, bf16[2,160,2048]{2,1,0:T(8,128)(2,1)}, u32[]{:S(2)}, u32[]{:S(2)}) %collective-permute-start.6) | collective-permute-done | bytes 1310752 | tf_op jit(solution)/shard_map/ppermute | solution.py:37
  97.4 2.8 %broadcast_select_fusion = bf16[2,160,2048]{2,1,0:T(8,128)(2,1)S(1)} fusion(bf16[2,160,2048]{2,1,0:T(8,128)(2,1)} %collective-permute-done.6.refs_1_, pred[]{:T(512)S(6)} %eq.193, bf16[2,20,8,2048]{3,0,1,2:T(2,128)(2,1)S(1)} %bitcast.93), kind=kLoop, calls=%fused_computation.10 | loop fusion | flops 655360 | bytes 3932161 | tf_op jit(solution)/shard_map/jit(_where)/select_n | solution.py:173
  100.1 0.3 collective-permute-start.7
  100.4 3.5 %collective-permute-start.5 = (bf16[2,160,2048]{2,1,0:T(8,128)(2,1)}, bf16[2,160,2048]{2,1,0:T(8,128)(2,1)}, u32[]{:S(2)}, u32[]{:S(2)}) collective-permute-start(bf16[2,160,2048]{2,1,0:T(8,128)(2,1)} %collective-permute-done.2.refs_1_), channel_id=1, source_target_pairs={{0,8},{4,12},{8,16},{12,20},{16,24},{20,28},{1,9},{5,13},{9,17},{1... | collective-permute-start | bytes 3932168 | tf_op jit(solution)/shard_map/ppermute | solution.py:37
  103.9 17.7 %collective-permute-done.3.refs_0_ = bf16[2,160,2048]{2,1,0:T(8,128)(2,1)S(1)} collective-permute-done((bf16[2,160,2048]{2,1,0:T(8,128)(2,1)S(1)}, bf16[2,160,2048]{2,1,0:T(8,128)(2,1)S(1)}, u32[]{:S(2)}, u32[]{:S(2)}) %collective-permute-start.3) | collective-permute-done | bytes 1310752 | tf_op jit(solution)/shard_map/ppermute | solution.py:42
  121.6 5.5 %collective-permute-start.4 = (bf16[2,160,2048]{2,1,0:T(8,128)(2,1)S(1)}, bf16[2,160,2048]{2,1,0:T(8,128)(2,1)}, u32[]{:S(2)}, u32[]{:S(2)}) collective-permute-start(bf16[2,160,2048]{2,1,0:T(8,128)(2,1)S(1)} %collective-permute-done.3.refs_0_), channel_id=1, source_target_pairs={{0,8},{4,12},{8,16},{12,20},{16,24},{20,28},{1,9},{5,13},{9,17},{1... | collective-permute-start | bytes 3932168 | tf_op jit(solution)/shard_map/ppermute | solution.py:37
  127.0 1.3 collective-permute-start.9
  128.3 21.3 %collective-permute-done.7.refs_0_ = bf16[2,160,2048]{2,1,0:T(8,128)(2,1)S(1)} collective-permute-done((bf16[2,160,2048]{2,1,0:T(8,128)(2,1)S(1)}, bf16[2,160,2048]{2,1,0:T(8,128)(2,1)S(1)}, u32[]{:S(2)}, u32[]{:S(2)}) %collective-permute-start.7) | collective-permute-done | bytes 1310752 | tf_op jit(solution)/shard_map/ppermute | solution.py:42
  149.6 0.0 copy-done.1
  149.6 1.3 collective-permute-start.8
  151.0 0.0 collective-permute-done.5.refs_3_
  151.0 9.3 %collective-permute-done.4.refs_2_ = bf16[2,160,2048]{2,1,0:T(8,128)(2,1)} collective-permute-done((bf16[2,160,2048]{2,1,0:T(8,128)(2,1)S(1)}, bf16[2,160,2048]{2,1,0:T(8,128)(2,1)}, u32[]{:S(2)}, u32[]{:S(2)}) %collective-permute-start.4) | collective-permute-done | bytes 1310752 | tf_op jit(solution)/shard_map/ppermute | solution.py:37
  160.3 6.8 %shard_map.65 = (f32[2,8,512]{2,1,0:T(8,128)}, f32[2,8,512]{2,1,0:T(8,128)}, f32[2,8,512]{2,1,0:T(8,128)}, f32[2,8,512]{2,1,0:T(8,128)}) custom-call(bf16[2,160,2048]{2,1,0:T(8,128)(2,1)} %bitcast.88.first_ref, bf16[2,160,2048]{2,1,0:T(8,128)(2,1)} %copy-done.1, bf16[2,160,2048]{2,1,0:T(8,128)(2,1)} %collective-permute-done.2.refs_1_, ...), custom_call_target="tpu_custom_call" | custom-call | flops 52428800 | bytes 6553600 | tf_op jit(solution)/shard_map/pallas_call | solution.py:144
  167.0 0.0 copy-done
  167.0 0.0 copy-start.3
  167.0 0.0 copy-start.4
  167.1 0.0 copy-start.5
  167.1 0.0 copy-start.6
  167.1 0.0 copy-start.11
  167.1 0.0 collective-permute-done.9.refs_3_
  167.1 0.0 copy-start.2
  167.1 21.2 %collective-permute-done.8.refs_2_ = bf16[2,160,2048]{2,1,0:T(8,128)(2,1)} collective-permute-done((bf16[2,160,2048]{2,1,0:T(8,128)(2,1)S(1)}, bf16[2,160,2048]{2,1,0:T(8,128)(2,1)}, u32[]{:S(2)}, u32[]{:S(2)}) %collective-permute-start.8) | collective-permute-done | bytes 1310752 | tf_op jit(solution)/shard_map/ppermute | solution.py:37
  188.3 0.0 copy-done.2
  188.3 6.8 %shard_map.66 = (f32[2,8,512]{2,1,0:T(8,128)}, f32[2,8,512]{2,1,0:T(8,128)}, f32[2,8,512]{2,1,0:T(8,128)}, f32[2,8,512]{2,1,0:T(8,128)}) custom-call(bf16[2,160,2048]{2,1,0:T(8,128)(2,1)} %bitcast.87.first_ref, bf16[2,160,2048]{2,1,0:T(8,128)(2,1)} %copy-done, bf16[2,160,2048]{2,1,0:T(8,128)(2,1)} %collective-permute-done.6.refs_1_, ...), custom_call_target="tpu_custom_call" | custom-call | flops 52428800 | bytes 6553600 | tf_op jit(solution)/shard_map/pallas_call | solution.py:144
  195.0 0.0 copy-start.9
  195.0 0.0 copy-start.10
  195.1 0.0 copy-done.3
  195.1 0.0 copy-done.4
  195.1 0.0 copy-done.5
  195.1 0.0 copy-done.6
  195.1 1.7 select_select_fusion
  196.8 5.1 %all-to-all-start = ((f32[8,2,8,512]{3,2,1,0:T(8,128)}), f32[8,2,8,512]{3,2,1,0:T(8,128)S(1)}, u32[]{:S(2)}, u32[]{:S(2)}) async-start(f32[8,2,8,512]{3,2,1,0:T(8,128)} %select_select_fusion), calls=%async_computation | async-start | bytes 524288 | tf_op jit(solution)/shard_map/all_to_all | solution.py:189
  201.9 0.0 copy-done.11
  201.9 0.7 fusion.49
  222.6 0.0 all-to-all-done
  222.8 0.0 copy-done.7
  223.0 0.7 maximum_bitcast_fusion
  (27 shorter events, 0.3 us)
Async XLA Ops:
  1.1 10.2 %collective-permute-start = (bf16[1,2,16,4096]{3,2,1,0:T(8,128)(2,1)S(1)}, bf16[1,2,16,4096]{3,2,1,0:T(8,128)(2,1)S(1)}, u32[]{:S(2)}, u32[]{:S(2)}) collective-permute-start(bf16[1,2,16,4096]{3,2,1,0:T(8,128)(2,1)S(1)} %get-tuple-element.24), channel_id=1, source_target_pairs={{0,1},{1,2},{2,3},{4,5},{5,6},{6,7},{8,9},{9,10},{10,11},{12,13},{... | collective-permute-start | bytes 786440 | tf_op jit(solution)/shard_map/ppermute | solution.py:25
  3.4 7.8 %collective-permute-start.1 = (bf16[1,2,16,4096]{3,2,1,0:T(8,128)(2,1)S(1)}, bf16[1,2,16,4096]{3,2,1,0:T(8,128)(2,1)S(1)}, u32[]{:S(2)}, u32[]{:S(2)}) collective-permute-start(bf16[1,2,16,4096]{3,2,1,0:T(8,128)(2,1)S(1)} %get-tuple-element.23), channel_id=1, source_target_pairs={{1,0},{2,1},{3,2},{5,4},{6,5},{7,6},{9,8},{10,9},{11,10},{13,12},{... | collective-permute-start | bytes 786440 | tf_op jit(solution)/shard_map/ppermute | solution.py:27
  56.1 32.3 %collective-permute-start.2 = (bf16[2,160,2048]{2,1,0:T(8,128)(2,1)}, bf16[2,160,2048]{2,1,0:T(8,128)(2,1)}, u32[]{:S(2)}, u32[]{:S(2)}) collective-permute-start(bf16[2,160,2048]{2,1,0:T(8,128)(2,1)} %bitcast.88.first_ref), channel_id=1, source_target_pairs={{0,8},{4,12},{8,16},{12,20},{16,24},{20,28},{1,9},{5,13},{9,17},{1... | collective-permute-start | bytes 3932168 | tf_op jit(solution)/shard_map/ppermute | solution.py:37
  64.7 32.7 %collective-permute-start.6 = (bf16[2,160,2048]{2,1,0:T(8,128)(2,1)}, bf16[2,160,2048]{2,1,0:T(8,128)(2,1)}, u32[]{:S(2)}, u32[]{:S(2)}) collective-permute-start(bf16[2,160,2048]{2,1,0:T(8,128)(2,1)} %bitcast.87.first_ref), channel_id=1, source_target_pairs={{8,0},{12,4},{16,8},{20,12},{24,16},{28,20},{9,1},{13,5},{17,9},{2... | collective-permute-start | bytes 3932168 | tf_op jit(solution)/shard_map/ppermute | solution.py:37
  89.9 31.6 %collective-permute-start.3 = (bf16[2,160,2048]{2,1,0:T(8,128)(2,1)S(1)}, bf16[2,160,2048]{2,1,0:T(8,128)(2,1)S(1)}, u32[]{:S(2)}, u32[]{:S(2)}) collective-permute-start(bf16[2,160,2048]{2,1,0:T(8,128)(2,1)S(1)} %broadcast_select_fusion.1), channel_id=1, source_target_pairs={{0,4},{4,0},{8,12},{12,8},{16,20},{20,16},{24,28},{28,24},{1,5},{5... | collective-permute-start | bytes 3932168 | tf_op jit(solution)/shard_map/ppermute | solution.py:42
  100.1 49.5 %collective-permute-start.7 = (bf16[2,160,2048]{2,1,0:T(8,128)(2,1)S(1)}, bf16[2,160,2048]{2,1,0:T(8,128)(2,1)S(1)}, u32[]{:S(2)}, u32[]{:S(2)}) collective-permute-start(bf16[2,160,2048]{2,1,0:T(8,128)(2,1)S(1)} %broadcast_select_fusion), channel_id=1, source_target_pairs={{0,4},{4,0},{8,12},{12,8},{16,20},{20,16},{24,28},{28,24},{1,5},{5... | collective-permute-start | bytes 3932168 | tf_op jit(solution)/shard_map/ppermute | solution.py:42
  100.4 50.6 %collective-permute-start.5 = (bf16[2,160,2048]{2,1,0:T(8,128)(2,1)}, bf16[2,160,2048]{2,1,0:T(8,128)(2,1)}, u32[]{:S(2)}, u32[]{:S(2)}) collective-permute-start(bf16[2,160,2048]{2,1,0:T(8,128)(2,1)} %collective-permute-done.2.refs_1_), channel_id=1, source_target_pairs={{0,8},{4,12},{8,16},{12,20},{16,24},{20,28},{1,9},{5,13},{9,17},{1... | collective-permute-start | bytes 3932168 | tf_op jit(solution)/shard_map/ppermute | solution.py:37
  121.6 28.1 %copy-start.1 = (bf16[2,160,2048]{2,1,0:T(8,128)(2,1)}, bf16[2,160,2048]{2,1,0:T(8,128)(2,1)S(1)}, u32[]{:S(2)}) copy-start(bf16[2,160,2048]{2,1,0:T(8,128)(2,1)S(1)} %collective-permute-done.3.refs_0_) | copy-start | bytes 3932164
  121.6 38.7 %collective-permute-start.4 = (bf16[2,160,2048]{2,1,0:T(8,128)(2,1)S(1)}, bf16[2,160,2048]{2,1,0:T(8,128)(2,1)}, u32[]{:S(2)}, u32[]{:S(2)}) collective-permute-start(bf16[2,160,2048]{2,1,0:T(8,128)(2,1)S(1)} %collective-permute-done.3.refs_0_), channel_id=1, source_target_pairs={{0,8},{4,12},{8,16},{12,20},{16,24},{20,28},{1,9},{5,13},{9,17},{1... | collective-permute-start | bytes 3932168 | tf_op jit(solution)/shard_map/ppermute | solution.py:37
  127.0 40.1 %collective-permute-start.9 = (bf16[2,160,2048]{2,1,0:T(8,128)(2,1)}, bf16[2,160,2048]{2,1,0:T(8,128)(2,1)S(1)}, u32[]{:S(2)}, u32[]{:S(2)}) collective-permute-start(bf16[2,160,2048]{2,1,0:T(8,128)(2,1)} %collective-permute-done.6.refs_1_), channel_id=1, source_target_pairs={{8,0},{12,4},{16,8},{20,12},{24,16},{28,20},{9,1},{13,5},{17,9},{2... | collective-permute-start | bytes 3932168 | tf_op jit(solution)/shard_map/ppermute | solution.py:37
  149.6 17.4 %copy-start = (bf16[2,160,2048]{2,1,0:T(8,128)(2,1)}, bf16[2,160,2048]{2,1,0:T(8,128)(2,1)S(1)}, u32[]{:S(2)}) copy-start(bf16[2,160,2048]{2,1,0:T(8,128)(2,1)S(1)} %collective-permute-done.7.refs_0_) | copy-start | bytes 3932164
  149.6 38.6 %collective-permute-start.8 = (bf16[2,160,2048]{2,1,0:T(8,128)(2,1)S(1)}, bf16[2,160,2048]{2,1,0:T(8,128)(2,1)}, u32[]{:S(2)}, u32[]{:S(2)}) collective-permute-start(bf16[2,160,2048]{2,1,0:T(8,128)(2,1)S(1)} %collective-permute-done.7.refs_0_), channel_id=1, source_target_pairs={{8,0},{12,4},{16,8},{20,12},{24,16},{28,20},{9,1},{13,5},{17,9},{2... | collective-permute-start | bytes 3932168 | tf_op jit(solution)/shard_map/ppermute | solution.py:37
  167.0 28.0 %copy-start.3 = (f32[2,8,512]{2,1,0:T(8,128)S(1)}, f32[2,8,512]{2,1,0:T(8,128)}, u32[]{:S(2)}) copy-start(f32[2,8,512]{2,1,0:T(8,128)} %get-tuple-element.19) | copy-start | bytes 98308
  167.0 28.0 %copy-start.4 = (f32[2,8,512]{2,1,0:T(8,128)S(1)}, f32[2,8,512]{2,1,0:T(8,128)}, u32[]{:S(2)}) copy-start(f32[2,8,512]{2,1,0:T(8,128)} %get-tuple-element.17) | copy-start | bytes 98308
  167.1 28.0 %copy-start.5 = (f32[2,8,512]{2,1,0:T(8,128)S(1)}, f32[2,8,512]{2,1,0:T(8,128)}, u32[]{:S(2)}) copy-start(f32[2,8,512]{2,1,0:T(8,128)} %get-tuple-element.15) | copy-start | bytes 98308
  167.1 28.0 %copy-start.6 = (f32[2,8,512]{2,1,0:T(8,128)S(1)}, f32[2,8,512]{2,1,0:T(8,128)}, u32[]{:S(2)}) copy-start(f32[2,8,512]{2,1,0:T(8,128)} %get-tuple-element.13) | copy-start | bytes 98308
  167.1 34.8 %copy-start.11 = (s32[1,4]{1,0:T(1,128)S(1)}, s32[1,4]{1,0:T(1,128)}, u32[]{:S(2)}) copy-start(s32[1,4]{1,0:T(1,128)} %param.11) | copy-start | bytes 52
  167.1 21.2 %copy-start.2 = (bf16[2,160,2048]{2,1,0:T(8,128)(2,1)}, bf16[2,160,2048]{2,1,0:T(8,128)(2,1)S(1)}, u32[]{:S(2)}) copy-start(bf16[2,160,2048]{2,1,0:T(8,128)(2,1)S(1)} %collective-permute-done.9.refs_3_) | copy-start | bytes 3932164
  195.0 27.8 %copy-start.7 = (f32[2,8,512]{2,1,0:T(8,128)S(1)}, f32[2,8,512]{2,1,0:T(8,128)}, u32[]{:S(2)}) copy-start(f32[2,8,512]{2,1,0:T(8,128)} %get-tuple-element.20) | copy-start | bytes 98308
  195.0 27.8 %copy-start.8 = (f32[2,8,512]{2,1,0:T(8,128)S(1)}, f32[2,8,512]{2,1,0:T(8,128)}, u32[]{:S(2)}) copy-start(f32[2,8,512]{2,1,0:T(8,128)} %get-tuple-element.18) | copy-start | bytes 98308
  195.0 27.8 %copy-start.9 = (f32[2,8,512]{2,1,0:T(8,128)S(1)}, f32[2,8,512]{2,1,0:T(8,128)}, u32[]{:S(2)}) copy-start(f32[2,8,512]{2,1,0:T(8,128)} %get-tuple-element.16) | copy-start | bytes 98308
  195.0 27.8 %copy-start.10 = (f32[2,8,512]{2,1,0:T(8,128)S(1)}, f32[2,8,512]{2,1,0:T(8,128)}, u32[]{:S(2)}) copy-start(f32[2,8,512]{2,1,0:T(8,128)} %get-tuple-element.14) | copy-start | bytes 98308
  196.8 25.9 %all-to-all-start = ((f32[8,2,8,512]{3,2,1,0:T(8,128)}), f32[8,2,8,512]{3,2,1,0:T(8,128)S(1)}, u32[]{:S(2)}, u32[]{:S(2)}) async-start(f32[8,2,8,512]{3,2,1,0:T(8,128)} %select_select_fusion), calls=%async_computation | async-start | bytes 524288 | tf_op jit(solution)/shard_map/all_to_all | solution.py:189

commit v11 on v10

--- a/solution.py
+++ b/solution.py
@@ -31,15 +31,10 @@
     return cells
 
 
-def shifted(block, axis, distance):
+def routed(block, axis, distance, keep):
     count = lax.axis_size(axis)
-    route = [(i + distance, i) for i in range(count) if 0 <= i + distance < count]
+    route = [(i + distance, i) for i in range(count) if 0 <= i + distance < count and keep(i, count)]
     return lax.ppermute(block, axis, route)
-
-
-def swapped(block, axis):
-    count = lax.axis_size(axis)
-    return lax.ppermute(block, axis, [(i, i ^ 1) for i in range(count)])
 
 
 def kernel_table():
@@ -169,14 +164,22 @@
     date = lax.axis_index("date")
     even = date % 2 == 0
 
-    left_2 = shifted(own_left, "date", 2)
-    left_1 = swapped(jnp.where(even, left_2, own_left), "date")
-    left_4 = shifted(left_2, "date", 2)
-    left_3 = shifted(left_1, "date", 2)
-    right_2 = shifted(own_right, "date", -2)
-    right_1 = swapped(jnp.where(even, own_right, right_2), "date")
-    right_4 = shifted(right_2, "date", -2)
-    right_3 = shifted(right_1, "date", -2)
+    left_2 = routed(own_left, "date", 2, lambda i, n: True)
+    left_1_even = routed(own_left, "date", 1, lambda i, n: i % 2 == 0)
+    left_4 = routed(left_2, "date", 2, lambda i, n: i + 4 < n)
+    left_1_odd = routed(left_2, "date", -1, lambda i, n: i % 2 == 1 and i + 1 < n)
+    left_3_even = routed(left_1_even, "date", 2, lambda i, n: i % 2 == 0 and i + 3 < n)
+    left_3_odd = routed(left_1_odd, "date", 2, lambda i, n: i % 2 == 1 and i + 3 < n)
+    left_1 = jnp.where(even, left_1_even, left_1_odd)
+    left_3 = jnp.where(even, left_3_even, left_3_odd)
+    right_2 = routed(own_right, "date", -2, lambda i, n: True)
+    right_1_odd = routed(own_right, "date", -1, lambda i, n: i % 2 == 1)
+    right_4 = routed(right_2, "date", -2, lambda i, n: i >= 4)
+    right_1_even = routed(right_2, "date", 1, lambda i, n: i % 2 == 0 and i >= 1)
+    right_3_odd = routed(right_1_odd, "date", -2, lambda i, n: i % 2 == 1 and i >= 3)
+    right_3_even = routed(right_1_even, "date", -2, lambda i, n: i % 2 == 0 and i >= 3)
+    right_1 = jnp.where(even, right_1_even, right_1_odd)
+    right_3 = jnp.where(even, right_3_even, right_3_odd)
 
     ahead = dict(zip((1, 2, 3, 4), looks(own_left, [left_1, left_2, left_3, left_4])))
     behind = dict(zip((1, 2, 3, 4), looks(own_right, [right_1, right_2, right_3, right_4])))

time: 225 us -> 248 us (1.10)
  starting transfers between devices: 30.4 us -> 76.3 us
  waiting for transfers between devices: 96.3 us -> 69.9 us
  other arithmetic: 16.3 us -> 21 us
    all_to_all x1, starting transfers between devices: 5.13 us -> 46.8 us  [shards(): got = lax.all_to_all(sent, 'date', 0, 0, tiled=True)]
    ppermute x8 -> x12, waiting for transfers between devices: 96.3 us -> 69.9 us  [routed(): return lax.ppermute(block, axis, route)]
    select_n x2 -> x4, other arithmetic: 4.24 us -> 8.86 us  [the longest x1 2.58 us: shards(): right_3 = jnp.where(even, right_3_even, right_3_odd)]
    ppermute x8 -> x12, starting transfers between devices: 21.6 us -> 25.9 us  [routed(): return lax.ppermute(block, axis, route)]
  transfers between devices with their start and end apart: 11 -> 15, of which waited for: 6 -> 3; matrix products, arithmetic and copies ran while one was open for 6% -> 7% of each run, Pallas kernels for 3% -> 3%
where the time goes in v11:
time: 248 us; the launch traced here: 247 us
  starting transfers between devices  76.3 us (31%)
  waiting for transfers between devices  69.9 us (28%)
  Pallas kernels  46.7 us (19%)
  between operations  21.6 us (9%)
  other arithmetic  21 us (8%)
  local copies, waits for them, and re-layouts  11.2 us (5%)
    ppermute x12, waiting for transfers between devices, routed(): return lax.ppermute(block, axis, route)  69.9 us
    all_to_all x1, starting transfers between devices, shards(): got = lax.all_to_all(sent, 'date', 0, 0, tiled=True)  46.8 us
    pallas_call x1, Pallas kernels, resample_block(): pl.pallas_call(resample_kernel, grid=(2, nlines // ROWS), in_specs=[pl.Bl...  33.2 us
    ppermute x12, starting transfers between devices, routed(): return lax.ppermute(block, axis, route)  25.9 us
    pallas_call x2, Pallas kernels, looks(): pl.pallas_call(looks_kernel, grid=(width // CHUNK,), in_specs=[spec] * (c...  13.5 us
  transfers between devices with their start and end apart: 15, of which 3 were waited for; matrix products, arithmetic and copies ran while one was open for 7% of the time, Pallas kernels for 3%

profile of v11, /device:TPU:0, one launch (start us, length us, event | category | flops | bytes accessed | tf_op | source)
XLA Modules:
  0.0 246.7 jit_solution(4037767524569738794)
XLA Ops:
  0.0 1.1 fusion.48
  1.1 2.4 collective-permute-start
  3.4 1.3 collective-permute-start.1
  4.8 0.7 compare_select_fusion
  5.5 0.7 compare_and_fusion
  6.1 0.7 add_bitcast_fusion
  6.8 0.1 fusion.17
  7.6 0.1 copy.20
  7.7 0.7 fusion.14.weights_ref
  9.0 0.7 copy.21.shift_ref
  9.8 0.7 gather_fusion
  10.4 0.7 broadcast_select_fusion.4.coeff_ref
  11.2 0.0 collective-permute-done
  11.2 0.0 collective-permute-done.1
  11.2 3.5 %fusion.2 = bf16[2,167,4096]{2,1,0:T(8,128)(2,1)S(1)} fusion(s32[]{:T(128)S(6)} %select_n.552, bf16[1,2,16,4096]{3,2,1,0:T(8,128)(2,1)S(1)} %collective-permute-done, bf16[1,2,160,4096]{3,2,1,0:T(8,128)(2,1)} %param.6, bf16[1,2,16,4096]{3,2,1,0:T(8,128)(2,1)S(1)} %collective-permute-done.1), kind=kLoop, calls=%fused_computation.6 | loop fusion | flops 8208384 | bytes 5881860 | tf_op jit(solution)/shard_map/convert_element_type | solution.py:81
  14.7 3.1 %pad_convert_fusion.window_ref = f32[2,168,4096]{2,1,0:T(8,128)} fusion(bf16[2,167,4096]{2,1,0:T(8,128)(2,1)S(1)} %fusion.2), kind=kLoop, calls=%fused_computation.7 | loop fusion | flops 1376256 | bytes 8241152 | tf_op jit(solution)/shard_map/jit(_pad)/pad | solution.py:82
  17.8 33.2 %shard_map.64 = bf16[2,160,4096]{2,1,0:T(8,128)(2,1)} custom-call(f32[8]{0:T(128)} %fusion.14.weights_ref, f32[2,168,4096]{2,1,0:T(8,128)} %pad_convert_fusion.window_ref, f32[160,8]{1,0:T(8,128)} %broadcast_select_fusion.4.coeff_ref, s32[160,1]{1,0:T(8,128)} %copy.21.shift_ref), custom_call_target="tpu_custom_call" | custom-call | flops 78643200 | bytes 7864320 | tf_op jit(solution)/shard_map/pallas_call | solution.py:86
  50.9 2.0 fusion.47
  53.0 1.3 copy.24
  54.3 0.7 copy.28
  55.1 1.3 collective-permute-start.9
  56.4 1.3 copy.22
  57.7 0.7 copy.29
  58.4 0.0 copy-start
  58.5 6.0 %collective-permute-start.2 = (bf16[2,160,2048]{2,1,0:T(8,128)(2,1)S(1)}, bf16[2,160,2048]{2,1,0:T(8,128)(2,1)}, u32[]{:S(2)}, u32[]{:S(2)}) collective-permute-start(bf16[2,160,2048]{2,1,0:T(8,128)(2,1)S(1)} %bitcast.90), channel_id=1, source_target_pairs={{0,8},{4,12},{8,16},{12,20},{16,24},{20,28},{1,9},{5,13},{9,17},{1... | collective-permute-start | bytes 3932168 | tf_op jit(solution)/shard_map/ppermute | solution.py:37
  64.4 1.3 collective-permute-start.8
  65.7 21.4 %collective-permute-done.9.refs_1_ = bf16[2,160,2048]{2,1,0:T(8,128)(2,1)} collective-permute-done((bf16[2,160,2048]{2,1,0:T(8,128)(2,1)S(1)}, bf16[2,160,2048]{2,1,0:T(8,128)(2,1)}, u32[]{:S(2)}, u32[]{:S(2)}) %collective-permute-start.9) | collective-permute-done | bytes 1310752 | tf_op jit(solution)/shard_map/ppermute | solution.py:37
  87.1 5.5 %collective-permute-start.10 = (bf16[2,160,2048]{2,1,0:T(8,128)(2,1)}, bf16[2,160,2048]{2,1,0:T(8,128)(2,1)}, u32[]{:S(2)}, u32[]{:S(2)}) collective-permute-start(bf16[2,160,2048]{2,1,0:T(8,128)(2,1)} %collective-permute-done.9.refs_1_), channel_id=1, source_target_pairs={{0,4},{8,12},{16,20},{1,5},{9,13},{17,21},{2,6},{10,14},{18,22},{3... | collective-permute-start | bytes 3932168 | tf_op jit(solution)/shard_map/ppermute | solution.py:37
  92.6 2.4 collective-permute-start.4
  95.0 0.0 collective-permute-done.2.refs_1_
  95.0 1.7 collective-permute-start.3
  96.7 0.0 collective-permute-done.8
  96.7 1.3 collective-permute-start.11
  98.1 22.6 %collective-permute-done.10 = bf16[2,160,2048]{2,1,0:T(8,128)(2,1)} collective-permute-done((bf16[2,160,2048]{2,1,0:T(8,128)(2,1)}, bf16[2,160,2048]{2,1,0:T(8,128)(2,1)}, u32[]{:S(2)}, u32[]{:S(2)}) %collective-permute-start.10) | collective-permute-done | bytes 1310752 | tf_op jit(solution)/shard_map/ppermute | solution.py:37
  120.6 0.7 collective-permute-start.12
  121.4 1.3 collective-permute-start.13
  122.7 25.9 %collective-permute-done.4 = bf16[2,160,2048]{2,1,0:T(8,128)(2,1)} collective-permute-done((bf16[2,160,2048]{2,1,0:T(8,128)(2,1)S(1)}, bf16[2,160,2048]{2,1,0:T(8,128)(2,1)}, u32[]{:S(2)}, u32[]{:S(2)}) %collective-permute-start.4) | collective-permute-done | bytes 1310752 | tf_op jit(solution)/shard_map/ppermute | solution.py:37
  148.6 1.7 collective-permute-start.6
  150.3 0.0 collective-permute-done.3
  150.3 1.8 collective-permute-start.5
  152.1 2.5 %broadcast_select_fusion.1.refs_0_ = bf16[2,160,2048]{2,1,0:T(8,128)(2,1)} fusion(bf16[2,160,2048]{2,1,0:T(8,128)(2,1)} %collective-permute-done.8, bf16[2,160,2048]{2,1,0:T(8,128)(2,1)} %collective-permute-done.10, pred[]{:T(512)S(6)} %eq.193), kind=kLoop, calls=%fused_computation.11 | loop fusion | flops 655360 | bytes 3932161 | tf_op jit(solution)/shard_map/jit(_where)/select_n | solution.py:173
  154.6 0.0 collective-permute-done.11
  154.6 0.9 collective-permute-start.7
  155.5 2.5 %broadcast_select_fusion.3.refs_0_ = bf16[2,160,2048]{2,1,0:T(8,128)(2,1)} fusion(bf16[2,160,2048]{2,1,0:T(8,128)(2,1)} %collective-permute-done.3, bf16[2,160,2048]{2,1,0:T(8,128)(2,1)} %collective-permute-done.4, pred[]{:T(512)S(6)} %eq.193), kind=kLoop, calls=%fused_computation.13 | loop fusion | flops 655360 | bytes 3932161 | tf_op jit(solution)/shard_map/jit(_where)/select_n | solution.py:181
  158.0 0.0 collective-permute-done.12
  158.0 1.2 broadcast_select_fusion.refs_2_
  159.3 0.0 collective-permute-done.13.refs_3_
  159.3 6.8 %shard_map.66 = (f32[2,8,512]{2,1,0:T(8,128)}, f32[2,8,512]{2,1,0:T(8,128)}, f32[2,8,512]{2,1,0:T(8,128)}, f32[2,8,512]{2,1,0:T(8,128)}) custom-call(bf16[2,160,2048]{2,1,0:T(8,128)(2,1)} %bitcast.95, bf16[2,160,2048]{2,1,0:T(8,128)(2,1)} %broadcast_select_fusion.1.refs_0_, bf16[2,160,2048]{2,1,0:T(8,128)(2,1)} %collective-permute-done.9.refs_1_, ...), custom_call_target="tpu_custom_call" | custom-call | flops 52428800 | bytes 6553600 | tf_op jit(solution)/shard_map/pallas_call | solution.py:139
  166.0 0.0 collective-permute-done.6
  166.1 0.0 collective-permute-done.5
  166.1 2.6 %broadcast_select_fusion.2.refs_2_ = bf16[2,160,2048]{2,1,0:T(8,128)(2,1)} fusion(bf16[2,160,2048]{2,1,0:T(8,128)(2,1)} %collective-permute-done.5, bf16[2,160,2048]{2,1,0:T(8,128)(2,1)} %collective-permute-done.6, pred[]{:T(512)S(6)} %eq.193), kind=kLoop, calls=%fused_computation.12 | loop fusion | flops 655360 | bytes 3932161 | tf_op jit(solution)/shard_map/jit(_where)/select_n | solution.py:182
  168.7 0.0 copy-start.11
  168.7 0.0 collective-permute-done.7.refs_3_
  168.7 1.1 copy-done.2
  169.7 6.8 %shard_map.65 = (f32[2,8,512]{2,1,0:T(8,128)}, f32[2,8,512]{2,1,0:T(8,128)}, f32[2,8,512]{2,1,0:T(8,128)}, f32[2,8,512]{2,1,0:T(8,128)}) custom-call(bf16[2,160,2048]{2,1,0:T(8,128)(2,1)} %bitcast.92, bf16[2,160,2048]{2,1,0:T(8,128)(2,1)} %broadcast_select_fusion.3.refs_0_, bf16[2,160,2048]{2,1,0:T(8,128)(2,1)} %collective-permute-done.2.refs_1_, ...), custom_call_target="tpu_custom_call" | custom-call | flops 52428800 | bytes 6553600 | tf_op jit(solution)/shard_map/pallas_call | solution.py:139
  176.5 0.0 copy-start.9
  176.5 0.0 copy-start.10
  176.5 0.0 copy-done.3
  176.5 0.0 copy-done.4
  176.6 1.7 select_select_fusion
  178.2 46.8 %all-to-all-start = ((f32[8,2,8,512]{3,2,1,0:T(8,128)}), f32[8,2,8,512]{3,2,1,0:T(8,128)S(1)}, u32[]{:S(2)}, u32[]{:S(2)}) async-start(f32[8,2,8,512]{3,2,1,0:T(8,128)} %select_select_fusion), calls=%async_computation | async-start | bytes 524288 | tf_op jit(solution)/shard_map/all_to_all | solution.py:192
  225.0 0.7 fusion.49
  245.6 0.0 all-to-all-done
  245.9 0.7 maximum_bitcast_fusion
  (37 shorter events, 0.3 us)
Async XLA Ops:
  1.1 10.1 %collective-permute-start = (bf16[1,2,16,4096]{3,2,1,0:T(8,128)(2,1)S(1)}, bf16[1,2,16,4096]{3,2,1,0:T(8,128)(2,1)S(1)}, u32[]{:S(2)}, u32[]{:S(2)}) collective-permute-start(bf16[1,2,16,4096]{3,2,1,0:T(8,128)(2,1)S(1)} %get-tuple-element.24), channel_id=1, source_target_pairs={{0,1},{1,2},{2,3},{4,5},{5,6},{6,7},{8,9},{9,10},{10,11},{12,13},{... | collective-permute-start | bytes 786440 | tf_op jit(solution)/shard_map/ppermute | solution.py:25
  3.4 7.7 %collective-permute-start.1 = (bf16[1,2,16,4096]{3,2,1,0:T(8,128)(2,1)S(1)}, bf16[1,2,16,4096]{3,2,1,0:T(8,128)(2,1)S(1)}, u32[]{:S(2)}, u32[]{:S(2)}) collective-permute-start(bf16[1,2,16,4096]{3,2,1,0:T(8,128)(2,1)S(1)} %get-tuple-element.23), channel_id=1, source_target_pairs={{1,0},{2,1},{3,2},{5,4},{6,5},{7,6},{9,8},{10,9},{11,10},{13,12},{... | collective-permute-start | bytes 786440 | tf_op jit(solution)/shard_map/ppermute | solution.py:27
  55.0 9.4 %copy-start.1 = (bf16[2,20,8,2048]{3,2,1,0:T(8,128)(2,1)}, bf16[2,20,8,2048]{3,2,1,0:T(8,128)(2,1)S(1)}, u32[]{:S(2)}) copy-start(bf16[2,20,8,2048]{3,2,1,0:T(8,128)(2,1)S(1)} %copy.28) | copy-start | bytes 3932164
  55.1 32.0 %collective-permute-start.9 = (bf16[2,160,2048]{2,1,0:T(8,128)(2,1)S(1)}, bf16[2,160,2048]{2,1,0:T(8,128)(2,1)}, u32[]{:S(2)}, u32[]{:S(2)}) collective-permute-start(bf16[2,160,2048]{2,1,0:T(8,128)(2,1)S(1)} %bitcast.93), channel_id=1, source_target_pairs={{8,0},{12,4},{16,8},{20,12},{24,16},{28,20},{9,1},{13,5},{17,9},{2... | collective-permute-start | bytes 3932168 | tf_op jit(solution)/shard_map/ppermute | solution.py:37
  58.4 96.1 %copy-start = (bf16[2,20,8,2048]{3,2,1,0:T(8,128)(2,1)}, bf16[2,20,8,2048]{3,2,1,0:T(8,128)(2,1)S(1)}, u32[]{:S(2)}) copy-start(bf16[2,20,8,2048]{3,2,1,0:T(8,128)(2,1)S(1)} %copy.29) | copy-start | bytes 3932164
  58.5 36.5 %collective-permute-start.2 = (bf16[2,160,2048]{2,1,0:T(8,128)(2,1)S(1)}, bf16[2,160,2048]{2,1,0:T(8,128)(2,1)}, u32[]{:S(2)}, u32[]{:S(2)}) collective-permute-start(bf16[2,160,2048]{2,1,0:T(8,128)(2,1)S(1)} %bitcast.90), channel_id=1, source_target_pairs={{0,8},{4,12},{8,16},{12,20},{16,24},{20,28},{1,9},{5,13},{9,17},{1... | collective-permute-start | bytes 3932168 | tf_op jit(solution)/shard_map/ppermute | solution.py:37
  64.4 32.3 %collective-permute-start.8 = (bf16[2,160,2048]{2,1,0:T(8,128)(2,1)S(1)}, bf16[2,160,2048]{2,1,0:T(8,128)(2,1)}, u32[]{:S(2)}, u32[]{:S(2)}) collective-permute-start(bf16[2,160,2048]{2,1,0:T(8,128)(2,1)S(1)} %bitcast.94), channel_id=1, source_target_pairs={{4,0},{12,8},{20,16},{28,24},{5,1},{13,9},{21,17},{29,25},{6,2},{1... | collective-permute-start | bytes 3932168 | tf_op jit(solution)/shard_map/ppermute | solution.py:37
  87.1 33.5 %collective-permute-start.10 = (bf16[2,160,2048]{2,1,0:T(8,128)(2,1)}, bf16[2,160,2048]{2,1,0:T(8,128)(2,1)}, u32[]{:S(2)}, u32[]{:S(2)}) collective-permute-start(bf16[2,160,2048]{2,1,0:T(8,128)(2,1)} %collective-permute-done.9.refs_1_), channel_id=1, source_target_pairs={{0,4},{8,12},{16,20},{1,5},{9,13},{17,21},{2,6},{10,14},{18,22},{3... | collective-permute-start | bytes 3932168 | tf_op jit(solution)/shard_map/ppermute | solution.py:37
  92.6 56.0 %collective-permute-start.4 = (bf16[2,160,2048]{2,1,0:T(8,128)(2,1)S(1)}, bf16[2,160,2048]{2,1,0:T(8,128)(2,1)}, u32[]{:S(2)}, u32[]{:S(2)}) collective-permute-start(bf16[2,160,2048]{2,1,0:T(8,128)(2,1)S(1)} %bitcast.91), channel_id=1, source_target_pairs={{0,4},{8,12},{16,20},{24,28},{1,5},{9,13},{17,21},{25,29},{2,6},{1... | collective-permute-start | bytes 3932168 | tf_op jit(solution)/shard_map/ppermute | solution.py:37
  95.0 55.3 %collective-permute-start.3 = (bf16[2,160,2048]{2,1,0:T(8,128)(2,1)}, bf16[2,160,2048]{2,1,0:T(8,128)(2,1)}, u32[]{:S(2)}, u32[]{:S(2)}) collective-permute-start(bf16[2,160,2048]{2,1,0:T(8,128)(2,1)} %collective-permute-done.2.refs_1_), channel_id=1, source_target_pairs={{12,8},{20,16},{28,24},{13,9},{21,17},{29,25},{14,10},{22,18},{30,... | collective-permute-start | bytes 3932168 | tf_op jit(solution)/shard_map/ppermute | solution.py:37
  96.7 57.8 %collective-permute-start.11 = (bf16[2,160,2048]{2,1,0:T(8,128)(2,1)}, bf16[2,160,2048]{2,1,0:T(8,128)(2,1)S(1)}, u32[]{:S(2)}, u32[]{:S(2)}) collective-permute-start(bf16[2,160,2048]{2,1,0:T(8,128)(2,1)} %collective-permute-done.8), channel_id=1, source_target_pairs={{8,0},{16,8},{24,16},{9,1},{17,9},{25,17},{10,2},{18,10},{26,18},{... | collective-permute-start | bytes 3932168 | tf_op jit(solution)/shard_map/ppermute | solution.py:37
  120.6 37.4 %collective-permute-start.12 = (bf16[2,160,2048]{2,1,0:T(8,128)(2,1)}, bf16[2,160,2048]{2,1,0:T(8,128)(2,1)S(1)}, u32[]{:S(2)}, u32[]{:S(2)}) collective-permute-start(bf16[2,160,2048]{2,1,0:T(8,128)(2,1)} %collective-permute-done.10), channel_id=1, source_target_pairs={{12,4},{20,12},{13,5},{21,13},{14,6},{22,14},{15,7},{23,15}} | collective-permute-start | bytes 3932168 | tf_op jit(solution)/shard_map/ppermute | solution.py:37
  121.4 37.9 %collective-permute-start.13 = (bf16[2,160,2048]{2,1,0:T(8,128)(2,1)}, bf16[2,160,2048]{2,1,0:T(8,128)(2,1)}, u32[]{:S(2)}, u32[]{:S(2)}) collective-permute-start(bf16[2,160,2048]{2,1,0:T(8,128)(2,1)} %collective-permute-done.9.refs_1_), channel_id=1, source_target_pairs={{8,0},{12,4},{16,8},{20,12},{9,1},{13,5},{17,9},{21,13},{10,2},{14... | collective-permute-start | bytes 3932168 | tf_op jit(solution)/shard_map/ppermute | solution.py:37
  148.6 17.4 %collective-permute-start.6 = (bf16[2,160,2048]{2,1,0:T(8,128)(2,1)}, bf16[2,160,2048]{2,1,0:T(8,128)(2,1)}, u32[]{:S(2)}, u32[]{:S(2)}) collective-permute-start(bf16[2,160,2048]{2,1,0:T(8,128)(2,1)} %collective-permute-done.4), channel_id=1, source_target_pairs={{4,12},{12,20},{20,28},{5,13},{13,21},{21,29},{6,14},{14,22},{22,3... | collective-permute-start | bytes 3932168 | tf_op jit(solution)/shard_map/ppermute | solution.py:37
  150.3 15.7 %collective-permute-start.5 = (bf16[2,160,2048]{2,1,0:T(8,128)(2,1)}, bf16[2,160,2048]{2,1,0:T(8,128)(2,1)}, u32[]{:S(2)}, u32[]{:S(2)}) collective-permute-start(bf16[2,160,2048]{2,1,0:T(8,128)(2,1)} %collective-permute-done.3), channel_id=1, source_target_pairs={{8,16},{16,24},{9,17},{17,25},{10,18},{18,26},{11,19},{19,27}} | collective-permute-start | bytes 3932168 | tf_op jit(solution)/shard_map/ppermute | solution.py:37
  154.6 14.1 %collective-permute-start.7 = (bf16[2,160,2048]{2,1,0:T(8,128)(2,1)}, bf16[2,160,2048]{2,1,0:T(8,128)(2,1)S(1)}, u32[]{:S(2)}, u32[]{:S(2)}) collective-permute-start(bf16[2,160,2048]{2,1,0:T(8,128)(2,1)} %collective-permute-done.2.refs_1_), channel_id=1, source_target_pairs={{8,16},{12,20},{16,24},{20,28},{9,17},{13,21},{17,25},{21,29},{10,... | collective-permute-start | bytes 3932168 | tf_op jit(solution)/shard_map/ppermute | solution.py:37
  168.6 7.9 %copy-start.3 = (f32[2,8,512]{2,1,0:T(8,128)S(1)}, f32[2,8,512]{2,1,0:T(8,128)}, u32[]{:S(2)}) copy-start(f32[2,8,512]{2,1,0:T(8,128)} %get-tuple-element.20) | copy-start | bytes 98308
  168.6 7.9 %copy-start.4 = (f32[2,8,512]{2,1,0:T(8,128)S(1)}, f32[2,8,512]{2,1,0:T(8,128)}, u32[]{:S(2)}) copy-start(f32[2,8,512]{2,1,0:T(8,128)} %get-tuple-element.18) | copy-start | bytes 98308
  168.6 7.9 %copy-start.5 = (f32[2,8,512]{2,1,0:T(8,128)S(1)}, f32[2,8,512]{2,1,0:T(8,128)}, u32[]{:S(2)}) copy-start(f32[2,8,512]{2,1,0:T(8,128)} %get-tuple-element.16) | copy-start | bytes 98308
  168.6 7.9 %copy-start.6 = (f32[2,8,512]{2,1,0:T(8,128)S(1)}, f32[2,8,512]{2,1,0:T(8,128)}, u32[]{:S(2)}) copy-start(f32[2,8,512]{2,1,0:T(8,128)} %get-tuple-element.14) | copy-start | bytes 98308
  168.7 56.4 %copy-start.11 = (s32[1,4]{1,0:T(1,128)S(1)}, s32[1,4]{1,0:T(1,128)}, u32[]{:S(2)}) copy-start(s32[1,4]{1,0:T(1,128)} %param.11) | copy-start | bytes 52
  168.7 1.1 copy-start.2
  176.5 69.2 %copy-start.7 = (f32[2,8,512]{2,1,0:T(8,128)S(1)}, f32[2,8,512]{2,1,0:T(8,128)}, u32[]{:S(2)}) copy-start(f32[2,8,512]{2,1,0:T(8,128)} %get-tuple-element.19) | copy-start | bytes 98308
  176.5 69.2 %copy-start.8 = (f32[2,8,512]{2,1,0:T(8,128)S(1)}, f32[2,8,512]{2,1,0:T(8,128)}, u32[]{:S(2)}) copy-start(f32[2,8,512]{2,1,0:T(8,128)} %get-tuple-element.17) | copy-start | bytes 98308
  176.5 69.2 %copy-start.9 = (f32[2,8,512]{2,1,0:T(8,128)S(1)}, f32[2,8,512]{2,1,0:T(8,128)}, u32[]{:S(2)}) copy-start(f32[2,8,512]{2,1,0:T(8,128)} %get-tuple-element.15) | copy-start | bytes 98308
  176.5 69.2 %copy-start.10 = (f32[2,8,512]{2,1,0:T(8,128)S(1)}, f32[2,8,512]{2,1,0:T(8,128)}, u32[]{:S(2)}) copy-start(f32[2,8,512]{2,1,0:T(8,128)} %get-tuple-element.13) | copy-start | bytes 98308
  178.2 67.3 %all-to-all-start = ((f32[8,2,8,512]{3,2,1,0:T(8,128)}), f32[8,2,8,512]{3,2,1,0:T(8,128)S(1)}, u32[]{:S(2)}, u32[]{:S(2)}) async-start(f32[8,2,8,512]{3,2,1,0:T(8,128)} %select_select_fusion), calls=%async_computation | async-start | bytes 524288 | tf_op jit(solution)/shard_map/all_to_all | solution.py:192

commit v12 on v10

--- a/solution.py
+++ b/solution.py
@@ -31,15 +31,14 @@
     return cells
 
 
-def shifted(block, axis, distance):
+def gathered(block, axis, source):
     count = lax.axis_size(axis)
-    route = [(i + distance, i) for i in range(count) if 0 <= i + distance < count]
+    route = [(source(i, count), i) for i in range(count) if source(i, count) is not None]
     return lax.ppermute(block, axis, route)
 
 
-def swapped(block, axis):
-    count = lax.axis_size(axis)
-    return lax.ppermute(block, axis, [(i, i ^ 1) for i in range(count)])
+def within(i, n):
+    return i if 0 <= i < n else None
 
 
 def kernel_table():
@@ -169,14 +168,22 @@
     date = lax.axis_index("date")
     even = date % 2 == 0
 
-    left_2 = shifted(own_left, "date", 2)
-    left_1 = swapped(jnp.where(even, left_2, own_left), "date")
-    left_4 = shifted(left_2, "date", 2)
-    left_3 = shifted(left_1, "date", 2)
-    right_2 = shifted(own_right, "date", -2)
-    right_1 = swapped(jnp.where(even, own_right, right_2), "date")
-    right_4 = shifted(right_2, "date", -2)
-    right_3 = shifted(right_1, "date", -2)
+    left_2 = gathered(own_left, "date", lambda i, n: within(i + 2, n))
+    right_2 = gathered(own_right, "date", lambda i, n: within(i - 2, n))
+    pair_own = gathered(jnp.where(even, own_right, own_left), "date", lambda i, n: i ^ 1)
+    left_4 = gathered(left_2, "date", lambda i, n: within(i + 2, n) if i + 4 < n else None)
+    right_4 = gathered(right_2, "date", lambda i, n: within(i - 2, n) if i >= 4 else None)
+    pair_relay = gathered(jnp.where(even, left_2, right_2), "date", lambda i, n: i ^ 1)
+    third_own = gathered(
+        pair_own, "date", lambda i, n: (i + 2 if i + 3 < n else None) if i % 2 == 0 else (i - 2 if i >= 3 else None)
+    )
+    third_relay = gathered(
+        pair_relay, "date", lambda i, n: (i + 2 if i + 3 < n else None) if i % 2 == 1 else (i - 2 if i >= 3 else None)
+    )
+    left_1 = jnp.where(even, pair_own, pair_relay)
+    right_1 = jnp.where(even, pair_relay, pair_own)
+    left_3 = jnp.where(even, third_own, third_relay)
+    right_3 = jnp.where(even, third_relay, third_own)
 
     ahead = dict(zip((1, 2, 3, 4), looks(own_left, [left_1, left_2, left_3, left_4])))
     behind = dict(zip((1, 2, 3, 4), looks(own_right, [right_1, right_2, right_3, right_4])))

time: 225 us -> 234 us (1.040)
  starting transfers between devices: 30.4 us -> 53.7 us
  waiting for transfers between devices: 96.3 us -> 77.7 us
  other arithmetic: 16.3 us -> 19.8 us
    all_to_all x1, starting transfers between devices: 5.13 us -> 34.2 us  [shards(): got = lax.all_to_all(sent, 'date', 0, 0, tiled=True)]
    ppermute x8, waiting for transfers between devices: 96.3 us -> 77.7 us  [gathered(): return lax.ppermute(block, axis, route)]
    ppermute x8, starting transfers between devices: 21.6 us -> 15.9 us  [gathered(): return lax.ppermute(block, axis, route)]
    select_n x2 -> x4, other arithmetic: 4.24 us -> 7.72 us  [the longest x1 2.79 us: shards(): jnp.where(even, own_right, own_left)]
  transfers between devices with their start and end apart: 11 -> 11, of which waited for: 6 -> 5; matrix products, arithmetic and copies ran while one was open for 6% -> 7% of each run, Pallas kernels for 3% -> 3%
where the time goes in v12:
time: 234 us; the launch traced here: 233 us
  waiting for transfers between devices  77.7 us (33%)
  starting transfers between devices  53.7 us (23%)
  Pallas kernels  46.7 us (20%)
  between operations  20.7 us (9%)
  other arithmetic  19.8 us (8%)
  local copies, waits for them, and re-layouts  14.4 us (6%)
    ppermute x8, waiting for transfers between devices, gathered(): return lax.ppermute(block, axis, route)  77.7 us
    all_to_all x1, starting transfers between devices, shards(): got = lax.all_to_all(sent, 'date', 0, 0, tiled=True)  34.2 us
    pallas_call x1, Pallas kernels, resample_block(): pl.pallas_call(resample_kernel, grid=(2, nlines // ROWS), in_specs=[pl.Bl...  33.2 us
    ppermute x8, starting transfers between devices, gathered(): return lax.ppermute(block, axis, route)  15.9 us
    pallas_call x2, Pallas kernels, looks(): pl.pallas_call(looks_kernel, grid=(width // CHUNK,), in_specs=[spec] * (c...  13.6 us
    slice x3, local copies, waits for them, and re-layouts, resample_block(): return (look_order(out[:, :, :half]), look_order(out[:, :, half:]))  4.72 us
  transfers between devices with their start and end apart: 11, of which 5 were waited for; matrix products, arithmetic and copies ran while one was open for 7% of the time, Pallas kernels for 3%

profile of v12, /device:TPU:0, one launch (start us, length us, event | category | flops | bytes accessed | tf_op | source)
XLA Modules:
  0.0 233.1 jit_solution(16883764335866449520)
XLA Ops:
  0.0 1.1 fusion.48
  1.1 2.4 %collective-permute-start = (bf16[1,2,16,4096]{3,2,1,0:T(8,128)(2,1)S(1)}, bf16[1,2,16,4096]{3,2,1,0:T(8,128)(2,1)S(1)}, u32[]{:S(2)}, u32[]{:S(2)}) collective-permute-start(bf16[1,2,16,4096]{3,2,1,0:T(8,128)(2,1)S(1)} %get-tuple-element.28), channel_id=1, source_target_pairs={{0,1},{1,2},{2,3},{4,5},{5,6},{6,7},{8,9},{9,10},{10,11},{12,13},{... | collective-permute-start | bytes 786440 | tf_op jit(solution)/shard_map/ppermute | solution.py:25
  3.4 1.3 collective-permute-start.1
  4.8 0.7 compare_select_fusion
  5.5 0.7 compare_and_fusion
  6.1 0.7 add_bitcast_fusion
  6.8 0.1 fusion.17
  8.3 0.1 copy.20
  8.3 0.8 fusion.14.weights_ref
  9.1 0.7 copy.21.shift_ref
  9.8 0.7 gather_fusion
  10.5 0.7 broadcast_select_fusion.6.coeff_ref
  11.2 0.0 collective-permute-done
  11.2 0.0 collective-permute-done.1
  11.2 3.5 %fusion.2 = bf16[2,167,4096]{2,1,0:T(8,128)(2,1)S(1)} fusion(s32[]{:T(128)S(6)} %select_n.560, bf16[1,2,16,4096]{3,2,1,0:T(8,128)(2,1)S(1)} %collective-permute-done, bf16[1,2,160,4096]{3,2,1,0:T(8,128)(2,1)} %param.6, bf16[1,2,16,4096]{3,2,1,0:T(8,128)(2,1)S(1)} %collective-permute-done.1), kind=kLoop, calls=%fused_computation.6 | loop fusion | flops 8208384 | bytes 5881860 | tf_op jit(solution)/shard_map/convert_element_type | solution.py:85
  14.7 3.1 %pad_convert_fusion.window_ref = f32[2,168,4096]{2,1,0:T(8,128)} fusion(bf16[2,167,4096]{2,1,0:T(8,128)(2,1)S(1)} %fusion.2), kind=kLoop, calls=%fused_computation.7 | loop fusion | flops 1376256 | bytes 8241152 | tf_op jit(solution)/shard_map/jit(_pad)/pad | solution.py:86
  17.8 33.2 %shard_map.64 = bf16[2,160,4096]{2,1,0:T(8,128)(2,1)} custom-call(f32[8]{0:T(128)} %fusion.14.weights_ref, f32[2,168,4096]{2,1,0:T(8,128)} %pad_convert_fusion.window_ref, f32[160,8]{1,0:T(8,128)} %broadcast_select_fusion.6.coeff_ref, s32[160,1]{1,0:T(8,128)} %copy.21.shift_ref), custom_call_target="tpu_custom_call" | custom-call | flops 78643200 | bytes 7864320 | tf_op jit(solution)/shard_map/pallas_call | solution.py:90
  51.0 2.0 fusion.47
  53.0 1.3 copy.22
  54.3 1.3 copy.24
  55.7 1.8 copy.32
  57.5 1.3 collective-permute-start.2
  58.8 1.8 copy.33
  60.6 6.0 %collective-permute-start.3 = (bf16[2,160,2048]{2,1,0:T(8,128)(2,1)}, bf16[2,160,2048]{2,1,0:T(8,128)(2,1)}, u32[]{:S(2)}, u32[]{:S(2)}) collective-permute-start(bf16[2,160,2048]{2,1,0:T(8,128)(2,1)} %bitcast.88.first_ref), channel_id=1, source_target_pairs={{0,8},{4,12},{8,16},{12,20},{16,24},{20,28},{1,9},{5,13},{9,17},{1... | collective-permute-start | bytes 3932168 | tf_op jit(solution)/shard_map/ppermute | solution.py:37
  66.6 2.8 %broadcast_select_fusion.4 = bf16[2,160,2048]{2,1,0:T(8,128)(2,1)S(1)} fusion(pred[]{:T(512)S(6)} %eq.193, bf16[2,20,8,2048]{3,0,1,2:T(2,128)(2,1)S(1)} %bitcast.93, bf16[2,20,8,2048]{3,0,1,2:T(2,128)(2,1)S(1)} %bitcast.95), kind=kLoop, calls=%fused_computation.14 | loop fusion | flops 655360 | bytes 3932161 | tf_op jit(solution)/shard_map/jit(_where)/select_n | solution.py:173
  69.4 2.0 collective-permute-start.5
  71.4 18.5 %collective-permute-done.2.refs_1_ = bf16[2,160,2048]{2,1,0:T(8,128)(2,1)} collective-permute-done((bf16[2,160,2048]{2,1,0:T(8,128)(2,1)}, bf16[2,160,2048]{2,1,0:T(8,128)(2,1)}, u32[]{:S(2)}, u32[]{:S(2)}) %collective-permute-start.2) | collective-permute-done | bytes 1310752 | tf_op jit(solution)/shard_map/ppermute | solution.py:37
  89.9 3.5 %collective-permute-done.3.refs_1_ = bf16[2,160,2048]{2,1,0:T(8,128)(2,1)} collective-permute-done((bf16[2,160,2048]{2,1,0:T(8,128)(2,1)}, bf16[2,160,2048]{2,1,0:T(8,128)(2,1)}, u32[]{:S(2)}, u32[]{:S(2)}) %collective-permute-start.3) | collective-permute-done | bytes 1310752 | tf_op jit(solution)/shard_map/ppermute | solution.py:37
  93.4 1.5 broadcast_select_fusion.5
  94.9 2.5 %collective-permute-start.4 = (bf16[2,160,2048]{2,1,0:T(8,128)(2,1)S(1)}, bf16[2,160,2048]{2,1,0:T(8,128)(2,1)S(1)}, u32[]{:S(2)}, u32[]{:S(2)}) collective-permute-start(bf16[2,160,2048]{2,1,0:T(8,128)(2,1)S(1)} %broadcast_select_fusion.5), channel_id=1, source_target_pairs={{4,0},{0,4},{12,8},{8,12},{20,16},{16,20},{28,24},{24,28},{5,1},{1... | collective-permute-start | bytes 3932168 | tf_op jit(solution)/shard_map/ppermute | solution.py:37
  97.3 2.5 %collective-permute-done.5 = bf16[2,160,2048]{2,1,0:T(8,128)(2,1)S(1)} collective-permute-done((bf16[2,160,2048]{2,1,0:T(8,128)(2,1)S(1)}, bf16[2,160,2048]{2,1,0:T(8,128)(2,1)S(1)}, u32[]{:S(2)}, u32[]{:S(2)}) %collective-permute-start.5) | collective-permute-done | bytes 1310752 | tf_op jit(solution)/shard_map/ppermute | solution.py:37
  99.8 1.3 collective-permute-start.7
  101.1 26.8 %collective-permute-done.4 = bf16[2,160,2048]{2,1,0:T(8,128)(2,1)S(1)} collective-permute-done((bf16[2,160,2048]{2,1,0:T(8,128)(2,1)S(1)}, bf16[2,160,2048]{2,1,0:T(8,128)(2,1)S(1)}, u32[]{:S(2)}, u32[]{:S(2)}) %collective-permute-start.4) | collective-permute-done | bytes 1310752 | tf_op jit(solution)/shard_map/ppermute | solution.py:37
  127.9 0.7 collective-permute-start.6
  128.7 0.7 collective-permute-start.8
  129.4 1.3 collective-permute-start.9
  130.8 1.8 broadcast_select_fusion.3
  132.6 0.0 collective-permute-done.7
  132.6 0.0 collective-permute-done.6
  132.6 1.7 broadcast_select_fusion.2
  134.2 0.0 collective-permute-done.8.refs_3_
  134.3 1.1 copy-done.1
  135.3 6.8 %shard_map.65 = (f32[2,8,512]{2,1,0:T(8,128)}, f32[2,8,512]{2,1,0:T(8,128)}, f32[2,8,512]{2,1,0:T(8,128)}, f32[2,8,512]{2,1,0:T(8,128)}) custom-call(bf16[2,160,2048]{2,1,0:T(8,128)(2,1)} %bitcast.88.first_ref, bf16[2,160,2048]{2,1,0:T(8,128)(2,1)} %get-tuple-element.23.refs_0_, bf16[2,160,2048]{2,1,0:T(8,128)(2,1)} %collective-permute-done.3.refs_1_, ...), custom_call_target="tpu_custom_call" | custom-call | flops 52428800 | bytes 6553600 | tf_op jit(solution)/shard_map/pallas_call | solution.py:143
  142.1 26.4 %collective-permute-done.9.refs_3_ = bf16[2,160,2048]{2,1,0:T(8,128)(2,1)S(1)} collective-permute-done((bf16[2,160,2048]{2,1,0:T(8,128)(2,1)}, bf16[2,160,2048]{2,1,0:T(8,128)(2,1)S(1)}, u32[]{:S(2)}, u32[]{:S(2)}) %collective-permute-start.9) | collective-permute-done | bytes 1310752 | tf_op jit(solution)/shard_map/ppermute | solution.py:37
  168.5 0.0 copy-start
  168.5 1.1 copy-done
  169.6 0.0 copy-start.10
  169.6 6.8 %shard_map.66 = (f32[2,8,512]{2,1,0:T(8,128)}, f32[2,8,512]{2,1,0:T(8,128)}, f32[2,8,512]{2,1,0:T(8,128)}, f32[2,8,512]{2,1,0:T(8,128)}) custom-call(bf16[2,160,2048]{2,1,0:T(8,128)(2,1)} %bitcast.87.first_ref, bf16[2,160,2048]{2,1,0:T(8,128)(2,1)} %get-tuple-element.24.refs_0_, bf16[2,160,2048]{2,1,0:T(8,128)(2,1)} %collective-permute-done.2.refs_1_, ...), custom_call_target="tpu_custom_call" | custom-call | flops 52428800 | bytes 6553600 | tf_op jit(solution)/shard_map/pallas_call | solution.py:143
  176.4 0.0 copy-start.8
  176.4 0.0 copy-start.9
  176.4 0.0 copy-done.2
  176.4 0.0 copy-done.3
  176.4 0.0 copy-done.4
  176.5 0.0 copy-done.5
  176.5 1.7 select_select_fusion
  178.1 34.2 %all-to-all-start = ((f32[8,2,8,512]{3,2,1,0:T(8,128)}), f32[8,2,8,512]{3,2,1,0:T(8,128)S(1)}, u32[]{:S(2)}, u32[]{:S(2)}) async-start(f32[8,2,8,512]{3,2,1,0:T(8,128)} %select_select_fusion), calls=%async_computation | async-start | bytes 524288 | tf_op jit(solution)/shard_map/all_to_all | solution.py:196
  212.3 0.0 copy-done.10
  212.4 0.7 fusion.49
  232.0 0.0 all-to-all-done
  232.2 0.0 copy-done.6
  232.2 0.0 copy-done.7
  232.2 0.0 copy-done.8
  232.2 0.0 copy-done.9
  232.4 0.7 maximum_bitcast_fusion
  (27 shorter events, 0.3 us)
Async XLA Ops:
  1.1 10.2 %collective-permute-start = (bf16[1,2,16,4096]{3,2,1,0:T(8,128)(2,1)S(1)}, bf16[1,2,16,4096]{3,2,1,0:T(8,128)(2,1)S(1)}, u32[]{:S(2)}, u32[]{:S(2)}) collective-permute-start(bf16[1,2,16,4096]{3,2,1,0:T(8,128)(2,1)S(1)} %get-tuple-element.28), channel_id=1, source_target_pairs={{0,1},{1,2},{2,3},{4,5},{5,6},{6,7},{8,9},{9,10},{10,11},{12,13},{... | collective-permute-start | bytes 786440 | tf_op jit(solution)/shard_map/ppermute | solution.py:25
  3.4 7.8 %collective-permute-start.1 = (bf16[1,2,16,4096]{3,2,1,0:T(8,128)(2,1)S(1)}, bf16[1,2,16,4096]{3,2,1,0:T(8,128)(2,1)S(1)}, u32[]{:S(2)}, u32[]{:S(2)}) collective-permute-start(bf16[1,2,16,4096]{3,2,1,0:T(8,128)(2,1)S(1)} %get-tuple-element.27), channel_id=1, source_target_pairs={{1,0},{2,1},{3,2},{5,4},{6,5},{7,6},{9,8},{10,9},{11,10},{13,12},{... | collective-permute-start | bytes 786440 | tf_op jit(solution)/shard_map/ppermute | solution.py:27
  57.5 32.4 %collective-permute-start.2 = (bf16[2,160,2048]{2,1,0:T(8,128)(2,1)}, bf16[2,160,2048]{2,1,0:T(8,128)(2,1)}, u32[]{:S(2)}, u32[]{:S(2)}) collective-permute-start(bf16[2,160,2048]{2,1,0:T(8,128)(2,1)} %bitcast.87.first_ref), channel_id=1, source_target_pairs={{8,0},{12,4},{16,8},{20,12},{24,16},{28,20},{9,1},{13,5},{17,9},{2... | collective-permute-start | bytes 3932168 | tf_op jit(solution)/shard_map/ppermute | solution.py:37
  60.6 32.8 %collective-permute-start.3 = (bf16[2,160,2048]{2,1,0:T(8,128)(2,1)}, bf16[2,160,2048]{2,1,0:T(8,128)(2,1)}, u32[]{:S(2)}, u32[]{:S(2)}) collective-permute-start(bf16[2,160,2048]{2,1,0:T(8,128)(2,1)} %bitcast.88.first_ref), channel_id=1, source_target_pairs={{0,8},{4,12},{8,16},{12,20},{16,24},{20,28},{1,9},{5,13},{9,17},{1... | collective-permute-start | bytes 3932168 | tf_op jit(solution)/shard_map/ppermute | solution.py:37
  69.4 30.4 %collective-permute-start.5 = (bf16[2,160,2048]{2,1,0:T(8,128)(2,1)S(1)}, bf16[2,160,2048]{2,1,0:T(8,128)(2,1)S(1)}, u32[]{:S(2)}, u32[]{:S(2)}) collective-permute-start(bf16[2,160,2048]{2,1,0:T(8,128)(2,1)S(1)} %broadcast_select_fusion.4), channel_id=1, source_target_pairs={{4,0},{0,4},{12,8},{8,12},{20,16},{16,20},{28,24},{24,28},{5,1},{1... | collective-permute-start | bytes 3932168 | tf_op jit(solution)/shard_map/ppermute | solution.py:37
  94.9 33.0 %collective-permute-start.4 = (bf16[2,160,2048]{2,1,0:T(8,128)(2,1)S(1)}, bf16[2,160,2048]{2,1,0:T(8,128)(2,1)S(1)}, u32[]{:S(2)}, u32[]{:S(2)}) collective-permute-start(bf16[2,160,2048]{2,1,0:T(8,128)(2,1)S(1)} %broadcast_select_fusion.5), channel_id=1, source_target_pairs={{4,0},{0,4},{12,8},{8,12},{20,16},{16,20},{28,24},{24,28},{5,1},{1... | collective-permute-start | bytes 3932168 | tf_op jit(solution)/shard_map/ppermute | solution.py:37
  99.8 32.8 %collective-permute-start.7 = (bf16[2,160,2048]{2,1,0:T(8,128)(2,1)S(1)}, bf16[2,160,2048]{2,1,0:T(8,128)(2,1)S(1)}, u32[]{:S(2)}, u32[]{:S(2)}) collective-permute-start(bf16[2,160,2048]{2,1,0:T(8,128)(2,1)S(1)} %collective-permute-done.5), channel_id=1, source_target_pairs={{8,0},{16,8},{4,12},{24,16},{12,20},{20,28},{9,1},{17,9},{5,13},{2... | collective-permute-start | bytes 3932168 | tf_op jit(solution)/shard_map/ppermute | solution.py:37
  127.9 4.7 %collective-permute-start.6 = (bf16[2,160,2048]{2,1,0:T(8,128)(2,1)S(1)}, bf16[2,160,2048]{2,1,0:T(8,128)(2,1)S(1)}, u32[]{:S(2)}, u32[]{:S(2)}) collective-permute-start(bf16[2,160,2048]{2,1,0:T(8,128)(2,1)S(1)} %collective-permute-done.4), channel_id=1, source_target_pairs={{12,4},{20,12},{8,16},{16,24},{13,5},{21,13},{9,17},{17,25},{14,6}... | collective-permute-start | bytes 3932168 | tf_op jit(solution)/shard_map/ppermute | solution.py:37
  128.7 5.6 %collective-permute-start.8 = (bf16[2,160,2048]{2,1,0:T(8,128)(2,1)}, bf16[2,160,2048]{2,1,0:T(8,128)(2,1)S(1)}, u32[]{:S(2)}, u32[]{:S(2)}) collective-permute-start(bf16[2,160,2048]{2,1,0:T(8,128)(2,1)} %collective-permute-done.3.refs_1_), channel_id=1, source_target_pairs={{8,16},{12,20},{16,24},{20,28},{9,17},{13,21},{17,25},{21,29},{10,... | collective-permute-start | bytes 3932168 | tf_op jit(solution)/shard_map/ppermute | solution.py:37
  129.4 39.1 %collective-permute-start.9 = (bf16[2,160,2048]{2,1,0:T(8,128)(2,1)}, bf16[2,160,2048]{2,1,0:T(8,128)(2,1)S(1)}, u32[]{:S(2)}, u32[]{:S(2)}) collective-permute-start(bf16[2,160,2048]{2,1,0:T(8,128)(2,1)} %collective-permute-done.2.refs_1_), channel_id=1, source_target_pairs={{8,0},{12,4},{16,8},{20,12},{9,1},{13,5},{17,9},{21,13},{10,2},{14... | collective-permute-start | bytes 3932168 | tf_op jit(solution)/shard_map/ppermute | solution.py:37
  134.3 1.1 copy-start.1
  168.5 1.1 copy-start
  169.6 6.9 %copy-start.2 = (f32[2,8,512]{2,1,0:T(8,128)S(1)}, f32[2,8,512]{2,1,0:T(8,128)}, u32[]{:S(2)}) copy-start(f32[2,8,512]{2,1,0:T(8,128)} %get-tuple-element.19) | copy-start | bytes 98308
  169.6 6.9 %copy-start.3 = (f32[2,8,512]{2,1,0:T(8,128)S(1)}, f32[2,8,512]{2,1,0:T(8,128)}, u32[]{:S(2)}) copy-start(f32[2,8,512]{2,1,0:T(8,128)} %get-tuple-element.17) | copy-start | bytes 98308
  169.6 6.9 %copy-start.4 = (f32[2,8,512]{2,1,0:T(8,128)S(1)}, f32[2,8,512]{2,1,0:T(8,128)}, u32[]{:S(2)}) copy-start(f32[2,8,512]{2,1,0:T(8,128)} %get-tuple-element.15) | copy-start | bytes 98308
  169.6 6.9 %copy-start.5 = (f32[2,8,512]{2,1,0:T(8,128)S(1)}, f32[2,8,512]{2,1,0:T(8,128)}, u32[]{:S(2)}) copy-start(f32[2,8,512]{2,1,0:T(8,128)} %get-tuple-element.13) | copy-start | bytes 98308
  169.6 42.8 %copy-start.10 = (s32[1,4]{1,0:T(1,128)S(1)}, s32[1,4]{1,0:T(1,128)}, u32[]{:S(2)}) copy-start(s32[1,4]{1,0:T(1,128)} %param.11) | copy-start | bytes 52
  176.4 55.8 %copy-start.6 = (f32[2,8,512]{2,1,0:T(8,128)S(1)}, f32[2,8,512]{2,1,0:T(8,128)}, u32[]{:S(2)}) copy-start(f32[2,8,512]{2,1,0:T(8,128)} %get-tuple-element.20) | copy-start | bytes 98308
  176.4 55.8 %copy-start.7 = (f32[2,8,512]{2,1,0:T(8,128)S(1)}, f32[2,8,512]{2,1,0:T(8,128)}, u32[]{:S(2)}) copy-start(f32[2,8,512]{2,1,0:T(8,128)} %get-tuple-element.18) | copy-start | bytes 98308
  176.4 55.8 %copy-start.8 = (f32[2,8,512]{2,1,0:T(8,128)S(1)}, f32[2,8,512]{2,1,0:T(8,128)}, u32[]{:S(2)}) copy-start(f32[2,8,512]{2,1,0:T(8,128)} %get-tuple-element.16) | copy-start | bytes 98308
  176.4 55.8 %copy-start.9 = (f32[2,8,512]{2,1,0:T(8,128)S(1)}, f32[2,8,512]{2,1,0:T(8,128)}, u32[]{:S(2)}) copy-start(f32[2,8,512]{2,1,0:T(8,128)} %get-tuple-element.14) | copy-start | bytes 98308
  178.1 53.9 %all-to-all-start = ((f32[8,2,8,512]{3,2,1,0:T(8,128)}), f32[8,2,8,512]{3,2,1,0:T(8,128)S(1)}, u32[]{:S(2)}, u32[]{:S(2)}) async-start(f32[8,2,8,512]{3,2,1,0:T(8,128)} %select_select_fusion), calls=%async_computation | async-start | bytes 524288 | tf_op jit(solution)/shard_map/all_to_all | solution.py:196

commit v13 on v9

--- a/solution.py
+++ b/solution.py
@@ -1,3 +1,5 @@
+import functools
+
 import jax
 import jax.numpy as jnp
 from jax import lax
@@ -53,16 +55,18 @@
 EDGE = 128
 
 
-def resample_kernel(weights_ref, window_ref, coeff_ref, shift_ref, out_ref):
+def resample_kernel(side, weights_ref, window_ref, coeff_ref, shift_ref, out_ref):
     step = pl.program_id(1)
     first = pl.multiple_of(step * ROWS, ROWS)
-    window = window_ref[0, pl.ds(first, ROWS + 8), :]
+    half = out_ref.shape[2]
+    low = max(side * half - EDGE, 0)
+    high = min(side * half + half + EDGE, window_ref.shape[2])
+    window = window_ref[0, pl.ds(first, ROWS + 8), low:high]
     along = weights_ref[0] * window[0:ROWS, :]
     for tap in range(1, 8):
         along = along + weights_ref[tap] * window[tap : tap + ROWS, :]
-    nrange = along.shape[1]
     zeros = jnp.zeros((ROWS, EDGE), jnp.float32)
-    row = jnp.concatenate([zeros, along, zeros], axis=1)
+    row = jnp.concatenate([zeros, along] if side == 0 else [along, zeros], axis=1)
     width = row.shape[1]
     shift = shift_ref[...]
     for bit in range(5):
@@ -71,16 +75,35 @@
     coeff = coeff_ref[...]
     result = None
     for tap in range(8):
-        moved = pltpu.roll(row, width - (EDGE - 15 + tap), 1)[:, :nrange]
+        moved = pltpu.roll(row, width - (EDGE - 15 + tap), 1)[:, :half]
         term = coeff[:, tap : tap + 1] * moved
         result = term if result is None else result + term
     out_ref[0] = result.astype(out_ref.dtype)
 
 
+def resample_half(side, weights, window, coeff, shift):
+    nlines = coeff.shape[0]
+    half = window.shape[2] // 2
+    return pl.pallas_call(
+        functools.partial(resample_kernel, side),
+        grid=(2, nlines // ROWS),
+        in_specs=[
+            pl.BlockSpec(memory_space=pltpu.SMEM),
+            pl.BlockSpec((1,) + window.shape[1:], lambda c, t: (c, 0, 0)),
+            pl.BlockSpec((ROWS, 8), lambda c, t: (t, 0)),
+            pl.BlockSpec((ROWS, 1), lambda c, t: (t, 0)),
+        ],
+        out_specs=pl.BlockSpec((1, ROWS, half), lambda c, t: (c, t, 0)),
+        out_shape=jax.ShapeDtypeStruct((2, nlines, half), jnp.bfloat16),
+        cost_estimate=pl.CostEstimate(
+            flops=2 * nlines * half * 60, transcendentals=0, bytes_accessed=2 * nlines * half * 6
+        ),
+    )(weights, window, coeff, shift)
+
+
 def resample_block(padded, shift_lines, kern_lines, shift_range, kern_range):
     table = kernel_table()
     nlines = shift_range.shape[0]
-    nrange = padded.shape[2]
     border = OFFAZ + 4
     start = border + shift_lines - 3
     window = lax.dynamic_slice_in_dim(padded, start, nlines + 7, 1).astype(jnp.float32)
@@ -88,23 +111,9 @@
     weights = table[kern_lines]
     coeff = jnp.take(table, kern_range, axis=0)
     shift = (shift_range + OFFRG)[:, None]
-    out = pl.pallas_call(
-        resample_kernel,
-        grid=(2, nlines // ROWS),
-        in_specs=[
-            pl.BlockSpec(memory_space=pltpu.SMEM),
-            pl.BlockSpec((1, nlines + 8, nrange), lambda c, t: (c, 0, 0)),
-            pl.BlockSpec((ROWS, 8), lambda c, t: (t, 0)),
-            pl.BlockSpec((ROWS, 1), lambda c, t: (t, 0)),
-        ],
-        out_specs=pl.BlockSpec((1, ROWS, nrange), lambda c, t: (c, t, 0)),
-        out_shape=jax.ShapeDtypeStruct((2, nlines, nrange), jnp.bfloat16),
-        cost_estimate=pl.CostEstimate(
-            flops=2 * nlines * nrange * 60, transcendentals=0, bytes_accessed=2 * nlines * nrange * 6
-        ),
-    )(weights, window, coeff, shift)
-    half = nrange // 2
-    return look_order(out[:, :, :half]), look_order(out[:, :, half:])
+    left = look_order(resample_half(0, weights, window, coeff, shift))
+    right = look_order(resample_half(1, weights, window, coeff, shift))
+    return left, right
 
 
 CHUNK = 512

time: 221 us -> 210 us (0.950)
  waiting for transfers between devices: 68.3 us -> 48.8 us
  Pallas kernels: 68.1 us -> 75.9 us
    ppermute x2, waiting for transfers between devices: 44.5 us -> 20 us  [swapped(): return lax.ppermute(block, axis, [(i, i ^ 1) for i in range(count)])]
    pallas_call x1 -> x2, Pallas kernels: 33.2 us -> 40.9 us  [resample_half(): pl.pallas_call(functools.partial(resample_kernel, side), grid=(2, nlines...]
    pallas_call x0 -> x2, local copies, waits for them, and re-layouts: none -> 5.33 us  [resample_half(): pl.pallas_call(functools.partial(resample_kernel, side), grid=(2, nlines...]
    ppermute x6, waiting for transfers between devices: 23.8 us -> 28.8 us  [shifted(): return lax.ppermute(block, axis, route)]
    slice x3 -> x0, local copies, waits for them, and re-layouts: 4.72 us -> none  [resample_block(): return (look_order(out[:, :, :half]), look_order(out[:, :, half:]))]
    all_to_all x1, starting transfers between devices: 3.41 us -> 6.5 us  [shards(): got = lax.all_to_all(sent, 'date', 0, 0, tiled=True)]
    ppermute x6, starting transfers between devices: 22.1 us -> 19.2 us  [shifted(): return lax.ppermute(block, axis, route)]
  transfers between devices with their start and end apart: 11 -> 11, of which waited for: 3 -> 5; matrix products, arithmetic and copies ran while one was open for 6% -> 7% of each run, Pallas kernels for 14% -> 25%
where the time goes in v13:
time: 210 us; the launch traced here: 208 us
  Pallas kernels  75.9 us (36%)
  waiting for transfers between devices  48.8 us (23%)
  starting transfers between devices  32.3 us (15%)
  between operations  21.8 us (10%)
  other arithmetic  17.7 us (8%)
  local copies, waits for them, and re-layouts  11.4 us (5%)
    pallas_call x2, Pallas kernels, resample_half(): pl.pallas_call(functools.partial(resample_kernel, side), grid=(2, nlines...  40.9 us
    pallas_call x8, Pallas kernels, looks(): pl.pallas_call(looks_kernel, grid=(width // CHUNK,), in_specs=[spec, spec...  34.9 us
    ppermute x6, waiting for transfers between devices, shifted(): return lax.ppermute(block, axis, route)  28.8 us
    ppermute x2, waiting for transfers between devices, swapped(): return lax.ppermute(block, axis, [(i, i ^ 1) for i in range(count)])  20 us
    ppermute x6, starting transfers between devices, shifted(): return lax.ppermute(block, axis, route)  19.2 us
    all_to_all x1, starting transfers between devices, shards(): got = lax.all_to_all(sent, 'date', 0, 0, tiled=True)  6.5 us
    pallas_call x2, local copies, waits for them, and re-layouts, resample_half(): pl.pallas_call(functools.partial(resample_kernel, side), grid=(2, nlines...  5.33 us
  transfers between devices with their start and end apart: 11, of which 5 were waited for; matrix products, arithmetic and copies ran while one was open for 7% of the time, Pallas kernels for 25%

profile of v13, /device:TPU:0, one launch (start us, length us, event | category | flops | bytes accessed | tf_op | source)
XLA Modules:
  0.0 207.8 jit_solution(5441051674412004945)
XLA Ops:
  0.0 1.1 fusion.47
  1.1 1.3 collective-permute-start.1
  2.4 3.0 %collective-permute-start = (bf16[1,2,16,4096]{3,2,1,0:T(8,128)(2,1)S(1)}, bf16[1,2,16,4096]{3,2,1,0:T(8,128)(2,1)S(1)}, u32[]{:S(2)}, u32[]{:S(2)}) collective-permute-start(bf16[1,2,16,4096]{3,2,1,0:T(8,128)(2,1)S(1)} %get-tuple-element.6), channel_id=1, source_target_pairs={{0,1},{1,2},{2,3},{4,5},{5,6},{6,7},{8,9},{9,10},{10,11},{12,13},{... | collective-permute-start | bytes 786440 | tf_op jit(solution)/shard_map/ppermute | solution.py:27
  5.4 0.7 compare_select_fusion
  6.1 0.7 compare_and_fusion
  6.8 0.7 add_bitcast_fusion
  7.5 0.1 fusion.17
  8.9 0.1 copy.22
  9.0 0.7 fusion.14.weights_ref
  9.7 0.7 copy.23.shift_ref
  10.4 0.7 gather_fusion
  11.1 0.7 broadcast_select_fusion.2.coeff_ref
  11.8 0.0 collective-permute-done.1
  11.9 0.0 collective-permute-done
  11.9 3.5 %fusion.2 = bf16[2,167,4096]{2,1,0:T(8,128)(2,1)S(1)} fusion(s32[]{:T(128)S(6)} %select_n.544, bf16[1,2,16,4096]{3,2,1,0:T(8,128)(2,1)S(1)} %collective-permute-done, bf16[1,2,160,4096]{3,2,1,0:T(8,128)(2,1)} %param.6, bf16[1,2,16,4096]{3,2,1,0:T(8,128)(2,1)S(1)} %collective-permute-done.1), kind=kLoop, calls=%fused_computation.6 | loop fusion | flops 8208384 | bytes 5881860 | tf_op jit(solution)/shard_map/convert_element_type | solution.py:109
  15.4 3.0 %pad_convert_fusion.window_ref = f32[2,168,4096]{2,1,0:T(8,128)} fusion(bf16[2,167,4096]{2,1,0:T(8,128)(2,1)S(1)} %fusion.2), kind=kLoop, calls=%fused_computation.7 | loop fusion | flops 1376256 | bytes 8241152 | tf_op jit(solution)/shard_map/jit(_pad)/pad | solution.py:110
  18.4 20.5 %shard_map.64 = bf16[2,160,2048]{2,1,0:T(8,128)(2,1)} custom-call(f32[8]{0:T(128)} %fusion.14.weights_ref, f32[2,168,4096]{2,1,0:T(8,128)} %pad_convert_fusion.window_ref, f32[160,8]{1,0:T(8,128)} %broadcast_select_fusion.2.coeff_ref, s32[160,1]{1,0:T(8,128)} %copy.23.shift_ref), custom_call_target="tpu_custom_call" | custom-call | flops 39321600 | bytes 3932160 | tf_op jit(solution)/shard_map/pallas_call | solution.py:87
  38.9 2.7 %copy.24 = bf16[2,160,2048]{2,0,1:T(2,128)(2,1)S(1)} copy(bf16[2,160,2048]{2,1,0:T(8,128)(2,1)} %shard_map.64) | data formatting | bytes 2621440 | tf_op jit(solution)/shard_map/pallas_call | solution.py:87
  41.6 0.0 copy-start.2
  41.6 0.7 copy.36
  42.3 0.3 copy-done.2
  42.7 6.0 %collective-permute-start.2 = (bf16[2,160,2048]{2,1,0:T(8,128)(2,1)S(1)}, bf16[2,160,2048]{2,1,0:T(8,128)(2,1)}, u32[]{:S(2)}, u32[]{:S(2)}) collective-permute-start(bf16[2,160,2048]{2,1,0:T(8,128)(2,1)S(1)} %bitcast.92), channel_id=1, source_target_pairs={{0,8},{4,12},{8,16},{12,20},{16,24},{20,28},{1,9},{5,13},{9,17},{1... | collective-permute-start | bytes 3932168 | tf_op jit(solution)/shard_map/ppermute | solution.py:39
  48.7 20.4 %shard_map.66 = bf16[2,160,2048]{2,1,0:T(8,128)(2,1)} custom-call(f32[8]{0:T(128)} %fusion.14.weights_ref, f32[2,168,4096]{2,1,0:T(8,128)} %pad_convert_fusion.window_ref, f32[160,8]{1,0:T(8,128)} %broadcast_select_fusion.2.coeff_ref, s32[160,1]{1,0:T(8,128)} %copy.23.shift_ref), custom_call_target="tpu_custom_call" | custom-call | flops 39321600 | bytes 3932160 | tf_op jit(solution)/shard_map/pallas_call | solution.py:87
  69.1 0.0 copy-done
  69.1 2.7 %copy.27 = bf16[2,160,2048]{2,0,1:T(2,128)(2,1)S(1)} copy(bf16[2,160,2048]{2,1,0:T(8,128)(2,1)} %shard_map.66) | data formatting | bytes 2621440 | tf_op jit(solution)/shard_map/pallas_call | solution.py:87
  71.8 0.0 copy-start.3
  71.8 0.7 copy.35
  72.5 0.3 copy-done.3
  72.8 1.5 collective-permute-start.4
  74.3 0.0 copy-start.4
  74.3 2.3 %collective-permute-done.2.second_ref = bf16[2,160,2048]{2,1,0:T(8,128)(2,1)} collective-permute-done((bf16[2,160,2048]{2,1,0:T(8,128)(2,1)S(1)}, bf16[2,160,2048]{2,1,0:T(8,128)(2,1)}, u32[]{:S(2)}, u32[]{:S(2)}) %collective-permute-start.2) | collective-permute-done | bytes 1310752 | tf_op jit(solution)/shard_map/ppermute | solution.py:39
  76.6 2.8 %broadcast_select_fusion.1 = bf16[2,160,2048]{2,1,0:T(8,128)(2,1)S(1)} fusion(bf16[2,160,2048]{2,1,0:T(8,128)(2,1)} %collective-permute-done.2.second_ref, pred[]{:T(512)S(6)} %eq.195, bf16[2,20,8,2048]{3,0,1,2:T(2,128)(2,1)} %bitcast.103), kind=kLoop, calls=%fused_computation.11 | loop fusion | flops 655360 | bytes 3932161 | tf_op jit(solution)/shard_map/jit(_where)/select_n | solution.py:181
  79.4 2.0 collective-permute-start.6
  81.4 24.9 %collective-permute-done.4.second_ref = bf16[2,160,2048]{2,1,0:T(8,128)(2,1)} collective-permute-done((bf16[2,160,2048]{2,1,0:T(8,128)(2,1)S(1)}, bf16[2,160,2048]{2,1,0:T(8,128)(2,1)}, u32[]{:S(2)}, u32[]{:S(2)}) %collective-permute-start.4) | collective-permute-done | bytes 1310752 | tf_op jit(solution)/shard_map/ppermute | solution.py:39
  106.3 0.0 copy-done.4
  106.3 2.8 %broadcast_select_fusion = bf16[2,160,2048]{2,1,0:T(8,128)(2,1)S(1)} fusion(bf16[2,160,2048]{2,1,0:T(8,128)(2,1)} %collective-permute-done.4.second_ref, pred[]{:T(512)S(6)} %eq.195, bf16[2,20,8,2048]{3,0,1,2:T(2,128)(2,1)S(1)} %bitcast.105), kind=kLoop, calls=%fused_computation.10 | loop fusion | flops 655360 | bytes 3932161 | tf_op jit(solution)/shard_map/jit(_where)/select_n | solution.py:177
  109.1 0.3 collective-permute-start.8
  109.4 3.5 %collective-permute-start.3 = (bf16[2,160,2048]{2,1,0:T(8,128)(2,1)}, bf16[2,160,2048]{2,1,0:T(8,128)(2,1)}, u32[]{:S(2)}, u32[]{:S(2)}) collective-permute-start(bf16[2,160,2048]{2,1,0:T(8,128)(2,1)} %collective-permute-done.2.second_ref), channel_id=1, source_target_pairs={{0,8},{4,12},{8,16},{12,20},{16,24},{20,28},{1,9},{5,13},{9,17},{1... | collective-permute-start | bytes 3932168 | tf_op jit(solution)/shard_map/ppermute | solution.py:39
  112.9 1.3 collective-permute-start.5
  114.2 0.0 collective-permute-done.6.second_ref
  114.2 5.6 %collective-permute-start.7 = (bf16[2,160,2048]{2,1,0:T(8,128)(2,1)S(1)}, bf16[2,160,2048]{2,1,0:T(8,128)(2,1)}, u32[]{:S(2)}, u32[]{:S(2)}) collective-permute-start(bf16[2,160,2048]{2,1,0:T(8,128)(2,1)S(1)} %collective-permute-done.6.second_ref), channel_id=1, source_target_pairs={{0,8},{4,12},{8,16},{12,20},{16,24},{20,28},{1,9},{5,13},{9,17},{1... | collective-permute-start | bytes 3932168 | tf_op jit(solution)/shard_map/ppermute | solution.py:39
  119.9 20.0 %collective-permute-done.8.second_ref = bf16[2,160,2048]{2,1,0:T(8,128)(2,1)S(1)} collective-permute-done((bf16[2,160,2048]{2,1,0:T(8,128)(2,1)S(1)}, bf16[2,160,2048]{2,1,0:T(8,128)(2,1)S(1)}, u32[]{:S(2)}, u32[]{:S(2)}) %collective-permute-start.8) | collective-permute-done | bytes 1310752 | tf_op jit(solution)/shard_map/ppermute | solution.py:44
  139.8 1.3 collective-permute-start.9
  141.2 4.4 %shard_map.70 = f32[2,8,512]{2,1,0:T(8,128)} custom-call(bf16[2,160,2048]{2,1,0:T(8,128)(2,1)} %bitcast.93, bf16[2,160,2048]{2,1,0:T(8,128)(2,1)} %collective-permute-done.2.second_ref), custom_call_target="tpu_custom_call" | custom-call | flops 13107200 | bytes 2621440 | tf_op jit(solution)/shard_map/pallas_call | solution.py:148
  145.6 4.4 %shard_map.71 = f32[2,8,512]{2,1,0:T(8,128)} custom-call(bf16[2,160,2048]{2,1,0:T(8,128)(2,1)} %bitcast.98, bf16[2,160,2048]{2,1,0:T(8,128)(2,1)} %collective-permute-done.4.second_ref), custom_call_target="tpu_custom_call" | custom-call | flops 13107200 | bytes 2621440 | tf_op jit(solution)/shard_map/pallas_call | solution.py:148
  149.9 4.4 %shard_map.72 = f32[2,8,512]{2,1,0:T(8,128)} custom-call(bf16[2,160,2048]{2,1,0:T(8,128)(2,1)} %bitcast.94, bf16[2,160,2048]{2,1,0:T(8,128)(2,1)} %copy-done.5), custom_call_target="tpu_custom_call" | custom-call | flops 13107200 | bytes 2621440 | tf_op jit(solution)/shard_map/pallas_call | solution.py:148
  154.3 4.4 %shard_map.73 = f32[2,8,512]{2,1,0:T(8,128)} custom-call(bf16[2,160,2048]{2,1,0:T(8,128)(2,1)} %bitcast.99, bf16[2,160,2048]{2,1,0:T(8,128)(2,1)} %copy-done.6), custom_call_target="tpu_custom_call" | custom-call | flops 13107200 | bytes 2621440 | tf_op jit(solution)/shard_map/pallas_call | solution.py:148
  158.7 0.0 collective-permute-done.3.second_ref
  158.7 4.4 %shard_map.65 = f32[2,8,512]{2,1,0:T(8,128)} custom-call(bf16[2,160,2048]{2,1,0:T(8,128)(2,1)} %bitcast.95, bf16[2,160,2048]{2,1,0:T(8,128)(2,1)} %collective-permute-done.3.second_ref), custom_call_target="tpu_custom_call" | custom-call | flops 13107200 | bytes 2621440 | tf_op jit(solution)/shard_map/pallas_call | solution.py:148
  163.0 0.0 collective-permute-done.5.second_ref
  163.0 4.4 %shard_map.67 = f32[2,8,512]{2,1,0:T(8,128)} custom-call(bf16[2,160,2048]{2,1,0:T(8,128)(2,1)} %bitcast.100, bf16[2,160,2048]{2,1,0:T(8,128)(2,1)} %collective-permute-done.5.second_ref), custom_call_target="tpu_custom_call" | custom-call | flops 13107200 | bytes 2621440 | tf_op jit(solution)/shard_map/pallas_call | solution.py:148
  167.4 0.7 collective-permute-done.7.second_ref
  168.1 4.4 %shard_map.68 = f32[2,8,512]{2,1,0:T(8,128)} custom-call(bf16[2,160,2048]{2,1,0:T(8,128)(2,1)} %bitcast.96, bf16[2,160,2048]{2,1,0:T(8,128)(2,1)} %collective-permute-done.7.second_ref), custom_call_target="tpu_custom_call" | custom-call | flops 13107200 | bytes 2621440 | tf_op jit(solution)/shard_map/pallas_call | solution.py:148
  172.4 0.0 copy-start.10
  172.5 0.0 copy-start.15
  172.5 0.9 collective-permute-done.9.second_ref
  173.4 4.4 %shard_map.69 = f32[2,8,512]{2,1,0:T(8,128)} custom-call(bf16[2,160,2048]{2,1,0:T(8,128)(2,1)} %bitcast.101, bf16[2,160,2048]{2,1,0:T(8,128)(2,1)} %collective-permute-done.9.second_ref), custom_call_target="tpu_custom_call" | custom-call | flops 13107200 | bytes 2621440 | tf_op jit(solution)/shard_map/pallas_call | solution.py:148
  177.7 0.0 copy-done.7
  177.8 1.6 select_select_fusion
  179.4 6.5 %all-to-all-start = ((f32[8,2,8,512]{3,2,1,0:T(8,128)}), f32[8,2,8,512]{3,2,1,0:T(8,128)S(1)}, u32[]{:S(2)}, u32[]{:S(2)}) async-start(f32[8,2,8,512]{3,2,1,0:T(8,128)} %select_select_fusion), calls=%async_computation | async-start | bytes 524288 | tf_op jit(solution)/shard_map/all_to_all | solution.py:203
  185.9 0.7 fusion.48
  206.8 0.0 all-to-all-done
  206.9 0.0 copy-done.14
  207.1 0.7 maximum_bitcast_fusion
  (41 shorter events, 0.3 us)
Async XLA Ops:
  1.1 10.8 %collective-permute-start.1 = (bf16[1,2,16,4096]{3,2,1,0:T(8,128)(2,1)S(1)}, bf16[1,2,16,4096]{3,2,1,0:T(8,128)(2,1)S(1)}, u32[]{:S(2)}, u32[]{:S(2)}) collective-permute-start(bf16[1,2,16,4096]{3,2,1,0:T(8,128)(2,1)S(1)} %get-tuple-element.5), channel_id=1, source_target_pairs={{1,0},{2,1},{3,2},{5,4},{6,5},{7,6},{9,8},{10,9},{11,10},{13,12},{... | collective-permute-start | bytes 786440 | tf_op jit(solution)/shard_map/ppermute | solution.py:29
  2.4 9.5 %collective-permute-start = (bf16[1,2,16,4096]{3,2,1,0:T(8,128)(2,1)S(1)}, bf16[1,2,16,4096]{3,2,1,0:T(8,128)(2,1)S(1)}, u32[]{:S(2)}, u32[]{:S(2)}) collective-permute-start(bf16[1,2,16,4096]{3,2,1,0:T(8,128)(2,1)S(1)} %get-tuple-element.6), channel_id=1, source_target_pairs={{0,1},{1,2},{2,3},{4,5},{5,6},{6,7},{8,9},{9,10},{10,11},{12,13},{... | collective-permute-start | bytes 786440 | tf_op jit(solution)/shard_map/ppermute | solution.py:27
  41.6 1.1 copy-start.2
  42.7 26.4 %copy-start = (bf16[2,20,8,2048]{3,2,1,0:T(8,128)(2,1)}, bf16[2,20,8,2048]{3,2,1,0:T(8,128)(2,1)S(1)}, u32[]{:S(2)}) copy-start(bf16[2,20,8,2048]{3,2,1,0:T(8,128)(2,1)S(1)} %copy.36) | copy-start | bytes 3932164
  42.7 33.9 %collective-permute-start.2 = (bf16[2,160,2048]{2,1,0:T(8,128)(2,1)S(1)}, bf16[2,160,2048]{2,1,0:T(8,128)(2,1)}, u32[]{:S(2)}, u32[]{:S(2)}) collective-permute-start(bf16[2,160,2048]{2,1,0:T(8,128)(2,1)S(1)} %bitcast.92), channel_id=1, source_target_pairs={{0,8},{4,12},{8,16},{12,20},{16,24},{20,28},{1,9},{5,13},{9,17},{1... | collective-permute-start | bytes 3932168 | tf_op jit(solution)/shard_map/ppermute | solution.py:39
  71.8 1.1 copy-start.3
  72.8 6.6 %copy-start.1 = (bf16[2,20,8,2048]{3,2,1,0:T(8,128)(2,1)}, bf16[2,20,8,2048]{3,2,1,0:T(8,128)(2,1)S(1)}, u32[]{:S(2)}) copy-start(bf16[2,20,8,2048]{3,2,1,0:T(8,128)(2,1)S(1)} %copy.35) | copy-start | bytes 3932164
  72.8 33.5 %collective-permute-start.4 = (bf16[2,160,2048]{2,1,0:T(8,128)(2,1)S(1)}, bf16[2,160,2048]{2,1,0:T(8,128)(2,1)}, u32[]{:S(2)}, u32[]{:S(2)}) collective-permute-start(bf16[2,160,2048]{2,1,0:T(8,128)(2,1)S(1)} %bitcast.97), channel_id=1, source_target_pairs={{8,0},{12,4},{16,8},{20,12},{24,16},{28,20},{9,1},{13,5},{17,9},{2... | collective-permute-start | bytes 3932168 | tf_op jit(solution)/shard_map/ppermute | solution.py:39
  74.3 32.0 %copy-start.4 = (bf16[2,160,2048]{2,0,1:T(2,128)(2,1)S(1)}, bf16[2,160,2048]{2,0,1:T(2,128)(2,1)}, u32[]{:S(2)}) copy-start(bf16[2,160,2048]{2,0,1:T(2,128)(2,1)} %copy-done.3) | copy-start | bytes 3932164
  79.4 34.8 %collective-permute-start.6 = (bf16[2,160,2048]{2,1,0:T(8,128)(2,1)S(1)}, bf16[2,160,2048]{2,1,0:T(8,128)(2,1)S(1)}, u32[]{:S(2)}, u32[]{:S(2)}) collective-permute-start(bf16[2,160,2048]{2,1,0:T(8,128)(2,1)S(1)} %broadcast_select_fusion.1), channel_id=1, source_target_pairs={{0,4},{4,0},{8,12},{12,8},{16,20},{20,16},{24,28},{28,24},{1,5},{5... | collective-permute-start | bytes 3932168 | tf_op jit(solution)/shard_map/ppermute | solution.py:44
  109.1 30.7 %collective-permute-start.8 = (bf16[2,160,2048]{2,1,0:T(8,128)(2,1)S(1)}, bf16[2,160,2048]{2,1,0:T(8,128)(2,1)S(1)}, u32[]{:S(2)}, u32[]{:S(2)}) collective-permute-start(bf16[2,160,2048]{2,1,0:T(8,128)(2,1)S(1)} %broadcast_select_fusion), channel_id=1, source_target_pairs={{0,4},{4,0},{8,12},{12,8},{16,20},{20,16},{24,28},{28,24},{1,5},{5... | collective-permute-start | bytes 3932168 | tf_op jit(solution)/shard_map/ppermute | solution.py:44
  109.4 49.3 %collective-permute-start.3 = (bf16[2,160,2048]{2,1,0:T(8,128)(2,1)}, bf16[2,160,2048]{2,1,0:T(8,128)(2,1)}, u32[]{:S(2)}, u32[]{:S(2)}) collective-permute-start(bf16[2,160,2048]{2,1,0:T(8,128)(2,1)} %collective-permute-done.2.second_ref), channel_id=1, source_target_pairs={{0,8},{4,12},{8,16},{12,20},{16,24},{20,28},{1,9},{5,13},{9,17},{1... | collective-permute-start | bytes 3932168 | tf_op jit(solution)/shard_map/ppermute | solution.py:39
  112.9 50.1 %collective-permute-start.5 = (bf16[2,160,2048]{2,1,0:T(8,128)(2,1)}, bf16[2,160,2048]{2,1,0:T(8,128)(2,1)}, u32[]{:S(2)}, u32[]{:S(2)}) collective-permute-start(bf16[2,160,2048]{2,1,0:T(8,128)(2,1)} %collective-permute-done.4.second_ref), channel_id=1, source_target_pairs={{8,0},{12,4},{16,8},{20,12},{24,16},{28,20},{9,1},{13,5},{17,9},{2... | collective-permute-start | bytes 3932168 | tf_op jit(solution)/shard_map/ppermute | solution.py:39
  114.2 31.4 %copy-start.5 = (bf16[2,160,2048]{2,1,0:T(8,128)(2,1)}, bf16[2,160,2048]{2,1,0:T(8,128)(2,1)S(1)}, u32[]{:S(2)}) copy-start(bf16[2,160,2048]{2,1,0:T(8,128)(2,1)S(1)} %collective-permute-done.6.second_ref) | copy-start | bytes 3932164
  114.2 53.9 %collective-permute-start.7 = (bf16[2,160,2048]{2,1,0:T(8,128)(2,1)S(1)}, bf16[2,160,2048]{2,1,0:T(8,128)(2,1)}, u32[]{:S(2)}, u32[]{:S(2)}) collective-permute-start(bf16[2,160,2048]{2,1,0:T(8,128)(2,1)S(1)} %collective-permute-done.6.second_ref), channel_id=1, source_target_pairs={{0,8},{4,12},{8,16},{12,20},{16,24},{20,28},{1,9},{5,13},{9,17},{1... | collective-permute-start | bytes 3932168 | tf_op jit(solution)/shard_map/ppermute | solution.py:39
  139.8 5.7 %copy-start.6 = (bf16[2,160,2048]{2,1,0:T(8,128)(2,1)}, bf16[2,160,2048]{2,1,0:T(8,128)(2,1)S(1)}, u32[]{:S(2)}) copy-start(bf16[2,160,2048]{2,1,0:T(8,128)(2,1)S(1)} %collective-permute-done.8.second_ref) | copy-start | bytes 3932164
  139.8 33.5 %collective-permute-start.9 = (bf16[2,160,2048]{2,1,0:T(8,128)(2,1)S(1)}, bf16[2,160,2048]{2,1,0:T(8,128)(2,1)}, u32[]{:S(2)}, u32[]{:S(2)}) collective-permute-start(bf16[2,160,2048]{2,1,0:T(8,128)(2,1)S(1)} %collective-permute-done.8.second_ref), channel_id=1, source_target_pairs={{8,0},{12,4},{16,8},{20,12},{24,16},{28,20},{9,1},{13,5},{17,9},{2... | collective-permute-start | bytes 3932168 | tf_op jit(solution)/shard_map/ppermute | solution.py:39
  172.4 5.3 %copy-start.7 = (f32[2,8,512]{2,1,0:T(8,128)S(1)}, f32[2,8,512]{2,1,0:T(8,128)}, u32[]{:S(2)}) copy-start(f32[2,8,512]{2,1,0:T(8,128)} %shard_map.70) | copy-start | bytes 98308
  172.4 5.3 %copy-start.8 = (f32[2,8,512]{2,1,0:T(8,128)S(1)}, f32[2,8,512]{2,1,0:T(8,128)}, u32[]{:S(2)}) copy-start(f32[2,8,512]{2,1,0:T(8,128)} %shard_map.71) | copy-start | bytes 98308
  172.4 5.3 %copy-start.9 = (f32[2,8,512]{2,1,0:T(8,128)S(1)}, f32[2,8,512]{2,1,0:T(8,128)}, u32[]{:S(2)}) copy-start(f32[2,8,512]{2,1,0:T(8,128)} %shard_map.72) | copy-start | bytes 98308
  172.4 5.3 %copy-start.10 = (f32[2,8,512]{2,1,0:T(8,128)S(1)}, f32[2,8,512]{2,1,0:T(8,128)}, u32[]{:S(2)}) copy-start(f32[2,8,512]{2,1,0:T(8,128)} %shard_map.73) | copy-start | bytes 98308
  172.5 5.3 %copy-start.11 = (f32[2,8,512]{2,1,0:T(8,128)S(1)}, f32[2,8,512]{2,1,0:T(8,128)}, u32[]{:S(2)}) copy-start(f32[2,8,512]{2,1,0:T(8,128)} %shard_map.65) | copy-start | bytes 98308
  172.5 5.3 %copy-start.12 = (f32[2,8,512]{2,1,0:T(8,128)S(1)}, f32[2,8,512]{2,1,0:T(8,128)}, u32[]{:S(2)}) copy-start(f32[2,8,512]{2,1,0:T(8,128)} %shard_map.67) | copy-start | bytes 98308
  172.5 5.3 %copy-start.13 = (f32[2,8,512]{2,1,0:T(8,128)S(1)}, f32[2,8,512]{2,1,0:T(8,128)}, u32[]{:S(2)}) copy-start(f32[2,8,512]{2,1,0:T(8,128)} %shard_map.68) | copy-start | bytes 98308
  172.5 13.4 %copy-start.15 = (s32[1,4]{1,0:T(1,128)S(1)}, s32[1,4]{1,0:T(1,128)}, u32[]{:S(2)}) copy-start(s32[1,4]{1,0:T(1,128)} %param.11) | copy-start | bytes 52
  177.7 29.2 %copy-start.14 = (f32[2,8,512]{2,1,0:T(8,128)S(1)}, f32[2,8,512]{2,1,0:T(8,128)}, u32[]{:S(2)}) copy-start(f32[2,8,512]{2,1,0:T(8,128)} %shard_map.69) | copy-start | bytes 98308
  179.4 27.3 %all-to-all-start = ((f32[8,2,8,512]{3,2,1,0:T(8,128)}), f32[8,2,8,512]{3,2,1,0:T(8,128)S(1)}, u32[]{:S(2)}, u32[]{:S(2)}) async-start(f32[8,2,8,512]{3,2,1,0:T(8,128)} %select_select_fusion), calls=%async_computation | async-start | bytes 524288 | tf_op jit(solution)/shard_map/all_to_all | solution.py:203

commit v14 on v13

--- a/solution.py
+++ b/solution.py
@@ -176,24 +176,19 @@
     left_2 = shifted(own_left, "date", 2)
     left_1 = swapped(jnp.where(even, left_2, own_left), "date")
     left_4 = shifted(left_2, "date", 2)
-    left_3 = shifted(left_1, "date", 2)
     right_2 = shifted(own_right, "date", -2)
     right_1 = swapped(jnp.where(even, own_right, right_2), "date")
     right_4 = shifted(right_2, "date", -2)
+    ahead = {2: looks(own_left, left_2)}
+    behind = {2: looks(own_right, right_2)}
+    left_1, ahead[2] = lax.optimization_barrier((left_1, ahead[2]))
+    right_1, behind[2] = lax.optimization_barrier((right_1, behind[2]))
+    left_3 = shifted(left_1, "date", 2)
     right_3 = shifted(right_1, "date", -2)
-
-    ahead = {
-        1: looks(own_left, left_1),
-        2: looks(own_left, left_2),
-        3: looks(own_left, left_3),
-        4: looks(own_left, left_4),
-    }
-    behind = {
-        1: looks(own_right, right_1),
-        2: looks(own_right, right_2),
-        3: looks(own_right, right_3),
-        4: looks(own_right, right_4),
-    }
+    for s, other in ((1, left_1), (4, left_4), (3, left_3)):
+        ahead[s] = looks(own_left, other)
+    for s, other in ((1, right_1), (4, right_4), (3, right_3)):
+        behind[s] = looks(own_right, other)
     count = lax.axis_size("date")
     target = lax.broadcasted_iota(jnp.int32, (count, 1, 1, 1), 0) - date
     sent = jnp.zeros((count,) + ahead[1].shape, jnp.float32)

time: 210 us -> 209 us (level)
  local copies, waits for them, and re-layouts: 11.4 us -> 13.7 us
    ppermute x6, waiting for transfers between devices: 28.8 us -> 36.6 us  [shifted(): return lax.ppermute(block, axis, route)]
    ppermute x2, waiting for transfers between devices: 20 us -> 12.5 us  [swapped(): return lax.ppermute(block, axis, [(i, i ^ 1) for i in range(count)])]
    unnamed x32, local copies, waits for them, and re-layouts: 0.71 us -> 2.95 us
  transfers between devices with their start and end apart: 11 -> 11, of which waited for: 5 -> 4; matrix products, arithmetic and copies ran while one was open for 7% -> 7% of each run, Pallas kernels for 25% -> 25%
where the time goes in v14:
time: 209 us; the launch traced here: 208 us
  Pallas kernels  75.9 us (36%)
  waiting for transfers between devices  49.1 us (23%)
  starting transfers between devices  30.5 us (15%)
  between operations  20.7 us (10%)
  other arithmetic  17.7 us (8%)
  local copies, waits for them, and re-layouts  13.7 us (7%)
    pallas_call x2, Pallas kernels, resample_half(): pl.pallas_call(functools.partial(resample_kernel, side), grid=(2, nlines...  41 us
    ppermute x6, waiting for transfers between devices, shifted(): return lax.ppermute(block, axis, route)  36.6 us
    pallas_call x8, Pallas kernels, looks(): pl.pallas_call(looks_kernel, grid=(width // CHUNK,), in_specs=[spec, spec...  35 us
    ppermute x6, starting transfers between devices, shifted(): return lax.ppermute(block, axis, route)  18.1 us
    ppermute x2, waiting for transfers between devices, swapped(): return lax.ppermute(block, axis, [(i, i ^ 1) for i in range(count)])  12.5 us
    all_to_all x1, starting transfers between devices, shards(): got = lax.all_to_all(sent, 'date', 0, 0, tiled=True)  5.81 us
    pallas_call x2, local copies, waits for them, and re-layouts, resample_half(): pl.pallas_call(functools.partial(resample_kernel, side), grid=(2, nlines...  5.33 us
  transfers between devices with their start and end apart: 11, of which 4 were waited for; matrix products, arithmetic and copies ran while one was open for 7% of the time, Pallas kernels for 25%

profile of v14, /device:TPU:0, one launch (start us, length us, event | category | flops | bytes accessed | tf_op | source)
XLA Modules:
  0.0 207.5 jit_solution(5062436820088950060)
XLA Ops:
  0.0 1.1 fusion.47
  1.1 1.3 collective-permute-start.1
  2.4 3.0 %collective-permute-start = (bf16[1,2,16,4096]{3,2,1,0:T(8,128)(2,1)S(1)}, bf16[1,2,16,4096]{3,2,1,0:T(8,128)(2,1)S(1)}, u32[]{:S(2)}, u32[]{:S(2)}) collective-permute-start(bf16[1,2,16,4096]{3,2,1,0:T(8,128)(2,1)S(1)} %get-tuple-element.14), channel_id=1, source_target_pairs={{0,1},{1,2},{2,3},{4,5},{5,6},{6,7},{8,9},{9,10},{10,11},{12,13},{... | collective-permute-start | bytes 786440 | tf_op jit(solution)/shard_map/ppermute | solution.py:27
  5.4 0.7 compare_select_fusion
  6.1 0.7 compare_and_fusion
  6.8 0.7 add_bitcast_fusion
  7.5 0.1 fusion.17
  8.9 0.1 copy.22
  9.0 0.7 fusion.14.weights_ref
  9.7 0.7 copy.23.shift_ref
  10.5 0.7 gather_fusion
  11.1 0.7 broadcast_select_fusion.2.coeff_ref
  11.9 0.0 collective-permute-done.1
  11.9 0.0 collective-permute-done
  11.9 3.5 %fusion.2 = bf16[2,167,4096]{2,1,0:T(8,128)(2,1)S(1)} fusion(s32[]{:T(128)S(6)} %select_n.544, bf16[1,2,16,4096]{3,2,1,0:T(8,128)(2,1)S(1)} %collective-permute-done, bf16[1,2,160,4096]{3,2,1,0:T(8,128)(2,1)} %param.6, bf16[1,2,16,4096]{3,2,1,0:T(8,128)(2,1)S(1)} %collective-permute-done.1), kind=kLoop, calls=%fused_computation.6 | loop fusion | flops 8208384 | bytes 5881860 | tf_op jit(solution)/shard_map/convert_element_type | solution.py:109
  15.4 3.1 %pad_convert_fusion.window_ref = f32[2,168,4096]{2,1,0:T(8,128)} fusion(bf16[2,167,4096]{2,1,0:T(8,128)(2,1)S(1)} %fusion.2), kind=kLoop, calls=%fused_computation.7 | loop fusion | flops 1376256 | bytes 8241152 | tf_op jit(solution)/shard_map/jit(_pad)/pad | solution.py:110
  18.5 20.5 %shard_map.64 = bf16[2,160,2048]{2,1,0:T(8,128)(2,1)} custom-call(f32[8]{0:T(128)} %fusion.14.weights_ref, f32[2,168,4096]{2,1,0:T(8,128)} %pad_convert_fusion.window_ref, f32[160,8]{1,0:T(8,128)} %broadcast_select_fusion.2.coeff_ref, s32[160,1]{1,0:T(8,128)} %copy.23.shift_ref), custom_call_target="tpu_custom_call" | custom-call | flops 39321600 | bytes 3932160 | tf_op jit(solution)/shard_map/pallas_call | solution.py:87
  39.0 2.7 %copy.24 = bf16[2,160,2048]{2,0,1:T(2,128)(2,1)S(1)} copy(bf16[2,160,2048]{2,1,0:T(8,128)(2,1)} %shard_map.64) | data formatting | bytes 2621440 | tf_op jit(solution)/shard_map/pallas_call | solution.py:87
  41.6 0.0 copy-start.2
  41.7 0.7 copy.36
  42.4 0.4 copy-done.2
  42.8 6.0 %collective-permute-start.2 = (bf16[2,160,2048]{2,1,0:T(8,128)(2,1)S(1)}, bf16[2,160,2048]{2,1,0:T(8,128)(2,1)}, u32[]{:S(2)}, u32[]{:S(2)}) collective-permute-start(bf16[2,160,2048]{2,1,0:T(8,128)(2,1)S(1)} %bitcast.92), channel_id=1, source_target_pairs={{0,8},{4,12},{8,16},{12,20},{16,24},{20,28},{1,9},{5,13},{9,17},{1... | collective-permute-start | bytes 3932168 | tf_op jit(solution)/shard_map/ppermute | solution.py:39
  48.8 20.4 %shard_map.66 = bf16[2,160,2048]{2,1,0:T(8,128)(2,1)} custom-call(f32[8]{0:T(128)} %fusion.14.weights_ref, f32[2,168,4096]{2,1,0:T(8,128)} %pad_convert_fusion.window_ref, f32[160,8]{1,0:T(8,128)} %broadcast_select_fusion.2.coeff_ref, s32[160,1]{1,0:T(8,128)} %copy.23.shift_ref), custom_call_target="tpu_custom_call" | custom-call | flops 39321600 | bytes 3932160 | tf_op jit(solution)/shard_map/pallas_call | solution.py:87
  69.3 0.0 copy-done
  69.3 2.7 %copy.27 = bf16[2,160,2048]{2,0,1:T(2,128)(2,1)S(1)} copy(bf16[2,160,2048]{2,1,0:T(8,128)(2,1)} %shard_map.66) | data formatting | bytes 2621440 | tf_op jit(solution)/shard_map/pallas_call | solution.py:87
  71.9 0.0 copy-start.3
  71.9 0.7 copy.35
  72.7 0.3 copy-done.3
  73.0 1.5 collective-permute-start.4
  74.5 0.0 copy-start.4
  74.5 2.2 %collective-permute-done.2.second_ref = bf16[2,160,2048]{2,1,0:T(8,128)(2,1)} collective-permute-done((bf16[2,160,2048]{2,1,0:T(8,128)(2,1)S(1)}, bf16[2,160,2048]{2,1,0:T(8,128)(2,1)}, u32[]{:S(2)}, u32[]{:S(2)}) %collective-permute-start.2) | collective-permute-done | bytes 1310752 | tf_op jit(solution)/shard_map/ppermute | solution.py:39
  76.7 2.8 %broadcast_select_fusion.1 = bf16[2,160,2048]{2,1,0:T(8,128)(2,1)S(1)} fusion(bf16[2,160,2048]{2,1,0:T(8,128)(2,1)} %collective-permute-done.2.second_ref, pred[]{:T(512)S(6)} %eq.195, bf16[2,20,8,2048]{3,0,1,2:T(2,128)(2,1)} %bitcast.103), kind=kLoop, calls=%fused_computation.11 | loop fusion | flops 655360 | bytes 3932161 | tf_op jit(solution)/shard_map/jit(_where)/select_n | solution.py:180
  79.5 0.0 copy-done.1
  79.5 2.0 collective-permute-start.6
  81.5 25.0 %collective-permute-done.4.second_ref = bf16[2,160,2048]{2,1,0:T(8,128)(2,1)} collective-permute-done((bf16[2,160,2048]{2,1,0:T(8,128)(2,1)S(1)}, bf16[2,160,2048]{2,1,0:T(8,128)(2,1)}, u32[]{:S(2)}, u32[]{:S(2)}) %collective-permute-start.4) | collective-permute-done | bytes 1310752 | tf_op jit(solution)/shard_map/ppermute | solution.py:39
  106.5 2.8 %broadcast_select_fusion = bf16[2,160,2048]{2,1,0:T(8,128)(2,1)S(1)} fusion(bf16[2,160,2048]{2,1,0:T(8,128)(2,1)} %collective-permute-done.4.second_ref, pred[]{:T(512)S(6)} %eq.195, bf16[2,20,8,2048]{3,0,1,2:T(2,128)(2,1)S(1)} %bitcast.105), kind=kLoop, calls=%fused_computation.10 | loop fusion | flops 655360 | bytes 3932161 | tf_op jit(solution)/shard_map/jit(_where)/select_n | solution.py:177
  109.3 0.3 collective-permute-start.8
  109.6 3.4 %collective-permute-start.3 = (bf16[2,160,2048]{2,1,0:T(8,128)(2,1)}, bf16[2,160,2048]{2,1,0:T(8,128)(2,1)}, u32[]{:S(2)}, u32[]{:S(2)}) collective-permute-start(bf16[2,160,2048]{2,1,0:T(8,128)(2,1)} %collective-permute-done.2.second_ref), channel_id=1, source_target_pairs={{0,8},{4,12},{8,16},{12,20},{16,24},{20,28},{1,9},{5,13},{9,17},{1... | collective-permute-start | bytes 3932168 | tf_op jit(solution)/shard_map/ppermute | solution.py:39
  113.0 1.3 collective-permute-start.5
  114.3 4.4 %shard_map.68 = f32[2,8,512]{2,1,0:T(8,128)} custom-call(bf16[2,160,2048]{2,1,0:T(8,128)(2,1)} %bitcast.93, bf16[2,160,2048]{2,1,0:T(8,128)(2,1)} %collective-permute-done.2.second_ref), custom_call_target="tpu_custom_call" | custom-call | flops 13107200 | bytes 2621440 | tf_op jit(solution)/shard_map/pallas_call | solution.py:148
  118.7 0.0 collective-permute-done.6.second_ref
  118.7 4.6 %collective-permute-start.7 = (bf16[2,160,2048]{2,1,0:T(8,128)(2,1)}, bf16[2,160,2048]{2,1,0:T(8,128)(2,1)S(1)}, u32[]{:S(2)}, u32[]{:S(2)}) collective-permute-start(bf16[2,160,2048]{2,1,0:T(8,128)(2,1)} %collective-permute-done.6.second_ref), channel_id=1, source_target_pairs={{0,8},{4,12},{8,16},{12,20},{16,24},{20,28},{1,9},{5,13},{9,17},{1... | collective-permute-start | bytes 3932168 | tf_op jit(solution)/shard_map/ppermute | solution.py:39
  123.3 4.4 %shard_map.70 = f32[2,8,512]{2,1,0:T(8,128)} custom-call(bf16[2,160,2048]{2,1,0:T(8,128)(2,1)} %bitcast.98, bf16[2,160,2048]{2,1,0:T(8,128)(2,1)} %collective-permute-done.4.second_ref), custom_call_target="tpu_custom_call" | custom-call | flops 13107200 | bytes 2621440 | tf_op jit(solution)/shard_map/pallas_call | solution.py:148
  127.7 12.5 %collective-permute-done.8.second_ref = bf16[2,160,2048]{2,1,0:T(8,128)(2,1)} collective-permute-done((bf16[2,160,2048]{2,1,0:T(8,128)(2,1)S(1)}, bf16[2,160,2048]{2,1,0:T(8,128)(2,1)}, u32[]{:S(2)}, u32[]{:S(2)}) %collective-permute-start.8) | collective-permute-done | bytes 1310752 | tf_op jit(solution)/shard_map/ppermute | solution.py:44
  140.1 1.3 collective-permute-start.9
  141.5 4.4 %shard_map.72 = f32[2,8,512]{2,1,0:T(8,128)} custom-call(bf16[2,160,2048]{2,1,0:T(8,128)(2,1)} %bitcast.94, bf16[2,160,2048]{2,1,0:T(8,128)(2,1)} %collective-permute-done.6.second_ref), custom_call_target="tpu_custom_call" | custom-call | flops 13107200 | bytes 2621440 | tf_op jit(solution)/shard_map/pallas_call | solution.py:148
  145.8 4.4 %shard_map.73 = f32[2,8,512]{2,1,0:T(8,128)} custom-call(bf16[2,160,2048]{2,1,0:T(8,128)(2,1)} %bitcast.99, bf16[2,160,2048]{2,1,0:T(8,128)(2,1)} %collective-permute-done.8.second_ref), custom_call_target="tpu_custom_call" | custom-call | flops 13107200 | bytes 2621440 | tf_op jit(solution)/shard_map/pallas_call | solution.py:148
  150.2 0.0 collective-permute-done.3.second_ref
  150.2 4.4 %shard_map.65 = f32[2,8,512]{2,1,0:T(8,128)} custom-call(bf16[2,160,2048]{2,1,0:T(8,128)(2,1)} %bitcast.95, bf16[2,160,2048]{2,1,0:T(8,128)(2,1)} %collective-permute-done.3.second_ref), custom_call_target="tpu_custom_call" | custom-call | flops 13107200 | bytes 2621440 | tf_op jit(solution)/shard_map/pallas_call | solution.py:148
  154.6 0.0 collective-permute-done.5.second_ref
  154.6 4.4 %shard_map.67 = f32[2,8,512]{2,1,0:T(8,128)} custom-call(bf16[2,160,2048]{2,1,0:T(8,128)(2,1)} %bitcast.100, bf16[2,160,2048]{2,1,0:T(8,128)(2,1)} %collective-permute-done.5.second_ref), custom_call_target="tpu_custom_call" | custom-call | flops 13107200 | bytes 2621440 | tf_op jit(solution)/shard_map/pallas_call | solution.py:148
  159.0 9.4 %collective-permute-done.7.second_ref = bf16[2,160,2048]{2,1,0:T(8,128)(2,1)S(1)} collective-permute-done((bf16[2,160,2048]{2,1,0:T(8,128)(2,1)}, bf16[2,160,2048]{2,1,0:T(8,128)(2,1)S(1)}, u32[]{:S(2)}, u32[]{:S(2)}) %collective-permute-start.7) | collective-permute-done | bytes 1310752 | tf_op jit(solution)/shard_map/ppermute | solution.py:39
  168.3 1.1 copy-done.5
  169.4 4.4 %shard_map.69 = f32[2,8,512]{2,1,0:T(8,128)} custom-call(bf16[2,160,2048]{2,1,0:T(8,128)(2,1)} %bitcast.96, bf16[2,160,2048]{2,1,0:T(8,128)(2,1)} %copy-done.5), custom_call_target="tpu_custom_call" | custom-call | flops 13107200 | bytes 2621440 | tf_op jit(solution)/shard_map/pallas_call | solution.py:148
  173.8 0.0 copy-start.10
  173.8 0.0 copy-start.15
  173.9 0.0 collective-permute-done.9.second_ref
  173.9 1.1 copy-done.6
  174.9 4.4 %shard_map.71 = f32[2,8,512]{2,1,0:T(8,128)} custom-call(bf16[2,160,2048]{2,1,0:T(8,128)(2,1)} %bitcast.101, bf16[2,160,2048]{2,1,0:T(8,128)(2,1)} %copy-done.6), custom_call_target="tpu_custom_call" | custom-call | flops 13107200 | bytes 2621440 | tf_op jit(solution)/shard_map/pallas_call | solution.py:148
  179.4 1.6 select_select_fusion
  181.0 5.8 %all-to-all-start = ((f32[8,2,8,512]{3,2,1,0:T(8,128)}), f32[8,2,8,512]{3,2,1,0:T(8,128)S(1)}, u32[]{:S(2)}, u32[]{:S(2)}) async-start(f32[8,2,8,512]{3,2,1,0:T(8,128)} %select_select_fusion), calls=%async_computation | async-start | bytes 524288 | tf_op jit(solution)/shard_map/all_to_all | solution.py:198
  186.8 0.7 fusion.48
  206.5 0.0 all-to-all-done
  206.8 0.7 maximum_bitcast_fusion
  (41 shorter events, 0.3 us)
Async XLA Ops:
  1.1 10.8 %collective-permute-start.1 = (bf16[1,2,16,4096]{3,2,1,0:T(8,128)(2,1)S(1)}, bf16[1,2,16,4096]{3,2,1,0:T(8,128)(2,1)S(1)}, u32[]{:S(2)}, u32[]{:S(2)}) collective-permute-start(bf16[1,2,16,4096]{3,2,1,0:T(8,128)(2,1)S(1)} %get-tuple-element.13), channel_id=1, source_target_pairs={{1,0},{2,1},{3,2},{5,4},{6,5},{7,6},{9,8},{10,9},{11,10},{13,12},{... | collective-permute-start | bytes 786440 | tf_op jit(solution)/shard_map/ppermute | solution.py:29
  2.4 9.5 %collective-permute-start = (bf16[1,2,16,4096]{3,2,1,0:T(8,128)(2,1)S(1)}, bf16[1,2,16,4096]{3,2,1,0:T(8,128)(2,1)S(1)}, u32[]{:S(2)}, u32[]{:S(2)}) collective-permute-start(bf16[1,2,16,4096]{3,2,1,0:T(8,128)(2,1)S(1)} %get-tuple-element.14), channel_id=1, source_target_pairs={{0,1},{1,2},{2,3},{4,5},{5,6},{6,7},{8,9},{9,10},{10,11},{12,13},{... | collective-permute-start | bytes 786440 | tf_op jit(solution)/shard_map/ppermute | solution.py:27
  41.6 1.1 copy-start.2
  42.8 26.5 %copy-start = (bf16[2,20,8,2048]{3,2,1,0:T(8,128)(2,1)}, bf16[2,20,8,2048]{3,2,1,0:T(8,128)(2,1)S(1)}, u32[]{:S(2)}) copy-start(bf16[2,20,8,2048]{3,2,1,0:T(8,128)(2,1)S(1)} %copy.36) | copy-start | bytes 3932164
  42.8 33.9 %collective-permute-start.2 = (bf16[2,160,2048]{2,1,0:T(8,128)(2,1)S(1)}, bf16[2,160,2048]{2,1,0:T(8,128)(2,1)}, u32[]{:S(2)}, u32[]{:S(2)}) collective-permute-start(bf16[2,160,2048]{2,1,0:T(8,128)(2,1)S(1)} %bitcast.92), channel_id=1, source_target_pairs={{0,8},{4,12},{8,16},{12,20},{16,24},{20,28},{1,9},{5,13},{9,17},{1... | collective-permute-start | bytes 3932168 | tf_op jit(solution)/shard_map/ppermute | solution.py:39
  71.9 1.1 copy-start.3
  73.0 6.5 %copy-start.1 = (bf16[2,20,8,2048]{3,2,1,0:T(8,128)(2,1)}, bf16[2,20,8,2048]{3,2,1,0:T(8,128)(2,1)S(1)}, u32[]{:S(2)}) copy-start(bf16[2,20,8,2048]{3,2,1,0:T(8,128)(2,1)S(1)} %copy.35) | copy-start | bytes 3932164
  73.0 33.5 %collective-permute-start.4 = (bf16[2,160,2048]{2,1,0:T(8,128)(2,1)S(1)}, bf16[2,160,2048]{2,1,0:T(8,128)(2,1)}, u32[]{:S(2)}, u32[]{:S(2)}) collective-permute-start(bf16[2,160,2048]{2,1,0:T(8,128)(2,1)S(1)} %bitcast.97), channel_id=1, source_target_pairs={{8,0},{12,4},{16,8},{20,12},{24,16},{28,20},{9,1},{13,5},{17,9},{2... | collective-permute-start | bytes 3932168 | tf_op jit(solution)/shard_map/ppermute | solution.py:39
  74.5 32.0 %copy-start.4 = (bf16[2,160,2048]{2,0,1:T(2,128)(2,1)S(1)}, bf16[2,160,2048]{2,0,1:T(2,128)(2,1)}, u32[]{:S(2)}) copy-start(bf16[2,160,2048]{2,0,1:T(2,128)(2,1)} %copy-done.3) | copy-start | bytes 3932164
  79.5 39.2 %collective-permute-start.6 = (bf16[2,160,2048]{2,1,0:T(8,128)(2,1)S(1)}, bf16[2,160,2048]{2,1,0:T(8,128)(2,1)}, u32[]{:S(2)}, u32[]{:S(2)}) collective-permute-start(bf16[2,160,2048]{2,1,0:T(8,128)(2,1)S(1)} %broadcast_select_fusion.1), channel_id=1, source_target_pairs={{0,4},{4,0},{8,12},{12,8},{16,20},{20,16},{24,28},{28,24},{1,5},{5... | collective-permute-start | bytes 3932168 | tf_op jit(solution)/shard_map/ppermute | solution.py:44
  109.3 30.8 %collective-permute-start.8 = (bf16[2,160,2048]{2,1,0:T(8,128)(2,1)S(1)}, bf16[2,160,2048]{2,1,0:T(8,128)(2,1)}, u32[]{:S(2)}, u32[]{:S(2)}) collective-permute-start(bf16[2,160,2048]{2,1,0:T(8,128)(2,1)S(1)} %broadcast_select_fusion), channel_id=1, source_target_pairs={{0,4},{4,0},{8,12},{12,8},{16,20},{20,16},{24,28},{28,24},{1,5},{5... | collective-permute-start | bytes 3932168 | tf_op jit(solution)/shard_map/ppermute | solution.py:44
  109.6 40.6 %collective-permute-start.3 = (bf16[2,160,2048]{2,1,0:T(8,128)(2,1)}, bf16[2,160,2048]{2,1,0:T(8,128)(2,1)}, u32[]{:S(2)}, u32[]{:S(2)}) collective-permute-start(bf16[2,160,2048]{2,1,0:T(8,128)(2,1)} %collective-permute-done.2.second_ref), channel_id=1, source_target_pairs={{0,8},{4,12},{8,16},{12,20},{16,24},{20,28},{1,9},{5,13},{9,17},{1... | collective-permute-start | bytes 3932168 | tf_op jit(solution)/shard_map/ppermute | solution.py:39
  113.0 41.6 %collective-permute-start.5 = (bf16[2,160,2048]{2,1,0:T(8,128)(2,1)}, bf16[2,160,2048]{2,1,0:T(8,128)(2,1)}, u32[]{:S(2)}, u32[]{:S(2)}) collective-permute-start(bf16[2,160,2048]{2,1,0:T(8,128)(2,1)} %collective-permute-done.4.second_ref), channel_id=1, source_target_pairs={{8,0},{12,4},{16,8},{20,12},{24,16},{28,20},{9,1},{13,5},{17,9},{2... | collective-permute-start | bytes 3932168 | tf_op jit(solution)/shard_map/ppermute | solution.py:39
  118.7 49.7 %collective-permute-start.7 = (bf16[2,160,2048]{2,1,0:T(8,128)(2,1)}, bf16[2,160,2048]{2,1,0:T(8,128)(2,1)S(1)}, u32[]{:S(2)}, u32[]{:S(2)}) collective-permute-start(bf16[2,160,2048]{2,1,0:T(8,128)(2,1)} %collective-permute-done.6.second_ref), channel_id=1, source_target_pairs={{0,8},{4,12},{8,16},{12,20},{16,24},{20,28},{1,9},{5,13},{9,17},{1... | collective-permute-start | bytes 3932168 | tf_op jit(solution)/shard_map/ppermute | solution.py:39
  140.1 33.7 %collective-permute-start.9 = (bf16[2,160,2048]{2,1,0:T(8,128)(2,1)}, bf16[2,160,2048]{2,1,0:T(8,128)(2,1)S(1)}, u32[]{:S(2)}, u32[]{:S(2)}) collective-permute-start(bf16[2,160,2048]{2,1,0:T(8,128)(2,1)} %collective-permute-done.8.second_ref), channel_id=1, source_target_pairs={{8,0},{12,4},{16,8},{20,12},{24,16},{28,20},{9,1},{13,5},{17,9},{2... | collective-permute-start | bytes 3932168 | tf_op jit(solution)/shard_map/ppermute | solution.py:39
  168.3 1.1 copy-start.5
  173.8 5.5 %copy-start.7 = (f32[2,8,512]{2,1,0:T(8,128)S(1)}, f32[2,8,512]{2,1,0:T(8,128)}, u32[]{:S(2)}) copy-start(f32[2,8,512]{2,1,0:T(8,128)} %shard_map.68) | copy-start | bytes 98308
  173.8 5.5 %copy-start.8 = (f32[2,8,512]{2,1,0:T(8,128)S(1)}, f32[2,8,512]{2,1,0:T(8,128)}, u32[]{:S(2)}) copy-start(f32[2,8,512]{2,1,0:T(8,128)} %shard_map.70) | copy-start | bytes 98308
  173.8 5.5 %copy-start.9 = (f32[2,8,512]{2,1,0:T(8,128)S(1)}, f32[2,8,512]{2,1,0:T(8,128)}, u32[]{:S(2)}) copy-start(f32[2,8,512]{2,1,0:T(8,128)} %shard_map.72) | copy-start | bytes 98308
  173.8 5.5 %copy-start.10 = (f32[2,8,512]{2,1,0:T(8,128)S(1)}, f32[2,8,512]{2,1,0:T(8,128)}, u32[]{:S(2)}) copy-start(f32[2,8,512]{2,1,0:T(8,128)} %shard_map.73) | copy-start | bytes 98308
  173.8 5.5 %copy-start.11 = (f32[2,8,512]{2,1,0:T(8,128)S(1)}, f32[2,8,512]{2,1,0:T(8,128)}, u32[]{:S(2)}) copy-start(f32[2,8,512]{2,1,0:T(8,128)} %shard_map.65) | copy-start | bytes 98308
  173.8 5.5 %copy-start.12 = (f32[2,8,512]{2,1,0:T(8,128)S(1)}, f32[2,8,512]{2,1,0:T(8,128)}, u32[]{:S(2)}) copy-start(f32[2,8,512]{2,1,0:T(8,128)} %shard_map.67) | copy-start | bytes 98308
  173.8 5.5 %copy-start.13 = (f32[2,8,512]{2,1,0:T(8,128)S(1)}, f32[2,8,512]{2,1,0:T(8,128)}, u32[]{:S(2)}) copy-start(f32[2,8,512]{2,1,0:T(8,128)} %shard_map.69) | copy-start | bytes 98308
  173.8 13.0 %copy-start.15 = (s32[1,4]{1,0:T(1,128)S(1)}, s32[1,4]{1,0:T(1,128)}, u32[]{:S(2)}) copy-start(s32[1,4]{1,0:T(1,128)} %param.11) | copy-start | bytes 52
  173.9 1.1 copy-start.6
  179.3 27.3 %copy-start.14 = (f32[2,8,512]{2,1,0:T(8,128)S(1)}, f32[2,8,512]{2,1,0:T(8,128)}, u32[]{:S(2)}) copy-start(f32[2,8,512]{2,1,0:T(8,128)} %shard_map.71) | copy-start | bytes 98308
  181.0 25.5 %all-to-all-start = ((f32[8,2,8,512]{3,2,1,0:T(8,128)}), f32[8,2,8,512]{3,2,1,0:T(8,128)S(1)}, u32[]{:S(2)}, u32[]{:S(2)}) async-start(f32[8,2,8,512]{3,2,1,0:T(8,128)} %select_select_fusion), calls=%async_computation | async-start | bytes 524288 | tf_op jit(solution)/shard_map/all_to_all | solution.py:198

commit v15 on v14

--- a/solution.py
+++ b/solution.py
@@ -192,14 +192,18 @@
     count = lax.axis_size("date")
     target = lax.broadcasted_iota(jnp.int32, (count, 1, 1, 1), 0) - date
     sent = jnp.zeros((count,) + ahead[1].shape, jnp.float32)
-    for s in range(1, GAP + 1):
+    for s in (1, 2, 4):
         sent = jnp.where(target == s, ahead[s][None], sent)
         sent = jnp.where(target == -s, behind[s][None], sent)
     got = lax.all_to_all(sent, "date", 0, 0, tiled=True)
     full = {}
     for s in range(1, GAP + 1):
-        right_of_ahead = conj(lax.dynamic_index_in_dim(got, jnp.minimum(date + s, count - 1), 0, keepdims=False))
-        left_of_behind = conj(lax.dynamic_index_in_dim(got, jnp.maximum(date - s, 0), 0, keepdims=False))
+        if s == 3:
+            right_of_ahead = conj(shifted(behind[s], "date", s))
+            left_of_behind = conj(shifted(ahead[s], "date", -s))
+        else:
+            right_of_ahead = conj(lax.dynamic_index_in_dim(got, jnp.minimum(date + s, count - 1), 0, keepdims=False))
+            left_of_behind = conj(lax.dynamic_index_in_dim(got, jnp.maximum(date - s, 0), 0, keepdims=False))
         full[s] = jnp.concatenate([ahead[s], right_of_ahead], axis=2)
         full[-s] = jnp.concatenate([left_of_behind, behind[s]], axis=2)
 

time: 209 us -> 214 us (1.024); the launches traced: 208 us -> 210 us
  starting transfers between devices: 30.5 us -> 39.6 us
  waiting for transfers between devices: 49.1 us -> 40.5 us
    ppermute x6 -> x8, starting transfers between devices: 18.1 us -> 26 us  [shifted(): return lax.ppermute(block, axis, route)]
    ppermute x6 -> x8, waiting for transfers between devices: 36.6 us -> 29.1 us  [shifted(): return lax.ppermute(block, axis, route)]
  transfers between devices with their start and end apart: 11 -> 13, of which waited for: 4 -> 4; matrix products, arithmetic and copies ran while one was open for 7% -> 8% of each run, Pallas kernels for 25% -> 26%
where the time goes in v15:
time: 214 us; the launch traced here: 210 us
  Pallas kernels  75.9 us (35%)
  waiting for transfers between devices  40.5 us (19%)
  starting transfers between devices  39.6 us (19%)
  between operations  22.4 us (10%)
  other arithmetic  19.2 us (9%)
  local copies, waits for them, and re-layouts  12.6 us (6%)
    pallas_call x2, Pallas kernels, resample_half(): pl.pallas_call(functools.partial(resample_kernel, side), grid=(2, nlines...  40.9 us
    pallas_call x8, Pallas kernels, looks(): pl.pallas_call(looks_kernel, grid=(width // CHUNK,), in_specs=[spec, spec...  35 us
    ppermute x8, waiting for transfers between devices, shifted(): return lax.ppermute(block, axis, route)  29.1 us
    ppermute x8, starting transfers between devices, shifted(): return lax.ppermute(block, axis, route)  26 us
    ppermute x2, waiting for transfers between devices, swapped(): return lax.ppermute(block, axis, [(i, i ^ 1) for i in range(count)])  11.4 us
    all_to_all x1, starting transfers between devices, shards(): got = lax.all_to_all(sent, 'date', 0, 0, tiled=True)  6.98 us
    pallas_call x2, local copies, waits for them, and re-layouts, resample_half(): pl.pallas_call(functools.partial(resample_kernel, side), grid=(2, nlines...  5.33 us
  transfers between devices with their start and end apart: 13, of which 4 were waited for; matrix products, arithmetic and copies ran while one was open for 8% of the time, Pallas kernels for 26%

profile of v15, /device:TPU:0, one launch (start us, length us, event | category | flops | bytes accessed | tf_op | source)
XLA Modules:
  0.0 210.2 jit_solution(2459044182403797551)
XLA Ops:
  0.0 1.1 fusion.42
  1.1 1.3 collective-permute-start.1
  2.4 3.0 %collective-permute-start = (bf16[1,2,16,4096]{3,2,1,0:T(8,128)(2,1)S(1)}, bf16[1,2,16,4096]{3,2,1,0:T(8,128)(2,1)S(1)}, u32[]{:S(2)}, u32[]{:S(2)}) collective-permute-start(bf16[1,2,16,4096]{3,2,1,0:T(8,128)(2,1)S(1)} %get-tuple-element.14), channel_id=1, source_target_pairs={{0,1},{1,2},{2,3},{4,5},{5,6},{6,7},{8,9},{9,10},{10,11},{12,13},{... | collective-permute-start | bytes 786440 | tf_op jit(solution)/shard_map/ppermute | solution.py:27
  5.4 0.7 compare_select_fusion
  6.1 0.7 compare_and_fusion
  6.8 0.7 add_bitcast_fusion
  7.5 0.1 fusion.14
  8.9 0.1 copy.22
  9.0 0.8 dynamic-slice_reduce_fusion.weights_ref
  9.8 0.7 copy.23.shift_ref
  10.5 0.7 gather_fusion
  11.2 0.7 broadcast_select_fusion.2.coeff_ref
  11.9 0.0 collective-permute-done.1
  11.9 0.0 collective-permute-done
  11.9 3.5 %fusion.2 = bf16[2,167,4096]{2,1,0:T(8,128)(2,1)S(1)} fusion(s32[]{:T(128)S(6)} %select_n.534, bf16[1,2,16,4096]{3,2,1,0:T(8,128)(2,1)S(1)} %collective-permute-done, bf16[1,2,160,4096]{3,2,1,0:T(8,128)(2,1)} %param.6, bf16[1,2,16,4096]{3,2,1,0:T(8,128)(2,1)S(1)} %collective-permute-done.1), kind=kLoop, calls=%fused_computation.6 | loop fusion | flops 8208384 | bytes 5881860 | tf_op jit(solution)/shard_map/convert_element_type | solution.py:109
  15.4 3.1 %pad_convert_fusion.window_ref = f32[2,168,4096]{2,1,0:T(8,128)} fusion(bf16[2,167,4096]{2,1,0:T(8,128)(2,1)S(1)} %fusion.2), kind=kLoop, calls=%fused_computation.7 | loop fusion | flops 1376256 | bytes 8241152 | tf_op jit(solution)/shard_map/jit(_pad)/pad | solution.py:110
  18.5 20.5 %shard_map.64 = bf16[2,160,2048]{2,1,0:T(8,128)(2,1)} custom-call(f32[8]{0:T(128)} %dynamic-slice_reduce_fusion.weights_ref, f32[2,168,4096]{2,1,0:T(8,128)} %pad_convert_fusion.window_ref, f32[160,8]{1,0:T(8,128)} %broadcast_select_fusion.2.coeff_ref, s32[160,1]{1,0:T(8,128)} %copy.23.shift_ref), custom_call_target="tpu_custom_call" | custom-call | flops 39321600 | bytes 3932160 | tf_op jit(solution)/shard_map/pallas_call | solution.py:87
  39.0 2.7 %copy.24 = bf16[2,160,2048]{2,0,1:T(2,128)(2,1)S(1)} copy(bf16[2,160,2048]{2,1,0:T(8,128)(2,1)} %shard_map.64) | data formatting | bytes 2621440 | tf_op jit(solution)/shard_map/pallas_call | solution.py:87
  41.7 0.7 copy.36
  42.5 0.3 copy-done.2
  42.8 6.1 %collective-permute-start.2 = (bf16[2,160,2048]{2,1,0:T(8,128)(2,1)S(1)}, bf16[2,160,2048]{2,1,0:T(8,128)(2,1)}, u32[]{:S(2)}, u32[]{:S(2)}) collective-permute-start(bf16[2,160,2048]{2,1,0:T(8,128)(2,1)S(1)} %bitcast.89), channel_id=1, source_target_pairs={{0,8},{4,12},{8,16},{12,20},{16,24},{20,28},{1,9},{5,13},{9,17},{1... | collective-permute-start | bytes 3932168 | tf_op jit(solution)/shard_map/ppermute | solution.py:39
  48.8 20.4 %shard_map.66 = bf16[2,160,2048]{2,1,0:T(8,128)(2,1)} custom-call(f32[8]{0:T(128)} %dynamic-slice_reduce_fusion.weights_ref, f32[2,168,4096]{2,1,0:T(8,128)} %pad_convert_fusion.window_ref, f32[160,8]{1,0:T(8,128)} %broadcast_select_fusion.2.coeff_ref, s32[160,1]{1,0:T(8,128)} %copy.23.shift_ref), custom_call_target="tpu_custom_call" | custom-call | flops 39321600 | bytes 3932160 | tf_op jit(solution)/shard_map/pallas_call | solution.py:87
  69.2 2.7 %copy.27 = bf16[2,160,2048]{2,0,1:T(2,128)(2,1)S(1)} copy(bf16[2,160,2048]{2,1,0:T(8,128)(2,1)} %shard_map.66) | data formatting | bytes 2621440 | tf_op jit(solution)/shard_map/pallas_call | solution.py:87
  71.9 0.7 copy.35
  72.6 0.3 copy-done.3
  73.0 1.5 collective-permute-start.4
  74.5 2.2 %collective-permute-done.2.second_ref = bf16[2,160,2048]{2,1,0:T(8,128)(2,1)} collective-permute-done((bf16[2,160,2048]{2,1,0:T(8,128)(2,1)S(1)}, bf16[2,160,2048]{2,1,0:T(8,128)(2,1)}, u32[]{:S(2)}, u32[]{:S(2)}) %collective-permute-start.2) | collective-permute-done | bytes 1310752 | tf_op jit(solution)/shard_map/ppermute | solution.py:39
  76.7 2.8 %broadcast_select_fusion.1 = bf16[2,160,2048]{2,1,0:T(8,128)(2,1)S(1)} fusion(bf16[2,160,2048]{2,1,0:T(8,128)(2,1)} %collective-permute-done.2.second_ref, pred[]{:T(512)S(6)} %eq.179, bf16[2,20,8,2048]{3,0,1,2:T(2,128)(2,1)} %bitcast.95), kind=kLoop, calls=%fused_computation.11 | loop fusion | flops 655360 | bytes 3932161 | tf_op jit(solution)/shard_map/jit(_where)/select_n | solution.py:180
  79.5 2.0 collective-permute-start.6
  81.5 25.0 %collective-permute-done.4.second_ref = bf16[2,160,2048]{2,1,0:T(8,128)(2,1)} collective-permute-done((bf16[2,160,2048]{2,1,0:T(8,128)(2,1)S(1)}, bf16[2,160,2048]{2,1,0:T(8,128)(2,1)}, u32[]{:S(2)}, u32[]{:S(2)}) %collective-permute-start.4) | collective-permute-done | bytes 1310752 | tf_op jit(solution)/shard_map/ppermute | solution.py:39
  106.5 2.8 %broadcast_select_fusion = bf16[2,160,2048]{2,1,0:T(8,128)(2,1)S(1)} fusion(bf16[2,160,2048]{2,1,0:T(8,128)(2,1)} %collective-permute-done.4.second_ref, pred[]{:T(512)S(6)} %eq.179, bf16[2,20,8,2048]{3,0,1,2:T(2,128)(2,1)S(1)} %bitcast.97), kind=kLoop, calls=%fused_computation.10 | loop fusion | flops 655360 | bytes 3932161 | tf_op jit(solution)/shard_map/jit(_where)/select_n | solution.py:177
  109.3 0.3 collective-permute-start.7
  109.6 3.4 %collective-permute-start.3 = (bf16[2,160,2048]{2,1,0:T(8,128)(2,1)}, bf16[2,160,2048]{2,1,0:T(8,128)(2,1)}, u32[]{:S(2)}, u32[]{:S(2)}) collective-permute-start(bf16[2,160,2048]{2,1,0:T(8,128)(2,1)} %collective-permute-done.2.second_ref), channel_id=1, source_target_pairs={{0,8},{4,12},{8,16},{12,20},{16,24},{20,28},{1,9},{5,13},{9,17},{1... | collective-permute-start | bytes 3932168 | tf_op jit(solution)/shard_map/ppermute | solution.py:39
  113.0 1.3 collective-permute-start.5
  114.3 4.4 %shard_map.68 = f32[2,8,512]{2,1,0:T(8,128)} custom-call(bf16[2,160,2048]{2,1,0:T(8,128)(2,1)} %bitcast.90, bf16[2,160,2048]{2,1,0:T(8,128)(2,1)} %collective-permute-done.2.second_ref), custom_call_target="tpu_custom_call" | custom-call | flops 13107200 | bytes 2621440 | tf_op jit(solution)/shard_map/pallas_call | solution.py:148
  118.7 4.4 %shard_map.69 = f32[2,8,512]{2,1,0:T(8,128)} custom-call(bf16[2,160,2048]{2,1,0:T(8,128)(2,1)} %bitcast.85, bf16[2,160,2048]{2,1,0:T(8,128)(2,1)} %collective-permute-done.4.second_ref), custom_call_target="tpu_custom_call" | custom-call | flops 13107200 | bytes 2621440 | tf_op jit(solution)/shard_map/pallas_call | solution.py:148
  123.1 0.0 collective-permute-done.6.second_ref
  123.1 5.7 %collective-permute-start.10 = (bf16[2,160,2048]{2,1,0:T(8,128)(2,1)}, bf16[2,160,2048]{2,1,0:T(8,128)(2,1)}, u32[]{:S(2)}, u32[]{:S(2)}) collective-permute-start(bf16[2,160,2048]{2,1,0:T(8,128)(2,1)} %collective-permute-done.6.second_ref), channel_id=1, source_target_pairs={{0,8},{4,12},{8,16},{12,20},{16,24},{20,28},{1,9},{5,13},{9,17},{1... | collective-permute-start | bytes 3932168 | tf_op jit(solution)/shard_map/ppermute | solution.py:39
  128.7 11.4 %collective-permute-done.7.second_ref = bf16[2,160,2048]{2,1,0:T(8,128)(2,1)} collective-permute-done((bf16[2,160,2048]{2,1,0:T(8,128)(2,1)S(1)}, bf16[2,160,2048]{2,1,0:T(8,128)(2,1)}, u32[]{:S(2)}, u32[]{:S(2)}) %collective-permute-start.7) | collective-permute-done | bytes 1310752 | tf_op jit(solution)/shard_map/ppermute | solution.py:44
  140.1 1.3 collective-permute-start.8
  141.4 4.4 %shard_map.70 = f32[2,8,512]{2,1,0:T(8,128)} custom-call(bf16[2,160,2048]{2,1,0:T(8,128)(2,1)} %bitcast.91, bf16[2,160,2048]{2,1,0:T(8,128)(2,1)} %collective-permute-done.6.second_ref), custom_call_target="tpu_custom_call" | custom-call | flops 13107200 | bytes 2621440 | tf_op jit(solution)/shard_map/pallas_call | solution.py:148
  145.8 4.4 %shard_map.71 = f32[2,8,512]{2,1,0:T(8,128)} custom-call(bf16[2,160,2048]{2,1,0:T(8,128)(2,1)} %bitcast.86, bf16[2,160,2048]{2,1,0:T(8,128)(2,1)} %collective-permute-done.7.second_ref), custom_call_target="tpu_custom_call" | custom-call | flops 13107200 | bytes 2621440 | tf_op jit(solution)/shard_map/pallas_call | solution.py:148
  150.2 0.0 collective-permute-done.3.second_ref
  150.2 4.4 %shard_map.65 = f32[2,8,512]{2,1,0:T(8,128)} custom-call(bf16[2,160,2048]{2,1,0:T(8,128)(2,1)} %bitcast.92, bf16[2,160,2048]{2,1,0:T(8,128)(2,1)} %collective-permute-done.3.second_ref), custom_call_target="tpu_custom_call" | custom-call | flops 13107200 | bytes 2621440 | tf_op jit(solution)/shard_map/pallas_call | solution.py:148
  154.5 0.0 copy-start.9
  154.6 0.0 copy-start.14
  154.6 0.0 collective-permute-done.5.second_ref
  154.6 4.4 %shard_map.67 = f32[2,8,512]{2,1,0:T(8,128)} custom-call(bf16[2,160,2048]{2,1,0:T(8,128)(2,1)} %bitcast.87, bf16[2,160,2048]{2,1,0:T(8,128)(2,1)} %collective-permute-done.5.second_ref), custom_call_target="tpu_custom_call" | custom-call | flops 13107200 | bytes 2621440 | tf_op jit(solution)/shard_map/pallas_call | solution.py:148
  159.0 1.6 select_select_fusion
  160.6 7.0 %all-to-all-start = ((f32[8,2,8,512]{3,2,1,0:T(8,128)}), f32[8,2,8,512]{3,2,1,0:T(8,128)S(1)}, u32[]{:S(2)}, u32[]{:S(2)}) async-start(f32[8,2,8,512]{3,2,1,0:T(8,128)} %select_select_fusion), calls=%async_computation | async-start | bytes 524288 | tf_op jit(solution)/shard_map/all_to_all | solution.py:198
  167.6 0.7 fusion.45
  189.0 0.0 all-to-all-done
  189.1 0.0 collective-permute-done.10.second_ref
  189.1 4.4 %shard_map.73 = f32[2,8,512]{2,1,0:T(8,128)} custom-call(bf16[2,160,2048]{2,1,0:T(8,128)(2,1)} %bitcast.93, bf16[2,160,2048]{2,1,0:T(8,128)(2,1)} %collective-permute-done.10.second_ref), custom_call_target="tpu_custom_call" | custom-call | flops 13107200 | bytes 2621440 | tf_op jit(solution)/shard_map/pallas_call | solution.py:148
  193.5 1.3 collective-permute-start.11
  194.8 0.0 copy-start.12
  194.8 0.0 collective-permute-done.8.second_ref
  194.8 1.1 copy-done.5
  195.9 4.4 %shard_map.72 = f32[2,8,512]{2,1,0:T(8,128)} custom-call(bf16[2,160,2048]{2,1,0:T(8,128)(2,1)} %bitcast.88, bf16[2,160,2048]{2,1,0:T(8,128)(2,1)} %copy-done.5), custom_call_target="tpu_custom_call" | custom-call | flops 13107200 | bytes 2621440 | tf_op jit(solution)/shard_map/pallas_call | solution.py:148
  200.2 5.6 %collective-permute-start.9 = (f32[2,8,512]{2,1,0:T(8,128)}, f32[2,8,512]{2,1,0:T(8,128)S(1)}, u32[]{:S(2)}, u32[]{:S(2)}) collective-permute-start(f32[2,8,512]{2,1,0:T(8,128)} %shard_map.72), channel_id=1, source_target_pairs={{0,12},{4,16},{8,20},{12,24},{16,28},{1,13},{5,17},{9,21},{13,25},... | collective-permute-start | bytes 98312 | tf_op jit(solution)/shard_map/ppermute | solution.py:39
  205.9 1.9 collective-permute-done.9
  207.7 0.8 select_select_fusion.3
  208.5 0.8 select_select_fusion.2
  209.4 0.7 maximum_bitcast_fusion
  (44 shorter events, 0.3 us)
Async XLA Ops:
  1.1 10.9 %collective-permute-start.1 = (bf16[1,2,16,4096]{3,2,1,0:T(8,128)(2,1)S(1)}, bf16[1,2,16,4096]{3,2,1,0:T(8,128)(2,1)S(1)}, u32[]{:S(2)}, u32[]{:S(2)}) collective-permute-start(bf16[1,2,16,4096]{3,2,1,0:T(8,128)(2,1)S(1)} %get-tuple-element.13), channel_id=1, source_target_pairs={{1,0},{2,1},{3,2},{5,4},{6,5},{7,6},{9,8},{10,9},{11,10},{13,12},{... | collective-permute-start | bytes 786440 | tf_op jit(solution)/shard_map/ppermute | solution.py:29
  2.4 9.6 %collective-permute-start = (bf16[1,2,16,4096]{3,2,1,0:T(8,128)(2,1)S(1)}, bf16[1,2,16,4096]{3,2,1,0:T(8,128)(2,1)S(1)}, u32[]{:S(2)}, u32[]{:S(2)}) collective-permute-start(bf16[1,2,16,4096]{3,2,1,0:T(8,128)(2,1)S(1)} %get-tuple-element.14), channel_id=1, source_target_pairs={{0,1},{1,2},{2,3},{4,5},{5,6},{6,7},{8,9},{9,10},{10,11},{12,13},{... | collective-permute-start | bytes 786440 | tf_op jit(solution)/shard_map/ppermute | solution.py:27
  41.7 1.1 copy-start.2
  42.8 26.5 %copy-start.1 = (bf16[2,20,8,2048]{3,2,1,0:T(8,128)(2,1)}, bf16[2,20,8,2048]{3,2,1,0:T(8,128)(2,1)S(1)}, u32[]{:S(2)}) copy-start(bf16[2,20,8,2048]{3,2,1,0:T(8,128)(2,1)S(1)} %copy.36) | copy-start | bytes 3932164
  42.8 34.0 %collective-permute-start.2 = (bf16[2,160,2048]{2,1,0:T(8,128)(2,1)S(1)}, bf16[2,160,2048]{2,1,0:T(8,128)(2,1)}, u32[]{:S(2)}, u32[]{:S(2)}) collective-permute-start(bf16[2,160,2048]{2,1,0:T(8,128)(2,1)S(1)} %bitcast.89), channel_id=1, source_target_pairs={{0,8},{4,12},{8,16},{12,20},{16,24},{20,28},{1,9},{5,13},{9,17},{1... | collective-permute-start | bytes 3932168 | tf_op jit(solution)/shard_map/ppermute | solution.py:39
  71.9 1.1 copy-start.3
  73.0 6.5 %copy-start = (bf16[2,20,8,2048]{3,2,1,0:T(8,128)(2,1)}, bf16[2,20,8,2048]{3,2,1,0:T(8,128)(2,1)S(1)}, u32[]{:S(2)}) copy-start(bf16[2,20,8,2048]{3,2,1,0:T(8,128)(2,1)S(1)} %copy.35) | copy-start | bytes 3932164
  73.0 33.5 %collective-permute-start.4 = (bf16[2,160,2048]{2,1,0:T(8,128)(2,1)S(1)}, bf16[2,160,2048]{2,1,0:T(8,128)(2,1)}, u32[]{:S(2)}, u32[]{:S(2)}) collective-permute-start(bf16[2,160,2048]{2,1,0:T(8,128)(2,1)S(1)} %bitcast.84), channel_id=1, source_target_pairs={{8,0},{12,4},{16,8},{20,12},{24,16},{28,20},{9,1},{13,5},{17,9},{2... | collective-permute-start | bytes 3932168 | tf_op jit(solution)/shard_map/ppermute | solution.py:39
  74.5 32.0 %copy-start.4 = (bf16[2,160,2048]{2,0,1:T(2,128)(2,1)S(1)}, bf16[2,160,2048]{2,0,1:T(2,128)(2,1)}, u32[]{:S(2)}) copy-start(bf16[2,160,2048]{2,0,1:T(2,128)(2,1)} %copy-done.3) | copy-start | bytes 3932164
  79.5 43.5 %collective-permute-start.6 = (bf16[2,160,2048]{2,1,0:T(8,128)(2,1)S(1)}, bf16[2,160,2048]{2,1,0:T(8,128)(2,1)}, u32[]{:S(2)}, u32[]{:S(2)}) collective-permute-start(bf16[2,160,2048]{2,1,0:T(8,128)(2,1)S(1)} %broadcast_select_fusion.1), channel_id=1, source_target_pairs={{0,4},{4,0},{8,12},{12,8},{16,20},{20,16},{24,28},{28,24},{1,5},{5... | collective-permute-start | bytes 3932168 | tf_op jit(solution)/shard_map/ppermute | solution.py:44
  109.3 30.8 %collective-permute-start.7 = (bf16[2,160,2048]{2,1,0:T(8,128)(2,1)S(1)}, bf16[2,160,2048]{2,1,0:T(8,128)(2,1)}, u32[]{:S(2)}, u32[]{:S(2)}) collective-permute-start(bf16[2,160,2048]{2,1,0:T(8,128)(2,1)S(1)} %broadcast_select_fusion), channel_id=1, source_target_pairs={{0,4},{4,0},{8,12},{12,8},{16,20},{20,16},{24,28},{28,24},{1,5},{5... | collective-permute-start | bytes 3932168 | tf_op jit(solution)/shard_map/ppermute | solution.py:44
  109.6 40.6 %collective-permute-start.3 = (bf16[2,160,2048]{2,1,0:T(8,128)(2,1)}, bf16[2,160,2048]{2,1,0:T(8,128)(2,1)}, u32[]{:S(2)}, u32[]{:S(2)}) collective-permute-start(bf16[2,160,2048]{2,1,0:T(8,128)(2,1)} %collective-permute-done.2.second_ref), channel_id=1, source_target_pairs={{0,8},{4,12},{8,16},{12,20},{16,24},{20,28},{1,9},{5,13},{9,17},{1... | collective-permute-start | bytes 3932168 | tf_op jit(solution)/shard_map/ppermute | solution.py:39
  113.0 41.6 %collective-permute-start.5 = (bf16[2,160,2048]{2,1,0:T(8,128)(2,1)}, bf16[2,160,2048]{2,1,0:T(8,128)(2,1)}, u32[]{:S(2)}, u32[]{:S(2)}) collective-permute-start(bf16[2,160,2048]{2,1,0:T(8,128)(2,1)} %collective-permute-done.4.second_ref), channel_id=1, source_target_pairs={{8,0},{12,4},{16,8},{20,12},{24,16},{28,20},{9,1},{13,5},{17,9},{2... | collective-permute-start | bytes 3932168 | tf_op jit(solution)/shard_map/ppermute | solution.py:39
  123.1 66.0 %collective-permute-start.10 = (bf16[2,160,2048]{2,1,0:T(8,128)(2,1)}, bf16[2,160,2048]{2,1,0:T(8,128)(2,1)}, u32[]{:S(2)}, u32[]{:S(2)}) collective-permute-start(bf16[2,160,2048]{2,1,0:T(8,128)(2,1)} %collective-permute-done.6.second_ref), channel_id=1, source_target_pairs={{0,8},{4,12},{8,16},{12,20},{16,24},{20,28},{1,9},{5,13},{9,17},{1... | collective-permute-start | bytes 3932168 | tf_op jit(solution)/shard_map/ppermute | solution.py:39
  140.1 54.7 %collective-permute-start.8 = (bf16[2,160,2048]{2,1,0:T(8,128)(2,1)}, bf16[2,160,2048]{2,1,0:T(8,128)(2,1)S(1)}, u32[]{:S(2)}, u32[]{:S(2)}) collective-permute-start(bf16[2,160,2048]{2,1,0:T(8,128)(2,1)} %collective-permute-done.7.second_ref), channel_id=1, source_target_pairs={{8,0},{12,4},{16,8},{20,12},{24,16},{28,20},{9,1},{13,5},{17,9},{2... | collective-permute-start | bytes 3932168 | tf_op jit(solution)/shard_map/ppermute | solution.py:39
  154.5 4.5 %copy-start.6 = (f32[2,8,512]{2,1,0:T(8,128)S(1)}, f32[2,8,512]{2,1,0:T(8,128)}, u32[]{:S(2)}) copy-start(f32[2,8,512]{2,1,0:T(8,128)} %shard_map.68) | copy-start | bytes 98308
  154.5 4.5 %copy-start.7 = (f32[2,8,512]{2,1,0:T(8,128)S(1)}, f32[2,8,512]{2,1,0:T(8,128)}, u32[]{:S(2)}) copy-start(f32[2,8,512]{2,1,0:T(8,128)} %shard_map.69) | copy-start | bytes 98308
  154.5 4.5 %copy-start.8 = (f32[2,8,512]{2,1,0:T(8,128)S(1)}, f32[2,8,512]{2,1,0:T(8,128)}, u32[]{:S(2)}) copy-start(f32[2,8,512]{2,1,0:T(8,128)} %shard_map.70) | copy-start | bytes 98308
  154.5 4.5 %copy-start.9 = (f32[2,8,512]{2,1,0:T(8,128)S(1)}, f32[2,8,512]{2,1,0:T(8,128)}, u32[]{:S(2)}) copy-start(f32[2,8,512]{2,1,0:T(8,128)} %shard_map.71) | copy-start | bytes 98308
  154.5 4.5 %copy-start.10 = (f32[2,8,512]{2,1,0:T(8,128)S(1)}, f32[2,8,512]{2,1,0:T(8,128)}, u32[]{:S(2)}) copy-start(f32[2,8,512]{2,1,0:T(8,128)} %shard_map.65) | copy-start | bytes 98308
  154.6 13.0 %copy-start.14 = (s32[1,4]{1,0:T(1,128)S(1)}, s32[1,4]{1,0:T(1,128)}, u32[]{:S(2)}) copy-start(s32[1,4]{1,0:T(1,128)} %param.11) | copy-start | bytes 52
  160.6 28.3 %all-to-all-start = ((f32[8,2,8,512]{3,2,1,0:T(8,128)}), f32[8,2,8,512]{3,2,1,0:T(8,128)S(1)}, u32[]{:S(2)}, u32[]{:S(2)}) async-start(f32[8,2,8,512]{3,2,1,0:T(8,128)} %select_select_fusion), calls=%async_computation | async-start | bytes 524288 | tf_op jit(solution)/shard_map/all_to_all | solution.py:198
  193.5 12.4 %collective-permute-start.11 = (f32[2,8,512]{2,1,0:T(8,128)}, f32[2,8,512]{2,1,0:T(8,128)S(1)}, u32[]{:S(2)}, u32[]{:S(2)}) collective-permute-start(f32[2,8,512]{2,1,0:T(8,128)} %shard_map.73), channel_id=1, source_target_pairs={{12,0},{16,4},{20,8},{24,12},{28,16},{13,1},{17,5},{21,9},{25,13},... | collective-permute-start | bytes 98312 | tf_op jit(solution)/shard_map/ppermute | solution.py:39
  194.8 13.0 %copy-start.11 = (f32[2,8,512]{2,1,0:T(8,128)S(1)}, f32[2,8,512]{2,1,0:T(8,128)}, u32[]{:S(2)}) copy-start(f32[2,8,512]{2,1,0:T(8,128)} %shard_map.67) | copy-start | bytes 98308
  194.8 13.0 %copy-start.12 = (f32[2,8,512]{2,1,0:T(8,128)S(1)}, f32[2,8,512]{2,1,0:T(8,128)}, u32[]{:S(2)}) copy-start(f32[2,8,512]{2,1,0:T(8,128)} %shard_map.73) | copy-start | bytes 98308
  194.8 1.1 copy-start.5
  200.2 9.1 %copy-start.13 = (f32[2,8,512]{2,1,0:T(8,128)S(1)}, f32[2,8,512]{2,1,0:T(8,128)}, u32[]{:S(2)}) copy-start(f32[2,8,512]{2,1,0:T(8,128)} %shard_map.72) | copy-start | bytes 98308
  200.2 7.5 %collective-permute-start.9 = (f32[2,8,512]{2,1,0:T(8,128)}, f32[2,8,512]{2,1,0:T(8,128)S(1)}, u32[]{:S(2)}, u32[]{:S(2)}) collective-permute-start(f32[2,8,512]{2,1,0:T(8,128)} %shard_map.72), channel_id=1, source_target_pairs={{0,12},{4,16},{8,20},{12,24},{16,28},{1,13},{5,17},{9,21},{13,25},... | collective-permute-start | bytes 98312 | tf_op jit(solution)/shard_map/ppermute | solution.py:39

commit v16 on v14

--- a/solution.py
+++ b/solution.py
@@ -61,7 +61,7 @@
     half = out_ref.shape[2]
     low = max(side * half - EDGE, 0)
     high = min(side * half + half + EDGE, window_ref.shape[2])
-    window = window_ref[0, pl.ds(first, ROWS + 8), low:high]
+    window = window_ref[0, pl.ds(first, ROWS + 16), low:high].astype(jnp.float32)
     along = weights_ref[0] * window[0:ROWS, :]
     for tap in range(1, 8):
         along = along + weights_ref[tap] * window[tap : tap + ROWS, :]
@@ -106,8 +106,8 @@
     nlines = shift_range.shape[0]
     border = OFFAZ + 4
     start = border + shift_lines - 3
-    window = lax.dynamic_slice_in_dim(padded, start, nlines + 7, 1).astype(jnp.float32)
-    window = jnp.pad(window, ((0, 0), (0, 1), (0, 0)))
+    window = lax.dynamic_slice_in_dim(padded, start, nlines + 7, 1)
+    window = jnp.pad(window, ((0, 0), (0, 9), (0, 0)))
     weights = table[kern_lines]
     coeff = jnp.take(table, kern_range, axis=0)
     shift = (shift_range + OFFRG)[:, None]

time: 209 us -> 208 us (level)
  other arithmetic: 17.7 us -> 14.6 us
    convert_element_type x1 -> x0, other arithmetic: 3.5 us -> none  [resample_block(): lax.dynamic_slice_in_dim(padded, start, nlines + 7, 1).astype(jnp.float32)]
    dynamic_slice x0 -> x1, other arithmetic: none -> 3.46 us  [resample_block(): window = lax.dynamic_slice_in_dim(padded, start, nlines + 7, 1)]
    pad x1 -> x0, other arithmetic: 3.07 us -> none  [resample_block(): window = jnp.pad(window, ((0, 0), (0, 1), (0, 0)))]
  transfers between devices with their start and end apart: 11 -> 11, of which waited for: 4 -> 4; matrix products, arithmetic and copies ran while one was open for 7% -> 7% of each run, Pallas kernels for 25% -> 24%
where the time goes in v16:
time: 208 us; the launch traced here: 207 us
  Pallas kernels  75.2 us (36%)
  waiting for transfers between devices  49.1 us (24%)
  starting transfers between devices  30.6 us (15%)
  between operations  21.9 us (11%)
  local copies, waits for them, and re-layouts  15.6 us (8%)
  other arithmetic  14.6 us (7%)
    pallas_call x2, Pallas kernels, resample_half(): pl.pallas_call(functools.partial(resample_kernel, side), grid=(2, nlines...  40.2 us
    ppermute x6, waiting for transfers between devices, shifted(): return lax.ppermute(block, axis, route)  36.7 us
    pallas_call x8, Pallas kernels, looks(): pl.pallas_call(looks_kernel, grid=(width // CHUNK,), in_specs=[spec, spec...  34.9 us
    ppermute x6, starting transfers between devices, shifted(): return lax.ppermute(block, axis, route)  18.2 us
    ppermute x2, waiting for transfers between devices, swapped(): return lax.ppermute(block, axis, [(i, i ^ 1) for i in range(count)])  12.4 us
    all_to_all x1, starting transfers between devices, shards(): got = lax.all_to_all(sent, 'date', 0, 0, tiled=True)  5.83 us
    pallas_call x2, local copies, waits for them, and re-layouts, resample_half(): pl.pallas_call(functools.partial(resample_kernel, side), grid=(2, nlines...  5.33 us
  transfers between devices with their start and end apart: 11, of which 4 were waited for; matrix products, arithmetic and copies ran while one was open for 7% of the time, Pallas kernels for 24%

profile of v16, /device:TPU:0, one launch (start us, length us, event | category | flops | bytes accessed | tf_op | source)
XLA Modules:
  0.0 206.9 jit_solution(1839654812343415760)
XLA Ops:
  0.0 1.1 fusion.47
  1.1 1.3 collective-permute-start.1
  2.4 3.0 %collective-permute-start = (bf16[1,2,16,4096]{3,2,1,0:T(8,128)(2,1)S(1)}, bf16[1,2,16,4096]{3,2,1,0:T(8,128)(2,1)S(1)}, u32[]{:S(2)}, u32[]{:S(2)}) collective-permute-start(bf16[1,2,16,4096]{3,2,1,0:T(8,128)(2,1)S(1)} %get-tuple-element.14), channel_id=1, source_target_pairs={{0,1},{1,2},{2,3},{4,5},{5,6},{6,7},{8,9},{9,10},{10,11},{12,13},{... | collective-permute-start | bytes 786440 | tf_op jit(solution)/shard_map/ppermute | solution.py:27
  5.4 0.7 compare_select_fusion
  6.1 0.7 compare_and_fusion
  6.8 0.7 add_bitcast_fusion
  7.5 0.1 fusion.17
  8.9 0.1 copy.22
  9.0 0.7 fusion.14.weights_ref
  9.7 0.7 copy.23.shift_ref
  10.4 0.7 gather_fusion
  11.1 0.7 broadcast_select_fusion.2.coeff_ref
  11.8 0.0 collective-permute-done.1
  11.8 0.0 collective-permute-done
  11.9 3.5 %fusion.2 = bf16[2,167,4096]{2,1,0:T(8,128)(2,1)S(1)} fusion(s32[]{:T(128)S(6)} %select_n.544, bf16[1,2,16,4096]{3,2,1,0:T(8,128)(2,1)S(1)} %collective-permute-done, bf16[1,2,160,4096]{3,2,1,0:T(8,128)(2,1)} %param.6, bf16[1,2,16,4096]{3,2,1,0:T(8,128)(2,1)S(1)} %collective-permute-done.1), kind=kLoop, calls=%fused_computation.6 | loop fusion | flops 8208384 | bytes 5881860 | tf_op jit(solution)/shard_map/dynamic_slice | solution.py:109
  15.3 1.9 pad.4.window_ref
  17.3 20.2 %shard_map.64 = bf16[2,160,2048]{2,1,0:T(8,128)(2,1)} custom-call(f32[8]{0:T(128)} %fusion.14.weights_ref, bf16[2,176,4096]{2,1,0:T(8,128)(2,1)} %pad.4.window_ref, f32[160,8]{1,0:T(8,128)} %broadcast_select_fusion.2.coeff_ref, s32[160,1]{1,0:T(8,128)} %copy.23.shift_ref), custom_call_target="tpu_custom_call" | custom-call | flops 39321600 | bytes 3932160 | tf_op jit(solution)/shard_map/pallas_call | solution.py:87
  37.5 2.7 %copy.24 = bf16[2,160,2048]{2,0,1:T(2,128)(2,1)S(1)} copy(bf16[2,160,2048]{2,1,0:T(8,128)(2,1)} %shard_map.64) | data formatting | bytes 2621440 | tf_op jit(solution)/shard_map/pallas_call | solution.py:87
  40.1 0.7 copy.36
  40.9 0.4 copy-done.2
  41.2 6.0 %collective-permute-start.2 = (bf16[2,160,2048]{2,1,0:T(8,128)(2,1)S(1)}, bf16[2,160,2048]{2,1,0:T(8,128)(2,1)}, u32[]{:S(2)}, u32[]{:S(2)}) collective-permute-start(bf16[2,160,2048]{2,1,0:T(8,128)(2,1)S(1)} %bitcast.92), channel_id=1, source_target_pairs={{0,8},{4,12},{8,16},{12,20},{16,24},{20,28},{1,9},{5,13},{9,17},{1... | collective-permute-start | bytes 3932168 | tf_op jit(solution)/shard_map/ppermute | solution.py:39
  47.3 20.0 %shard_map.66 = bf16[2,160,2048]{2,1,0:T(8,128)(2,1)} custom-call(f32[8]{0:T(128)} %fusion.14.weights_ref, bf16[2,176,4096]{2,1,0:T(8,128)(2,1)} %pad.4.window_ref, f32[160,8]{1,0:T(8,128)} %broadcast_select_fusion.2.coeff_ref, s32[160,1]{1,0:T(8,128)} %copy.23.shift_ref), custom_call_target="tpu_custom_call" | custom-call | flops 39321600 | bytes 3932160 | tf_op jit(solution)/shard_map/pallas_call | solution.py:87
  67.3 0.0 copy-done
  67.3 2.7 %copy.27 = bf16[2,160,2048]{2,0,1:T(2,128)(2,1)S(1)} copy(bf16[2,160,2048]{2,1,0:T(8,128)(2,1)} %shard_map.66) | data formatting | bytes 2621440 | tf_op jit(solution)/shard_map/pallas_call | solution.py:87
  70.0 0.0 copy-start.3
  70.0 0.7 copy.35
  70.7 0.4 copy-done.3
  71.1 1.5 collective-permute-start.4
  72.6 2.6 %collective-permute-done.2.second_ref = bf16[2,160,2048]{2,1,0:T(8,128)(2,1)} collective-permute-done((bf16[2,160,2048]{2,1,0:T(8,128)(2,1)S(1)}, bf16[2,160,2048]{2,1,0:T(8,128)(2,1)}, u32[]{:S(2)}, u32[]{:S(2)}) %collective-permute-start.2) | collective-permute-done | bytes 1310752 | tf_op jit(solution)/shard_map/ppermute | solution.py:39
  75.2 2.8 %broadcast_select_fusion.1 = bf16[2,160,2048]{2,1,0:T(8,128)(2,1)S(1)} fusion(bf16[2,160,2048]{2,1,0:T(8,128)(2,1)} %collective-permute-done.2.second_ref, pred[]{:T(512)S(6)} %eq.195, bf16[2,20,8,2048]{3,0,1,2:T(2,128)(2,1)} %bitcast.103), kind=kLoop, calls=%fused_computation.10 | loop fusion | flops 655360 | bytes 3932161 | tf_op jit(solution)/shard_map/jit(_where)/select_n | solution.py:180
  78.0 2.0 collective-permute-start.6
  80.0 24.6 %collective-permute-done.4.second_ref = bf16[2,160,2048]{2,1,0:T(8,128)(2,1)} collective-permute-done((bf16[2,160,2048]{2,1,0:T(8,128)(2,1)S(1)}, bf16[2,160,2048]{2,1,0:T(8,128)(2,1)}, u32[]{:S(2)}, u32[]{:S(2)}) %collective-permute-start.4) | collective-permute-done | bytes 1310752 | tf_op jit(solution)/shard_map/ppermute | solution.py:39
  104.6 2.8 %broadcast_select_fusion = bf16[2,160,2048]{2,1,0:T(8,128)(2,1)S(1)} fusion(bf16[2,160,2048]{2,1,0:T(8,128)(2,1)} %collective-permute-done.4.second_ref, pred[]{:T(512)S(6)} %eq.195, bf16[2,20,8,2048]{3,0,1,2:T(2,128)(2,1)S(1)} %bitcast.105), kind=kLoop, calls=%fused_computation.9 | loop fusion | flops 655360 | bytes 3932161 | tf_op jit(solution)/shard_map/jit(_where)/select_n | solution.py:177
  107.4 0.3 collective-permute-start.8
  107.7 3.5 %collective-permute-start.3 = (bf16[2,160,2048]{2,1,0:T(8,128)(2,1)}, bf16[2,160,2048]{2,1,0:T(8,128)(2,1)}, u32[]{:S(2)}, u32[]{:S(2)}) collective-permute-start(bf16[2,160,2048]{2,1,0:T(8,128)(2,1)} %collective-permute-done.2.second_ref), channel_id=1, source_target_pairs={{0,8},{4,12},{8,16},{12,20},{16,24},{20,28},{1,9},{5,13},{9,17},{1... | collective-permute-start | bytes 3932168 | tf_op jit(solution)/shard_map/ppermute | solution.py:39
  111.2 1.3 collective-permute-start.5
  112.5 4.4 %shard_map.68 = f32[2,8,512]{2,1,0:T(8,128)} custom-call(bf16[2,160,2048]{2,1,0:T(8,128)(2,1)} %bitcast.93, bf16[2,160,2048]{2,1,0:T(8,128)(2,1)} %collective-permute-done.2.second_ref), custom_call_target="tpu_custom_call" | custom-call | flops 13107200 | bytes 2621440 | tf_op jit(solution)/shard_map/pallas_call | solution.py:148
  116.9 0.0 collective-permute-done.6.second_ref
  116.9 4.6 %collective-permute-start.7 = (bf16[2,160,2048]{2,1,0:T(8,128)(2,1)}, bf16[2,160,2048]{2,1,0:T(8,128)(2,1)S(1)}, u32[]{:S(2)}, u32[]{:S(2)}) collective-permute-start(bf16[2,160,2048]{2,1,0:T(8,128)(2,1)} %collective-permute-done.6.second_ref), channel_id=1, source_target_pairs={{0,8},{4,12},{8,16},{12,20},{16,24},{20,28},{1,9},{5,13},{9,17},{1... | collective-permute-start | bytes 3932168 | tf_op jit(solution)/shard_map/ppermute | solution.py:39
  121.5 4.4 %shard_map.70 = f32[2,8,512]{2,1,0:T(8,128)} custom-call(bf16[2,160,2048]{2,1,0:T(8,128)(2,1)} %bitcast.98, bf16[2,160,2048]{2,1,0:T(8,128)(2,1)} %collective-permute-done.4.second_ref), custom_call_target="tpu_custom_call" | custom-call | flops 13107200 | bytes 2621440 | tf_op jit(solution)/shard_map/pallas_call | solution.py:148
  125.9 12.4 %collective-permute-done.8.second_ref = bf16[2,160,2048]{2,1,0:T(8,128)(2,1)} collective-permute-done((bf16[2,160,2048]{2,1,0:T(8,128)(2,1)S(1)}, bf16[2,160,2048]{2,1,0:T(8,128)(2,1)}, u32[]{:S(2)}, u32[]{:S(2)}) %collective-permute-start.8) | collective-permute-done | bytes 1310752 | tf_op jit(solution)/shard_map/ppermute | solution.py:44
  138.2 1.3 collective-permute-start.9
  139.6 4.4 %shard_map.72 = f32[2,8,512]{2,1,0:T(8,128)} custom-call(bf16[2,160,2048]{2,1,0:T(8,128)(2,1)} %bitcast.94, bf16[2,160,2048]{2,1,0:T(8,128)(2,1)} %collective-permute-done.6.second_ref), custom_call_target="tpu_custom_call" | custom-call | flops 13107200 | bytes 2621440 | tf_op jit(solution)/shard_map/pallas_call | solution.py:148
  144.0 4.4 %shard_map.73 = f32[2,8,512]{2,1,0:T(8,128)} custom-call(bf16[2,160,2048]{2,1,0:T(8,128)(2,1)} %bitcast.99, bf16[2,160,2048]{2,1,0:T(8,128)(2,1)} %collective-permute-done.8.second_ref), custom_call_target="tpu_custom_call" | custom-call | flops 13107200 | bytes 2621440 | tf_op jit(solution)/shard_map/pallas_call | solution.py:148
  148.3 0.0 collective-permute-done.3.second_ref
  148.3 4.4 %shard_map.65 = f32[2,8,512]{2,1,0:T(8,128)} custom-call(bf16[2,160,2048]{2,1,0:T(8,128)(2,1)} %bitcast.95, bf16[2,160,2048]{2,1,0:T(8,128)(2,1)} %collective-permute-done.3.second_ref), custom_call_target="tpu_custom_call" | custom-call | flops 13107200 | bytes 2621440 | tf_op jit(solution)/shard_map/pallas_call | solution.py:148
  152.7 0.0 collective-permute-done.5.second_ref
  152.7 4.4 %shard_map.67 = f32[2,8,512]{2,1,0:T(8,128)} custom-call(bf16[2,160,2048]{2,1,0:T(8,128)(2,1)} %bitcast.100, bf16[2,160,2048]{2,1,0:T(8,128)(2,1)} %collective-permute-done.5.second_ref), custom_call_target="tpu_custom_call" | custom-call | flops 13107200 | bytes 2621440 | tf_op jit(solution)/shard_map/pallas_call | solution.py:148
  157.1 9.4 %collective-permute-done.7.second_ref = bf16[2,160,2048]{2,1,0:T(8,128)(2,1)S(1)} collective-permute-done((bf16[2,160,2048]{2,1,0:T(8,128)(2,1)}, bf16[2,160,2048]{2,1,0:T(8,128)(2,1)S(1)}, u32[]{:S(2)}, u32[]{:S(2)}) %collective-permute-start.7) | collective-permute-done | bytes 1310752 | tf_op jit(solution)/shard_map/ppermute | solution.py:39
  166.5 1.1 copy-done.5
  167.6 4.4 %shard_map.69 = f32[2,8,512]{2,1,0:T(8,128)} custom-call(bf16[2,160,2048]{2,1,0:T(8,128)(2,1)} %bitcast.96, bf16[2,160,2048]{2,1,0:T(8,128)(2,1)} %copy-done.5), custom_call_target="tpu_custom_call" | custom-call | flops 13107200 | bytes 2621440 | tf_op jit(solution)/shard_map/pallas_call | solution.py:148
  172.0 0.0 copy-start.10
  172.0 0.0 copy-start.11
  172.0 0.0 copy-start.12
  172.0 0.0 copy-start.13
  172.0 0.0 copy-start.15
  172.0 0.0 collective-permute-done.9.second_ref
  172.0 1.1 copy-done.6
  173.1 4.4 %shard_map.71 = f32[2,8,512]{2,1,0:T(8,128)} custom-call(bf16[2,160,2048]{2,1,0:T(8,128)(2,1)} %bitcast.101, bf16[2,160,2048]{2,1,0:T(8,128)(2,1)} %copy-done.6), custom_call_target="tpu_custom_call" | custom-call | flops 13107200 | bytes 2621440 | tf_op jit(solution)/shard_map/pallas_call | solution.py:148
  177.5 1.6 select_select_fusion
  179.2 5.8 %all-to-all-start = ((f32[8,2,8,512]{3,2,1,0:T(8,128)}), f32[8,2,8,512]{3,2,1,0:T(8,128)S(1)}, u32[]{:S(2)}, u32[]{:S(2)}) async-start(f32[8,2,8,512]{3,2,1,0:T(8,128)} %select_select_fusion), calls=%async_computation | async-start | bytes 524288 | tf_op jit(solution)/shard_map/all_to_all | solution.py:198
  185.0 0.7 fusion.48
  205.8 0.0 all-to-all-done
  206.2 0.7 maximum_bitcast_fusion
  (41 shorter events, 0.3 us)
Async XLA Ops:
  1.1 10.8 %collective-permute-start.1 = (bf16[1,2,16,4096]{3,2,1,0:T(8,128)(2,1)S(1)}, bf16[1,2,16,4096]{3,2,1,0:T(8,128)(2,1)S(1)}, u32[]{:S(2)}, u32[]{:S(2)}) collective-permute-start(bf16[1,2,16,4096]{3,2,1,0:T(8,128)(2,1)S(1)} %get-tuple-element.13), channel_id=1, source_target_pairs={{1,0},{2,1},{3,2},{5,4},{6,5},{7,6},{9,8},{10,9},{11,10},{13,12},{... | collective-permute-start | bytes 786440 | tf_op jit(solution)/shard_map/ppermute | solution.py:29
  2.4 9.5 %collective-permute-start = (bf16[1,2,16,4096]{3,2,1,0:T(8,128)(2,1)S(1)}, bf16[1,2,16,4096]{3,2,1,0:T(8,128)(2,1)S(1)}, u32[]{:S(2)}, u32[]{:S(2)}) collective-permute-start(bf16[1,2,16,4096]{3,2,1,0:T(8,128)(2,1)S(1)} %get-tuple-element.14), channel_id=1, source_target_pairs={{0,1},{1,2},{2,3},{4,5},{5,6},{6,7},{8,9},{9,10},{10,11},{12,13},{... | collective-permute-start | bytes 786440 | tf_op jit(solution)/shard_map/ppermute | solution.py:27
  40.1 1.1 copy-start.2
  41.2 26.1 %copy-start = (bf16[2,20,8,2048]{3,2,1,0:T(8,128)(2,1)}, bf16[2,20,8,2048]{3,2,1,0:T(8,128)(2,1)S(1)}, u32[]{:S(2)}) copy-start(bf16[2,20,8,2048]{3,2,1,0:T(8,128)(2,1)S(1)} %copy.36) | copy-start | bytes 3932164
  41.2 34.0 %collective-permute-start.2 = (bf16[2,160,2048]{2,1,0:T(8,128)(2,1)S(1)}, bf16[2,160,2048]{2,1,0:T(8,128)(2,1)}, u32[]{:S(2)}, u32[]{:S(2)}) collective-permute-start(bf16[2,160,2048]{2,1,0:T(8,128)(2,1)S(1)} %bitcast.92), channel_id=1, source_target_pairs={{0,8},{4,12},{8,16},{12,20},{16,24},{20,28},{1,9},{5,13},{9,17},{1... | collective-permute-start | bytes 3932168 | tf_op jit(solution)/shard_map/ppermute | solution.py:39
  70.0 1.1 copy-start.3
  71.1 6.9 %copy-start.1 = (bf16[2,20,8,2048]{3,2,1,0:T(8,128)(2,1)}, bf16[2,20,8,2048]{3,2,1,0:T(8,128)(2,1)S(1)}, u32[]{:S(2)}) copy-start(bf16[2,20,8,2048]{3,2,1,0:T(8,128)(2,1)S(1)} %copy.35) | copy-start | bytes 3932164
  71.1 33.5 %collective-permute-start.4 = (bf16[2,160,2048]{2,1,0:T(8,128)(2,1)S(1)}, bf16[2,160,2048]{2,1,0:T(8,128)(2,1)}, u32[]{:S(2)}, u32[]{:S(2)}) collective-permute-start(bf16[2,160,2048]{2,1,0:T(8,128)(2,1)S(1)} %bitcast.97), channel_id=1, source_target_pairs={{8,0},{12,4},{16,8},{20,12},{24,16},{28,20},{9,1},{13,5},{17,9},{2... | collective-permute-start | bytes 3932168 | tf_op jit(solution)/shard_map/ppermute | solution.py:39
  72.6 32.0 %copy-start.4 = (bf16[2,160,2048]{2,0,1:T(2,128)(2,1)S(1)}, bf16[2,160,2048]{2,0,1:T(2,128)(2,1)}, u32[]{:S(2)}) copy-start(bf16[2,160,2048]{2,0,1:T(2,128)(2,1)} %copy-done.3) | copy-start | bytes 3932164
  78.0 38.9 %collective-permute-start.6 = (bf16[2,160,2048]{2,1,0:T(8,128)(2,1)S(1)}, bf16[2,160,2048]{2,1,0:T(8,128)(2,1)}, u32[]{:S(2)}, u32[]{:S(2)}) collective-permute-start(bf16[2,160,2048]{2,1,0:T(8,128)(2,1)S(1)} %broadcast_select_fusion.1), channel_id=1, source_target_pairs={{0,4},{4,0},{8,12},{12,8},{16,20},{20,16},{24,28},{28,24},{1,5},{5... | collective-permute-start | bytes 3932168 | tf_op jit(solution)/shard_map/ppermute | solution.py:44
  107.4 30.8 %collective-permute-start.8 = (bf16[2,160,2048]{2,1,0:T(8,128)(2,1)S(1)}, bf16[2,160,2048]{2,1,0:T(8,128)(2,1)}, u32[]{:S(2)}, u32[]{:S(2)}) collective-permute-start(bf16[2,160,2048]{2,1,0:T(8,128)(2,1)S(1)} %broadcast_select_fusion), channel_id=1, source_target_pairs={{0,4},{4,0},{8,12},{12,8},{16,20},{20,16},{24,28},{28,24},{1,5},{5... | collective-permute-start | bytes 3932168 | tf_op jit(solution)/shard_map/ppermute | solution.py:44
  107.7 40.6 %collective-permute-start.3 = (bf16[2,160,2048]{2,1,0:T(8,128)(2,1)}, bf16[2,160,2048]{2,1,0:T(8,128)(2,1)}, u32[]{:S(2)}, u32[]{:S(2)}) collective-permute-start(bf16[2,160,2048]{2,1,0:T(8,128)(2,1)} %collective-permute-done.2.second_ref), channel_id=1, source_target_pairs={{0,8},{4,12},{8,16},{12,20},{16,24},{20,28},{1,9},{5,13},{9,17},{1... | collective-permute-start | bytes 3932168 | tf_op jit(solution)/shard_map/ppermute | solution.py:39
  111.2 41.5 %collective-permute-start.5 = (bf16[2,160,2048]{2,1,0:T(8,128)(2,1)}, bf16[2,160,2048]{2,1,0:T(8,128)(2,1)}, u32[]{:S(2)}, u32[]{:S(2)}) collective-permute-start(bf16[2,160,2048]{2,1,0:T(8,128)(2,1)} %collective-permute-done.4.second_ref), channel_id=1, source_target_pairs={{8,0},{12,4},{16,8},{20,12},{24,16},{28,20},{9,1},{13,5},{17,9},{2... | collective-permute-start | bytes 3932168 | tf_op jit(solution)/shard_map/ppermute | solution.py:39
  116.9 49.6 %collective-permute-start.7 = (bf16[2,160,2048]{2,1,0:T(8,128)(2,1)}, bf16[2,160,2048]{2,1,0:T(8,128)(2,1)S(1)}, u32[]{:S(2)}, u32[]{:S(2)}) collective-permute-start(bf16[2,160,2048]{2,1,0:T(8,128)(2,1)} %collective-permute-done.6.second_ref), channel_id=1, source_target_pairs={{0,8},{4,12},{8,16},{12,20},{16,24},{20,28},{1,9},{5,13},{9,17},{1... | collective-permute-start | bytes 3932168 | tf_op jit(solution)/shard_map/ppermute | solution.py:39
  138.2 33.8 %collective-permute-start.9 = (bf16[2,160,2048]{2,1,0:T(8,128)(2,1)}, bf16[2,160,2048]{2,1,0:T(8,128)(2,1)S(1)}, u32[]{:S(2)}, u32[]{:S(2)}) collective-permute-start(bf16[2,160,2048]{2,1,0:T(8,128)(2,1)} %collective-permute-done.8.second_ref), channel_id=1, source_target_pairs={{8,0},{12,4},{16,8},{20,12},{24,16},{28,20},{9,1},{13,5},{17,9},{2... | collective-permute-start | bytes 3932168 | tf_op jit(solution)/shard_map/ppermute | solution.py:39
  166.5 1.1 copy-start.5
  171.9 5.5 %copy-start.7 = (f32[2,8,512]{2,1,0:T(8,128)S(1)}, f32[2,8,512]{2,1,0:T(8,128)}, u32[]{:S(2)}) copy-start(f32[2,8,512]{2,1,0:T(8,128)} %shard_map.68) | copy-start | bytes 98308
  172.0 5.5 %copy-start.8 = (f32[2,8,512]{2,1,0:T(8,128)S(1)}, f32[2,8,512]{2,1,0:T(8,128)}, u32[]{:S(2)}) copy-start(f32[2,8,512]{2,1,0:T(8,128)} %shard_map.70) | copy-start | bytes 98308
  172.0 5.5 %copy-start.9 = (f32[2,8,512]{2,1,0:T(8,128)S(1)}, f32[2,8,512]{2,1,0:T(8,128)}, u32[]{:S(2)}) copy-start(f32[2,8,512]{2,1,0:T(8,128)} %shard_map.72) | copy-start | bytes 98308
  172.0 5.5 %copy-start.10 = (f32[2,8,512]{2,1,0:T(8,128)S(1)}, f32[2,8,512]{2,1,0:T(8,128)}, u32[]{:S(2)}) copy-start(f32[2,8,512]{2,1,0:T(8,128)} %shard_map.73) | copy-start | bytes 98308
  172.0 5.5 %copy-start.11 = (f32[2,8,512]{2,1,0:T(8,128)S(1)}, f32[2,8,512]{2,1,0:T(8,128)}, u32[]{:S(2)}) copy-start(f32[2,8,512]{2,1,0:T(8,128)} %shard_map.65) | copy-start | bytes 98308
  172.0 5.5 %copy-start.12 = (f32[2,8,512]{2,1,0:T(8,128)S(1)}, f32[2,8,512]{2,1,0:T(8,128)}, u32[]{:S(2)}) copy-start(f32[2,8,512]{2,1,0:T(8,128)} %shard_map.67) | copy-start | bytes 98308
  172.0 5.5 %copy-start.13 = (f32[2,8,512]{2,1,0:T(8,128)S(1)}, f32[2,8,512]{2,1,0:T(8,128)}, u32[]{:S(2)}) copy-start(f32[2,8,512]{2,1,0:T(8,128)} %shard_map.69) | copy-start | bytes 98308
  172.0 13.0 %copy-start.15 = (s32[1,4]{1,0:T(1,128)S(1)}, s32[1,4]{1,0:T(1,128)}, u32[]{:S(2)}) copy-start(s32[1,4]{1,0:T(1,128)} %param.11) | copy-start | bytes 52
  172.0 1.1 copy-start.6
  177.5 28.5 %copy-start.14 = (f32[2,8,512]{2,1,0:T(8,128)S(1)}, f32[2,8,512]{2,1,0:T(8,128)}, u32[]{:S(2)}) copy-start(f32[2,8,512]{2,1,0:T(8,128)} %shard_map.71) | copy-start | bytes 98308
  179.2 26.7 %all-to-all-start = ((f32[8,2,8,512]{3,2,1,0:T(8,128)}), f32[8,2,8,512]{3,2,1,0:T(8,128)S(1)}, u32[]{:S(2)}, u32[]{:S(2)}) async-start(f32[8,2,8,512]{3,2,1,0:T(8,128)} %select_select_fusion), calls=%async_computation | async-start | bytes 524288 | tf_op jit(solution)/shard_map/all_to_all | solution.py:198

commit v17 on v16

--- a/solution.py
+++ b/solution.py
@@ -16,11 +16,11 @@
 LOOK_RG = 4
 
 
-def padded_2(cells, sides, width):
+def padded_2(cells, sides, width, extra):
     for axis, dim in sides:
         count = lax.axis_size(axis)
         ends = count - 1
-        head = lax.slice_in_dim(cells, 0, width, axis=dim)
+        head = lax.slice_in_dim(cells, 0, width + extra, axis=dim)
         tail = lax.slice_in_dim(cells, cells.shape[dim] - width, cells.shape[dim], axis=dim)
         cells = jnp.concatenate(
             [
@@ -106,8 +106,7 @@
     nlines = shift_range.shape[0]
     border = OFFAZ + 4
     start = border + shift_lines - 3
-    window = lax.dynamic_slice_in_dim(padded, start, nlines + 7, 1)
-    window = jnp.pad(window, ((0, 0), (0, 9), (0, 0)))
+    window = lax.dynamic_slice_in_dim(padded, start, nlines + 16, 1)
     weights = table[kern_lines]
     coeff = jnp.take(table, kern_range, axis=0)
     shift = (shift_range + OFFRG)[:, None]
@@ -168,7 +167,7 @@
 
 
 def shards(slc, az_offset, az_kernel, rg_offset, rg_kernel, partners):
-    padded = padded_2(slc, (("az", 2),), OFFAZ + 4)
+    padded = padded_2(slc, (("az", 2),), OFFAZ + 4, 9)
     own_left, own_right = resample_block(padded[0], az_offset[0], az_kernel[0], rg_offset[0], rg_kernel[0])
     date = lax.axis_index("date")
     even = date % 2 == 0

time: 208 us -> 204 us (0.981)
  waiting for transfers between devices: 49.1 us -> 45.2 us
  starting transfers between devices: 30.6 us -> 28.4 us
    slice x1 -> x2, local copies, waits for them, and re-layouts: 1.06 us -> 3.71 us  [the longest x1 1.89 us: padded_2(): head = lax.slice_in_dim(cells, 0, width + extra, axis=dim)]
    ppermute x6, waiting for transfers between devices: 36.7 us -> 34.1 us  [shifted(): return lax.ppermute(block, axis, route)]
  transfers between devices with their start and end apart: 11 -> 11, of which waited for: 4 -> 4; matrix products, arithmetic and copies ran while one was open for 7% -> 8% of each run, Pallas kernels for 24% -> 25%
where the time goes in v17:
time: 204 us; the launch traced here: 201 us
  Pallas kernels  75.2 us (37%)
  waiting for transfers between devices  45.2 us (22%)
  starting transfers between devices  28.4 us (14%)
  between operations  20.7 us (10%)
  local copies, waits for them, and re-layouts  16.3 us (8%)
  other arithmetic  15.2 us (7%)
    pallas_call x2, Pallas kernels, resample_half(): pl.pallas_call(functools.partial(resample_kernel, side), grid=(2, nlines...  40.3 us
    pallas_call x8, Pallas kernels, looks(): pl.pallas_call(looks_kernel, grid=(width // CHUNK,), in_specs=[spec, spec...  34.9 us
    ppermute x6, waiting for transfers between devices, shifted(): return lax.ppermute(block, axis, route)  34.1 us
    ppermute x6, starting transfers between devices, shifted(): return lax.ppermute(block, axis, route)  17.5 us
    ppermute x2, waiting for transfers between devices, swapped(): return lax.ppermute(block, axis, [(i, i ^ 1) for i in range(count)])  11.1 us
    pallas_call x2, local copies, waits for them, and re-layouts, resample_half(): pl.pallas_call(functools.partial(resample_kernel, side), grid=(2, nlines...  5.33 us
    all_to_all x1, starting transfers between devices, shards(): got = lax.all_to_all(sent, 'date', 0, 0, tiled=True)  5 us
  transfers between devices with their start and end apart: 11, of which 4 were waited for; matrix products, arithmetic and copies ran while one was open for 8% of the time, Pallas kernels for 25%

profile of v17, /device:TPU:0, one launch (start us, length us, event | category | flops | bytes accessed | tf_op | source)
XLA Modules:
  0.0 200.9 jit_solution(4886627479663813674)
XLA Ops:
  0.0 1.8 slice.131
  1.8 2.4 %collective-permute-start = (bf16[1,2,16,4096]{3,2,1,0:T(8,128)(2,1)}, bf16[1,2,16,4096]{3,2,1,0:T(8,128)(2,1)S(1)}, u32[]{:S(2)}, u32[]{:S(2)}) collective-permute-start(bf16[1,2,16,4096]{3,2,1,0:T(8,128)(2,1)} %slice.131), channel_id=1, source_target_pairs={{0,1},{1,2},{2,3},{4,5},{5,6},{6,7},{8,9},{9,10},{10,11},{12,13},{... | collective-permute-start | bytes 786440 | tf_op jit(solution)/shard_map/ppermute | solution.py:27
  4.2 1.9 slice.132
  6.1 1.3 collective-permute-start.1
  7.4 0.7 add_bitcast_fusion
  8.1 0.7 compare_select_fusion
  8.8 0.1 fusion.17
  8.9 0.7 compare_and_fusion
  10.9 0.1 copy.22
  11.0 0.7 fusion.14.weights_ref
  11.7 0.7 copy.23.shift_ref
  12.4 0.7 gather_fusion
  13.1 0.7 broadcast_select_fusion.2.coeff_ref
  13.8 0.0 collective-permute-done
  13.8 0.0 collective-permute-done.1
  13.8 3.9 %fusion.2.window_ref = bf16[2,176,4096]{2,1,0:T(8,128)(2,1)} fusion(s32[]{:T(128)S(6)} %select_n.544, bf16[1,2,16,4096]{3,2,1,0:T(8,128)(2,1)S(1)} %collective-permute-done, bf16[1,2,160,4096]{3,2,1,0:T(8,128)(2,1)S(1)} %copy-done.5, bf16[1,2,25,4096]{3,2,1,0:T(8,128)(2,1)S(1)} %collective-permute-done.1), kind=kLoop, calls=%fused_computation.6 | loop fusion | flops 8650752 | bytes 6176772 | tf_op jit(solution)/shard_map/dynamic_slice | solution.py:109
  17.7 20.2 %shard_map.64 = bf16[2,160,2048]{2,1,0:T(8,128)(2,1)} custom-call(f32[8]{0:T(128)} %fusion.14.weights_ref, bf16[2,176,4096]{2,1,0:T(8,128)(2,1)} %fusion.2.window_ref, f32[160,8]{1,0:T(8,128)} %broadcast_select_fusion.2.coeff_ref, s32[160,1]{1,0:T(8,128)} %copy.23.shift_ref), custom_call_target="tpu_custom_call" | custom-call | flops 39321600 | bytes 3932160 | tf_op jit(solution)/shard_map/pallas_call | solution.py:87
  37.9 2.7 %copy.24 = bf16[2,160,2048]{2,0,1:T(2,128)(2,1)S(1)} copy(bf16[2,160,2048]{2,1,0:T(8,128)(2,1)} %shard_map.64) | data formatting | bytes 2621440 | tf_op jit(solution)/shard_map/pallas_call | solution.py:87
  40.6 0.7 copy.36
  41.3 0.4 copy-done.2
  41.7 5.4 %collective-permute-start.2 = (bf16[2,160,2048]{2,1,0:T(8,128)(2,1)S(1)}, bf16[2,160,2048]{2,1,0:T(8,128)(2,1)}, u32[]{:S(2)}, u32[]{:S(2)}) collective-permute-start(bf16[2,160,2048]{2,1,0:T(8,128)(2,1)S(1)} %bitcast.92), channel_id=1, source_target_pairs={{0,8},{4,12},{8,16},{12,20},{16,24},{20,28},{1,9},{5,13},{9,17},{1... | collective-permute-start | bytes 3932168 | tf_op jit(solution)/shard_map/ppermute | solution.py:39
  47.1 20.0 %shard_map.66 = bf16[2,160,2048]{2,1,0:T(8,128)(2,1)} custom-call(f32[8]{0:T(128)} %fusion.14.weights_ref, bf16[2,176,4096]{2,1,0:T(8,128)(2,1)} %fusion.2.window_ref, f32[160,8]{1,0:T(8,128)} %broadcast_select_fusion.2.coeff_ref, s32[160,1]{1,0:T(8,128)} %copy.23.shift_ref), custom_call_target="tpu_custom_call" | custom-call | flops 39321600 | bytes 3932160 | tf_op jit(solution)/shard_map/pallas_call | solution.py:87
  67.1 2.7 %copy.27 = bf16[2,160,2048]{2,0,1:T(2,128)(2,1)S(1)} copy(bf16[2,160,2048]{2,1,0:T(8,128)(2,1)} %shard_map.66) | data formatting | bytes 2621440 | tf_op jit(solution)/shard_map/pallas_call | solution.py:87
  69.8 0.7 copy.35
  70.5 0.4 copy-done.3
  71.0 1.5 collective-permute-start.4
  72.4 0.0 collective-permute-done.2.second_ref
  72.5 2.9 %broadcast_select_fusion.1 = bf16[2,160,2048]{2,1,0:T(8,128)(2,1)S(1)} fusion(bf16[2,160,2048]{2,1,0:T(8,128)(2,1)} %collective-permute-done.2.second_ref, pred[]{:T(512)S(6)} %eq.195, bf16[2,20,8,2048]{3,0,1,2:T(2,128)(2,1)} %bitcast.103), kind=kLoop, calls=%fused_computation.10 | loop fusion | flops 655360 | bytes 3932161 | tf_op jit(solution)/shard_map/jit(_where)/select_n | solution.py:179
  75.4 2.0 collective-permute-start.6
  77.3 23.7 %collective-permute-done.4.second_ref = bf16[2,160,2048]{2,1,0:T(8,128)(2,1)} collective-permute-done((bf16[2,160,2048]{2,1,0:T(8,128)(2,1)S(1)}, bf16[2,160,2048]{2,1,0:T(8,128)(2,1)}, u32[]{:S(2)}, u32[]{:S(2)}) %collective-permute-start.4) | collective-permute-done | bytes 1310752 | tf_op jit(solution)/shard_map/ppermute | solution.py:39
  101.0 0.0 copy-done.4
  101.0 2.8 %broadcast_select_fusion = bf16[2,160,2048]{2,1,0:T(8,128)(2,1)S(1)} fusion(bf16[2,160,2048]{2,1,0:T(8,128)(2,1)} %collective-permute-done.4.second_ref, pred[]{:T(512)S(6)} %eq.195, bf16[2,20,8,2048]{3,0,1,2:T(2,128)(2,1)S(1)} %bitcast.105), kind=kLoop, calls=%fused_computation.9 | loop fusion | flops 655360 | bytes 3932161 | tf_op jit(solution)/shard_map/jit(_where)/select_n | solution.py:176
  103.9 0.3 collective-permute-start.8
  104.1 3.5 %collective-permute-start.3 = (bf16[2,160,2048]{2,1,0:T(8,128)(2,1)}, bf16[2,160,2048]{2,1,0:T(8,128)(2,1)}, u32[]{:S(2)}, u32[]{:S(2)}) collective-permute-start(bf16[2,160,2048]{2,1,0:T(8,128)(2,1)} %collective-permute-done.2.second_ref), channel_id=1, source_target_pairs={{0,8},{4,12},{8,16},{12,20},{16,24},{20,28},{1,9},{5,13},{9,17},{1... | collective-permute-start | bytes 3932168 | tf_op jit(solution)/shard_map/ppermute | solution.py:39
  107.6 1.3 collective-permute-start.5
  108.9 4.4 %shard_map.68 = f32[2,8,512]{2,1,0:T(8,128)} custom-call(bf16[2,160,2048]{2,1,0:T(8,128)(2,1)} %bitcast.93, bf16[2,160,2048]{2,1,0:T(8,128)(2,1)} %collective-permute-done.2.second_ref), custom_call_target="tpu_custom_call" | custom-call | flops 13107200 | bytes 2621440 | tf_op jit(solution)/shard_map/pallas_call | solution.py:147
  113.3 0.0 collective-permute-done.6.second_ref
  113.3 4.6 %collective-permute-start.7 = (bf16[2,160,2048]{2,1,0:T(8,128)(2,1)}, bf16[2,160,2048]{2,1,0:T(8,128)(2,1)S(1)}, u32[]{:S(2)}, u32[]{:S(2)}) collective-permute-start(bf16[2,160,2048]{2,1,0:T(8,128)(2,1)} %collective-permute-done.6.second_ref), channel_id=1, source_target_pairs={{0,8},{4,12},{8,16},{12,20},{16,24},{20,28},{1,9},{5,13},{9,17},{1... | collective-permute-start | bytes 3932168 | tf_op jit(solution)/shard_map/ppermute | solution.py:39
  117.9 4.4 %shard_map.70 = f32[2,8,512]{2,1,0:T(8,128)} custom-call(bf16[2,160,2048]{2,1,0:T(8,128)(2,1)} %bitcast.98, bf16[2,160,2048]{2,1,0:T(8,128)(2,1)} %collective-permute-done.4.second_ref), custom_call_target="tpu_custom_call" | custom-call | flops 13107200 | bytes 2621440 | tf_op jit(solution)/shard_map/pallas_call | solution.py:147
  122.3 11.1 %collective-permute-done.8.second_ref = bf16[2,160,2048]{2,1,0:T(8,128)(2,1)} collective-permute-done((bf16[2,160,2048]{2,1,0:T(8,128)(2,1)S(1)}, bf16[2,160,2048]{2,1,0:T(8,128)(2,1)}, u32[]{:S(2)}, u32[]{:S(2)}) %collective-permute-start.8) | collective-permute-done | bytes 1310752 | tf_op jit(solution)/shard_map/ppermute | solution.py:44
  133.4 1.3 collective-permute-start.9
  134.7 4.4 %shard_map.72 = f32[2,8,512]{2,1,0:T(8,128)} custom-call(bf16[2,160,2048]{2,1,0:T(8,128)(2,1)} %bitcast.94, bf16[2,160,2048]{2,1,0:T(8,128)(2,1)} %collective-permute-done.6.second_ref), custom_call_target="tpu_custom_call" | custom-call | flops 13107200 | bytes 2621440 | tf_op jit(solution)/shard_map/pallas_call | solution.py:147
  139.1 4.4 %shard_map.73 = f32[2,8,512]{2,1,0:T(8,128)} custom-call(bf16[2,160,2048]{2,1,0:T(8,128)(2,1)} %bitcast.99, bf16[2,160,2048]{2,1,0:T(8,128)(2,1)} %collective-permute-done.8.second_ref), custom_call_target="tpu_custom_call" | custom-call | flops 13107200 | bytes 2621440 | tf_op jit(solution)/shard_map/pallas_call | solution.py:147
  143.5 0.0 collective-permute-done.3.second_ref
  143.5 4.4 %shard_map.65 = f32[2,8,512]{2,1,0:T(8,128)} custom-call(bf16[2,160,2048]{2,1,0:T(8,128)(2,1)} %bitcast.95, bf16[2,160,2048]{2,1,0:T(8,128)(2,1)} %collective-permute-done.3.second_ref), custom_call_target="tpu_custom_call" | custom-call | flops 13107200 | bytes 2621440 | tf_op jit(solution)/shard_map/pallas_call | solution.py:147
  147.8 0.0 collective-permute-done.5.second_ref
  147.8 4.4 %shard_map.67 = f32[2,8,512]{2,1,0:T(8,128)} custom-call(bf16[2,160,2048]{2,1,0:T(8,128)(2,1)} %bitcast.100, bf16[2,160,2048]{2,1,0:T(8,128)(2,1)} %collective-permute-done.5.second_ref), custom_call_target="tpu_custom_call" | custom-call | flops 13107200 | bytes 2621440 | tf_op jit(solution)/shard_map/pallas_call | solution.py:147
  152.2 9.3 %collective-permute-done.7.second_ref = bf16[2,160,2048]{2,1,0:T(8,128)(2,1)S(1)} collective-permute-done((bf16[2,160,2048]{2,1,0:T(8,128)(2,1)}, bf16[2,160,2048]{2,1,0:T(8,128)(2,1)S(1)}, u32[]{:S(2)}, u32[]{:S(2)}) %collective-permute-start.7) | collective-permute-done | bytes 1310752 | tf_op jit(solution)/shard_map/ppermute | solution.py:39
  161.5 1.1 copy-done.6
  162.6 4.3 %shard_map.69 = f32[2,8,512]{2,1,0:T(8,128)} custom-call(bf16[2,160,2048]{2,1,0:T(8,128)(2,1)} %bitcast.96, bf16[2,160,2048]{2,1,0:T(8,128)(2,1)} %copy-done.6), custom_call_target="tpu_custom_call" | custom-call | flops 13107200 | bytes 2621440 | tf_op jit(solution)/shard_map/pallas_call | solution.py:147
  167.0 0.0 copy-start.11
  167.0 0.0 copy-start.16
  167.0 1.0 collective-permute-done.9.second_ref
  168.1 1.1 copy-done.7
  169.1 4.4 %shard_map.71 = f32[2,8,512]{2,1,0:T(8,128)} custom-call(bf16[2,160,2048]{2,1,0:T(8,128)(2,1)} %bitcast.101, bf16[2,160,2048]{2,1,0:T(8,128)(2,1)} %copy-done.7), custom_call_target="tpu_custom_call" | custom-call | flops 13107200 | bytes 2621440 | tf_op jit(solution)/shard_map/pallas_call | solution.py:147
  173.5 0.0 copy-done.10
  173.5 0.0 copy-done.11
  173.5 0.0 copy-done.12
  173.5 0.0 copy-done.13
  173.6 1.6 select_select_fusion
  175.2 5.0 %all-to-all-start = ((f32[8,2,8,512]{3,2,1,0:T(8,128)}), f32[8,2,8,512]{3,2,1,0:T(8,128)S(1)}, u32[]{:S(2)}, u32[]{:S(2)}) async-start(f32[8,2,8,512]{3,2,1,0:T(8,128)} %select_select_fusion), calls=%async_computation | async-start | bytes 524288 | tf_op jit(solution)/shard_map/all_to_all | solution.py:197
  180.2 0.7 fusion.47
  199.8 0.0 all-to-all-done
  200.2 0.7 maximum_bitcast_fusion
  (43 shorter events, 0.4 us)
Async XLA Ops:
  0.0 13.8 %copy-start.5 = (bf16[1,2,160,4096]{3,2,1,0:T(8,128)(2,1)S(1)}, bf16[1,2,160,4096]{3,2,1,0:T(8,128)(2,1)}, u32[]{:S(2)}) copy-start(bf16[1,2,160,4096]{3,2,1,0:T(8,128)(2,1)} %param.6) | copy-start | bytes 7864324
  1.8 12.0 %collective-permute-start = (bf16[1,2,16,4096]{3,2,1,0:T(8,128)(2,1)}, bf16[1,2,16,4096]{3,2,1,0:T(8,128)(2,1)S(1)}, u32[]{:S(2)}, u32[]{:S(2)}) collective-permute-start(bf16[1,2,16,4096]{3,2,1,0:T(8,128)(2,1)} %slice.131), channel_id=1, source_target_pairs={{0,1},{1,2},{2,3},{4,5},{5,6},{6,7},{8,9},{9,10},{10,11},{12,13},{... | collective-permute-start | bytes 786440 | tf_op jit(solution)/shard_map/ppermute | solution.py:27
  6.1 7.7 %collective-permute-start.1 = (bf16[1,2,25,4096]{3,2,1,0:T(8,128)(2,1)}, bf16[1,2,25,4096]{3,2,1,0:T(8,128)(2,1)S(1)}, u32[]{:S(2)}, u32[]{:S(2)}) collective-permute-start(bf16[1,2,25,4096]{3,2,1,0:T(8,128)(2,1)} %slice.132), channel_id=1, source_target_pairs={{1,0},{2,1},{3,2},{5,4},{6,5},{7,6},{9,8},{10,9},{11,10},{13,12},{... | collective-permute-start | bytes 1228808 | tf_op jit(solution)/shard_map/ppermute | solution.py:29
  40.6 1.1 copy-start.2
  41.7 25.4 %copy-start = (bf16[2,20,8,2048]{3,2,1,0:T(8,128)(2,1)}, bf16[2,20,8,2048]{3,2,1,0:T(8,128)(2,1)S(1)}, u32[]{:S(2)}) copy-start(bf16[2,20,8,2048]{3,2,1,0:T(8,128)(2,1)S(1)} %copy.36) | copy-start | bytes 3932164
  41.7 30.8 %collective-permute-start.2 = (bf16[2,160,2048]{2,1,0:T(8,128)(2,1)S(1)}, bf16[2,160,2048]{2,1,0:T(8,128)(2,1)}, u32[]{:S(2)}, u32[]{:S(2)}) collective-permute-start(bf16[2,160,2048]{2,1,0:T(8,128)(2,1)S(1)} %bitcast.92), channel_id=1, source_target_pairs={{0,8},{4,12},{8,16},{12,20},{16,24},{20,28},{1,9},{5,13},{9,17},{1... | collective-permute-start | bytes 3932168 | tf_op jit(solution)/shard_map/ppermute | solution.py:39
  69.8 1.1 copy-start.3
  71.0 4.4 %copy-start.1 = (bf16[2,20,8,2048]{3,2,1,0:T(8,128)(2,1)}, bf16[2,20,8,2048]{3,2,1,0:T(8,128)(2,1)S(1)}, u32[]{:S(2)}) copy-start(bf16[2,20,8,2048]{3,2,1,0:T(8,128)(2,1)S(1)} %copy.35) | copy-start | bytes 3932164
  71.0 30.1 %collective-permute-start.4 = (bf16[2,160,2048]{2,1,0:T(8,128)(2,1)S(1)}, bf16[2,160,2048]{2,1,0:T(8,128)(2,1)}, u32[]{:S(2)}, u32[]{:S(2)}) collective-permute-start(bf16[2,160,2048]{2,1,0:T(8,128)(2,1)S(1)} %bitcast.97), channel_id=1, source_target_pairs={{8,0},{12,4},{16,8},{20,12},{24,16},{28,20},{9,1},{13,5},{17,9},{2... | collective-permute-start | bytes 3932168 | tf_op jit(solution)/shard_map/ppermute | solution.py:39
  72.4 28.6 %copy-start.4 = (bf16[2,160,2048]{2,0,1:T(2,128)(2,1)S(1)}, bf16[2,160,2048]{2,0,1:T(2,128)(2,1)}, u32[]{:S(2)}) copy-start(bf16[2,160,2048]{2,0,1:T(2,128)(2,1)} %copy-done.3) | copy-start | bytes 3932164
  75.4 37.9 %collective-permute-start.6 = (bf16[2,160,2048]{2,1,0:T(8,128)(2,1)S(1)}, bf16[2,160,2048]{2,1,0:T(8,128)(2,1)}, u32[]{:S(2)}, u32[]{:S(2)}) collective-permute-start(bf16[2,160,2048]{2,1,0:T(8,128)(2,1)S(1)} %broadcast_select_fusion.1), channel_id=1, source_target_pairs={{0,4},{4,0},{8,12},{12,8},{16,20},{20,16},{24,28},{28,24},{1,5},{5... | collective-permute-start | bytes 3932168 | tf_op jit(solution)/shard_map/ppermute | solution.py:44
  103.9 29.5 %collective-permute-start.8 = (bf16[2,160,2048]{2,1,0:T(8,128)(2,1)S(1)}, bf16[2,160,2048]{2,1,0:T(8,128)(2,1)}, u32[]{:S(2)}, u32[]{:S(2)}) collective-permute-start(bf16[2,160,2048]{2,1,0:T(8,128)(2,1)S(1)} %broadcast_select_fusion), channel_id=1, source_target_pairs={{0,4},{4,0},{8,12},{12,8},{16,20},{20,16},{24,28},{28,24},{1,5},{5... | collective-permute-start | bytes 3932168 | tf_op jit(solution)/shard_map/ppermute | solution.py:44
  104.1 39.3 %collective-permute-start.3 = (bf16[2,160,2048]{2,1,0:T(8,128)(2,1)}, bf16[2,160,2048]{2,1,0:T(8,128)(2,1)}, u32[]{:S(2)}, u32[]{:S(2)}) collective-permute-start(bf16[2,160,2048]{2,1,0:T(8,128)(2,1)} %collective-permute-done.2.second_ref), channel_id=1, source_target_pairs={{0,8},{4,12},{8,16},{12,20},{16,24},{20,28},{1,9},{5,13},{9,17},{1... | collective-permute-start | bytes 3932168 | tf_op jit(solution)/shard_map/ppermute | solution.py:39
  107.6 40.2 %collective-permute-start.5 = (bf16[2,160,2048]{2,1,0:T(8,128)(2,1)}, bf16[2,160,2048]{2,1,0:T(8,128)(2,1)}, u32[]{:S(2)}, u32[]{:S(2)}) collective-permute-start(bf16[2,160,2048]{2,1,0:T(8,128)(2,1)} %collective-permute-done.4.second_ref), channel_id=1, source_target_pairs={{8,0},{12,4},{16,8},{20,12},{24,16},{28,20},{9,1},{13,5},{17,9},{2... | collective-permute-start | bytes 3932168 | tf_op jit(solution)/shard_map/ppermute | solution.py:39
  113.3 48.2 %collective-permute-start.7 = (bf16[2,160,2048]{2,1,0:T(8,128)(2,1)}, bf16[2,160,2048]{2,1,0:T(8,128)(2,1)S(1)}, u32[]{:S(2)}, u32[]{:S(2)}) collective-permute-start(bf16[2,160,2048]{2,1,0:T(8,128)(2,1)} %collective-permute-done.6.second_ref), channel_id=1, source_target_pairs={{0,8},{4,12},{8,16},{12,20},{16,24},{20,28},{1,9},{5,13},{9,17},{1... | collective-permute-start | bytes 3932168 | tf_op jit(solution)/shard_map/ppermute | solution.py:39
  133.4 34.7 %collective-permute-start.9 = (bf16[2,160,2048]{2,1,0:T(8,128)(2,1)}, bf16[2,160,2048]{2,1,0:T(8,128)(2,1)S(1)}, u32[]{:S(2)}, u32[]{:S(2)}) collective-permute-start(bf16[2,160,2048]{2,1,0:T(8,128)(2,1)} %collective-permute-done.8.second_ref), channel_id=1, source_target_pairs={{8,0},{12,4},{16,8},{20,12},{24,16},{28,20},{9,1},{13,5},{17,9},{2... | collective-permute-start | bytes 3932168 | tf_op jit(solution)/shard_map/ppermute | solution.py:39
  161.5 1.1 copy-start.6
  167.0 6.5 %copy-start.8 = (f32[2,8,512]{2,1,0:T(8,128)S(1)}, f32[2,8,512]{2,1,0:T(8,128)}, u32[]{:S(2)}) copy-start(f32[2,8,512]{2,1,0:T(8,128)} %shard_map.68) | copy-start | bytes 98308
  167.0 6.5 %copy-start.9 = (f32[2,8,512]{2,1,0:T(8,128)S(1)}, f32[2,8,512]{2,1,0:T(8,128)}, u32[]{:S(2)}) copy-start(f32[2,8,512]{2,1,0:T(8,128)} %shard_map.70) | copy-start | bytes 98308
  167.0 6.5 %copy-start.10 = (f32[2,8,512]{2,1,0:T(8,128)S(1)}, f32[2,8,512]{2,1,0:T(8,128)}, u32[]{:S(2)}) copy-start(f32[2,8,512]{2,1,0:T(8,128)} %shard_map.72) | copy-start | bytes 98308
  167.0 6.6 %copy-start.11 = (f32[2,8,512]{2,1,0:T(8,128)S(1)}, f32[2,8,512]{2,1,0:T(8,128)}, u32[]{:S(2)}) copy-start(f32[2,8,512]{2,1,0:T(8,128)} %shard_map.73) | copy-start | bytes 98308
  167.0 6.5 %copy-start.12 = (f32[2,8,512]{2,1,0:T(8,128)S(1)}, f32[2,8,512]{2,1,0:T(8,128)}, u32[]{:S(2)}) copy-start(f32[2,8,512]{2,1,0:T(8,128)} %shard_map.65) | copy-start | bytes 98308
  167.0 6.5 %copy-start.13 = (f32[2,8,512]{2,1,0:T(8,128)S(1)}, f32[2,8,512]{2,1,0:T(8,128)}, u32[]{:S(2)}) copy-start(f32[2,8,512]{2,1,0:T(8,128)} %shard_map.67) | copy-start | bytes 98308
  167.0 6.5 %copy-start.14 = (f32[2,8,512]{2,1,0:T(8,128)S(1)}, f32[2,8,512]{2,1,0:T(8,128)}, u32[]{:S(2)}) copy-start(f32[2,8,512]{2,1,0:T(8,128)} %shard_map.69) | copy-start | bytes 98308
  167.0 13.2 %copy-start.16 = (s32[1,4]{1,0:T(1,128)S(1)}, s32[1,4]{1,0:T(1,128)}, u32[]{:S(2)}) copy-start(s32[1,4]{1,0:T(1,128)} %param.11) | copy-start | bytes 52
  168.1 1.1 copy-start.7
  173.5 26.5 %copy-start.15 = (f32[2,8,512]{2,1,0:T(8,128)S(1)}, f32[2,8,512]{2,1,0:T(8,128)}, u32[]{:S(2)}) copy-start(f32[2,8,512]{2,1,0:T(8,128)} %shard_map.71) | copy-start | bytes 98308
  175.2 24.6 %all-to-all-start = ((f32[8,2,8,512]{3,2,1,0:T(8,128)}), f32[8,2,8,512]{3,2,1,0:T(8,128)S(1)}, u32[]{:S(2)}, u32[]{:S(2)}) async-start(f32[8,2,8,512]{3,2,1,0:T(8,128)} %select_select_fusion), calls=%async_computation | async-start | bytes 524288 | tf_op jit(solution)/shard_map/all_to_all | solution.py:197

commit v18 on v17

--- a/solution.py
+++ b/solution.py
@@ -51,7 +51,7 @@
     return jnp.sinc(place) * (0.5 + 0.5 * jnp.cos(jnp.pi * place / 4.5))
 
 
-ROWS = 32
+ROWS = 80
 EDGE = 128
 
 

time: 204 us -> 200 us (0.980)
  Pallas kernels: 75.2 us -> 70.6 us
    pallas_call x2, Pallas kernels: 40.3 us -> 35.7 us  [resample_half(): pl.pallas_call(functools.partial(resample_kernel, side), grid=(2, nlines...]
  transfers between devices with their start and end apart: 11 -> 11, of which waited for: 4 -> 5; matrix products, arithmetic and copies ran while one was open for 8% -> 8% of each run, Pallas kernels for 25% -> 25%
where the time goes in v18:
time: 200 us; the launch traced here: 197 us
  Pallas kernels  70.6 us (35%)
  waiting for transfers between devices  45.3 us (23%)
  starting transfers between devices  28.6 us (14%)
  between operations  20.7 us (10%)
  local copies, waits for them, and re-layouts  16.3 us (8%)
  other arithmetic  15.1 us (8%)
    pallas_call x2, Pallas kernels, resample_half(): pl.pallas_call(functools.partial(resample_kernel, side), grid=(2, nlines...  35.7 us
    pallas_call x8, Pallas kernels, looks(): pl.pallas_call(looks_kernel, grid=(width // CHUNK,), in_specs=[spec, spec...  34.9 us
    ppermute x6, waiting for transfers between devices, shifted(): return lax.ppermute(block, axis, route)  33.5 us
    ppermute x6, starting transfers between devices, shifted(): return lax.ppermute(block, axis, route)  17.7 us
    ppermute x2, waiting for transfers between devices, swapped(): return lax.ppermute(block, axis, [(i, i ^ 1) for i in range(count)])  11.8 us
    pallas_call x2, local copies, waits for them, and re-layouts, resample_half(): pl.pallas_call(functools.partial(resample_kernel, side), grid=(2, nlines...  5.33 us
    all_to_all x1, starting transfers between devices, shards(): got = lax.all_to_all(sent, 'date', 0, 0, tiled=True)  4.99 us
  transfers between devices with their start and end apart: 11, of which 5 were waited for; matrix products, arithmetic and copies ran while one was open for 8% of the time, Pallas kernels for 25%

profile of v18, /device:TPU:0, one launch (start us, length us, event | category | flops | bytes accessed | tf_op | source)
XLA Modules:
  0.0 196.5 jit_solution(5457076831506834885)
XLA Ops:
  0.0 1.8 slice.131
  1.8 2.4 %collective-permute-start = (bf16[1,2,16,4096]{3,2,1,0:T(8,128)(2,1)}, bf16[1,2,16,4096]{3,2,1,0:T(8,128)(2,1)S(1)}, u32[]{:S(2)}, u32[]{:S(2)}) collective-permute-start(bf16[1,2,16,4096]{3,2,1,0:T(8,128)(2,1)} %slice.131), channel_id=1, source_target_pairs={{0,1},{1,2},{2,3},{4,5},{5,6},{6,7},{8,9},{9,10},{10,11},{12,13},{... | collective-permute-start | bytes 786440 | tf_op jit(solution)/shard_map/ppermute | solution.py:27
  4.2 1.9 slice.132
  6.1 1.3 collective-permute-start.1
  7.4 0.7 add_bitcast_fusion
  8.1 0.7 compare_select_fusion
  8.8 0.1 fusion.17
  8.9 0.7 compare_and_fusion
  10.9 0.1 copy.22
  11.0 0.7 fusion.14.weights_ref
  11.7 0.7 copy.23.shift_ref
  12.4 0.7 gather_fusion
  13.1 0.7 broadcast_select_fusion.2.coeff_ref
  13.8 0.0 collective-permute-done
  13.8 0.0 collective-permute-done.1
  13.8 0.0 copy-done.5
  13.8 3.9 %fusion.2.window_ref = bf16[2,176,4096]{2,1,0:T(8,128)(2,1)} fusion(s32[]{:T(128)S(6)} %select_n.544, bf16[1,2,16,4096]{3,2,1,0:T(8,128)(2,1)S(1)} %collective-permute-done, bf16[1,2,160,4096]{3,2,1,0:T(8,128)(2,1)S(1)} %copy-done.5, bf16[1,2,25,4096]{3,2,1,0:T(8,128)(2,1)S(1)} %collective-permute-done.1), kind=kLoop, calls=%fused_computation.6 | loop fusion | flops 8650752 | bytes 6176772 | tf_op jit(solution)/shard_map/dynamic_slice | solution.py:109
  17.7 18.0 %shard_map.64 = bf16[2,160,2048]{2,1,0:T(8,128)(2,1)} custom-call(f32[8]{0:T(128)} %fusion.14.weights_ref, bf16[2,176,4096]{2,1,0:T(8,128)(2,1)} %fusion.2.window_ref, f32[160,8]{1,0:T(8,128)} %broadcast_select_fusion.2.coeff_ref, s32[160,1]{1,0:T(8,128)} %copy.23.shift_ref), custom_call_target="tpu_custom_call" | custom-call | flops 39321600 | bytes 3932160 | tf_op jit(solution)/shard_map/pallas_call | solution.py:87
  35.7 2.7 %copy.24 = bf16[2,160,2048]{2,0,1:T(2,128)(2,1)S(1)} copy(bf16[2,160,2048]{2,1,0:T(8,128)(2,1)} %shard_map.64) | data formatting | bytes 2621440 | tf_op jit(solution)/shard_map/pallas_call | solution.py:87
  38.4 0.7 copy.36
  39.1 0.4 copy-done.2
  39.4 5.4 %collective-permute-start.2 = (bf16[2,160,2048]{2,1,0:T(8,128)(2,1)S(1)}, bf16[2,160,2048]{2,1,0:T(8,128)(2,1)}, u32[]{:S(2)}, u32[]{:S(2)}) collective-permute-start(bf16[2,160,2048]{2,1,0:T(8,128)(2,1)S(1)} %bitcast.92), channel_id=1, source_target_pairs={{0,8},{4,12},{8,16},{12,20},{16,24},{20,28},{1,9},{5,13},{9,17},{1... | collective-permute-start | bytes 3932168 | tf_op jit(solution)/shard_map/ppermute | solution.py:39
  44.8 17.7 %shard_map.66 = bf16[2,160,2048]{2,1,0:T(8,128)(2,1)} custom-call(f32[8]{0:T(128)} %fusion.14.weights_ref, bf16[2,176,4096]{2,1,0:T(8,128)(2,1)} %fusion.2.window_ref, f32[160,8]{1,0:T(8,128)} %broadcast_select_fusion.2.coeff_ref, s32[160,1]{1,0:T(8,128)} %copy.23.shift_ref), custom_call_target="tpu_custom_call" | custom-call | flops 39321600 | bytes 3932160 | tf_op jit(solution)/shard_map/pallas_call | solution.py:87
  62.6 2.7 %copy.27 = bf16[2,160,2048]{2,0,1:T(2,128)(2,1)S(1)} copy(bf16[2,160,2048]{2,1,0:T(8,128)(2,1)} %shard_map.66) | data formatting | bytes 2621440 | tf_op jit(solution)/shard_map/pallas_call | solution.py:87
  65.2 0.7 copy.35
  66.0 0.4 copy-done.3
  66.4 1.3 collective-permute-start.4
  67.7 1.4 collective-permute-done.2.second_ref
  69.1 2.8 %broadcast_select_fusion.1 = bf16[2,160,2048]{2,1,0:T(8,128)(2,1)S(1)} fusion(bf16[2,160,2048]{2,1,0:T(8,128)(2,1)} %collective-permute-done.2.second_ref, pred[]{:T(512)S(6)} %eq.195, bf16[2,20,8,2048]{3,0,1,2:T(2,128)(2,1)} %bitcast.103), kind=kLoop, calls=%fused_computation.10 | loop fusion | flops 655360 | bytes 3932161 | tf_op jit(solution)/shard_map/jit(_where)/select_n | solution.py:179
  71.8 0.0 copy-done.1
  71.9 2.0 %collective-permute-start.6 = (bf16[2,160,2048]{2,1,0:T(8,128)(2,1)S(1)}, bf16[2,160,2048]{2,1,0:T(8,128)(2,1)}, u32[]{:S(2)}, u32[]{:S(2)}) collective-permute-start(bf16[2,160,2048]{2,1,0:T(8,128)(2,1)S(1)} %broadcast_select_fusion.1), channel_id=1, source_target_pairs={{0,4},{4,0},{8,12},{12,8},{16,20},{20,16},{24,28},{28,24},{1,5},{5... | collective-permute-start | bytes 3932168 | tf_op jit(solution)/shard_map/ppermute | solution.py:44
  73.8 22.6 %collective-permute-done.4.second_ref = bf16[2,160,2048]{2,1,0:T(8,128)(2,1)} collective-permute-done((bf16[2,160,2048]{2,1,0:T(8,128)(2,1)S(1)}, bf16[2,160,2048]{2,1,0:T(8,128)(2,1)}, u32[]{:S(2)}, u32[]{:S(2)}) %collective-permute-start.4) | collective-permute-done | bytes 1310752 | tf_op jit(solution)/shard_map/ppermute | solution.py:39
  96.5 2.8 %broadcast_select_fusion = bf16[2,160,2048]{2,1,0:T(8,128)(2,1)S(1)} fusion(bf16[2,160,2048]{2,1,0:T(8,128)(2,1)} %collective-permute-done.4.second_ref, pred[]{:T(512)S(6)} %eq.195, bf16[2,20,8,2048]{3,0,1,2:T(2,128)(2,1)S(1)} %bitcast.105), kind=kLoop, calls=%fused_computation.9 | loop fusion | flops 655360 | bytes 3932161 | tf_op jit(solution)/shard_map/jit(_where)/select_n | solution.py:176
  99.3 0.3 collective-permute-start.8
  99.6 3.7 %collective-permute-start.3 = (bf16[2,160,2048]{2,1,0:T(8,128)(2,1)}, bf16[2,160,2048]{2,1,0:T(8,128)(2,1)}, u32[]{:S(2)}, u32[]{:S(2)}) collective-permute-start(bf16[2,160,2048]{2,1,0:T(8,128)(2,1)} %collective-permute-done.2.second_ref), channel_id=1, source_target_pairs={{0,8},{4,12},{8,16},{12,20},{16,24},{20,28},{1,9},{5,13},{9,17},{1... | collective-permute-start | bytes 3932168 | tf_op jit(solution)/shard_map/ppermute | solution.py:39
  103.2 1.3 collective-permute-start.5
  104.5 4.4 %shard_map.68 = f32[2,8,512]{2,1,0:T(8,128)} custom-call(bf16[2,160,2048]{2,1,0:T(8,128)(2,1)} %bitcast.93, bf16[2,160,2048]{2,1,0:T(8,128)(2,1)} %collective-permute-done.2.second_ref), custom_call_target="tpu_custom_call" | custom-call | flops 13107200 | bytes 2621440 | tf_op jit(solution)/shard_map/pallas_call | solution.py:147
  108.9 0.0 collective-permute-done.6.second_ref
  108.9 4.6 %collective-permute-start.7 = (bf16[2,160,2048]{2,1,0:T(8,128)(2,1)}, bf16[2,160,2048]{2,1,0:T(8,128)(2,1)S(1)}, u32[]{:S(2)}, u32[]{:S(2)}) collective-permute-start(bf16[2,160,2048]{2,1,0:T(8,128)(2,1)} %collective-permute-done.6.second_ref), channel_id=1, source_target_pairs={{0,8},{4,12},{8,16},{12,20},{16,24},{20,28},{1,9},{5,13},{9,17},{1... | collective-permute-start | bytes 3932168 | tf_op jit(solution)/shard_map/ppermute | solution.py:39
  113.5 4.4 %shard_map.70 = f32[2,8,512]{2,1,0:T(8,128)} custom-call(bf16[2,160,2048]{2,1,0:T(8,128)(2,1)} %bitcast.98, bf16[2,160,2048]{2,1,0:T(8,128)(2,1)} %collective-permute-done.4.second_ref), custom_call_target="tpu_custom_call" | custom-call | flops 13107200 | bytes 2621440 | tf_op jit(solution)/shard_map/pallas_call | solution.py:147
  117.9 11.8 %collective-permute-done.8.second_ref = bf16[2,160,2048]{2,1,0:T(8,128)(2,1)} collective-permute-done((bf16[2,160,2048]{2,1,0:T(8,128)(2,1)S(1)}, bf16[2,160,2048]{2,1,0:T(8,128)(2,1)}, u32[]{:S(2)}, u32[]{:S(2)}) %collective-permute-start.8) | collective-permute-done | bytes 1310752 | tf_op jit(solution)/shard_map/ppermute | solution.py:44
  129.7 1.5 collective-permute-start.9
  131.2 4.4 %shard_map.72 = f32[2,8,512]{2,1,0:T(8,128)} custom-call(bf16[2,160,2048]{2,1,0:T(8,128)(2,1)} %bitcast.94, bf16[2,160,2048]{2,1,0:T(8,128)(2,1)} %collective-permute-done.6.second_ref), custom_call_target="tpu_custom_call" | custom-call | flops 13107200 | bytes 2621440 | tf_op jit(solution)/shard_map/pallas_call | solution.py:147
  135.6 4.4 %shard_map.73 = f32[2,8,512]{2,1,0:T(8,128)} custom-call(bf16[2,160,2048]{2,1,0:T(8,128)(2,1)} %bitcast.99, bf16[2,160,2048]{2,1,0:T(8,128)(2,1)} %collective-permute-done.8.second_ref), custom_call_target="tpu_custom_call" | custom-call | flops 13107200 | bytes 2621440 | tf_op jit(solution)/shard_map/pallas_call | solution.py:147
  140.0 0.0 collective-permute-done.3.second_ref
  140.0 4.4 %shard_map.65 = f32[2,8,512]{2,1,0:T(8,128)} custom-call(bf16[2,160,2048]{2,1,0:T(8,128)(2,1)} %bitcast.95, bf16[2,160,2048]{2,1,0:T(8,128)(2,1)} %collective-permute-done.3.second_ref), custom_call_target="tpu_custom_call" | custom-call | flops 13107200 | bytes 2621440 | tf_op jit(solution)/shard_map/pallas_call | solution.py:147
  144.3 0.0 collective-permute-done.5.second_ref
  144.3 4.4 %shard_map.67 = f32[2,8,512]{2,1,0:T(8,128)} custom-call(bf16[2,160,2048]{2,1,0:T(8,128)(2,1)} %bitcast.100, bf16[2,160,2048]{2,1,0:T(8,128)(2,1)} %collective-permute-done.5.second_ref), custom_call_target="tpu_custom_call" | custom-call | flops 13107200 | bytes 2621440 | tf_op jit(solution)/shard_map/pallas_call | solution.py:147
  148.7 8.4 %collective-permute-done.7.second_ref = bf16[2,160,2048]{2,1,0:T(8,128)(2,1)S(1)} collective-permute-done((bf16[2,160,2048]{2,1,0:T(8,128)(2,1)}, bf16[2,160,2048]{2,1,0:T(8,128)(2,1)S(1)}, u32[]{:S(2)}, u32[]{:S(2)}) %collective-permute-start.7) | collective-permute-done | bytes 1310752 | tf_op jit(solution)/shard_map/ppermute | solution.py:39
  157.1 1.1 copy-done.6
  158.2 4.3 %shard_map.69 = f32[2,8,512]{2,1,0:T(8,128)} custom-call(bf16[2,160,2048]{2,1,0:T(8,128)(2,1)} %bitcast.96, bf16[2,160,2048]{2,1,0:T(8,128)(2,1)} %copy-done.6), custom_call_target="tpu_custom_call" | custom-call | flops 13107200 | bytes 2621440 | tf_op jit(solution)/shard_map/pallas_call | solution.py:147
  162.6 0.0 copy-start.11
  162.6 0.0 copy-start.16
  162.6 1.0 collective-permute-done.9.second_ref
  163.7 1.1 copy-done.7
  164.8 4.4 %shard_map.71 = f32[2,8,512]{2,1,0:T(8,128)} custom-call(bf16[2,160,2048]{2,1,0:T(8,128)(2,1)} %bitcast.101, bf16[2,160,2048]{2,1,0:T(8,128)(2,1)} %copy-done.7), custom_call_target="tpu_custom_call" | custom-call | flops 13107200 | bytes 2621440 | tf_op jit(solution)/shard_map/pallas_call | solution.py:147
  169.1 0.0 copy-done.9
  169.1 0.0 copy-done.10
  169.1 0.0 copy-done.11
  169.2 1.6 select_select_fusion
  170.8 5.0 %all-to-all-start = ((f32[8,2,8,512]{3,2,1,0:T(8,128)}), f32[8,2,8,512]{3,2,1,0:T(8,128)S(1)}, u32[]{:S(2)}, u32[]{:S(2)}) async-start(f32[8,2,8,512]{3,2,1,0:T(8,128)} %select_select_fusion), calls=%async_computation | async-start | bytes 524288 | tf_op jit(solution)/shard_map/all_to_all | solution.py:197
  175.8 0.7 fusion.47
  195.5 0.0 all-to-all-done
  195.8 0.7 maximum_bitcast_fusion
  (43 shorter events, 0.4 us)
Async XLA Ops:
  0.0 13.8 %copy-start.5 = (bf16[1,2,160,4096]{3,2,1,0:T(8,128)(2,1)S(1)}, bf16[1,2,160,4096]{3,2,1,0:T(8,128)(2,1)}, u32[]{:S(2)}) copy-start(bf16[1,2,160,4096]{3,2,1,0:T(8,128)(2,1)} %param.6) | copy-start | bytes 7864324
  1.8 12.0 %collective-permute-start = (bf16[1,2,16,4096]{3,2,1,0:T(8,128)(2,1)}, bf16[1,2,16,4096]{3,2,1,0:T(8,128)(2,1)S(1)}, u32[]{:S(2)}, u32[]{:S(2)}) collective-permute-start(bf16[1,2,16,4096]{3,2,1,0:T(8,128)(2,1)} %slice.131), channel_id=1, source_target_pairs={{0,1},{1,2},{2,3},{4,5},{5,6},{6,7},{8,9},{9,10},{10,11},{12,13},{... | collective-permute-start | bytes 786440 | tf_op jit(solution)/shard_map/ppermute | solution.py:27
  6.1 7.7 %collective-permute-start.1 = (bf16[1,2,25,4096]{3,2,1,0:T(8,128)(2,1)}, bf16[1,2,25,4096]{3,2,1,0:T(8,128)(2,1)S(1)}, u32[]{:S(2)}, u32[]{:S(2)}) collective-permute-start(bf16[1,2,25,4096]{3,2,1,0:T(8,128)(2,1)} %slice.132), channel_id=1, source_target_pairs={{1,0},{2,1},{3,2},{5,4},{6,5},{7,6},{9,8},{10,9},{11,10},{13,12},{... | collective-permute-start | bytes 1228808 | tf_op jit(solution)/shard_map/ppermute | solution.py:29
  38.3 1.1 copy-start.2
  39.4 23.1 %copy-start = (bf16[2,20,8,2048]{3,2,1,0:T(8,128)(2,1)}, bf16[2,20,8,2048]{3,2,1,0:T(8,128)(2,1)S(1)}, u32[]{:S(2)}) copy-start(bf16[2,20,8,2048]{3,2,1,0:T(8,128)(2,1)S(1)} %copy.36) | copy-start | bytes 3932164
  39.4 29.6 %collective-permute-start.2 = (bf16[2,160,2048]{2,1,0:T(8,128)(2,1)S(1)}, bf16[2,160,2048]{2,1,0:T(8,128)(2,1)}, u32[]{:S(2)}, u32[]{:S(2)}) collective-permute-start(bf16[2,160,2048]{2,1,0:T(8,128)(2,1)S(1)} %bitcast.92), channel_id=1, source_target_pairs={{0,8},{4,12},{8,16},{12,20},{16,24},{20,28},{1,9},{5,13},{9,17},{1... | collective-permute-start | bytes 3932168 | tf_op jit(solution)/shard_map/ppermute | solution.py:39
  65.2 1.1 copy-start.3
  66.4 5.5 %copy-start.1 = (bf16[2,20,8,2048]{3,2,1,0:T(8,128)(2,1)}, bf16[2,20,8,2048]{3,2,1,0:T(8,128)(2,1)S(1)}, u32[]{:S(2)}) copy-start(bf16[2,20,8,2048]{3,2,1,0:T(8,128)(2,1)S(1)} %copy.35) | copy-start | bytes 3932164
  66.4 30.1 %collective-permute-start.4 = (bf16[2,160,2048]{2,1,0:T(8,128)(2,1)S(1)}, bf16[2,160,2048]{2,1,0:T(8,128)(2,1)}, u32[]{:S(2)}, u32[]{:S(2)}) collective-permute-start(bf16[2,160,2048]{2,1,0:T(8,128)(2,1)S(1)} %bitcast.97), channel_id=1, source_target_pairs={{8,0},{12,4},{16,8},{20,12},{24,16},{28,20},{9,1},{13,5},{17,9},{2... | collective-permute-start | bytes 3932168 | tf_op jit(solution)/shard_map/ppermute | solution.py:39
  67.7 28.8 %copy-start.4 = (bf16[2,160,2048]{2,0,1:T(2,128)(2,1)S(1)}, bf16[2,160,2048]{2,0,1:T(2,128)(2,1)}, u32[]{:S(2)}) copy-start(bf16[2,160,2048]{2,0,1:T(2,128)(2,1)} %copy-done.3) | copy-start | bytes 3932164
  71.9 37.0 %collective-permute-start.6 = (bf16[2,160,2048]{2,1,0:T(8,128)(2,1)S(1)}, bf16[2,160,2048]{2,1,0:T(8,128)(2,1)}, u32[]{:S(2)}, u32[]{:S(2)}) collective-permute-start(bf16[2,160,2048]{2,1,0:T(8,128)(2,1)S(1)} %broadcast_select_fusion.1), channel_id=1, source_target_pairs={{0,4},{4,0},{8,12},{12,8},{16,20},{20,16},{24,28},{28,24},{1,5},{5... | collective-permute-start | bytes 3932168 | tf_op jit(solution)/shard_map/ppermute | solution.py:44
  99.3 30.3 %collective-permute-start.8 = (bf16[2,160,2048]{2,1,0:T(8,128)(2,1)S(1)}, bf16[2,160,2048]{2,1,0:T(8,128)(2,1)}, u32[]{:S(2)}, u32[]{:S(2)}) collective-permute-start(bf16[2,160,2048]{2,1,0:T(8,128)(2,1)S(1)} %broadcast_select_fusion), channel_id=1, source_target_pairs={{0,4},{4,0},{8,12},{12,8},{16,20},{20,16},{24,28},{28,24},{1,5},{5... | collective-permute-start | bytes 3932168 | tf_op jit(solution)/shard_map/ppermute | solution.py:44
  99.6 40.4 %collective-permute-start.3 = (bf16[2,160,2048]{2,1,0:T(8,128)(2,1)}, bf16[2,160,2048]{2,1,0:T(8,128)(2,1)}, u32[]{:S(2)}, u32[]{:S(2)}) collective-permute-start(bf16[2,160,2048]{2,1,0:T(8,128)(2,1)} %collective-permute-done.2.second_ref), channel_id=1, source_target_pairs={{0,8},{4,12},{8,16},{12,20},{16,24},{20,28},{1,9},{5,13},{9,17},{1... | collective-permute-start | bytes 3932168 | tf_op jit(solution)/shard_map/ppermute | solution.py:39
  103.2 41.1 %collective-permute-start.5 = (bf16[2,160,2048]{2,1,0:T(8,128)(2,1)}, bf16[2,160,2048]{2,1,0:T(8,128)(2,1)}, u32[]{:S(2)}, u32[]{:S(2)}) collective-permute-start(bf16[2,160,2048]{2,1,0:T(8,128)(2,1)} %collective-permute-done.4.second_ref), channel_id=1, source_target_pairs={{8,0},{12,4},{16,8},{20,12},{24,16},{28,20},{9,1},{13,5},{17,9},{2... | collective-permute-start | bytes 3932168 | tf_op jit(solution)/shard_map/ppermute | solution.py:39
  108.9 48.2 %collective-permute-start.7 = (bf16[2,160,2048]{2,1,0:T(8,128)(2,1)}, bf16[2,160,2048]{2,1,0:T(8,128)(2,1)S(1)}, u32[]{:S(2)}, u32[]{:S(2)}) collective-permute-start(bf16[2,160,2048]{2,1,0:T(8,128)(2,1)} %collective-permute-done.6.second_ref), channel_id=1, source_target_pairs={{0,8},{4,12},{8,16},{12,20},{16,24},{20,28},{1,9},{5,13},{9,17},{1... | collective-permute-start | bytes 3932168 | tf_op jit(solution)/shard_map/ppermute | solution.py:39
  129.7 34.0 %collective-permute-start.9 = (bf16[2,160,2048]{2,1,0:T(8,128)(2,1)}, bf16[2,160,2048]{2,1,0:T(8,128)(2,1)S(1)}, u32[]{:S(2)}, u32[]{:S(2)}) collective-permute-start(bf16[2,160,2048]{2,1,0:T(8,128)(2,1)} %collective-permute-done.8.second_ref), channel_id=1, source_target_pairs={{8,0},{12,4},{16,8},{20,12},{24,16},{28,20},{9,1},{13,5},{17,9},{2... | collective-permute-start | bytes 3932168 | tf_op jit(solution)/shard_map/ppermute | solution.py:39
  157.1 1.1 copy-start.6
  162.6 6.5 %copy-start.8 = (f32[2,8,512]{2,1,0:T(8,128)S(1)}, f32[2,8,512]{2,1,0:T(8,128)}, u32[]{:S(2)}) copy-start(f32[2,8,512]{2,1,0:T(8,128)} %shard_map.68) | copy-start | bytes 98308
  162.6 6.5 %copy-start.9 = (f32[2,8,512]{2,1,0:T(8,128)S(1)}, f32[2,8,512]{2,1,0:T(8,128)}, u32[]{:S(2)}) copy-start(f32[2,8,512]{2,1,0:T(8,128)} %shard_map.70) | copy-start | bytes 98308
  162.6 6.6 %copy-start.10 = (f32[2,8,512]{2,1,0:T(8,128)S(1)}, f32[2,8,512]{2,1,0:T(8,128)}, u32[]{:S(2)}) copy-start(f32[2,8,512]{2,1,0:T(8,128)} %shard_map.72) | copy-start | bytes 98308
  162.6 6.6 %copy-start.11 = (f32[2,8,512]{2,1,0:T(8,128)S(1)}, f32[2,8,512]{2,1,0:T(8,128)}, u32[]{:S(2)}) copy-start(f32[2,8,512]{2,1,0:T(8,128)} %shard_map.73) | copy-start | bytes 98308
  162.6 6.6 %copy-start.12 = (f32[2,8,512]{2,1,0:T(8,128)S(1)}, f32[2,8,512]{2,1,0:T(8,128)}, u32[]{:S(2)}) copy-start(f32[2,8,512]{2,1,0:T(8,128)} %shard_map.65) | copy-start | bytes 98308
  162.6 6.6 %copy-start.13 = (f32[2,8,512]{2,1,0:T(8,128)S(1)}, f32[2,8,512]{2,1,0:T(8,128)}, u32[]{:S(2)}) copy-start(f32[2,8,512]{2,1,0:T(8,128)} %shard_map.67) | copy-start | bytes 98308
  162.6 6.6 %copy-start.14 = (f32[2,8,512]{2,1,0:T(8,128)S(1)}, f32[2,8,512]{2,1,0:T(8,128)}, u32[]{:S(2)}) copy-start(f32[2,8,512]{2,1,0:T(8,128)} %shard_map.69) | copy-start | bytes 98308
  162.6 13.2 %copy-start.16 = (s32[1,4]{1,0:T(1,128)S(1)}, s32[1,4]{1,0:T(1,128)}, u32[]{:S(2)}) copy-start(s32[1,4]{1,0:T(1,128)} %param.11) | copy-start | bytes 52
  163.7 1.1 copy-start.7
  169.1 26.5 %copy-start.15 = (f32[2,8,512]{2,1,0:T(8,128)S(1)}, f32[2,8,512]{2,1,0:T(8,128)}, u32[]{:S(2)}) copy-start(f32[2,8,512]{2,1,0:T(8,128)} %shard_map.71) | copy-start | bytes 98308
  170.8 24.6 %all-to-all-start = ((f32[8,2,8,512]{3,2,1,0:T(8,128)}), f32[8,2,8,512]{3,2,1,0:T(8,128)S(1)}, u32[]{:S(2)}, u32[]{:S(2)}) async-start(f32[8,2,8,512]{3,2,1,0:T(8,128)} %select_select_fusion), calls=%async_computation | async-start | bytes 524288 | tf_op jit(solution)/shard_map/all_to_all | solution.py:197

commit v19 on v18

--- a/solution.py
+++ b/solution.py
@@ -51,7 +51,7 @@
     return jnp.sinc(place) * (0.5 + 0.5 * jnp.cos(jnp.pi * place / 4.5))
 
 
-ROWS = 80
+ROWS = 160
 EDGE = 128
 
 

time: 200 us -> 199 us (level)
  transfers between devices with their start and end apart: 11 -> 11, of which waited for: 5 -> 5; matrix products, arithmetic and copies ran while one was open for 8% -> 9% of each run, Pallas kernels for 25% -> 24%
where the time goes in v19:
time: 199 us; the launch traced here: 196 us
  Pallas kernels  69.5 us (35%)
  waiting for transfers between devices  45.6 us (23%)
  starting transfers between devices  28.4 us (14%)
  between operations  20.7 us (10%)
  local copies, waits for them, and re-layouts  16.3 us (8%)
  other arithmetic  15.1 us (8%)
    pallas_call x8, Pallas kernels, looks(): pl.pallas_call(looks_kernel, grid=(width // CHUNK,), in_specs=[spec, spec...  34.9 us
    pallas_call x2, Pallas kernels, resample_half(): pl.pallas_call(functools.partial(resample_kernel, side), grid=(2, nlines...  34.6 us
    ppermute x6, waiting for transfers between devices, shifted(): return lax.ppermute(block, axis, route)  32.7 us
    ppermute x6, starting transfers between devices, shifted(): return lax.ppermute(block, axis, route)  17.8 us
    ppermute x2, waiting for transfers between devices, swapped(): return lax.ppermute(block, axis, [(i, i ^ 1) for i in range(count)])  12.9 us
    pallas_call x2, local copies, waits for them, and re-layouts, resample_half(): pl.pallas_call(functools.partial(resample_kernel, side), grid=(2, nlines...  5.33 us
    all_to_all x1, starting transfers between devices, shards(): got = lax.all_to_all(sent, 'date', 0, 0, tiled=True)  4.62 us
  transfers between devices with their start and end apart: 11, of which 5 were waited for; matrix products, arithmetic and copies ran while one was open for 9% of the time, Pallas kernels for 24%

profile of v19, /device:TPU:0, one launch (start us, length us, event | category | flops | bytes accessed | tf_op | source)
XLA Modules:
  0.0 195.5 jit_solution(17834916504026920065)
XLA Ops:
  0.0 1.8 slice.131
  1.8 2.4 %collective-permute-start = (bf16[1,2,16,4096]{3,2,1,0:T(8,128)(2,1)}, bf16[1,2,16,4096]{3,2,1,0:T(8,128)(2,1)S(1)}, u32[]{:S(2)}, u32[]{:S(2)}) collective-permute-start(bf16[1,2,16,4096]{3,2,1,0:T(8,128)(2,1)} %slice.131), channel_id=1, source_target_pairs={{0,1},{1,2},{2,3},{4,5},{5,6},{6,7},{8,9},{9,10},{10,11},{12,13},{... | collective-permute-start | bytes 786440 | tf_op jit(solution)/shard_map/ppermute | solution.py:27
  4.2 1.9 slice.132
  6.1 1.3 collective-permute-start.1
  7.4 0.7 add_bitcast_fusion
  8.1 0.7 compare_select_fusion
  8.8 0.1 fusion.17
  8.9 0.7 compare_and_fusion
  10.9 0.1 copy.22
  11.0 0.7 fusion.14.weights_ref
  11.7 0.7 copy.23.shift_ref
  12.4 0.7 gather_fusion
  13.1 0.7 broadcast_select_fusion.2.coeff_ref
  13.8 0.0 collective-permute-done
  13.8 0.0 collective-permute-done.1
  13.8 0.0 copy-done.5
  13.8 3.9 %fusion.2.window_ref = bf16[2,176,4096]{2,1,0:T(8,128)(2,1)} fusion(s32[]{:T(128)S(6)} %select_n.544, bf16[1,2,16,4096]{3,2,1,0:T(8,128)(2,1)S(1)} %collective-permute-done, bf16[1,2,160,4096]{3,2,1,0:T(8,128)(2,1)S(1)} %copy-done.5, bf16[1,2,25,4096]{3,2,1,0:T(8,128)(2,1)S(1)} %collective-permute-done.1), kind=kLoop, calls=%fused_computation.6 | loop fusion | flops 8650752 | bytes 6176772 | tf_op jit(solution)/shard_map/dynamic_slice | solution.py:109
  17.7 17.5 %shard_map.64 = bf16[2,160,2048]{2,1,0:T(8,128)(2,1)} custom-call(f32[8]{0:T(128)} %fusion.14.weights_ref, bf16[2,176,4096]{2,1,0:T(8,128)(2,1)} %fusion.2.window_ref, f32[160,8]{1,0:T(8,128)} %broadcast_select_fusion.2.coeff_ref, s32[160,1]{1,0:T(8,128)} %copy.23.shift_ref), custom_call_target="tpu_custom_call" | custom-call | flops 39321600 | bytes 3932160 | tf_op jit(solution)/shard_map/pallas_call | solution.py:87
  35.2 2.7 %copy.24 = bf16[2,160,2048]{2,0,1:T(2,128)(2,1)S(1)} copy(bf16[2,160,2048]{2,1,0:T(8,128)(2,1)} %shard_map.64) | data formatting | bytes 2621440 | tf_op jit(solution)/shard_map/pallas_call | solution.py:87
  37.9 0.7 copy.36
  38.6 0.4 copy-done.2
  38.9 5.4 %collective-permute-start.2 = (bf16[2,160,2048]{2,1,0:T(8,128)(2,1)S(1)}, bf16[2,160,2048]{2,1,0:T(8,128)(2,1)}, u32[]{:S(2)}, u32[]{:S(2)}) collective-permute-start(bf16[2,160,2048]{2,1,0:T(8,128)(2,1)S(1)} %bitcast.92), channel_id=1, source_target_pairs={{0,8},{4,12},{8,16},{12,20},{16,24},{20,28},{1,9},{5,13},{9,17},{1... | collective-permute-start | bytes 3932168 | tf_op jit(solution)/shard_map/ppermute | solution.py:39
  44.3 17.2 %shard_map.66 = bf16[2,160,2048]{2,1,0:T(8,128)(2,1)} custom-call(f32[8]{0:T(128)} %fusion.14.weights_ref, bf16[2,176,4096]{2,1,0:T(8,128)(2,1)} %fusion.2.window_ref, f32[160,8]{1,0:T(8,128)} %broadcast_select_fusion.2.coeff_ref, s32[160,1]{1,0:T(8,128)} %copy.23.shift_ref), custom_call_target="tpu_custom_call" | custom-call | flops 39321600 | bytes 3932160 | tf_op jit(solution)/shard_map/pallas_call | solution.py:87
  61.5 2.7 %copy.27 = bf16[2,160,2048]{2,0,1:T(2,128)(2,1)S(1)} copy(bf16[2,160,2048]{2,1,0:T(8,128)(2,1)} %shard_map.66) | data formatting | bytes 2621440 | tf_op jit(solution)/shard_map/pallas_call | solution.py:87
  64.2 0.7 copy.35
  64.9 0.4 copy-done.3
  65.3 1.5 collective-permute-start.4
  66.9 0.0 copy-start.4
  66.9 1.7 collective-permute-done.2.second_ref
  68.6 2.8 %broadcast_select_fusion.1 = bf16[2,160,2048]{2,1,0:T(8,128)(2,1)S(1)} fusion(bf16[2,160,2048]{2,1,0:T(8,128)(2,1)} %collective-permute-done.2.second_ref, pred[]{:T(512)S(6)} %eq.195, bf16[2,20,8,2048]{3,0,1,2:T(2,128)(2,1)} %bitcast.103), kind=kLoop, calls=%fused_computation.10 | loop fusion | flops 655360 | bytes 3932161 | tf_op jit(solution)/shard_map/jit(_where)/select_n | solution.py:179
  71.4 2.0 %collective-permute-start.6 = (bf16[2,160,2048]{2,1,0:T(8,128)(2,1)S(1)}, bf16[2,160,2048]{2,1,0:T(8,128)(2,1)}, u32[]{:S(2)}, u32[]{:S(2)}) collective-permute-start(bf16[2,160,2048]{2,1,0:T(8,128)(2,1)S(1)} %broadcast_select_fusion.1), channel_id=1, source_target_pairs={{0,4},{4,0},{8,12},{12,8},{16,20},{20,16},{24,28},{28,24},{1,5},{5... | collective-permute-start | bytes 3932168 | tf_op jit(solution)/shard_map/ppermute | solution.py:44
  73.3 22.1 %collective-permute-done.4.second_ref = bf16[2,160,2048]{2,1,0:T(8,128)(2,1)} collective-permute-done((bf16[2,160,2048]{2,1,0:T(8,128)(2,1)S(1)}, bf16[2,160,2048]{2,1,0:T(8,128)(2,1)}, u32[]{:S(2)}, u32[]{:S(2)}) %collective-permute-start.4) | collective-permute-done | bytes 1310752 | tf_op jit(solution)/shard_map/ppermute | solution.py:39
  95.4 2.8 %broadcast_select_fusion = bf16[2,160,2048]{2,1,0:T(8,128)(2,1)S(1)} fusion(bf16[2,160,2048]{2,1,0:T(8,128)(2,1)} %collective-permute-done.4.second_ref, pred[]{:T(512)S(6)} %eq.195, bf16[2,20,8,2048]{3,0,1,2:T(2,128)(2,1)S(1)} %bitcast.105), kind=kLoop, calls=%fused_computation.9 | loop fusion | flops 655360 | bytes 3932161 | tf_op jit(solution)/shard_map/jit(_where)/select_n | solution.py:176
  98.2 0.3 collective-permute-start.8
  98.5 3.7 %collective-permute-start.3 = (bf16[2,160,2048]{2,1,0:T(8,128)(2,1)}, bf16[2,160,2048]{2,1,0:T(8,128)(2,1)}, u32[]{:S(2)}, u32[]{:S(2)}) collective-permute-start(bf16[2,160,2048]{2,1,0:T(8,128)(2,1)} %collective-permute-done.2.second_ref), channel_id=1, source_target_pairs={{0,8},{4,12},{8,16},{12,20},{16,24},{20,28},{1,9},{5,13},{9,17},{1... | collective-permute-start | bytes 3932168 | tf_op jit(solution)/shard_map/ppermute | solution.py:39
  102.2 1.3 collective-permute-start.5
  103.5 4.4 %shard_map.68 = f32[2,8,512]{2,1,0:T(8,128)} custom-call(bf16[2,160,2048]{2,1,0:T(8,128)(2,1)} %bitcast.93, bf16[2,160,2048]{2,1,0:T(8,128)(2,1)} %collective-permute-done.2.second_ref), custom_call_target="tpu_custom_call" | custom-call | flops 13107200 | bytes 2621440 | tf_op jit(solution)/shard_map/pallas_call | solution.py:147
  107.9 0.0 collective-permute-done.6.second_ref
  107.9 4.6 %collective-permute-start.7 = (bf16[2,160,2048]{2,1,0:T(8,128)(2,1)}, bf16[2,160,2048]{2,1,0:T(8,128)(2,1)S(1)}, u32[]{:S(2)}, u32[]{:S(2)}) collective-permute-start(bf16[2,160,2048]{2,1,0:T(8,128)(2,1)} %collective-permute-done.6.second_ref), channel_id=1, source_target_pairs={{0,8},{4,12},{8,16},{12,20},{16,24},{20,28},{1,9},{5,13},{9,17},{1... | collective-permute-start | bytes 3932168 | tf_op jit(solution)/shard_map/ppermute | solution.py:39
  112.5 4.4 %shard_map.70 = f32[2,8,512]{2,1,0:T(8,128)} custom-call(bf16[2,160,2048]{2,1,0:T(8,128)(2,1)} %bitcast.98, bf16[2,160,2048]{2,1,0:T(8,128)(2,1)} %collective-permute-done.4.second_ref), custom_call_target="tpu_custom_call" | custom-call | flops 13107200 | bytes 2621440 | tf_op jit(solution)/shard_map/pallas_call | solution.py:147
  116.9 12.9 %collective-permute-done.8.second_ref = bf16[2,160,2048]{2,1,0:T(8,128)(2,1)} collective-permute-done((bf16[2,160,2048]{2,1,0:T(8,128)(2,1)S(1)}, bf16[2,160,2048]{2,1,0:T(8,128)(2,1)}, u32[]{:S(2)}, u32[]{:S(2)}) %collective-permute-start.8) | collective-permute-done | bytes 1310752 | tf_op jit(solution)/shard_map/ppermute | solution.py:44
  129.7 1.3 collective-permute-start.9
  131.1 4.4 %shard_map.72 = f32[2,8,512]{2,1,0:T(8,128)} custom-call(bf16[2,160,2048]{2,1,0:T(8,128)(2,1)} %bitcast.94, bf16[2,160,2048]{2,1,0:T(8,128)(2,1)} %collective-permute-done.6.second_ref), custom_call_target="tpu_custom_call" | custom-call | flops 13107200 | bytes 2621440 | tf_op jit(solution)/shard_map/pallas_call | solution.py:147
  135.5 4.4 %shard_map.73 = f32[2,8,512]{2,1,0:T(8,128)} custom-call(bf16[2,160,2048]{2,1,0:T(8,128)(2,1)} %bitcast.99, bf16[2,160,2048]{2,1,0:T(8,128)(2,1)} %collective-permute-done.8.second_ref), custom_call_target="tpu_custom_call" | custom-call | flops 13107200 | bytes 2621440 | tf_op jit(solution)/shard_map/pallas_call | solution.py:147
  139.8 0.0 collective-permute-done.3.second_ref
  139.8 4.4 %shard_map.65 = f32[2,8,512]{2,1,0:T(8,128)} custom-call(bf16[2,160,2048]{2,1,0:T(8,128)(2,1)} %bitcast.95, bf16[2,160,2048]{2,1,0:T(8,128)(2,1)} %collective-permute-done.3.second_ref), custom_call_target="tpu_custom_call" | custom-call | flops 13107200 | bytes 2621440 | tf_op jit(solution)/shard_map/pallas_call | solution.py:147
  144.2 0.0 collective-permute-done.5.second_ref
  144.2 4.4 %shard_map.67 = f32[2,8,512]{2,1,0:T(8,128)} custom-call(bf16[2,160,2048]{2,1,0:T(8,128)(2,1)} %bitcast.100, bf16[2,160,2048]{2,1,0:T(8,128)(2,1)} %collective-permute-done.5.second_ref), custom_call_target="tpu_custom_call" | custom-call | flops 13107200 | bytes 2621440 | tf_op jit(solution)/shard_map/pallas_call | solution.py:147
  148.5 7.6 %collective-permute-done.7.second_ref = bf16[2,160,2048]{2,1,0:T(8,128)(2,1)S(1)} collective-permute-done((bf16[2,160,2048]{2,1,0:T(8,128)(2,1)}, bf16[2,160,2048]{2,1,0:T(8,128)(2,1)S(1)}, u32[]{:S(2)}, u32[]{:S(2)}) %collective-permute-start.7) | collective-permute-done | bytes 1310752 | tf_op jit(solution)/shard_map/ppermute | solution.py:39
  156.1 1.1 copy-done.6
  157.2 4.3 %shard_map.69 = f32[2,8,512]{2,1,0:T(8,128)} custom-call(bf16[2,160,2048]{2,1,0:T(8,128)(2,1)} %bitcast.96, bf16[2,160,2048]{2,1,0:T(8,128)(2,1)} %copy-done.6), custom_call_target="tpu_custom_call" | custom-call | flops 13107200 | bytes 2621440 | tf_op jit(solution)/shard_map/pallas_call | solution.py:147
  161.6 0.0 copy-start.11
  161.6 0.0 copy-start.16
  161.6 1.4 collective-permute-done.9.second_ref
  163.0 1.1 copy-done.7
  164.1 4.4 %shard_map.71 = f32[2,8,512]{2,1,0:T(8,128)} custom-call(bf16[2,160,2048]{2,1,0:T(8,128)(2,1)} %bitcast.101, bf16[2,160,2048]{2,1,0:T(8,128)(2,1)} %copy-done.7), custom_call_target="tpu_custom_call" | custom-call | flops 13107200 | bytes 2621440 | tf_op jit(solution)/shard_map/pallas_call | solution.py:147
  168.5 0.0 copy-done.10
  168.5 0.0 copy-done.11
  168.5 0.0 copy-done.12
  168.5 1.6 select_select_fusion
  170.2 4.6 %all-to-all-start = ((f32[8,2,8,512]{3,2,1,0:T(8,128)}), f32[8,2,8,512]{3,2,1,0:T(8,128)S(1)}, u32[]{:S(2)}, u32[]{:S(2)}) async-start(f32[8,2,8,512]{3,2,1,0:T(8,128)} %select_select_fusion), calls=%async_computation | async-start | bytes 524288 | tf_op jit(solution)/shard_map/all_to_all | solution.py:197
  174.8 0.7 fusion.47
  194.4 0.0 all-to-all-done
  194.8 0.7 maximum_bitcast_fusion
  (43 shorter events, 0.4 us)
Async XLA Ops:
  0.0 13.8 %copy-start.5 = (bf16[1,2,160,4096]{3,2,1,0:T(8,128)(2,1)S(1)}, bf16[1,2,160,4096]{3,2,1,0:T(8,128)(2,1)}, u32[]{:S(2)}) copy-start(bf16[1,2,160,4096]{3,2,1,0:T(8,128)(2,1)} %param.6) | copy-start | bytes 7864324
  1.8 12.0 %collective-permute-start = (bf16[1,2,16,4096]{3,2,1,0:T(8,128)(2,1)}, bf16[1,2,16,4096]{3,2,1,0:T(8,128)(2,1)S(1)}, u32[]{:S(2)}, u32[]{:S(2)}) collective-permute-start(bf16[1,2,16,4096]{3,2,1,0:T(8,128)(2,1)} %slice.131), channel_id=1, source_target_pairs={{0,1},{1,2},{2,3},{4,5},{5,6},{6,7},{8,9},{9,10},{10,11},{12,13},{... | collective-permute-start | bytes 786440 | tf_op jit(solution)/shard_map/ppermute | solution.py:27
  6.1 7.7 %collective-permute-start.1 = (bf16[1,2,25,4096]{3,2,1,0:T(8,128)(2,1)}, bf16[1,2,25,4096]{3,2,1,0:T(8,128)(2,1)S(1)}, u32[]{:S(2)}, u32[]{:S(2)}) collective-permute-start(bf16[1,2,25,4096]{3,2,1,0:T(8,128)(2,1)} %slice.132), channel_id=1, source_target_pairs={{1,0},{2,1},{3,2},{5,4},{6,5},{7,6},{9,8},{10,9},{11,10},{13,12},{... | collective-permute-start | bytes 1228808 | tf_op jit(solution)/shard_map/ppermute | solution.py:29
  37.9 1.1 copy-start.2
  38.9 22.6 %copy-start = (bf16[2,20,8,2048]{3,2,1,0:T(8,128)(2,1)}, bf16[2,20,8,2048]{3,2,1,0:T(8,128)(2,1)S(1)}, u32[]{:S(2)}) copy-start(bf16[2,20,8,2048]{3,2,1,0:T(8,128)(2,1)S(1)} %copy.36) | copy-start | bytes 3932164
  38.9 29.6 %collective-permute-start.2 = (bf16[2,160,2048]{2,1,0:T(8,128)(2,1)S(1)}, bf16[2,160,2048]{2,1,0:T(8,128)(2,1)}, u32[]{:S(2)}, u32[]{:S(2)}) collective-permute-start(bf16[2,160,2048]{2,1,0:T(8,128)(2,1)S(1)} %bitcast.92), channel_id=1, source_target_pairs={{0,8},{4,12},{8,16},{12,20},{16,24},{20,28},{1,9},{5,13},{9,17},{1... | collective-permute-start | bytes 3932168 | tf_op jit(solution)/shard_map/ppermute | solution.py:39
  64.2 1.1 copy-start.3
  65.3 6.0 %copy-start.1 = (bf16[2,20,8,2048]{3,2,1,0:T(8,128)(2,1)}, bf16[2,20,8,2048]{3,2,1,0:T(8,128)(2,1)S(1)}, u32[]{:S(2)}) copy-start(bf16[2,20,8,2048]{3,2,1,0:T(8,128)(2,1)S(1)} %copy.35) | copy-start | bytes 3932164
  65.3 30.1 %collective-permute-start.4 = (bf16[2,160,2048]{2,1,0:T(8,128)(2,1)S(1)}, bf16[2,160,2048]{2,1,0:T(8,128)(2,1)}, u32[]{:S(2)}, u32[]{:S(2)}) collective-permute-start(bf16[2,160,2048]{2,1,0:T(8,128)(2,1)S(1)} %bitcast.97), channel_id=1, source_target_pairs={{8,0},{12,4},{16,8},{20,12},{24,16},{28,20},{9,1},{13,5},{17,9},{2... | collective-permute-start | bytes 3932168 | tf_op jit(solution)/shard_map/ppermute | solution.py:39
  66.9 28.5 %copy-start.4 = (bf16[2,160,2048]{2,0,1:T(2,128)(2,1)S(1)}, bf16[2,160,2048]{2,0,1:T(2,128)(2,1)}, u32[]{:S(2)}) copy-start(bf16[2,160,2048]{2,0,1:T(2,128)(2,1)} %copy-done.3) | copy-start | bytes 3932164
  71.4 36.5 %collective-permute-start.6 = (bf16[2,160,2048]{2,1,0:T(8,128)(2,1)S(1)}, bf16[2,160,2048]{2,1,0:T(8,128)(2,1)}, u32[]{:S(2)}, u32[]{:S(2)}) collective-permute-start(bf16[2,160,2048]{2,1,0:T(8,128)(2,1)S(1)} %broadcast_select_fusion.1), channel_id=1, source_target_pairs={{0,4},{4,0},{8,12},{12,8},{16,20},{20,16},{24,28},{28,24},{1,5},{5... | collective-permute-start | bytes 3932168 | tf_op jit(solution)/shard_map/ppermute | solution.py:44
  98.2 31.5 %collective-permute-start.8 = (bf16[2,160,2048]{2,1,0:T(8,128)(2,1)S(1)}, bf16[2,160,2048]{2,1,0:T(8,128)(2,1)}, u32[]{:S(2)}, u32[]{:S(2)}) collective-permute-start(bf16[2,160,2048]{2,1,0:T(8,128)(2,1)S(1)} %broadcast_select_fusion), channel_id=1, source_target_pairs={{0,4},{4,0},{8,12},{12,8},{16,20},{20,16},{24,28},{28,24},{1,5},{5... | collective-permute-start | bytes 3932168 | tf_op jit(solution)/shard_map/ppermute | solution.py:44
  98.5 41.3 %collective-permute-start.3 = (bf16[2,160,2048]{2,1,0:T(8,128)(2,1)}, bf16[2,160,2048]{2,1,0:T(8,128)(2,1)}, u32[]{:S(2)}, u32[]{:S(2)}) collective-permute-start(bf16[2,160,2048]{2,1,0:T(8,128)(2,1)} %collective-permute-done.2.second_ref), channel_id=1, source_target_pairs={{0,8},{4,12},{8,16},{12,20},{16,24},{20,28},{1,9},{5,13},{9,17},{1... | collective-permute-start | bytes 3932168 | tf_op jit(solution)/shard_map/ppermute | solution.py:39
  102.2 42.0 %collective-permute-start.5 = (bf16[2,160,2048]{2,1,0:T(8,128)(2,1)}, bf16[2,160,2048]{2,1,0:T(8,128)(2,1)}, u32[]{:S(2)}, u32[]{:S(2)}) collective-permute-start(bf16[2,160,2048]{2,1,0:T(8,128)(2,1)} %collective-permute-done.4.second_ref), channel_id=1, source_target_pairs={{8,0},{12,4},{16,8},{20,12},{24,16},{28,20},{9,1},{13,5},{17,9},{2... | collective-permute-start | bytes 3932168 | tf_op jit(solution)/shard_map/ppermute | solution.py:39
  107.9 48.2 %collective-permute-start.7 = (bf16[2,160,2048]{2,1,0:T(8,128)(2,1)}, bf16[2,160,2048]{2,1,0:T(8,128)(2,1)S(1)}, u32[]{:S(2)}, u32[]{:S(2)}) collective-permute-start(bf16[2,160,2048]{2,1,0:T(8,128)(2,1)} %collective-permute-done.6.second_ref), channel_id=1, source_target_pairs={{0,8},{4,12},{8,16},{12,20},{16,24},{20,28},{1,9},{5,13},{9,17},{1... | collective-permute-start | bytes 3932168 | tf_op jit(solution)/shard_map/ppermute | solution.py:39
  129.7 33.3 %collective-permute-start.9 = (bf16[2,160,2048]{2,1,0:T(8,128)(2,1)}, bf16[2,160,2048]{2,1,0:T(8,128)(2,1)S(1)}, u32[]{:S(2)}, u32[]{:S(2)}) collective-permute-start(bf16[2,160,2048]{2,1,0:T(8,128)(2,1)} %collective-permute-done.8.second_ref), channel_id=1, source_target_pairs={{8,0},{12,4},{16,8},{20,12},{24,16},{28,20},{9,1},{13,5},{17,9},{2... | collective-permute-start | bytes 3932168 | tf_op jit(solution)/shard_map/ppermute | solution.py:39
  156.1 1.1 copy-start.6
  161.6 6.9 %copy-start.8 = (f32[2,8,512]{2,1,0:T(8,128)S(1)}, f32[2,8,512]{2,1,0:T(8,128)}, u32[]{:S(2)}) copy-start(f32[2,8,512]{2,1,0:T(8,128)} %shard_map.68) | copy-start | bytes 98308
  161.6 6.9 %copy-start.9 = (f32[2,8,512]{2,1,0:T(8,128)S(1)}, f32[2,8,512]{2,1,0:T(8,128)}, u32[]{:S(2)}) copy-start(f32[2,8,512]{2,1,0:T(8,128)} %shard_map.70) | copy-start | bytes 98308
  161.6 6.9 %copy-start.10 = (f32[2,8,512]{2,1,0:T(8,128)S(1)}, f32[2,8,512]{2,1,0:T(8,128)}, u32[]{:S(2)}) copy-start(f32[2,8,512]{2,1,0:T(8,128)} %shard_map.72) | copy-start | bytes 98308
  161.6 6.9 %copy-start.11 = (f32[2,8,512]{2,1,0:T(8,128)S(1)}, f32[2,8,512]{2,1,0:T(8,128)}, u32[]{:S(2)}) copy-start(f32[2,8,512]{2,1,0:T(8,128)} %shard_map.73) | copy-start | bytes 98308
  161.6 6.9 %copy-start.12 = (f32[2,8,512]{2,1,0:T(8,128)S(1)}, f32[2,8,512]{2,1,0:T(8,128)}, u32[]{:S(2)}) copy-start(f32[2,8,512]{2,1,0:T(8,128)} %shard_map.65) | copy-start | bytes 98308
  161.6 6.9 %copy-start.13 = (f32[2,8,512]{2,1,0:T(8,128)S(1)}, f32[2,8,512]{2,1,0:T(8,128)}, u32[]{:S(2)}) copy-start(f32[2,8,512]{2,1,0:T(8,128)} %shard_map.67) | copy-start | bytes 98308
  161.6 6.9 %copy-start.14 = (f32[2,8,512]{2,1,0:T(8,128)S(1)}, f32[2,8,512]{2,1,0:T(8,128)}, u32[]{:S(2)}) copy-start(f32[2,8,512]{2,1,0:T(8,128)} %shard_map.69) | copy-start | bytes 98308
  161.6 13.2 %copy-start.16 = (s32[1,4]{1,0:T(1,128)S(1)}, s32[1,4]{1,0:T(1,128)}, u32[]{:S(2)}) copy-start(s32[1,4]{1,0:T(1,128)} %param.11) | copy-start | bytes 52
  163.0 1.1 copy-start.7
  168.5 26.1 %copy-start.15 = (f32[2,8,512]{2,1,0:T(8,128)S(1)}, f32[2,8,512]{2,1,0:T(8,128)}, u32[]{:S(2)}) copy-start(f32[2,8,512]{2,1,0:T(8,128)} %shard_map.71) | copy-start | bytes 98308
  170.2 24.3 %all-to-all-start = ((f32[8,2,8,512]{3,2,1,0:T(8,128)}), f32[8,2,8,512]{3,2,1,0:T(8,128)S(1)}, u32[]{:S(2)}, u32[]{:S(2)}) async-start(f32[8,2,8,512]{3,2,1,0:T(8,128)} %select_select_fusion), calls=%async_computation | async-start | bytes 524288 | tf_op jit(solution)/shard_map/all_to_all | solution.py:197

commit v20 on v19

--- a/solution.py
+++ b/solution.py
@@ -61,10 +61,15 @@
     half = out_ref.shape[2]
     low = max(side * half - EDGE, 0)
     high = min(side * half + half + EDGE, window_ref.shape[2])
-    window = window_ref[0, pl.ds(first, ROWS + 16), low:high].astype(jnp.float32)
-    along = weights_ref[0] * window[0:ROWS, :]
-    for tap in range(1, 8):
-        along = along + weights_ref[tap] * window[tap : tap + ROWS, :]
+    window = window_ref[0, :, low:high].astype(jnp.float32)
+    groups = ROWS // LOOK_AZ
+    place = lax.broadcasted_iota(jnp.int32, (ROWS, window.shape[0]), 0)
+    line = LOOK_AZ * (place % groups) + place // groups
+    offset = lax.broadcasted_iota(jnp.int32, (ROWS, window.shape[0]), 1) - line
+    taps = jnp.zeros((ROWS, window.shape[0]), jnp.float32)
+    for tap in range(8):
+        taps = jnp.where(offset == tap, weights_ref[tap], taps)
+    along = jnp.dot(taps, window, precision=lax.Precision.HIGHEST, preferred_element_type=jnp.float32)
     zeros = jnp.zeros((ROWS, EDGE), jnp.float32)
     row = jnp.concatenate([zeros, along] if side == 0 else [along, zeros], axis=1)
     width = row.shape[1]
@@ -108,11 +113,16 @@
     start = border + shift_lines - 3
     window = lax.dynamic_slice_in_dim(padded, start, nlines + 16, 1)
     weights = table[kern_lines]
-    coeff = jnp.take(table, kern_range, axis=0)
-    shift = (shift_range + OFFRG)[:, None]
-    left = look_order(resample_half(0, weights, window, coeff, shift))
-    right = look_order(resample_half(1, weights, window, coeff, shift))
+    coeff = lines_in_look_order(jnp.take(table, kern_range, axis=0))
+    shift = lines_in_look_order((shift_range + OFFRG)[:, None])
+    left = resample_half(0, weights, window, coeff, shift)
+    right = resample_half(1, weights, window, coeff, shift)
     return left, right
+
+
+def lines_in_look_order(values):
+    nlines = values.shape[0]
+    return values.reshape(nlines // LOOK_AZ, LOOK_AZ, -1).transpose(1, 0, 2).reshape(nlines, -1)
 
 
 CHUNK = 512

time: 199 us -> 196 us (0.985); the launches traced: 196 us -> 195 us
  waiting for transfers between devices: 45.6 us -> 55.3 us
  local copies, waits for them, and re-layouts: 16.3 us -> 9.46 us
  Pallas kernels: 69.5 us -> 66.4 us
  other arithmetic: 15.1 us -> 12.2 us
    pallas_call x2 -> x0, local copies, waits for them, and re-layouts: 5.33 us -> none  [resample_half(): pl.pallas_call(functools.partial(resample_kernel, side), grid=(2, nlines...]
    ppermute x6, waiting for transfers between devices: 32.7 us -> 37.8 us  [shifted(): return lax.ppermute(block, axis, route)]
    ppermute x2, waiting for transfers between devices: 12.9 us -> 17.5 us  [swapped(): return lax.ppermute(block, axis, [(i, i ^ 1) for i in range(count)])]
    pallas_call x2, Pallas kernels: 34.6 us -> 31.5 us  [resample_half(): pl.pallas_call(functools.partial(resample_kernel, side), grid=(2, nlines...]
  transfers between devices with their start and end apart: 11 -> 11, of which waited for: 5 -> 5; matrix products, arithmetic and copies ran while one was open for 9% -> 6% of each run, Pallas kernels for 24% -> 24%
where the time goes in v20:
time: 196 us; the launch traced here: 195 us
  Pallas kernels  66.4 us (34%)
  waiting for transfers between devices  55.3 us (28%)
  starting transfers between devices  29.6 us (15%)
  between operations  21.8 us (11%)
  other arithmetic  12.2 us (6%)
  local copies, waits for them, and re-layouts  9.46 us (5%)
    ppermute x6, waiting for transfers between devices, shifted(): return lax.ppermute(block, axis, route)  37.8 us
    pallas_call x8, Pallas kernels, looks(): pl.pallas_call(looks_kernel, grid=(width // CHUNK,), in_specs=[spec, spec...  34.9 us
    pallas_call x2, Pallas kernels, resample_half(): pl.pallas_call(functools.partial(resample_kernel, side), grid=(2, nlines...  31.5 us
    ppermute x6, starting transfers between devices, shifted(): return lax.ppermute(block, axis, route)  18.6 us
    ppermute x2, waiting for transfers between devices, swapped(): return lax.ppermute(block, axis, [(i, i ^ 1) for i in range(count)])  17.5 us
    all_to_all x1, starting transfers between devices, shards(): got = lax.all_to_all(sent, 'date', 0, 0, tiled=True)  5.58 us
    dynamic_slice x1, other arithmetic, resample_block(): window = lax.dynamic_slice_in_dim(padded, start, nlines + 16, 1)  3.94 us
  transfers between devices with their start and end apart: 11, of which 5 were waited for; matrix products, arithmetic and copies ran while one was open for 6% of the time, Pallas kernels for 24%

profile of v20, /device:TPU:0, one launch (start us, length us, event | category | flops | bytes accessed | tf_op | source)
XLA Modules:
  0.0 194.8 jit_solution(11831260349396628969)
XLA Ops:
  0.0 1.8 slice.131
  1.8 2.4 %collective-permute-start = (bf16[1,2,16,4096]{3,2,1,0:T(8,128)(2,1)}, bf16[1,2,16,4096]{3,2,1,0:T(8,128)(2,1)S(1)}, u32[]{:S(2)}, u32[]{:S(2)}) collective-permute-start(bf16[1,2,16,4096]{3,2,1,0:T(8,128)(2,1)} %slice.131), channel_id=1, source_target_pairs={{0,1},{1,2},{2,3},{4,5},{5,6},{6,7},{8,9},{9,10},{10,11},{12,13},{... | collective-permute-start | bytes 786440 | tf_op jit(solution)/shard_map/ppermute | solution.py:27
  4.2 1.9 slice.132
  6.1 1.3 collective-permute-start.1
  7.4 0.7 compare_select_fusion.1
  8.1 0.5 broadcast.448
  8.6 1.3 reduce.9
  9.9 0.1 squeeze.28
  10.0 0.1 fusion.17
  10.1 0.7 add_reduce_fusion
  12.1 0.1 copy.21
  12.2 0.8 fusion.14.weights_ref
  13.0 0.1 add.231
  13.1 0.1 copy.24
  13.2 0.7 gather_fusion
  13.8 0.1 copy.22
  13.9 0.1 gather.7
  14.0 0.8 copy.23
  14.8 0.7 reshape.1168.shift_ref
  15.5 0.0 collective-permute-done
  15.5 0.0 collective-permute-done.1
  15.5 0.0 copy-done.3
  15.5 3.9 %fusion.2.window_ref = bf16[2,176,4096]{2,1,0:T(8,128)(2,1)} fusion(s32[]{:T(128)S(6)} %select_n.546, bf16[1,2,16,4096]{3,2,1,0:T(8,128)(2,1)S(1)} %collective-permute-done, bf16[1,2,160,4096]{3,2,1,0:T(8,128)(2,1)S(1)} %copy-done.3, bf16[1,2,25,4096]{3,2,1,0:T(8,128)(2,1)S(1)} %collective-permute-done.1), kind=kLoop, calls=%fused_computation.6 | loop fusion | flops 8650752 | bytes 6176772 | tf_op jit(solution)/shard_map/dynamic_slice | solution.py:114
  19.4 15.7 %shard_map.64.first_ref = bf16[2,160,2048]{2,1,0:T(8,128)(2,1)} custom-call(f32[8]{0:T(128)} %fusion.14.weights_ref, bf16[2,176,4096]{2,1,0:T(8,128)(2,1)} %fusion.2.window_ref, f32[160,8]{1,0:T(8,128)} %bitcast.113, s32[160,1]{1,0:T(8,128)} %reshape.1168.shift_ref), custom_call_target="tpu_custom_call" | custom-call | flops 39321600 | bytes 3932160 | tf_op jit(solution)/shard_map/pallas_call | solution.py:92
  35.2 4.7 %collective-permute-start.2 = (bf16[2,160,2048]{2,1,0:T(8,128)(2,1)}, bf16[2,160,2048]{2,1,0:T(8,128)(2,1)S(1)}, u32[]{:S(2)}, u32[]{:S(2)}) collective-permute-start(bf16[2,160,2048]{2,1,0:T(8,128)(2,1)} %shard_map.64.first_ref), channel_id=1, source_target_pairs={{0,8},{4,12},{8,16},{12,20},{16,24},{20,28},{1,9},{5,13},{9,17},{1... | collective-permute-start | bytes 3932168 | tf_op jit(solution)/shard_map/ppermute | solution.py:39
  39.9 15.8 %shard_map.66.first_ref = bf16[2,160,2048]{2,1,0:T(8,128)(2,1)} custom-call(f32[8]{0:T(128)} %fusion.14.weights_ref, bf16[2,176,4096]{2,1,0:T(8,128)(2,1)} %fusion.2.window_ref, f32[160,8]{1,0:T(8,128)} %bitcast.114, s32[160,1]{1,0:T(8,128)} %reshape.1168.shift_ref), custom_call_target="tpu_custom_call" | custom-call | flops 39321600 | bytes 3932160 | tf_op jit(solution)/shard_map/pallas_call | solution.py:92
  55.6 1.3 collective-permute-start.4
  56.9 0.0 copy-start
  57.0 10.0 %collective-permute-done.2.second_ref = bf16[2,160,2048]{2,1,0:T(8,128)(2,1)S(1)} collective-permute-done((bf16[2,160,2048]{2,1,0:T(8,128)(2,1)}, bf16[2,160,2048]{2,1,0:T(8,128)(2,1)S(1)}, u32[]{:S(2)}, u32[]{:S(2)}) %collective-permute-start.2) | collective-permute-done | bytes 1310752 | tf_op jit(solution)/shard_map/ppermute | solution.py:39
  67.0 0.0 copy-done.1
  67.0 1.3 broadcast_select_fusion.1
  68.3 1.5 collective-permute-start.6
  69.8 17.8 %collective-permute-done.4.second_ref = bf16[2,160,2048]{2,1,0:T(8,128)(2,1)} collective-permute-done((bf16[2,160,2048]{2,1,0:T(8,128)(2,1)}, bf16[2,160,2048]{2,1,0:T(8,128)(2,1)}, u32[]{:S(2)}, u32[]{:S(2)}) %collective-permute-start.4) | collective-permute-done | bytes 1310752 | tf_op jit(solution)/shard_map/ppermute | solution.py:39
  87.7 0.0 copy-done
  87.7 1.5 broadcast_select_fusion
  89.2 0.3 collective-permute-start.8
  89.4 4.5 %collective-permute-start.3 = (bf16[2,160,2048]{2,1,0:T(8,128)(2,1)S(1)}, bf16[2,160,2048]{2,1,0:T(8,128)(2,1)}, u32[]{:S(2)}, u32[]{:S(2)}) collective-permute-start(bf16[2,160,2048]{2,1,0:T(8,128)(2,1)S(1)} %collective-permute-done.2.second_ref), channel_id=1, source_target_pairs={{0,8},{4,12},{8,16},{12,20},{16,24},{20,28},{1,9},{5,13},{9,17},{1... | collective-permute-start | bytes 3932168 | tf_op jit(solution)/shard_map/ppermute | solution.py:39
  93.9 1.3 collective-permute-start.5
  95.2 4.4 %shard_map.68 = f32[2,8,512]{2,1,0:T(8,128)} custom-call(bf16[2,160,2048]{2,1,0:T(8,128)(2,1)} %shard_map.64.first_ref, bf16[2,160,2048]{2,1,0:T(8,128)(2,1)} %copy-done.2), custom_call_target="tpu_custom_call" | custom-call | flops 13107200 | bytes 2621440 | tf_op jit(solution)/shard_map/pallas_call | solution.py:157
  99.6 0.0 collective-permute-done.6.second_ref
  99.6 5.6 %collective-permute-start.7 = (bf16[2,160,2048]{2,1,0:T(8,128)(2,1)}, bf16[2,160,2048]{2,1,0:T(8,128)(2,1)}, u32[]{:S(2)}, u32[]{:S(2)}) collective-permute-start(bf16[2,160,2048]{2,1,0:T(8,128)(2,1)} %collective-permute-done.6.second_ref), channel_id=1, source_target_pairs={{0,8},{4,12},{8,16},{12,20},{16,24},{20,28},{1,9},{5,13},{9,17},{1... | collective-permute-start | bytes 3932168 | tf_op jit(solution)/shard_map/ppermute | solution.py:39
  105.2 4.4 %shard_map.70 = f32[2,8,512]{2,1,0:T(8,128)} custom-call(bf16[2,160,2048]{2,1,0:T(8,128)(2,1)} %shard_map.66.first_ref, bf16[2,160,2048]{2,1,0:T(8,128)(2,1)} %collective-permute-done.4.second_ref), custom_call_target="tpu_custom_call" | custom-call | flops 13107200 | bytes 2621440 | tf_op jit(solution)/shard_map/pallas_call | solution.py:157
  109.6 17.5 %collective-permute-done.8.second_ref = bf16[2,160,2048]{2,1,0:T(8,128)(2,1)} collective-permute-done((bf16[2,160,2048]{2,1,0:T(8,128)(2,1)S(1)}, bf16[2,160,2048]{2,1,0:T(8,128)(2,1)}, u32[]{:S(2)}, u32[]{:S(2)}) %collective-permute-start.8) | collective-permute-done | bytes 1310752 | tf_op jit(solution)/shard_map/ppermute | solution.py:44
  127.1 1.3 collective-permute-start.9
  128.4 4.4 %shard_map.72 = f32[2,8,512]{2,1,0:T(8,128)} custom-call(bf16[2,160,2048]{2,1,0:T(8,128)(2,1)} %shard_map.64.first_ref, bf16[2,160,2048]{2,1,0:T(8,128)(2,1)} %collective-permute-done.6.second_ref), custom_call_target="tpu_custom_call" | custom-call | flops 13107200 | bytes 2621440 | tf_op jit(solution)/shard_map/pallas_call | solution.py:157
  132.8 4.4 %shard_map.73 = f32[2,8,512]{2,1,0:T(8,128)} custom-call(bf16[2,160,2048]{2,1,0:T(8,128)(2,1)} %shard_map.66.first_ref, bf16[2,160,2048]{2,1,0:T(8,128)(2,1)} %collective-permute-done.8.second_ref), custom_call_target="tpu_custom_call" | custom-call | flops 13107200 | bytes 2621440 | tf_op jit(solution)/shard_map/pallas_call | solution.py:157
  137.1 0.0 collective-permute-done.3.second_ref
  137.1 4.4 %shard_map.65 = f32[2,8,512]{2,1,0:T(8,128)} custom-call(bf16[2,160,2048]{2,1,0:T(8,128)(2,1)} %shard_map.64.first_ref, bf16[2,160,2048]{2,1,0:T(8,128)(2,1)} %collective-permute-done.3.second_ref), custom_call_target="tpu_custom_call" | custom-call | flops 13107200 | bytes 2621440 | tf_op jit(solution)/shard_map/pallas_call | solution.py:157
  141.5 0.0 collective-permute-done.5.second_ref
  141.5 4.4 %shard_map.67 = f32[2,8,512]{2,1,0:T(8,128)} custom-call(bf16[2,160,2048]{2,1,0:T(8,128)(2,1)} %shard_map.66.first_ref, bf16[2,160,2048]{2,1,0:T(8,128)(2,1)} %collective-permute-done.5.second_ref), custom_call_target="tpu_custom_call" | custom-call | flops 13107200 | bytes 2621440 | tf_op jit(solution)/shard_map/pallas_call | solution.py:157
  145.9 3.5 %collective-permute-done.7.second_ref = bf16[2,160,2048]{2,1,0:T(8,128)(2,1)} collective-permute-done((bf16[2,160,2048]{2,1,0:T(8,128)(2,1)}, bf16[2,160,2048]{2,1,0:T(8,128)(2,1)}, u32[]{:S(2)}, u32[]{:S(2)}) %collective-permute-start.7) | collective-permute-done | bytes 1310752 | tf_op jit(solution)/shard_map/ppermute | solution.py:39
  149.4 4.4 %shard_map.69 = f32[2,8,512]{2,1,0:T(8,128)} custom-call(bf16[2,160,2048]{2,1,0:T(8,128)(2,1)} %shard_map.64.first_ref, bf16[2,160,2048]{2,1,0:T(8,128)(2,1)} %collective-permute-done.7.second_ref), custom_call_target="tpu_custom_call" | custom-call | flops 13107200 | bytes 2621440 | tf_op jit(solution)/shard_map/pallas_call | solution.py:157
  153.8 0.0 copy-start.8
  153.8 0.0 copy-start.13
  153.8 6.4 %collective-permute-done.9.second_ref = bf16[2,160,2048]{2,1,0:T(8,128)(2,1)S(1)} collective-permute-done((bf16[2,160,2048]{2,1,0:T(8,128)(2,1)}, bf16[2,160,2048]{2,1,0:T(8,128)(2,1)S(1)}, u32[]{:S(2)}, u32[]{:S(2)}) %collective-permute-start.9) | collective-permute-done | bytes 1310752 | tf_op jit(solution)/shard_map/ppermute | solution.py:39
  160.2 1.1 copy-done.4
  161.3 4.4 %shard_map.71 = f32[2,8,512]{2,1,0:T(8,128)} custom-call(bf16[2,160,2048]{2,1,0:T(8,128)(2,1)} %shard_map.66.first_ref, bf16[2,160,2048]{2,1,0:T(8,128)(2,1)} %copy-done.4), custom_call_target="tpu_custom_call" | custom-call | flops 13107200 | bytes 2621440 | tf_op jit(solution)/shard_map/pallas_call | solution.py:157
  165.7 0.0 copy-done.5
  165.7 1.6 select_select_fusion
  167.4 5.6 %all-to-all-start = ((f32[8,2,8,512]{3,2,1,0:T(8,128)}), f32[8,2,8,512]{3,2,1,0:T(8,128)S(1)}, u32[]{:S(2)}, u32[]{:S(2)}) async-start(f32[8,2,8,512]{3,2,1,0:T(8,128)} %select_select_fusion), calls=%async_computation | async-start | bytes 524288 | tf_op jit(solution)/shard_map/all_to_all | solution.py:207
  172.9 0.0 copy-done.13
  172.9 0.7 fusion.47
  193.7 0.0 all-to-all-done
  194.1 0.7 maximum_bitcast_fusion
  (41 shorter events, 0.3 us)
Async XLA Ops:
  0.0 15.5 %copy-start.3 = (bf16[1,2,160,4096]{3,2,1,0:T(8,128)(2,1)S(1)}, bf16[1,2,160,4096]{3,2,1,0:T(8,128)(2,1)}, u32[]{:S(2)}) copy-start(bf16[1,2,160,4096]{3,2,1,0:T(8,128)(2,1)} %param.6) | copy-start | bytes 7864324
  1.8 13.7 %collective-permute-start = (bf16[1,2,16,4096]{3,2,1,0:T(8,128)(2,1)}, bf16[1,2,16,4096]{3,2,1,0:T(8,128)(2,1)S(1)}, u32[]{:S(2)}, u32[]{:S(2)}) collective-permute-start(bf16[1,2,16,4096]{3,2,1,0:T(8,128)(2,1)} %slice.131), channel_id=1, source_target_pairs={{0,1},{1,2},{2,3},{4,5},{5,6},{6,7},{8,9},{9,10},{10,11},{12,13},{... | collective-permute-start | bytes 786440 | tf_op jit(solution)/shard_map/ppermute | solution.py:27
  6.1 9.4 %collective-permute-start.1 = (bf16[1,2,25,4096]{3,2,1,0:T(8,128)(2,1)}, bf16[1,2,25,4096]{3,2,1,0:T(8,128)(2,1)S(1)}, u32[]{:S(2)}, u32[]{:S(2)}) collective-permute-start(bf16[1,2,25,4096]{3,2,1,0:T(8,128)(2,1)} %slice.132), channel_id=1, source_target_pairs={{1,0},{2,1},{3,2},{5,4},{6,5},{7,6},{9,8},{10,9},{11,10},{13,12},{... | collective-permute-start | bytes 1228808 | tf_op jit(solution)/shard_map/ppermute | solution.py:29
  35.2 31.8 %copy-start.1 = (bf16[2,160,2048]{2,1,0:T(8,128)(2,1)S(1)}, bf16[2,160,2048]{2,1,0:T(8,128)(2,1)}, u32[]{:S(2)}) copy-start(bf16[2,160,2048]{2,1,0:T(8,128)(2,1)} %shard_map.64.first_ref) | copy-start | bytes 3932164
  35.2 31.8 %collective-permute-start.2 = (bf16[2,160,2048]{2,1,0:T(8,128)(2,1)}, bf16[2,160,2048]{2,1,0:T(8,128)(2,1)S(1)}, u32[]{:S(2)}, u32[]{:S(2)}) collective-permute-start(bf16[2,160,2048]{2,1,0:T(8,128)(2,1)} %shard_map.64.first_ref), channel_id=1, source_target_pairs={{0,8},{4,12},{8,16},{12,20},{16,24},{20,28},{1,9},{5,13},{9,17},{1... | collective-permute-start | bytes 3932168 | tf_op jit(solution)/shard_map/ppermute | solution.py:39
  55.6 32.0 %collective-permute-start.4 = (bf16[2,160,2048]{2,1,0:T(8,128)(2,1)}, bf16[2,160,2048]{2,1,0:T(8,128)(2,1)}, u32[]{:S(2)}, u32[]{:S(2)}) collective-permute-start(bf16[2,160,2048]{2,1,0:T(8,128)(2,1)} %shard_map.66.first_ref), channel_id=1, source_target_pairs={{8,0},{12,4},{16,8},{20,12},{24,16},{28,20},{9,1},{13,5},{17,9},{2... | collective-permute-start | bytes 3932168 | tf_op jit(solution)/shard_map/ppermute | solution.py:39
  56.9 30.7 %copy-start = (bf16[2,160,2048]{2,1,0:T(8,128)(2,1)S(1)}, bf16[2,160,2048]{2,1,0:T(8,128)(2,1)}, u32[]{:S(2)}) copy-start(bf16[2,160,2048]{2,1,0:T(8,128)(2,1)} %shard_map.66.first_ref) | copy-start | bytes 3932164
  67.0 22.5 %copy-start.2 = (bf16[2,160,2048]{2,1,0:T(8,128)(2,1)}, bf16[2,160,2048]{2,1,0:T(8,128)(2,1)S(1)}, u32[]{:S(2)}) copy-start(bf16[2,160,2048]{2,1,0:T(8,128)(2,1)S(1)} %collective-permute-done.2.second_ref) | copy-start | bytes 3932164
  68.3 31.3 %collective-permute-start.6 = (bf16[2,160,2048]{2,1,0:T(8,128)(2,1)}, bf16[2,160,2048]{2,1,0:T(8,128)(2,1)}, u32[]{:S(2)}, u32[]{:S(2)}) collective-permute-start(bf16[2,160,2048]{2,1,0:T(8,128)(2,1)} %broadcast_select_fusion.1), channel_id=1, source_target_pairs={{0,4},{4,0},{8,12},{12,8},{16,20},{20,16},{24,28},{28,24},{1,5},{5... | collective-permute-start | bytes 3932168 | tf_op jit(solution)/shard_map/ppermute | solution.py:44
  89.2 37.9 %collective-permute-start.8 = (bf16[2,160,2048]{2,1,0:T(8,128)(2,1)S(1)}, bf16[2,160,2048]{2,1,0:T(8,128)(2,1)}, u32[]{:S(2)}, u32[]{:S(2)}) collective-permute-start(bf16[2,160,2048]{2,1,0:T(8,128)(2,1)S(1)} %broadcast_select_fusion), channel_id=1, source_target_pairs={{0,4},{4,0},{8,12},{12,8},{16,20},{20,16},{24,28},{28,24},{1,5},{5... | collective-permute-start | bytes 3932168 | tf_op jit(solution)/shard_map/ppermute | solution.py:44
  89.4 47.7 %collective-permute-start.3 = (bf16[2,160,2048]{2,1,0:T(8,128)(2,1)S(1)}, bf16[2,160,2048]{2,1,0:T(8,128)(2,1)}, u32[]{:S(2)}, u32[]{:S(2)}) collective-permute-start(bf16[2,160,2048]{2,1,0:T(8,128)(2,1)S(1)} %collective-permute-done.2.second_ref), channel_id=1, source_target_pairs={{0,8},{4,12},{8,16},{12,20},{16,24},{20,28},{1,9},{5,13},{9,17},{1... | collective-permute-start | bytes 3932168 | tf_op jit(solution)/shard_map/ppermute | solution.py:39
  93.9 47.6 %collective-permute-start.5 = (bf16[2,160,2048]{2,1,0:T(8,128)(2,1)}, bf16[2,160,2048]{2,1,0:T(8,128)(2,1)}, u32[]{:S(2)}, u32[]{:S(2)}) collective-permute-start(bf16[2,160,2048]{2,1,0:T(8,128)(2,1)} %collective-permute-done.4.second_ref), channel_id=1, source_target_pairs={{8,0},{12,4},{16,8},{20,12},{24,16},{28,20},{9,1},{13,5},{17,9},{2... | collective-permute-start | bytes 3932168 | tf_op jit(solution)/shard_map/ppermute | solution.py:39
  99.6 49.8 %collective-permute-start.7 = (bf16[2,160,2048]{2,1,0:T(8,128)(2,1)}, bf16[2,160,2048]{2,1,0:T(8,128)(2,1)}, u32[]{:S(2)}, u32[]{:S(2)}) collective-permute-start(bf16[2,160,2048]{2,1,0:T(8,128)(2,1)} %collective-permute-done.6.second_ref), channel_id=1, source_target_pairs={{0,8},{4,12},{8,16},{12,20},{16,24},{20,28},{1,9},{5,13},{9,17},{1... | collective-permute-start | bytes 3932168 | tf_op jit(solution)/shard_map/ppermute | solution.py:39
  127.1 33.2 %collective-permute-start.9 = (bf16[2,160,2048]{2,1,0:T(8,128)(2,1)}, bf16[2,160,2048]{2,1,0:T(8,128)(2,1)S(1)}, u32[]{:S(2)}, u32[]{:S(2)}) collective-permute-start(bf16[2,160,2048]{2,1,0:T(8,128)(2,1)} %collective-permute-done.8.second_ref), channel_id=1, source_target_pairs={{8,0},{12,4},{16,8},{20,12},{24,16},{28,20},{9,1},{13,5},{17,9},{2... | collective-permute-start | bytes 3932168 | tf_op jit(solution)/shard_map/ppermute | solution.py:39
  153.7 11.9 %copy-start.5 = (f32[2,8,512]{2,1,0:T(8,128)S(1)}, f32[2,8,512]{2,1,0:T(8,128)}, u32[]{:S(2)}) copy-start(f32[2,8,512]{2,1,0:T(8,128)} %shard_map.68) | copy-start | bytes 98308
  153.7 11.9 %copy-start.6 = (f32[2,8,512]{2,1,0:T(8,128)S(1)}, f32[2,8,512]{2,1,0:T(8,128)}, u32[]{:S(2)}) copy-start(f32[2,8,512]{2,1,0:T(8,128)} %shard_map.70) | copy-start | bytes 98308
  153.8 11.9 %copy-start.7 = (f32[2,8,512]{2,1,0:T(8,128)S(1)}, f32[2,8,512]{2,1,0:T(8,128)}, u32[]{:S(2)}) copy-start(f32[2,8,512]{2,1,0:T(8,128)} %shard_map.72) | copy-start | bytes 98308
  153.8 11.9 %copy-start.8 = (f32[2,8,512]{2,1,0:T(8,128)S(1)}, f32[2,8,512]{2,1,0:T(8,128)}, u32[]{:S(2)}) copy-start(f32[2,8,512]{2,1,0:T(8,128)} %shard_map.73) | copy-start | bytes 98308
  153.8 11.9 %copy-start.9 = (f32[2,8,512]{2,1,0:T(8,128)S(1)}, f32[2,8,512]{2,1,0:T(8,128)}, u32[]{:S(2)}) copy-start(f32[2,8,512]{2,1,0:T(8,128)} %shard_map.65) | copy-start | bytes 98308
  153.8 11.9 %copy-start.10 = (f32[2,8,512]{2,1,0:T(8,128)S(1)}, f32[2,8,512]{2,1,0:T(8,128)}, u32[]{:S(2)}) copy-start(f32[2,8,512]{2,1,0:T(8,128)} %shard_map.67) | copy-start | bytes 98308
  153.8 11.9 %copy-start.11 = (f32[2,8,512]{2,1,0:T(8,128)S(1)}, f32[2,8,512]{2,1,0:T(8,128)}, u32[]{:S(2)}) copy-start(f32[2,8,512]{2,1,0:T(8,128)} %shard_map.69) | copy-start | bytes 98308
  153.8 19.1 %copy-start.13 = (s32[1,4]{1,0:T(1,128)S(1)}, s32[1,4]{1,0:T(1,128)}, u32[]{:S(2)}) copy-start(s32[1,4]{1,0:T(1,128)} %param.11) | copy-start | bytes 52
  160.2 1.1 copy-start.4
  165.7 28.2 %copy-start.12 = (f32[2,8,512]{2,1,0:T(8,128)S(1)}, f32[2,8,512]{2,1,0:T(8,128)}, u32[]{:S(2)}) copy-start(f32[2,8,512]{2,1,0:T(8,128)} %shard_map.71) | copy-start | bytes 98308
  167.4 26.4 %all-to-all-start = ((f32[8,2,8,512]{3,2,1,0:T(8,128)}), f32[8,2,8,512]{3,2,1,0:T(8,128)S(1)}, u32[]{:S(2)}, u32[]{:S(2)}) async-start(f32[8,2,8,512]{3,2,1,0:T(8,128)} %select_select_fusion), calls=%async_computation | async-start | bytes 524288 | tf_op jit(solution)/shard_map/all_to_all | solution.py:207

commit v21 on v20

--- a/solution.py
+++ b/solution.py
@@ -128,37 +128,42 @@
 CHUNK = 512
 
 
+BLOCK = 1024
+
+
 def looks_kernel(first_ref, second_ref, out_ref):
-    first_re = first_ref[0].astype(jnp.float32)
-    first_im = first_ref[1].astype(jnp.float32)
-    second_re = second_ref[0].astype(jnp.float32)
-    second_im = second_ref[1].astype(jnp.float32)
-    real_part = first_re * second_re + first_im * second_im
-    imag_part = first_im * second_re - first_re * second_im
-    rows = real_part.shape[0]
+    rows = first_ref.shape[1]
     groups = rows // LOOK_AZ
-    real_lines = real_part.reshape(LOOK_AZ, groups, CHUNK).sum(axis=0)
-    imag_lines = imag_part.reshape(LOOK_AZ, groups, CHUNK).sum(axis=0)
     pooling = (
         lax.broadcasted_iota(jnp.int32, (CHUNK, CHUNK // LOOK_RG), 0) // LOOK_RG
         == lax.broadcasted_iota(jnp.int32, (CHUNK, CHUNK // LOOK_RG), 1)
     ).astype(jnp.float32)
-    real_looks = jnp.dot(real_lines, pooling, precision=lax.Precision.HIGHEST, preferred_element_type=jnp.float32)
-    imag_looks = jnp.dot(imag_lines, pooling, precision=lax.Precision.HIGHEST, preferred_element_type=jnp.float32)
-    out_ref[0] = real_looks / (LOOK_AZ * LOOK_RG)
-    out_ref[1] = imag_looks / (LOOK_AZ * LOOK_RG)
+    for low in range(0, first_ref.shape[2], CHUNK):
+        first_re = first_ref[0, :, low : low + CHUNK].astype(jnp.float32)
+        first_im = first_ref[1, :, low : low + CHUNK].astype(jnp.float32)
+        second_re = second_ref[0, :, low : low + CHUNK].astype(jnp.float32)
+        second_im = second_ref[1, :, low : low + CHUNK].astype(jnp.float32)
+        real_part = first_re * second_re + first_im * second_im
+        imag_part = first_im * second_re - first_re * second_im
+        real_lines = real_part.reshape(LOOK_AZ, groups, CHUNK).sum(axis=0)
+        imag_lines = imag_part.reshape(LOOK_AZ, groups, CHUNK).sum(axis=0)
+        real_looks = jnp.dot(real_lines, pooling, precision=lax.Precision.HIGHEST, preferred_element_type=jnp.float32)
+        imag_looks = jnp.dot(imag_lines, pooling, precision=lax.Precision.HIGHEST, preferred_element_type=jnp.float32)
+        out = slice(low // LOOK_RG, (low + CHUNK) // LOOK_RG)
+        out_ref[0, :, out] = real_looks / (LOOK_AZ * LOOK_RG)
+        out_ref[1, :, out] = imag_looks / (LOOK_AZ * LOOK_RG)
 
 
 def looks(first, second):
     nlines = first.shape[1]
     width = first.shape[2]
     groups = nlines // LOOK_AZ
-    spec = pl.BlockSpec((2, nlines, CHUNK), lambda j: (0, 0, j))
+    spec = pl.BlockSpec((2, nlines, BLOCK), lambda j: (0, 0, j))
     return pl.pallas_call(
         looks_kernel,
-        grid=(width // CHUNK,),
+        grid=(width // BLOCK,),
         in_specs=[spec, spec],
-        out_specs=pl.BlockSpec((2, groups, CHUNK // LOOK_RG), lambda j: (0, 0, j)),
+        out_specs=pl.BlockSpec((2, groups, BLOCK // LOOK_RG), lambda j: (0, 0, j)),
         out_shape=jax.ShapeDtypeStruct((2, groups, width // LOOK_RG), jnp.float32),
         cost_estimate=pl.CostEstimate(
             flops=nlines * width * 40, transcendentals=0, bytes_accessed=2 * 2 * nlines * width * 2

time: 196 us -> 195 us (level)
  Pallas kernels: 66.4 us -> 58 us
  waiting for transfers between devices: 55.3 us -> 62.8 us
    pallas_call x8, Pallas kernels: 34.9 us -> 26.5 us  [looks(): pl.pallas_call(looks_kernel, grid=(width // BLOCK,), in_specs=[spec, spec...]
    ppermute x6, waiting for transfers between devices: 37.8 us -> 42.8 us  [shifted(): return lax.ppermute(block, axis, route)]
    ppermute x2, waiting for transfers between devices: 17.5 us -> 20 us  [swapped(): return lax.ppermute(block, axis, [(i, i ^ 1) for i in range(count)])]
  transfers between devices with their start and end apart: 11 -> 11, of which waited for: 5 -> 6; matrix products, arithmetic and copies ran while one was open for 6% -> 6% of each run, Pallas kernels for 24% -> 20%
where the time goes in v21:
time: 195 us; the launch traced here: 194 us
  waiting for transfers between devices  62.8 us (32%)
  Pallas kernels  58 us (30%)
  starting transfers between devices  29.5 us (15%)
  between operations  21.8 us (11%)
  other arithmetic  12.2 us (6%)
  local copies, waits for them, and re-layouts  9.46 us (5%)
    ppermute x6, waiting for transfers between devices, shifted(): return lax.ppermute(block, axis, route)  42.8 us
    pallas_call x2, Pallas kernels, resample_half(): pl.pallas_call(functools.partial(resample_kernel, side), grid=(2, nlines...  31.5 us
    pallas_call x8, Pallas kernels, looks(): pl.pallas_call(looks_kernel, grid=(width // BLOCK,), in_specs=[spec, spec...  26.5 us
    ppermute x2, waiting for transfers between devices, swapped(): return lax.ppermute(block, axis, [(i, i ^ 1) for i in range(count)])  20 us
    ppermute x6, starting transfers between devices, shifted(): return lax.ppermute(block, axis, route)  18.5 us
    all_to_all x1, starting transfers between devices, shards(): got = lax.all_to_all(sent, 'date', 0, 0, tiled=True)  5.58 us
    dynamic_slice x1, other arithmetic, resample_block(): window = lax.dynamic_slice_in_dim(padded, start, nlines + 16, 1)  3.94 us
  transfers between devices with their start and end apart: 11, of which 6 were waited for; matrix products, arithmetic and copies ran while one was open for 6% of the time, Pallas kernels for 20%

profile of v21, /device:TPU:0, one launch (start us, length us, event | category | flops | bytes accessed | tf_op | source)
XLA Modules:
  0.0 193.7 jit_solution(6470784372970520212)
XLA Ops:
  0.0 1.8 slice.131
  1.8 2.4 %collective-permute-start = (bf16[1,2,16,4096]{3,2,1,0:T(8,128)(2,1)}, bf16[1,2,16,4096]{3,2,1,0:T(8,128)(2,1)S(1)}, u32[]{:S(2)}, u32[]{:S(2)}) collective-permute-start(bf16[1,2,16,4096]{3,2,1,0:T(8,128)(2,1)} %slice.131), channel_id=1, source_target_pairs={{0,1},{1,2},{2,3},{4,5},{5,6},{6,7},{8,9},{9,10},{10,11},{12,13},{... | collective-permute-start | bytes 786440 | tf_op jit(solution)/shard_map/ppermute | solution.py:27
  4.2 1.9 slice.132
  6.1 1.3 collective-permute-start.1
  7.4 0.7 compare_select_fusion.1
  8.1 0.5 broadcast.448
  8.6 1.3 reduce.9
  9.9 0.1 squeeze.28
  10.0 0.1 fusion.17
  10.1 0.7 add_reduce_fusion
  12.1 0.1 copy.21
  12.2 0.8 fusion.14.weights_ref
  13.0 0.1 add.231
  13.1 0.1 copy.24
  13.2 0.7 gather_fusion
  13.8 0.1 copy.22
  13.9 0.1 gather.7
  14.0 0.8 copy.23
  14.8 0.7 reshape.1168.shift_ref
  15.5 0.0 collective-permute-done
  15.5 0.0 collective-permute-done.1
  15.5 0.0 copy-done.3
  15.5 3.9 %fusion.2.window_ref = bf16[2,176,4096]{2,1,0:T(8,128)(2,1)} fusion(s32[]{:T(128)S(6)} %select_n.546, bf16[1,2,16,4096]{3,2,1,0:T(8,128)(2,1)S(1)} %collective-permute-done, bf16[1,2,160,4096]{3,2,1,0:T(8,128)(2,1)S(1)} %copy-done.3, bf16[1,2,25,4096]{3,2,1,0:T(8,128)(2,1)S(1)} %collective-permute-done.1), kind=kLoop, calls=%fused_computation.6 | loop fusion | flops 8650752 | bytes 6176772 | tf_op jit(solution)/shard_map/dynamic_slice | solution.py:114
  19.4 15.7 %shard_map.64.first_ref = bf16[2,160,2048]{2,1,0:T(8,128)(2,1)} custom-call(f32[8]{0:T(128)} %fusion.14.weights_ref, bf16[2,176,4096]{2,1,0:T(8,128)(2,1)} %fusion.2.window_ref, f32[160,8]{1,0:T(8,128)} %bitcast.113, s32[160,1]{1,0:T(8,128)} %reshape.1168.shift_ref), custom_call_target="tpu_custom_call" | custom-call | flops 39321600 | bytes 3932160 | tf_op jit(solution)/shard_map/pallas_call | solution.py:92
  35.2 4.7 %collective-permute-start.2 = (bf16[2,160,2048]{2,1,0:T(8,128)(2,1)}, bf16[2,160,2048]{2,1,0:T(8,128)(2,1)S(1)}, u32[]{:S(2)}, u32[]{:S(2)}) collective-permute-start(bf16[2,160,2048]{2,1,0:T(8,128)(2,1)} %shard_map.64.first_ref), channel_id=1, source_target_pairs={{0,8},{4,12},{8,16},{12,20},{16,24},{20,28},{1,9},{5,13},{9,17},{1... | collective-permute-start | bytes 3932168 | tf_op jit(solution)/shard_map/ppermute | solution.py:39
  39.9 15.8 %shard_map.66.first_ref = bf16[2,160,2048]{2,1,0:T(8,128)(2,1)} custom-call(f32[8]{0:T(128)} %fusion.14.weights_ref, bf16[2,176,4096]{2,1,0:T(8,128)(2,1)} %fusion.2.window_ref, f32[160,8]{1,0:T(8,128)} %bitcast.114, s32[160,1]{1,0:T(8,128)} %reshape.1168.shift_ref), custom_call_target="tpu_custom_call" | custom-call | flops 39321600 | bytes 3932160 | tf_op jit(solution)/shard_map/pallas_call | solution.py:92
  55.6 1.3 collective-permute-start.4
  56.9 0.0 copy-start
  57.0 10.0 %collective-permute-done.2.second_ref = bf16[2,160,2048]{2,1,0:T(8,128)(2,1)S(1)} collective-permute-done((bf16[2,160,2048]{2,1,0:T(8,128)(2,1)}, bf16[2,160,2048]{2,1,0:T(8,128)(2,1)S(1)}, u32[]{:S(2)}, u32[]{:S(2)}) %collective-permute-start.2) | collective-permute-done | bytes 1310752 | tf_op jit(solution)/shard_map/ppermute | solution.py:39
  67.0 0.0 copy-done.1
  67.0 1.3 broadcast_select_fusion.1
  68.3 1.5 collective-permute-start.6
  69.8 17.8 %collective-permute-done.4.second_ref = bf16[2,160,2048]{2,1,0:T(8,128)(2,1)} collective-permute-done((bf16[2,160,2048]{2,1,0:T(8,128)(2,1)}, bf16[2,160,2048]{2,1,0:T(8,128)(2,1)}, u32[]{:S(2)}, u32[]{:S(2)}) %collective-permute-start.4) | collective-permute-done | bytes 1310752 | tf_op jit(solution)/shard_map/ppermute | solution.py:39
  87.7 0.0 copy-done
  87.7 1.5 broadcast_select_fusion
  89.2 0.3 collective-permute-start.8
  89.4 0.0 copy-done.2
  89.4 4.5 %collective-permute-start.3 = (bf16[2,160,2048]{2,1,0:T(8,128)(2,1)S(1)}, bf16[2,160,2048]{2,1,0:T(8,128)(2,1)}, u32[]{:S(2)}, u32[]{:S(2)}) collective-permute-start(bf16[2,160,2048]{2,1,0:T(8,128)(2,1)S(1)} %collective-permute-done.2.second_ref), channel_id=1, source_target_pairs={{0,8},{4,12},{8,16},{12,20},{16,24},{20,28},{1,9},{5,13},{9,17},{1... | collective-permute-start | bytes 3932168 | tf_op jit(solution)/shard_map/ppermute | solution.py:39
  93.9 1.3 collective-permute-start.5
  95.2 3.3 %shard_map.68 = f32[2,8,512]{2,1,0:T(8,128)} custom-call(bf16[2,160,2048]{2,1,0:T(8,128)(2,1)} %shard_map.64.first_ref, bf16[2,160,2048]{2,1,0:T(8,128)(2,1)} %copy-done.2), custom_call_target="tpu_custom_call" | custom-call | flops 13107200 | bytes 2621440 | tf_op jit(solution)/shard_map/pallas_call | solution.py:162
  98.5 0.4 collective-permute-done.6.second_ref
  99.0 5.2 %collective-permute-start.7 = (bf16[2,160,2048]{2,1,0:T(8,128)(2,1)}, bf16[2,160,2048]{2,1,0:T(8,128)(2,1)}, u32[]{:S(2)}, u32[]{:S(2)}) collective-permute-start(bf16[2,160,2048]{2,1,0:T(8,128)(2,1)} %collective-permute-done.6.second_ref), channel_id=1, source_target_pairs={{0,8},{4,12},{8,16},{12,20},{16,24},{20,28},{1,9},{5,13},{9,17},{1... | collective-permute-start | bytes 3932168 | tf_op jit(solution)/shard_map/ppermute | solution.py:39
  104.2 3.3 %shard_map.70 = f32[2,8,512]{2,1,0:T(8,128)} custom-call(bf16[2,160,2048]{2,1,0:T(8,128)(2,1)} %shard_map.66.first_ref, bf16[2,160,2048]{2,1,0:T(8,128)(2,1)} %collective-permute-done.4.second_ref), custom_call_target="tpu_custom_call" | custom-call | flops 13107200 | bytes 2621440 | tf_op jit(solution)/shard_map/pallas_call | solution.py:162
  107.5 19.6 %collective-permute-done.8.second_ref = bf16[2,160,2048]{2,1,0:T(8,128)(2,1)} collective-permute-done((bf16[2,160,2048]{2,1,0:T(8,128)(2,1)S(1)}, bf16[2,160,2048]{2,1,0:T(8,128)(2,1)}, u32[]{:S(2)}, u32[]{:S(2)}) %collective-permute-start.8) | collective-permute-done | bytes 1310752 | tf_op jit(solution)/shard_map/ppermute | solution.py:44
  127.1 1.5 collective-permute-start.9
  128.6 3.3 %shard_map.72 = f32[2,8,512]{2,1,0:T(8,128)} custom-call(bf16[2,160,2048]{2,1,0:T(8,128)(2,1)} %shard_map.64.first_ref, bf16[2,160,2048]{2,1,0:T(8,128)(2,1)} %collective-permute-done.6.second_ref), custom_call_target="tpu_custom_call" | custom-call | flops 13107200 | bytes 2621440 | tf_op jit(solution)/shard_map/pallas_call | solution.py:162
  131.9 3.3 %shard_map.73 = f32[2,8,512]{2,1,0:T(8,128)} custom-call(bf16[2,160,2048]{2,1,0:T(8,128)(2,1)} %shard_map.66.first_ref, bf16[2,160,2048]{2,1,0:T(8,128)(2,1)} %collective-permute-done.8.second_ref), custom_call_target="tpu_custom_call" | custom-call | flops 13107200 | bytes 2621440 | tf_op jit(solution)/shard_map/pallas_call | solution.py:162
  135.3 0.0 collective-permute-done.3.second_ref
  135.3 3.3 %shard_map.65 = f32[2,8,512]{2,1,0:T(8,128)} custom-call(bf16[2,160,2048]{2,1,0:T(8,128)(2,1)} %shard_map.64.first_ref, bf16[2,160,2048]{2,1,0:T(8,128)(2,1)} %collective-permute-done.3.second_ref), custom_call_target="tpu_custom_call" | custom-call | flops 13107200 | bytes 2621440 | tf_op jit(solution)/shard_map/pallas_call | solution.py:162
  138.6 0.0 collective-permute-done.5.second_ref
  138.6 3.3 %shard_map.67 = f32[2,8,512]{2,1,0:T(8,128)} custom-call(bf16[2,160,2048]{2,1,0:T(8,128)(2,1)} %shard_map.66.first_ref, bf16[2,160,2048]{2,1,0:T(8,128)(2,1)} %collective-permute-done.5.second_ref), custom_call_target="tpu_custom_call" | custom-call | flops 13107200 | bytes 2621440 | tf_op jit(solution)/shard_map/pallas_call | solution.py:162
  141.9 7.5 %collective-permute-done.7.second_ref = bf16[2,160,2048]{2,1,0:T(8,128)(2,1)} collective-permute-done((bf16[2,160,2048]{2,1,0:T(8,128)(2,1)}, bf16[2,160,2048]{2,1,0:T(8,128)(2,1)}, u32[]{:S(2)}, u32[]{:S(2)}) %collective-permute-start.7) | collective-permute-done | bytes 1310752 | tf_op jit(solution)/shard_map/ppermute | solution.py:39
  149.4 3.3 %shard_map.69 = f32[2,8,512]{2,1,0:T(8,128)} custom-call(bf16[2,160,2048]{2,1,0:T(8,128)(2,1)} %shard_map.64.first_ref, bf16[2,160,2048]{2,1,0:T(8,128)(2,1)} %collective-permute-done.7.second_ref), custom_call_target="tpu_custom_call" | custom-call | flops 13107200 | bytes 2621440 | tf_op jit(solution)/shard_map/pallas_call | solution.py:162
  152.7 0.0 copy-start.8
  152.7 0.0 copy-start.13
  152.8 7.5 %collective-permute-done.9.second_ref = bf16[2,160,2048]{2,1,0:T(8,128)(2,1)S(1)} collective-permute-done((bf16[2,160,2048]{2,1,0:T(8,128)(2,1)}, bf16[2,160,2048]{2,1,0:T(8,128)(2,1)S(1)}, u32[]{:S(2)}, u32[]{:S(2)}) %collective-permute-start.9) | collective-permute-done | bytes 1310752 | tf_op jit(solution)/shard_map/ppermute | solution.py:39
  160.2 1.1 copy-done.4
  161.3 3.3 %shard_map.71 = f32[2,8,512]{2,1,0:T(8,128)} custom-call(bf16[2,160,2048]{2,1,0:T(8,128)(2,1)} %shard_map.66.first_ref, bf16[2,160,2048]{2,1,0:T(8,128)(2,1)} %copy-done.4), custom_call_target="tpu_custom_call" | custom-call | flops 13107200 | bytes 2621440 | tf_op jit(solution)/shard_map/pallas_call | solution.py:162
  164.6 0.0 copy-done.5
  164.7 1.6 select_select_fusion
  166.3 5.6 %all-to-all-start = ((f32[8,2,8,512]{3,2,1,0:T(8,128)}), f32[8,2,8,512]{3,2,1,0:T(8,128)S(1)}, u32[]{:S(2)}, u32[]{:S(2)}) async-start(f32[8,2,8,512]{3,2,1,0:T(8,128)} %select_select_fusion), calls=%async_computation | async-start | bytes 524288 | tf_op jit(solution)/shard_map/all_to_all | solution.py:212
  171.9 0.7 fusion.47
  192.7 0.0 all-to-all-done
  193.0 0.7 maximum_bitcast_fusion
  (41 shorter events, 0.3 us)
Async XLA Ops:
  0.0 15.5 %copy-start.3 = (bf16[1,2,160,4096]{3,2,1,0:T(8,128)(2,1)S(1)}, bf16[1,2,160,4096]{3,2,1,0:T(8,128)(2,1)}, u32[]{:S(2)}) copy-start(bf16[1,2,160,4096]{3,2,1,0:T(8,128)(2,1)} %param.6) | copy-start | bytes 7864324
  1.8 13.7 %collective-permute-start = (bf16[1,2,16,4096]{3,2,1,0:T(8,128)(2,1)}, bf16[1,2,16,4096]{3,2,1,0:T(8,128)(2,1)S(1)}, u32[]{:S(2)}, u32[]{:S(2)}) collective-permute-start(bf16[1,2,16,4096]{3,2,1,0:T(8,128)(2,1)} %slice.131), channel_id=1, source_target_pairs={{0,1},{1,2},{2,3},{4,5},{5,6},{6,7},{8,9},{9,10},{10,11},{12,13},{... | collective-permute-start | bytes 786440 | tf_op jit(solution)/shard_map/ppermute | solution.py:27
  6.1 9.4 %collective-permute-start.1 = (bf16[1,2,25,4096]{3,2,1,0:T(8,128)(2,1)}, bf16[1,2,25,4096]{3,2,1,0:T(8,128)(2,1)S(1)}, u32[]{:S(2)}, u32[]{:S(2)}) collective-permute-start(bf16[1,2,25,4096]{3,2,1,0:T(8,128)(2,1)} %slice.132), channel_id=1, source_target_pairs={{1,0},{2,1},{3,2},{5,4},{6,5},{7,6},{9,8},{10,9},{11,10},{13,12},{... | collective-permute-start | bytes 1228808 | tf_op jit(solution)/shard_map/ppermute | solution.py:29
  35.2 31.8 %copy-start.1 = (bf16[2,160,2048]{2,1,0:T(8,128)(2,1)S(1)}, bf16[2,160,2048]{2,1,0:T(8,128)(2,1)}, u32[]{:S(2)}) copy-start(bf16[2,160,2048]{2,1,0:T(8,128)(2,1)} %shard_map.64.first_ref) | copy-start | bytes 3932164
  35.2 31.8 %collective-permute-start.2 = (bf16[2,160,2048]{2,1,0:T(8,128)(2,1)}, bf16[2,160,2048]{2,1,0:T(8,128)(2,1)S(1)}, u32[]{:S(2)}, u32[]{:S(2)}) collective-permute-start(bf16[2,160,2048]{2,1,0:T(8,128)(2,1)} %shard_map.64.first_ref), channel_id=1, source_target_pairs={{0,8},{4,12},{8,16},{12,20},{16,24},{20,28},{1,9},{5,13},{9,17},{1... | collective-permute-start | bytes 3932168 | tf_op jit(solution)/shard_map/ppermute | solution.py:39
  55.6 32.0 %collective-permute-start.4 = (bf16[2,160,2048]{2,1,0:T(8,128)(2,1)}, bf16[2,160,2048]{2,1,0:T(8,128)(2,1)}, u32[]{:S(2)}, u32[]{:S(2)}) collective-permute-start(bf16[2,160,2048]{2,1,0:T(8,128)(2,1)} %shard_map.66.first_ref), channel_id=1, source_target_pairs={{8,0},{12,4},{16,8},{20,12},{24,16},{28,20},{9,1},{13,5},{17,9},{2... | collective-permute-start | bytes 3932168 | tf_op jit(solution)/shard_map/ppermute | solution.py:39
  56.9 30.7 %copy-start = (bf16[2,160,2048]{2,1,0:T(8,128)(2,1)S(1)}, bf16[2,160,2048]{2,1,0:T(8,128)(2,1)}, u32[]{:S(2)}) copy-start(bf16[2,160,2048]{2,1,0:T(8,128)(2,1)} %shard_map.66.first_ref) | copy-start | bytes 3932164
  67.0 22.5 %copy-start.2 = (bf16[2,160,2048]{2,1,0:T(8,128)(2,1)}, bf16[2,160,2048]{2,1,0:T(8,128)(2,1)S(1)}, u32[]{:S(2)}) copy-start(bf16[2,160,2048]{2,1,0:T(8,128)(2,1)S(1)} %collective-permute-done.2.second_ref) | copy-start | bytes 3932164
  68.3 30.7 %collective-permute-start.6 = (bf16[2,160,2048]{2,1,0:T(8,128)(2,1)}, bf16[2,160,2048]{2,1,0:T(8,128)(2,1)}, u32[]{:S(2)}, u32[]{:S(2)}) collective-permute-start(bf16[2,160,2048]{2,1,0:T(8,128)(2,1)} %broadcast_select_fusion.1), channel_id=1, source_target_pairs={{0,4},{4,0},{8,12},{12,8},{16,20},{20,16},{24,28},{28,24},{1,5},{5... | collective-permute-start | bytes 3932168 | tf_op jit(solution)/shard_map/ppermute | solution.py:44
  89.2 37.9 %collective-permute-start.8 = (bf16[2,160,2048]{2,1,0:T(8,128)(2,1)S(1)}, bf16[2,160,2048]{2,1,0:T(8,128)(2,1)}, u32[]{:S(2)}, u32[]{:S(2)}) collective-permute-start(bf16[2,160,2048]{2,1,0:T(8,128)(2,1)S(1)} %broadcast_select_fusion), channel_id=1, source_target_pairs={{0,4},{4,0},{8,12},{12,8},{16,20},{20,16},{24,28},{28,24},{1,5},{5... | collective-permute-start | bytes 3932168 | tf_op jit(solution)/shard_map/ppermute | solution.py:44
  89.4 45.8 %collective-permute-start.3 = (bf16[2,160,2048]{2,1,0:T(8,128)(2,1)S(1)}, bf16[2,160,2048]{2,1,0:T(8,128)(2,1)}, u32[]{:S(2)}, u32[]{:S(2)}) collective-permute-start(bf16[2,160,2048]{2,1,0:T(8,128)(2,1)S(1)} %collective-permute-done.2.second_ref), channel_id=1, source_target_pairs={{0,8},{4,12},{8,16},{12,20},{16,24},{20,28},{1,9},{5,13},{9,17},{1... | collective-permute-start | bytes 3932168 | tf_op jit(solution)/shard_map/ppermute | solution.py:39
  93.9 44.7 %collective-permute-start.5 = (bf16[2,160,2048]{2,1,0:T(8,128)(2,1)}, bf16[2,160,2048]{2,1,0:T(8,128)(2,1)}, u32[]{:S(2)}, u32[]{:S(2)}) collective-permute-start(bf16[2,160,2048]{2,1,0:T(8,128)(2,1)} %collective-permute-done.4.second_ref), channel_id=1, source_target_pairs={{8,0},{12,4},{16,8},{20,12},{24,16},{28,20},{9,1},{13,5},{17,9},{2... | collective-permute-start | bytes 3932168 | tf_op jit(solution)/shard_map/ppermute | solution.py:39
  99.0 50.4 %collective-permute-start.7 = (bf16[2,160,2048]{2,1,0:T(8,128)(2,1)}, bf16[2,160,2048]{2,1,0:T(8,128)(2,1)}, u32[]{:S(2)}, u32[]{:S(2)}) collective-permute-start(bf16[2,160,2048]{2,1,0:T(8,128)(2,1)} %collective-permute-done.6.second_ref), channel_id=1, source_target_pairs={{0,8},{4,12},{8,16},{12,20},{16,24},{20,28},{1,9},{5,13},{9,17},{1... | collective-permute-start | bytes 3932168 | tf_op jit(solution)/shard_map/ppermute | solution.py:39
  127.1 33.2 %collective-permute-start.9 = (bf16[2,160,2048]{2,1,0:T(8,128)(2,1)}, bf16[2,160,2048]{2,1,0:T(8,128)(2,1)S(1)}, u32[]{:S(2)}, u32[]{:S(2)}) collective-permute-start(bf16[2,160,2048]{2,1,0:T(8,128)(2,1)} %collective-permute-done.8.second_ref), channel_id=1, source_target_pairs={{8,0},{12,4},{16,8},{20,12},{24,16},{28,20},{9,1},{13,5},{17,9},{2... | collective-permute-start | bytes 3932168 | tf_op jit(solution)/shard_map/ppermute | solution.py:39
  152.7 11.9 %copy-start.5 = (f32[2,8,512]{2,1,0:T(8,128)S(1)}, f32[2,8,512]{2,1,0:T(8,128)}, u32[]{:S(2)}) copy-start(f32[2,8,512]{2,1,0:T(8,128)} %shard_map.68) | copy-start | bytes 98308
  152.7 11.9 %copy-start.6 = (f32[2,8,512]{2,1,0:T(8,128)S(1)}, f32[2,8,512]{2,1,0:T(8,128)}, u32[]{:S(2)}) copy-start(f32[2,8,512]{2,1,0:T(8,128)} %shard_map.70) | copy-start | bytes 98308
  152.7 11.9 %copy-start.7 = (f32[2,8,512]{2,1,0:T(8,128)S(1)}, f32[2,8,512]{2,1,0:T(8,128)}, u32[]{:S(2)}) copy-start(f32[2,8,512]{2,1,0:T(8,128)} %shard_map.72) | copy-start | bytes 98308
  152.7 11.9 %copy-start.8 = (f32[2,8,512]{2,1,0:T(8,128)S(1)}, f32[2,8,512]{2,1,0:T(8,128)}, u32[]{:S(2)}) copy-start(f32[2,8,512]{2,1,0:T(8,128)} %shard_map.73) | copy-start | bytes 98308
  152.7 11.9 %copy-start.9 = (f32[2,8,512]{2,1,0:T(8,128)S(1)}, f32[2,8,512]{2,1,0:T(8,128)}, u32[]{:S(2)}) copy-start(f32[2,8,512]{2,1,0:T(8,128)} %shard_map.65) | copy-start | bytes 98308
  152.7 11.9 %copy-start.10 = (f32[2,8,512]{2,1,0:T(8,128)S(1)}, f32[2,8,512]{2,1,0:T(8,128)}, u32[]{:S(2)}) copy-start(f32[2,8,512]{2,1,0:T(8,128)} %shard_map.67) | copy-start | bytes 98308
  152.7 11.9 %copy-start.11 = (f32[2,8,512]{2,1,0:T(8,128)S(1)}, f32[2,8,512]{2,1,0:T(8,128)}, u32[]{:S(2)}) copy-start(f32[2,8,512]{2,1,0:T(8,128)} %shard_map.69) | copy-start | bytes 98308
  152.7 19.1 %copy-start.13 = (s32[1,4]{1,0:T(1,128)S(1)}, s32[1,4]{1,0:T(1,128)}, u32[]{:S(2)}) copy-start(s32[1,4]{1,0:T(1,128)} %param.11) | copy-start | bytes 52
  160.2 1.1 copy-start.4
  164.6 28.2 %copy-start.12 = (f32[2,8,512]{2,1,0:T(8,128)S(1)}, f32[2,8,512]{2,1,0:T(8,128)}, u32[]{:S(2)}) copy-start(f32[2,8,512]{2,1,0:T(8,128)} %shard_map.71) | copy-start | bytes 98308
  166.3 26.4 %all-to-all-start = ((f32[8,2,8,512]{3,2,1,0:T(8,128)}), f32[8,2,8,512]{3,2,1,0:T(8,128)S(1)}, u32[]{:S(2)}, u32[]{:S(2)}) async-start(f32[8,2,8,512]{3,2,1,0:T(8,128)} %select_select_fusion), calls=%async_computation | async-start | bytes 524288 | tf_op jit(solution)/shard_map/all_to_all | solution.py:212

commit v22 on v21

--- a/solution.py
+++ b/solution.py
@@ -128,7 +128,7 @@
 CHUNK = 512
 
 
-BLOCK = 1024
+BLOCK = 2048
 
 
 def looks_kernel(first_ref, second_ref, out_ref):

time: 195 us -> 195 us (level)
  transfers between devices with their start and end apart: 11 -> 11, of which waited for: 6 -> 6; matrix products, arithmetic and copies ran while one was open for 6% -> 6% of each run, Pallas kernels for 20% -> 21%
where the time goes in v22:
time: 195 us; the launch traced here: 194 us
  waiting for transfers between devices  61.6 us (32%)
  Pallas kernels  59.3 us (30%)
  starting transfers between devices  29.6 us (15%)
  between operations  21.8 us (11%)
  other arithmetic  12.2 us (6%)
  local copies, waits for them, and re-layouts  9.45 us (5%)
    ppermute x6, waiting for transfers between devices, shifted(): return lax.ppermute(block, axis, route)  42 us
    pallas_call x2, Pallas kernels, resample_half(): pl.pallas_call(functools.partial(resample_kernel, side), grid=(2, nlines...  31.5 us
    pallas_call x8, Pallas kernels, looks(): pl.pallas_call(looks_kernel, grid=(width // BLOCK,), in_specs=[spec, spec...  27.8 us
    ppermute x2, waiting for transfers between devices, swapped(): return lax.ppermute(block, axis, [(i, i ^ 1) for i in range(count)])  19.6 us
    ppermute x6, starting transfers between devices, shifted(): return lax.ppermute(block, axis, route)  18.6 us
    all_to_all x1, starting transfers between devices, shards(): got = lax.all_to_all(sent, 'date', 0, 0, tiled=True)  5.58 us
    dynamic_slice x1, other arithmetic, resample_block(): window = lax.dynamic_slice_in_dim(padded, start, nlines + 16, 1)  3.94 us
  transfers between devices with their start and end apart: 11, of which 6 were waited for; matrix products, arithmetic and copies ran while one was open for 6% of the time, Pallas kernels for 21%

profile of v22, /device:TPU:0, one launch (start us, length us, event | category | flops | bytes accessed | tf_op | source)
XLA Modules:
  0.0 193.9 jit_solution(6783747798646438808)
XLA Ops:
  0.0 1.8 slice.131
  1.8 2.4 %collective-permute-start = (bf16[1,2,16,4096]{3,2,1,0:T(8,128)(2,1)}, bf16[1,2,16,4096]{3,2,1,0:T(8,128)(2,1)S(1)}, u32[]{:S(2)}, u32[]{:S(2)}) collective-permute-start(bf16[1,2,16,4096]{3,2,1,0:T(8,128)(2,1)} %slice.131), channel_id=1, source_target_pairs={{0,1},{1,2},{2,3},{4,5},{5,6},{6,7},{8,9},{9,10},{10,11},{12,13},{... | collective-permute-start | bytes 786440 | tf_op jit(solution)/shard_map/ppermute | solution.py:27
  4.2 1.9 slice.132
  6.1 1.3 collective-permute-start.1
  7.4 0.7 compare_select_fusion.1
  8.1 0.5 broadcast.448
  8.6 1.3 reduce.9
  9.9 0.1 squeeze.28
  10.0 0.1 fusion.17
  10.1 0.7 add_reduce_fusion
  12.1 0.1 copy.21
  12.2 0.8 fusion.14.weights_ref
  13.0 0.1 add.231
  13.1 0.1 copy.24
  13.2 0.7 gather_fusion
  13.8 0.1 copy.22
  13.9 0.1 gather.7
  14.0 0.8 copy.23
  14.8 0.7 reshape.1168.shift_ref
  15.5 0.0 collective-permute-done
  15.5 0.0 collective-permute-done.1
  15.5 0.0 copy-done.3
  15.5 3.9 %fusion.2.window_ref = bf16[2,176,4096]{2,1,0:T(8,128)(2,1)} fusion(s32[]{:T(128)S(6)} %select_n.546, bf16[1,2,16,4096]{3,2,1,0:T(8,128)(2,1)S(1)} %collective-permute-done, bf16[1,2,160,4096]{3,2,1,0:T(8,128)(2,1)S(1)} %copy-done.3, bf16[1,2,25,4096]{3,2,1,0:T(8,128)(2,1)S(1)} %collective-permute-done.1), kind=kLoop, calls=%fused_computation.6 | loop fusion | flops 8650752 | bytes 6176772 | tf_op jit(solution)/shard_map/dynamic_slice | solution.py:114
  19.4 15.7 %shard_map.64.first_ref = bf16[2,160,2048]{2,1,0:T(8,128)(2,1)} custom-call(f32[8]{0:T(128)} %fusion.14.weights_ref, bf16[2,176,4096]{2,1,0:T(8,128)(2,1)} %fusion.2.window_ref, f32[160,8]{1,0:T(8,128)} %bitcast.113, s32[160,1]{1,0:T(8,128)} %reshape.1168.shift_ref), custom_call_target="tpu_custom_call" | custom-call | flops 39321600 | bytes 3932160 | tf_op jit(solution)/shard_map/pallas_call | solution.py:92
  35.2 4.7 %collective-permute-start.2 = (bf16[2,160,2048]{2,1,0:T(8,128)(2,1)}, bf16[2,160,2048]{2,1,0:T(8,128)(2,1)S(1)}, u32[]{:S(2)}, u32[]{:S(2)}) collective-permute-start(bf16[2,160,2048]{2,1,0:T(8,128)(2,1)} %shard_map.64.first_ref), channel_id=1, source_target_pairs={{0,8},{4,12},{8,16},{12,20},{16,24},{20,28},{1,9},{5,13},{9,17},{1... | collective-permute-start | bytes 3932168 | tf_op jit(solution)/shard_map/ppermute | solution.py:39
  39.9 15.8 %shard_map.66.first_ref = bf16[2,160,2048]{2,1,0:T(8,128)(2,1)} custom-call(f32[8]{0:T(128)} %fusion.14.weights_ref, bf16[2,176,4096]{2,1,0:T(8,128)(2,1)} %fusion.2.window_ref, f32[160,8]{1,0:T(8,128)} %bitcast.114, s32[160,1]{1,0:T(8,128)} %reshape.1168.shift_ref), custom_call_target="tpu_custom_call" | custom-call | flops 39321600 | bytes 3932160 | tf_op jit(solution)/shard_map/pallas_call | solution.py:92
  55.6 1.3 collective-permute-start.4
  56.9 0.0 copy-start
  57.0 10.0 %collective-permute-done.2.second_ref = bf16[2,160,2048]{2,1,0:T(8,128)(2,1)S(1)} collective-permute-done((bf16[2,160,2048]{2,1,0:T(8,128)(2,1)}, bf16[2,160,2048]{2,1,0:T(8,128)(2,1)S(1)}, u32[]{:S(2)}, u32[]{:S(2)}) %collective-permute-start.2) | collective-permute-done | bytes 1310752 | tf_op jit(solution)/shard_map/ppermute | solution.py:39
  67.0 0.0 copy-done.1
  67.0 1.3 broadcast_select_fusion.1
  68.3 1.5 collective-permute-start.6
  69.8 17.8 %collective-permute-done.4.second_ref = bf16[2,160,2048]{2,1,0:T(8,128)(2,1)} collective-permute-done((bf16[2,160,2048]{2,1,0:T(8,128)(2,1)}, bf16[2,160,2048]{2,1,0:T(8,128)(2,1)}, u32[]{:S(2)}, u32[]{:S(2)}) %collective-permute-start.4) | collective-permute-done | bytes 1310752 | tf_op jit(solution)/shard_map/ppermute | solution.py:39
  87.7 0.0 copy-done
  87.7 1.5 broadcast_select_fusion
  89.2 0.3 collective-permute-start.8
  89.4 0.0 copy-done.2
  89.4 4.5 %collective-permute-start.3 = (bf16[2,160,2048]{2,1,0:T(8,128)(2,1)S(1)}, bf16[2,160,2048]{2,1,0:T(8,128)(2,1)}, u32[]{:S(2)}, u32[]{:S(2)}) collective-permute-start(bf16[2,160,2048]{2,1,0:T(8,128)(2,1)S(1)} %collective-permute-done.2.second_ref), channel_id=1, source_target_pairs={{0,8},{4,12},{8,16},{12,20},{16,24},{20,28},{1,9},{5,13},{9,17},{1... | collective-permute-start | bytes 3932168 | tf_op jit(solution)/shard_map/ppermute | solution.py:39
  93.9 1.3 collective-permute-start.5
  95.2 3.5 %shard_map.68 = f32[2,8,512]{2,1,0:T(8,128)} custom-call(bf16[2,160,2048]{2,1,0:T(8,128)(2,1)} %shard_map.64.first_ref, bf16[2,160,2048]{2,1,0:T(8,128)(2,1)} %copy-done.2), custom_call_target="tpu_custom_call" | custom-call | flops 13107200 | bytes 2621440 | tf_op jit(solution)/shard_map/pallas_call | solution.py:162
  98.7 0.3 collective-permute-done.6.second_ref
  99.0 5.3 %collective-permute-start.7 = (bf16[2,160,2048]{2,1,0:T(8,128)(2,1)}, bf16[2,160,2048]{2,1,0:T(8,128)(2,1)}, u32[]{:S(2)}, u32[]{:S(2)}) collective-permute-start(bf16[2,160,2048]{2,1,0:T(8,128)(2,1)} %collective-permute-done.6.second_ref), channel_id=1, source_target_pairs={{0,8},{4,12},{8,16},{12,20},{16,24},{20,28},{1,9},{5,13},{9,17},{1... | collective-permute-start | bytes 3932168 | tf_op jit(solution)/shard_map/ppermute | solution.py:39
  104.3 3.5 %shard_map.70 = f32[2,8,512]{2,1,0:T(8,128)} custom-call(bf16[2,160,2048]{2,1,0:T(8,128)(2,1)} %shard_map.66.first_ref, bf16[2,160,2048]{2,1,0:T(8,128)(2,1)} %collective-permute-done.4.second_ref), custom_call_target="tpu_custom_call" | custom-call | flops 13107200 | bytes 2621440 | tf_op jit(solution)/shard_map/pallas_call | solution.py:162
  107.8 19.3 %collective-permute-done.8.second_ref = bf16[2,160,2048]{2,1,0:T(8,128)(2,1)} collective-permute-done((bf16[2,160,2048]{2,1,0:T(8,128)(2,1)S(1)}, bf16[2,160,2048]{2,1,0:T(8,128)(2,1)}, u32[]{:S(2)}, u32[]{:S(2)}) %collective-permute-start.8) | collective-permute-done | bytes 1310752 | tf_op jit(solution)/shard_map/ppermute | solution.py:44
  127.1 1.5 collective-permute-start.9
  128.6 3.5 %shard_map.72 = f32[2,8,512]{2,1,0:T(8,128)} custom-call(bf16[2,160,2048]{2,1,0:T(8,128)(2,1)} %shard_map.64.first_ref, bf16[2,160,2048]{2,1,0:T(8,128)(2,1)} %collective-permute-done.6.second_ref), custom_call_target="tpu_custom_call" | custom-call | flops 13107200 | bytes 2621440 | tf_op jit(solution)/shard_map/pallas_call | solution.py:162
  132.1 3.5 %shard_map.73 = f32[2,8,512]{2,1,0:T(8,128)} custom-call(bf16[2,160,2048]{2,1,0:T(8,128)(2,1)} %shard_map.66.first_ref, bf16[2,160,2048]{2,1,0:T(8,128)(2,1)} %collective-permute-done.8.second_ref), custom_call_target="tpu_custom_call" | custom-call | flops 13107200 | bytes 2621440 | tf_op jit(solution)/shard_map/pallas_call | solution.py:162
  135.6 0.0 collective-permute-done.3.second_ref
  135.6 3.5 %shard_map.65 = f32[2,8,512]{2,1,0:T(8,128)} custom-call(bf16[2,160,2048]{2,1,0:T(8,128)(2,1)} %shard_map.64.first_ref, bf16[2,160,2048]{2,1,0:T(8,128)(2,1)} %collective-permute-done.3.second_ref), custom_call_target="tpu_custom_call" | custom-call | flops 13107200 | bytes 2621440 | tf_op jit(solution)/shard_map/pallas_call | solution.py:162
  139.1 0.0 collective-permute-done.5.second_ref
  139.1 3.5 %shard_map.67 = f32[2,8,512]{2,1,0:T(8,128)} custom-call(bf16[2,160,2048]{2,1,0:T(8,128)(2,1)} %shard_map.66.first_ref, bf16[2,160,2048]{2,1,0:T(8,128)(2,1)} %collective-permute-done.5.second_ref), custom_call_target="tpu_custom_call" | custom-call | flops 13107200 | bytes 2621440 | tf_op jit(solution)/shard_map/pallas_call | solution.py:162
  142.6 6.8 %collective-permute-done.7.second_ref = bf16[2,160,2048]{2,1,0:T(8,128)(2,1)} collective-permute-done((bf16[2,160,2048]{2,1,0:T(8,128)(2,1)}, bf16[2,160,2048]{2,1,0:T(8,128)(2,1)}, u32[]{:S(2)}, u32[]{:S(2)}) %collective-permute-start.7) | collective-permute-done | bytes 1310752 | tf_op jit(solution)/shard_map/ppermute | solution.py:39
  149.4 3.5 %shard_map.69 = f32[2,8,512]{2,1,0:T(8,128)} custom-call(bf16[2,160,2048]{2,1,0:T(8,128)(2,1)} %shard_map.64.first_ref, bf16[2,160,2048]{2,1,0:T(8,128)(2,1)} %collective-permute-done.7.second_ref), custom_call_target="tpu_custom_call" | custom-call | flops 13107200 | bytes 2621440 | tf_op jit(solution)/shard_map/pallas_call | solution.py:162
  152.9 0.0 copy-start.9
  152.9 0.0 copy-start.13
  152.9 7.3 %collective-permute-done.9.second_ref = bf16[2,160,2048]{2,1,0:T(8,128)(2,1)S(1)} collective-permute-done((bf16[2,160,2048]{2,1,0:T(8,128)(2,1)}, bf16[2,160,2048]{2,1,0:T(8,128)(2,1)S(1)}, u32[]{:S(2)}, u32[]{:S(2)}) %collective-permute-start.9) | collective-permute-done | bytes 1310752 | tf_op jit(solution)/shard_map/ppermute | solution.py:39
  160.2 1.1 copy-done.4
  161.3 3.5 %shard_map.71 = f32[2,8,512]{2,1,0:T(8,128)} custom-call(bf16[2,160,2048]{2,1,0:T(8,128)(2,1)} %shard_map.66.first_ref, bf16[2,160,2048]{2,1,0:T(8,128)(2,1)} %copy-done.4), custom_call_target="tpu_custom_call" | custom-call | flops 13107200 | bytes 2621440 | tf_op jit(solution)/shard_map/pallas_call | solution.py:162
  164.8 0.0 copy-done.5
  164.8 1.6 select_select_fusion
  166.5 5.6 %all-to-all-start = ((f32[8,2,8,512]{3,2,1,0:T(8,128)}), f32[8,2,8,512]{3,2,1,0:T(8,128)S(1)}, u32[]{:S(2)}, u32[]{:S(2)}) async-start(f32[8,2,8,512]{3,2,1,0:T(8,128)} %select_select_fusion), calls=%async_computation | async-start | bytes 524288 | tf_op jit(solution)/shard_map/all_to_all | solution.py:212
  172.1 0.7 fusion.47
  192.8 0.0 all-to-all-done
  193.2 0.7 maximum_bitcast_fusion
  (41 shorter events, 0.3 us)
Async XLA Ops:
  0.0 15.5 %copy-start.3 = (bf16[1,2,160,4096]{3,2,1,0:T(8,128)(2,1)S(1)}, bf16[1,2,160,4096]{3,2,1,0:T(8,128)(2,1)}, u32[]{:S(2)}) copy-start(bf16[1,2,160,4096]{3,2,1,0:T(8,128)(2,1)} %param.6) | copy-start | bytes 7864324
  1.8 13.7 %collective-permute-start = (bf16[1,2,16,4096]{3,2,1,0:T(8,128)(2,1)}, bf16[1,2,16,4096]{3,2,1,0:T(8,128)(2,1)S(1)}, u32[]{:S(2)}, u32[]{:S(2)}) collective-permute-start(bf16[1,2,16,4096]{3,2,1,0:T(8,128)(2,1)} %slice.131), channel_id=1, source_target_pairs={{0,1},{1,2},{2,3},{4,5},{5,6},{6,7},{8,9},{9,10},{10,11},{12,13},{... | collective-permute-start | bytes 786440 | tf_op jit(solution)/shard_map/ppermute | solution.py:27
  6.1 9.4 %collective-permute-start.1 = (bf16[1,2,25,4096]{3,2,1,0:T(8,128)(2,1)}, bf16[1,2,25,4096]{3,2,1,0:T(8,128)(2,1)S(1)}, u32[]{:S(2)}, u32[]{:S(2)}) collective-permute-start(bf16[1,2,25,4096]{3,2,1,0:T(8,128)(2,1)} %slice.132), channel_id=1, source_target_pairs={{1,0},{2,1},{3,2},{5,4},{6,5},{7,6},{9,8},{10,9},{11,10},{13,12},{... | collective-permute-start | bytes 1228808 | tf_op jit(solution)/shard_map/ppermute | solution.py:29
  35.2 31.8 %copy-start.1 = (bf16[2,160,2048]{2,1,0:T(8,128)(2,1)S(1)}, bf16[2,160,2048]{2,1,0:T(8,128)(2,1)}, u32[]{:S(2)}) copy-start(bf16[2,160,2048]{2,1,0:T(8,128)(2,1)} %shard_map.64.first_ref) | copy-start | bytes 3932164
  35.2 31.8 %collective-permute-start.2 = (bf16[2,160,2048]{2,1,0:T(8,128)(2,1)}, bf16[2,160,2048]{2,1,0:T(8,128)(2,1)S(1)}, u32[]{:S(2)}, u32[]{:S(2)}) collective-permute-start(bf16[2,160,2048]{2,1,0:T(8,128)(2,1)} %shard_map.64.first_ref), channel_id=1, source_target_pairs={{0,8},{4,12},{8,16},{12,20},{16,24},{20,28},{1,9},{5,13},{9,17},{1... | collective-permute-start | bytes 3932168 | tf_op jit(solution)/shard_map/ppermute | solution.py:39
  55.6 32.0 %collective-permute-start.4 = (bf16[2,160,2048]{2,1,0:T(8,128)(2,1)}, bf16[2,160,2048]{2,1,0:T(8,128)(2,1)}, u32[]{:S(2)}, u32[]{:S(2)}) collective-permute-start(bf16[2,160,2048]{2,1,0:T(8,128)(2,1)} %shard_map.66.first_ref), channel_id=1, source_target_pairs={{8,0},{12,4},{16,8},{20,12},{24,16},{28,20},{9,1},{13,5},{17,9},{2... | collective-permute-start | bytes 3932168 | tf_op jit(solution)/shard_map/ppermute | solution.py:39
  56.9 30.7 %copy-start = (bf16[2,160,2048]{2,1,0:T(8,128)(2,1)S(1)}, bf16[2,160,2048]{2,1,0:T(8,128)(2,1)}, u32[]{:S(2)}) copy-start(bf16[2,160,2048]{2,1,0:T(8,128)(2,1)} %shard_map.66.first_ref) | copy-start | bytes 3932164
  67.0 22.5 %copy-start.2 = (bf16[2,160,2048]{2,1,0:T(8,128)(2,1)}, bf16[2,160,2048]{2,1,0:T(8,128)(2,1)S(1)}, u32[]{:S(2)}) copy-start(bf16[2,160,2048]{2,1,0:T(8,128)(2,1)S(1)} %collective-permute-done.2.second_ref) | copy-start | bytes 3932164
  68.3 30.7 %collective-permute-start.6 = (bf16[2,160,2048]{2,1,0:T(8,128)(2,1)}, bf16[2,160,2048]{2,1,0:T(8,128)(2,1)}, u32[]{:S(2)}, u32[]{:S(2)}) collective-permute-start(bf16[2,160,2048]{2,1,0:T(8,128)(2,1)} %broadcast_select_fusion.1), channel_id=1, source_target_pairs={{0,4},{4,0},{8,12},{12,8},{16,20},{20,16},{24,28},{28,24},{1,5},{5... | collective-permute-start | bytes 3932168 | tf_op jit(solution)/shard_map/ppermute | solution.py:44
  89.2 37.9 %collective-permute-start.8 = (bf16[2,160,2048]{2,1,0:T(8,128)(2,1)S(1)}, bf16[2,160,2048]{2,1,0:T(8,128)(2,1)}, u32[]{:S(2)}, u32[]{:S(2)}) collective-permute-start(bf16[2,160,2048]{2,1,0:T(8,128)(2,1)S(1)} %broadcast_select_fusion), channel_id=1, source_target_pairs={{0,4},{4,0},{8,12},{12,8},{16,20},{20,16},{24,28},{28,24},{1,5},{5... | collective-permute-start | bytes 3932168 | tf_op jit(solution)/shard_map/ppermute | solution.py:44
  89.4 46.2 %collective-permute-start.3 = (bf16[2,160,2048]{2,1,0:T(8,128)(2,1)S(1)}, bf16[2,160,2048]{2,1,0:T(8,128)(2,1)}, u32[]{:S(2)}, u32[]{:S(2)}) collective-permute-start(bf16[2,160,2048]{2,1,0:T(8,128)(2,1)S(1)} %collective-permute-done.2.second_ref), channel_id=1, source_target_pairs={{0,8},{4,12},{8,16},{12,20},{16,24},{20,28},{1,9},{5,13},{9,17},{1... | collective-permute-start | bytes 3932168 | tf_op jit(solution)/shard_map/ppermute | solution.py:39
  93.9 45.2 %collective-permute-start.5 = (bf16[2,160,2048]{2,1,0:T(8,128)(2,1)}, bf16[2,160,2048]{2,1,0:T(8,128)(2,1)}, u32[]{:S(2)}, u32[]{:S(2)}) collective-permute-start(bf16[2,160,2048]{2,1,0:T(8,128)(2,1)} %collective-permute-done.4.second_ref), channel_id=1, source_target_pairs={{8,0},{12,4},{16,8},{20,12},{24,16},{28,20},{9,1},{13,5},{17,9},{2... | collective-permute-start | bytes 3932168 | tf_op jit(solution)/shard_map/ppermute | solution.py:39
  99.0 50.4 %collective-permute-start.7 = (bf16[2,160,2048]{2,1,0:T(8,128)(2,1)}, bf16[2,160,2048]{2,1,0:T(8,128)(2,1)}, u32[]{:S(2)}, u32[]{:S(2)}) collective-permute-start(bf16[2,160,2048]{2,1,0:T(8,128)(2,1)} %collective-permute-done.6.second_ref), channel_id=1, source_target_pairs={{0,8},{4,12},{8,16},{12,20},{16,24},{20,28},{1,9},{5,13},{9,17},{1... | collective-permute-start | bytes 3932168 | tf_op jit(solution)/shard_map/ppermute | solution.py:39
  127.1 33.2 %collective-permute-start.9 = (bf16[2,160,2048]{2,1,0:T(8,128)(2,1)}, bf16[2,160,2048]{2,1,0:T(8,128)(2,1)S(1)}, u32[]{:S(2)}, u32[]{:S(2)}) collective-permute-start(bf16[2,160,2048]{2,1,0:T(8,128)(2,1)} %collective-permute-done.8.second_ref), channel_id=1, source_target_pairs={{8,0},{12,4},{16,8},{20,12},{24,16},{28,20},{9,1},{13,5},{17,9},{2... | collective-permute-start | bytes 3932168 | tf_op jit(solution)/shard_map/ppermute | solution.py:39
  152.9 11.9 %copy-start.5 = (f32[2,8,512]{2,1,0:T(8,128)S(1)}, f32[2,8,512]{2,1,0:T(8,128)}, u32[]{:S(2)}) copy-start(f32[2,8,512]{2,1,0:T(8,128)} %shard_map.68) | copy-start | bytes 98308
  152.9 11.9 %copy-start.6 = (f32[2,8,512]{2,1,0:T(8,128)S(1)}, f32[2,8,512]{2,1,0:T(8,128)}, u32[]{:S(2)}) copy-start(f32[2,8,512]{2,1,0:T(8,128)} %shard_map.70) | copy-start | bytes 98308
  152.9 11.9 %copy-start.7 = (f32[2,8,512]{2,1,0:T(8,128)S(1)}, f32[2,8,512]{2,1,0:T(8,128)}, u32[]{:S(2)}) copy-start(f32[2,8,512]{2,1,0:T(8,128)} %shard_map.72) | copy-start | bytes 98308
  152.9 11.9 %copy-start.8 = (f32[2,8,512]{2,1,0:T(8,128)S(1)}, f32[2,8,512]{2,1,0:T(8,128)}, u32[]{:S(2)}) copy-start(f32[2,8,512]{2,1,0:T(8,128)} %shard_map.73) | copy-start | bytes 98308
  152.9 11.9 %copy-start.9 = (f32[2,8,512]{2,1,0:T(8,128)S(1)}, f32[2,8,512]{2,1,0:T(8,128)}, u32[]{:S(2)}) copy-start(f32[2,8,512]{2,1,0:T(8,128)} %shard_map.65) | copy-start | bytes 98308
  152.9 11.9 %copy-start.10 = (f32[2,8,512]{2,1,0:T(8,128)S(1)}, f32[2,8,512]{2,1,0:T(8,128)}, u32[]{:S(2)}) copy-start(f32[2,8,512]{2,1,0:T(8,128)} %shard_map.67) | copy-start | bytes 98308
  152.9 11.9 %copy-start.11 = (f32[2,8,512]{2,1,0:T(8,128)S(1)}, f32[2,8,512]{2,1,0:T(8,128)}, u32[]{:S(2)}) copy-start(f32[2,8,512]{2,1,0:T(8,128)} %shard_map.69) | copy-start | bytes 98308
  152.9 19.1 %copy-start.13 = (s32[1,4]{1,0:T(1,128)S(1)}, s32[1,4]{1,0:T(1,128)}, u32[]{:S(2)}) copy-start(s32[1,4]{1,0:T(1,128)} %param.11) | copy-start | bytes 52
  160.2 1.1 copy-start.4
  164.8 28.2 %copy-start.12 = (f32[2,8,512]{2,1,0:T(8,128)S(1)}, f32[2,8,512]{2,1,0:T(8,128)}, u32[]{:S(2)}) copy-start(f32[2,8,512]{2,1,0:T(8,128)} %shard_map.71) | copy-start | bytes 98308
  166.5 26.4 %all-to-all-start = ((f32[8,2,8,512]{3,2,1,0:T(8,128)}), f32[8,2,8,512]{3,2,1,0:T(8,128)S(1)}, u32[]{:S(2)}, u32[]{:S(2)}) async-start(f32[8,2,8,512]{3,2,1,0:T(8,128)} %select_select_fusion), calls=%async_computation | async-start | bytes 524288 | tf_op jit(solution)/shard_map/all_to_all | solution.py:212

commit v23 on v21

--- a/solution.py
+++ b/solution.py
@@ -69,7 +69,7 @@
     taps = jnp.zeros((ROWS, window.shape[0]), jnp.float32)
     for tap in range(8):
         taps = jnp.where(offset == tap, weights_ref[tap], taps)
-    along = jnp.dot(taps, window, precision=lax.Precision.HIGHEST, preferred_element_type=jnp.float32)
+    along = jnp.dot(taps, window, precision=lax.Precision.HIGH, preferred_element_type=jnp.float32)
     zeros = jnp.zeros((ROWS, EDGE), jnp.float32)
     row = jnp.concatenate([zeros, along] if side == 0 else [along, zeros], axis=1)
     width = row.shape[1]

time: 195 us -> 195 us (level)
  no operation moved by 1% of the time
where the time goes in v23:
time: 195 us; the launch traced here: 193 us
  waiting for transfers between devices  63.1 us (32%)
  Pallas kernels  57.5 us (29%)
  starting transfers between devices  29.5 us (15%)
  between operations  21.8 us (11%)
  other arithmetic  12.2 us (6%)
  local copies, waits for them, and re-layouts  9.46 us (5%)
    ppermute x6, waiting for transfers between devices, shifted(): return lax.ppermute(block, axis, route)  42.8 us
    pallas_call x2, Pallas kernels, resample_half(): pl.pallas_call(functools.partial(resample_kernel, side), grid=(2, nlines...  31 us
    pallas_call x8, Pallas kernels, looks(): pl.pallas_call(looks_kernel, grid=(width // BLOCK,), in_specs=[spec, spec...  26.5 us
    ppermute x2, waiting for transfers between devices, swapped(): return lax.ppermute(block, axis, [(i, i ^ 1) for i in range(count)])  20.3 us
    ppermute x6, starting transfers between devices, shifted(): return lax.ppermute(block, axis, route)  18.5 us
    all_to_all x1, starting transfers between devices, shards(): got = lax.all_to_all(sent, 'date', 0, 0, tiled=True)  5.58 us
    dynamic_slice x1, other arithmetic, resample_block(): window = lax.dynamic_slice_in_dim(padded, start, nlines + 16, 1)  3.94 us
  transfers between devices with their start and end apart: 11, of which 6 were waited for; matrix products, arithmetic and copies ran while one was open for 6% of the time, Pallas kernels for 20%

profile of v23, /device:TPU:0, one launch (start us, length us, event | category | flops | bytes accessed | tf_op | source)
XLA Modules:
  0.0 193.5 jit_solution(12154037749948576327)
XLA Ops:
  0.0 1.8 slice.131
  1.8 2.4 %collective-permute-start = (bf16[1,2,16,4096]{3,2,1,0:T(8,128)(2,1)}, bf16[1,2,16,4096]{3,2,1,0:T(8,128)(2,1)S(1)}, u32[]{:S(2)}, u32[]{:S(2)}) collective-permute-start(bf16[1,2,16,4096]{3,2,1,0:T(8,128)(2,1)} %slice.131), channel_id=1, source_target_pairs={{0,1},{1,2},{2,3},{4,5},{5,6},{6,7},{8,9},{9,10},{10,11},{12,13},{... | collective-permute-start | bytes 786440 | tf_op jit(solution)/shard_map/ppermute | solution.py:27
  4.2 1.9 slice.132
  6.1 1.3 collective-permute-start.1
  7.4 0.7 compare_select_fusion.1
  8.1 0.5 broadcast.448
  8.6 1.3 reduce.9
  9.9 0.1 squeeze.28
  10.0 0.1 fusion.17
  10.1 0.7 add_reduce_fusion
  12.1 0.1 copy.21
  12.2 0.8 fusion.14.weights_ref
  13.0 0.1 add.231
  13.1 0.1 copy.24
  13.2 0.7 gather_fusion
  13.8 0.1 copy.22
  13.9 0.1 gather.7
  14.0 0.8 copy.23
  14.8 0.7 reshape.1168.shift_ref
  15.5 0.0 collective-permute-done
  15.5 0.0 collective-permute-done.1
  15.5 0.0 copy-done.3
  15.5 3.9 %fusion.2.window_ref = bf16[2,176,4096]{2,1,0:T(8,128)(2,1)} fusion(s32[]{:T(128)S(6)} %select_n.546, bf16[1,2,16,4096]{3,2,1,0:T(8,128)(2,1)S(1)} %collective-permute-done, bf16[1,2,160,4096]{3,2,1,0:T(8,128)(2,1)S(1)} %copy-done.3, bf16[1,2,25,4096]{3,2,1,0:T(8,128)(2,1)S(1)} %collective-permute-done.1), kind=kLoop, calls=%fused_computation.6 | loop fusion | flops 8650752 | bytes 6176772 | tf_op jit(solution)/shard_map/dynamic_slice | solution.py:114
  19.4 15.5 %shard_map.64.first_ref = bf16[2,160,2048]{2,1,0:T(8,128)(2,1)} custom-call(f32[8]{0:T(128)} %fusion.14.weights_ref, bf16[2,176,4096]{2,1,0:T(8,128)(2,1)} %fusion.2.window_ref, f32[160,8]{1,0:T(8,128)} %bitcast.113, s32[160,1]{1,0:T(8,128)} %reshape.1168.shift_ref), custom_call_target="tpu_custom_call" | custom-call | flops 39321600 | bytes 3932160 | tf_op jit(solution)/shard_map/pallas_call | solution.py:92
  34.9 4.7 %collective-permute-start.2 = (bf16[2,160,2048]{2,1,0:T(8,128)(2,1)}, bf16[2,160,2048]{2,1,0:T(8,128)(2,1)S(1)}, u32[]{:S(2)}, u32[]{:S(2)}) collective-permute-start(bf16[2,160,2048]{2,1,0:T(8,128)(2,1)} %shard_map.64.first_ref), channel_id=1, source_target_pairs={{0,8},{4,12},{8,16},{12,20},{16,24},{20,28},{1,9},{5,13},{9,17},{1... | collective-permute-start | bytes 3932168 | tf_op jit(solution)/shard_map/ppermute | solution.py:39
  39.6 15.5 %shard_map.66.first_ref = bf16[2,160,2048]{2,1,0:T(8,128)(2,1)} custom-call(f32[8]{0:T(128)} %fusion.14.weights_ref, bf16[2,176,4096]{2,1,0:T(8,128)(2,1)} %fusion.2.window_ref, f32[160,8]{1,0:T(8,128)} %bitcast.114, s32[160,1]{1,0:T(8,128)} %reshape.1168.shift_ref), custom_call_target="tpu_custom_call" | custom-call | flops 39321600 | bytes 3932160 | tf_op jit(solution)/shard_map/pallas_call | solution.py:92
  55.1 1.3 collective-permute-start.4
  56.5 0.0 copy-start
  56.5 10.3 %collective-permute-done.2.second_ref = bf16[2,160,2048]{2,1,0:T(8,128)(2,1)S(1)} collective-permute-done((bf16[2,160,2048]{2,1,0:T(8,128)(2,1)}, bf16[2,160,2048]{2,1,0:T(8,128)(2,1)S(1)}, u32[]{:S(2)}, u32[]{:S(2)}) %collective-permute-start.2) | collective-permute-done | bytes 1310752 | tf_op jit(solution)/shard_map/ppermute | solution.py:39
  66.7 0.0 copy-done.1
  66.7 1.3 broadcast_select_fusion.1
  68.1 1.5 collective-permute-start.6
  69.6 17.6 %collective-permute-done.4.second_ref = bf16[2,160,2048]{2,1,0:T(8,128)(2,1)} collective-permute-done((bf16[2,160,2048]{2,1,0:T(8,128)(2,1)}, bf16[2,160,2048]{2,1,0:T(8,128)(2,1)}, u32[]{:S(2)}, u32[]{:S(2)}) %collective-permute-start.4) | collective-permute-done | bytes 1310752 | tf_op jit(solution)/shard_map/ppermute | solution.py:39
  87.2 1.5 broadcast_select_fusion
  88.7 0.3 collective-permute-start.8
  88.9 4.5 %collective-permute-start.3 = (bf16[2,160,2048]{2,1,0:T(8,128)(2,1)S(1)}, bf16[2,160,2048]{2,1,0:T(8,128)(2,1)}, u32[]{:S(2)}, u32[]{:S(2)}) collective-permute-start(bf16[2,160,2048]{2,1,0:T(8,128)(2,1)S(1)} %collective-permute-done.2.second_ref), channel_id=1, source_target_pairs={{0,8},{4,12},{8,16},{12,20},{16,24},{20,28},{1,9},{5,13},{9,17},{1... | collective-permute-start | bytes 3932168 | tf_op jit(solution)/shard_map/ppermute | solution.py:39
  93.4 1.3 collective-permute-start.5
  94.7 3.3 %shard_map.68 = f32[2,8,512]{2,1,0:T(8,128)} custom-call(bf16[2,160,2048]{2,1,0:T(8,128)(2,1)} %shard_map.64.first_ref, bf16[2,160,2048]{2,1,0:T(8,128)(2,1)} %copy-done.2), custom_call_target="tpu_custom_call" | custom-call | flops 13107200 | bytes 2621440 | tf_op jit(solution)/shard_map/pallas_call | solution.py:162
  98.0 0.7 collective-permute-done.6.second_ref
  98.7 5.2 %collective-permute-start.7 = (bf16[2,160,2048]{2,1,0:T(8,128)(2,1)}, bf16[2,160,2048]{2,1,0:T(8,128)(2,1)}, u32[]{:S(2)}, u32[]{:S(2)}) collective-permute-start(bf16[2,160,2048]{2,1,0:T(8,128)(2,1)} %collective-permute-done.6.second_ref), channel_id=1, source_target_pairs={{0,8},{4,12},{8,16},{12,20},{16,24},{20,28},{1,9},{5,13},{9,17},{1... | collective-permute-start | bytes 3932168 | tf_op jit(solution)/shard_map/ppermute | solution.py:39
  103.9 3.3 %shard_map.70 = f32[2,8,512]{2,1,0:T(8,128)} custom-call(bf16[2,160,2048]{2,1,0:T(8,128)(2,1)} %shard_map.66.first_ref, bf16[2,160,2048]{2,1,0:T(8,128)(2,1)} %collective-permute-done.4.second_ref), custom_call_target="tpu_custom_call" | custom-call | flops 13107200 | bytes 2621440 | tf_op jit(solution)/shard_map/pallas_call | solution.py:162
  107.2 19.6 %collective-permute-done.8.second_ref = bf16[2,160,2048]{2,1,0:T(8,128)(2,1)} collective-permute-done((bf16[2,160,2048]{2,1,0:T(8,128)(2,1)S(1)}, bf16[2,160,2048]{2,1,0:T(8,128)(2,1)}, u32[]{:S(2)}, u32[]{:S(2)}) %collective-permute-start.8) | collective-permute-done | bytes 1310752 | tf_op jit(solution)/shard_map/ppermute | solution.py:44
  126.8 1.5 collective-permute-start.9
  128.4 3.3 %shard_map.72 = f32[2,8,512]{2,1,0:T(8,128)} custom-call(bf16[2,160,2048]{2,1,0:T(8,128)(2,1)} %shard_map.64.first_ref, bf16[2,160,2048]{2,1,0:T(8,128)(2,1)} %collective-permute-done.6.second_ref), custom_call_target="tpu_custom_call" | custom-call | flops 13107200 | bytes 2621440 | tf_op jit(solution)/shard_map/pallas_call | solution.py:162
  131.7 3.3 %shard_map.73 = f32[2,8,512]{2,1,0:T(8,128)} custom-call(bf16[2,160,2048]{2,1,0:T(8,128)(2,1)} %shard_map.66.first_ref, bf16[2,160,2048]{2,1,0:T(8,128)(2,1)} %collective-permute-done.8.second_ref), custom_call_target="tpu_custom_call" | custom-call | flops 13107200 | bytes 2621440 | tf_op jit(solution)/shard_map/pallas_call | solution.py:162
  135.0 0.0 collective-permute-done.3.second_ref
  135.0 3.3 %shard_map.65 = f32[2,8,512]{2,1,0:T(8,128)} custom-call(bf16[2,160,2048]{2,1,0:T(8,128)(2,1)} %shard_map.64.first_ref, bf16[2,160,2048]{2,1,0:T(8,128)(2,1)} %collective-permute-done.3.second_ref), custom_call_target="tpu_custom_call" | custom-call | flops 13107200 | bytes 2621440 | tf_op jit(solution)/shard_map/pallas_call | solution.py:162
  138.3 0.0 collective-permute-done.5.second_ref
  138.3 3.3 %shard_map.67 = f32[2,8,512]{2,1,0:T(8,128)} custom-call(bf16[2,160,2048]{2,1,0:T(8,128)(2,1)} %shard_map.66.first_ref, bf16[2,160,2048]{2,1,0:T(8,128)(2,1)} %collective-permute-done.5.second_ref), custom_call_target="tpu_custom_call" | custom-call | flops 13107200 | bytes 2621440 | tf_op jit(solution)/shard_map/pallas_call | solution.py:162
  141.6 7.3 %collective-permute-done.7.second_ref = bf16[2,160,2048]{2,1,0:T(8,128)(2,1)} collective-permute-done((bf16[2,160,2048]{2,1,0:T(8,128)(2,1)}, bf16[2,160,2048]{2,1,0:T(8,128)(2,1)}, u32[]{:S(2)}, u32[]{:S(2)}) %collective-permute-start.7) | collective-permute-done | bytes 1310752 | tf_op jit(solution)/shard_map/ppermute | solution.py:39
  148.9 3.3 %shard_map.69 = f32[2,8,512]{2,1,0:T(8,128)} custom-call(bf16[2,160,2048]{2,1,0:T(8,128)(2,1)} %shard_map.64.first_ref, bf16[2,160,2048]{2,1,0:T(8,128)(2,1)} %collective-permute-done.7.second_ref), custom_call_target="tpu_custom_call" | custom-call | flops 13107200 | bytes 2621440 | tf_op jit(solution)/shard_map/pallas_call | solution.py:162
  152.2 0.0 copy-start.8
  152.2 0.0 copy-start.9
  152.2 0.0 copy-start.10
  152.2 0.0 copy-start.11
  152.3 0.0 copy-start.13
  152.3 7.7 %collective-permute-done.9.second_ref = bf16[2,160,2048]{2,1,0:T(8,128)(2,1)S(1)} collective-permute-done((bf16[2,160,2048]{2,1,0:T(8,128)(2,1)}, bf16[2,160,2048]{2,1,0:T(8,128)(2,1)S(1)}, u32[]{:S(2)}, u32[]{:S(2)}) %collective-permute-start.9) | collective-permute-done | bytes 1310752 | tf_op jit(solution)/shard_map/ppermute | solution.py:39
  160.0 1.1 copy-done.4
  161.0 3.3 %shard_map.71 = f32[2,8,512]{2,1,0:T(8,128)} custom-call(bf16[2,160,2048]{2,1,0:T(8,128)(2,1)} %shard_map.66.first_ref, bf16[2,160,2048]{2,1,0:T(8,128)(2,1)} %copy-done.4), custom_call_target="tpu_custom_call" | custom-call | flops 13107200 | bytes 2621440 | tf_op jit(solution)/shard_map/pallas_call | solution.py:162
  164.4 1.6 select_select_fusion
  166.1 5.6 %all-to-all-start = ((f32[8,2,8,512]{3,2,1,0:T(8,128)}), f32[8,2,8,512]{3,2,1,0:T(8,128)S(1)}, u32[]{:S(2)}, u32[]{:S(2)}) async-start(f32[8,2,8,512]{3,2,1,0:T(8,128)} %select_select_fusion), calls=%async_computation | async-start | bytes 524288 | tf_op jit(solution)/shard_map/all_to_all | solution.py:212
  171.6 0.7 fusion.47
  192.4 0.0 all-to-all-done
  192.8 0.7 maximum_bitcast_fusion
  (41 shorter events, 0.3 us)
Async XLA Ops:
  0.0 15.5 %copy-start.3 = (bf16[1,2,160,4096]{3,2,1,0:T(8,128)(2,1)S(1)}, bf16[1,2,160,4096]{3,2,1,0:T(8,128)(2,1)}, u32[]{:S(2)}) copy-start(bf16[1,2,160,4096]{3,2,1,0:T(8,128)(2,1)} %param.6) | copy-start | bytes 7864324
  1.8 13.7 %collective-permute-start = (bf16[1,2,16,4096]{3,2,1,0:T(8,128)(2,1)}, bf16[1,2,16,4096]{3,2,1,0:T(8,128)(2,1)S(1)}, u32[]{:S(2)}, u32[]{:S(2)}) collective-permute-start(bf16[1,2,16,4096]{3,2,1,0:T(8,128)(2,1)} %slice.131), channel_id=1, source_target_pairs={{0,1},{1,2},{2,3},{4,5},{5,6},{6,7},{8,9},{9,10},{10,11},{12,13},{... | collective-permute-start | bytes 786440 | tf_op jit(solution)/shard_map/ppermute | solution.py:27
  6.1 9.4 %collective-permute-start.1 = (bf16[1,2,25,4096]{3,2,1,0:T(8,128)(2,1)}, bf16[1,2,25,4096]{3,2,1,0:T(8,128)(2,1)S(1)}, u32[]{:S(2)}, u32[]{:S(2)}) collective-permute-start(bf16[1,2,25,4096]{3,2,1,0:T(8,128)(2,1)} %slice.132), channel_id=1, source_target_pairs={{1,0},{2,1},{3,2},{5,4},{6,5},{7,6},{9,8},{10,9},{11,10},{13,12},{... | collective-permute-start | bytes 1228808 | tf_op jit(solution)/shard_map/ppermute | solution.py:29
  34.9 31.8 %copy-start.1 = (bf16[2,160,2048]{2,1,0:T(8,128)(2,1)S(1)}, bf16[2,160,2048]{2,1,0:T(8,128)(2,1)}, u32[]{:S(2)}) copy-start(bf16[2,160,2048]{2,1,0:T(8,128)(2,1)} %shard_map.64.first_ref) | copy-start | bytes 3932164
  34.9 31.8 %collective-permute-start.2 = (bf16[2,160,2048]{2,1,0:T(8,128)(2,1)}, bf16[2,160,2048]{2,1,0:T(8,128)(2,1)S(1)}, u32[]{:S(2)}, u32[]{:S(2)}) collective-permute-start(bf16[2,160,2048]{2,1,0:T(8,128)(2,1)} %shard_map.64.first_ref), channel_id=1, source_target_pairs={{0,8},{4,12},{8,16},{12,20},{16,24},{20,28},{1,9},{5,13},{9,17},{1... | collective-permute-start | bytes 3932168 | tf_op jit(solution)/shard_map/ppermute | solution.py:39
  55.1 32.0 %collective-permute-start.4 = (bf16[2,160,2048]{2,1,0:T(8,128)(2,1)}, bf16[2,160,2048]{2,1,0:T(8,128)(2,1)}, u32[]{:S(2)}, u32[]{:S(2)}) collective-permute-start(bf16[2,160,2048]{2,1,0:T(8,128)(2,1)} %shard_map.66.first_ref), channel_id=1, source_target_pairs={{8,0},{12,4},{16,8},{20,12},{24,16},{28,20},{9,1},{13,5},{17,9},{2... | collective-permute-start | bytes 3932168 | tf_op jit(solution)/shard_map/ppermute | solution.py:39
  56.5 30.7 %copy-start = (bf16[2,160,2048]{2,1,0:T(8,128)(2,1)S(1)}, bf16[2,160,2048]{2,1,0:T(8,128)(2,1)}, u32[]{:S(2)}) copy-start(bf16[2,160,2048]{2,1,0:T(8,128)(2,1)} %shard_map.66.first_ref) | copy-start | bytes 3932164
  66.7 22.2 %copy-start.2 = (bf16[2,160,2048]{2,1,0:T(8,128)(2,1)}, bf16[2,160,2048]{2,1,0:T(8,128)(2,1)S(1)}, u32[]{:S(2)}) copy-start(bf16[2,160,2048]{2,1,0:T(8,128)(2,1)S(1)} %collective-permute-done.2.second_ref) | copy-start | bytes 3932164
  68.1 30.7 %collective-permute-start.6 = (bf16[2,160,2048]{2,1,0:T(8,128)(2,1)}, bf16[2,160,2048]{2,1,0:T(8,128)(2,1)}, u32[]{:S(2)}, u32[]{:S(2)}) collective-permute-start(bf16[2,160,2048]{2,1,0:T(8,128)(2,1)} %broadcast_select_fusion.1), channel_id=1, source_target_pairs={{0,4},{4,0},{8,12},{12,8},{16,20},{20,16},{24,28},{28,24},{1,5},{5... | collective-permute-start | bytes 3932168 | tf_op jit(solution)/shard_map/ppermute | solution.py:44
  88.7 38.2 %collective-permute-start.8 = (bf16[2,160,2048]{2,1,0:T(8,128)(2,1)S(1)}, bf16[2,160,2048]{2,1,0:T(8,128)(2,1)}, u32[]{:S(2)}, u32[]{:S(2)}) collective-permute-start(bf16[2,160,2048]{2,1,0:T(8,128)(2,1)S(1)} %broadcast_select_fusion), channel_id=1, source_target_pairs={{0,4},{4,0},{8,12},{12,8},{16,20},{20,16},{24,28},{28,24},{1,5},{5... | collective-permute-start | bytes 3932168 | tf_op jit(solution)/shard_map/ppermute | solution.py:44
  88.9 46.1 %collective-permute-start.3 = (bf16[2,160,2048]{2,1,0:T(8,128)(2,1)S(1)}, bf16[2,160,2048]{2,1,0:T(8,128)(2,1)}, u32[]{:S(2)}, u32[]{:S(2)}) collective-permute-start(bf16[2,160,2048]{2,1,0:T(8,128)(2,1)S(1)} %collective-permute-done.2.second_ref), channel_id=1, source_target_pairs={{0,8},{4,12},{8,16},{12,20},{16,24},{20,28},{1,9},{5,13},{9,17},{1... | collective-permute-start | bytes 3932168 | tf_op jit(solution)/shard_map/ppermute | solution.py:39
  93.4 44.9 %collective-permute-start.5 = (bf16[2,160,2048]{2,1,0:T(8,128)(2,1)}, bf16[2,160,2048]{2,1,0:T(8,128)(2,1)}, u32[]{:S(2)}, u32[]{:S(2)}) collective-permute-start(bf16[2,160,2048]{2,1,0:T(8,128)(2,1)} %collective-permute-done.4.second_ref), channel_id=1, source_target_pairs={{8,0},{12,4},{16,8},{20,12},{24,16},{28,20},{9,1},{13,5},{17,9},{2... | collective-permute-start | bytes 3932168 | tf_op jit(solution)/shard_map/ppermute | solution.py:39
  98.7 50.2 %collective-permute-start.7 = (bf16[2,160,2048]{2,1,0:T(8,128)(2,1)}, bf16[2,160,2048]{2,1,0:T(8,128)(2,1)}, u32[]{:S(2)}, u32[]{:S(2)}) collective-permute-start(bf16[2,160,2048]{2,1,0:T(8,128)(2,1)} %collective-permute-done.6.second_ref), channel_id=1, source_target_pairs={{0,8},{4,12},{8,16},{12,20},{16,24},{20,28},{1,9},{5,13},{9,17},{1... | collective-permute-start | bytes 3932168 | tf_op jit(solution)/shard_map/ppermute | solution.py:39
  126.8 33.2 %collective-permute-start.9 = (bf16[2,160,2048]{2,1,0:T(8,128)(2,1)}, bf16[2,160,2048]{2,1,0:T(8,128)(2,1)S(1)}, u32[]{:S(2)}, u32[]{:S(2)}) collective-permute-start(bf16[2,160,2048]{2,1,0:T(8,128)(2,1)} %collective-permute-done.8.second_ref), channel_id=1, source_target_pairs={{8,0},{12,4},{16,8},{20,12},{24,16},{28,20},{9,1},{13,5},{17,9},{2... | collective-permute-start | bytes 3932168 | tf_op jit(solution)/shard_map/ppermute | solution.py:39
  152.2 12.2 %copy-start.5 = (f32[2,8,512]{2,1,0:T(8,128)S(1)}, f32[2,8,512]{2,1,0:T(8,128)}, u32[]{:S(2)}) copy-start(f32[2,8,512]{2,1,0:T(8,128)} %shard_map.68) | copy-start | bytes 98308
  152.2 12.2 %copy-start.6 = (f32[2,8,512]{2,1,0:T(8,128)S(1)}, f32[2,8,512]{2,1,0:T(8,128)}, u32[]{:S(2)}) copy-start(f32[2,8,512]{2,1,0:T(8,128)} %shard_map.70) | copy-start | bytes 98308
  152.2 12.2 %copy-start.7 = (f32[2,8,512]{2,1,0:T(8,128)S(1)}, f32[2,8,512]{2,1,0:T(8,128)}, u32[]{:S(2)}) copy-start(f32[2,8,512]{2,1,0:T(8,128)} %shard_map.72) | copy-start | bytes 98308
  152.2 12.2 %copy-start.8 = (f32[2,8,512]{2,1,0:T(8,128)S(1)}, f32[2,8,512]{2,1,0:T(8,128)}, u32[]{:S(2)}) copy-start(f32[2,8,512]{2,1,0:T(8,128)} %shard_map.73) | copy-start | bytes 98308
  152.2 12.2 %copy-start.9 = (f32[2,8,512]{2,1,0:T(8,128)S(1)}, f32[2,8,512]{2,1,0:T(8,128)}, u32[]{:S(2)}) copy-start(f32[2,8,512]{2,1,0:T(8,128)} %shard_map.65) | copy-start | bytes 98308
  152.2 12.2 %copy-start.10 = (f32[2,8,512]{2,1,0:T(8,128)S(1)}, f32[2,8,512]{2,1,0:T(8,128)}, u32[]{:S(2)}) copy-start(f32[2,8,512]{2,1,0:T(8,128)} %shard_map.67) | copy-start | bytes 98308
  152.2 12.2 %copy-start.11 = (f32[2,8,512]{2,1,0:T(8,128)S(1)}, f32[2,8,512]{2,1,0:T(8,128)}, u32[]{:S(2)}) copy-start(f32[2,8,512]{2,1,0:T(8,128)} %shard_map.69) | copy-start | bytes 98308
  152.3 19.4 %copy-start.13 = (s32[1,4]{1,0:T(1,128)S(1)}, s32[1,4]{1,0:T(1,128)}, u32[]{:S(2)}) copy-start(s32[1,4]{1,0:T(1,128)} %param.11) | copy-start | bytes 52
  160.0 1.1 copy-start.4
  164.4 28.2 %copy-start.12 = (f32[2,8,512]{2,1,0:T(8,128)S(1)}, f32[2,8,512]{2,1,0:T(8,128)}, u32[]{:S(2)}) copy-start(f32[2,8,512]{2,1,0:T(8,128)} %shard_map.71) | copy-start | bytes 98308
  166.1 26.4 %all-to-all-start = ((f32[8,2,8,512]{3,2,1,0:T(8,128)}), f32[8,2,8,512]{3,2,1,0:T(8,128)S(1)}, u32[]{:S(2)}, u32[]{:S(2)}) async-start(f32[8,2,8,512]{3,2,1,0:T(8,128)} %select_select_fusion), calls=%async_computation | async-start | bytes 524288 | tf_op jit(solution)/shard_map/all_to_all | solution.py:212

commit v24 on v20

--- a/solution.py
+++ b/solution.py
@@ -128,42 +128,56 @@
 CHUNK = 512
 
 
-def looks_kernel(first_ref, second_ref, out_ref):
-    first_re = first_ref[0].astype(jnp.float32)
-    first_im = first_ref[1].astype(jnp.float32)
-    second_re = second_ref[0].astype(jnp.float32)
-    second_im = second_ref[1].astype(jnp.float32)
-    real_part = first_re * second_re + first_im * second_im
-    imag_part = first_im * second_re - first_re * second_im
-    rows = real_part.shape[0]
-    groups = rows // LOOK_AZ
-    real_lines = real_part.reshape(LOOK_AZ, groups, CHUNK).sum(axis=0)
-    imag_lines = imag_part.reshape(LOOK_AZ, groups, CHUNK).sum(axis=0)
+BLOCK = 1024
+
+
+def looks_kernel(*refs):
+    count = len(refs) // 3
     pooling = (
         lax.broadcasted_iota(jnp.int32, (CHUNK, CHUNK // LOOK_RG), 0) // LOOK_RG
         == lax.broadcasted_iota(jnp.int32, (CHUNK, CHUNK // LOOK_RG), 1)
     ).astype(jnp.float32)
-    real_looks = jnp.dot(real_lines, pooling, precision=lax.Precision.HIGHEST, preferred_element_type=jnp.float32)
-    imag_looks = jnp.dot(imag_lines, pooling, precision=lax.Precision.HIGHEST, preferred_element_type=jnp.float32)
-    out_ref[0] = real_looks / (LOOK_AZ * LOOK_RG)
-    out_ref[1] = imag_looks / (LOOK_AZ * LOOK_RG)
-
-
-def looks(first, second):
-    nlines = first.shape[1]
-    width = first.shape[2]
+    for pair in range(count):
+        first_ref, second_ref, out_ref = refs[2 * pair], refs[2 * pair + 1], refs[2 * count + pair]
+        rows = first_ref.shape[1]
+        groups = rows // LOOK_AZ
+        for low in range(0, first_ref.shape[2], CHUNK):
+            first_re = first_ref[0, :, low : low + CHUNK].astype(jnp.float32)
+            first_im = first_ref[1, :, low : low + CHUNK].astype(jnp.float32)
+            second_re = second_ref[0, :, low : low + CHUNK].astype(jnp.float32)
+            second_im = second_ref[1, :, low : low + CHUNK].astype(jnp.float32)
+            real_part = first_re * second_re + first_im * second_im
+            imag_part = first_im * second_re - first_re * second_im
+            real_lines = real_part.reshape(LOOK_AZ, groups, CHUNK).sum(axis=0)
+            imag_lines = imag_part.reshape(LOOK_AZ, groups, CHUNK).sum(axis=0)
+            real_looks = jnp.dot(real_lines, pooling, precision=lax.Precision.HIGHEST, preferred_element_type=jnp.float32)
+            imag_looks = jnp.dot(imag_lines, pooling, precision=lax.Precision.HIGHEST, preferred_element_type=jnp.float32)
+            out = slice(low // LOOK_RG, (low + CHUNK) // LOOK_RG)
+            out_ref[0, :, out] = real_looks / (LOOK_AZ * LOOK_RG)
+            out_ref[1, :, out] = imag_looks / (LOOK_AZ * LOOK_RG)
+
+
+def looks_pairs(*arrays):
+    nlines = arrays[0].shape[1]
+    width = arrays[0].shape[2]
     groups = nlines // LOOK_AZ
-    spec = pl.BlockSpec((2, nlines, CHUNK), lambda j: (0, 0, j))
+    count = len(arrays) // 2
+    spec = pl.BlockSpec((2, nlines, BLOCK), lambda j: (0, 0, j))
+    out_spec = pl.BlockSpec((2, groups, BLOCK // LOOK_RG), lambda j: (0, 0, j))
     return pl.pallas_call(
         looks_kernel,
-        grid=(width // CHUNK,),
-        in_specs=[spec, spec],
-        out_specs=pl.BlockSpec((2, groups, CHUNK // LOOK_RG), lambda j: (0, 0, j)),
-        out_shape=jax.ShapeDtypeStruct((2, groups, width // LOOK_RG), jnp.float32),
+        grid=(width // BLOCK,),
+        in_specs=[spec] * (2 * count),
+        out_specs=[out_spec] * count,
+        out_shape=[jax.ShapeDtypeStruct((2, groups, width // LOOK_RG), jnp.float32)] * count,
         cost_estimate=pl.CostEstimate(
-            flops=nlines * width * 40, transcendentals=0, bytes_accessed=2 * 2 * nlines * width * 2
+            flops=count * nlines * width * 40, transcendentals=0, bytes_accessed=count * 2 * 2 * nlines * width * 2
         ),
-    )(first, second)
+    )(*arrays)
+
+
+def looks(first, second):
+    return looks_pairs(first, second)[0]
 
 
 def look_order(image):
@@ -194,10 +208,11 @@
     right_1, behind[2] = lax.optimization_barrier((right_1, behind[2]))
     left_3 = shifted(left_1, "date", 2)
     right_3 = shifted(right_1, "date", -2)
-    for s, other in ((1, left_1), (4, left_4), (3, left_3)):
+    for s, other in ((1, left_1), (4, left_4)):
         ahead[s] = looks(own_left, other)
-    for s, other in ((1, right_1), (4, right_4), (3, right_3)):
+    for s, other in ((1, right_1), (4, right_4)):
         behind[s] = looks(own_right, other)
+    ahead[3], behind[3] = looks_pairs(own_left, left_3, own_right, right_3)
     count = lax.axis_size("date")
     target = lax.broadcasted_iota(jnp.int32, (count, 1, 1, 1), 0) - date
     sent = jnp.zeros((count,) + ahead[1].shape, jnp.float32)

time: 196 us -> 199 us (1.015)
  Pallas kernels: 66.4 us -> 56 us
  waiting for transfers between devices: 55.3 us -> 65.3 us
    pallas_call x8 -> x7, Pallas kernels: 34.9 us -> 24.5 us  [looks_pairs(): pl.pallas_call(looks_kernel, grid=(width // BLOCK,), in_specs=[spec] * (2...]
    ppermute x6, waiting for transfers between devices: 37.8 us -> 45.3 us  [shifted(): return lax.ppermute(block, axis, route)]
    ppermute x2, waiting for transfers between devices: 17.5 us -> 20 us  [swapped(): return lax.ppermute(block, axis, [(i, i ^ 1) for i in range(count)])]
  transfers between devices with their start and end apart: 11 -> 11, of which waited for: 5 -> 5; matrix products, arithmetic and copies ran while one was open for 6% -> 7% of each run, Pallas kernels for 24% -> 18%
where the time goes in v24:
time: 199 us; the launch traced here: 197 us
  waiting for transfers between devices  65.3 us (33%)
  Pallas kernels  56 us (28%)
  starting transfers between devices  31.2 us (16%)
  between operations  22.2 us (11%)
  other arithmetic  13.3 us (7%)
  local copies, waits for them, and re-layouts  9.47 us (5%)
    ppermute x6, waiting for transfers between devices, shifted(): return lax.ppermute(block, axis, route)  45.3 us
    pallas_call x2, Pallas kernels, resample_half(): pl.pallas_call(functools.partial(resample_kernel, side), grid=(2, nlines...  31.5 us
    pallas_call x7, Pallas kernels, looks_pairs(): pl.pallas_call(looks_kernel, grid=(width // BLOCK,), in_specs=[spec] * (2...  24.5 us
    ppermute x2, waiting for transfers between devices, swapped(): return lax.ppermute(block, axis, [(i, i ^ 1) for i in range(count)])  20 us
    ppermute x6, starting transfers between devices, shifted(): return lax.ppermute(block, axis, route)  17.9 us
    all_to_all x1, starting transfers between devices, shards(): got = lax.all_to_all(sent, 'date', 0, 0, tiled=True)  6.65 us
  transfers between devices with their start and end apart: 11, of which 5 were waited for; matrix products, arithmetic and copies ran while one was open for 7% of the time, Pallas kernels for 18%

profile of v24, /device:TPU:0, one launch (start us, length us, event | category | flops | bytes accessed | tf_op | source)
XLA Modules:
  0.0 197.4 jit_solution(7295699471427035231)
XLA Ops:
  0.0 1.8 slice.131
  1.8 2.4 %collective-permute-start = (bf16[1,2,16,4096]{3,2,1,0:T(8,128)(2,1)}, bf16[1,2,16,4096]{3,2,1,0:T(8,128)(2,1)S(1)}, u32[]{:S(2)}, u32[]{:S(2)}) collective-permute-start(bf16[1,2,16,4096]{3,2,1,0:T(8,128)(2,1)} %slice.131), channel_id=1, source_target_pairs={{0,1},{1,2},{2,3},{4,5},{5,6},{6,7},{8,9},{9,10},{10,11},{12,13},{... | collective-permute-start | bytes 786440 | tf_op jit(solution)/shard_map/ppermute | solution.py:27
  4.2 1.9 slice.132
  6.1 1.3 collective-permute-start.1
  7.4 0.7 compare_select_fusion.1
  8.1 0.6 broadcast.448
  8.7 1.4 reduce.9
  10.0 0.1 squeeze.28
  10.1 0.1 fusion.17
  10.2 0.7 add_reduce_fusion
  12.2 0.1 copy.21
  12.3 0.8 fusion.14.weights_ref
  13.1 0.1 add.231
  13.2 0.1 copy.24
  13.3 0.7 gather_fusion
  13.9 0.1 copy.22
  14.0 0.1 gather.7
  14.1 0.8 copy.23
  14.9 0.7 reshape.1168.shift_ref
  15.6 0.0 collective-permute-done
  15.6 0.0 collective-permute-done.1
  15.6 0.0 copy-done.2
  15.6 3.9 %fusion.2.window_ref = bf16[2,176,4096]{2,1,0:T(8,128)(2,1)} fusion(s32[]{:T(128)S(6)} %select_n.546, bf16[1,2,16,4096]{3,2,1,0:T(8,128)(2,1)S(1)} %collective-permute-done, bf16[1,2,160,4096]{3,2,1,0:T(8,128)(2,1)S(1)} %copy-done.2, bf16[1,2,25,4096]{3,2,1,0:T(8,128)(2,1)S(1)} %collective-permute-done.1), kind=kLoop, calls=%fused_computation.6 | loop fusion | flops 8650752 | bytes 6176772 | tf_op jit(solution)/shard_map/dynamic_slice | solution.py:114
  19.5 15.8 %shard_map.64.refs_0_.refs_2_ = bf16[2,160,2048]{2,1,0:T(8,128)(2,1)} custom-call(f32[8]{0:T(128)} %fusion.14.weights_ref, bf16[2,176,4096]{2,1,0:T(8,128)(2,1)} %fusion.2.window_ref, f32[160,8]{1,0:T(8,128)} %bitcast.113, s32[160,1]{1,0:T(8,128)} %reshape.1168.shift_ref), custom_call_target="tpu_custom_call" | custom-call | flops 39321600 | bytes 3932160 | tf_op jit(solution)/shard_map/pallas_call | solution.py:92
  35.3 5.5 %collective-permute-start.2 = (bf16[2,160,2048]{2,1,0:T(8,128)(2,1)}, bf16[2,160,2048]{2,1,0:T(8,128)(2,1)}, u32[]{:S(2)}, u32[]{:S(2)}) collective-permute-start(bf16[2,160,2048]{2,1,0:T(8,128)(2,1)} %shard_map.64.refs_0_.refs_2_), channel_id=1, source_target_pairs={{0,8},{4,12},{8,16},{12,20},{16,24},{20,28},{1,9},{5,13},{9,17},{1... | collective-permute-start | bytes 3932168 | tf_op jit(solution)/shard_map/ppermute | solution.py:39
  40.8 15.7 %shard_map.66.refs_0_ = bf16[2,160,2048]{2,1,0:T(8,128)(2,1)} custom-call(f32[8]{0:T(128)} %fusion.14.weights_ref, bf16[2,176,4096]{2,1,0:T(8,128)(2,1)} %fusion.2.window_ref, f32[160,8]{1,0:T(8,128)} %bitcast.114, s32[160,1]{1,0:T(8,128)} %reshape.1168.shift_ref), custom_call_target="tpu_custom_call" | custom-call | flops 39321600 | bytes 3932160 | tf_op jit(solution)/shard_map/pallas_call | solution.py:92
  56.5 1.3 collective-permute-start.4
  57.8 0.0 copy-start.1
  57.9 9.3 %collective-permute-done.2.refs_1_ = bf16[2,160,2048]{2,1,0:T(8,128)(2,1)} collective-permute-done((bf16[2,160,2048]{2,1,0:T(8,128)(2,1)}, bf16[2,160,2048]{2,1,0:T(8,128)(2,1)}, u32[]{:S(2)}, u32[]{:S(2)}) %collective-permute-start.2) | collective-permute-done | bytes 1310752 | tf_op jit(solution)/shard_map/ppermute | solution.py:39
  67.2 1.2 broadcast_select_fusion
  68.4 2.8 %collective-permute-start.8 = (bf16[2,160,2048]{2,1,0:T(8,128)(2,1)}, bf16[2,160,2048]{2,1,0:T(8,128)(2,1)}, u32[]{:S(2)}, u32[]{:S(2)}) collective-permute-start(bf16[2,160,2048]{2,1,0:T(8,128)(2,1)} %broadcast_select_fusion), channel_id=1, source_target_pairs={{0,4},{4,0},{8,12},{12,8},{16,20},{20,16},{24,28},{28,24},{1,5},{5... | collective-permute-start | bytes 3932168 | tf_op jit(solution)/shard_map/ppermute | solution.py:44
  71.2 17.4 %collective-permute-done.4.refs_1_ = bf16[2,160,2048]{2,1,0:T(8,128)(2,1)} collective-permute-done((bf16[2,160,2048]{2,1,0:T(8,128)(2,1)}, bf16[2,160,2048]{2,1,0:T(8,128)(2,1)}, u32[]{:S(2)}, u32[]{:S(2)}) %collective-permute-start.4) | collective-permute-done | bytes 1310752 | tf_op jit(solution)/shard_map/ppermute | solution.py:39
  88.6 0.0 copy-done.1
  88.7 2.6 %broadcast_select_fusion.1 = bf16[2,160,2048]{2,1,0:T(8,128)(2,1)} fusion(bf16[2,160,2048]{2,1,0:T(8,128)(2,1)} %collective-permute-done.4.refs_1_, bf16[2,160,2048]{2,1,0:T(8,128)(2,1)S(1)} %copy-done.1, pred[]{:T(512)S(6)} %eq.195), kind=kLoop, calls=%fused_computation.8 | loop fusion | flops 655360 | bytes 3932161 | tf_op jit(solution)/shard_map/jit(_where)/select_n | solution.py:200
  91.2 0.2 collective-permute-start.6
  91.5 3.7 %collective-permute-start.3 = (bf16[2,160,2048]{2,1,0:T(8,128)(2,1)}, bf16[2,160,2048]{2,1,0:T(8,128)(2,1)}, u32[]{:S(2)}, u32[]{:S(2)}) collective-permute-start(bf16[2,160,2048]{2,1,0:T(8,128)(2,1)} %collective-permute-done.2.refs_1_), channel_id=1, source_target_pairs={{0,8},{4,12},{8,16},{12,20},{16,24},{20,28},{1,9},{5,13},{9,17},{1... | collective-permute-start | bytes 3932168 | tf_op jit(solution)/shard_map/ppermute | solution.py:39
  95.1 1.3 collective-permute-start.5
  96.4 3.3 %shard_map.69 = f32[2,8,512]{2,1,0:T(8,128)} custom-call(bf16[2,160,2048]{2,1,0:T(8,128)(2,1)} %shard_map.64.refs_0_.refs_2_, bf16[2,160,2048]{2,1,0:T(8,128)(2,1)} %collective-permute-done.2.refs_1_), custom_call_target="tpu_custom_call" | custom-call | flops 13107200 | bytes 2621440 | tf_op jit(solution)/shard_map/pallas_call | solution.py:167
  99.8 3.3 %shard_map.68 = f32[2,8,512]{2,1,0:T(8,128)} custom-call(bf16[2,160,2048]{2,1,0:T(8,128)(2,1)} %shard_map.66.refs_0_, bf16[2,160,2048]{2,1,0:T(8,128)(2,1)} %collective-permute-done.4.refs_1_), custom_call_target="tpu_custom_call" | custom-call | flops 13107200 | bytes 2621440 | tf_op jit(solution)/shard_map/pallas_call | solution.py:167
  103.1 0.0 collective-permute-done.8.refs_1_
  103.1 4.6 %collective-permute-start.9 = (bf16[2,160,2048]{2,1,0:T(8,128)(2,1)}, bf16[2,160,2048]{2,1,0:T(8,128)(2,1)S(1)}, u32[]{:S(2)}, u32[]{:S(2)}) collective-permute-start(bf16[2,160,2048]{2,1,0:T(8,128)(2,1)} %collective-permute-done.8.refs_1_), channel_id=1, source_target_pairs={{0,8},{4,12},{8,16},{12,20},{16,24},{20,28},{1,9},{5,13},{9,17},{1... | collective-permute-start | bytes 3932168 | tf_op jit(solution)/shard_map/ppermute | solution.py:39
  107.7 20.0 %collective-permute-done.6.refs_1_ = bf16[2,160,2048]{2,1,0:T(8,128)(2,1)} collective-permute-done((bf16[2,160,2048]{2,1,0:T(8,128)(2,1)}, bf16[2,160,2048]{2,1,0:T(8,128)(2,1)}, u32[]{:S(2)}, u32[]{:S(2)}) %collective-permute-start.6) | collective-permute-done | bytes 1310752 | tf_op jit(solution)/shard_map/ppermute | solution.py:44
  127.7 1.5 collective-permute-start.7
  129.3 3.3 %shard_map.71 = f32[2,8,512]{2,1,0:T(8,128)} custom-call(bf16[2,160,2048]{2,1,0:T(8,128)(2,1)} %shard_map.64.refs_0_.refs_2_, bf16[2,160,2048]{2,1,0:T(8,128)(2,1)} %collective-permute-done.8.refs_1_), custom_call_target="tpu_custom_call" | custom-call | flops 13107200 | bytes 2621440 | tf_op jit(solution)/shard_map/pallas_call | solution.py:167
  132.6 3.3 %shard_map.72 = f32[2,8,512]{2,1,0:T(8,128)} custom-call(bf16[2,160,2048]{2,1,0:T(8,128)(2,1)} %shard_map.66.refs_0_, bf16[2,160,2048]{2,1,0:T(8,128)(2,1)} %collective-permute-done.6.refs_1_), custom_call_target="tpu_custom_call" | custom-call | flops 13107200 | bytes 2621440 | tf_op jit(solution)/shard_map/pallas_call | solution.py:167
  135.9 0.0 collective-permute-done.3.refs_1_
  135.9 3.3 %shard_map.65 = f32[2,8,512]{2,1,0:T(8,128)} custom-call(bf16[2,160,2048]{2,1,0:T(8,128)(2,1)} %shard_map.64.refs_0_.refs_2_, bf16[2,160,2048]{2,1,0:T(8,128)(2,1)} %collective-permute-done.3.refs_1_), custom_call_target="tpu_custom_call" | custom-call | flops 13107200 | bytes 2621440 | tf_op jit(solution)/shard_map/pallas_call | solution.py:167
  139.2 0.0 collective-permute-done.5.refs_1_
  139.2 3.3 %shard_map.67 = f32[2,8,512]{2,1,0:T(8,128)} custom-call(bf16[2,160,2048]{2,1,0:T(8,128)(2,1)} %shard_map.66.refs_0_, bf16[2,160,2048]{2,1,0:T(8,128)(2,1)} %collective-permute-done.5.refs_1_), custom_call_target="tpu_custom_call" | custom-call | flops 13107200 | bytes 2621440 | tf_op jit(solution)/shard_map/pallas_call | solution.py:167
  142.6 0.0 copy-start.8
  142.6 0.0 copy-start.13
  142.6 8.4 %collective-permute-done.9.refs_3_ = bf16[2,160,2048]{2,1,0:T(8,128)(2,1)S(1)} collective-permute-done((bf16[2,160,2048]{2,1,0:T(8,128)(2,1)}, bf16[2,160,2048]{2,1,0:T(8,128)(2,1)S(1)}, u32[]{:S(2)}, u32[]{:S(2)}) %collective-permute-start.9) | collective-permute-done | bytes 1310752 | tf_op jit(solution)/shard_map/ppermute | solution.py:39
  151.0 10.2 %collective-permute-done.7.refs_1_ = bf16[2,160,2048]{2,1,0:T(8,128)(2,1)S(1)} collective-permute-done((bf16[2,160,2048]{2,1,0:T(8,128)(2,1)}, bf16[2,160,2048]{2,1,0:T(8,128)(2,1)S(1)}, u32[]{:S(2)}, u32[]{:S(2)}) %collective-permute-start.7) | collective-permute-done | bytes 1310752 | tf_op jit(solution)/shard_map/ppermute | solution.py:39
  161.1 1.1 copy-done.4
  162.2 4.6 %shard_map.70 = (f32[2,8,512]{2,1,0:T(8,128)}, f32[2,8,512]{2,1,0:T(8,128)}) custom-call(bf16[2,160,2048]{2,1,0:T(8,128)(2,1)} %shard_map.66.refs_0_, bf16[2,160,2048]{2,1,0:T(8,128)(2,1)} %copy-done.4, bf16[2,160,2048]{2,1,0:T(8,128)(2,1)} %shard_map.64.refs_0_.refs_2_, bf16[2,160,2048]{2,1,0:T(8,128)(2,1)} %copy-done.3), custom_call_target="tpu_custom_call" | custom-call | flops 26214400 | bytes 5242880 | tf_op jit(solution)/shard_map/pallas_call | solution.py:167
  166.8 0.0 copy-done.5
  166.8 0.0 copy-done.6
  166.8 0.0 copy-done.7
  166.8 0.0 copy-done.8
  166.8 1.6 select_select_fusion
  168.5 6.7 %all-to-all-start = ((f32[8,2,8,512]{3,2,1,0:T(8,128)}), f32[8,2,8,512]{3,2,1,0:T(8,128)S(1)}, u32[]{:S(2)}, u32[]{:S(2)}) async-start(f32[8,2,8,512]{3,2,1,0:T(8,128)} %select_select_fusion), calls=%async_computation | async-start | bytes 524288 | tf_op jit(solution)/shard_map/all_to_all | solution.py:222
  175.1 0.7 fusion.47
  196.3 0.0 all-to-all-done
  196.7 0.7 maximum_bitcast_fusion
  (40 shorter events, 0.3 us)
Async XLA Ops:
  0.0 15.6 %copy-start.2 = (bf16[1,2,160,4096]{3,2,1,0:T(8,128)(2,1)S(1)}, bf16[1,2,160,4096]{3,2,1,0:T(8,128)(2,1)}, u32[]{:S(2)}) copy-start(bf16[1,2,160,4096]{3,2,1,0:T(8,128)(2,1)} %param.6) | copy-start | bytes 7864324
  1.8 13.8 %collective-permute-start = (bf16[1,2,16,4096]{3,2,1,0:T(8,128)(2,1)}, bf16[1,2,16,4096]{3,2,1,0:T(8,128)(2,1)S(1)}, u32[]{:S(2)}, u32[]{:S(2)}) collective-permute-start(bf16[1,2,16,4096]{3,2,1,0:T(8,128)(2,1)} %slice.131), channel_id=1, source_target_pairs={{0,1},{1,2},{2,3},{4,5},{5,6},{6,7},{8,9},{9,10},{10,11},{12,13},{... | collective-permute-start | bytes 786440 | tf_op jit(solution)/shard_map/ppermute | solution.py:27
  6.1 9.5 %collective-permute-start.1 = (bf16[1,2,25,4096]{3,2,1,0:T(8,128)(2,1)}, bf16[1,2,25,4096]{3,2,1,0:T(8,128)(2,1)S(1)}, u32[]{:S(2)}, u32[]{:S(2)}) collective-permute-start(bf16[1,2,25,4096]{3,2,1,0:T(8,128)(2,1)} %slice.132), channel_id=1, source_target_pairs={{1,0},{2,1},{3,2},{5,4},{6,5},{7,6},{9,8},{10,9},{11,10},{13,12},{... | collective-permute-start | bytes 1228808 | tf_op jit(solution)/shard_map/ppermute | solution.py:29
  35.3 31.9 %copy-start = (bf16[2,160,2048]{2,1,0:T(8,128)(2,1)S(1)}, bf16[2,160,2048]{2,1,0:T(8,128)(2,1)}, u32[]{:S(2)}) copy-start(bf16[2,160,2048]{2,1,0:T(8,128)(2,1)} %shard_map.64.refs_0_.refs_2_) | copy-start | bytes 3932164
  35.3 31.9 %collective-permute-start.2 = (bf16[2,160,2048]{2,1,0:T(8,128)(2,1)}, bf16[2,160,2048]{2,1,0:T(8,128)(2,1)}, u32[]{:S(2)}, u32[]{:S(2)}) collective-permute-start(bf16[2,160,2048]{2,1,0:T(8,128)(2,1)} %shard_map.64.refs_0_.refs_2_), channel_id=1, source_target_pairs={{0,8},{4,12},{8,16},{12,20},{16,24},{20,28},{1,9},{5,13},{9,17},{1... | collective-permute-start | bytes 3932168 | tf_op jit(solution)/shard_map/ppermute | solution.py:39
  56.5 32.1 %collective-permute-start.4 = (bf16[2,160,2048]{2,1,0:T(8,128)(2,1)}, bf16[2,160,2048]{2,1,0:T(8,128)(2,1)}, u32[]{:S(2)}, u32[]{:S(2)}) collective-permute-start(bf16[2,160,2048]{2,1,0:T(8,128)(2,1)} %shard_map.66.refs_0_), channel_id=1, source_target_pairs={{8,0},{12,4},{16,8},{20,12},{24,16},{28,20},{9,1},{13,5},{17,9},{2... | collective-permute-start | bytes 3932168 | tf_op jit(solution)/shard_map/ppermute | solution.py:39
  57.8 30.8 %copy-start.1 = (bf16[2,160,2048]{2,1,0:T(8,128)(2,1)S(1)}, bf16[2,160,2048]{2,1,0:T(8,128)(2,1)}, u32[]{:S(2)}) copy-start(bf16[2,160,2048]{2,1,0:T(8,128)(2,1)} %shard_map.66.refs_0_) | copy-start | bytes 3932164
  68.4 34.7 %collective-permute-start.8 = (bf16[2,160,2048]{2,1,0:T(8,128)(2,1)}, bf16[2,160,2048]{2,1,0:T(8,128)(2,1)}, u32[]{:S(2)}, u32[]{:S(2)}) collective-permute-start(bf16[2,160,2048]{2,1,0:T(8,128)(2,1)} %broadcast_select_fusion), channel_id=1, source_target_pairs={{0,4},{4,0},{8,12},{12,8},{16,20},{20,16},{24,28},{28,24},{1,5},{5... | collective-permute-start | bytes 3932168 | tf_op jit(solution)/shard_map/ppermute | solution.py:44
  91.2 36.5 %collective-permute-start.6 = (bf16[2,160,2048]{2,1,0:T(8,128)(2,1)}, bf16[2,160,2048]{2,1,0:T(8,128)(2,1)}, u32[]{:S(2)}, u32[]{:S(2)}) collective-permute-start(bf16[2,160,2048]{2,1,0:T(8,128)(2,1)} %broadcast_select_fusion.1), channel_id=1, source_target_pairs={{0,4},{4,0},{8,12},{12,8},{16,20},{20,16},{24,28},{28,24},{1,5},{5... | collective-permute-start | bytes 3932168 | tf_op jit(solution)/shard_map/ppermute | solution.py:44
  91.5 44.5 %collective-permute-start.3 = (bf16[2,160,2048]{2,1,0:T(8,128)(2,1)}, bf16[2,160,2048]{2,1,0:T(8,128)(2,1)}, u32[]{:S(2)}, u32[]{:S(2)}) collective-permute-start(bf16[2,160,2048]{2,1,0:T(8,128)(2,1)} %collective-permute-done.2.refs_1_), channel_id=1, source_target_pairs={{0,8},{4,12},{8,16},{12,20},{16,24},{20,28},{1,9},{5,13},{9,17},{1... | collective-permute-start | bytes 3932168 | tf_op jit(solution)/shard_map/ppermute | solution.py:39
  95.1 44.1 %collective-permute-start.5 = (bf16[2,160,2048]{2,1,0:T(8,128)(2,1)}, bf16[2,160,2048]{2,1,0:T(8,128)(2,1)}, u32[]{:S(2)}, u32[]{:S(2)}) collective-permute-start(bf16[2,160,2048]{2,1,0:T(8,128)(2,1)} %collective-permute-done.4.refs_1_), channel_id=1, source_target_pairs={{8,0},{12,4},{16,8},{20,12},{24,16},{28,20},{9,1},{13,5},{17,9},{2... | collective-permute-start | bytes 3932168 | tf_op jit(solution)/shard_map/ppermute | solution.py:39
  103.1 47.9 %collective-permute-start.9 = (bf16[2,160,2048]{2,1,0:T(8,128)(2,1)}, bf16[2,160,2048]{2,1,0:T(8,128)(2,1)S(1)}, u32[]{:S(2)}, u32[]{:S(2)}) collective-permute-start(bf16[2,160,2048]{2,1,0:T(8,128)(2,1)} %collective-permute-done.8.refs_1_), channel_id=1, source_target_pairs={{0,8},{4,12},{8,16},{12,20},{16,24},{20,28},{1,9},{5,13},{9,17},{1... | collective-permute-start | bytes 3932168 | tf_op jit(solution)/shard_map/ppermute | solution.py:39
  127.7 33.4 %collective-permute-start.7 = (bf16[2,160,2048]{2,1,0:T(8,128)(2,1)}, bf16[2,160,2048]{2,1,0:T(8,128)(2,1)S(1)}, u32[]{:S(2)}, u32[]{:S(2)}) collective-permute-start(bf16[2,160,2048]{2,1,0:T(8,128)(2,1)} %collective-permute-done.6.refs_1_), channel_id=1, source_target_pairs={{8,0},{12,4},{16,8},{20,12},{24,16},{28,20},{9,1},{13,5},{17,9},{2... | collective-permute-start | bytes 3932168 | tf_op jit(solution)/shard_map/ppermute | solution.py:39
  142.6 24.2 %copy-start.5 = (f32[2,8,512]{2,1,0:T(8,128)S(1)}, f32[2,8,512]{2,1,0:T(8,128)}, u32[]{:S(2)}) copy-start(f32[2,8,512]{2,1,0:T(8,128)} %shard_map.69) | copy-start | bytes 98308
  142.6 24.2 %copy-start.6 = (f32[2,8,512]{2,1,0:T(8,128)S(1)}, f32[2,8,512]{2,1,0:T(8,128)}, u32[]{:S(2)}) copy-start(f32[2,8,512]{2,1,0:T(8,128)} %shard_map.68) | copy-start | bytes 98308
  142.6 24.2 %copy-start.7 = (f32[2,8,512]{2,1,0:T(8,128)S(1)}, f32[2,8,512]{2,1,0:T(8,128)}, u32[]{:S(2)}) copy-start(f32[2,8,512]{2,1,0:T(8,128)} %shard_map.71) | copy-start | bytes 98308
  142.6 24.2 %copy-start.8 = (f32[2,8,512]{2,1,0:T(8,128)S(1)}, f32[2,8,512]{2,1,0:T(8,128)}, u32[]{:S(2)}) copy-start(f32[2,8,512]{2,1,0:T(8,128)} %shard_map.72) | copy-start | bytes 98308
  142.6 24.2 %copy-start.9 = (f32[2,8,512]{2,1,0:T(8,128)S(1)}, f32[2,8,512]{2,1,0:T(8,128)}, u32[]{:S(2)}) copy-start(f32[2,8,512]{2,1,0:T(8,128)} %shard_map.65) | copy-start | bytes 98308
  142.6 24.2 %copy-start.10 = (f32[2,8,512]{2,1,0:T(8,128)S(1)}, f32[2,8,512]{2,1,0:T(8,128)}, u32[]{:S(2)}) copy-start(f32[2,8,512]{2,1,0:T(8,128)} %shard_map.67) | copy-start | bytes 98308
  142.6 32.5 %copy-start.13 = (s32[1,4]{1,0:T(1,128)S(1)}, s32[1,4]{1,0:T(1,128)}, u32[]{:S(2)}) copy-start(s32[1,4]{1,0:T(1,128)} %param.11) | copy-start | bytes 52
  151.0 10.2 %copy-start.3 = (bf16[2,160,2048]{2,1,0:T(8,128)(2,1)}, bf16[2,160,2048]{2,1,0:T(8,128)(2,1)S(1)}, u32[]{:S(2)}) copy-start(bf16[2,160,2048]{2,1,0:T(8,128)(2,1)S(1)} %collective-permute-done.9.refs_3_) | copy-start | bytes 3932164
  161.1 1.1 copy-start.4
  166.8 29.7 %copy-start.11 = (f32[2,8,512]{2,1,0:T(8,128)S(1)}, f32[2,8,512]{2,1,0:T(8,128)}, u32[]{:S(2)}) copy-start(f32[2,8,512]{2,1,0:T(8,128)} %get-tuple-element.14) | copy-start | bytes 98308
  166.8 29.7 %copy-start.12 = (f32[2,8,512]{2,1,0:T(8,128)S(1)}, f32[2,8,512]{2,1,0:T(8,128)}, u32[]{:S(2)}) copy-start(f32[2,8,512]{2,1,0:T(8,128)} %get-tuple-element.13) | copy-start | bytes 98308
  168.5 27.8 %all-to-all-start = ((f32[8,2,8,512]{3,2,1,0:T(8,128)}), f32[8,2,8,512]{3,2,1,0:T(8,128)S(1)}, u32[]{:S(2)}, u32[]{:S(2)}) async-start(f32[8,2,8,512]{3,2,1,0:T(8,128)} %select_select_fusion), calls=%async_computation | async-start | bytes 524288 | tf_op jit(solution)/shard_map/all_to_all | solution.py:222

commit v25 on v21

--- a/solution.py
+++ b/solution.py
@@ -195,8 +195,6 @@
     right_4 = shifted(right_2, "date", -2)
     ahead = {2: looks(own_left, left_2)}
     behind = {2: looks(own_right, right_2)}
-    left_1, ahead[2] = lax.optimization_barrier((left_1, ahead[2]))
-    right_1, behind[2] = lax.optimization_barrier((right_1, behind[2]))
     left_3 = shifted(left_1, "date", 2)
     right_3 = shifted(right_1, "date", -2)
     for s, other in ((1, left_1), (4, left_4), (3, left_3)):

time: 195 us -> 193 us (0.990)
    ppermute x6, waiting for transfers between devices: 42.8 us -> 37.4 us  [shifted(): return lax.ppermute(block, axis, route)]
    ppermute x2, waiting for transfers between devices: 20 us -> 25.3 us  [swapped(): return lax.ppermute(block, axis, [(i, i ^ 1) for i in range(count)])]
where the time goes in v25:
time: 193 us; the launch traced here: 191 us
  waiting for transfers between devices  62.7 us (32%)
  Pallas kernels  58 us (30%)
  starting transfers between devices  29.5 us (15%)
  between operations  21.7 us (11%)
  other arithmetic  11.1 us (6%)
  local copies, waits for them, and re-layouts  8.38 us (4%)
    ppermute x6, waiting for transfers between devices, shifted(): return lax.ppermute(block, axis, route)  37.4 us
    pallas_call x2, Pallas kernels, resample_half(): pl.pallas_call(functools.partial(resample_kernel, side), grid=(2, nlines...  31.5 us
    pallas_call x8, Pallas kernels, looks(): pl.pallas_call(looks_kernel, grid=(width // BLOCK,), in_specs=[spec, spec...  26.5 us
    ppermute x2, waiting for transfers between devices, swapped(): return lax.ppermute(block, axis, [(i, i ^ 1) for i in range(count)])  25.3 us
    ppermute x6, starting transfers between devices, shifted(): return lax.ppermute(block, axis, route)  18.5 us
    all_to_all x1, starting transfers between devices, shards(): got = lax.all_to_all(sent, 'date', 0, 0, tiled=True)  5.58 us
    dynamic_slice x1, other arithmetic, resample_block(): window = lax.dynamic_slice_in_dim(padded, start, nlines + 16, 1)  3.94 us
  transfers between devices with their start and end apart: 11, of which 6 were waited for; matrix products, arithmetic and copies ran while one was open for 6% of the time, Pallas kernels for 20%

profile of v25, /device:TPU:0, one launch (start us, length us, event | category | flops | bytes accessed | tf_op | source)
XLA Modules:
  0.0 191.4 jit_solution(7178738620620242325)
XLA Ops:
  0.0 1.8 slice.131
  1.8 2.4 %collective-permute-start = (bf16[1,2,16,4096]{3,2,1,0:T(8,128)(2,1)}, bf16[1,2,16,4096]{3,2,1,0:T(8,128)(2,1)S(1)}, u32[]{:S(2)}, u32[]{:S(2)}) collective-permute-start(bf16[1,2,16,4096]{3,2,1,0:T(8,128)(2,1)} %slice.131), channel_id=1, source_target_pairs={{0,1},{1,2},{2,3},{4,5},{5,6},{6,7},{8,9},{9,10},{10,11},{12,13},{... | collective-permute-start | bytes 786440 | tf_op jit(solution)/shard_map/ppermute | solution.py:27
  4.2 1.9 slice.132
  6.1 1.3 collective-permute-start.1
  7.4 0.7 compare_select_fusion.1
  8.1 0.5 broadcast.448
  8.6 1.3 reduce.9
  9.9 0.1 squeeze.28
  10.0 0.1 fusion.17
  10.1 0.7 add_reduce_fusion
  12.1 0.1 copy.21
  12.2 0.8 fusion.14.weights_ref
  13.0 0.1 add.231
  13.1 0.1 copy.24
  13.2 0.7 gather_fusion
  13.8 0.1 copy.22
  13.9 0.1 gather.7
  14.0 0.8 copy.23
  14.8 0.7 reshape.1168.shift_ref
  15.5 0.0 collective-permute-done
  15.5 0.0 collective-permute-done.1
  15.5 0.0 copy-done.3
  15.5 3.9 %fusion.2.window_ref = bf16[2,176,4096]{2,1,0:T(8,128)(2,1)} fusion(s32[]{:T(128)S(6)} %select_n.546, bf16[1,2,16,4096]{3,2,1,0:T(8,128)(2,1)S(1)} %collective-permute-done, bf16[1,2,160,4096]{3,2,1,0:T(8,128)(2,1)S(1)} %copy-done.3, bf16[1,2,25,4096]{3,2,1,0:T(8,128)(2,1)S(1)} %collective-permute-done.1), kind=kLoop, calls=%fused_computation.6 | loop fusion | flops 8650752 | bytes 6176772 | tf_op jit(solution)/shard_map/dynamic_slice | solution.py:114
  19.4 15.7 %shard_map.64.first_ref = bf16[2,160,2048]{2,1,0:T(8,128)(2,1)} custom-call(f32[8]{0:T(128)} %fusion.14.weights_ref, bf16[2,176,4096]{2,1,0:T(8,128)(2,1)} %fusion.2.window_ref, f32[160,8]{1,0:T(8,128)} %bitcast.113, s32[160,1]{1,0:T(8,128)} %reshape.1168.shift_ref), custom_call_target="tpu_custom_call" | custom-call | flops 39321600 | bytes 3932160 | tf_op jit(solution)/shard_map/pallas_call | solution.py:92
  35.2 4.7 %collective-permute-start.2 = (bf16[2,160,2048]{2,1,0:T(8,128)(2,1)}, bf16[2,160,2048]{2,1,0:T(8,128)(2,1)S(1)}, u32[]{:S(2)}, u32[]{:S(2)}) collective-permute-start(bf16[2,160,2048]{2,1,0:T(8,128)(2,1)} %shard_map.64.first_ref), channel_id=1, source_target_pairs={{0,8},{4,12},{8,16},{12,20},{16,24},{20,28},{1,9},{5,13},{9,17},{1... | collective-permute-start | bytes 3932168 | tf_op jit(solution)/shard_map/ppermute | solution.py:39
  39.9 15.8 %shard_map.66.first_ref = bf16[2,160,2048]{2,1,0:T(8,128)(2,1)} custom-call(f32[8]{0:T(128)} %fusion.14.weights_ref, bf16[2,176,4096]{2,1,0:T(8,128)(2,1)} %fusion.2.window_ref, f32[160,8]{1,0:T(8,128)} %bitcast.114, s32[160,1]{1,0:T(8,128)} %reshape.1168.shift_ref), custom_call_target="tpu_custom_call" | custom-call | flops 39321600 | bytes 3932160 | tf_op jit(solution)/shard_map/pallas_call | solution.py:92
  55.6 1.3 collective-permute-start.4
  56.9 0.0 copy-start
  57.0 10.0 %collective-permute-done.2.second_ref = bf16[2,160,2048]{2,1,0:T(8,128)(2,1)S(1)} collective-permute-done((bf16[2,160,2048]{2,1,0:T(8,128)(2,1)}, bf16[2,160,2048]{2,1,0:T(8,128)(2,1)S(1)}, u32[]{:S(2)}, u32[]{:S(2)}) %collective-permute-start.2) | collective-permute-done | bytes 1310752 | tf_op jit(solution)/shard_map/ppermute | solution.py:39
  67.0 0.0 copy-done.1
  67.0 0.1 broadcast_select_fusion.1
  67.1 1.6 collective-permute-start.6
  68.7 19.0 %collective-permute-done.4.second_ref = bf16[2,160,2048]{2,1,0:T(8,128)(2,1)} collective-permute-done((bf16[2,160,2048]{2,1,0:T(8,128)(2,1)}, bf16[2,160,2048]{2,1,0:T(8,128)(2,1)}, u32[]{:S(2)}, u32[]{:S(2)}) %collective-permute-start.4) | collective-permute-done | bytes 1310752 | tf_op jit(solution)/shard_map/ppermute | solution.py:39
  87.7 0.0 copy-done
  87.7 1.5 broadcast_select_fusion
  89.2 0.3 collective-permute-start.8
  89.4 4.5 %collective-permute-start.3 = (bf16[2,160,2048]{2,1,0:T(8,128)(2,1)S(1)}, bf16[2,160,2048]{2,1,0:T(8,128)(2,1)}, u32[]{:S(2)}, u32[]{:S(2)}) collective-permute-start(bf16[2,160,2048]{2,1,0:T(8,128)(2,1)S(1)} %collective-permute-done.2.second_ref), channel_id=1, source_target_pairs={{0,8},{4,12},{8,16},{12,20},{16,24},{20,28},{1,9},{5,13},{9,17},{1... | collective-permute-start | bytes 3932168 | tf_op jit(solution)/shard_map/ppermute | solution.py:39
  93.9 1.3 collective-permute-start.5
  95.2 2.3 %collective-permute-done.6.second_ref = bf16[2,160,2048]{2,1,0:T(8,128)(2,1)S(1)} collective-permute-done((bf16[2,160,2048]{2,1,0:T(8,128)(2,1)S(1)}, bf16[2,160,2048]{2,1,0:T(8,128)(2,1)S(1)}, u32[]{:S(2)}, u32[]{:S(2)}) %collective-permute-start.6) | collective-permute-done | bytes 1310752 | tf_op jit(solution)/shard_map/ppermute | solution.py:44
  97.5 5.2 %collective-permute-start.7 = (bf16[2,160,2048]{2,1,0:T(8,128)(2,1)S(1)}, bf16[2,160,2048]{2,1,0:T(8,128)(2,1)}, u32[]{:S(2)}, u32[]{:S(2)}) collective-permute-start(bf16[2,160,2048]{2,1,0:T(8,128)(2,1)S(1)} %collective-permute-done.6.second_ref), channel_id=1, source_target_pairs={{0,8},{4,12},{8,16},{12,20},{16,24},{20,28},{1,9},{5,13},{9,17},{1... | collective-permute-start | bytes 3932168 | tf_op jit(solution)/shard_map/ppermute | solution.py:39
  102.8 23.0 %collective-permute-done.8.second_ref = bf16[2,160,2048]{2,1,0:T(8,128)(2,1)} collective-permute-done((bf16[2,160,2048]{2,1,0:T(8,128)(2,1)S(1)}, bf16[2,160,2048]{2,1,0:T(8,128)(2,1)}, u32[]{:S(2)}, u32[]{:S(2)}) %collective-permute-start.8) | collective-permute-done | bytes 1310752 | tf_op jit(solution)/shard_map/ppermute | solution.py:44
  125.7 1.5 collective-permute-start.9
  127.3 3.3 %shard_map.70 = f32[2,8,512]{2,1,0:T(8,128)} custom-call(bf16[2,160,2048]{2,1,0:T(8,128)(2,1)} %shard_map.64.first_ref, bf16[2,160,2048]{2,1,0:T(8,128)(2,1)} %copy-done.2), custom_call_target="tpu_custom_call" | custom-call | flops 13107200 | bytes 2621440 | tf_op jit(solution)/shard_map/pallas_call | solution.py:162
  130.6 0.0 copy-done.4
  130.6 3.3 %shard_map.71 = f32[2,8,512]{2,1,0:T(8,128)} custom-call(bf16[2,160,2048]{2,1,0:T(8,128)(2,1)} %shard_map.66.first_ref, bf16[2,160,2048]{2,1,0:T(8,128)(2,1)} %collective-permute-done.4.second_ref), custom_call_target="tpu_custom_call" | custom-call | flops 13107200 | bytes 2621440 | tf_op jit(solution)/shard_map/pallas_call | solution.py:162
  133.9 3.3 %shard_map.72 = f32[2,8,512]{2,1,0:T(8,128)} custom-call(bf16[2,160,2048]{2,1,0:T(8,128)(2,1)} %shard_map.64.first_ref, bf16[2,160,2048]{2,1,0:T(8,128)(2,1)} %copy-done.4), custom_call_target="tpu_custom_call" | custom-call | flops 13107200 | bytes 2621440 | tf_op jit(solution)/shard_map/pallas_call | solution.py:162
  137.2 3.3 %shard_map.73 = f32[2,8,512]{2,1,0:T(8,128)} custom-call(bf16[2,160,2048]{2,1,0:T(8,128)(2,1)} %shard_map.66.first_ref, bf16[2,160,2048]{2,1,0:T(8,128)(2,1)} %collective-permute-done.8.second_ref), custom_call_target="tpu_custom_call" | custom-call | flops 13107200 | bytes 2621440 | tf_op jit(solution)/shard_map/pallas_call | solution.py:162
  140.5 0.0 collective-permute-done.3.second_ref
  140.5 3.3 %shard_map.65 = f32[2,8,512]{2,1,0:T(8,128)} custom-call(bf16[2,160,2048]{2,1,0:T(8,128)(2,1)} %shard_map.64.first_ref, bf16[2,160,2048]{2,1,0:T(8,128)(2,1)} %collective-permute-done.3.second_ref), custom_call_target="tpu_custom_call" | custom-call | flops 13107200 | bytes 2621440 | tf_op jit(solution)/shard_map/pallas_call | solution.py:162
  143.8 0.0 collective-permute-done.5.second_ref
  143.9 3.3 %shard_map.67 = f32[2,8,512]{2,1,0:T(8,128)} custom-call(bf16[2,160,2048]{2,1,0:T(8,128)(2,1)} %shard_map.66.first_ref, bf16[2,160,2048]{2,1,0:T(8,128)(2,1)} %collective-permute-done.5.second_ref), custom_call_target="tpu_custom_call" | custom-call | flops 13107200 | bytes 2621440 | tf_op jit(solution)/shard_map/pallas_call | solution.py:162
  147.2 2.2 %collective-permute-done.7.second_ref = bf16[2,160,2048]{2,1,0:T(8,128)(2,1)} collective-permute-done((bf16[2,160,2048]{2,1,0:T(8,128)(2,1)S(1)}, bf16[2,160,2048]{2,1,0:T(8,128)(2,1)}, u32[]{:S(2)}, u32[]{:S(2)}) %collective-permute-start.7) | collective-permute-done | bytes 1310752 | tf_op jit(solution)/shard_map/ppermute | solution.py:39
  149.4 3.3 %shard_map.68 = f32[2,8,512]{2,1,0:T(8,128)} custom-call(bf16[2,160,2048]{2,1,0:T(8,128)(2,1)} %shard_map.64.first_ref, bf16[2,160,2048]{2,1,0:T(8,128)(2,1)} %collective-permute-done.7.second_ref), custom_call_target="tpu_custom_call" | custom-call | flops 13107200 | bytes 2621440 | tf_op jit(solution)/shard_map/pallas_call | solution.py:162
  152.7 0.0 copy-start.8
  152.8 0.0 copy-start.13
  152.8 6.2 %collective-permute-done.9.second_ref = bf16[2,160,2048]{2,1,0:T(8,128)(2,1)} collective-permute-done((bf16[2,160,2048]{2,1,0:T(8,128)(2,1)}, bf16[2,160,2048]{2,1,0:T(8,128)(2,1)}, u32[]{:S(2)}, u32[]{:S(2)}) %collective-permute-start.9) | collective-permute-done | bytes 1310752 | tf_op jit(solution)/shard_map/ppermute | solution.py:39
  159.0 3.3 %shard_map.69 = f32[2,8,512]{2,1,0:T(8,128)} custom-call(bf16[2,160,2048]{2,1,0:T(8,128)(2,1)} %shard_map.66.first_ref, bf16[2,160,2048]{2,1,0:T(8,128)(2,1)} %collective-permute-done.9.second_ref), custom_call_target="tpu_custom_call" | custom-call | flops 13107200 | bytes 2621440 | tf_op jit(solution)/shard_map/pallas_call | solution.py:162
  162.4 1.6 select_select_fusion
  164.0 5.6 %all-to-all-start = ((f32[8,2,8,512]{3,2,1,0:T(8,128)}), f32[8,2,8,512]{3,2,1,0:T(8,128)S(1)}, u32[]{:S(2)}, u32[]{:S(2)}) async-start(f32[8,2,8,512]{3,2,1,0:T(8,128)} %select_select_fusion), calls=%async_computation | async-start | bytes 524288 | tf_op jit(solution)/shard_map/all_to_all | solution.py:210
  169.6 0.0 copy-done.13
  169.6 0.7 fusion.47
  190.4 0.0 all-to-all-done
  190.5 0.0 copy-done.12
  190.7 0.7 maximum_bitcast_fusion
  (41 shorter events, 0.4 us)
Async XLA Ops:
  0.0 15.5 %copy-start.3 = (bf16[1,2,160,4096]{3,2,1,0:T(8,128)(2,1)S(1)}, bf16[1,2,160,4096]{3,2,1,0:T(8,128)(2,1)}, u32[]{:S(2)}) copy-start(bf16[1,2,160,4096]{3,2,1,0:T(8,128)(2,1)} %param.6) | copy-start | bytes 7864324
  1.8 13.7 %collective-permute-start = (bf16[1,2,16,4096]{3,2,1,0:T(8,128)(2,1)}, bf16[1,2,16,4096]{3,2,1,0:T(8,128)(2,1)S(1)}, u32[]{:S(2)}, u32[]{:S(2)}) collective-permute-start(bf16[1,2,16,4096]{3,2,1,0:T(8,128)(2,1)} %slice.131), channel_id=1, source_target_pairs={{0,1},{1,2},{2,3},{4,5},{5,6},{6,7},{8,9},{9,10},{10,11},{12,13},{... | collective-permute-start | bytes 786440 | tf_op jit(solution)/shard_map/ppermute | solution.py:27
  6.1 9.4 %collective-permute-start.1 = (bf16[1,2,25,4096]{3,2,1,0:T(8,128)(2,1)}, bf16[1,2,25,4096]{3,2,1,0:T(8,128)(2,1)S(1)}, u32[]{:S(2)}, u32[]{:S(2)}) collective-permute-start(bf16[1,2,25,4096]{3,2,1,0:T(8,128)(2,1)} %slice.132), channel_id=1, source_target_pairs={{1,0},{2,1},{3,2},{5,4},{6,5},{7,6},{9,8},{10,9},{11,10},{13,12},{... | collective-permute-start | bytes 1228808 | tf_op jit(solution)/shard_map/ppermute | solution.py:29
  35.2 31.8 %copy-start.1 = (bf16[2,160,2048]{2,1,0:T(8,128)(2,1)S(1)}, bf16[2,160,2048]{2,1,0:T(8,128)(2,1)}, u32[]{:S(2)}) copy-start(bf16[2,160,2048]{2,1,0:T(8,128)(2,1)} %shard_map.64.first_ref) | copy-start | bytes 3932164
  35.2 31.8 %collective-permute-start.2 = (bf16[2,160,2048]{2,1,0:T(8,128)(2,1)}, bf16[2,160,2048]{2,1,0:T(8,128)(2,1)S(1)}, u32[]{:S(2)}, u32[]{:S(2)}) collective-permute-start(bf16[2,160,2048]{2,1,0:T(8,128)(2,1)} %shard_map.64.first_ref), channel_id=1, source_target_pairs={{0,8},{4,12},{8,16},{12,20},{16,24},{20,28},{1,9},{5,13},{9,17},{1... | collective-permute-start | bytes 3932168 | tf_op jit(solution)/shard_map/ppermute | solution.py:39
  55.6 32.0 %collective-permute-start.4 = (bf16[2,160,2048]{2,1,0:T(8,128)(2,1)}, bf16[2,160,2048]{2,1,0:T(8,128)(2,1)}, u32[]{:S(2)}, u32[]{:S(2)}) collective-permute-start(bf16[2,160,2048]{2,1,0:T(8,128)(2,1)} %shard_map.66.first_ref), channel_id=1, source_target_pairs={{8,0},{12,4},{16,8},{20,12},{24,16},{28,20},{9,1},{13,5},{17,9},{2... | collective-permute-start | bytes 3932168 | tf_op jit(solution)/shard_map/ppermute | solution.py:39
  56.9 30.7 %copy-start = (bf16[2,160,2048]{2,1,0:T(8,128)(2,1)S(1)}, bf16[2,160,2048]{2,1,0:T(8,128)(2,1)}, u32[]{:S(2)}) copy-start(bf16[2,160,2048]{2,1,0:T(8,128)(2,1)} %shard_map.66.first_ref) | copy-start | bytes 3932164
  67.0 22.5 %copy-start.2 = (bf16[2,160,2048]{2,1,0:T(8,128)(2,1)}, bf16[2,160,2048]{2,1,0:T(8,128)(2,1)S(1)}, u32[]{:S(2)}) copy-start(bf16[2,160,2048]{2,1,0:T(8,128)(2,1)S(1)} %collective-permute-done.2.second_ref) | copy-start | bytes 3932164
  67.1 30.4 %collective-permute-start.6 = (bf16[2,160,2048]{2,1,0:T(8,128)(2,1)S(1)}, bf16[2,160,2048]{2,1,0:T(8,128)(2,1)S(1)}, u32[]{:S(2)}, u32[]{:S(2)}) collective-permute-start(bf16[2,160,2048]{2,1,0:T(8,128)(2,1)S(1)} %broadcast_select_fusion.1), channel_id=1, source_target_pairs={{0,4},{4,0},{8,12},{12,8},{16,20},{20,16},{24,28},{28,24},{1,5},{5... | collective-permute-start | bytes 3932168 | tf_op jit(solution)/shard_map/ppermute | solution.py:44
  89.2 36.6 %collective-permute-start.8 = (bf16[2,160,2048]{2,1,0:T(8,128)(2,1)S(1)}, bf16[2,160,2048]{2,1,0:T(8,128)(2,1)}, u32[]{:S(2)}, u32[]{:S(2)}) collective-permute-start(bf16[2,160,2048]{2,1,0:T(8,128)(2,1)S(1)} %broadcast_select_fusion), channel_id=1, source_target_pairs={{0,4},{4,0},{8,12},{12,8},{16,20},{20,16},{24,28},{28,24},{1,5},{5... | collective-permute-start | bytes 3932168 | tf_op jit(solution)/shard_map/ppermute | solution.py:44
  89.4 51.1 %collective-permute-start.3 = (bf16[2,160,2048]{2,1,0:T(8,128)(2,1)S(1)}, bf16[2,160,2048]{2,1,0:T(8,128)(2,1)}, u32[]{:S(2)}, u32[]{:S(2)}) collective-permute-start(bf16[2,160,2048]{2,1,0:T(8,128)(2,1)S(1)} %collective-permute-done.2.second_ref), channel_id=1, source_target_pairs={{0,8},{4,12},{8,16},{12,20},{16,24},{20,28},{1,9},{5,13},{9,17},{1... | collective-permute-start | bytes 3932168 | tf_op jit(solution)/shard_map/ppermute | solution.py:39
  93.9 49.9 %collective-permute-start.5 = (bf16[2,160,2048]{2,1,0:T(8,128)(2,1)}, bf16[2,160,2048]{2,1,0:T(8,128)(2,1)}, u32[]{:S(2)}, u32[]{:S(2)}) collective-permute-start(bf16[2,160,2048]{2,1,0:T(8,128)(2,1)} %collective-permute-done.4.second_ref), channel_id=1, source_target_pairs={{8,0},{12,4},{16,8},{20,12},{24,16},{28,20},{9,1},{13,5},{17,9},{2... | collective-permute-start | bytes 3932168 | tf_op jit(solution)/shard_map/ppermute | solution.py:39
  97.5 33.1 %copy-start.4 = (bf16[2,160,2048]{2,1,0:T(8,128)(2,1)}, bf16[2,160,2048]{2,1,0:T(8,128)(2,1)S(1)}, u32[]{:S(2)}) copy-start(bf16[2,160,2048]{2,1,0:T(8,128)(2,1)S(1)} %collective-permute-done.6.second_ref) | copy-start | bytes 3932164
  97.5 51.9 %collective-permute-start.7 = (bf16[2,160,2048]{2,1,0:T(8,128)(2,1)S(1)}, bf16[2,160,2048]{2,1,0:T(8,128)(2,1)}, u32[]{:S(2)}, u32[]{:S(2)}) collective-permute-start(bf16[2,160,2048]{2,1,0:T(8,128)(2,1)S(1)} %collective-permute-done.6.second_ref), channel_id=1, source_target_pairs={{0,8},{4,12},{8,16},{12,20},{16,24},{20,28},{1,9},{5,13},{9,17},{1... | collective-permute-start | bytes 3932168 | tf_op jit(solution)/shard_map/ppermute | solution.py:39
  125.7 33.3 %collective-permute-start.9 = (bf16[2,160,2048]{2,1,0:T(8,128)(2,1)}, bf16[2,160,2048]{2,1,0:T(8,128)(2,1)}, u32[]{:S(2)}, u32[]{:S(2)}) collective-permute-start(bf16[2,160,2048]{2,1,0:T(8,128)(2,1)} %collective-permute-done.8.second_ref), channel_id=1, source_target_pairs={{8,0},{12,4},{16,8},{20,12},{24,16},{28,20},{9,1},{13,5},{17,9},{2... | collective-permute-start | bytes 3932168 | tf_op jit(solution)/shard_map/ppermute | solution.py:39
  152.7 9.6 %copy-start.5 = (f32[2,8,512]{2,1,0:T(8,128)S(1)}, f32[2,8,512]{2,1,0:T(8,128)}, u32[]{:S(2)}) copy-start(f32[2,8,512]{2,1,0:T(8,128)} %shard_map.70) | copy-start | bytes 98308
  152.7 9.6 %copy-start.6 = (f32[2,8,512]{2,1,0:T(8,128)S(1)}, f32[2,8,512]{2,1,0:T(8,128)}, u32[]{:S(2)}) copy-start(f32[2,8,512]{2,1,0:T(8,128)} %shard_map.71) | copy-start | bytes 98308
  152.7 9.6 %copy-start.7 = (f32[2,8,512]{2,1,0:T(8,128)S(1)}, f32[2,8,512]{2,1,0:T(8,128)}, u32[]{:S(2)}) copy-start(f32[2,8,512]{2,1,0:T(8,128)} %shard_map.72) | copy-start | bytes 98308
  152.7 9.6 %copy-start.8 = (f32[2,8,512]{2,1,0:T(8,128)S(1)}, f32[2,8,512]{2,1,0:T(8,128)}, u32[]{:S(2)}) copy-start(f32[2,8,512]{2,1,0:T(8,128)} %shard_map.73) | copy-start | bytes 98308
  152.7 9.6 %copy-start.9 = (f32[2,8,512]{2,1,0:T(8,128)S(1)}, f32[2,8,512]{2,1,0:T(8,128)}, u32[]{:S(2)}) copy-start(f32[2,8,512]{2,1,0:T(8,128)} %shard_map.65) | copy-start | bytes 98308
  152.7 9.6 %copy-start.10 = (f32[2,8,512]{2,1,0:T(8,128)S(1)}, f32[2,8,512]{2,1,0:T(8,128)}, u32[]{:S(2)}) copy-start(f32[2,8,512]{2,1,0:T(8,128)} %shard_map.67) | copy-start | bytes 98308
  152.8 9.6 %copy-start.11 = (f32[2,8,512]{2,1,0:T(8,128)S(1)}, f32[2,8,512]{2,1,0:T(8,128)}, u32[]{:S(2)}) copy-start(f32[2,8,512]{2,1,0:T(8,128)} %shard_map.68) | copy-start | bytes 98308
  152.8 16.8 %copy-start.13 = (s32[1,4]{1,0:T(1,128)S(1)}, s32[1,4]{1,0:T(1,128)}, u32[]{:S(2)}) copy-start(s32[1,4]{1,0:T(1,128)} %param.11) | copy-start | bytes 52
  162.3 28.2 %copy-start.12 = (f32[2,8,512]{2,1,0:T(8,128)S(1)}, f32[2,8,512]{2,1,0:T(8,128)}, u32[]{:S(2)}) copy-start(f32[2,8,512]{2,1,0:T(8,128)} %shard_map.69) | copy-start | bytes 98308
  164.0 26.4 %all-to-all-start = ((f32[8,2,8,512]{3,2,1,0:T(8,128)}), f32[8,2,8,512]{3,2,1,0:T(8,128)S(1)}, u32[]{:S(2)}, u32[]{:S(2)}) async-start(f32[8,2,8,512]{3,2,1,0:T(8,128)} %select_select_fusion), calls=%async_computation | async-start | bytes 524288 | tf_op jit(solution)/shard_map/all_to_all | solution.py:210
